TPU v7x, 32 devices: a whole 2x2x4 slice. The times are simulated.
32 devices in a mesh: seq: 16 (over z, y, core), dp: 2 (over x).
Axes of the slice: x: 2, y: 2, z: 4, core: 2. Of those that a mesh axis runs over, the one named last changes fastest.
Arguments:
- query: bfloat16 [4096, 32, 128], P(('dp', 'seq')), parts along dimension 0, may hold values from -6 to 6
- normed_key_rows: bfloat16 [4096, 16, 128], P(('dp', 'seq')), parts along dimension 0, may hold values from -6 to 6
- value_rows: bfloat16 [4096, 16, 128], P(('dp', 'seq')), parts along dimension 0, may hold values from -6 to 6
- out_in: bfloat16 [4096, 32, 128], P(('dp', 'seq')), parts along dimension 0, may hold values from -6 to 6
- grad_out: bfloat16 [4096, 32, 128], P(('dp', 'seq')), parts along dimension 0, may hold values from -6 to 6
- lse: float32 [32, 4096], P(None, ('dp', 'seq')), parts along dimension 1, may hold values from 4 to 5
Outputs:
- grad_query: bfloat16 [4096, 32, 128], P(('dp', 'seq')), parts along dimension 0
- grad_key: bfloat16 [4096, 16, 128], P(('dp', 'seq')), parts along dimension 0
- grad_value: bfloat16 [4096, 16, 128], P(('dp', 'seq')), parts along dimension 0
There are 2 independent parts, one for each index of `dp`. A program takes and returns all parts, laid end to end along the dimension named above; each array names one. Nothing has to cross between parts.
All inputs are finite; a program needn't handle non-finite values.
Results may differ from a plain program's by a relative error of at most 0.007.
Values may be sent and summed in bfloat16 or wider, within the bound.
No kernel may reach another device: no remote copies, remote signals or barrier semaphores. Data moves between devices by JAX's collectives and lax.ppermute only.
A program may use at most 128 MiB of HBM per device.

v0:
```python
import jax
import jax.numpy as jnp
from jax import lax
from jax.sharding import PartitionSpec as P

WINDOW = 1024
HOPS = 8


SCALE = 168.0 ** (-0.5)


def from_behind(block, axis, distance):
    devices = range(lax.axis_size(axis))
    route = [(i - distance, i) for i in devices if i - distance in devices]
    return lax.ppermute(block, axis, route)


def per_device(query, normed_key_rows, value_rows, out_in, grad_out, lse):
    tok, heads_q, width = query.shape
    heads_kv = normed_key_rows.shape[1]
    groups = heads_q // heads_kv
    hops = HOPS
    n_keys = (hops + 1) * tok
    index = lax.axis_index("seq")
    paired = jnp.stack([normed_key_rows, value_rows])
    pieces = []
    for step in range(hops):
        pieces.append(from_behind(paired, "seq", step + 1))
    window_kv = jnp.concatenate(pieces[::-1] + [paired], axis=1)
    delta = jnp.sum(grad_out.astype(jnp.float32) * out_in.astype(jnp.float32), axis=-1)
    q_start = index * tok
    k_start = q_start - hops * tok
    q_pos = q_start + jnp.arange(tok, dtype=jnp.int32)
    k_pos = k_start + jnp.arange(n_keys, dtype=jnp.int32)
    diff = q_pos[:, None] - k_pos[None, :]
    valid = (diff >= 0) & (diff < WINDOW) & (k_pos[None, :] >= 0)
    q_heads = query.reshape(tok, heads_kv, groups, width).transpose(1, 0, 2, 3)
    do_heads = grad_out.reshape(tok, heads_kv, groups, width).transpose(1, 0, 2, 3)
    lse_heads = lse.reshape(heads_kv, groups, tok)
    delta_heads = delta.T.reshape(heads_kv, groups, tok)
    k_heads = window_kv[0].transpose(1, 0, 2)
    v_heads = window_kv[1].transpose(1, 0, 2)

    def one_head(items):
        q_h, do_h, lse_h, delta_h, k_h, v_h = items
        score = jnp.einsum("tgd,kd->gtk", q_h, k_h, preferred_element_type=jnp.float32) * SCALE
        prob = jnp.where(valid, jnp.exp(score - lse_h[..., None]), 0.0)
        dprob = jnp.einsum("tgd,kd->gtk", do_h, v_h, preferred_element_type=jnp.float32)
        dscore = (prob * (dprob - delta_h[..., None])).astype(jnp.bfloat16)
        prob_b = prob.astype(jnp.bfloat16)
        grad_v = jnp.einsum("gtk,tgd->kd", prob_b, do_h, preferred_element_type=jnp.float32)
        grad_k = jnp.einsum("gtk,tgd->kd", dscore, q_h, preferred_element_type=jnp.float32) * SCALE
        grad_q = jnp.einsum("gtk,kd->tgd", dscore, k_h, preferred_element_type=jnp.float32) * SCALE
        return (grad_q, jnp.stack([grad_k, grad_v]))

    grad_q_heads, grad_kv_heads = lax.map(
        one_head, (q_heads, do_heads, lse_heads, delta_heads, k_heads, v_heads)
    )
    grad_query = (
        grad_q_heads.transpose(1, 0, 2, 3).reshape(tok, heads_q, width).astype(jnp.bfloat16)
    )
    blocks = grad_kv_heads.reshape(heads_kv, 2, hops + 1, tok, width).transpose(2, 1, 3, 0, 4)
    rounded = lax.optimization_barrier(blocks.astype(jnp.bfloat16))
    total = rounded[hops].astype(jnp.float32)
    for offset in range(1, hops + 1):
        total = total + from_behind(rounded[hops - offset], "seq", -offset).astype(jnp.float32)
    return (grad_query, total[0].astype(jnp.bfloat16), total[1].astype(jnp.bfloat16))


def solution(mesh):
    placed = (
        P(("dp", "seq"), None, None),
        P(("dp", "seq"), None, None),
        P(("dp", "seq"), None, None),
        P(("dp", "seq"), None, None),
        P(("dp", "seq"), None, None),
        P(None, ("dp", "seq")),
    )
    return jax.shard_map(
        per_device,
        mesh=mesh,
        in_specs=placed,
        out_specs=(
            P(("dp", "seq"), None, None),
            P(("dp", "seq"), None, None),
            P(("dp", "seq"), None, None),
        ),
        check_vma=False,
    )
```

profile of v0, /device:TPU:1, one launch (start us, length us, event | category | flops | bytes accessed | tf_op | source)
XLA Modules:
  0.0 669.1 jit_solution(1343503316071368015)
XLA Ops:
  0.7 1.6 copy_bitcast_fusion
  4.1 6.0 collective-permute-start.2
  10.1 4.2 collective-permute-start.1
  14.3 1.4 collective-permute-start
  15.6 2.3 collective-permute-start.3
  17.9 2.5 collective-permute-start.5
  20.4 10.9 %collective-permute-done.2 = bf16[2,128,16,128]{3,1,2,0:T(8,128)(2,1)} collective-permute-done((bf16[2,128,16,128]{3,1,2,0:T(8,128)(2,1)}, bf16[2,128,16,128]{3,1,2,0:T(8,128)(2,1)}, u32[]{:S(2)}, u32[]{:S(2)}) %collective-permute-start.2) | collective-permute-done | bytes 1048608 | tf_op jit(solution)/shard_map/ppermute | solution.py:16
  31.3 4.2 collective-permute-start.4
  36.2 1.4 copy.56
  37.6 1.4 copy.55
  39.0 14.7 %collective-permute-done.1 = bf16[2,128,16,128]{3,1,2,0:T(8,128)(2,1)S(1)} collective-permute-done((bf16[2,128,16,128]{3,1,2,0:T(8,128)(2,1)}, bf16[2,128,16,128]{3,1,2,0:T(8,128)(2,1)S(1)}, u32[]{:S(2)}, u32[]{:S(2)}) %collective-permute-start.1) | collective-permute-done | bytes 1048608 | tf_op jit(solution)/shard_map/ppermute | solution.py:16
  53.8 68.0 %collective-permute-start.6 = (bf16[2,128,16,128]{3,1,2,0:T(8,128)(2,1)}, bf16[2,128,16,128]{3,1,2,0:T(8,128)(2,1)S(1)}, u32[]{:S(2)}, u32[]{:S(2)}) collective-permute-start(bf16[2,128,16,128]{3,1,2,0:T(8,128)(2,1)} %pad_maximum_fusion), channel_id=1, source_target_pairs={{0,4},{2,6},{4,8},{6,10},{8,12},{10,14},{12,16},{14,18},{16,20},{1... | collective-permute-start | bytes 3145736 | tf_op jit(solution)/shard_map/ppermute | solution.py:16
  121.8 2.6 collective-permute-start.7
  124.5 1.3 constant_dynamic-update-slice_fusion.8
  125.8 1.4 constant_dynamic-update-slice_fusion.7
  127.2 1.4 constant_dynamic-update-slice_fusion.6
  128.6 1.4 constant_dynamic-update-slice_fusion.5
  130.1 3.5 collective-permute-done.4
  133.6 1.4 constant_dynamic-update-slice_fusion.4
  135.0 1.4 constant_dynamic-update-slice_fusion.3
  136.4 7.2 %collective-permute-done.6 = bf16[2,128,16,128]{3,1,2,0:T(8,128)(2,1)S(1)} collective-permute-done((bf16[2,128,16,128]{3,1,2,0:T(8,128)(2,1)}, bf16[2,128,16,128]{3,1,2,0:T(8,128)(2,1)S(1)}, u32[]{:S(2)}, u32[]{:S(2)}) %collective-permute-start.6) | collective-permute-done | bytes 1048608 | tf_op jit(solution)/shard_map/ppermute | solution.py:16
  143.8 12.5 %collective-permute-done.7 = bf16[2,128,16,128]{3,1,2,0:T(8,128)(2,1)S(1)} collective-permute-done((bf16[2,128,16,128]{3,1,2,0:T(8,128)(2,1)}, bf16[2,128,16,128]{3,1,2,0:T(8,128)(2,1)S(1)}, u32[]{:S(2)}, u32[]{:S(2)}) %collective-permute-start.7) | collective-permute-done | bytes 1048608 | tf_op jit(solution)/shard_map/ppermute | solution.py:16
  156.5 4.7 slice_bitcast_fusion
  161.2 148.1 %while.13 = (s32[]{:T(128)}, bf16[16,128,2,128]{1,3,2,0:T(8,128)(2,1)}, bf16[16,2,1152,128]{3,2,1,0:T(8,128)(2,1)}, bf16[16,1152,128]{2,1,0:T(8,128)(2,1)}, bf16...) while((s32[]{:T(128)}, ...), condition=%wide.region_2.3_spmd.clone, body=%wide.region_1.2_spmd.clone.sunk | while | flops 381796352 | bytes 8666389 | solution.py:57
  162.8 1.4 fusion.77
  167.7 1.9 fusion.79
  172.0 1.4 fusion.77
  177.0 1.9 fusion.79
  181.3 1.4 fusion.77
  186.2 1.9 fusion.79
  190.5 1.4 fusion.77
  195.5 1.9 fusion.79
  199.7 1.4 fusion.77
  204.7 1.9 fusion.79
  209.0 1.4 fusion.77
  214.0 1.9 fusion.79
  218.3 1.4 fusion.77
  223.3 1.9 fusion.79
  227.5 1.4 fusion.77
  232.5 1.9 fusion.79
  236.8 1.4 fusion.77
  241.7 1.9 fusion.79
  246.0 1.4 fusion.77
  251.0 1.9 fusion.79
  255.2 1.4 fusion.77
  260.2 1.9 fusion.79
  264.5 1.4 fusion.77
  269.5 1.9 fusion.79
  273.8 1.4 fusion.77
  278.7 1.9 fusion.79
  283.0 1.4 fusion.77
  288.0 1.9 fusion.79
  292.3 1.4 fusion.77
  297.3 1.9 fusion.79
  301.7 1.4 fusion.77
  306.6 1.9 fusion.79
  309.3 5.3 slice_bitcast_fusion.9
  314.6 1.9 collective-permute-start.8
  321.8 21.2 %collective-permute-done.8 = bf16[2,128,16,128]{3,1,0,2:T(8,128)(2,1)S(1)} collective-permute-done((bf16[2,128,16,128]{3,1,0,2:T(8,128)(2,1)S(1)}, bf16[2,128,16,128]{3,1,0,2:T(8,128)(2,1)S(1)}, u32[]{:S(2)}, u32[]{:S(2)}) %collective-permute-start.8) | collective-permute-done | bytes 1048608 | tf_op jit(solution)/shard_map/ppermute | solution.py:16
  344.2 100.8 %collective-permute-done.13 = bf16[2,128,16,128]{3,1,0,2:T(8,128)(2,1)S(1)} collective-permute-done((bf16[2,128,16,128]{3,1,0,2:T(8,128)(2,1)S(1)}, bf16[2,128,16,128]{3,1,0,2:T(8,128)(2,1)S(1)}, u32[]{:S(2)}, u32[]{:S(2)}) %collective-permute-start.13) | collective-permute-done | bytes 1048608 | tf_op jit(solution)/shard_map/ppermute | solution.py:16
  447.8 3.7 copy.58
  451.5 176.9 %collective-permute-done.15 = bf16[2,128,16,128]{3,1,0,2:T(8,128)(2,1)} collective-permute-done((bf16[2,128,16,128]{3,1,0,2:T(8,128)(2,1)}, bf16[2,128,16,128]{3,1,0,2:T(8,128)(2,1)}, u32[]{:S(2)}, u32[]{:S(2)}) %collective-permute-start.15) | collective-permute-done | bytes 1048608 | tf_op jit(solution)/shard_map/ppermute | solution.py:16
  628.4 33.3 %collective-permute-done.14 = bf16[2,128,16,128]{3,1,0,2:T(8,128)(2,1)} collective-permute-done((bf16[2,128,16,128]{3,1,0,2:T(8,128)(2,1)S(1)}, bf16[2,128,16,128]{3,1,0,2:T(8,128)(2,1)}, u32[]{:S(2)}, u32[]{:S(2)}) %collective-permute-start.14) | collective-permute-done | bytes 1048608 | tf_op jit(solution)/shard_map/ppermute | solution.py:16
  661.7 5.0 fusion.45
  (144 shorter events, 110.3 us)
Async XLA Ops:
  0.6 34.9 %copy-start.4 = (bf16[128,32,128]{2,1,0:T(8,128)(2,1)S(1)}, bf16[128,32,128]{2,1,0:T(8,128)(2,1)}, u32[]{:S(2)}) copy-start(bf16[128,32,128]{2,1,0:T(8,128)(2,1)} %param.12) | copy-start | bytes 3145732
  0.6 34.9 %copy-start.6 = (bf16[128,32,128]{2,1,0:T(8,128)(2,1)S(1)}, bf16[128,32,128]{2,1,0:T(8,128)(2,1)}, u32[]{:S(2)}) copy-start(bf16[128,32,128]{2,1,0:T(8,128)(2,1)} %param.11) | copy-start | bytes 3145732
  0.7 37.0 %copy-start.7 = (bf16[128,32,128]{2,1,0:T(8,128)(2,1)S(1)}, bf16[128,32,128]{2,1,0:T(8,128)(2,1)}, u32[]{:S(2)}) copy-start(bf16[128,32,128]{2,1,0:T(8,128)(2,1)} %param.8) | copy-start | bytes 3145732
  2.3 0.8 copy-start
  2.3 1.8 copy-start.2
  4.1 27.2 %collective-permute-start.2 = (bf16[2,128,16,128]{3,1,2,0:T(8,128)(2,1)}, bf16[2,128,16,128]{3,1,2,0:T(8,128)(2,1)}, u32[]{:S(2)}, u32[]{:S(2)}) collective-permute-start(bf16[2,128,16,128]{3,1,2,0:T(8,128)(2,1)} %pad_maximum_fusion), channel_id=1, source_target_pairs={{0,12},{2,14},{4,16},{6,18},{8,20},{10,22},{12,24},{14,26},{16,28}... | collective-permute-start | bytes 3145736 | tf_op jit(solution)/shard_map/ppermute | solution.py:16
  10.1 43.7 %collective-permute-start.1 = (bf16[2,128,16,128]{3,1,2,0:T(8,128)(2,1)}, bf16[2,128,16,128]{3,1,2,0:T(8,128)(2,1)S(1)}, u32[]{:S(2)}, u32[]{:S(2)}) collective-permute-start(bf16[2,128,16,128]{3,1,2,0:T(8,128)(2,1)} %pad_maximum_fusion), channel_id=1, source_target_pairs={{0,14},{2,16},{4,18},{6,20},{8,22},{10,24},{12,26},{14,28},{16,30}... | collective-permute-start | bytes 3145736 | tf_op jit(solution)/shard_map/ppermute | solution.py:16
  14.3 107.5 %collective-permute-start = (bf16[2,128,16,128]{3,1,2,0:T(8,128)(2,1)}, bf16[2,128,16,128]{3,1,2,0:T(8,128)(2,1)S(1)}, u32[]{:S(2)}, u32[]{:S(2)}) collective-permute-start(bf16[2,128,16,128]{3,1,2,0:T(8,128)(2,1)} %pad_maximum_fusion), channel_id=1, source_target_pairs={{0,16},{2,18},{4,20},{6,22},{8,24},{10,26},{12,28},{14,30},{1,17},... | collective-permute-start | bytes 3145736 | tf_op jit(solution)/shard_map/ppermute | solution.py:16
  15.6 113.0 %collective-permute-start.3 = (bf16[2,128,16,128]{3,1,2,0:T(8,128)(2,1)}, bf16[2,128,16,128]{3,1,2,0:T(8,128)(2,1)}, u32[]{:S(2)}, u32[]{:S(2)}) collective-permute-start(bf16[2,128,16,128]{3,1,2,0:T(8,128)(2,1)} %pad_maximum_fusion), channel_id=1, source_target_pairs={{0,10},{2,12},{4,14},{6,16},{8,18},{10,20},{12,22},{14,24},{16,26}... | collective-permute-start | bytes 3145736 | tf_op jit(solution)/shard_map/ppermute | solution.py:16
  17.9 117.1 %collective-permute-start.5 = (bf16[2,128,16,128]{3,1,2,0:T(8,128)(2,1)}, bf16[2,128,16,128]{3,1,2,0:T(8,128)(2,1)}, u32[]{:S(2)}, u32[]{:S(2)}) collective-permute-start(bf16[2,128,16,128]{3,1,2,0:T(8,128)(2,1)} %pad_maximum_fusion), channel_id=1, source_target_pairs={{0,6},{2,8},{4,10},{6,12},{8,14},{10,16},{12,18},{14,20},{16,22},{... | collective-permute-start | bytes 3145736 | tf_op jit(solution)/shard_map/ppermute | solution.py:16
  31.3 102.3 %collective-permute-start.4 = (bf16[2,128,16,128]{3,1,2,0:T(8,128)(2,1)}, bf16[2,128,16,128]{3,1,2,0:T(8,128)(2,1)}, u32[]{:S(2)}, u32[]{:S(2)}) collective-permute-start(bf16[2,128,16,128]{3,1,2,0:T(8,128)(2,1)} %pad_maximum_fusion), channel_id=1, source_target_pairs={{0,8},{2,10},{4,12},{6,14},{8,16},{10,18},{12,20},{14,22},{16,24},... | collective-permute-start | bytes 3145736 | tf_op jit(solution)/shard_map/ppermute | solution.py:16
  53.8 70.7 %copy-start.8 = (bf16[2,128,16,128]{3,1,2,0:T(8,128)(2,1)}, bf16[2,128,16,128]{3,1,2,0:T(8,128)(2,1)S(1)}, u32[]{:S(2)}) copy-start(bf16[2,128,16,128]{3,1,2,0:T(8,128)(2,1)S(1)} %collective-permute-done.1) | copy-start | bytes 3145732
  53.8 89.9 %collective-permute-start.6 = (bf16[2,128,16,128]{3,1,2,0:T(8,128)(2,1)}, bf16[2,128,16,128]{3,1,2,0:T(8,128)(2,1)S(1)}, u32[]{:S(2)}, u32[]{:S(2)}) collective-permute-start(bf16[2,128,16,128]{3,1,2,0:T(8,128)(2,1)} %pad_maximum_fusion), channel_id=1, source_target_pairs={{0,4},{2,6},{4,8},{6,10},{8,12},{10,14},{12,16},{14,18},{16,20},{1... | collective-permute-start | bytes 3145736 | tf_op jit(solution)/shard_map/ppermute | solution.py:16
  121.8 2.6 copy-start.9
  121.8 34.4 %collective-permute-start.7 = (bf16[2,128,16,128]{3,1,2,0:T(8,128)(2,1)}, bf16[2,128,16,128]{3,1,2,0:T(8,128)(2,1)S(1)}, u32[]{:S(2)}, u32[]{:S(2)}) collective-permute-start(bf16[2,128,16,128]{3,1,2,0:T(8,128)(2,1)} %pad_maximum_fusion), channel_id=1, source_target_pairs={{0,2},{2,4},{4,6},{6,8},{8,10},{10,12},{12,14},{14,16},{16,18},{18... | collective-permute-start | bytes 3145736 | tf_op jit(solution)/shard_map/ppermute | solution.py:16
  130.0 26.3 %copy-start.1 = (bf16[1,128,16,128]{3,1,2,0:T(8,128)(2,1)S(1)}, bf16[1,128,16,128]{3,1,2,0:T(8,128)(2,1)}, u32[]{:S(2)}) copy-start(bf16[1,128,16,128]{3,1,2,0:T(8,128)(2,1)} %copy-done) | copy-start | bytes 1572868
  130.1 26.3 %copy-start.3 = (bf16[1,128,16,128]{3,1,2,0:T(8,128)(2,1)S(1)}, bf16[1,128,16,128]{3,1,2,0:T(8,128)(2,1)}, u32[]{:S(2)}) copy-start(bf16[1,128,16,128]{3,1,2,0:T(8,128)(2,1)} %copy-done.2) | copy-start | bytes 1572868
  314.6 28.3 %collective-permute-start.8 = (bf16[2,128,16,128]{3,1,0,2:T(8,128)(2,1)S(1)}, bf16[2,128,16,128]{3,1,0,2:T(8,128)(2,1)S(1)}, u32[]{:S(2)}, u32[]{:S(2)}) collective-permute-start(bf16[2,128,16,128]{3,1,0,2:T(8,128)(2,1)S(1)} %get-tuple-element.134), channel_id=1, source_target_pairs={{2,0},{4,2},{6,4},{8,6},{10,8},{12,10},{14,12},{16,14},{18,16},{20... | collective-permute-start | bytes 3145736 | tf_op jit(solution)/shard_map/ppermute | solution.py:16
  316.6 128.5 %collective-permute-start.13 = (bf16[2,128,16,128]{3,1,0,2:T(8,128)(2,1)S(1)}, bf16[2,128,16,128]{3,1,0,2:T(8,128)(2,1)S(1)}, u32[]{:S(2)}, u32[]{:S(2)}) collective-permute-start(bf16[2,128,16,128]{3,1,0,2:T(8,128)(2,1)S(1)} %get-tuple-element.135), channel_id=1, source_target_pairs={{12,0},{14,2},{16,4},{18,6},{20,8},{22,10},{24,12},{26,14},{28,16}... | collective-permute-start | bytes 3145736 | tf_op jit(solution)/shard_map/ppermute | solution.py:16
  317.9 128.7 %collective-permute-start.12 = (bf16[2,128,16,128]{3,1,0,2:T(8,128)(2,1)S(1)}, bf16[2,128,16,128]{3,1,0,2:T(8,128)(2,1)S(1)}, u32[]{:S(2)}, u32[]{:S(2)}) collective-permute-start(bf16[2,128,16,128]{3,1,0,2:T(8,128)(2,1)S(1)} %get-tuple-element.136), channel_id=1, source_target_pairs={{10,0},{12,2},{14,4},{16,6},{18,8},{20,10},{22,12},{24,14},{26,16}... | collective-permute-start | bytes 3145736 | tf_op jit(solution)/shard_map/ppermute | solution.py:16
  319.2 132.4 %collective-permute-start.11 = (bf16[2,128,16,128]{3,1,0,2:T(8,128)(2,1)}, bf16[2,128,16,128]{3,1,0,2:T(8,128)(2,1)}, u32[]{:S(2)}, u32[]{:S(2)}) collective-permute-start(bf16[2,128,16,128]{3,1,0,2:T(8,128)(2,1)} %get-tuple-element.137), channel_id=1, source_target_pairs={{8,0},{10,2},{12,4},{14,6},{16,8},{18,10},{20,12},{22,14},{24,16},... | collective-permute-start | bytes 3145736 | tf_op jit(solution)/shard_map/ppermute | solution.py:16
  320.5 131.1 %collective-permute-start.10 = (bf16[2,128,16,128]{3,1,0,2:T(8,128)(2,1)}, bf16[2,128,16,128]{3,1,0,2:T(8,128)(2,1)}, u32[]{:S(2)}, u32[]{:S(2)}) collective-permute-start(bf16[2,128,16,128]{3,1,0,2:T(8,128)(2,1)} %get-tuple-element.138), channel_id=1, source_target_pairs={{6,0},{8,2},{10,4},{12,6},{14,8},{16,10},{18,12},{20,14},{22,16},{... | collective-permute-start | bytes 3145736 | tf_op jit(solution)/shard_map/ppermute | solution.py:16
  342.9 108.6 %collective-permute-start.9 = (bf16[2,128,16,128]{3,1,0,2:T(8,128)(2,1)}, bf16[2,128,16,128]{3,1,0,2:T(8,128)(2,1)}, u32[]{:S(2)}, u32[]{:S(2)}) collective-permute-start(bf16[2,128,16,128]{3,1,0,2:T(8,128)(2,1)} %get-tuple-element.139), channel_id=1, source_target_pairs={{4,0},{6,2},{8,4},{10,6},{12,8},{14,10},{16,12},{18,14},{20,16},{2... | collective-permute-start | bytes 3145736 | tf_op jit(solution)/shard_map/ppermute | solution.py:16
  445.0 183.4 %collective-permute-start.15 = (bf16[2,128,16,128]{3,1,0,2:T(8,128)(2,1)}, bf16[2,128,16,128]{3,1,0,2:T(8,128)(2,1)}, u32[]{:S(2)}, u32[]{:S(2)}) collective-permute-start(bf16[2,128,16,128]{3,1,0,2:T(8,128)(2,1)} %get-tuple-element.140), channel_id=1, source_target_pairs={{16,0},{18,2},{20,4},{22,6},{24,8},{26,10},{28,12},{30,14},{17,1},... | collective-permute-start | bytes 3145736 | tf_op jit(solution)/shard_map/ppermute | solution.py:16
  446.5 1.3 copy-start.5
  446.6 215.2 %collective-permute-start.14 = (bf16[2,128,16,128]{3,1,0,2:T(8,128)(2,1)S(1)}, bf16[2,128,16,128]{3,1,0,2:T(8,128)(2,1)}, u32[]{:S(2)}, u32[]{:S(2)}) collective-permute-start(bf16[2,128,16,128]{3,1,0,2:T(8,128)(2,1)S(1)} %get-tuple-element.141), channel_id=1, source_target_pairs={{14,0},{16,2},{18,4},{20,6},{22,8},{24,10},{26,12},{28,14},{30,16}... | collective-permute-start | bytes 3145736 | tf_op jit(solution)/shard_map/ppermute | solution.py:16
where the time goes:
time: 673 us; the launch traced here: 669 us
  waiting for transfers between devices  381 us (57%)
  matrix products  109 us (16%)
  starting transfers between devices  102 us (15%)
  local copies, waits for them, and re-layouts  40.8 us (6%)
  other arithmetic  34.2 us (5%)
    ppermute x16, waiting for transfers between devices, from_behind(): return lax.ppermute(block, axis, route)  381 us
    ppermute x16, starting transfers between devices, from_behind(): return lax.ppermute(block, axis, route)  102 us
    dot_general x16, matrix products, one_head(): jnp.einsum('gtk,kd->tgd', dscore, k_h, preferred_element_type=jnp.float32)  30.1 us
    dot_general x16, matrix products, one_head(): jnp.einsum('tgd,kd->gtk', q_h, k_h, preferred_element_type=jnp.float32)  21.8 us
    dot_general x16, matrix products, one_head(): jnp.einsum('tgd,kd->gtk', do_h, v_h, preferred_element_type=jnp.float32)  20.5 us
    dot_general x16, matrix products, one_head(): jnp.einsum('gtk,tgd->kd', dscore, q_h, preferred_element_type=jnp.float32)  18.5 us
    dot_general x16, matrix products, one_head(): jnp.einsum('gtk,tgd->kd', prob_b, do_h, preferred_element_type=jnp.float32)  18.5 us
    unnamed x32, local copies, waits for them, and re-layouts  14.5 us
  transfers between devices with their start and end apart: 16, of which 10 were waited for; matrix products, arithmetic and copies ran while one was open for 2% of the time, Pallas kernels for 0%

commit v1 on v0

v1 whole, which is shorter than its diff:
```python
import functools

import jax
import jax.numpy as jnp
from jax import lax
from jax.experimental import pallas as pl
from jax.experimental.pallas import tpu as pltpu
from jax.sharding import PartitionSpec as P

WINDOW = 1024
HOPS = 8
PLANE = 4
HEADS_PER_STEP = 2

SCALE = 168.0 ** (-0.5)


def shift(x, n, distance):
    pairs = [(i, i + distance) for i in range(n) if 0 <= i + distance < n]
    return lax.ppermute(x, "seq", pairs)


def swap(x, n, bit):
    return lax.ppermute(x, "seq", [(i, i ^ bit) for i in range(n)])


def _blocks_kernel(modes, valid_ref, q_ref, do_ref, lse_ref, delta_ref, *refs):
    nb = len(modes)
    kv_refs = refs[:nb]
    dq_ref = refs[nb]
    dkv_refs = refs[nb + 1:]
    gb, grp, tok, width = q_ref.shape
    rows = grp * tok
    kk = lax.broadcasted_iota(jnp.int32, (tok, rows), 0)
    tt = lax.broadcasted_iota(jnp.int32, (tok, rows), 1) % tok
    causal = kk <= tt
    strict = kk > tt
    for g in range(gb):
        q = q_ref[g].reshape(rows, width)
        do = do_ref[g].reshape(rows, width)
        lse = lse_ref[g]
        delta = delta_ref[g]
        dq = jnp.zeros((rows, width), jnp.float32)
        for b, mode in enumerate(modes):
            k = kv_refs[b][0, g]
            v = kv_refs[b][1, g]
            off = jnp.where(valid_ref[b] > 0, 0.0, 1e30).astype(jnp.float32)
            s = lax.dot_general(k, q, (((1,), (1,)), ((), ())), preferred_element_type=jnp.float32)
            e = jnp.exp(s * SCALE - lse - off)
            if mode == 0:
                p = jnp.where(causal, e, 0.0)
            elif mode == 2:
                p = jnp.where(strict, e, 0.0)
            else:
                p = e
            dp = lax.dot_general(v, do, (((1,), (1,)), ((), ())), preferred_element_type=jnp.float32)
            ds = p * (dp - delta)
            pb = p.astype(jnp.bfloat16)
            dsb = ds.astype(jnp.bfloat16)
            dv = jnp.dot(pb, do, preferred_element_type=jnp.float32)
            dk = jnp.dot(dsb, q, preferred_element_type=jnp.float32) * SCALE
            dq = dq + lax.dot_general(dsb, k, (((0,), (0,)), ((), ())), preferred_element_type=jnp.float32)
            dkv_refs[b][0, g] = dk.astype(jnp.bfloat16)
            dkv_refs[b][1, g] = dv.astype(jnp.bfloat16)
        dq_ref[g] = (dq * SCALE).astype(dq_ref.dtype).reshape(grp, tok, width)


def attend_blocks(modes, valid, q4, do4, lse3, delta3, kvs):
    nh, grp, tok, width = q4.shape
    gb = HEADS_PER_STEP
    nb = len(modes)
    hspec = pl.BlockSpec((gb, grp, tok, width), lambda i, v: (i, 0, 0, 0))
    rspec = pl.BlockSpec((gb, 1, grp * tok), lambda i, v: (i, 0, 0))
    kvspec = pl.BlockSpec((2, gb, tok, width), lambda i, v: (0, i, 0, 0))
    out_shape = [jax.ShapeDtypeStruct(q4.shape, jnp.bfloat16)]
    out_shape += [jax.ShapeDtypeStruct(kv.shape, jnp.bfloat16) for kv in kvs]
    grid_spec = pltpu.PrefetchScalarGridSpec(
        num_scalar_prefetch=1,
        grid=(nh // gb,),
        in_specs=[hspec, hspec, rspec, rspec] + [kvspec] * nb,
        out_specs=[hspec] + [kvspec] * nb,
    )
    outs = pl.pallas_call(
        functools.partial(_blocks_kernel, tuple(modes)),
        grid_spec=grid_spec,
        out_shape=out_shape,
        compiler_params=pltpu.CompilerParams(dimension_semantics=("arbitrary",)),
    )(valid, q4, do4, lse3, delta3, *kvs)
    return outs[0], list(outs[1:])


def per_device(query, normed_key_rows, value_rows, out_in, grad_out, lse):
    tok, heads_q, width = query.shape
    heads_kv = normed_key_rows.shape[1]
    groups = heads_q // heads_kv
    n = lax.axis_size("seq")
    levels = HOPS // PLANE
    idx = lax.axis_index("seq")
    half = (idx % PLANE) // 2
    core = idx % 2

    q4 = query.transpose(1, 0, 2).reshape(heads_kv, groups, tok, width)
    do4 = grad_out.transpose(1, 0, 2).reshape(heads_kv, groups, tok, width)
    delta = jnp.sum(grad_out.astype(jnp.float32) * out_in.astype(jnp.float32), axis=-1)
    delta3 = delta.T.reshape(heads_kv, 1, groups * tok)
    lse3 = lse.reshape(heads_kv, 1, groups * tok)
    own = jnp.stack([normed_key_rows, value_rows]).transpose(0, 2, 1, 3)

    xs = [own]
    for _ in range(levels):
        xs.append(shift(xs[-1], n, PLANE))
    cs = [swap(jnp.where(core == 0, xs[k], xs[k + 1]), n, 1) for k in range(levels)]
    ys = [swap(jnp.where(half == 0, xs[0], xs[1]), n, 2)]
    for _ in range(1, levels):
        ys.append(shift(ys[-1], n, PLANE))
    ds = [swap(y, n, 1) for y in ys]

    blocks = xs + cs + ys + ds
    modes = [0] + [1] * (levels - 1) + [2] + [1] * (3 * levels)
    dist = [a * PLANE for a in range(levels + 1)]
    dist += [k * PLANE + 3 - 2 * core for k in range(levels)]
    dist += [k * PLANE + 2 for k in range(levels)]
    dist += [k * PLANE + 1 + 2 * core for k in range(levels)]
    valid = jnp.stack([(idx >= d).astype(jnp.int32) for d in dist])

    dq4, terms = attend_blocks(modes, valid, q4, do4, lse3, delta3, blocks)
    tx = terms[: levels + 1]
    tc = terms[levels + 1: 2 * levels + 1]
    ty = terms[2 * levels + 1: 3 * levels + 1]
    td = terms[3 * levels + 1:]

    f32 = jnp.float32
    bf16 = jnp.bfloat16
    ysum = [ty[k].astype(f32) + swap(td[k], n, 1).astype(f32) for k in range(levels)]
    for k in range(levels - 1, 0, -1):
        ysum[k - 1] = ysum[k - 1] + shift(ysum[k].astype(bf16), n, -PLANE).astype(f32)
    yret = swap(ysum[0].astype(bf16), n, 2).astype(f32)
    cret = [swap(tc[k], n, 1).astype(f32) for k in range(levels)]
    part = [tx[a].astype(f32) for a in range(levels + 1)]
    zero = jnp.zeros_like(part[0])
    for a in range(levels + 1):
        if a <= 1:
            part[a] = part[a] + jnp.where(half == a, yret, zero)
        for k in range(levels):
            if 0 <= a - k <= 1:
                part[a] = part[a] + jnp.where(core == a - k, cret[k], zero)
    for a in range(levels, 0, -1):
        part[a - 1] = part[a - 1] + shift(part[a].astype(bf16), n, -PLANE).astype(f32)
    grad = part[0].astype(bf16)

    grad_query = dq4.reshape(heads_q, tok, width).transpose(1, 0, 2)
    return (grad_query, grad[0].transpose(1, 0, 2), grad[1].transpose(1, 0, 2))


def solution(mesh):
    placed = (
        P(("dp", "seq"), None, None),
        P(("dp", "seq"), None, None),
        P(("dp", "seq"), None, None),
        P(("dp", "seq"), None, None),
        P(("dp", "seq"), None, None),
        P(None, ("dp", "seq")),
    )
    return jax.shard_map(
        per_device,
        mesh=mesh,
        in_specs=placed,
        out_specs=(
            P(("dp", "seq"), None, None),
            P(("dp", "seq"), None, None),
            P(("dp", "seq"), None, None),
        ),
        check_vma=False,
    )
```

time: 673 us -> 239 us (0.36)
  the two profiles are of different devices: /device:TPU:1 before, /device:TPU:0 now
where the time goes in v1:
time: 239 us; the launch traced here: 238 us
  waiting for transfers between devices  154 us (64%)
  Pallas kernels  32.5 us (14%)
  starting transfers between devices  24.8 us (10%)
  other arithmetic  16 us (7%)
  local copies, waits for them, and re-layouts  10.3 us (4%)
    ppermute x6, waiting for transfers between devices, shift(): return lax.ppermute(x, 'seq', pairs)  124 us
    pallas_call x1, Pallas kernels, attend_blocks(): pl.pallas_call(functools.partial(_blocks_kernel, tuple(modes)), grid_spec...  32.5 us
    ppermute x10, waiting for transfers between devices, swap(): return lax.ppermute(x, 'seq', [(i, i ^ bit) for i in range(n)])  29.6 us
    ppermute x6, starting transfers between devices, shift(): return lax.ppermute(x, 'seq', pairs)  19.7 us
    convert_element_type x2, other arithmetic, per_device(): part[a].astype(bf16)  5.29 us
    ppermute x10, starting transfers between devices, swap(): return lax.ppermute(x, 'seq', [(i, i ^ bit) for i in range(n)])  5.1 us
  transfers between devices with their start and end apart: 16, of which 9 were waited for; matrix products, arithmetic and copies ran while one was open for 7% of the time, Pallas kernels for 0%

profile of v1, /device:TPU:0, one launch (start us, length us, event | category | flops | bytes accessed | tf_op | source)
XLA Modules:
  0.0 238.3 jit_solution(1563824688805046493)
XLA Ops:
  0.6 1.5 copy_bitcast_fusion.1
  2.1 0.1 maximum_bitcast_fusion.refs_0_
  2.2 0.0 copy-start
  2.2 5.9 %collective-permute-start = (bf16[2,16,128,128]{3,2,1,0:T(8,128)(2,1)S(1)}, bf16[2,16,128,128]{3,2,1,0:T(8,128)(2,1)}, u32[]{:S(2)}, u32[]{:S(2)}) collective-permute-start(bf16[2,16,128,128]{3,2,1,0:T(8,128)(2,1)S(1)} %maximum_bitcast_fusion.refs_0_), channel_id=1, source_target_pairs={{0,8},{2,10},{4,12},{6,14},{8,16},{10,18},{12,20},{14,22},{16,24},... | collective-permute-start | bytes 3145736 | tf_op jit(solution)/shard_map/ppermute | solution.py:20
  8.1 21.4 %collective-permute-done.refs_1_ = bf16[2,16,128,128]{3,2,1,0:T(8,128)(2,1)} collective-permute-done((bf16[2,16,128,128]{3,2,1,0:T(8,128)(2,1)S(1)}, bf16[2,16,128,128]{3,2,1,0:T(8,128)(2,1)}, u32[]{:S(2)}, u32[]{:S(2)}) %collective-permute-start) | collective-permute-done | bytes 1048608 | tf_op jit(solution)/shard_map/ppermute | solution.py:20
  29.6 5.5 %collective-permute-start.1 = (bf16[2,16,128,128]{3,2,1,0:T(8,128)(2,1)}, bf16[2,16,128,128]{3,2,1,0:T(8,128)(2,1)}, u32[]{:S(2)}, u32[]{:S(2)}) collective-permute-start(bf16[2,16,128,128]{3,2,1,0:T(8,128)(2,1)} %collective-permute-done.refs_1_), channel_id=1, source_target_pairs={{0,8},{2,10},{4,12},{6,14},{8,16},{10,18},{12,20},{14,22},{16,24},... | collective-permute-start | bytes 3145736 | tf_op jit(solution)/shard_map/ppermute | solution.py:20
  35.0 0.0 copy-start.1
  35.0 20.8 %collective-permute-done.1.refs_2_ = bf16[2,16,128,128]{3,2,1,0:T(8,128)(2,1)} collective-permute-done((bf16[2,16,128,128]{3,2,1,0:T(8,128)(2,1)}, bf16[2,16,128,128]{3,2,1,0:T(8,128)(2,1)}, u32[]{:S(2)}, u32[]{:S(2)}) %collective-permute-start.1) | collective-permute-done | bytes 1048608 | tf_op jit(solution)/shard_map/ppermute | solution.py:20
  55.9 2.8 %broadcast_select_fusion = (bf16[2,16,128,128]{3,2,1,0:T(8,128)(2,1)S(1)}, bf16[2,16,128,128]{3,2,1,0:T(8,128)(2,1)}, bf16[2,16,128,128]{3,2,1,0:T(8,128)(2,1)}) fusion(bf16[2,16,128,128]{3,2,1,0:T(8,128)(2,1)} %collective-permute-done.refs_1_, pred[]{:T(512)S(6)} %eq.21, bf16[1,128,16,128]{3,1,2,0:T(8,128)(2,1)S(1)} %get-tuple-element.34, ...), kind=kLoop, calls=%fused_computation.22 | loop fusion | flops 2097152 | bytes 6291458 | tf_op jit(solution)/shard_map/jit(_where)/select_n | solution.py:113
  58.7 0.0 copy-done
  58.7 1.5 collective-permute-start.4
  60.2 21.9 %collective-permute-done.4.refs_5_ = bf16[2,16,128,128]{3,2,1,0:T(8,128)(2,1)S(1)} collective-permute-done((bf16[2,16,128,128]{3,2,1,0:T(8,128)(2,1)S(1)}, bf16[2,16,128,128]{3,2,1,0:T(8,128)(2,1)S(1)}, u32[]{:S(2)}, u32[]{:S(2)}) %collective-permute-start.4) | collective-permute-done | bytes 1048608 | tf_op jit(solution)/shard_map/ppermute | solution.py:24
  82.1 0.0 copy-start.2
  82.1 4.4 %collective-permute-start.5 = (bf16[2,16,128,128]{3,2,1,0:T(8,128)(2,1)S(1)}, bf16[2,16,128,128]{3,2,1,0:T(8,128)(2,1)S(1)}, u32[]{:S(2)}, u32[]{:S(2)}) collective-permute-start(bf16[2,16,128,128]{3,2,1,0:T(8,128)(2,1)S(1)} %collective-permute-done.4.refs_5_), channel_id=1, source_target_pairs={{0,8},{2,10},{4,12},{6,14},{8,16},{10,18},{12,20},{14,22},{16,24},... | collective-permute-start | bytes 3145736 | tf_op jit(solution)/shard_map/ppermute | solution.py:20
  86.5 0.1 collective-permute-start.2
  86.6 0.5 collective-permute-start.3
  87.1 0.1 collective-permute-start.6
  87.2 19.3 %collective-permute-done.5.refs_6_ = bf16[2,16,128,128]{3,2,1,0:T(8,128)(2,1)S(1)} collective-permute-done((bf16[2,16,128,128]{3,2,1,0:T(8,128)(2,1)S(1)}, bf16[2,16,128,128]{3,2,1,0:T(8,128)(2,1)S(1)}, u32[]{:S(2)}, u32[]{:S(2)}) %collective-permute-start.5) | collective-permute-done | bytes 1048608 | tf_op jit(solution)/shard_map/ppermute | solution.py:20
  106.5 0.0 copy-start.3
  106.5 0.0 collective-permute-start.7
  106.5 0.1 stack.59
  106.6 0.6 stack.60.valid_ref
  107.2 0.0 copy-done.1
  107.2 1.8 multiply_reduce_fusion
  109.0 0.0 copy-done.2
  109.1 0.0 copy-done.3
  109.1 0.7 copy.18
  109.8 2.6 %copy.16 = bf16[32,128,128]{2,1,0:T(8,128)(2,1)} copy(bf16[32,128,128]{2,0,1:T(8,128)(2,1)} %bitcast.41) | data formatting | bytes 2097152 | tf_op jit(solution)/shard_map/transpose | solution.py:102
  112.4 1.4 copy.17
  113.8 0.0 collective-permute-done.2.refs_3_
  113.8 0.0 collective-permute-done.3.refs_4_
  113.8 0.0 collective-permute-done.6.refs_7_
  113.8 0.0 collective-permute-done.7.refs_8_
  113.8 32.5 %shard_map.85 = (bf16[16,2,128,128]{3,2,1,0:T(8,128)(2,1)}, bf16[2,16,128,128]{3,2,1,0:T(8,128)(2,1)}, bf16[2,16,128,128]{3,2,1,0:T(8,128)(2,1)}, bf16[2,16,128,...) custom-call(s32[9]{0:T(128)} %stack.60.valid_ref, ...), custom_call_target="tpu_custom_call" | custom-call | tf_op jit(solution)/shard_map/pallas_call | solution.py:83
  146.3 0.5 collective-permute-start.9
  146.7 0.1 collective-permute-start.13
  146.8 0.4 collective-permute-start.8
  147.2 2.0 collective-permute-done.9
  149.2 1.6 add_convert_fusion.1
  150.8 1.3 collective-permute-start.10
  152.1 0.4 collective-permute-start.12
  152.6 0.0 collective-permute-done.13
  152.6 0.0 copy-start.6
  152.6 2.7 %fusion.10 = bf16[2,16,128,128]{3,2,1,0:T(8,128)(2,1)} fusion(bf16[2,16,128,128]{3,2,1,0:T(8,128)(2,1)S(1)} %collective-permute-done.13, bf16[2,16,128,128]{3,2,1,0:T(8,128)(2,1)} %get-tuple-element.22, pred[]{:T(512)S(6)} %eq.23), kind=kLoop, calls=%fused_computation.16 | loop fusion | flops 2621440 | bytes 3145729 | tf_op jit(solution)/shard_map/convert_element_type | solution.py:148
  155.3 1.3 collective-permute-start.14
  156.5 0.0 collective-permute-done.8
  156.6 22.8 %collective-permute-done.10 = bf16[2,16,128,128]{3,2,1,0:T(8,128)(2,1)} collective-permute-done((bf16[2,16,128,128]{3,2,1,0:T(8,128)(2,1)S(1)}, bf16[2,16,128,128]{3,2,1,0:T(8,128)(2,1)}, u32[]{:S(2)}, u32[]{:S(2)}) %collective-permute-start.10) | collective-permute-done | bytes 1048608 | tf_op jit(solution)/shard_map/ppermute | solution.py:20
  179.3 0.0 copy-done.6
  179.3 3.0 %add_convert_fusion = bf16[2,16,128,128]{3,2,1,0:T(8,128)(2,1)} fusion(bf16[2,16,128,128]{3,2,1,0:T(8,128)(2,1)} %collective-permute-done.10, bf16[2,16,128,128]{3,2,1,0:T(8,128)(2,1)} %collective-permute-done.8, bf16[2,16,128,128]{3,2,1,0:T(8,128)(2,1)S(1)} %copy-done.6), kind=kLoop, calls=%fused_computation.17 | loop fusion | flops 3145728 | bytes 4194304 | tf_op jit(solution)/shard_map/convert_element_type | solution.py:137
  182.4 1.5 collective-permute-start.11
  183.9 0.0 collective-permute-done.12
  183.9 17.6 %collective-permute-done.14 = bf16[2,16,128,128]{3,2,1,0:T(8,128)(2,1)} collective-permute-done((bf16[2,16,128,128]{3,2,1,0:T(8,128)(2,1)}, bf16[2,16,128,128]{3,2,1,0:T(8,128)(2,1)}, u32[]{:S(2)}, u32[]{:S(2)}) %collective-permute-start.14) | collective-permute-done | bytes 1048608 | tf_op jit(solution)/shard_map/ppermute | solution.py:20
  201.5 5.7 %collective-permute-done.11 = bf16[2,16,128,128]{3,2,1,0:T(8,128)(2,1)S(1)} collective-permute-done((bf16[2,16,128,128]{3,2,1,0:T(8,128)(2,1)}, bf16[2,16,128,128]{3,2,1,0:T(8,128)(2,1)S(1)}, u32[]{:S(2)}, u32[]{:S(2)}) %collective-permute-start.11) | collective-permute-done | bytes 1048608 | tf_op jit(solution)/shard_map/ppermute | solution.py:24
  207.1 2.6 %fusion.8 = bf16[2,16,128,128]{3,2,1,0:T(8,128)(2,1)S(1)} fusion(bf16[2,16,128,128]{3,2,1,0:T(8,128)(2,1)S(1)} %collective-permute-done.11, bf16[2,16,128,128]{3,2,1,0:T(8,128)(2,1)S(1)} %collective-permute-done.12, bf16[2,16,128,128]{3,2,1,0:T(8,128)(2,1)S(1)} %collective-permute-done.13, bf16[2,16,128,128]{3,2,1,0:T(8,128)(2,1)} %collective-permute-done.14, ...), kind=kLoop, calls=%fused_computation.14 | loop fusion | flops 6815744 | bytes 6291459 | tf_op jit(solution)/shard_map/convert_element_type | solution.py:148
  209.8 1.3 collective-permute-start.15
  211.1 0.0 copy-done.4
  211.1 0.0 copy-start.5
  211.1 1.6 copy.27
  212.7 22.6 %collective-permute-done.15 = bf16[2,16,128,128]{3,2,1,0:T(8,128)(2,1)S(1)} collective-permute-done((bf16[2,16,128,128]{3,2,1,0:T(8,128)(2,1)S(1)}, bf16[2,16,128,128]{3,2,1,0:T(8,128)(2,1)S(1)}, u32[]{:S(2)}, u32[]{:S(2)}) %collective-permute-start.15) | collective-permute-done | bytes 1048608 | tf_op jit(solution)/shard_map/ppermute | solution.py:20
  235.3 0.0 copy-done.5
  235.3 0.7 fusion.3
  236.0 0.1 slice_bitcast_fusion
  236.1 1.1 copy.23
  237.2 1.1 copy.22
  (1 shorter events, 0.0 us)
Async XLA Ops:
  2.2 56.4 %copy-start = (bf16[2,16,128,128]{3,2,1,0:T(8,128)(2,1)}, bf16[2,16,128,128]{3,2,1,0:T(8,128)(2,1)S(1)}, u32[]{:S(2)}) copy-start(bf16[2,16,128,128]{3,2,1,0:T(8,128)(2,1)S(1)} %maximum_bitcast_fusion.refs_0_) | copy-start | bytes 3145732
  2.2 27.3 %collective-permute-start = (bf16[2,16,128,128]{3,2,1,0:T(8,128)(2,1)S(1)}, bf16[2,16,128,128]{3,2,1,0:T(8,128)(2,1)}, u32[]{:S(2)}, u32[]{:S(2)}) collective-permute-start(bf16[2,16,128,128]{3,2,1,0:T(8,128)(2,1)S(1)} %maximum_bitcast_fusion.refs_0_), channel_id=1, source_target_pairs={{0,8},{2,10},{4,12},{6,14},{8,16},{10,18},{12,20},{14,22},{16,24},... | collective-permute-start | bytes 3145736 | tf_op jit(solution)/shard_map/ppermute | solution.py:20
  29.6 26.3 %collective-permute-start.1 = (bf16[2,16,128,128]{3,2,1,0:T(8,128)(2,1)}, bf16[2,16,128,128]{3,2,1,0:T(8,128)(2,1)}, u32[]{:S(2)}, u32[]{:S(2)}) collective-permute-start(bf16[2,16,128,128]{3,2,1,0:T(8,128)(2,1)} %collective-permute-done.refs_1_), channel_id=1, source_target_pairs={{0,8},{2,10},{4,12},{6,14},{8,16},{10,18},{12,20},{14,22},{16,24},... | collective-permute-start | bytes 3145736 | tf_op jit(solution)/shard_map/ppermute | solution.py:20
  35.0 72.2 %copy-start.1 = (bf16[128,32,128]{2,1,0:T(8,128)(2,1)S(1)}, bf16[128,32,128]{2,1,0:T(8,128)(2,1)}, u32[]{:S(2)}) copy-start(bf16[128,32,128]{2,1,0:T(8,128)(2,1)} %param.10) | copy-start | bytes 3145732
  58.7 23.4 %collective-permute-start.4 = (bf16[2,16,128,128]{3,2,1,0:T(8,128)(2,1)S(1)}, bf16[2,16,128,128]{3,2,1,0:T(8,128)(2,1)S(1)}, u32[]{:S(2)}, u32[]{:S(2)}) collective-permute-start(bf16[2,16,128,128]{3,2,1,0:T(8,128)(2,1)S(1)} %get-tuple-element.29), channel_id=1, source_target_pairs={{0,4},{2,6},{4,0},{6,2},{8,12},{10,14},{12,8},{14,10},{16,20},{18,... | collective-permute-start | bytes 3145736 | tf_op jit(solution)/shard_map/ppermute | solution.py:24
  82.1 27.0 %copy-start.2 = (bf16[2,16,128,128]{3,2,1,0:T(8,128)(2,1)}, bf16[2,16,128,128]{3,2,1,0:T(8,128)(2,1)S(1)}, u32[]{:S(2)}) copy-start(bf16[2,16,128,128]{3,2,1,0:T(8,128)(2,1)S(1)} %collective-permute-done.4.refs_5_) | copy-start | bytes 3145732
  82.1 24.4 %collective-permute-start.5 = (bf16[2,16,128,128]{3,2,1,0:T(8,128)(2,1)S(1)}, bf16[2,16,128,128]{3,2,1,0:T(8,128)(2,1)S(1)}, u32[]{:S(2)}, u32[]{:S(2)}) collective-permute-start(bf16[2,16,128,128]{3,2,1,0:T(8,128)(2,1)S(1)} %collective-permute-done.4.refs_5_), channel_id=1, source_target_pairs={{0,8},{2,10},{4,12},{6,14},{8,16},{10,18},{12,20},{14,22},{16,24},... | collective-permute-start | bytes 3145736 | tf_op jit(solution)/shard_map/ppermute | solution.py:20
  86.5 27.2 %collective-permute-start.2 = (bf16[2,16,128,128]{3,2,1,0:T(8,128)(2,1)}, bf16[2,16,128,128]{3,2,1,0:T(8,128)(2,1)}, u32[]{:S(2)}, u32[]{:S(2)}) collective-permute-start(bf16[2,16,128,128]{3,2,1,0:T(8,128)(2,1)} %get-tuple-element.30), channel_id=1, source_target_pairs={{0,2},{2,0},{4,6},{6,4},{8,10},{10,8},{12,14},{14,12},{16,18},{18,... | collective-permute-start | bytes 3145736 | tf_op jit(solution)/shard_map/ppermute | solution.py:24
  86.6 27.2 %collective-permute-start.3 = (bf16[2,16,128,128]{3,2,1,0:T(8,128)(2,1)}, bf16[2,16,128,128]{3,2,1,0:T(8,128)(2,1)}, u32[]{:S(2)}, u32[]{:S(2)}) collective-permute-start(bf16[2,16,128,128]{3,2,1,0:T(8,128)(2,1)} %get-tuple-element.33), channel_id=1, source_target_pairs={{0,2},{2,0},{4,6},{6,4},{8,10},{10,8},{12,14},{14,12},{16,18},{18,... | collective-permute-start | bytes 3145736 | tf_op jit(solution)/shard_map/ppermute | solution.py:24
  87.1 26.7 %collective-permute-start.6 = (bf16[2,16,128,128]{3,2,1,0:T(8,128)(2,1)S(1)}, bf16[2,16,128,128]{3,2,1,0:T(8,128)(2,1)}, u32[]{:S(2)}, u32[]{:S(2)}) collective-permute-start(bf16[2,16,128,128]{3,2,1,0:T(8,128)(2,1)S(1)} %collective-permute-done.4.refs_5_), channel_id=1, source_target_pairs={{0,2},{2,0},{4,6},{6,4},{8,10},{10,8},{12,14},{14,12},{16,18},{18,... | collective-permute-start | bytes 3145736 | tf_op jit(solution)/shard_map/ppermute | solution.py:24
  106.5 2.6 %copy-start.3 = (bf16[2,16,128,128]{3,2,1,0:T(8,128)(2,1)}, bf16[2,16,128,128]{3,2,1,0:T(8,128)(2,1)S(1)}, u32[]{:S(2)}) copy-start(bf16[2,16,128,128]{3,2,1,0:T(8,128)(2,1)S(1)} %collective-permute-done.5.refs_6_) | copy-start | bytes 3145732
  106.5 7.3 %collective-permute-start.7 = (bf16[2,16,128,128]{3,2,1,0:T(8,128)(2,1)S(1)}, bf16[2,16,128,128]{3,2,1,0:T(8,128)(2,1)}, u32[]{:S(2)}, u32[]{:S(2)}) collective-permute-start(bf16[2,16,128,128]{3,2,1,0:T(8,128)(2,1)S(1)} %collective-permute-done.5.refs_6_), channel_id=1, source_target_pairs={{0,2},{2,0},{4,6},{6,4},{8,10},{10,8},{12,14},{14,12},{16,18},{18,... | collective-permute-start | bytes 3145736 | tf_op jit(solution)/shard_map/ppermute | solution.py:24
  146.3 3.0 %collective-permute-start.9 = (bf16[2,16,128,128]{3,2,1,0:T(8,128)(2,1)}, bf16[2,16,128,128]{3,2,1,0:T(8,128)(2,1)S(1)}, u32[]{:S(2)}, u32[]{:S(2)}) collective-permute-start(bf16[2,16,128,128]{3,2,1,0:T(8,128)(2,1)} %get-tuple-element.18), channel_id=1, source_target_pairs={{0,2},{2,0},{4,6},{6,4},{8,10},{10,8},{12,14},{14,12},{16,18},{18,... | collective-permute-start | bytes 3145736 | tf_op jit(solution)/shard_map/ppermute | solution.py:24
  146.7 5.8 %collective-permute-start.13 = (bf16[2,16,128,128]{3,2,1,0:T(8,128)(2,1)}, bf16[2,16,128,128]{3,2,1,0:T(8,128)(2,1)S(1)}, u32[]{:S(2)}, u32[]{:S(2)}) collective-permute-start(bf16[2,16,128,128]{3,2,1,0:T(8,128)(2,1)} %get-tuple-element.21), channel_id=1, source_target_pairs={{0,2},{2,0},{4,6},{6,4},{8,10},{10,8},{12,14},{14,12},{16,18},{18,... | collective-permute-start | bytes 3145736 | tf_op jit(solution)/shard_map/ppermute | solution.py:24
  146.8 9.7 %collective-permute-start.8 = (bf16[2,16,128,128]{3,2,1,0:T(8,128)(2,1)}, bf16[2,16,128,128]{3,2,1,0:T(8,128)(2,1)}, u32[]{:S(2)}, u32[]{:S(2)}) collective-permute-start(bf16[2,16,128,128]{3,2,1,0:T(8,128)(2,1)} %get-tuple-element.16), channel_id=1, source_target_pairs={{0,2},{2,0},{4,6},{6,4},{8,10},{10,8},{12,14},{14,12},{16,18},{18,... | collective-permute-start | bytes 3145736 | tf_op jit(solution)/shard_map/ppermute | solution.py:24
  150.8 28.5 %collective-permute-start.10 = (bf16[2,16,128,128]{3,2,1,0:T(8,128)(2,1)S(1)}, bf16[2,16,128,128]{3,2,1,0:T(8,128)(2,1)}, u32[]{:S(2)}, u32[]{:S(2)}) collective-permute-start(bf16[2,16,128,128]{3,2,1,0:T(8,128)(2,1)S(1)} %add_convert_fusion.1), channel_id=1, source_target_pairs={{8,0},{10,2},{12,4},{14,6},{16,8},{18,10},{20,12},{22,14},{24,16},... | collective-permute-start | bytes 3145736 | tf_op jit(solution)/shard_map/ppermute | solution.py:20
  152.1 31.8 %collective-permute-start.12 = (bf16[2,16,128,128]{3,2,1,0:T(8,128)(2,1)}, bf16[2,16,128,128]{3,2,1,0:T(8,128)(2,1)S(1)}, u32[]{:S(2)}, u32[]{:S(2)}) collective-permute-start(bf16[2,16,128,128]{3,2,1,0:T(8,128)(2,1)} %get-tuple-element.19), channel_id=1, source_target_pairs={{0,2},{2,0},{4,6},{6,4},{8,10},{10,8},{12,14},{14,12},{16,18},{18,... | collective-permute-start | bytes 3145736 | tf_op jit(solution)/shard_map/ppermute | solution.py:24
  152.6 26.8 %copy-start.6 = (bf16[2,16,128,128]{3,2,1,0:T(8,128)(2,1)S(1)}, bf16[2,16,128,128]{3,2,1,0:T(8,128)(2,1)}, u32[]{:S(2)}) copy-start(bf16[2,16,128,128]{3,2,1,0:T(8,128)(2,1)} %get-tuple-element.15) | copy-start | bytes 3145732
  155.3 46.2 %collective-permute-start.14 = (bf16[2,16,128,128]{3,2,1,0:T(8,128)(2,1)}, bf16[2,16,128,128]{3,2,1,0:T(8,128)(2,1)}, u32[]{:S(2)}, u32[]{:S(2)}) collective-permute-start(bf16[2,16,128,128]{3,2,1,0:T(8,128)(2,1)} %fusion.10), channel_id=1, source_target_pairs={{8,0},{10,2},{12,4},{14,6},{16,8},{18,10},{20,12},{22,14},{24,16},... | collective-permute-start | bytes 3145736 | tf_op jit(solution)/shard_map/ppermute | solution.py:20
  182.4 24.8 %collective-permute-start.11 = (bf16[2,16,128,128]{3,2,1,0:T(8,128)(2,1)}, bf16[2,16,128,128]{3,2,1,0:T(8,128)(2,1)S(1)}, u32[]{:S(2)}, u32[]{:S(2)}) collective-permute-start(bf16[2,16,128,128]{3,2,1,0:T(8,128)(2,1)} %add_convert_fusion), channel_id=1, source_target_pairs={{0,4},{2,6},{4,0},{6,2},{8,12},{10,14},{12,8},{14,10},{16,20},{18,... | collective-permute-start | bytes 3145736 | tf_op jit(solution)/shard_map/ppermute | solution.py:24
  207.1 3.9 %copy-start.4 = (bf16[16,2,128,128]{3,2,1,0:T(8,128)(2,1)S(1)}, bf16[16,2,128,128]{3,2,1,0:T(8,128)(2,1)}, u32[]{:S(2)}) copy-start(bf16[16,2,128,128]{3,2,1,0:T(8,128)(2,1)} %get-tuple-element.13) | copy-start | bytes 3145732
  209.8 25.5 %collective-permute-start.15 = (bf16[2,16,128,128]{3,2,1,0:T(8,128)(2,1)S(1)}, bf16[2,16,128,128]{3,2,1,0:T(8,128)(2,1)S(1)}, u32[]{:S(2)}, u32[]{:S(2)}) collective-permute-start(bf16[2,16,128,128]{3,2,1,0:T(8,128)(2,1)S(1)} %fusion.8), channel_id=1, source_target_pairs={{8,0},{10,2},{12,4},{14,6},{16,8},{18,10},{20,12},{22,14},{24,16},... | collective-permute-start | bytes 3145736 | tf_op jit(solution)/shard_map/ppermute | solution.py:20
  211.1 24.2 %copy-start.5 = (bf16[2,16,128,128]{3,2,1,0:T(8,128)(2,1)S(1)}, bf16[2,16,128,128]{3,2,1,0:T(8,128)(2,1)}, u32[]{:S(2)}) copy-start(bf16[2,16,128,128]{3,2,1,0:T(8,128)(2,1)} %get-tuple-element.14) | copy-start | bytes 3145732

commit v2 on v1

v2 whole, which is shorter than its diff:
```python
import functools

import jax
import jax.numpy as jnp
from jax import lax
from jax.experimental import pallas as pl
from jax.experimental.pallas import tpu as pltpu
from jax.sharding import PartitionSpec as P

WINDOW = 1024
HOPS = 8
PLANE = 4
HEADS_PER_STEP = 2

SCALE = 168.0 ** (-0.5)


def shift(x, n, distance):
    pairs = [(i, i + distance) for i in range(n) if 0 <= i + distance < n]
    return lax.ppermute(x, "seq", pairs)


def swap(x, n, bit):
    return lax.ppermute(x, "seq", [(i, i ^ bit) for i in range(n)])


def one_way(x, n, bit, side):
    pairs = [(i, i ^ bit) for i in range(n) if (i & bit) == side]
    return lax.ppermute(x, "seq", pairs)


def _blocks_kernel(modes, has_acc, valid_ref, q_ref, do_ref, lse_ref, delta_ref, *refs):
    nb = len(modes)
    if has_acc:
        acc_ref = refs[0]
        refs = refs[1:]
    kv_refs = refs[:nb]
    dq_ref = refs[nb]
    dkv_refs = refs[nb + 1:]
    gb, grp, tok, width = q_ref.shape
    rows = grp * tok
    kk = lax.broadcasted_iota(jnp.int32, (tok, rows), 0)
    tt = lax.broadcasted_iota(jnp.int32, (tok, rows), 1) % tok
    causal = kk <= tt
    strict = kk > tt
    for g in range(gb):
        q = q_ref[g].reshape(rows, width)
        do = do_ref[g].reshape(rows, width)
        lse = lse_ref[g]
        delta = delta_ref[g]
        if has_acc:
            dq = acc_ref[g].reshape(rows, width)
        else:
            dq = jnp.zeros((rows, width), jnp.float32)
        for b, mode in enumerate(modes):
            k = kv_refs[b][0, g]
            v = kv_refs[b][1, g]
            off = jnp.where(valid_ref[b] > 0, 0.0, 1e30).astype(jnp.float32)
            s = lax.dot_general(k, q, (((1,), (1,)), ((), ())), preferred_element_type=jnp.float32)
            e = jnp.exp(s * SCALE - lse - off)
            if mode == 0:
                p = jnp.where(causal, e, 0.0)
            elif mode == 2:
                p = jnp.where(strict, e, 0.0)
            else:
                p = e
            dp = lax.dot_general(v, do, (((1,), (1,)), ((), ())), preferred_element_type=jnp.float32)
            ds = p * (dp - delta)
            pb = p.astype(jnp.bfloat16)
            dsb = ds.astype(jnp.bfloat16)
            dv = jnp.dot(pb, do, preferred_element_type=jnp.float32)
            dk = jnp.dot(dsb, q, preferred_element_type=jnp.float32) * SCALE
            dq = dq + lax.dot_general(dsb, k, (((0,), (0,)), ((), ())), preferred_element_type=jnp.float32)
            dkv_refs[b][0, g] = dk.astype(jnp.bfloat16)
            dkv_refs[b][1, g] = dv.astype(jnp.bfloat16)
        dq_ref[g] = dq.reshape(grp, tok, width)


def attend_blocks(modes, dist, idx, q4, do4, lse3, delta3, acc, kvs):
    nh, grp, tok, width = q4.shape
    gb = HEADS_PER_STEP
    nb = len(modes)
    valid = jnp.stack([(idx >= d).astype(jnp.int32) for d in dist])
    hspec = pl.BlockSpec((gb, grp, tok, width), lambda i, v: (i, 0, 0, 0))
    rspec = pl.BlockSpec((gb, 1, grp * tok), lambda i, v: (i, 0, 0))
    kvspec = pl.BlockSpec((2, gb, tok, width), lambda i, v: (0, i, 0, 0))
    accs = [] if acc is None else [acc]
    out_shape = [jax.ShapeDtypeStruct(q4.shape, jnp.float32)]
    out_shape += [jax.ShapeDtypeStruct(kv.shape, jnp.bfloat16) for kv in kvs]
    grid_spec = pltpu.PrefetchScalarGridSpec(
        num_scalar_prefetch=1,
        grid=(nh // gb,),
        in_specs=[hspec, hspec, rspec, rspec] + [hspec] * len(accs) + [kvspec] * nb,
        out_specs=[hspec] + [kvspec] * nb,
    )
    outs = pl.pallas_call(
        functools.partial(_blocks_kernel, tuple(modes), acc is not None),
        grid_spec=grid_spec,
        out_shape=out_shape,
        compiler_params=pltpu.CompilerParams(dimension_semantics=("arbitrary",)),
    )(valid, q4, do4, lse3, delta3, *accs, *kvs)
    return outs[0], list(outs[1:])


def per_device(query, normed_key_rows, value_rows, out_in, grad_out, lse):
    tok, heads_q, width = query.shape
    heads_kv = normed_key_rows.shape[1]
    groups = heads_q // heads_kv
    n = lax.axis_size("seq")
    assert HOPS == 2 * PLANE
    idx = lax.axis_index("seq")
    half = (idx % PLANE) // 2
    core = idx % 2

    q4 = query.transpose(1, 0, 2).reshape(heads_kv, groups, tok, width)
    do4 = grad_out.transpose(1, 0, 2).reshape(heads_kv, groups, tok, width)
    delta = jnp.sum(grad_out.astype(jnp.float32) * out_in.astype(jnp.float32), axis=-1)
    delta3 = delta.T.reshape(heads_kv, 1, groups * tok)
    lse3 = lse.reshape(heads_kv, 1, groups * tok)
    x0 = jnp.stack([normed_key_rows, value_rows]).transpose(0, 2, 1, 3)

    x1 = shift(x0, n, PLANE)
    ya = one_way(x0, n, 2, 0)
    cx1 = swap(x1, n, 1)
    yb = one_way(x1, n, 2, 2)
    x2 = shift(x1, n, PLANE)
    ca = one_way(x0, n, 1, 0)
    cb = one_way(x2, n, 1, 1)
    y0 = jnp.where(half == 1, ya, yb)
    d0 = swap(y0, n, 1)
    y1 = shift(y0, n, PLANE)
    cxo = jnp.where(core == 1, ca, cb)
    d1 = swap(y1, n, 1)

    run = functools.partial(attend_blocks, idx=idx, q4=q4, do4=do4, lse3=lse3, delta3=delta3)
    acc, (tx0, tx1, tcx1) = run([0, 1, 1], [0, PLANE, 3 + 2 * core], acc=None, kvs=[x0, x1, cx1])
    acc, (tx2, tcxo, ty0, td0) = run(
        [2, 1, 1, 1], [2 * PLANE, 7 - 6 * core, 2, 1 + 2 * core], acc=acc, kvs=[x2, cxo, y0, d0])
    acc, (ty1, td1) = run([1, 1], [6, 5 + 2 * core], acc=acc, kvs=[y1, d1])

    f32 = jnp.float32
    bf16 = jnp.bfloat16
    r1 = swap(tcx1, n, 1).astype(f32)
    ro = swap(tcxo, n, 1).astype(f32)
    yret0 = swap((ty0.astype(f32) + swap(td0, n, 1).astype(f32)).astype(bf16), n, 2).astype(f32)
    yret1 = swap((ty1.astype(f32) + swap(td1, n, 1).astype(f32)).astype(bf16), n, 2).astype(f32)
    zero = jnp.zeros_like(r1)
    lo = half == 0
    part2 = tx2.astype(f32) + jnp.where(core == 1, ro, zero) + jnp.where(lo, zero, yret1)
    part1 = tx1.astype(f32) + r1 + jnp.where(lo, yret1, yret0)
    part1 = part1 + shift(part2.astype(bf16), n, -PLANE).astype(f32)
    part0 = tx0.astype(f32) + jnp.where(core == 0, ro, zero) + jnp.where(lo, yret0, zero)
    part0 = part0 + shift(part1.astype(bf16), n, -PLANE).astype(f32)
    grad = part0.astype(bf16)

    grad_query = (acc * SCALE).astype(bf16).reshape(heads_q, tok, width).transpose(1, 0, 2)
    return (grad_query, grad[0].transpose(1, 0, 2), grad[1].transpose(1, 0, 2))


def solution(mesh):
    placed = (
        P(("dp", "seq"), None, None),
        P(("dp", "seq"), None, None),
        P(("dp", "seq"), None, None),
        P(("dp", "seq"), None, None),
        P(("dp", "seq"), None, None),
        P(None, ("dp", "seq")),
    )
    return jax.shard_map(
        per_device,
        mesh=mesh,
        in_specs=placed,
        out_specs=(
            P(("dp", "seq"), None, None),
            P(("dp", "seq"), None, None),
            P(("dp", "seq"), None, None),
        ),
        check_vma=False,
    )
```

time: 239 us -> 228 us (0.954)
  waiting for transfers between devices: 154 us -> 120 us
  Pallas kernels: 32.5 us -> 43.2 us
  starting transfers between devices: 24.8 us -> 34.4 us
    ppermute x6 -> x5, waiting for transfers between devices: 124 us -> 57.9 us  [shift(): return lax.ppermute(x, 'seq', pairs)]
    ppermute x0 -> x4, waiting for transfers between devices: none -> 18.5 us  [one_way(): return lax.ppermute(x, 'seq', pairs)]
    ppermute x10 -> x9, waiting for transfers between devices: 29.6 us -> 43.9 us  [swap(): return lax.ppermute(x, 'seq', [(i, i ^ bit) for i in range(n)])]
    pallas_call x1 -> x3, Pallas kernels: 32.5 us -> 43.2 us  [attend_blocks(): pl.pallas_call(functools.partial(_blocks_kernel, tuple(modes), acc is not...]
    ppermute x0 -> x4, starting transfers between devices: none -> 9.42 us  [one_way(): return lax.ppermute(x, 'seq', pairs)]
    ppermute x10 -> x9, starting transfers between devices: 5.1 us -> 5.39 us  [swap(): return lax.ppermute(x, 'seq', [(i, i ^ bit) for i in range(n)])]
    convert_element_type x5 -> x6, other arithmetic: 10.6 us -> 10.6 us  [the longest x1 2.57 us: per_device(): (ty1.astype(f32) + swap(td1, n, 1).astype(f32)).astype(bf16)]
    ppermute x6 -> x5, starting transfers between devices: 19.7 us -> 19.6 us  [shift(): return lax.ppermute(x, 'seq', pairs)]
  transfers between devices with their start and end apart: 16 -> 18, of which waited for: 9 -> 8; matrix products, arithmetic and copies ran while one was open for 7% -> 9% of each run, Pallas kernels for 0% -> 14%
where the time goes in v2:
time: 228 us; the launch traced here: 227 us
  waiting for transfers between devices  120 us (53%)
  Pallas kernels  43.2 us (19%)
  starting transfers between devices  34.4 us (15%)
  other arithmetic  16.7 us (7%)
  local copies, waits for them, and re-layouts  11.3 us (5%)
    ppermute x5, waiting for transfers between devices, shift(): return lax.ppermute(x, 'seq', pairs)  57.9 us
    ppermute x9, waiting for transfers between devices, swap(): return lax.ppermute(x, 'seq', [(i, i ^ bit) for i in range(n)])  43.9 us
    pallas_call x3, Pallas kernels, attend_blocks(): pl.pallas_call(functools.partial(_blocks_kernel, tuple(modes), acc is not...  43.2 us
    ppermute x5, starting transfers between devices, shift(): return lax.ppermute(x, 'seq', pairs)  19.6 us
    ppermute x4, waiting for transfers between devices, one_way(): return lax.ppermute(x, 'seq', pairs)  18.5 us
    ppermute x4, starting transfers between devices, one_way(): return lax.ppermute(x, 'seq', pairs)  9.42 us
    ppermute x9, starting transfers between devices, swap(): return lax.ppermute(x, 'seq', [(i, i ^ bit) for i in range(n)])  5.39 us
  transfers between devices with their start and end apart: 18, of which 8 were waited for; matrix products, arithmetic and copies ran while one was open for 9% of the time, Pallas kernels for 14%

profile of v2, /device:TPU:0, one launch (start us, length us, event | category | flops | bytes accessed | tf_op | source)
XLA Modules:
  0.0 226.8 jit_solution(14762777004602700358)
XLA Ops:
  0.6 1.5 copy_bitcast_fusion.1
  2.1 0.1 maximum_bitcast_fusion.refs_0_
  2.2 5.9 %collective-permute-start = (bf16[2,16,128,128]{3,2,1,0:T(8,128)(2,1)S(1)}, bf16[2,16,128,128]{3,2,1,0:T(8,128)(2,1)}, u32[]{:S(2)}, u32[]{:S(2)}) collective-permute-start(bf16[2,16,128,128]{3,2,1,0:T(8,128)(2,1)S(1)} %maximum_bitcast_fusion.refs_0_), channel_id=1, source_target_pairs={{0,8},{2,10},{4,12},{6,14},{8,16},{10,18},{12,20},{14,22},{16,24},... | collective-permute-start | bytes 3145736 | tf_op jit(solution)/shard_map/ppermute | solution.py:20
  8.1 3.5 %collective-permute-start.5 = (bf16[2,16,128,128]{3,2,1,0:T(8,128)(2,1)S(1)}, bf16[2,16,128,128]{3,2,1,0:T(8,128)(2,1)S(1)}, u32[]{:S(2)}, u32[]{:S(2)}) collective-permute-start(bf16[2,16,128,128]{3,2,1,0:T(8,128)(2,1)S(1)} %maximum_bitcast_fusion.refs_0_), channel_id=1, source_target_pairs={{0,4},{2,6},{8,12},{10,14},{16,20},{18,22},{24,28},{26,30},{1,5},{... | collective-permute-start | bytes 3145736 | tf_op jit(solution)/shard_map/ppermute | solution.py:29
  11.6 18.0 %collective-permute-done.refs_1_ = bf16[2,16,128,128]{3,2,1,0:T(8,128)(2,1)} collective-permute-done((bf16[2,16,128,128]{3,2,1,0:T(8,128)(2,1)S(1)}, bf16[2,16,128,128]{3,2,1,0:T(8,128)(2,1)}, u32[]{:S(2)}, u32[]{:S(2)}) %collective-permute-start) | collective-permute-done | bytes 1048608 | tf_op jit(solution)/shard_map/ppermute | solution.py:20
  29.6 1.3 collective-permute-start.6
  30.9 5.5 %collective-permute-start.2 = (bf16[2,16,128,128]{3,2,1,0:T(8,128)(2,1)}, bf16[2,16,128,128]{3,2,1,0:T(8,128)(2,1)}, u32[]{:S(2)}, u32[]{:S(2)}) collective-permute-start(bf16[2,16,128,128]{3,2,1,0:T(8,128)(2,1)} %collective-permute-done.refs_1_), channel_id=1, source_target_pairs={{0,8},{2,10},{4,12},{6,14},{8,16},{10,18},{12,20},{14,22},{16,24},... | collective-permute-start | bytes 3145736 | tf_op jit(solution)/shard_map/ppermute | solution.py:20
  36.3 0.0 collective-permute-done.5
  36.4 1.0 copy-done.6
  37.3 18.5 %collective-permute-done.6 = bf16[2,16,128,128]{3,2,1,0:T(8,128)(2,1)} collective-permute-done((bf16[2,16,128,128]{3,2,1,0:T(8,128)(2,1)}, bf16[2,16,128,128]{3,2,1,0:T(8,128)(2,1)}, u32[]{:S(2)}, u32[]{:S(2)}) %collective-permute-start.6) | collective-permute-done | bytes 1048608 | tf_op jit(solution)/shard_map/ppermute | solution.py:29
  55.8 1.3 broadcast_select_fusion.refs_3_
  57.1 5.5 %collective-permute-start.8 = (bf16[2,16,128,128]{3,2,1,0:T(8,128)(2,1)S(1)}, bf16[2,16,128,128]{3,2,1,0:T(8,128)(2,1)}, u32[]{:S(2)}, u32[]{:S(2)}) collective-permute-start(bf16[2,16,128,128]{3,2,1,0:T(8,128)(2,1)S(1)} %broadcast_select_fusion.refs_3_), channel_id=1, source_target_pairs={{0,8},{2,10},{4,12},{6,14},{8,16},{10,18},{12,20},{14,22},{16,24},... | collective-permute-start | bytes 3145736 | tf_op jit(solution)/shard_map/ppermute | solution.py:20
  62.6 0.0 collective-permute-start.1
  62.7 3.4 %collective-permute-start.3 = (bf16[2,16,128,128]{3,2,1,0:T(8,128)(2,1)S(1)}, bf16[2,16,128,128]{3,2,1,0:T(8,128)(2,1)}, u32[]{:S(2)}, u32[]{:S(2)}) collective-permute-start(bf16[2,16,128,128]{3,2,1,0:T(8,128)(2,1)S(1)} %maximum_bitcast_fusion.refs_0_), channel_id=1, source_target_pairs={{0,2},{4,6},{8,10},{12,14},{16,18},{20,22},{24,26},{28,30},{1,3},{... | collective-permute-start | bytes 3145736 | tf_op jit(solution)/shard_map/ppermute | solution.py:29
  66.0 0.0 collective-permute-done.2.refs_1_
  66.0 1.3 collective-permute-start.4
  67.3 2.1 collective-permute-start.7
  69.5 12.8 %collective-permute-done.8.refs_1_ = bf16[2,16,128,128]{3,2,1,0:T(8,128)(2,1)} collective-permute-done((bf16[2,16,128,128]{3,2,1,0:T(8,128)(2,1)S(1)}, bf16[2,16,128,128]{3,2,1,0:T(8,128)(2,1)}, u32[]{:S(2)}, u32[]{:S(2)}) %collective-permute-start.8) | collective-permute-done | bytes 1048608 | tf_op jit(solution)/shard_map/ppermute | solution.py:20
  82.2 0.0 collective-permute-start.9
  82.2 2.7 %copy.16 = bf16[32,128,128]{2,1,0:T(8,128)(2,1)} copy(bf16[32,128,128]{2,0,1:T(8,128)(2,1)} %bitcast.42) | data formatting | bytes 2097152 | tf_op jit(solution)/shard_map/transpose | solution.py:115
  84.9 0.0 copy-done.1
  84.9 1.5 copy.17
  86.4 0.0 copy-done
  86.4 0.6 multiply_reduce_fusion
  87.1 0.7 copy.18
  87.7 0.6 add_convert_fusion.2.valid_ref
  88.4 0.6 add_convert_fusion.4.valid_ref
  88.9 0.6 add_convert_fusion.3.valid_ref
  89.5 0.0 collective-permute-done.1.refs_2_
  89.5 14.2 %shard_map.85 = (f32[16,2,128,128]{3,2,1,0:T(8,128)}, bf16[2,16,128,128]{3,2,1,0:T(8,128)(2,1)}, bf16[2,16,128,128]{3,2,1,0:T(8,128)(2,1)}, bf16[2,16,128,128]{3,2,1,0:T(8,128)(2,1)}) custom-call(s32[3]{0:T(128)} %add_convert_fusion.4.valid_ref, bf16[16,2,128,128]{3,2,1,0:T(8,128)(2,1)} %bitcast.34, bf16[16,2,128,128]{3,2,1,0:T(8,128)(2,1)} %bitcast.37, ...), custom_call_target="tpu_custom_call" | custom-call | tf_op jit(solution)/shard_map/pallas_call | solution.py:96
  103.7 0.0 collective-permute-done.3
  103.7 0.0 collective-permute-done.4
  103.7 2.3 %broadcast_select_fusion.1.refs_2_ = bf16[2,16,128,128]{3,2,1,0:T(8,128)(2,1)} fusion(bf16[2,16,128,128]{3,2,1,0:T(8,128)(2,1)} %collective-permute-done.3, bf16[2,16,128,128]{3,2,1,0:T(8,128)(2,1)} %collective-permute-done.4, pred[]{:T(512)S(6)} %eq.16), kind=kLoop, calls=%fused_computation.22 | loop fusion | flops 524288 | bytes 3145729 | tf_op jit(solution)/shard_map/jit(_where)/select_n | solution.py:132
  106.0 0.0 collective-permute-done.7.refs_4_
  106.0 17.2 %shard_map.86 = (f32[16,2,128,128]{3,2,1,0:T(8,128)}, bf16[2,16,128,128]{3,2,1,0:T(8,128)(2,1)}, bf16[2,16,128,128]{3,2,1,0:T(8,128)(2,1)}, bf16[2,16,128,128]{3,2,1,0:T(8,128)(2,1)}, bf16[2,16,128,128]{3,2,1,0:T(8,128)(2,1)}) custom-call(s32[4]{0:T(128)} %add_convert_fusion.3.valid_ref, bf16[16,2,128,128]{3,2,1,0:T(8,128)(2,1)} %bitcast.35, ...), custom_call_target="tpu_custom_call" | custom-call | tf_op jit(solution)/shard_map/pallas_call | solution.py:96
  123.2 0.0 collective-permute-done.9.refs_2_
  123.2 11.9 %shard_map.87 = (f32[16,2,128,128]{3,2,1,0:T(8,128)}, bf16[2,16,128,128]{3,2,1,0:T(8,128)(2,1)}, bf16[2,16,128,128]{3,2,1,0:T(8,128)(2,1)}) custom-call(s32[2]{0:T(128)} %add_convert_fusion.2.valid_ref, bf16[16,2,128,128]{3,2,1,0:T(8,128)(2,1)} %bitcast.36, bf16[16,2,128,128]{3,2,1,0:T(8,128)(2,1)} %bitcast.39, f32[16,1,256]{2,1,0:T(1,128)} %bitcast.50, ...), custom_call_target="tpu_custom_call" | custom-call | tf_op jit(solution)/shard_map/pallas_call | solution.py:96
  135.1 0.6 collective-permute-start.14
  135.7 0.1 collective-permute-start.11
  135.8 0.4 collective-permute-start.10
  136.2 2.7 %collective-permute-done.14 = bf16[2,16,128,128]{3,2,1,0:T(8,128)(2,1)S(1)} collective-permute-done((bf16[2,16,128,128]{3,2,1,0:T(8,128)(2,1)}, bf16[2,16,128,128]{3,2,1,0:T(8,128)(2,1)S(1)}, u32[]{:S(2)}, u32[]{:S(2)}) %collective-permute-start.14) | collective-permute-done | bytes 1048608 | tf_op jit(solution)/shard_map/ppermute | solution.py:24
  138.9 2.6 %add_convert_fusion = bf16[2,16,128,128]{3,2,1,0:T(8,128)(2,1)} fusion(bf16[2,16,128,128]{3,2,1,0:T(8,128)(2,1)S(1)} %collective-permute-done.14, bf16[2,16,128,128]{3,2,1,0:T(8,128)(2,1)} %get-tuple-element.24), kind=kLoop, calls=%fused_computation.15 | loop fusion | flops 2097152 | bytes 3145728 | tf_op jit(solution)/shard_map/convert_element_type | solution.py:146
  141.5 0.7 collective-permute-start.15
  142.2 0.1 collective-permute-start.13
  142.2 0.0 collective-permute-done.11
  142.2 1.6 add_convert_fusion.1
  143.8 1.4 collective-permute-start.12
  145.3 0.0 collective-permute-done.10
  145.3 22.4 %collective-permute-done.15 = bf16[2,16,128,128]{3,2,1,0:T(8,128)(2,1)S(1)} collective-permute-done((bf16[2,16,128,128]{3,2,1,0:T(8,128)(2,1)}, bf16[2,16,128,128]{3,2,1,0:T(8,128)(2,1)S(1)}, u32[]{:S(2)}, u32[]{:S(2)}) %collective-permute-start.15) | collective-permute-done | bytes 1048608 | tf_op jit(solution)/shard_map/ppermute | solution.py:24
  167.7 1.9 fusion.6
  169.5 1.3 collective-permute-start.16
  170.8 0.0 collective-permute-done.13
  170.9 18.7 %collective-permute-done.12 = bf16[2,16,128,128]{3,2,1,0:T(8,128)(2,1)S(1)} collective-permute-done((bf16[2,16,128,128]{3,2,1,0:T(8,128)(2,1)S(1)}, bf16[2,16,128,128]{3,2,1,0:T(8,128)(2,1)S(1)}, u32[]{:S(2)}, u32[]{:S(2)}) %collective-permute-start.12) | collective-permute-done | bytes 1048608 | tf_op jit(solution)/shard_map/ppermute | solution.py:24
  189.6 6.8 %collective-permute-done.16 = bf16[2,16,128,128]{3,2,1,0:T(8,128)(2,1)S(1)} collective-permute-done((bf16[2,16,128,128]{3,2,1,0:T(8,128)(2,1)S(1)}, bf16[2,16,128,128]{3,2,1,0:T(8,128)(2,1)S(1)}, u32[]{:S(2)}, u32[]{:S(2)}) %collective-permute-start.16) | collective-permute-done | bytes 1048608 | tf_op jit(solution)/shard_map/ppermute | solution.py:20
  196.4 0.0 copy-done.3
  196.4 1.9 fusion.9
  198.2 1.5 collective-permute-start.17
  199.7 2.0 multiply_convert_fusion
  201.7 1.6 copy.27
  203.3 20.4 %collective-permute-done.17 = bf16[2,16,128,128]{3,2,1,0:T(8,128)(2,1)S(1)} collective-permute-done((bf16[2,16,128,128]{3,2,1,0:T(8,128)(2,1)}, bf16[2,16,128,128]{3,2,1,0:T(8,128)(2,1)S(1)}, u32[]{:S(2)}, u32[]{:S(2)}) %collective-permute-start.17) | collective-permute-done | bytes 1048608 | tf_op jit(solution)/shard_map/ppermute | solution.py:20
  223.7 0.7 fusion.3
  224.5 0.1 slice_bitcast_fusion
  224.5 1.1 copy.22
  225.7 1.1 copy.23
  (12 shorter events, 0.0 us)
Async XLA Ops:
  2.2 82.7 %copy-start.2 = (bf16[2,16,128,128]{3,2,1,0:T(8,128)(2,1)}, bf16[2,16,128,128]{3,2,1,0:T(8,128)(2,1)S(1)}, u32[]{:S(2)}) copy-start(bf16[2,16,128,128]{3,2,1,0:T(8,128)(2,1)S(1)} %maximum_bitcast_fusion.refs_0_) | copy-start | bytes 3145732
  2.2 27.3 %collective-permute-start = (bf16[2,16,128,128]{3,2,1,0:T(8,128)(2,1)S(1)}, bf16[2,16,128,128]{3,2,1,0:T(8,128)(2,1)}, u32[]{:S(2)}, u32[]{:S(2)}) collective-permute-start(bf16[2,16,128,128]{3,2,1,0:T(8,128)(2,1)S(1)} %maximum_bitcast_fusion.refs_0_), channel_id=1, source_target_pairs={{0,8},{2,10},{4,12},{6,14},{8,16},{10,18},{12,20},{14,22},{16,24},... | collective-permute-start | bytes 3145736 | tf_op jit(solution)/shard_map/ppermute | solution.py:20
  8.1 28.2 %collective-permute-start.5 = (bf16[2,16,128,128]{3,2,1,0:T(8,128)(2,1)S(1)}, bf16[2,16,128,128]{3,2,1,0:T(8,128)(2,1)S(1)}, u32[]{:S(2)}, u32[]{:S(2)}) collective-permute-start(bf16[2,16,128,128]{3,2,1,0:T(8,128)(2,1)S(1)} %maximum_bitcast_fusion.refs_0_), channel_id=1, source_target_pairs={{0,4},{2,6},{8,12},{10,14},{16,20},{18,22},{24,28},{26,30},{1,5},{... | collective-permute-start | bytes 3145736 | tf_op jit(solution)/shard_map/ppermute | solution.py:29
  29.6 26.2 %collective-permute-start.6 = (bf16[2,16,128,128]{3,2,1,0:T(8,128)(2,1)}, bf16[2,16,128,128]{3,2,1,0:T(8,128)(2,1)}, u32[]{:S(2)}, u32[]{:S(2)}) collective-permute-start(bf16[2,16,128,128]{3,2,1,0:T(8,128)(2,1)} %collective-permute-done.refs_1_), channel_id=1, source_target_pairs={{4,0},{6,2},{12,8},{14,10},{20,16},{22,18},{28,24},{30,26},{5,1},{... | collective-permute-start | bytes 3145736 | tf_op jit(solution)/shard_map/ppermute | solution.py:29
  30.9 35.2 %collective-permute-start.2 = (bf16[2,16,128,128]{3,2,1,0:T(8,128)(2,1)}, bf16[2,16,128,128]{3,2,1,0:T(8,128)(2,1)}, u32[]{:S(2)}, u32[]{:S(2)}) collective-permute-start(bf16[2,16,128,128]{3,2,1,0:T(8,128)(2,1)} %collective-permute-done.refs_1_), channel_id=1, source_target_pairs={{0,8},{2,10},{4,12},{6,14},{8,16},{10,18},{12,20},{14,22},{16,24},... | collective-permute-start | bytes 3145736 | tf_op jit(solution)/shard_map/ppermute | solution.py:20
  36.3 48.6 %copy-start.1 = (bf16[128,32,128]{2,1,0:T(8,128)(2,1)S(1)}, bf16[128,32,128]{2,1,0:T(8,128)(2,1)}, u32[]{:S(2)}) copy-start(bf16[128,32,128]{2,1,0:T(8,128)(2,1)} %param.10) | copy-start | bytes 3145732
  36.3 1.0 copy-start.6
  57.1 29.3 %copy-start = (bf16[2,16,128,128]{3,2,1,0:T(8,128)(2,1)}, bf16[2,16,128,128]{3,2,1,0:T(8,128)(2,1)S(1)}, u32[]{:S(2)}) copy-start(bf16[2,16,128,128]{3,2,1,0:T(8,128)(2,1)S(1)} %broadcast_select_fusion.refs_3_) | copy-start | bytes 3145732
  57.1 25.1 %collective-permute-start.8 = (bf16[2,16,128,128]{3,2,1,0:T(8,128)(2,1)S(1)}, bf16[2,16,128,128]{3,2,1,0:T(8,128)(2,1)}, u32[]{:S(2)}, u32[]{:S(2)}) collective-permute-start(bf16[2,16,128,128]{3,2,1,0:T(8,128)(2,1)S(1)} %broadcast_select_fusion.refs_3_), channel_id=1, source_target_pairs={{0,8},{2,10},{4,12},{6,14},{8,16},{10,18},{12,20},{14,22},{16,24},... | collective-permute-start | bytes 3145736 | tf_op jit(solution)/shard_map/ppermute | solution.py:20
  62.6 26.9 %collective-permute-start.1 = (bf16[2,16,128,128]{3,2,1,0:T(8,128)(2,1)}, bf16[2,16,128,128]{3,2,1,0:T(8,128)(2,1)}, u32[]{:S(2)}, u32[]{:S(2)}) collective-permute-start(bf16[2,16,128,128]{3,2,1,0:T(8,128)(2,1)} %collective-permute-done.refs_1_), channel_id=1, source_target_pairs={{0,2},{2,0},{4,6},{6,4},{8,10},{10,8},{12,14},{14,12},{16,18},{18,... | collective-permute-start | bytes 3145736 | tf_op jit(solution)/shard_map/ppermute | solution.py:24
  62.7 41.1 %collective-permute-start.3 = (bf16[2,16,128,128]{3,2,1,0:T(8,128)(2,1)S(1)}, bf16[2,16,128,128]{3,2,1,0:T(8,128)(2,1)}, u32[]{:S(2)}, u32[]{:S(2)}) collective-permute-start(bf16[2,16,128,128]{3,2,1,0:T(8,128)(2,1)S(1)} %maximum_bitcast_fusion.refs_0_), channel_id=1, source_target_pairs={{0,2},{4,6},{8,10},{12,14},{16,18},{20,22},{24,26},{28,30},{1,3},{... | collective-permute-start | bytes 3145736 | tf_op jit(solution)/shard_map/ppermute | solution.py:29
  66.0 37.7 %collective-permute-start.4 = (bf16[2,16,128,128]{3,2,1,0:T(8,128)(2,1)}, bf16[2,16,128,128]{3,2,1,0:T(8,128)(2,1)}, u32[]{:S(2)}, u32[]{:S(2)}) collective-permute-start(bf16[2,16,128,128]{3,2,1,0:T(8,128)(2,1)} %collective-permute-done.2.refs_1_), channel_id=1, source_target_pairs={{2,0},{6,4},{10,8},{14,12},{18,16},{22,20},{26,24},{30,28},{3,1},{... | collective-permute-start | bytes 3145736 | tf_op jit(solution)/shard_map/ppermute | solution.py:29
  67.3 38.7 %collective-permute-start.7 = (bf16[2,16,128,128]{3,2,1,0:T(8,128)(2,1)S(1)}, bf16[2,16,128,128]{3,2,1,0:T(8,128)(2,1)}, u32[]{:S(2)}, u32[]{:S(2)}) collective-permute-start(bf16[2,16,128,128]{3,2,1,0:T(8,128)(2,1)S(1)} %broadcast_select_fusion.refs_3_), channel_id=1, source_target_pairs={{0,2},{2,0},{4,6},{6,4},{8,10},{10,8},{12,14},{14,12},{16,18},{18,... | collective-permute-start | bytes 3145736 | tf_op jit(solution)/shard_map/ppermute | solution.py:24
  82.2 41.0 %collective-permute-start.9 = (bf16[2,16,128,128]{3,2,1,0:T(8,128)(2,1)}, bf16[2,16,128,128]{3,2,1,0:T(8,128)(2,1)}, u32[]{:S(2)}, u32[]{:S(2)}) collective-permute-start(bf16[2,16,128,128]{3,2,1,0:T(8,128)(2,1)} %collective-permute-done.8.refs_1_), channel_id=1, source_target_pairs={{0,2},{2,0},{4,6},{6,4},{8,10},{10,8},{12,14},{14,12},{16,18},{18,... | collective-permute-start | bytes 3145736 | tf_op jit(solution)/shard_map/ppermute | solution.py:24
  82.2 4.2 %copy-start.5 = (bf16[128,32,128]{2,1,0:T(8,128)(2,1)S(1)}, bf16[128,32,128]{2,1,0:T(8,128)(2,1)}, u32[]{:S(2)}) copy-start(bf16[128,32,128]{2,1,0:T(8,128)(2,1)} %param.9) | copy-start | bytes 3145732
  135.1 7.1 %copy-start.4 = (bf16[2,16,128,128]{3,2,1,0:T(8,128)(2,1)S(1)}, bf16[2,16,128,128]{3,2,1,0:T(8,128)(2,1)}, u32[]{:S(2)}) copy-start(bf16[2,16,128,128]{3,2,1,0:T(8,128)(2,1)} %get-tuple-element.20) | copy-start | bytes 3145732
  135.1 3.8 %collective-permute-start.14 = (bf16[2,16,128,128]{3,2,1,0:T(8,128)(2,1)}, bf16[2,16,128,128]{3,2,1,0:T(8,128)(2,1)S(1)}, u32[]{:S(2)}, u32[]{:S(2)}) collective-permute-start(bf16[2,16,128,128]{3,2,1,0:T(8,128)(2,1)} %get-tuple-element.25), channel_id=1, source_target_pairs={{0,2},{2,0},{4,6},{6,4},{8,10},{10,8},{12,14},{14,12},{16,18},{18,... | collective-permute-start | bytes 3145736 | tf_op jit(solution)/shard_map/ppermute | solution.py:24
  135.7 6.6 %collective-permute-start.11 = (bf16[2,16,128,128]{3,2,1,0:T(8,128)(2,1)}, bf16[2,16,128,128]{3,2,1,0:T(8,128)(2,1)}, u32[]{:S(2)}, u32[]{:S(2)}) collective-permute-start(bf16[2,16,128,128]{3,2,1,0:T(8,128)(2,1)} %get-tuple-element.21), channel_id=1, source_target_pairs={{0,2},{2,0},{4,6},{6,4},{8,10},{10,8},{12,14},{14,12},{16,18},{18,... | collective-permute-start | bytes 3145736 | tf_op jit(solution)/shard_map/ppermute | solution.py:24
  135.8 9.5 %collective-permute-start.10 = (bf16[2,16,128,128]{3,2,1,0:T(8,128)(2,1)}, bf16[2,16,128,128]{3,2,1,0:T(8,128)(2,1)S(1)}, u32[]{:S(2)}, u32[]{:S(2)}) collective-permute-start(bf16[2,16,128,128]{3,2,1,0:T(8,128)(2,1)} %get-tuple-element.19), channel_id=1, source_target_pairs={{0,2},{2,0},{4,6},{6,4},{8,10},{10,8},{12,14},{14,12},{16,18},{18,... | collective-permute-start | bytes 3145736 | tf_op jit(solution)/shard_map/ppermute | solution.py:24
  141.5 26.2 %collective-permute-start.15 = (bf16[2,16,128,128]{3,2,1,0:T(8,128)(2,1)}, bf16[2,16,128,128]{3,2,1,0:T(8,128)(2,1)S(1)}, u32[]{:S(2)}, u32[]{:S(2)}) collective-permute-start(bf16[2,16,128,128]{3,2,1,0:T(8,128)(2,1)} %add_convert_fusion), channel_id=1, source_target_pairs={{0,4},{2,6},{4,0},{6,2},{8,12},{10,14},{12,8},{14,10},{16,20},{18,... | collective-permute-start | bytes 3145736 | tf_op jit(solution)/shard_map/ppermute | solution.py:24
  142.2 28.7 %collective-permute-start.13 = (bf16[2,16,128,128]{3,2,1,0:T(8,128)(2,1)}, bf16[2,16,128,128]{3,2,1,0:T(8,128)(2,1)S(1)}, u32[]{:S(2)}, u32[]{:S(2)}) collective-permute-start(bf16[2,16,128,128]{3,2,1,0:T(8,128)(2,1)} %get-tuple-element.23), channel_id=1, source_target_pairs={{0,2},{2,0},{4,6},{6,4},{8,10},{10,8},{12,14},{14,12},{16,18},{18,... | collective-permute-start | bytes 3145736 | tf_op jit(solution)/shard_map/ppermute | solution.py:24
  143.8 45.7 %collective-permute-start.12 = (bf16[2,16,128,128]{3,2,1,0:T(8,128)(2,1)S(1)}, bf16[2,16,128,128]{3,2,1,0:T(8,128)(2,1)S(1)}, u32[]{:S(2)}, u32[]{:S(2)}) collective-permute-start(bf16[2,16,128,128]{3,2,1,0:T(8,128)(2,1)S(1)} %add_convert_fusion.1), channel_id=1, source_target_pairs={{0,4},{2,6},{4,0},{6,2},{8,12},{10,14},{12,8},{14,10},{16,20},{18,... | collective-permute-start | bytes 3145736 | tf_op jit(solution)/shard_map/ppermute | solution.py:24
  167.7 28.7 %copy-start.3 = (bf16[2,16,128,128]{3,2,1,0:T(8,128)(2,1)S(1)}, bf16[2,16,128,128]{3,2,1,0:T(8,128)(2,1)}, u32[]{:S(2)}) copy-start(bf16[2,16,128,128]{3,2,1,0:T(8,128)(2,1)} %get-tuple-element.22) | copy-start | bytes 3145732
  169.5 26.8 %collective-permute-start.16 = (bf16[2,16,128,128]{3,2,1,0:T(8,128)(2,1)S(1)}, bf16[2,16,128,128]{3,2,1,0:T(8,128)(2,1)S(1)}, u32[]{:S(2)}, u32[]{:S(2)}) collective-permute-start(bf16[2,16,128,128]{3,2,1,0:T(8,128)(2,1)S(1)} %fusion.6), channel_id=1, source_target_pairs={{8,0},{10,2},{12,4},{14,6},{16,8},{18,10},{20,12},{22,14},{24,16},... | collective-permute-start | bytes 3145736 | tf_op jit(solution)/shard_map/ppermute | solution.py:20
  198.2 25.5 %collective-permute-start.17 = (bf16[2,16,128,128]{3,2,1,0:T(8,128)(2,1)}, bf16[2,16,128,128]{3,2,1,0:T(8,128)(2,1)S(1)}, u32[]{:S(2)}, u32[]{:S(2)}) collective-permute-start(bf16[2,16,128,128]{3,2,1,0:T(8,128)(2,1)} %fusion.9), channel_id=1, source_target_pairs={{8,0},{10,2},{12,4},{14,6},{16,8},{18,10},{20,12},{22,14},{24,16},... | collective-permute-start | bytes 3145736 | tf_op jit(solution)/shard_map/ppermute | solution.py:20
  199.7 24.0 %copy-start.7 = (bf16[2,16,128,128]{3,2,1,0:T(8,128)(2,1)S(1)}, bf16[2,16,128,128]{3,2,1,0:T(8,128)(2,1)}, u32[]{:S(2)}) copy-start(bf16[2,16,128,128]{3,2,1,0:T(8,128)(2,1)} %get-tuple-element.18) | copy-start | bytes 3145732

commit v3 on v2

--- a/solution.py
+++ b/solution.py
@@ -93,10 +93,17 @@
         in_specs=[hspec, hspec, rspec, rspec] + [hspec] * len(accs) + [kvspec] * nb,
         out_specs=[hspec] + [kvspec] * nb,
     )
+    scores = nh * grp * tok * tok * nb
+    cost = pl.CostEstimate(
+        flops=10 * scores * width,
+        transcendentals=scores,
+        bytes_accessed=(2 + 2 * len(accs)) * q4.size * 2 + 2 * sum(kv.size for kv in kvs) * 2,
+    )
     outs = pl.pallas_call(
         functools.partial(_blocks_kernel, tuple(modes), acc is not None),
         grid_spec=grid_spec,
         out_shape=out_shape,
+        cost_estimate=cost,
         compiler_params=pltpu.CompilerParams(dimension_semantics=("arbitrary",)),
     )(valid, q4, do4, lse3, delta3, *accs, *kvs)
     return outs[0], list(outs[1:])
@@ -126,10 +133,12 @@
     x2 = shift(x1, n, PLANE)
     ca = one_way(x0, n, 1, 0)
     cb = one_way(x2, n, 1, 1)
+    yc = one_way(x1, n, 2, 0)
+    yd = one_way(x2, n, 2, 2)
     y0 = jnp.where(half == 1, ya, yb)
     d0 = swap(y0, n, 1)
-    y1 = shift(y0, n, PLANE)
     cxo = jnp.where(core == 1, ca, cb)
+    y1 = jnp.where(half == 1, yc, yd)
     d1 = swap(y1, n, 1)
 
     run = functools.partial(attend_blocks, idx=idx, q4=q4, do4=do4, lse3=lse3, delta3=delta3)

time: 228 us -> 229 us (level)
  other arithmetic: 16.7 us -> 19.3 us
    ppermute x4 -> x6, starting transfers between devices: 9.42 us -> 17.5 us  [one_way(): return lax.ppermute(x, 'seq', pairs)]
    ppermute x5 -> x4, starting transfers between devices: 19.6 us -> 14.3 us  [shift(): return lax.ppermute(x, 'seq', pairs)]
    ppermute x9, starting transfers between devices: 5.39 us -> 2.99 us  [swap(): return lax.ppermute(x, 'seq', [(i, i ^ bit) for i in range(n)])]
    ppermute x5 -> x4, waiting for transfers between devices: 57.9 us -> 56 us  [shift(): return lax.ppermute(x, 'seq', pairs)]
    ppermute x4 -> x6, waiting for transfers between devices: 18.5 us -> 19.8 us  [one_way(): return lax.ppermute(x, 'seq', pairs)]
  transfers between devices with their start and end apart: 18 -> 19, of which waited for: 8 -> 12; matrix products, arithmetic and copies ran while one was open for 9% -> 10% of each run, Pallas kernels for 14% -> 14%
where the time goes in v3:
time: 229 us; the launch traced here: 228 us
  waiting for transfers between devices  119 us (52%)
  Pallas kernels  43.4 us (19%)
  starting transfers between devices  34.7 us (15%)
  other arithmetic  19.3 us (8%)
  local copies, waits for them, and re-layouts  10.1 us (4%)
    ppermute x4, waiting for transfers between devices, shift(): return lax.ppermute(x, 'seq', pairs)  56 us
    ppermute x9, waiting for transfers between devices, swap(): return lax.ppermute(x, 'seq', [(i, i ^ bit) for i in range(n)])  43.4 us
    pallas_call x3, Pallas kernels, attend_blocks(): pl.pallas_call(functools.partial(_blocks_kernel, tuple(modes), acc is not...  43.4 us
    ppermute x6, waiting for transfers between devices, one_way(): return lax.ppermute(x, 'seq', pairs)  19.8 us
    ppermute x6, starting transfers between devices, one_way(): return lax.ppermute(x, 'seq', pairs)  17.5 us
    ppermute x4, starting transfers between devices, shift(): return lax.ppermute(x, 'seq', pairs)  14.3 us
  transfers between devices with their start and end apart: 19, of which 12 were waited for; matrix products, arithmetic and copies ran while one was open for 10% of the time, Pallas kernels for 14%

profile of v3, /device:TPU:0, one launch (start us, length us, event | category | flops | bytes accessed | tf_op | source)
XLA Modules:
  0.0 227.6 jit_solution(14393248732620525899)
XLA Ops:
  0.7 1.6 copy_bitcast_fusion.1
  2.3 0.0 copy-start.6
  2.3 0.1 maximum_bitcast_fusion.refs_0_
  2.4 6.0 %collective-permute-start = (bf16[2,16,128,128]{3,2,1,0:T(8,128)(2,1)S(1)}, bf16[2,16,128,128]{3,2,1,0:T(8,128)(2,1)}, u32[]{:S(2)}, u32[]{:S(2)}) collective-permute-start(bf16[2,16,128,128]{3,2,1,0:T(8,128)(2,1)S(1)} %maximum_bitcast_fusion.refs_0_), channel_id=1, source_target_pairs={{0,8},{2,10},{4,12},{6,14},{8,16},{10,18},{12,20},{14,22},{16,24},... | collective-permute-start | bytes 3145736 | tf_op jit(solution)/shard_map/ppermute | solution.py:20
  8.4 21.4 %collective-permute-done.refs_1_ = bf16[2,16,128,128]{3,2,1,0:T(8,128)(2,1)} collective-permute-done((bf16[2,16,128,128]{3,2,1,0:T(8,128)(2,1)S(1)}, bf16[2,16,128,128]{3,2,1,0:T(8,128)(2,1)}, u32[]{:S(2)}, u32[]{:S(2)}) %collective-permute-start) | collective-permute-done | bytes 1048608 | tf_op jit(solution)/shard_map/ppermute | solution.py:20
  29.9 5.5 %collective-permute-start.2 = (bf16[2,16,128,128]{3,2,1,0:T(8,128)(2,1)}, bf16[2,16,128,128]{3,2,1,0:T(8,128)(2,1)}, u32[]{:S(2)}, u32[]{:S(2)}) collective-permute-start(bf16[2,16,128,128]{3,2,1,0:T(8,128)(2,1)} %collective-permute-done.refs_1_), channel_id=1, source_target_pairs={{0,8},{2,10},{4,12},{6,14},{8,16},{10,18},{12,20},{14,22},{16,24},... | collective-permute-start | bytes 3145736 | tf_op jit(solution)/shard_map/ppermute | solution.py:20
  35.4 4.4 %collective-permute-start.5 = (bf16[2,16,128,128]{3,2,1,0:T(8,128)(2,1)S(1)}, bf16[2,16,128,128]{3,2,1,0:T(8,128)(2,1)}, u32[]{:S(2)}, u32[]{:S(2)}) collective-permute-start(bf16[2,16,128,128]{3,2,1,0:T(8,128)(2,1)S(1)} %maximum_bitcast_fusion.refs_0_), channel_id=1, source_target_pairs={{0,4},{2,6},{8,12},{10,14},{16,20},{18,22},{24,28},{26,30},{1,5},{... | collective-permute-start | bytes 3145736 | tf_op jit(solution)/shard_map/ppermute | solution.py:29
  39.8 1.3 collective-permute-start.6
  41.1 6.5 %collective-permute-start.8 = (bf16[2,16,128,128]{3,2,1,0:T(8,128)(2,1)}, bf16[2,16,128,128]{3,2,1,0:T(8,128)(2,1)}, u32[]{:S(2)}, u32[]{:S(2)}) collective-permute-start(bf16[2,16,128,128]{3,2,1,0:T(8,128)(2,1)} %collective-permute-done.refs_1_), channel_id=1, source_target_pairs={{0,4},{2,6},{8,12},{10,14},{16,20},{18,22},{24,28},{26,30},{1,5},{... | collective-permute-start | bytes 3145736 | tf_op jit(solution)/shard_map/ppermute | solution.py:29
  47.6 8.6 %collective-permute-done.2.refs_1_ = bf16[2,16,128,128]{3,2,1,0:T(8,128)(2,1)} collective-permute-done((bf16[2,16,128,128]{3,2,1,0:T(8,128)(2,1)}, bf16[2,16,128,128]{3,2,1,0:T(8,128)(2,1)}, u32[]{:S(2)}, u32[]{:S(2)}) %collective-permute-start.2) | collective-permute-done | bytes 1048608 | tf_op jit(solution)/shard_map/ppermute | solution.py:20
  56.2 1.3 collective-permute-start.9
  57.5 0.1 collective-permute-start.1
  57.6 0.6 multiply_reduce_fusion
  58.3 1.4 copy.16
  59.7 1.4 copy.17
  61.0 0.7 copy.18
  61.7 0.7 collective-permute-done.5
  62.4 2.7 %collective-permute-start.3 = (bf16[2,16,128,128]{3,2,1,0:T(8,128)(2,1)S(1)}, bf16[2,16,128,128]{3,2,1,0:T(8,128)(2,1)}, u32[]{:S(2)}, u32[]{:S(2)}) collective-permute-start(bf16[2,16,128,128]{3,2,1,0:T(8,128)(2,1)S(1)} %maximum_bitcast_fusion.refs_0_), channel_id=1, source_target_pairs={{0,2},{4,6},{8,10},{12,14},{16,18},{20,22},{24,26},{28,30},{1,3},{... | collective-permute-start | bytes 3145736 | tf_op jit(solution)/shard_map/ppermute | solution.py:29
  65.1 3.0 %collective-permute-done.6 = bf16[2,16,128,128]{3,2,1,0:T(8,128)(2,1)} collective-permute-done((bf16[2,16,128,128]{3,2,1,0:T(8,128)(2,1)}, bf16[2,16,128,128]{3,2,1,0:T(8,128)(2,1)}, u32[]{:S(2)}, u32[]{:S(2)}) %collective-permute-start.6) | collective-permute-done | bytes 1048608 | tf_op jit(solution)/shard_map/ppermute | solution.py:29
  68.1 1.3 collective-permute-start.4
  69.4 2.4 %broadcast_select_fusion.1.refs_3_ = bf16[2,16,128,128]{3,2,1,0:T(8,128)(2,1)} fusion(bf16[2,16,128,128]{3,2,1,0:T(8,128)(2,1)} %collective-permute-done.5, bf16[2,16,128,128]{3,2,1,0:T(8,128)(2,1)} %collective-permute-done.6, pred[]{:T(512)S(6)} %eq.18), kind=kLoop, calls=%fused_computation.22 | loop fusion | flops 524288 | bytes 3145729 | tf_op jit(solution)/shard_map/jit(_where)/select_n | solution.py:138
  71.7 10.9 %collective-permute-done.8 = bf16[2,16,128,128]{3,2,1,0:T(8,128)(2,1)} collective-permute-done((bf16[2,16,128,128]{3,2,1,0:T(8,128)(2,1)}, bf16[2,16,128,128]{3,2,1,0:T(8,128)(2,1)}, u32[]{:S(2)}, u32[]{:S(2)}) %collective-permute-start.8) | collective-permute-done | bytes 1048608 | tf_op jit(solution)/shard_map/ppermute | solution.py:29
  82.6 0.0 collective-permute-start.7
  82.6 5.3 %collective-permute-done.9 = bf16[2,16,128,128]{3,2,1,0:T(8,128)(2,1)} collective-permute-done((bf16[2,16,128,128]{3,2,1,0:T(8,128)(2,1)}, bf16[2,16,128,128]{3,2,1,0:T(8,128)(2,1)}, u32[]{:S(2)}, u32[]{:S(2)}) %collective-permute-start.9) | collective-permute-done | bytes 1048608 | tf_op jit(solution)/shard_map/ppermute | solution.py:29
  87.9 1.3 broadcast_select_fusion.refs_1_
  89.3 0.1 collective-permute-start.10
  89.4 0.7 add_convert_fusion.2.valid_ref
  90.1 0.6 add_convert_fusion.4.valid_ref
  90.7 0.6 add_convert_fusion.3.valid_ref
  91.3 0.0 collective-permute-done.1.refs_2_
  91.3 14.2 %shard_map.85 = (f32[16,2,128,128]{3,2,1,0:T(8,128)}, bf16[2,16,128,128]{3,2,1,0:T(8,128)(2,1)}, bf16[2,16,128,128]{3,2,1,0:T(8,128)(2,1)}, bf16[2,16,128,128]{3,2,1,0:T(8,128)(2,1)}) custom-call(s32[3]{0:T(128)} %add_convert_fusion.4.valid_ref, bf16[16,2,128,128]{3,2,1,0:T(8,128)(2,1)} %bitcast.34, bf16[16,2,128,128]{3,2,1,0:T(8,128)(2,1)} %bitcast.37, ...), custom_call_target="tpu_custom_call" | custom-call | flops 2013265920 | bytes 8388608 | tf_op jit(solution)/shard_map/pallas_call | solution.py:102
  105.5 0.0 collective-permute-done.3
  105.5 0.0 collective-permute-done.4
  105.5 2.3 %broadcast_select_fusion.2.refs_2_ = bf16[2,16,128,128]{3,2,1,0:T(8,128)(2,1)} fusion(bf16[2,16,128,128]{3,2,1,0:T(8,128)(2,1)} %collective-permute-done.3, bf16[2,16,128,128]{3,2,1,0:T(8,128)(2,1)} %collective-permute-done.4, pred[]{:T(512)S(6)} %eq.17), kind=kLoop, calls=%fused_computation.23 | loop fusion | flops 524288 | bytes 3145729 | tf_op jit(solution)/shard_map/jit(_where)/select_n | solution.py:140
  107.8 0.0 collective-permute-done.7.refs_4_
  107.8 17.3 %shard_map.86 = (f32[16,2,128,128]{3,2,1,0:T(8,128)}, bf16[2,16,128,128]{3,2,1,0:T(8,128)(2,1)}, bf16[2,16,128,128]{3,2,1,0:T(8,128)(2,1)}, bf16[2,16,128,128]{3,2,1,0:T(8,128)(2,1)}, bf16[2,16,128,128]{3,2,1,0:T(8,128)(2,1)}) custom-call(s32[4]{0:T(128)} %add_convert_fusion.3.valid_ref, bf16[16,2,128,128]{3,2,1,0:T(8,128)(2,1)} %bitcast.35, ...), custom_call_target="tpu_custom_call" | custom-call | flops 2684354560 | bytes 12582912 | tf_op jit(solution)/shard_map/pallas_call | solution.py:102
  125.1 0.0 collective-permute-done.10.refs_2_
  125.1 1.0 copy-done.3
  126.1 11.9 %shard_map.87 = (f32[16,2,128,128]{3,2,1,0:T(8,128)}, bf16[2,16,128,128]{3,2,1,0:T(8,128)(2,1)}, bf16[2,16,128,128]{3,2,1,0:T(8,128)(2,1)}) custom-call(s32[2]{0:T(128)} %add_convert_fusion.2.valid_ref, bf16[16,2,128,128]{3,2,1,0:T(8,128)(2,1)} %bitcast.36, bf16[16,2,128,128]{3,2,1,0:T(8,128)(2,1)} %bitcast.39, f32[16,1,256]{2,1,0:T(1,128)} %bitcast.50, ...), custom_call_target="tpu_custom_call" | custom-call | flops 1342177280 | bytes 8388608 | tf_op jit(solution)/shard_map/pallas_call | solution.py:102
  138.0 0.4 collective-permute-start.15
  138.4 0.2 collective-permute-start.12
  138.6 0.3 collective-permute-start.11
  139.0 2.0 collective-permute-done.15
  141.0 2.6 %add_convert_fusion = bf16[2,16,128,128]{3,2,1,0:T(8,128)(2,1)} fusion(bf16[2,16,128,128]{3,2,1,0:T(8,128)(2,1)S(1)} %collective-permute-done.15, bf16[2,16,128,128]{3,2,1,0:T(8,128)(2,1)} %get-tuple-element.24), kind=kLoop, calls=%fused_computation.15 | loop fusion | flops 2097152 | bytes 3145728 | tf_op jit(solution)/shard_map/convert_element_type | solution.py:155
  143.5 0.0 collective-permute-start.16
  143.6 0.3 collective-permute-start.14
  143.9 0.2 collective-permute-done.12
  144.1 1.6 add_convert_fusion.1
  145.7 1.6 collective-permute-start.13
  147.3 0.0 collective-permute-done.11
  147.3 22.4 %collective-permute-done.16 = bf16[2,16,128,128]{3,2,1,0:T(8,128)(2,1)S(1)} collective-permute-done((bf16[2,16,128,128]{3,2,1,0:T(8,128)(2,1)}, bf16[2,16,128,128]{3,2,1,0:T(8,128)(2,1)S(1)}, u32[]{:S(2)}, u32[]{:S(2)}) %collective-permute-start.16) | collective-permute-done | bytes 1048608 | tf_op jit(solution)/shard_map/ppermute | solution.py:24
  169.7 1.9 fusion.6
  171.6 1.3 collective-permute-start.17
  172.9 18.7 %collective-permute-done.13 = bf16[2,16,128,128]{3,2,1,0:T(8,128)(2,1)S(1)} collective-permute-done((bf16[2,16,128,128]{3,2,1,0:T(8,128)(2,1)S(1)}, bf16[2,16,128,128]{3,2,1,0:T(8,128)(2,1)S(1)}, u32[]{:S(2)}, u32[]{:S(2)}) %collective-permute-start.13) | collective-permute-done | bytes 1048608 | tf_op jit(solution)/shard_map/ppermute | solution.py:24
  191.6 5.9 %collective-permute-done.17 = bf16[2,16,128,128]{3,2,1,0:T(8,128)(2,1)S(1)} collective-permute-done((bf16[2,16,128,128]{3,2,1,0:T(8,128)(2,1)S(1)}, bf16[2,16,128,128]{3,2,1,0:T(8,128)(2,1)S(1)}, u32[]{:S(2)}, u32[]{:S(2)}) %collective-permute-start.17) | collective-permute-done | bytes 1048608 | tf_op jit(solution)/shard_map/ppermute | solution.py:20
  197.5 1.8 fusion.9
  199.4 1.5 collective-permute-start.18
  200.9 2.0 multiply_convert_fusion
  202.8 1.6 copy.27
  204.5 20.1 %collective-permute-done.18 = bf16[2,16,128,128]{3,2,1,0:T(8,128)(2,1)S(1)} collective-permute-done((bf16[2,16,128,128]{3,2,1,0:T(8,128)(2,1)}, bf16[2,16,128,128]{3,2,1,0:T(8,128)(2,1)S(1)}, u32[]{:S(2)}, u32[]{:S(2)}) %collective-permute-start.18) | collective-permute-done | bytes 1048608 | tf_op jit(solution)/shard_map/ppermute | solution.py:20
  224.6 0.7 fusion.3
  225.3 0.1 slice_bitcast_fusion
  225.4 1.1 copy.22
  226.5 1.1 copy.23
  (17 shorter events, 0.0 us)
Async XLA Ops:
  0.6 56.9 %copy-start.1 = (bf16[128,32,128]{2,1,0:T(8,128)(2,1)S(1)}, bf16[128,32,128]{2,1,0:T(8,128)(2,1)}, u32[]{:S(2)}) copy-start(bf16[128,32,128]{2,1,0:T(8,128)(2,1)} %param.10) | copy-start | bytes 3145732
  0.6 56.9 %copy-start.5 = (bf16[128,32,128]{2,1,0:T(8,128)(2,1)S(1)}, bf16[128,32,128]{2,1,0:T(8,128)(2,1)}, u32[]{:S(2)}) copy-start(bf16[128,32,128]{2,1,0:T(8,128)(2,1)} %param.9) | copy-start | bytes 3145732
  2.3 56.0 %copy-start.6 = (bf16[128,32,128]{2,1,0:T(8,128)(2,1)S(1)}, bf16[128,32,128]{2,1,0:T(8,128)(2,1)}, u32[]{:S(2)}) copy-start(bf16[128,32,128]{2,1,0:T(8,128)(2,1)} %param.6) | copy-start | bytes 3145732
  2.4 60.0 %copy-start.7 = (bf16[2,16,128,128]{3,2,1,0:T(8,128)(2,1)}, bf16[2,16,128,128]{3,2,1,0:T(8,128)(2,1)S(1)}, u32[]{:S(2)}) copy-start(bf16[2,16,128,128]{3,2,1,0:T(8,128)(2,1)S(1)} %maximum_bitcast_fusion.refs_0_) | copy-start | bytes 3145732
  2.4 27.5 %collective-permute-start = (bf16[2,16,128,128]{3,2,1,0:T(8,128)(2,1)S(1)}, bf16[2,16,128,128]{3,2,1,0:T(8,128)(2,1)}, u32[]{:S(2)}, u32[]{:S(2)}) collective-permute-start(bf16[2,16,128,128]{3,2,1,0:T(8,128)(2,1)S(1)} %maximum_bitcast_fusion.refs_0_), channel_id=1, source_target_pairs={{0,8},{2,10},{4,12},{6,14},{8,16},{10,18},{12,20},{14,22},{16,24},... | collective-permute-start | bytes 3145736 | tf_op jit(solution)/shard_map/ppermute | solution.py:20
  29.9 26.3 %collective-permute-start.2 = (bf16[2,16,128,128]{3,2,1,0:T(8,128)(2,1)}, bf16[2,16,128,128]{3,2,1,0:T(8,128)(2,1)}, u32[]{:S(2)}, u32[]{:S(2)}) collective-permute-start(bf16[2,16,128,128]{3,2,1,0:T(8,128)(2,1)} %collective-permute-done.refs_1_), channel_id=1, source_target_pairs={{0,8},{2,10},{4,12},{6,14},{8,16},{10,18},{12,20},{14,22},{16,24},... | collective-permute-start | bytes 3145736 | tf_op jit(solution)/shard_map/ppermute | solution.py:20
  35.4 27.0 %collective-permute-start.5 = (bf16[2,16,128,128]{3,2,1,0:T(8,128)(2,1)S(1)}, bf16[2,16,128,128]{3,2,1,0:T(8,128)(2,1)}, u32[]{:S(2)}, u32[]{:S(2)}) collective-permute-start(bf16[2,16,128,128]{3,2,1,0:T(8,128)(2,1)S(1)} %maximum_bitcast_fusion.refs_0_), channel_id=1, source_target_pairs={{0,4},{2,6},{8,12},{10,14},{16,20},{18,22},{24,28},{26,30},{1,5},{... | collective-permute-start | bytes 3145736 | tf_op jit(solution)/shard_map/ppermute | solution.py:29
  39.8 28.3 %collective-permute-start.6 = (bf16[2,16,128,128]{3,2,1,0:T(8,128)(2,1)}, bf16[2,16,128,128]{3,2,1,0:T(8,128)(2,1)}, u32[]{:S(2)}, u32[]{:S(2)}) collective-permute-start(bf16[2,16,128,128]{3,2,1,0:T(8,128)(2,1)} %collective-permute-done.refs_1_), channel_id=1, source_target_pairs={{4,0},{6,2},{12,8},{14,10},{20,16},{22,18},{28,24},{30,26},{5,1},{... | collective-permute-start | bytes 3145736 | tf_op jit(solution)/shard_map/ppermute | solution.py:29
  41.1 41.5 %collective-permute-start.8 = (bf16[2,16,128,128]{3,2,1,0:T(8,128)(2,1)}, bf16[2,16,128,128]{3,2,1,0:T(8,128)(2,1)}, u32[]{:S(2)}, u32[]{:S(2)}) collective-permute-start(bf16[2,16,128,128]{3,2,1,0:T(8,128)(2,1)} %collective-permute-done.refs_1_), channel_id=1, source_target_pairs={{0,4},{2,6},{8,12},{10,14},{16,20},{18,22},{24,28},{26,30},{1,5},{... | collective-permute-start | bytes 3145736 | tf_op jit(solution)/shard_map/ppermute | solution.py:29
  56.2 31.7 %collective-permute-start.9 = (bf16[2,16,128,128]{3,2,1,0:T(8,128)(2,1)}, bf16[2,16,128,128]{3,2,1,0:T(8,128)(2,1)}, u32[]{:S(2)}, u32[]{:S(2)}) collective-permute-start(bf16[2,16,128,128]{3,2,1,0:T(8,128)(2,1)} %collective-permute-done.2.refs_1_), channel_id=1, source_target_pairs={{4,0},{6,2},{12,8},{14,10},{20,16},{22,18},{28,24},{30,26},{5,1},{... | collective-permute-start | bytes 3145736 | tf_op jit(solution)/shard_map/ppermute | solution.py:29
  57.5 33.8 %collective-permute-start.1 = (bf16[2,16,128,128]{3,2,1,0:T(8,128)(2,1)}, bf16[2,16,128,128]{3,2,1,0:T(8,128)(2,1)}, u32[]{:S(2)}, u32[]{:S(2)}) collective-permute-start(bf16[2,16,128,128]{3,2,1,0:T(8,128)(2,1)} %collective-permute-done.refs_1_), channel_id=1, source_target_pairs={{0,2},{2,0},{4,6},{6,4},{8,10},{10,8},{12,14},{14,12},{16,18},{18,... | collective-permute-start | bytes 3145736 | tf_op jit(solution)/shard_map/ppermute | solution.py:24
  62.4 43.1 %collective-permute-start.3 = (bf16[2,16,128,128]{3,2,1,0:T(8,128)(2,1)S(1)}, bf16[2,16,128,128]{3,2,1,0:T(8,128)(2,1)}, u32[]{:S(2)}, u32[]{:S(2)}) collective-permute-start(bf16[2,16,128,128]{3,2,1,0:T(8,128)(2,1)S(1)} %maximum_bitcast_fusion.refs_0_), channel_id=1, source_target_pairs={{0,2},{4,6},{8,10},{12,14},{16,18},{20,22},{24,26},{28,30},{1,3},{... | collective-permute-start | bytes 3145736 | tf_op jit(solution)/shard_map/ppermute | solution.py:29
  68.1 37.4 %collective-permute-start.4 = (bf16[2,16,128,128]{3,2,1,0:T(8,128)(2,1)}, bf16[2,16,128,128]{3,2,1,0:T(8,128)(2,1)}, u32[]{:S(2)}, u32[]{:S(2)}) collective-permute-start(bf16[2,16,128,128]{3,2,1,0:T(8,128)(2,1)} %collective-permute-done.2.refs_1_), channel_id=1, source_target_pairs={{2,0},{6,4},{10,8},{14,12},{18,16},{22,20},{26,24},{30,28},{3,1},{... | collective-permute-start | bytes 3145736 | tf_op jit(solution)/shard_map/ppermute | solution.py:29
  82.6 25.2 %collective-permute-start.7 = (bf16[2,16,128,128]{3,2,1,0:T(8,128)(2,1)}, bf16[2,16,128,128]{3,2,1,0:T(8,128)(2,1)}, u32[]{:S(2)}, u32[]{:S(2)}) collective-permute-start(bf16[2,16,128,128]{3,2,1,0:T(8,128)(2,1)} %broadcast_select_fusion.1.refs_3_), channel_id=1, source_target_pairs={{0,2},{2,0},{4,6},{6,4},{8,10},{10,8},{12,14},{14,12},{16,18},{18,... | collective-permute-start | bytes 3145736 | tf_op jit(solution)/shard_map/ppermute | solution.py:24
  89.3 16.2 %copy-start = (bf16[2,16,128,128]{3,2,1,0:T(8,128)(2,1)}, bf16[2,16,128,128]{3,2,1,0:T(8,128)(2,1)S(1)}, u32[]{:S(2)}) copy-start(bf16[2,16,128,128]{3,2,1,0:T(8,128)(2,1)S(1)} %broadcast_select_fusion.refs_1_) | copy-start | bytes 3145732
  89.3 35.8 %collective-permute-start.10 = (bf16[2,16,128,128]{3,2,1,0:T(8,128)(2,1)S(1)}, bf16[2,16,128,128]{3,2,1,0:T(8,128)(2,1)S(1)}, u32[]{:S(2)}, u32[]{:S(2)}) collective-permute-start(bf16[2,16,128,128]{3,2,1,0:T(8,128)(2,1)S(1)} %broadcast_select_fusion.refs_1_), channel_id=1, source_target_pairs={{0,2},{2,0},{4,6},{6,4},{8,10},{10,8},{12,14},{14,12},{16,18},{18,... | collective-permute-start | bytes 3145736 | tf_op jit(solution)/shard_map/ppermute | solution.py:24
  125.1 1.0 copy-start.3
  138.0 6.1 %copy-start.4 = (bf16[2,16,128,128]{3,2,1,0:T(8,128)(2,1)S(1)}, bf16[2,16,128,128]{3,2,1,0:T(8,128)(2,1)}, u32[]{:S(2)}) copy-start(bf16[2,16,128,128]{3,2,1,0:T(8,128)(2,1)} %get-tuple-element.20) | copy-start | bytes 3145732
  138.0 2.9 %collective-permute-start.15 = (bf16[2,16,128,128]{3,2,1,0:T(8,128)(2,1)}, bf16[2,16,128,128]{3,2,1,0:T(8,128)(2,1)S(1)}, u32[]{:S(2)}, u32[]{:S(2)}) collective-permute-start(bf16[2,16,128,128]{3,2,1,0:T(8,128)(2,1)} %get-tuple-element.25), channel_id=1, source_target_pairs={{0,2},{2,0},{4,6},{6,4},{8,10},{10,8},{12,14},{14,12},{16,18},{18,... | collective-permute-start | bytes 3145736 | tf_op jit(solution)/shard_map/ppermute | solution.py:24
  138.4 5.7 %collective-permute-start.12 = (bf16[2,16,128,128]{3,2,1,0:T(8,128)(2,1)}, bf16[2,16,128,128]{3,2,1,0:T(8,128)(2,1)}, u32[]{:S(2)}, u32[]{:S(2)}) collective-permute-start(bf16[2,16,128,128]{3,2,1,0:T(8,128)(2,1)} %get-tuple-element.21), channel_id=1, source_target_pairs={{0,2},{2,0},{4,6},{6,4},{8,10},{10,8},{12,14},{14,12},{16,18},{18,... | collective-permute-start | bytes 3145736 | tf_op jit(solution)/shard_map/ppermute | solution.py:24
  138.6 8.7 %collective-permute-start.11 = (bf16[2,16,128,128]{3,2,1,0:T(8,128)(2,1)}, bf16[2,16,128,128]{3,2,1,0:T(8,128)(2,1)S(1)}, u32[]{:S(2)}, u32[]{:S(2)}) collective-permute-start(bf16[2,16,128,128]{3,2,1,0:T(8,128)(2,1)} %get-tuple-element.19), channel_id=1, source_target_pairs={{0,2},{2,0},{4,6},{6,4},{8,10},{10,8},{12,14},{14,12},{16,18},{18,... | collective-permute-start | bytes 3145736 | tf_op jit(solution)/shard_map/ppermute | solution.py:24
  143.5 26.2 %collective-permute-start.16 = (bf16[2,16,128,128]{3,2,1,0:T(8,128)(2,1)}, bf16[2,16,128,128]{3,2,1,0:T(8,128)(2,1)S(1)}, u32[]{:S(2)}, u32[]{:S(2)}) collective-permute-start(bf16[2,16,128,128]{3,2,1,0:T(8,128)(2,1)} %add_convert_fusion), channel_id=1, source_target_pairs={{0,4},{2,6},{4,0},{6,2},{8,12},{10,14},{12,8},{14,10},{16,20},{18,... | collective-permute-start | bytes 3145736 | tf_op jit(solution)/shard_map/ppermute | solution.py:24
  143.6 29.4 %collective-permute-start.14 = (bf16[2,16,128,128]{3,2,1,0:T(8,128)(2,1)}, bf16[2,16,128,128]{3,2,1,0:T(8,128)(2,1)S(1)}, u32[]{:S(2)}, u32[]{:S(2)}) collective-permute-start(bf16[2,16,128,128]{3,2,1,0:T(8,128)(2,1)} %get-tuple-element.23), channel_id=1, source_target_pairs={{0,2},{2,0},{4,6},{6,4},{8,10},{10,8},{12,14},{14,12},{16,18},{18,... | collective-permute-start | bytes 3145736 | tf_op jit(solution)/shard_map/ppermute | solution.py:24
  145.7 45.9 %collective-permute-start.13 = (bf16[2,16,128,128]{3,2,1,0:T(8,128)(2,1)S(1)}, bf16[2,16,128,128]{3,2,1,0:T(8,128)(2,1)S(1)}, u32[]{:S(2)}, u32[]{:S(2)}) collective-permute-start(bf16[2,16,128,128]{3,2,1,0:T(8,128)(2,1)S(1)} %add_convert_fusion.1), channel_id=1, source_target_pairs={{0,4},{2,6},{4,0},{6,2},{8,12},{10,14},{12,8},{14,10},{16,20},{18,... | collective-permute-start | bytes 3145736 | tf_op jit(solution)/shard_map/ppermute | solution.py:24
  169.7 27.8 %copy-start.2 = (bf16[2,16,128,128]{3,2,1,0:T(8,128)(2,1)S(1)}, bf16[2,16,128,128]{3,2,1,0:T(8,128)(2,1)}, u32[]{:S(2)}) copy-start(bf16[2,16,128,128]{3,2,1,0:T(8,128)(2,1)} %get-tuple-element.22) | copy-start | bytes 3145732
  171.6 25.9 %collective-permute-start.17 = (bf16[2,16,128,128]{3,2,1,0:T(8,128)(2,1)S(1)}, bf16[2,16,128,128]{3,2,1,0:T(8,128)(2,1)S(1)}, u32[]{:S(2)}, u32[]{:S(2)}) collective-permute-start(bf16[2,16,128,128]{3,2,1,0:T(8,128)(2,1)S(1)} %fusion.6), channel_id=1, source_target_pairs={{8,0},{10,2},{12,4},{14,6},{16,8},{18,10},{20,12},{22,14},{24,16},... | collective-permute-start | bytes 3145736 | tf_op jit(solution)/shard_map/ppermute | solution.py:20
  199.4 25.2 %collective-permute-start.18 = (bf16[2,16,128,128]{3,2,1,0:T(8,128)(2,1)}, bf16[2,16,128,128]{3,2,1,0:T(8,128)(2,1)S(1)}, u32[]{:S(2)}, u32[]{:S(2)}) collective-permute-start(bf16[2,16,128,128]{3,2,1,0:T(8,128)(2,1)} %fusion.9), channel_id=1, source_target_pairs={{8,0},{10,2},{12,4},{14,6},{16,8},{18,10},{20,12},{22,14},{24,16},... | collective-permute-start | bytes 3145736 | tf_op jit(solution)/shard_map/ppermute | solution.py:20
  200.8 23.7 %copy-start.8 = (bf16[2,16,128,128]{3,2,1,0:T(8,128)(2,1)S(1)}, bf16[2,16,128,128]{3,2,1,0:T(8,128)(2,1)}, u32[]{:S(2)}) copy-start(bf16[2,16,128,128]{3,2,1,0:T(8,128)(2,1)} %get-tuple-element.18) | copy-start | bytes 3145732

commit v4 on v3

--- a/solution.py
+++ b/solution.py
@@ -141,11 +141,11 @@
     y1 = jnp.where(half == 1, yc, yd)
     d1 = swap(y1, n, 1)
 
-    run = functools.partial(attend_blocks, idx=idx, q4=q4, do4=do4, lse3=lse3, delta3=delta3)
-    acc, (tx0, tx1, tcx1) = run([0, 1, 1], [0, PLANE, 3 + 2 * core], acc=None, kvs=[x0, x1, cx1])
-    acc, (tx2, tcxo, ty0, td0) = run(
-        [2, 1, 1, 1], [2 * PLANE, 7 - 6 * core, 2, 1 + 2 * core], acc=acc, kvs=[x2, cxo, y0, d0])
-    acc, (ty1, td1) = run([1, 1], [6, 5 + 2 * core], acc=acc, kvs=[y1, d1])
+    acc, terms = attend_blocks(
+        [0, 1, 1, 2, 1, 1, 1, 1, 1],
+        [0, PLANE, 3 + 2 * core, 2 * PLANE, 7 - 6 * core, 2, 1 + 2 * core, 6, 5 + 2 * core],
+        idx, q4, do4, lse3, delta3, None, [x0, x1, cx1, x2, cxo, y0, d0, y1, d1])
+    tx0, tx1, tcx1, tx2, tcxo, ty0, td0, ty1, td1 = terms
 
     f32 = jnp.float32
     bf16 = jnp.bfloat16

time: 229 us -> 221 us (0.965)
  Pallas kernels: 43.4 us -> 32.5 us
  waiting for transfers between devices: 119 us -> 127 us
    pallas_call x3 -> x1, Pallas kernels: 43.4 us -> 32.5 us  [attend_blocks(): pl.pallas_call(functools.partial(_blocks_kernel, tuple(modes), acc is not...]
    ppermute x6, waiting for transfers between devices: 19.8 us -> 24.8 us  [one_way(): return lax.ppermute(x, 'seq', pairs)]
  transfers between devices with their start and end apart: 19 -> 19, of which waited for: 12 -> 11; matrix products, arithmetic and copies ran while one was open for 10% -> 9% of each run, Pallas kernels for 14% -> 0%
where the time goes in v4:
time: 221 us; the launch traced here: 220 us
  waiting for transfers between devices  127 us (57%)
  starting transfers between devices  32.5 us (15%)
  Pallas kernels  32.5 us (15%)
  other arithmetic  18.7 us (8%)
  local copies, waits for them, and re-layouts  9.05 us (4%)
    ppermute x4, waiting for transfers between devices, shift(): return lax.ppermute(x, 'seq', pairs)  58.2 us
    ppermute x9, waiting for transfers between devices, swap(): return lax.ppermute(x, 'seq', [(i, i ^ bit) for i in range(n)])  43.9 us
    pallas_call x1, Pallas kernels, attend_blocks(): pl.pallas_call(functools.partial(_blocks_kernel, tuple(modes), acc is not...  32.5 us
    ppermute x6, waiting for transfers between devices, one_way(): return lax.ppermute(x, 'seq', pairs)  24.8 us
    ppermute x6, starting transfers between devices, one_way(): return lax.ppermute(x, 'seq', pairs)  15.2 us
    ppermute x4, starting transfers between devices, shift(): return lax.ppermute(x, 'seq', pairs)  14 us
  transfers between devices with their start and end apart: 19, of which 11 were waited for; matrix products, arithmetic and copies ran while one was open for 9% of the time, Pallas kernels for 0%

profile of v4, /device:TPU:0, one launch (start us, length us, event | category | flops | bytes accessed | tf_op | source)
XLA Modules:
  0.0 220.4 jit_solution(9576152984318856336)
XLA Ops:
  0.6 1.5 copy_bitcast_fusion.1
  2.1 1.1 maximum_bitcast_fusion.refs_0_
  3.2 5.9 %collective-permute-start = (bf16[2,16,128,128]{3,2,1,0:T(8,128)(2,1)}, bf16[2,16,128,128]{3,2,1,0:T(8,128)(2,1)}, u32[]{:S(2)}, u32[]{:S(2)}) collective-permute-start(bf16[2,16,128,128]{3,2,1,0:T(8,128)(2,1)} %maximum_bitcast_fusion.refs_0_), channel_id=1, source_target_pairs={{0,8},{2,10},{4,12},{6,14},{8,16},{10,18},{12,20},{14,22},{16,24},... | collective-permute-start | bytes 3145736 | tf_op jit(solution)/shard_map/ppermute | solution.py:20
  9.1 21.8 %collective-permute-done.refs_1_ = bf16[2,16,128,128]{3,2,1,0:T(8,128)(2,1)} collective-permute-done((bf16[2,16,128,128]{3,2,1,0:T(8,128)(2,1)}, bf16[2,16,128,128]{3,2,1,0:T(8,128)(2,1)}, u32[]{:S(2)}, u32[]{:S(2)}) %collective-permute-start) | collective-permute-done | bytes 1048608 | tf_op jit(solution)/shard_map/ppermute | solution.py:20
  30.8 5.4 %collective-permute-start.2 = (bf16[2,16,128,128]{3,2,1,0:T(8,128)(2,1)}, bf16[2,16,128,128]{3,2,1,0:T(8,128)(2,1)}, u32[]{:S(2)}, u32[]{:S(2)}) collective-permute-start(bf16[2,16,128,128]{3,2,1,0:T(8,128)(2,1)} %collective-permute-done.refs_1_), channel_id=1, source_target_pairs={{0,8},{2,10},{4,12},{6,14},{8,16},{10,18},{12,20},{14,22},{16,24},... | collective-permute-start | bytes 3145736 | tf_op jit(solution)/shard_map/ppermute | solution.py:20
  36.2 3.5 %collective-permute-start.5 = (bf16[2,16,128,128]{3,2,1,0:T(8,128)(2,1)}, bf16[2,16,128,128]{3,2,1,0:T(8,128)(2,1)S(1)}, u32[]{:S(2)}, u32[]{:S(2)}) collective-permute-start(bf16[2,16,128,128]{3,2,1,0:T(8,128)(2,1)} %maximum_bitcast_fusion.refs_0_), channel_id=1, source_target_pairs={{0,4},{2,6},{8,12},{10,14},{16,20},{18,22},{24,28},{26,30},{1,5},{... | collective-permute-start | bytes 3145736 | tf_op jit(solution)/shard_map/ppermute | solution.py:29
  39.7 1.3 collective-permute-start.6
  41.0 5.6 %collective-permute-start.8 = (bf16[2,16,128,128]{3,2,1,0:T(8,128)(2,1)}, bf16[2,16,128,128]{3,2,1,0:T(8,128)(2,1)}, u32[]{:S(2)}, u32[]{:S(2)}) collective-permute-start(bf16[2,16,128,128]{3,2,1,0:T(8,128)(2,1)} %collective-permute-done.refs_1_), channel_id=1, source_target_pairs={{0,4},{2,6},{8,12},{10,14},{16,20},{18,22},{24,28},{26,30},{1,5},{... | collective-permute-start | bytes 3145736 | tf_op jit(solution)/shard_map/ppermute | solution.py:29
  46.6 10.4 %collective-permute-done.2.refs_3_ = bf16[2,16,128,128]{3,2,1,0:T(8,128)(2,1)} collective-permute-done((bf16[2,16,128,128]{3,2,1,0:T(8,128)(2,1)}, bf16[2,16,128,128]{3,2,1,0:T(8,128)(2,1)}, u32[]{:S(2)}, u32[]{:S(2)}) %collective-permute-start.2) | collective-permute-done | bytes 1048608 | tf_op jit(solution)/shard_map/ppermute | solution.py:20
  57.1 1.3 collective-permute-start.9
  58.3 2.3 %collective-permute-start.3 = (bf16[2,16,128,128]{3,2,1,0:T(8,128)(2,1)}, bf16[2,16,128,128]{3,2,1,0:T(8,128)(2,1)}, u32[]{:S(2)}, u32[]{:S(2)}) collective-permute-start(bf16[2,16,128,128]{3,2,1,0:T(8,128)(2,1)} %maximum_bitcast_fusion.refs_0_), channel_id=1, source_target_pairs={{0,2},{4,6},{8,10},{12,14},{16,18},{20,22},{24,26},{28,30},{1,3},{... | collective-permute-start | bytes 3145736 | tf_op jit(solution)/shard_map/ppermute | solution.py:29
  60.6 2.9 %collective-permute-done.5 = bf16[2,16,128,128]{3,2,1,0:T(8,128)(2,1)S(1)} collective-permute-done((bf16[2,16,128,128]{3,2,1,0:T(8,128)(2,1)}, bf16[2,16,128,128]{3,2,1,0:T(8,128)(2,1)S(1)}, u32[]{:S(2)}, u32[]{:S(2)}) %collective-permute-start.5) | collective-permute-done | bytes 1048608 | tf_op jit(solution)/shard_map/ppermute | solution.py:29
  63.5 0.0 collective-permute-start.1
  63.6 4.3 %collective-permute-done.6 = bf16[2,16,128,128]{3,2,1,0:T(8,128)(2,1)S(1)} collective-permute-done((bf16[2,16,128,128]{3,2,1,0:T(8,128)(2,1)}, bf16[2,16,128,128]{3,2,1,0:T(8,128)(2,1)S(1)}, u32[]{:S(2)}, u32[]{:S(2)}) %collective-permute-start.6) | collective-permute-done | bytes 1048608 | tf_op jit(solution)/shard_map/ppermute | solution.py:29
  67.9 1.3 collective-permute-start.4
  69.2 1.1 broadcast_select_fusion.1.refs_5_
  70.3 13.4 %collective-permute-done.8 = bf16[2,16,128,128]{3,2,1,0:T(8,128)(2,1)} collective-permute-done((bf16[2,16,128,128]{3,2,1,0:T(8,128)(2,1)}, bf16[2,16,128,128]{3,2,1,0:T(8,128)(2,1)}, u32[]{:S(2)}, u32[]{:S(2)}) %collective-permute-start.8) | collective-permute-done | bytes 1048608 | tf_op jit(solution)/shard_map/ppermute | solution.py:29
  83.7 0.0 collective-permute-start.7
  83.7 4.2 %collective-permute-done.9 = bf16[2,16,128,128]{3,2,1,0:T(8,128)(2,1)} collective-permute-done((bf16[2,16,128,128]{3,2,1,0:T(8,128)(2,1)}, bf16[2,16,128,128]{3,2,1,0:T(8,128)(2,1)}, u32[]{:S(2)}, u32[]{:S(2)}) %collective-permute-start.9) | collective-permute-done | bytes 1048608 | tf_op jit(solution)/shard_map/ppermute | solution.py:29
  87.8 2.4 %broadcast_select_fusion.refs_7_ = bf16[2,16,128,128]{3,2,1,0:T(8,128)(2,1)} fusion(bf16[2,16,128,128]{3,2,1,0:T(8,128)(2,1)} %collective-permute-done.8, bf16[2,16,128,128]{3,2,1,0:T(8,128)(2,1)} %collective-permute-done.9, pred[]{:T(512)S(6)} %eq.18), kind=kLoop, calls=%fused_computation.21 | loop fusion | flops 524288 | bytes 3145729 | tf_op jit(solution)/shard_map/jit(_where)/select_n | solution.py:141
  90.3 0.0 collective-permute-start.10
  90.3 0.1 stack.59
  90.4 0.5 stack.60.valid_ref
  90.9 0.0 copy-done
  90.9 0.0 copy-done.3
  90.9 0.6 multiply_reduce_fusion
  91.5 0.7 copy.18
  92.2 1.4 copy.16
  93.6 1.4 copy.17
  95.0 0.0 collective-permute-done.3
  95.0 0.0 collective-permute-done.4
  95.0 2.4 %broadcast_select_fusion.2.refs_4_ = bf16[2,16,128,128]{3,2,1,0:T(8,128)(2,1)} fusion(bf16[2,16,128,128]{3,2,1,0:T(8,128)(2,1)} %collective-permute-done.3, bf16[2,16,128,128]{3,2,1,0:T(8,128)(2,1)} %collective-permute-done.4, pred[]{:T(512)S(6)} %eq.17), kind=kLoop, calls=%fused_computation.23 | loop fusion | flops 524288 | bytes 3145729 | tf_op jit(solution)/shard_map/jit(_where)/select_n | solution.py:140
  97.4 0.0 collective-permute-done.1.refs_2_
  97.4 0.0 collective-permute-done.7.refs_6_
  97.4 0.0 collective-permute-done.10.refs_8_
  97.4 32.5 %shard_map.85 = (f32[16,2,128,128]{3,2,1,0:T(8,128)}, bf16[2,16,128,128]{3,2,1,0:T(8,128)(2,1)}, bf16[2,16,128,128]{3,2,1,0:T(8,128)(2,1)}, bf16[2,16,128,128]{3...) custom-call(s32[9]{0:T(128)} %stack.60.valid_ref, ...), custom_call_target="tpu_custom_call" | custom-call | flops 6039797760 | bytes 20971520 | tf_op jit(solution)/shard_map/pallas_call | solution.py:102
  129.9 0.0 copy-start.2
  129.9 0.6 collective-permute-start.15
  130.5 0.1 collective-permute-start.12
  130.5 0.4 collective-permute-start.11
  131.0 2.7 %collective-permute-done.15 = bf16[2,16,128,128]{3,2,1,0:T(8,128)(2,1)S(1)} collective-permute-done((bf16[2,16,128,128]{3,2,1,0:T(8,128)(2,1)}, bf16[2,16,128,128]{3,2,1,0:T(8,128)(2,1)S(1)}, u32[]{:S(2)}, u32[]{:S(2)}) %collective-permute-start.15) | collective-permute-done | bytes 1048608 | tf_op jit(solution)/shard_map/ppermute | solution.py:24
  133.7 2.6 %add_convert_fusion = bf16[2,16,128,128]{3,2,1,0:T(8,128)(2,1)} fusion(bf16[2,16,128,128]{3,2,1,0:T(8,128)(2,1)S(1)} %collective-permute-done.15, bf16[2,16,128,128]{3,2,1,0:T(8,128)(2,1)} %get-tuple-element.20), kind=kLoop, calls=%fused_computation.15 | loop fusion | flops 2097152 | bytes 3145728 | tf_op jit(solution)/shard_map/convert_element_type | solution.py:155
  136.2 0.0 collective-permute-start.16
  136.3 0.4 collective-permute-start.14
  136.6 0.0 collective-permute-done.12
  136.6 1.6 add_convert_fusion.1
  138.2 1.8 collective-permute-start.13
  140.0 0.0 collective-permute-done.11
  140.0 22.4 %collective-permute-done.16 = bf16[2,16,128,128]{3,2,1,0:T(8,128)(2,1)S(1)} collective-permute-done((bf16[2,16,128,128]{3,2,1,0:T(8,128)(2,1)}, bf16[2,16,128,128]{3,2,1,0:T(8,128)(2,1)S(1)}, u32[]{:S(2)}, u32[]{:S(2)}) %collective-permute-start.16) | collective-permute-done | bytes 1048608 | tf_op jit(solution)/shard_map/ppermute | solution.py:24
  162.5 1.9 fusion.6
  164.3 1.3 collective-permute-start.17
  165.6 0.0 collective-permute-done.14
  165.6 18.7 %collective-permute-done.13 = bf16[2,16,128,128]{3,2,1,0:T(8,128)(2,1)S(1)} collective-permute-done((bf16[2,16,128,128]{3,2,1,0:T(8,128)(2,1)S(1)}, bf16[2,16,128,128]{3,2,1,0:T(8,128)(2,1)S(1)}, u32[]{:S(2)}, u32[]{:S(2)}) %collective-permute-start.13) | collective-permute-done | bytes 1048608 | tf_op jit(solution)/shard_map/ppermute | solution.py:24
  184.4 5.9 %collective-permute-done.17 = bf16[2,16,128,128]{3,2,1,0:T(8,128)(2,1)S(1)} collective-permute-done((bf16[2,16,128,128]{3,2,1,0:T(8,128)(2,1)S(1)}, bf16[2,16,128,128]{3,2,1,0:T(8,128)(2,1)S(1)}, u32[]{:S(2)}, u32[]{:S(2)}) %collective-permute-start.17) | collective-permute-done | bytes 1048608 | tf_op jit(solution)/shard_map/ppermute | solution.py:20
  190.3 1.9 fusion.9
  192.1 1.5 collective-permute-start.18
  193.6 0.0 copy-start.5
  193.6 2.0 multiply_convert_fusion
  195.6 1.6 copy.27
  197.3 20.1 %collective-permute-done.18 = bf16[2,16,128,128]{3,2,1,0:T(8,128)(2,1)S(1)} collective-permute-done((bf16[2,16,128,128]{3,2,1,0:T(8,128)(2,1)}, bf16[2,16,128,128]{3,2,1,0:T(8,128)(2,1)S(1)}, u32[]{:S(2)}, u32[]{:S(2)}) %collective-permute-start.18) | collective-permute-done | bytes 1048608 | tf_op jit(solution)/shard_map/ppermute | solution.py:20
  217.4 0.7 fusion.3
  218.1 0.1 slice_bitcast_fusion
  218.2 1.1 copy.23
  219.3 1.1 copy.22
  (8 shorter events, 0.0 us)
Async XLA Ops:
  3.2 27.6 %collective-permute-start = (bf16[2,16,128,128]{3,2,1,0:T(8,128)(2,1)}, bf16[2,16,128,128]{3,2,1,0:T(8,128)(2,1)}, u32[]{:S(2)}, u32[]{:S(2)}) collective-permute-start(bf16[2,16,128,128]{3,2,1,0:T(8,128)(2,1)} %maximum_bitcast_fusion.refs_0_), channel_id=1, source_target_pairs={{0,8},{2,10},{4,12},{6,14},{8,16},{10,18},{12,20},{14,22},{16,24},... | collective-permute-start | bytes 3145736 | tf_op jit(solution)/shard_map/ppermute | solution.py:20
  30.8 26.2 %collective-permute-start.2 = (bf16[2,16,128,128]{3,2,1,0:T(8,128)(2,1)}, bf16[2,16,128,128]{3,2,1,0:T(8,128)(2,1)}, u32[]{:S(2)}, u32[]{:S(2)}) collective-permute-start(bf16[2,16,128,128]{3,2,1,0:T(8,128)(2,1)} %collective-permute-done.refs_1_), channel_id=1, source_target_pairs={{0,8},{2,10},{4,12},{6,14},{8,16},{10,18},{12,20},{14,22},{16,24},... | collective-permute-start | bytes 3145736 | tf_op jit(solution)/shard_map/ppermute | solution.py:20
  36.2 27.3 %collective-permute-start.5 = (bf16[2,16,128,128]{3,2,1,0:T(8,128)(2,1)}, bf16[2,16,128,128]{3,2,1,0:T(8,128)(2,1)S(1)}, u32[]{:S(2)}, u32[]{:S(2)}) collective-permute-start(bf16[2,16,128,128]{3,2,1,0:T(8,128)(2,1)} %maximum_bitcast_fusion.refs_0_), channel_id=1, source_target_pairs={{0,4},{2,6},{8,12},{10,14},{16,20},{18,22},{24,28},{26,30},{1,5},{... | collective-permute-start | bytes 3145736 | tf_op jit(solution)/shard_map/ppermute | solution.py:29
  39.7 28.2 %collective-permute-start.6 = (bf16[2,16,128,128]{3,2,1,0:T(8,128)(2,1)}, bf16[2,16,128,128]{3,2,1,0:T(8,128)(2,1)S(1)}, u32[]{:S(2)}, u32[]{:S(2)}) collective-permute-start(bf16[2,16,128,128]{3,2,1,0:T(8,128)(2,1)} %collective-permute-done.refs_1_), channel_id=1, source_target_pairs={{4,0},{6,2},{12,8},{14,10},{20,16},{22,18},{28,24},{30,26},{5,1},{... | collective-permute-start | bytes 3145736 | tf_op jit(solution)/shard_map/ppermute | solution.py:29
  41.0 42.7 %collective-permute-start.8 = (bf16[2,16,128,128]{3,2,1,0:T(8,128)(2,1)}, bf16[2,16,128,128]{3,2,1,0:T(8,128)(2,1)}, u32[]{:S(2)}, u32[]{:S(2)}) collective-permute-start(bf16[2,16,128,128]{3,2,1,0:T(8,128)(2,1)} %collective-permute-done.refs_1_), channel_id=1, source_target_pairs={{0,4},{2,6},{8,12},{10,14},{16,20},{18,22},{24,28},{26,30},{1,5},{... | collective-permute-start | bytes 3145736 | tf_op jit(solution)/shard_map/ppermute | solution.py:29
  57.1 30.8 %collective-permute-start.9 = (bf16[2,16,128,128]{3,2,1,0:T(8,128)(2,1)}, bf16[2,16,128,128]{3,2,1,0:T(8,128)(2,1)}, u32[]{:S(2)}, u32[]{:S(2)}) collective-permute-start(bf16[2,16,128,128]{3,2,1,0:T(8,128)(2,1)} %collective-permute-done.2.refs_3_), channel_id=1, source_target_pairs={{4,0},{6,2},{12,8},{14,10},{20,16},{22,18},{28,24},{30,26},{5,1},{... | collective-permute-start | bytes 3145736 | tf_op jit(solution)/shard_map/ppermute | solution.py:29
  58.3 36.7 %collective-permute-start.3 = (bf16[2,16,128,128]{3,2,1,0:T(8,128)(2,1)}, bf16[2,16,128,128]{3,2,1,0:T(8,128)(2,1)}, u32[]{:S(2)}, u32[]{:S(2)}) collective-permute-start(bf16[2,16,128,128]{3,2,1,0:T(8,128)(2,1)} %maximum_bitcast_fusion.refs_0_), channel_id=1, source_target_pairs={{0,2},{4,6},{8,10},{12,14},{16,18},{20,22},{24,26},{28,30},{1,3},{... | collective-permute-start | bytes 3145736 | tf_op jit(solution)/shard_map/ppermute | solution.py:29
  63.5 33.8 %collective-permute-start.1 = (bf16[2,16,128,128]{3,2,1,0:T(8,128)(2,1)}, bf16[2,16,128,128]{3,2,1,0:T(8,128)(2,1)}, u32[]{:S(2)}, u32[]{:S(2)}) collective-permute-start(bf16[2,16,128,128]{3,2,1,0:T(8,128)(2,1)} %collective-permute-done.refs_1_), channel_id=1, source_target_pairs={{0,2},{2,0},{4,6},{6,4},{8,10},{10,8},{12,14},{14,12},{16,18},{18,... | collective-permute-start | bytes 3145736 | tf_op jit(solution)/shard_map/ppermute | solution.py:24
  67.9 27.1 %collective-permute-start.4 = (bf16[2,16,128,128]{3,2,1,0:T(8,128)(2,1)}, bf16[2,16,128,128]{3,2,1,0:T(8,128)(2,1)}, u32[]{:S(2)}, u32[]{:S(2)}) collective-permute-start(bf16[2,16,128,128]{3,2,1,0:T(8,128)(2,1)} %collective-permute-done.2.refs_3_), channel_id=1, source_target_pairs={{2,0},{6,4},{10,8},{14,12},{18,16},{22,20},{26,24},{30,28},{3,1},{... | collective-permute-start | bytes 3145736 | tf_op jit(solution)/shard_map/ppermute | solution.py:29
  70.3 20.6 %copy-start = (bf16[128,32,128]{2,1,0:T(8,128)(2,1)S(1)}, bf16[128,32,128]{2,1,0:T(8,128)(2,1)}, u32[]{:S(2)}) copy-start(bf16[128,32,128]{2,1,0:T(8,128)(2,1)} %param.10) | copy-start | bytes 3145732
  70.3 20.6 %copy-start.3 = (bf16[128,32,128]{2,1,0:T(8,128)(2,1)S(1)}, bf16[128,32,128]{2,1,0:T(8,128)(2,1)}, u32[]{:S(2)}) copy-start(bf16[128,32,128]{2,1,0:T(8,128)(2,1)} %param.9) | copy-start | bytes 3145732
  70.3 21.9 %copy-start.4 = (bf16[128,32,128]{2,1,0:T(8,128)(2,1)S(1)}, bf16[128,32,128]{2,1,0:T(8,128)(2,1)}, u32[]{:S(2)}) copy-start(bf16[128,32,128]{2,1,0:T(8,128)(2,1)} %param.6) | copy-start | bytes 3145732
  83.7 13.7 %collective-permute-start.7 = (bf16[2,16,128,128]{3,2,1,0:T(8,128)(2,1)}, bf16[2,16,128,128]{3,2,1,0:T(8,128)(2,1)}, u32[]{:S(2)}, u32[]{:S(2)}) collective-permute-start(bf16[2,16,128,128]{3,2,1,0:T(8,128)(2,1)} %broadcast_select_fusion.1.refs_5_), channel_id=1, source_target_pairs={{0,2},{2,0},{4,6},{6,4},{8,10},{10,8},{12,14},{14,12},{16,18},{18,... | collective-permute-start | bytes 3145736 | tf_op jit(solution)/shard_map/ppermute | solution.py:24
  90.3 7.1 %collective-permute-start.10 = (bf16[2,16,128,128]{3,2,1,0:T(8,128)(2,1)}, bf16[2,16,128,128]{3,2,1,0:T(8,128)(2,1)}, u32[]{:S(2)}, u32[]{:S(2)}) collective-permute-start(bf16[2,16,128,128]{3,2,1,0:T(8,128)(2,1)} %broadcast_select_fusion.refs_7_), channel_id=1, source_target_pairs={{0,2},{2,0},{4,6},{6,4},{8,10},{10,8},{12,14},{14,12},{16,18},{18,... | collective-permute-start | bytes 3145736 | tf_op jit(solution)/shard_map/ppermute | solution.py:24
  129.9 6.7 %copy-start.2 = (bf16[2,16,128,128]{3,2,1,0:T(8,128)(2,1)S(1)}, bf16[2,16,128,128]{3,2,1,0:T(8,128)(2,1)}, u32[]{:S(2)}) copy-start(bf16[2,16,128,128]{3,2,1,0:T(8,128)(2,1)} %get-tuple-element.16) | copy-start | bytes 3145732
  129.9 3.8 %collective-permute-start.15 = (bf16[2,16,128,128]{3,2,1,0:T(8,128)(2,1)}, bf16[2,16,128,128]{3,2,1,0:T(8,128)(2,1)S(1)}, u32[]{:S(2)}, u32[]{:S(2)}) collective-permute-start(bf16[2,16,128,128]{3,2,1,0:T(8,128)(2,1)} %get-tuple-element.21), channel_id=1, source_target_pairs={{0,2},{2,0},{4,6},{6,4},{8,10},{10,8},{12,14},{14,12},{16,18},{18,... | collective-permute-start | bytes 3145736 | tf_op jit(solution)/shard_map/ppermute | solution.py:24
  130.5 6.2 %collective-permute-start.12 = (bf16[2,16,128,128]{3,2,1,0:T(8,128)(2,1)}, bf16[2,16,128,128]{3,2,1,0:T(8,128)(2,1)}, u32[]{:S(2)}, u32[]{:S(2)}) collective-permute-start(bf16[2,16,128,128]{3,2,1,0:T(8,128)(2,1)} %get-tuple-element.17), channel_id=1, source_target_pairs={{0,2},{2,0},{4,6},{6,4},{8,10},{10,8},{12,14},{14,12},{16,18},{18,... | collective-permute-start | bytes 3145736 | tf_op jit(solution)/shard_map/ppermute | solution.py:24
  130.5 9.5 %collective-permute-start.11 = (bf16[2,16,128,128]{3,2,1,0:T(8,128)(2,1)}, bf16[2,16,128,128]{3,2,1,0:T(8,128)(2,1)S(1)}, u32[]{:S(2)}, u32[]{:S(2)}) collective-permute-start(bf16[2,16,128,128]{3,2,1,0:T(8,128)(2,1)} %get-tuple-element.15), channel_id=1, source_target_pairs={{0,2},{2,0},{4,6},{6,4},{8,10},{10,8},{12,14},{14,12},{16,18},{18,... | collective-permute-start | bytes 3145736 | tf_op jit(solution)/shard_map/ppermute | solution.py:24
  136.2 26.2 %collective-permute-start.16 = (bf16[2,16,128,128]{3,2,1,0:T(8,128)(2,1)}, bf16[2,16,128,128]{3,2,1,0:T(8,128)(2,1)S(1)}, u32[]{:S(2)}, u32[]{:S(2)}) collective-permute-start(bf16[2,16,128,128]{3,2,1,0:T(8,128)(2,1)} %add_convert_fusion), channel_id=1, source_target_pairs={{0,4},{2,6},{4,0},{6,2},{8,12},{10,14},{12,8},{14,10},{16,20},{18,... | collective-permute-start | bytes 3145736 | tf_op jit(solution)/shard_map/ppermute | solution.py:24
  136.3 29.4 %collective-permute-start.14 = (bf16[2,16,128,128]{3,2,1,0:T(8,128)(2,1)}, bf16[2,16,128,128]{3,2,1,0:T(8,128)(2,1)S(1)}, u32[]{:S(2)}, u32[]{:S(2)}) collective-permute-start(bf16[2,16,128,128]{3,2,1,0:T(8,128)(2,1)} %get-tuple-element.19), channel_id=1, source_target_pairs={{0,2},{2,0},{4,6},{6,4},{8,10},{10,8},{12,14},{14,12},{16,18},{18,... | collective-permute-start | bytes 3145736 | tf_op jit(solution)/shard_map/ppermute | solution.py:24
  138.2 46.1 %collective-permute-start.13 = (bf16[2,16,128,128]{3,2,1,0:T(8,128)(2,1)S(1)}, bf16[2,16,128,128]{3,2,1,0:T(8,128)(2,1)S(1)}, u32[]{:S(2)}, u32[]{:S(2)}) collective-permute-start(bf16[2,16,128,128]{3,2,1,0:T(8,128)(2,1)S(1)} %add_convert_fusion.1), channel_id=1, source_target_pairs={{0,4},{2,6},{4,0},{6,2},{8,12},{10,14},{12,8},{14,10},{16,20},{18,... | collective-permute-start | bytes 3145736 | tf_op jit(solution)/shard_map/ppermute | solution.py:24
  162.5 27.8 %copy-start.1 = (bf16[2,16,128,128]{3,2,1,0:T(8,128)(2,1)S(1)}, bf16[2,16,128,128]{3,2,1,0:T(8,128)(2,1)}, u32[]{:S(2)}) copy-start(bf16[2,16,128,128]{3,2,1,0:T(8,128)(2,1)} %get-tuple-element.18) | copy-start | bytes 3145732
  164.3 26.0 %collective-permute-start.17 = (bf16[2,16,128,128]{3,2,1,0:T(8,128)(2,1)S(1)}, bf16[2,16,128,128]{3,2,1,0:T(8,128)(2,1)S(1)}, u32[]{:S(2)}, u32[]{:S(2)}) collective-permute-start(bf16[2,16,128,128]{3,2,1,0:T(8,128)(2,1)S(1)} %fusion.6), channel_id=1, source_target_pairs={{8,0},{10,2},{12,4},{14,6},{16,8},{18,10},{20,12},{22,14},{24,16},... | collective-permute-start | bytes 3145736 | tf_op jit(solution)/shard_map/ppermute | solution.py:20
  192.1 25.2 %collective-permute-start.18 = (bf16[2,16,128,128]{3,2,1,0:T(8,128)(2,1)}, bf16[2,16,128,128]{3,2,1,0:T(8,128)(2,1)S(1)}, u32[]{:S(2)}, u32[]{:S(2)}) collective-permute-start(bf16[2,16,128,128]{3,2,1,0:T(8,128)(2,1)} %fusion.9), channel_id=1, source_target_pairs={{8,0},{10,2},{12,4},{14,6},{16,8},{18,10},{20,12},{22,14},{24,16},... | collective-permute-start | bytes 3145736 | tf_op jit(solution)/shard_map/ppermute | solution.py:20
  193.6 23.8 %copy-start.5 = (bf16[2,16,128,128]{3,2,1,0:T(8,128)(2,1)S(1)}, bf16[2,16,128,128]{3,2,1,0:T(8,128)(2,1)}, u32[]{:S(2)}) copy-start(bf16[2,16,128,128]{3,2,1,0:T(8,128)(2,1)} %get-tuple-element.14) | copy-start | bytes 3145732

commit v5 on v4

--- a/solution.py
+++ b/solution.py
@@ -34,9 +34,11 @@
     if has_acc:
         acc_ref = refs[0]
         refs = refs[1:]
-    kv_refs = refs[:nb]
-    dq_ref = refs[nb]
-    dkv_refs = refs[nb + 1:]
+    k_refs = refs[:nb]
+    v_refs = refs[nb:2 * nb]
+    dq_ref = refs[2 * nb]
+    dk_refs = refs[2 * nb + 1:3 * nb + 1]
+    dv_refs = refs[3 * nb + 1:]
     gb, grp, tok, width = q_ref.shape
     rows = grp * tok
     kk = lax.broadcasted_iota(jnp.int32, (tok, rows), 0)
@@ -53,8 +55,8 @@
         else:
             dq = jnp.zeros((rows, width), jnp.float32)
         for b, mode in enumerate(modes):
-            k = kv_refs[b][0, g]
-            v = kv_refs[b][1, g]
+            k = k_refs[b][0, g]
+            v = v_refs[b][0, g]
             off = jnp.where(valid_ref[b] > 0, 0.0, 1e30).astype(jnp.float32)
             s = lax.dot_general(k, q, (((1,), (1,)), ((), ())), preferred_element_type=jnp.float32)
             e = jnp.exp(s * SCALE - lse - off)
@@ -71,8 +73,8 @@
             dv = jnp.dot(pb, do, preferred_element_type=jnp.float32)
             dk = jnp.dot(dsb, q, preferred_element_type=jnp.float32) * SCALE
             dq = dq + lax.dot_general(dsb, k, (((0,), (0,)), ((), ())), preferred_element_type=jnp.float32)
-            dkv_refs[b][0, g] = dk.astype(jnp.bfloat16)
-            dkv_refs[b][1, g] = dv.astype(jnp.bfloat16)
+            dk_refs[b][0, g] = dk.astype(jnp.bfloat16)
+            dv_refs[b][0, g] = dv.astype(jnp.bfloat16)
         dq_ref[g] = dq.reshape(grp, tok, width)
 
 
@@ -83,15 +85,15 @@
     valid = jnp.stack([(idx >= d).astype(jnp.int32) for d in dist])
     hspec = pl.BlockSpec((gb, grp, tok, width), lambda i, v: (i, 0, 0, 0))
     rspec = pl.BlockSpec((gb, 1, grp * tok), lambda i, v: (i, 0, 0))
-    kvspec = pl.BlockSpec((2, gb, tok, width), lambda i, v: (0, i, 0, 0))
+    kvspec = pl.BlockSpec((1, gb, tok, width), lambda i, v: (0, i, 0, 0))
     accs = [] if acc is None else [acc]
     out_shape = [jax.ShapeDtypeStruct(q4.shape, jnp.float32)]
     out_shape += [jax.ShapeDtypeStruct(kv.shape, jnp.bfloat16) for kv in kvs]
     grid_spec = pltpu.PrefetchScalarGridSpec(
         num_scalar_prefetch=1,
         grid=(nh // gb,),
-        in_specs=[hspec, hspec, rspec, rspec] + [hspec] * len(accs) + [kvspec] * nb,
-        out_specs=[hspec] + [kvspec] * nb,
+        in_specs=[hspec, hspec, rspec, rspec] + [hspec] * len(accs) + [kvspec] * (2 * nb),
+        out_specs=[hspec] + [kvspec] * (2 * nb),
     )
     scores = nh * grp * tok * tok * nb
     cost = pl.CostEstimate(
@@ -109,6 +111,42 @@
     return outs[0], list(outs[1:])
 
 
+def route(x0, n, half, core):
+    x1 = shift(x0, n, PLANE)
+    ya = one_way(x0, n, 2, 0)
+    cx1 = swap(x1, n, 1)
+    yb = one_way(x1, n, 2, 2)
+    x2 = shift(x1, n, PLANE)
+    ca = one_way(x0, n, 1, 0)
+    cb = one_way(x2, n, 1, 1)
+    yc = one_way(x1, n, 2, 0)
+    yd = one_way(x2, n, 2, 2)
+    y0 = jnp.where(half == 1, ya, yb)
+    d0 = swap(y0, n, 1)
+    cxo = jnp.where(core == 1, ca, cb)
+    y1 = jnp.where(half == 1, yc, yd)
+    d1 = swap(y1, n, 1)
+    return [x0, x1, cx1, x2, cxo, y0, d0, y1, d1]
+
+
+def unroute(terms, n, half, core):
+    tx0, tx1, tcx1, tx2, tcxo, ty0, td0, ty1, td1 = terms
+    f32 = jnp.float32
+    bf16 = jnp.bfloat16
+    r1 = swap(tcx1, n, 1).astype(f32)
+    ro = swap(tcxo, n, 1).astype(f32)
+    yret0 = swap((ty0.astype(f32) + swap(td0, n, 1).astype(f32)).astype(bf16), n, 2).astype(f32)
+    yret1 = swap((ty1.astype(f32) + swap(td1, n, 1).astype(f32)).astype(bf16), n, 2).astype(f32)
+    zero = jnp.zeros_like(r1)
+    lo = half == 0
+    part2 = tx2.astype(f32) + jnp.where(core == 1, ro, zero) + jnp.where(lo, zero, yret1)
+    part1 = tx1.astype(f32) + r1 + jnp.where(lo, yret1, yret0)
+    part1 = part1 + shift(part2.astype(bf16), n, -PLANE).astype(f32)
+    part0 = tx0.astype(f32) + jnp.where(core == 0, ro, zero) + jnp.where(lo, yret0, zero)
+    part0 = part0 + shift(part1.astype(bf16), n, -PLANE).astype(f32)
+    return part0.astype(bf16)
+
+
 def per_device(query, normed_key_rows, value_rows, out_in, grad_out, lse):
     tok, heads_q, width = query.shape
     heads_kv = normed_key_rows.shape[1]
@@ -124,46 +162,18 @@
     delta = jnp.sum(grad_out.astype(jnp.float32) * out_in.astype(jnp.float32), axis=-1)
     delta3 = delta.T.reshape(heads_kv, 1, groups * tok)
     lse3 = lse.reshape(heads_kv, 1, groups * tok)
-    x0 = jnp.stack([normed_key_rows, value_rows]).transpose(0, 2, 1, 3)
-
-    x1 = shift(x0, n, PLANE)
-    ya = one_way(x0, n, 2, 0)
-    cx1 = swap(x1, n, 1)
-    yb = one_way(x1, n, 2, 2)
-    x2 = shift(x1, n, PLANE)
-    ca = one_way(x0, n, 1, 0)
-    cb = one_way(x2, n, 1, 1)
-    yc = one_way(x1, n, 2, 0)
-    yd = one_way(x2, n, 2, 2)
-    y0 = jnp.where(half == 1, ya, yb)
-    d0 = swap(y0, n, 1)
-    cxo = jnp.where(core == 1, ca, cb)
-    y1 = jnp.where(half == 1, yc, yd)
-    d1 = swap(y1, n, 1)
+    kb = route(normed_key_rows.transpose(1, 0, 2)[None], n, half, core)
+    vb = route(value_rows.transpose(1, 0, 2)[None], n, half, core)
 
     acc, terms = attend_blocks(
         [0, 1, 1, 2, 1, 1, 1, 1, 1],
         [0, PLANE, 3 + 2 * core, 2 * PLANE, 7 - 6 * core, 2, 1 + 2 * core, 6, 5 + 2 * core],
-        idx, q4, do4, lse3, delta3, None, [x0, x1, cx1, x2, cxo, y0, d0, y1, d1])
-    tx0, tx1, tcx1, tx2, tcxo, ty0, td0, ty1, td1 = terms
+        idx, q4, do4, lse3, delta3, None, kb + vb)
+    grad_k = unroute(terms[:9], n, half, core)
+    grad_v = unroute(terms[9:], n, half, core)
 
-    f32 = jnp.float32
-    bf16 = jnp.bfloat16
-    r1 = swap(tcx1, n, 1).astype(f32)
-    ro = swap(tcxo, n, 1).astype(f32)
-    yret0 = swap((ty0.astype(f32) + swap(td0, n, 1).astype(f32)).astype(bf16), n, 2).astype(f32)
-    yret1 = swap((ty1.astype(f32) + swap(td1, n, 1).astype(f32)).astype(bf16), n, 2).astype(f32)
-    zero = jnp.zeros_like(r1)
-    lo = half == 0
-    part2 = tx2.astype(f32) + jnp.where(core == 1, ro, zero) + jnp.where(lo, zero, yret1)
-    part1 = tx1.astype(f32) + r1 + jnp.where(lo, yret1, yret0)
-    part1 = part1 + shift(part2.astype(bf16), n, -PLANE).astype(f32)
-    part0 = tx0.astype(f32) + jnp.where(core == 0, ro, zero) + jnp.where(lo, yret0, zero)
-    part0 = part0 + shift(part1.astype(bf16), n, -PLANE).astype(f32)
-    grad = part0.astype(bf16)
-
-    grad_query = (acc * SCALE).astype(bf16).reshape(heads_q, tok, width).transpose(1, 0, 2)
-    return (grad_query, grad[0].transpose(1, 0, 2), grad[1].transpose(1, 0, 2))
+    grad_query = (acc * SCALE).astype(jnp.bfloat16).reshape(heads_q, tok, width).transpose(1, 0, 2)
+    return (grad_query, grad_k[0].transpose(1, 0, 2), grad_v[0].transpose(1, 0, 2))
 
 
 def solution(mesh):

time: 221 us -> 196 us (0.89)
  waiting for transfers between devices: 127 us -> 80.1 us
  starting transfers between devices: 32.5 us -> 53.2 us
  local copies, waits for them, and re-layouts: 9.05 us -> 12.4 us
  other arithmetic: 18.7 us -> 16.1 us
    ppermute x4 -> x8, waiting for transfers between devices: 58.2 us -> 25.7 us  [shift(): return lax.ppermute(x, 'seq', pairs)]
    ppermute x4 -> x8, starting transfers between devices: 14 us -> 25.2 us  [shift(): return lax.ppermute(x, 'seq', pairs)]
    ppermute x6 -> x12, waiting for transfers between devices: 24.8 us -> 14.8 us  [one_way(): return lax.ppermute(x, 'seq', pairs)]
    ppermute x6 -> x12, starting transfers between devices: 15.2 us -> 22.5 us  [one_way(): return lax.ppermute(x, 'seq', pairs)]
    unnamed x14 -> x54, local copies, waits for them, and re-layouts: 2.29 us -> 7.24 us
    ppermute x9 -> x18, waiting for transfers between devices: 43.9 us -> 39.6 us  [swap(): return lax.ppermute(x, 'seq', [(i, i ^ bit) for i in range(n)])]
    ppermute x9 -> x18, starting transfers between devices: 3.26 us -> 5.5 us  [swap(): return lax.ppermute(x, 'seq', [(i, i ^ bit) for i in range(n)])]
    select_n x3 -> x6, other arithmetic: 5.88 us -> 4.02 us  [the longest x2 2.22 us: route(): y0 = jnp.where(half == 1, ya, yb)]
  transfers between devices with their start and end apart: 19 -> 38, of which waited for: 11 -> 19; matrix products, arithmetic and copies ran while one was open for 9% -> 12% of each run, Pallas kernels for 0% -> 0%
where the time goes in v5:
time: 196 us; the launch traced here: 195 us
  waiting for transfers between devices  80.1 us (41%)
  starting transfers between devices  53.2 us (27%)
  Pallas kernels  32 us (16%)
  other arithmetic  16.1 us (8%)
  local copies, waits for them, and re-layouts  12.4 us (6%)
    ppermute x18, waiting for transfers between devices, swap(): return lax.ppermute(x, 'seq', [(i, i ^ bit) for i in range(n)])  39.6 us
    pallas_call x1, Pallas kernels, attend_blocks(): pl.pallas_call(functools.partial(_blocks_kernel, tuple(modes), acc is not...  32 us
    ppermute x8, waiting for transfers between devices, shift(): return lax.ppermute(x, 'seq', pairs)  25.7 us
    ppermute x8, starting transfers between devices, shift(): return lax.ppermute(x, 'seq', pairs)  25.2 us
    ppermute x12, starting transfers between devices, one_way(): return lax.ppermute(x, 'seq', pairs)  22.5 us
    ppermute x12, waiting for transfers between devices, one_way(): return lax.ppermute(x, 'seq', pairs)  14.8 us
    unnamed x54, local copies, waits for them, and re-layouts  7.24 us
    ppermute x18, starting transfers between devices, swap(): return lax.ppermute(x, 'seq', [(i, i ^ bit) for i in range(n)])  5.5 us
  transfers between devices with their start and end apart: 38, of which 19 were waited for; matrix products, arithmetic and copies ran while one was open for 12% of the time, Pallas kernels for 0%

profile of v5, /device:TPU:0, one launch (start us, length us, event | category | flops | bytes accessed | tf_op | source)
XLA Modules:
  0.0 195.0 jit_solution(1686604610507012270)
XLA Ops:
  0.7 1.3 copy.28
  2.0 5.7 %collective-permute-start.11 = (bf16[1,16,128,128]{3,2,1,0:T(8,128)(2,1)S(1)}, bf16[1,16,128,128]{3,2,1,0:T(8,128)(2,1)}, u32[]{:S(2)}, u32[]{:S(2)}) collective-permute-start(bf16[1,16,128,128]{3,2,1,0:T(8,128)(2,1)S(1)} %bitcast.44), channel_id=1, source_target_pairs={{0,8},{2,10},{4,12},{6,14},{8,16},{10,18},{12,20},{14,22},{16,24},... | collective-permute-start | bytes 1572872 | tf_op jit(solution)/shard_map/ppermute | solution.py:20
  7.7 2.0 %copy.29 = bf16[128,16,128]{2,0,1:T(8,128)(2,1)} copy(bf16[128,16,128]{2,1,0:T(8,128)(2,1)} %param.7) | data formatting | bytes 1048576 | tf_op args[1]
  9.7 3.5 %collective-permute-start = (bf16[1,16,128,128]{3,2,1,0:T(8,128)(2,1)}, bf16[1,16,128,128]{3,2,1,0:T(8,128)(2,1)}, u32[]{:S(2)}, u32[]{:S(2)}) collective-permute-start(bf16[1,16,128,128]{3,2,1,0:T(8,128)(2,1)} %bitcast.37.refs_0_), channel_id=1, source_target_pairs={{0,8},{2,10},{4,12},{6,14},{8,16},{10,18},{12,20},{14,22},{16,24},... | collective-permute-start | bytes 1572872 | tf_op jit(solution)/shard_map/ppermute | solution.py:20
  13.2 3.4 %collective-permute-start.16 = (bf16[1,16,128,128]{3,2,1,0:T(8,128)(2,1)S(1)}, bf16[1,16,128,128]{3,2,1,0:T(8,128)(2,1)S(1)}, u32[]{:S(2)}, u32[]{:S(2)}) collective-permute-start(bf16[1,16,128,128]{3,2,1,0:T(8,128)(2,1)S(1)} %bitcast.45), channel_id=1, source_target_pairs={{0,4},{2,6},{8,12},{10,14},{16,20},{18,22},{24,28},{26,30},{1,5},{... | collective-permute-start | bytes 1572872 | tf_op jit(solution)/shard_map/ppermute | solution.py:29
  16.6 2.1 %collective-permute-start.5 = (bf16[1,16,128,128]{3,2,1,0:T(8,128)(2,1)}, bf16[1,16,128,128]{3,2,1,0:T(8,128)(2,1)}, u32[]{:S(2)}, u32[]{:S(2)}) collective-permute-start(bf16[1,16,128,128]{3,2,1,0:T(8,128)(2,1)} %bitcast.37.refs_0_), channel_id=1, source_target_pairs={{0,4},{2,6},{8,12},{10,14},{16,20},{18,22},{24,28},{26,30},{1,5},{... | collective-permute-start | bytes 1572872 | tf_op jit(solution)/shard_map/ppermute | solution.py:29
  18.8 0.5 collective-permute-done.11.refs_10_
  19.2 1.3 collective-permute-start.17
  20.5 5.3 %collective-permute-start.13 = (bf16[1,16,128,128]{3,2,1,0:T(8,128)(2,1)}, bf16[1,16,128,128]{3,2,1,0:T(8,128)(2,1)}, u32[]{:S(2)}, u32[]{:S(2)}) collective-permute-start(bf16[1,16,128,128]{3,2,1,0:T(8,128)(2,1)} %collective-permute-done.11.refs_10_), channel_id=1, source_target_pairs={{0,8},{2,10},{4,12},{6,14},{8,16},{10,18},{12,20},{14,22},{16,24},... | collective-permute-start | bytes 1572872 | tf_op jit(solution)/shard_map/ppermute | solution.py:20
  25.8 4.7 %collective-permute-done.refs_1_ = bf16[1,16,128,128]{3,2,1,0:T(8,128)(2,1)} collective-permute-done((bf16[1,16,128,128]{3,2,1,0:T(8,128)(2,1)}, bf16[1,16,128,128]{3,2,1,0:T(8,128)(2,1)}, u32[]{:S(2)}, u32[]{:S(2)}) %collective-permute-start) | collective-permute-done | bytes 524320 | tf_op jit(solution)/shard_map/ppermute | solution.py:20
  30.6 5.2 %collective-permute-start.2 = (bf16[1,16,128,128]{3,2,1,0:T(8,128)(2,1)}, bf16[1,16,128,128]{3,2,1,0:T(8,128)(2,1)}, u32[]{:S(2)}, u32[]{:S(2)}) collective-permute-start(bf16[1,16,128,128]{3,2,1,0:T(8,128)(2,1)} %collective-permute-done.refs_1_), channel_id=1, source_target_pairs={{0,8},{2,10},{4,12},{6,14},{8,16},{10,18},{12,20},{14,22},{16,24},... | collective-permute-start | bytes 1572872 | tf_op jit(solution)/shard_map/ppermute | solution.py:20
  35.8 0.8 copy-done.10
  36.6 1.3 collective-permute-start.6
  38.0 0.6 stack.51.valid_ref
  38.6 0.6 multiply_reduce_fusion
  39.2 0.7 copy.18
  39.9 1.4 copy.16
  41.3 1.4 copy.17
  42.7 5.3 %collective-permute-start.19 = (bf16[1,16,128,128]{3,2,1,0:T(8,128)(2,1)}, bf16[1,16,128,128]{3,2,1,0:T(8,128)(2,1)S(1)}, u32[]{:S(2)}, u32[]{:S(2)}) collective-permute-start(bf16[1,16,128,128]{3,2,1,0:T(8,128)(2,1)} %collective-permute-done.11.refs_10_), channel_id=1, source_target_pairs={{0,4},{2,6},{8,12},{10,14},{16,20},{18,22},{24,28},{26,30},{1,5},{... | collective-permute-start | bytes 1572872 | tf_op jit(solution)/shard_map/ppermute | solution.py:29
  48.0 1.3 collective-permute-start.8
  49.4 1.3 collective-permute-start.20
  50.7 1.3 collective-permute-done.2.refs_3_
  51.9 1.3 collective-permute-start.9
  53.2 1.1 broadcast_select_fusion.1.refs_14_
  54.4 1.3 collective-permute-start.14
  55.7 1.1 broadcast_select_fusion.3.refs_5_
  56.8 3.8 %collective-permute-done.19 = bf16[1,16,128,128]{3,2,1,0:T(8,128)(2,1)S(1)} collective-permute-done((bf16[1,16,128,128]{3,2,1,0:T(8,128)(2,1)}, bf16[1,16,128,128]{3,2,1,0:T(8,128)(2,1)S(1)}, u32[]{:S(2)}, u32[]{:S(2)}) %collective-permute-start.19) | collective-permute-done | bytes 524320 | tf_op jit(solution)/shard_map/ppermute | solution.py:29
  60.6 1.3 collective-permute-start.3
  62.0 6.1 %collective-permute-done.8 = bf16[1,16,128,128]{3,2,1,0:T(8,128)(2,1)S(1)} collective-permute-done((bf16[1,16,128,128]{3,2,1,0:T(8,128)(2,1)}, bf16[1,16,128,128]{3,2,1,0:T(8,128)(2,1)S(1)}, u32[]{:S(2)}, u32[]{:S(2)}) %collective-permute-start.8) | collective-permute-done | bytes 524320 | tf_op jit(solution)/shard_map/ppermute | solution.py:29
  68.1 1.3 collective-permute-start.15
  69.4 4.1 %collective-permute-done.9 = bf16[1,16,128,128]{3,2,1,0:T(8,128)(2,1)S(1)} collective-permute-done((bf16[1,16,128,128]{3,2,1,0:T(8,128)(2,1)}, bf16[1,16,128,128]{3,2,1,0:T(8,128)(2,1)S(1)}, u32[]{:S(2)}, u32[]{:S(2)}) %collective-permute-start.9) | collective-permute-done | bytes 524320 | tf_op jit(solution)/shard_map/ppermute | solution.py:29
  73.5 1.3 collective-permute-start.4
  74.9 1.2 collective-permute-start.1
  76.3 0.4 collective-permute-start.7
  76.8 0.7 collective-permute-done.4
  77.6 0.8 broadcast_select_fusion.4.refs_13_
  78.5 0.8 broadcast_select_fusion.5.refs_4_
  79.5 0.7 collective-permute-done.21.refs_17_
  80.3 0.7 collective-permute-done.10.refs_8_
  81.0 0.8 copy-done.24
  81.9 32.0 %shard_map.85 = (f32[16,2,128,128]{3,2,1,0:T(8,128)}, bf16[1,16,128,128]{3,2,1,0:T(8,128)(2,1)}, bf16[1,16,128,128]{3,2,1,0:T(8,128)(2,1)}, bf16[1,16,128,128]{3...) custom-call(s32[9]{0:T(128)} %stack.51.valid_ref, ...), custom_call_target="tpu_custom_call" | custom-call | flops 6039797760 | bytes 20971520 | tf_op jit(solution)/shard_map/pallas_call | solution.py:104
  114.6 0.4 collective-permute-start.25
  115.1 1.0 collective-permute-done.26
  116.2 1.2 add_convert_fusion.2
  117.6 2.0 %add_convert_fusion.3 = bf16[1,16,128,128]{3,2,1,0:T(8,128)(2,1)} fusion(bf16[1,16,128,128]{3,2,1,0:T(8,128)(2,1)S(1)} %collective-permute-done.23, bf16[1,16,128,128]{3,2,1,0:T(8,128)(2,1)} %get-tuple-element.25), kind=kLoop, calls=%fused_computation.36 | loop fusion | flops 1048576 | bytes 1572864 | tf_op jit(solution)/shard_map/convert_element_type | solution.py:138
  120.1 1.7 collective-permute-start.24
  121.9 10.4 %collective-permute-done.27 = bf16[1,16,128,128]{3,2,1,0:T(8,128)(2,1)S(1)} collective-permute-done((bf16[1,16,128,128]{3,2,1,0:T(8,128)(2,1)S(1)}, bf16[1,16,128,128]{3,2,1,0:T(8,128)(2,1)S(1)}, u32[]{:S(2)}, u32[]{:S(2)}) %collective-permute-start.27) | collective-permute-done | bytes 524320 | tf_op jit(solution)/shard_map/ppermute | solution.py:24
  132.3 1.1 fusion.6
  133.4 1.3 collective-permute-start.28
  134.7 0.9 add_convert_fusion.1
  135.6 18.6 %collective-permute-done.35 = bf16[1,16,128,128]{3,2,1,0:T(8,128)(2,1)S(1)} collective-permute-done((bf16[1,16,128,128]{3,2,1,0:T(8,128)(2,1)S(1)}, bf16[1,16,128,128]{3,2,1,0:T(8,128)(2,1)S(1)}, u32[]{:S(2)}, u32[]{:S(2)}) %collective-permute-start.35) | collective-permute-done | bytes 524320 | tf_op jit(solution)/shard_map/ppermute | solution.py:24
  154.5 1.1 fusion.16
  155.6 1.3 collective-permute-start.36
  156.9 1.8 fusion.9
  158.7 1.4 collective-permute-start.29
  160.2 7.6 %collective-permute-done.32 = bf16[1,16,128,128]{3,2,1,0:T(8,128)(2,1)S(1)} collective-permute-done((bf16[1,16,128,128]{3,2,1,0:T(8,128)(2,1)}, bf16[1,16,128,128]{3,2,1,0:T(8,128)(2,1)S(1)}, u32[]{:S(2)}, u32[]{:S(2)}) %collective-permute-start.32) | collective-permute-done | bytes 524320 | tf_op jit(solution)/shard_map/ppermute | solution.py:24
  167.8 4.8 %collective-permute-done.36 = bf16[1,16,128,128]{3,2,1,0:T(8,128)(2,1)} collective-permute-done((bf16[1,16,128,128]{3,2,1,0:T(8,128)(2,1)}, bf16[1,16,128,128]{3,2,1,0:T(8,128)(2,1)}, u32[]{:S(2)}, u32[]{:S(2)}) %collective-permute-start.36) | collective-permute-done | bytes 524320 | tf_op jit(solution)/shard_map/ppermute | solution.py:20
  172.6 1.6 fusion.19
  174.2 1.5 collective-permute-start.37
  176.1 1.7 copy.27
  177.7 6.0 %collective-permute-done.29 = bf16[1,16,128,128]{3,2,1,0:T(8,128)(2,1)S(1)} collective-permute-done((bf16[1,16,128,128]{3,2,1,0:T(8,128)(2,1)S(1)}, bf16[1,16,128,128]{3,2,1,0:T(8,128)(2,1)S(1)}, u32[]{:S(2)}, u32[]{:S(2)}) %collective-permute-start.29) | collective-permute-done | bytes 524320 | tf_op jit(solution)/shard_map/ppermute | solution.py:20
  184.1 1.1 copy.22
  185.2 8.3 %collective-permute-done.37 = bf16[1,16,128,128]{3,2,1,0:T(8,128)(2,1)S(1)} collective-permute-done((bf16[1,16,128,128]{3,2,1,0:T(8,128)(2,1)S(1)}, bf16[1,16,128,128]{3,2,1,0:T(8,128)(2,1)S(1)}, u32[]{:S(2)}, u32[]{:S(2)}) %collective-permute-start.37) | collective-permute-done | bytes 524320 | tf_op jit(solution)/shard_map/ppermute | solution.py:20
  193.9 1.1 copy.23
  (91 shorter events, 3.8 us)
Async XLA Ops:
  0.6 38.0 %copy-start = (bf16[128,32,128]{2,1,0:T(8,128)(2,1)S(1)}, bf16[128,32,128]{2,1,0:T(8,128)(2,1)}, u32[]{:S(2)}) copy-start(bf16[128,32,128]{2,1,0:T(8,128)(2,1)} %param.10) | copy-start | bytes 3145732
  0.6 38.0 %copy-start.2 = (bf16[128,32,128]{2,1,0:T(8,128)(2,1)S(1)}, bf16[128,32,128]{2,1,0:T(8,128)(2,1)}, u32[]{:S(2)}) copy-start(bf16[128,32,128]{2,1,0:T(8,128)(2,1)} %param.9) | copy-start | bytes 3145732
  0.7 39.3 %copy-start.3 = (bf16[128,32,128]{2,1,0:T(8,128)(2,1)S(1)}, bf16[128,32,128]{2,1,0:T(8,128)(2,1)}, u32[]{:S(2)}) copy-start(bf16[128,32,128]{2,1,0:T(8,128)(2,1)} %param.6) | copy-start | bytes 3145732
  2.0 11.2 %copy-start.8 = (bf16[128,16,128]{2,0,1:T(8,128)(2,1)}, bf16[128,16,128]{2,0,1:T(8,128)(2,1)S(1)}, u32[]{:S(2)}) copy-start(bf16[128,16,128]{2,0,1:T(8,128)(2,1)S(1)} %copy.28) | copy-start | bytes 1572868
  2.0 17.2 %collective-permute-start.11 = (bf16[1,16,128,128]{3,2,1,0:T(8,128)(2,1)S(1)}, bf16[1,16,128,128]{3,2,1,0:T(8,128)(2,1)}, u32[]{:S(2)}, u32[]{:S(2)}) collective-permute-start(bf16[1,16,128,128]{3,2,1,0:T(8,128)(2,1)S(1)} %bitcast.44), channel_id=1, source_target_pairs={{0,8},{2,10},{4,12},{6,14},{8,16},{10,18},{12,20},{14,22},{16,24},... | collective-permute-start | bytes 1572872 | tf_op jit(solution)/shard_map/ppermute | solution.py:20
  9.7 20.9 %collective-permute-start = (bf16[1,16,128,128]{3,2,1,0:T(8,128)(2,1)}, bf16[1,16,128,128]{3,2,1,0:T(8,128)(2,1)}, u32[]{:S(2)}, u32[]{:S(2)}) collective-permute-start(bf16[1,16,128,128]{3,2,1,0:T(8,128)(2,1)} %bitcast.37.refs_0_), channel_id=1, source_target_pairs={{0,8},{2,10},{4,12},{6,14},{8,16},{10,18},{12,20},{14,22},{16,24},... | collective-permute-start | bytes 1572872 | tf_op jit(solution)/shard_map/ppermute | solution.py:20
  13.2 22.6 %collective-permute-start.16 = (bf16[1,16,128,128]{3,2,1,0:T(8,128)(2,1)S(1)}, bf16[1,16,128,128]{3,2,1,0:T(8,128)(2,1)S(1)}, u32[]{:S(2)}, u32[]{:S(2)}) collective-permute-start(bf16[1,16,128,128]{3,2,1,0:T(8,128)(2,1)S(1)} %bitcast.45), channel_id=1, source_target_pairs={{0,4},{2,6},{8,12},{10,14},{16,20},{18,22},{24,28},{26,30},{1,5},{... | collective-permute-start | bytes 1572872 | tf_op jit(solution)/shard_map/ppermute | solution.py:29
  16.6 26.0 %collective-permute-start.5 = (bf16[1,16,128,128]{3,2,1,0:T(8,128)(2,1)}, bf16[1,16,128,128]{3,2,1,0:T(8,128)(2,1)}, u32[]{:S(2)}, u32[]{:S(2)}) collective-permute-start(bf16[1,16,128,128]{3,2,1,0:T(8,128)(2,1)} %bitcast.37.refs_0_), channel_id=1, source_target_pairs={{0,4},{2,6},{8,12},{10,14},{16,20},{18,22},{24,28},{26,30},{1,5},{... | collective-permute-start | bytes 1572872 | tf_op jit(solution)/shard_map/ppermute | solution.py:29
  19.2 28.8 %collective-permute-start.17 = (bf16[1,16,128,128]{3,2,1,0:T(8,128)(2,1)}, bf16[1,16,128,128]{3,2,1,0:T(8,128)(2,1)}, u32[]{:S(2)}, u32[]{:S(2)}) collective-permute-start(bf16[1,16,128,128]{3,2,1,0:T(8,128)(2,1)} %collective-permute-done.11.refs_10_), channel_id=1, source_target_pairs={{4,0},{6,2},{12,8},{14,10},{20,16},{22,18},{28,24},{30,26},{5,1},{... | collective-permute-start | bytes 1572872 | tf_op jit(solution)/shard_map/ppermute | solution.py:29
  20.5 28.8 %collective-permute-start.13 = (bf16[1,16,128,128]{3,2,1,0:T(8,128)(2,1)}, bf16[1,16,128,128]{3,2,1,0:T(8,128)(2,1)}, u32[]{:S(2)}, u32[]{:S(2)}) collective-permute-start(bf16[1,16,128,128]{3,2,1,0:T(8,128)(2,1)} %collective-permute-done.11.refs_10_), channel_id=1, source_target_pairs={{0,8},{2,10},{4,12},{6,14},{8,16},{10,18},{12,20},{14,22},{16,24},... | collective-permute-start | bytes 1572872 | tf_op jit(solution)/shard_map/ppermute | solution.py:20
  30.6 21.3 %collective-permute-start.2 = (bf16[1,16,128,128]{3,2,1,0:T(8,128)(2,1)}, bf16[1,16,128,128]{3,2,1,0:T(8,128)(2,1)}, u32[]{:S(2)}, u32[]{:S(2)}) collective-permute-start(bf16[1,16,128,128]{3,2,1,0:T(8,128)(2,1)} %collective-permute-done.refs_1_), channel_id=1, source_target_pairs={{0,8},{2,10},{4,12},{6,14},{8,16},{10,18},{12,20},{14,22},{16,24},... | collective-permute-start | bytes 1572872 | tf_op jit(solution)/shard_map/ppermute | solution.py:20
  35.8 0.8 copy-start.10
  36.6 17.8 %collective-permute-start.6 = (bf16[1,16,128,128]{3,2,1,0:T(8,128)(2,1)}, bf16[1,16,128,128]{3,2,1,0:T(8,128)(2,1)}, u32[]{:S(2)}, u32[]{:S(2)}) collective-permute-start(bf16[1,16,128,128]{3,2,1,0:T(8,128)(2,1)} %collective-permute-done.refs_1_), channel_id=1, source_target_pairs={{4,0},{6,2},{12,8},{14,10},{20,16},{22,18},{28,24},{30,26},{5,1},{... | collective-permute-start | bytes 1572872 | tf_op jit(solution)/shard_map/ppermute | solution.py:29
  39.9 13.3 %copy-start.11 = (bf16[1,16,128,128]{3,2,1,0:T(8,128)(2,1)S(1)}, bf16[1,16,128,128]{3,2,1,0:T(8,128)(2,1)}, u32[]{:S(2)}) copy-start(bf16[1,16,128,128]{3,2,1,0:T(8,128)(2,1)} %copy-done.10) | copy-start | bytes 1572868
  41.3 13.1 %copy-start.9 = (bf16[128,16,128]{2,0,1:T(8,128)(2,1)S(1)}, bf16[128,16,128]{2,0,1:T(8,128)(2,1)}, u32[]{:S(2)}) copy-start(bf16[128,16,128]{2,0,1:T(8,128)(2,1)} %copy-done.8) | copy-start | bytes 1572868
  42.7 18.0 %collective-permute-start.19 = (bf16[1,16,128,128]{3,2,1,0:T(8,128)(2,1)}, bf16[1,16,128,128]{3,2,1,0:T(8,128)(2,1)S(1)}, u32[]{:S(2)}, u32[]{:S(2)}) collective-permute-start(bf16[1,16,128,128]{3,2,1,0:T(8,128)(2,1)} %collective-permute-done.11.refs_10_), channel_id=1, source_target_pairs={{0,4},{2,6},{8,12},{10,14},{16,20},{18,22},{24,28},{26,30},{1,5},{... | collective-permute-start | bytes 1572872 | tf_op jit(solution)/shard_map/ppermute | solution.py:29
  48.0 20.1 %collective-permute-start.8 = (bf16[1,16,128,128]{3,2,1,0:T(8,128)(2,1)}, bf16[1,16,128,128]{3,2,1,0:T(8,128)(2,1)S(1)}, u32[]{:S(2)}, u32[]{:S(2)}) collective-permute-start(bf16[1,16,128,128]{3,2,1,0:T(8,128)(2,1)} %collective-permute-done.refs_1_), channel_id=1, source_target_pairs={{0,4},{2,6},{8,12},{10,14},{16,20},{18,22},{24,28},{26,30},{1,5},{... | collective-permute-start | bytes 1572872 | tf_op jit(solution)/shard_map/ppermute | solution.py:29
  49.4 18.8 %collective-permute-start.20 = (bf16[1,16,128,128]{3,2,1,0:T(8,128)(2,1)}, bf16[1,16,128,128]{3,2,1,0:T(8,128)(2,1)S(1)}, u32[]{:S(2)}, u32[]{:S(2)}) collective-permute-start(bf16[1,16,128,128]{3,2,1,0:T(8,128)(2,1)} %collective-permute-done.13.refs_12_), channel_id=1, source_target_pairs={{4,0},{6,2},{12,8},{14,10},{20,16},{22,18},{28,24},{30,26},{5,1},{... | collective-permute-start | bytes 1572872 | tf_op jit(solution)/shard_map/ppermute | solution.py:29
  51.9 21.6 %collective-permute-start.9 = (bf16[1,16,128,128]{3,2,1,0:T(8,128)(2,1)}, bf16[1,16,128,128]{3,2,1,0:T(8,128)(2,1)S(1)}, u32[]{:S(2)}, u32[]{:S(2)}) collective-permute-start(bf16[1,16,128,128]{3,2,1,0:T(8,128)(2,1)} %collective-permute-done.2.refs_3_), channel_id=1, source_target_pairs={{4,0},{6,2},{12,8},{14,10},{20,16},{22,18},{28,24},{30,26},{5,1},{... | collective-permute-start | bytes 1572872 | tf_op jit(solution)/shard_map/ppermute | solution.py:29
  54.3 21.8 %copy-start.12 = (bf16[1,16,128,128]{3,2,1,0:T(8,128)(2,1)}, bf16[1,16,128,128]{3,2,1,0:T(8,128)(2,1)S(1)}, u32[]{:S(2)}) copy-start(bf16[1,16,128,128]{3,2,1,0:T(8,128)(2,1)S(1)} %broadcast_select_fusion.1.refs_14_) | copy-start | bytes 1572868
  54.4 20.6 %collective-permute-start.14 = (bf16[1,16,128,128]{3,2,1,0:T(8,128)(2,1)S(1)}, bf16[1,16,128,128]{3,2,1,0:T(8,128)(2,1)S(1)}, u32[]{:S(2)}, u32[]{:S(2)}) collective-permute-start(bf16[1,16,128,128]{3,2,1,0:T(8,128)(2,1)S(1)} %bitcast.47), channel_id=1, source_target_pairs={{0,2},{4,6},{8,10},{12,14},{16,18},{20,22},{24,26},{28,30},{1,3},{... | collective-permute-start | bytes 1572872 | tf_op jit(solution)/shard_map/ppermute | solution.py:29
  56.8 21.7 %copy-start.13 = (bf16[1,16,128,128]{3,2,1,0:T(8,128)(2,1)}, bf16[1,16,128,128]{3,2,1,0:T(8,128)(2,1)S(1)}, u32[]{:S(2)}) copy-start(bf16[1,16,128,128]{3,2,1,0:T(8,128)(2,1)S(1)} %broadcast_select_fusion.3.refs_5_) | copy-start | bytes 1572868
  60.6 15.5 %collective-permute-start.3 = (bf16[1,16,128,128]{3,2,1,0:T(8,128)(2,1)}, bf16[1,16,128,128]{3,2,1,0:T(8,128)(2,1)S(1)}, u32[]{:S(2)}, u32[]{:S(2)}) collective-permute-start(bf16[1,16,128,128]{3,2,1,0:T(8,128)(2,1)} %bitcast.37.refs_0_), channel_id=1, source_target_pairs={{0,2},{4,6},{8,10},{12,14},{16,18},{20,22},{24,26},{28,30},{1,3},{... | collective-permute-start | bytes 1572872 | tf_op jit(solution)/shard_map/ppermute | solution.py:29
  68.1 8.2 %collective-permute-start.12 = (bf16[1,16,128,128]{3,2,1,0:T(8,128)(2,1)}, bf16[1,16,128,128]{3,2,1,0:T(8,128)(2,1)S(1)}, u32[]{:S(2)}, u32[]{:S(2)}) collective-permute-start(bf16[1,16,128,128]{3,2,1,0:T(8,128)(2,1)} %collective-permute-done.11.refs_10_), channel_id=1, source_target_pairs={{0,2},{2,0},{4,6},{6,4},{8,10},{10,8},{12,14},{14,12},{16,18},{18,... | collective-permute-start | bytes 1572872 | tf_op jit(solution)/shard_map/ppermute | solution.py:24
  68.1 8.6 %collective-permute-start.15 = (bf16[1,16,128,128]{3,2,1,0:T(8,128)(2,1)}, bf16[1,16,128,128]{3,2,1,0:T(8,128)(2,1)S(1)}, u32[]{:S(2)}, u32[]{:S(2)}) collective-permute-start(bf16[1,16,128,128]{3,2,1,0:T(8,128)(2,1)} %collective-permute-done.13.refs_12_), channel_id=1, source_target_pairs={{2,0},{6,4},{10,8},{14,12},{18,16},{22,20},{26,24},{30,28},{3,1},{... | collective-permute-start | bytes 1572872 | tf_op jit(solution)/shard_map/ppermute | solution.py:29
  73.5 4.0 %collective-permute-start.4 = (bf16[1,16,128,128]{3,2,1,0:T(8,128)(2,1)}, bf16[1,16,128,128]{3,2,1,0:T(8,128)(2,1)S(1)}, u32[]{:S(2)}, u32[]{:S(2)}) collective-permute-start(bf16[1,16,128,128]{3,2,1,0:T(8,128)(2,1)} %collective-permute-done.2.refs_3_), channel_id=1, source_target_pairs={{2,0},{6,4},{10,8},{14,12},{18,16},{22,20},{26,24},{30,28},{3,1},{... | collective-permute-start | bytes 1572872 | tf_op jit(solution)/shard_map/ppermute | solution.py:29
  74.8 4.5 %copy-start.14 = (bf16[1,16,128,128]{3,2,1,0:T(8,128)(2,1)}, bf16[1,16,128,128]{3,2,1,0:T(8,128)(2,1)S(1)}, u32[]{:S(2)}) copy-start(bf16[1,16,128,128]{3,2,1,0:T(8,128)(2,1)S(1)} %broadcast_select_fusion.refs_16_) | copy-start | bytes 1572868
  74.9 6.9 %copy-start.15 = (bf16[1,16,128,128]{3,2,1,0:T(8,128)(2,1)}, bf16[1,16,128,128]{3,2,1,0:T(8,128)(2,1)S(1)}, u32[]{:S(2)}) copy-start(bf16[1,16,128,128]{3,2,1,0:T(8,128)(2,1)S(1)} %broadcast_select_fusion.2.refs_7_) | copy-start | bytes 1572868
  74.9 4.4 %collective-permute-start.1 = (bf16[1,16,128,128]{3,2,1,0:T(8,128)(2,1)}, bf16[1,16,128,128]{3,2,1,0:T(8,128)(2,1)S(1)}, u32[]{:S(2)}, u32[]{:S(2)}) collective-permute-start(bf16[1,16,128,128]{3,2,1,0:T(8,128)(2,1)} %collective-permute-done.refs_1_), channel_id=1, source_target_pairs={{0,2},{2,0},{4,6},{6,4},{8,10},{10,8},{12,14},{14,12},{16,18},{18,... | collective-permute-start | bytes 1572872 | tf_op jit(solution)/shard_map/ppermute | solution.py:24
  76.2 3.2 %collective-permute-start.18 = (bf16[1,16,128,128]{3,2,1,0:T(8,128)(2,1)S(1)}, bf16[1,16,128,128]{3,2,1,0:T(8,128)(2,1)S(1)}, u32[]{:S(2)}, u32[]{:S(2)}) collective-permute-start(bf16[1,16,128,128]{3,2,1,0:T(8,128)(2,1)S(1)} %broadcast_select_fusion.1.refs_14_), channel_id=1, source_target_pairs={{0,2},{2,0},{4,6},{6,4},{8,10},{10,8},{12,14},{14,12},{16,18},{18,... | collective-permute-start | bytes 1572872 | tf_op jit(solution)/shard_map/ppermute | solution.py:24
  76.3 5.6 %copy-start.19 = (bf16[1,16,128,128]{3,2,1,0:T(8,128)(2,1)}, bf16[1,16,128,128]{3,2,1,0:T(8,128)(2,1)S(1)}, u32[]{:S(2)}) copy-start(bf16[1,16,128,128]{3,2,1,0:T(8,128)(2,1)S(1)} %collective-permute-done.12.refs_11_) | copy-start | bytes 1572868
  76.3 3.3 %collective-permute-start.7 = (bf16[1,16,128,128]{3,2,1,0:T(8,128)(2,1)S(1)}, bf16[1,16,128,128]{3,2,1,0:T(8,128)(2,1)S(1)}, u32[]{:S(2)}, u32[]{:S(2)}) collective-permute-start(bf16[1,16,128,128]{3,2,1,0:T(8,128)(2,1)S(1)} %broadcast_select_fusion.3.refs_5_), channel_id=1, source_target_pairs={{0,2},{2,0},{4,6},{6,4},{8,10},{10,8},{12,14},{14,12},{16,18},{18,... | collective-permute-start | bytes 1572872 | tf_op jit(solution)/shard_map/ppermute | solution.py:24
  76.7 3.6 %collective-permute-start.21 = (bf16[1,16,128,128]{3,2,1,0:T(8,128)(2,1)S(1)}, bf16[1,16,128,128]{3,2,1,0:T(8,128)(2,1)S(1)}, u32[]{:S(2)}, u32[]{:S(2)}) collective-permute-start(bf16[1,16,128,128]{3,2,1,0:T(8,128)(2,1)S(1)} %broadcast_select_fusion.refs_16_), channel_id=1, source_target_pairs={{0,2},{2,0},{4,6},{6,4},{8,10},{10,8},{12,14},{14,12},{16,18},{18,... | collective-permute-start | bytes 1572872 | tf_op jit(solution)/shard_map/ppermute | solution.py:24
  77.5 3.5 %collective-permute-start.10 = (bf16[1,16,128,128]{3,2,1,0:T(8,128)(2,1)S(1)}, bf16[1,16,128,128]{3,2,1,0:T(8,128)(2,1)S(1)}, u32[]{:S(2)}, u32[]{:S(2)}) collective-permute-start(bf16[1,16,128,128]{3,2,1,0:T(8,128)(2,1)S(1)} %broadcast_select_fusion.2.refs_7_), channel_id=1, source_target_pairs={{0,2},{2,0},{4,6},{6,4},{8,10},{10,8},{12,14},{14,12},{16,18},{18,... | collective-permute-start | bytes 1572872 | tf_op jit(solution)/shard_map/ppermute | solution.py:24
  79.3 2.5 %copy-start.20 = (bf16[1,16,128,128]{3,2,1,0:T(8,128)(2,1)}, bf16[1,16,128,128]{3,2,1,0:T(8,128)(2,1)S(1)}, u32[]{:S(2)}) copy-start(bf16[1,16,128,128]{3,2,1,0:T(8,128)(2,1)S(1)} %collective-permute-done.1.refs_2_) | copy-start | bytes 1572868
  79.3 2.5 %copy-start.21 = (bf16[1,16,128,128]{3,2,1,0:T(8,128)(2,1)}, bf16[1,16,128,128]{3,2,1,0:T(8,128)(2,1)S(1)}, u32[]{:S(2)}) copy-start(bf16[1,16,128,128]{3,2,1,0:T(8,128)(2,1)S(1)} %collective-permute-done.18.refs_15_) | copy-start | bytes 1572868
  79.5 2.3 %copy-start.22 = (bf16[1,16,128,128]{3,2,1,0:T(8,128)(2,1)}, bf16[1,16,128,128]{3,2,1,0:T(8,128)(2,1)S(1)}, u32[]{:S(2)}) copy-start(bf16[1,16,128,128]{3,2,1,0:T(8,128)(2,1)S(1)} %collective-permute-done.7.refs_6_) | copy-start | bytes 1572868
  80.3 1.6 copy-start.23
  81.0 0.8 copy-start.24
  113.9 6.1 %copy-start.7 = (bf16[1,16,128,128]{3,2,1,0:T(8,128)(2,1)S(1)}, bf16[1,16,128,128]{3,2,1,0:T(8,128)(2,1)}, u32[]{:S(2)}) copy-start(bf16[1,16,128,128]{3,2,1,0:T(8,128)(2,1)} %get-tuple-element.38) | copy-start | bytes 1572868
  113.9 2.2 %collective-permute-start.26 = (bf16[1,16,128,128]{3,2,1,0:T(8,128)(2,1)}, bf16[1,16,128,128]{3,2,1,0:T(8,128)(2,1)S(1)}, u32[]{:S(2)}, u32[]{:S(2)}) collective-permute-start(bf16[1,16,128,128]{3,2,1,0:T(8,128)(2,1)} %get-tuple-element.30), channel_id=1, source_target_pairs={{0,2},{2,0},{4,6},{6,4},{8,10},{10,8},{12,14},{14,12},{16,18},{18,... | collective-permute-start | bytes 1572872 | tf_op jit(solution)/shard_map/ppermute | solution.py:24
  114.1 3.5 %collective-permute-start.23 = (bf16[1,16,128,128]{3,2,1,0:T(8,128)(2,1)}, bf16[1,16,128,128]{3,2,1,0:T(8,128)(2,1)S(1)}, u32[]{:S(2)}, u32[]{:S(2)}) collective-permute-start(bf16[1,16,128,128]{3,2,1,0:T(8,128)(2,1)} %get-tuple-element.26), channel_id=1, source_target_pairs={{0,2},{2,0},{4,6},{6,4},{8,10},{10,8},{12,14},{14,12},{16,18},{18,... | collective-permute-start | bytes 1572872 | tf_op jit(solution)/shard_map/ppermute | solution.py:24
  114.5 5.7 %collective-permute-start.22 = (bf16[1,16,128,128]{3,2,1,0:T(8,128)(2,1)}, bf16[1,16,128,128]{3,2,1,0:T(8,128)(2,1)S(1)}, u32[]{:S(2)}, u32[]{:S(2)}) collective-permute-start(bf16[1,16,128,128]{3,2,1,0:T(8,128)(2,1)} %get-tuple-element.24), channel_id=1, source_target_pairs={{0,2},{2,0},{4,6},{6,4},{8,10},{10,8},{12,14},{14,12},{16,18},{18,... | collective-permute-start | bytes 1572872 | tf_op jit(solution)/shard_map/ppermute | solution.py:24
  114.6 41.0 %collective-permute-start.25 = (bf16[1,16,128,128]{3,2,1,0:T(8,128)(2,1)}, bf16[1,16,128,128]{3,2,1,0:T(8,128)(2,1)}, u32[]{:S(2)}, u32[]{:S(2)}) collective-permute-start(bf16[1,16,128,128]{3,2,1,0:T(8,128)(2,1)} %get-tuple-element.28), channel_id=1, source_target_pairs={{0,2},{2,0},{4,6},{6,4},{8,10},{10,8},{12,14},{14,12},{16,18},{18,... | collective-permute-start | bytes 1572872 | tf_op jit(solution)/shard_map/ppermute | solution.py:24
  115.0 20.7 %collective-permute-start.30 = (bf16[1,16,128,128]{3,2,1,0:T(8,128)(2,1)}, bf16[1,16,128,128]{3,2,1,0:T(8,128)(2,1)S(1)}, u32[]{:S(2)}, u32[]{:S(2)}) collective-permute-start(bf16[1,16,128,128]{3,2,1,0:T(8,128)(2,1)} %get-tuple-element.33), channel_id=1, source_target_pairs={{0,2},{2,0},{4,6},{6,4},{8,10},{10,8},{12,14},{14,12},{16,18},{18,... | collective-permute-start | bytes 1572872 | tf_op jit(solution)/shard_map/ppermute | solution.py:24
  116.1 3.7 %collective-permute-start.34 = (bf16[1,16,128,128]{3,2,1,0:T(8,128)(2,1)}, bf16[1,16,128,128]{3,2,1,0:T(8,128)(2,1)S(1)}, u32[]{:S(2)}, u32[]{:S(2)}) collective-permute-start(bf16[1,16,128,128]{3,2,1,0:T(8,128)(2,1)} %get-tuple-element.39), channel_id=1, source_target_pairs={{0,2},{2,0},{4,6},{6,4},{8,10},{10,8},{12,14},{14,12},{16,18},{18,... | collective-permute-start | bytes 1572872 | tf_op jit(solution)/shard_map/ppermute | solution.py:24
  116.2 16.1 %copy-start.18 = (bf16[1,16,128,128]{3,2,1,0:T(8,128)(2,1)S(1)}, bf16[1,16,128,128]{3,2,1,0:T(8,128)(2,1)}, u32[]{:S(2)}) copy-start(bf16[1,16,128,128]{3,2,1,0:T(8,128)(2,1)} %get-tuple-element.31) | copy-start | bytes 1572868
  117.6 14.7 %collective-permute-start.27 = (bf16[1,16,128,128]{3,2,1,0:T(8,128)(2,1)S(1)}, bf16[1,16,128,128]{3,2,1,0:T(8,128)(2,1)S(1)}, u32[]{:S(2)}, u32[]{:S(2)}) collective-permute-start(bf16[1,16,128,128]{3,2,1,0:T(8,128)(2,1)S(1)} %add_convert_fusion.2), channel_id=1, source_target_pairs={{0,4},{2,6},{4,0},{6,2},{8,12},{10,14},{12,8},{14,10},{16,20},{18,... | collective-permute-start | bytes 1572872 | tf_op jit(solution)/shard_map/ppermute | solution.py:24
  119.6 15.1 %copy-start.6 = (bf16[1,16,128,128]{3,2,1,0:T(8,128)(2,1)S(1)}, bf16[1,16,128,128]{3,2,1,0:T(8,128)(2,1)}, u32[]{:S(2)}) copy-start(bf16[1,16,128,128]{3,2,1,0:T(8,128)(2,1)} %get-tuple-element.34) | copy-start | bytes 1572868
  119.8 13.6 %collective-permute-start.31 = (bf16[1,16,128,128]{3,2,1,0:T(8,128)(2,1)}, bf16[1,16,128,128]{3,2,1,0:T(8,128)(2,1)S(1)}, u32[]{:S(2)}, u32[]{:S(2)}) collective-permute-start(bf16[1,16,128,128]{3,2,1,0:T(8,128)(2,1)} %get-tuple-element.35), channel_id=1, source_target_pairs={{0,2},{2,0},{4,6},{6,4},{8,10},{10,8},{12,14},{14,12},{16,18},{18,... | collective-permute-start | bytes 1572872 | tf_op jit(solution)/shard_map/ppermute | solution.py:24
  120.1 34.4 %copy-start.17 = (bf16[1,16,128,128]{3,2,1,0:T(8,128)(2,1)S(1)}, bf16[1,16,128,128]{3,2,1,0:T(8,128)(2,1)}, u32[]{:S(2)}) copy-start(bf16[1,16,128,128]{3,2,1,0:T(8,128)(2,1)} %get-tuple-element.40) | copy-start | bytes 1572868
  120.1 36.7 %collective-permute-start.24 = (bf16[1,16,128,128]{3,2,1,0:T(8,128)(2,1)}, bf16[1,16,128,128]{3,2,1,0:T(8,128)(2,1)S(1)}, u32[]{:S(2)}, u32[]{:S(2)}) collective-permute-start(bf16[1,16,128,128]{3,2,1,0:T(8,128)(2,1)} %add_convert_fusion.3), channel_id=1, source_target_pairs={{0,4},{2,6},{4,0},{6,2},{8,12},{10,14},{12,8},{14,10},{16,20},{18,... | collective-permute-start | bytes 1572872 | tf_op jit(solution)/shard_map/ppermute | solution.py:24
  132.3 21.9 %collective-permute-start.35 = (bf16[1,16,128,128]{3,2,1,0:T(8,128)(2,1)S(1)}, bf16[1,16,128,128]{3,2,1,0:T(8,128)(2,1)S(1)}, u32[]{:S(2)}, u32[]{:S(2)}) collective-permute-start(bf16[1,16,128,128]{3,2,1,0:T(8,128)(2,1)S(1)} %add_convert_fusion), channel_id=1, source_target_pairs={{0,4},{2,6},{4,0},{6,2},{8,12},{10,14},{12,8},{14,10},{16,20},{18,... | collective-permute-start | bytes 1572872 | tf_op jit(solution)/shard_map/ppermute | solution.py:24
  133.4 23.5 %collective-permute-start.28 = (bf16[1,16,128,128]{3,2,1,0:T(8,128)(2,1)}, bf16[1,16,128,128]{3,2,1,0:T(8,128)(2,1)}, u32[]{:S(2)}, u32[]{:S(2)}) collective-permute-start(bf16[1,16,128,128]{3,2,1,0:T(8,128)(2,1)} %fusion.6), channel_id=1, source_target_pairs={{8,0},{10,2},{12,4},{14,6},{16,8},{18,10},{20,12},{22,14},{24,16},... | collective-permute-start | bytes 1572872 | tf_op jit(solution)/shard_map/ppermute | solution.py:20
  135.6 24.5 %collective-permute-start.33 = (bf16[1,16,128,128]{3,2,1,0:T(8,128)(2,1)}, bf16[1,16,128,128]{3,2,1,0:T(8,128)(2,1)}, u32[]{:S(2)}, u32[]{:S(2)}) collective-permute-start(bf16[1,16,128,128]{3,2,1,0:T(8,128)(2,1)} %get-tuple-element.37), channel_id=1, source_target_pairs={{0,2},{2,0},{4,6},{6,4},{8,10},{10,8},{12,14},{14,12},{16,18},{18,... | collective-permute-start | bytes 1572872 | tf_op jit(solution)/shard_map/ppermute | solution.py:24
  154.2 13.6 %collective-permute-start.32 = (bf16[1,16,128,128]{3,2,1,0:T(8,128)(2,1)}, bf16[1,16,128,128]{3,2,1,0:T(8,128)(2,1)S(1)}, u32[]{:S(2)}, u32[]{:S(2)}) collective-permute-start(bf16[1,16,128,128]{3,2,1,0:T(8,128)(2,1)} %add_convert_fusion.1), channel_id=1, source_target_pairs={{0,4},{2,6},{4,0},{6,2},{8,12},{10,14},{12,8},{14,10},{16,20},{18,... | collective-permute-start | bytes 1572872 | tf_op jit(solution)/shard_map/ppermute | solution.py:24
  155.6 17.0 %collective-permute-start.36 = (bf16[1,16,128,128]{3,2,1,0:T(8,128)(2,1)}, bf16[1,16,128,128]{3,2,1,0:T(8,128)(2,1)}, u32[]{:S(2)}, u32[]{:S(2)}) collective-permute-start(bf16[1,16,128,128]{3,2,1,0:T(8,128)(2,1)} %fusion.16), channel_id=1, source_target_pairs={{8,0},{10,2},{12,4},{14,6},{16,8},{18,10},{20,12},{22,14},{24,16},... | collective-permute-start | bytes 1572872 | tf_op jit(solution)/shard_map/ppermute | solution.py:20
  156.9 15.8 %copy-start.16 = (bf16[1,16,128,128]{3,2,1,0:T(8,128)(2,1)S(1)}, bf16[1,16,128,128]{3,2,1,0:T(8,128)(2,1)}, u32[]{:S(2)}) copy-start(bf16[1,16,128,128]{3,2,1,0:T(8,128)(2,1)} %get-tuple-element.36) | copy-start | bytes 1572868
  158.7 17.0 %copy-start.1 = (f32[16,2,128,128]{3,2,1,0:T(8,128)S(1)}, f32[16,2,128,128]{3,2,1,0:T(8,128)}, u32[]{:S(2)}) copy-start(f32[16,2,128,128]{3,2,1,0:T(8,128)} %get-tuple-element.22) | copy-start | bytes 6291460
  158.7 25.0 %collective-permute-start.29 = (bf16[1,16,128,128]{3,2,1,0:T(8,128)(2,1)S(1)}, bf16[1,16,128,128]{3,2,1,0:T(8,128)(2,1)S(1)}, u32[]{:S(2)}, u32[]{:S(2)}) collective-permute-start(bf16[1,16,128,128]{3,2,1,0:T(8,128)(2,1)S(1)} %fusion.9), channel_id=1, source_target_pairs={{8,0},{10,2},{12,4},{14,6},{16,8},{18,10},{20,12},{22,14},{24,16},... | collective-permute-start | bytes 1572872 | tf_op jit(solution)/shard_map/ppermute | solution.py:20
  174.2 19.3 %collective-permute-start.37 = (bf16[1,16,128,128]{3,2,1,0:T(8,128)(2,1)S(1)}, bf16[1,16,128,128]{3,2,1,0:T(8,128)(2,1)S(1)}, u32[]{:S(2)}, u32[]{:S(2)}) collective-permute-start(bf16[1,16,128,128]{3,2,1,0:T(8,128)(2,1)S(1)} %fusion.19), channel_id=1, source_target_pairs={{8,0},{10,2},{12,4},{14,6},{16,8},{18,10},{20,12},{22,14},{24,16},... | collective-permute-start | bytes 1572872 | tf_op jit(solution)/shard_map/ppermute | solution.py:20
  175.7 8.0 %copy-start.5 = (bf16[1,16,128,128]{3,2,1,0:T(8,128)(2,1)S(1)}, bf16[1,16,128,128]{3,2,1,0:T(8,128)(2,1)}, u32[]{:S(2)}) copy-start(bf16[1,16,128,128]{3,2,1,0:T(8,128)(2,1)} %get-tuple-element.23) | copy-start | bytes 1572868
  177.7 15.8 %copy-start.4 = (bf16[1,16,128,128]{3,2,1,0:T(8,128)(2,1)S(1)}, bf16[1,16,128,128]{3,2,1,0:T(8,128)(2,1)}, u32[]{:S(2)}) copy-start(bf16[1,16,128,128]{3,2,1,0:T(8,128)(2,1)} %get-tuple-element.32) | copy-start | bytes 1572868

commit v6 on v5

--- a/solution.py
+++ b/solution.py
@@ -51,9 +51,9 @@
         lse = lse_ref[g]
         delta = delta_ref[g]
         if has_acc:
-            dq = acc_ref[g].reshape(rows, width)
+            dq = acc_ref[g]
         else:
-            dq = jnp.zeros((rows, width), jnp.float32)
+            dq = jnp.zeros((width, rows), jnp.float32)
         for b, mode in enumerate(modes):
             k = k_refs[b][0, g]
             v = v_refs[b][0, g]
@@ -72,10 +72,10 @@
             dsb = ds.astype(jnp.bfloat16)
             dv = jnp.dot(pb, do, preferred_element_type=jnp.float32)
             dk = jnp.dot(dsb, q, preferred_element_type=jnp.float32) * SCALE
-            dq = dq + lax.dot_general(dsb, k, (((0,), (0,)), ((), ())), preferred_element_type=jnp.float32)
+            dq = dq + lax.dot_general(k, dsb, (((0,), (0,)), ((), ())), preferred_element_type=jnp.float32)
             dk_refs[b][0, g] = dk.astype(jnp.bfloat16)
             dv_refs[b][0, g] = dv.astype(jnp.bfloat16)
-        dq_ref[g] = dq.reshape(grp, tok, width)
+        dq_ref[g] = dq
 
 
 def attend_blocks(modes, dist, idx, q4, do4, lse3, delta3, acc, kvs):
@@ -84,16 +84,17 @@
     nb = len(modes)
     valid = jnp.stack([(idx >= d).astype(jnp.int32) for d in dist])
     hspec = pl.BlockSpec((gb, grp, tok, width), lambda i, v: (i, 0, 0, 0))
+    tspec = pl.BlockSpec((gb, width, grp * tok), lambda i, v: (i, 0, 0))
     rspec = pl.BlockSpec((gb, 1, grp * tok), lambda i, v: (i, 0, 0))
     kvspec = pl.BlockSpec((1, gb, tok, width), lambda i, v: (0, i, 0, 0))
     accs = [] if acc is None else [acc]
-    out_shape = [jax.ShapeDtypeStruct(q4.shape, jnp.float32)]
+    out_shape = [jax.ShapeDtypeStruct((nh, width, grp * tok), jnp.float32)]
     out_shape += [jax.ShapeDtypeStruct(kv.shape, jnp.bfloat16) for kv in kvs]
     grid_spec = pltpu.PrefetchScalarGridSpec(
         num_scalar_prefetch=1,
         grid=(nh // gb,),
-        in_specs=[hspec, hspec, rspec, rspec] + [hspec] * len(accs) + [kvspec] * (2 * nb),
-        out_specs=[hspec] + [kvspec] * (2 * nb),
+        in_specs=[hspec, hspec, rspec, rspec] + [tspec] * len(accs) + [kvspec] * (2 * nb),
+        out_specs=[tspec] + [kvspec] * (2 * nb),
     )
     scores = nh * grp * tok * tok * nb
     cost = pl.CostEstimate(
@@ -172,7 +173,8 @@
     grad_k = unroute(terms[:9], n, half, core)
     grad_v = unroute(terms[9:], n, half, core)
 
-    grad_query = (acc * SCALE).astype(jnp.bfloat16).reshape(heads_q, tok, width).transpose(1, 0, 2)
+    dq = (acc * SCALE).astype(jnp.bfloat16).reshape(heads_kv, width, groups, tok)
+    grad_query = dq.transpose(3, 0, 2, 1).reshape(tok, heads_q, width)
     return (grad_query, grad_k[0].transpose(1, 0, 2), grad_v[0].transpose(1, 0, 2))
 
 

time: 196 us -> 197 us (level)
  waiting for transfers between devices: 80.1 us -> 74.3 us
  other arithmetic: 16.1 us -> 20.1 us
  local copies, waits for them, and re-layouts: 12.4 us -> 14.8 us
    ppermute x8, waiting for transfers between devices: 25.7 us -> 21.6 us  [shift(): return lax.ppermute(x, 'seq', pairs)]
    transpose x0 -> x1, local copies, waits for them, and re-layouts: none -> 3.76 us  [per_device(): grad_query = dq.transpose(3, 0, 2, 1).reshape(tok, heads_q, width)]
    unnamed x54 -> x62, local copies, waits for them, and re-layouts: 7.24 us -> 7.26 us
  transfers between devices with their start and end apart: 38 -> 38, of which waited for: 19 -> 18; matrix products, arithmetic and copies ran while one was open for 12% -> 15% of each run, Pallas kernels for 0% -> 0%
where the time goes in v6:
time: 197 us; the launch traced here: 196 us
  waiting for transfers between devices  74.3 us (38%)
  starting transfers between devices  53.5 us (27%)
  Pallas kernels  31.9 us (16%)
  other arithmetic  20.1 us (10%)
  local copies, waits for them, and re-layouts  14.8 us (8%)
    ppermute x18, waiting for transfers between devices, swap(): return lax.ppermute(x, 'seq', [(i, i ^ bit) for i in range(n)])  38 us
    pallas_call x1, Pallas kernels, attend_blocks(): pl.pallas_call(functools.partial(_blocks_kernel, tuple(modes), acc is not...  31.9 us
    ppermute x8, starting transfers between devices, shift(): return lax.ppermute(x, 'seq', pairs)  25 us
    ppermute x12, starting transfers between devices, one_way(): return lax.ppermute(x, 'seq', pairs)  22.5 us
    ppermute x8, waiting for transfers between devices, shift(): return lax.ppermute(x, 'seq', pairs)  21.6 us
    ppermute x12, waiting for transfers between devices, one_way(): return lax.ppermute(x, 'seq', pairs)  14.8 us
    unnamed x62, local copies, waits for them, and re-layouts  7.26 us
    ppermute x18, starting transfers between devices, swap(): return lax.ppermute(x, 'seq', [(i, i ^ bit) for i in range(n)])  6.08 us
  transfers between devices with their start and end apart: 38, of which 18 were waited for; matrix products, arithmetic and copies ran while one was open for 15% of the time, Pallas kernels for 0%

profile of v6, /device:TPU:0, one launch (start us, length us, event | category | flops | bytes accessed | tf_op | source)
XLA Modules:
  0.0 195.9 jit_solution(16599151794673876051)
XLA Ops:
  0.7 1.3 copy.26
  2.0 5.7 %collective-permute-start.11 = (bf16[1,16,128,128]{3,2,1,0:T(8,128)(2,1)S(1)}, bf16[1,16,128,128]{3,2,1,0:T(8,128)(2,1)}, u32[]{:S(2)}, u32[]{:S(2)}) collective-permute-start(bf16[1,16,128,128]{3,2,1,0:T(8,128)(2,1)S(1)} %bitcast.42), channel_id=1, source_target_pairs={{0,8},{2,10},{4,12},{6,14},{8,16},{10,18},{12,20},{14,22},{16,24},... | collective-permute-start | bytes 1572872 | tf_op jit(solution)/shard_map/ppermute | solution.py:20
  7.7 2.0 %copy.27 = bf16[128,16,128]{2,0,1:T(8,128)(2,1)} copy(bf16[128,16,128]{2,1,0:T(8,128)(2,1)} %param.7) | data formatting | bytes 1048576 | tf_op args[1]
  9.7 3.5 %collective-permute-start = (bf16[1,16,128,128]{3,2,1,0:T(8,128)(2,1)}, bf16[1,16,128,128]{3,2,1,0:T(8,128)(2,1)}, u32[]{:S(2)}, u32[]{:S(2)}) collective-permute-start(bf16[1,16,128,128]{3,2,1,0:T(8,128)(2,1)} %bitcast.35.refs_0_), channel_id=1, source_target_pairs={{0,8},{2,10},{4,12},{6,14},{8,16},{10,18},{12,20},{14,22},{16,24},... | collective-permute-start | bytes 1572872 | tf_op jit(solution)/shard_map/ppermute | solution.py:20
  13.2 3.4 %collective-permute-start.16 = (bf16[1,16,128,128]{3,2,1,0:T(8,128)(2,1)S(1)}, bf16[1,16,128,128]{3,2,1,0:T(8,128)(2,1)S(1)}, u32[]{:S(2)}, u32[]{:S(2)}) collective-permute-start(bf16[1,16,128,128]{3,2,1,0:T(8,128)(2,1)S(1)} %bitcast.43), channel_id=1, source_target_pairs={{0,4},{2,6},{8,12},{10,14},{16,20},{18,22},{24,28},{26,30},{1,5},{... | collective-permute-start | bytes 1572872 | tf_op jit(solution)/shard_map/ppermute | solution.py:29
  16.6 2.1 %collective-permute-start.5 = (bf16[1,16,128,128]{3,2,1,0:T(8,128)(2,1)}, bf16[1,16,128,128]{3,2,1,0:T(8,128)(2,1)}, u32[]{:S(2)}, u32[]{:S(2)}) collective-permute-start(bf16[1,16,128,128]{3,2,1,0:T(8,128)(2,1)} %bitcast.35.refs_0_), channel_id=1, source_target_pairs={{0,4},{2,6},{8,12},{10,14},{16,20},{18,22},{24,28},{26,30},{1,5},{... | collective-permute-start | bytes 1572872 | tf_op jit(solution)/shard_map/ppermute | solution.py:29
  18.8 0.5 collective-permute-done.11.refs_10_
  19.2 1.3 collective-permute-start.17
  20.5 5.3 %collective-permute-start.13 = (bf16[1,16,128,128]{3,2,1,0:T(8,128)(2,1)}, bf16[1,16,128,128]{3,2,1,0:T(8,128)(2,1)}, u32[]{:S(2)}, u32[]{:S(2)}) collective-permute-start(bf16[1,16,128,128]{3,2,1,0:T(8,128)(2,1)} %collective-permute-done.11.refs_10_), channel_id=1, source_target_pairs={{0,8},{2,10},{4,12},{6,14},{8,16},{10,18},{12,20},{14,22},{16,24},... | collective-permute-start | bytes 1572872 | tf_op jit(solution)/shard_map/ppermute | solution.py:20
  25.8 4.8 %collective-permute-done.refs_1_ = bf16[1,16,128,128]{3,2,1,0:T(8,128)(2,1)} collective-permute-done((bf16[1,16,128,128]{3,2,1,0:T(8,128)(2,1)}, bf16[1,16,128,128]{3,2,1,0:T(8,128)(2,1)}, u32[]{:S(2)}, u32[]{:S(2)}) %collective-permute-start) | collective-permute-done | bytes 524320 | tf_op jit(solution)/shard_map/ppermute | solution.py:20
  30.6 5.2 %collective-permute-start.2 = (bf16[1,16,128,128]{3,2,1,0:T(8,128)(2,1)}, bf16[1,16,128,128]{3,2,1,0:T(8,128)(2,1)}, u32[]{:S(2)}, u32[]{:S(2)}) collective-permute-start(bf16[1,16,128,128]{3,2,1,0:T(8,128)(2,1)} %collective-permute-done.refs_1_), channel_id=1, source_target_pairs={{0,8},{2,10},{4,12},{6,14},{8,16},{10,18},{12,20},{14,22},{16,24},... | collective-permute-start | bytes 1572872 | tf_op jit(solution)/shard_map/ppermute | solution.py:20
  35.8 0.8 copy-done.13
  36.6 1.3 collective-permute-start.6
  38.0 0.6 stack.51.valid_ref
  38.6 0.6 multiply_reduce_fusion
  39.3 0.7 copy.18
  39.9 1.4 copy.16
  41.3 1.4 copy.17
  42.7 5.3 %collective-permute-start.19 = (bf16[1,16,128,128]{3,2,1,0:T(8,128)(2,1)}, bf16[1,16,128,128]{3,2,1,0:T(8,128)(2,1)S(1)}, u32[]{:S(2)}, u32[]{:S(2)}) collective-permute-start(bf16[1,16,128,128]{3,2,1,0:T(8,128)(2,1)} %collective-permute-done.11.refs_10_), channel_id=1, source_target_pairs={{0,4},{2,6},{8,12},{10,14},{16,20},{18,22},{24,28},{26,30},{1,5},{... | collective-permute-start | bytes 1572872 | tf_op jit(solution)/shard_map/ppermute | solution.py:29
  48.0 1.3 collective-permute-start.8
  49.4 1.3 collective-permute-start.20
  50.7 1.2 collective-permute-done.2.refs_3_
  51.9 1.3 collective-permute-start.9
  53.2 1.1 broadcast_select_fusion.1.refs_14_
  54.4 1.3 collective-permute-start.14
  55.7 1.1 broadcast_select_fusion.3.refs_5_
  56.8 3.9 %collective-permute-done.19 = bf16[1,16,128,128]{3,2,1,0:T(8,128)(2,1)S(1)} collective-permute-done((bf16[1,16,128,128]{3,2,1,0:T(8,128)(2,1)}, bf16[1,16,128,128]{3,2,1,0:T(8,128)(2,1)S(1)}, u32[]{:S(2)}, u32[]{:S(2)}) %collective-permute-start.19) | collective-permute-done | bytes 524320 | tf_op jit(solution)/shard_map/ppermute | solution.py:29
  60.7 1.3 collective-permute-start.3
  62.0 6.1 %collective-permute-done.8 = bf16[1,16,128,128]{3,2,1,0:T(8,128)(2,1)S(1)} collective-permute-done((bf16[1,16,128,128]{3,2,1,0:T(8,128)(2,1)}, bf16[1,16,128,128]{3,2,1,0:T(8,128)(2,1)S(1)}, u32[]{:S(2)}, u32[]{:S(2)}) %collective-permute-start.8) | collective-permute-done | bytes 524320 | tf_op jit(solution)/shard_map/ppermute | solution.py:29
  68.1 1.3 collective-permute-start.15
  69.4 4.1 %collective-permute-done.9 = bf16[1,16,128,128]{3,2,1,0:T(8,128)(2,1)S(1)} collective-permute-done((bf16[1,16,128,128]{3,2,1,0:T(8,128)(2,1)}, bf16[1,16,128,128]{3,2,1,0:T(8,128)(2,1)S(1)}, u32[]{:S(2)}, u32[]{:S(2)}) %collective-permute-start.9) | collective-permute-done | bytes 524320 | tf_op jit(solution)/shard_map/ppermute | solution.py:29
  73.5 1.3 collective-permute-start.4
  75.0 1.2 collective-permute-start.1
  76.8 0.7 collective-permute-done.4
  77.7 0.8 broadcast_select_fusion.4.refs_13_
  78.5 0.8 broadcast_select_fusion.5.refs_4_
  79.6 0.7 collective-permute-done.21.refs_17_
  80.3 0.7 collective-permute-done.10.refs_8_
  81.1 0.7 copy-done.28
  81.9 31.9 %shard_map.85 = (f32[16,128,256]{2,1,0:T(8,128)}, bf16[1,16,128,128]{3,2,1,0:T(8,128)(2,1)}, bf16[1,16,128,128]{3,2,1,0:T(8,128)(2,1)}, bf16[1,16,128,128]{3,2,1...) custom-call(s32[9]{0:T(128)} %stack.51.valid_ref, ...), custom_call_target="tpu_custom_call" | custom-call | flops 6039797760 | bytes 20971520 | tf_op jit(solution)/shard_map/pallas_call | solution.py:105
  115.2 0.8 collective-permute-done.26
  116.3 1.2 add_convert_fusion.2
  117.6 2.0 %add_convert_fusion.3 = bf16[1,16,128,128]{3,2,1,0:T(8,128)(2,1)} fusion(bf16[1,16,128,128]{3,2,1,0:T(8,128)(2,1)S(1)} %collective-permute-done.23, bf16[1,16,128,128]{3,2,1,0:T(8,128)(2,1)} %get-tuple-element.25), kind=kLoop, calls=%fused_computation.35 | loop fusion | flops 1048576 | bytes 1572864 | tf_op jit(solution)/shard_map/convert_element_type | solution.py:139
  120.2 1.7 collective-permute-start.24
  121.9 10.4 %collective-permute-done.27 = bf16[1,16,128,128]{3,2,1,0:T(8,128)(2,1)S(1)} collective-permute-done((bf16[1,16,128,128]{3,2,1,0:T(8,128)(2,1)S(1)}, bf16[1,16,128,128]{3,2,1,0:T(8,128)(2,1)S(1)}, u32[]{:S(2)}, u32[]{:S(2)}) %collective-permute-start.27) | collective-permute-done | bytes 524320 | tf_op jit(solution)/shard_map/ppermute | solution.py:24
  132.4 1.1 fusion.6
  133.5 1.3 collective-permute-start.28
  134.8 0.9 add_convert_fusion.1
  135.7 18.4 %collective-permute-done.35 = bf16[1,16,128,128]{3,2,1,0:T(8,128)(2,1)S(1)} collective-permute-done((bf16[1,16,128,128]{3,2,1,0:T(8,128)(2,1)S(1)}, bf16[1,16,128,128]{3,2,1,0:T(8,128)(2,1)S(1)}, u32[]{:S(2)}, u32[]{:S(2)}) %collective-permute-start.35) | collective-permute-done | bytes 524320 | tf_op jit(solution)/shard_map/ppermute | solution.py:24
  154.4 1.1 fusion.16
  155.5 1.3 collective-permute-start.36
  156.8 2.8 %fusion.9 = bf16[1,16,128,128]{3,2,1,0:T(8,128)(2,1)} fusion(bf16[1,16,128,128]{3,2,1,0:T(8,128)(2,1)S(1)} %collective-permute-done.24, bf16[1,16,128,128]{3,2,1,0:T(8,128)(2,1)S(1)} %collective-permute-done.27, bf16[1,16,128,128]{3,2,1,0:T(8,128)(2,1)} %collective-permute-done.28, bf16[1,16,128,128]{3,2,1,0:T(8,128)(2,1)} %collective-permute-done.25, ...), kind=kLoop, calls=%fused_computation.21 | loop fusion | flops 2621440 | bytes 3145729 | tf_op jit(solution)/shard_map/convert_element_type | solution.py:147
  159.6 1.4 collective-permute-start.29
  161.0 6.5 %collective-permute-done.32 = bf16[1,16,128,128]{3,2,1,0:T(8,128)(2,1)S(1)} collective-permute-done((bf16[1,16,128,128]{3,2,1,0:T(8,128)(2,1)}, bf16[1,16,128,128]{3,2,1,0:T(8,128)(2,1)S(1)}, u32[]{:S(2)}, u32[]{:S(2)}) %collective-permute-start.32) | collective-permute-done | bytes 524320 | tf_op jit(solution)/shard_map/ppermute | solution.py:24
  167.5 5.0 %collective-permute-done.36 = bf16[1,16,128,128]{3,2,1,0:T(8,128)(2,1)} collective-permute-done((bf16[1,16,128,128]{3,2,1,0:T(8,128)(2,1)}, bf16[1,16,128,128]{3,2,1,0:T(8,128)(2,1)}, u32[]{:S(2)}, u32[]{:S(2)}) %collective-permute-start.36) | collective-permute-done | bytes 524320 | tf_op jit(solution)/shard_map/ppermute | solution.py:20
  172.5 2.4 %fusion.19 = bf16[1,16,128,128]{3,2,1,0:T(8,128)(2,1)} fusion(bf16[1,16,128,128]{3,2,1,0:T(8,128)(2,1)S(1)} %collective-permute-done.32, bf16[1,16,128,128]{3,2,1,0:T(8,128)(2,1)S(1)} %collective-permute-done.35, bf16[1,16,128,128]{3,2,1,0:T(8,128)(2,1)} %collective-permute-done.36, bf16[1,16,128,128]{3,2,1,0:T(8,128)(2,1)} %collective-permute-done.33, ...), kind=kLoop, calls=%fused_computation.31 | loop fusion | flops 2621440 | bytes 3145729 | tf_op jit(solution)/shard_map/convert_element_type | solution.py:147
  175.0 1.3 collective-permute-start.37
  176.9 3.8 %copy.21 = bf16[128,16,2,128]{3,2,1,0:T(2,128)(2,1)} copy(bf16[128,16,2,128]{0,2,3,1:T(2,128)(2,1)S(1)} %bitcast.37) | data formatting | bytes 2097152 | tf_op jit(solution)/shard_map/transpose | solution.py:177
  180.6 3.1 %collective-permute-done.29 = bf16[1,16,128,128]{3,2,1,0:T(8,128)(2,1)} collective-permute-done((bf16[1,16,128,128]{3,2,1,0:T(8,128)(2,1)}, bf16[1,16,128,128]{3,2,1,0:T(8,128)(2,1)}, u32[]{:S(2)}, u32[]{:S(2)}) %collective-permute-start.29) | collective-permute-done | bytes 524320 | tf_op jit(solution)/shard_map/ppermute | solution.py:20
  183.8 1.6 fusion.21
  185.3 1.1 copy.22
  186.5 6.9 %collective-permute-done.37 = bf16[1,16,128,128]{3,2,1,0:T(8,128)(2,1)} collective-permute-done((bf16[1,16,128,128]{3,2,1,0:T(8,128)(2,1)}, bf16[1,16,128,128]{3,2,1,0:T(8,128)(2,1)}, u32[]{:S(2)}, u32[]{:S(2)}) %collective-permute-start.37) | collective-permute-done | bytes 524320 | tf_op jit(solution)/shard_map/ppermute | solution.py:20
  193.4 1.4 fusion.20
  194.8 1.1 copy.23
  (100 shorter events, 4.6 us)
Async XLA Ops:
  0.6 38.0 %copy-start = (bf16[128,32,128]{2,1,0:T(8,128)(2,1)S(1)}, bf16[128,32,128]{2,1,0:T(8,128)(2,1)}, u32[]{:S(2)}) copy-start(bf16[128,32,128]{2,1,0:T(8,128)(2,1)} %param.10) | copy-start | bytes 3145732
  0.6 38.0 %copy-start.6 = (bf16[128,32,128]{2,1,0:T(8,128)(2,1)S(1)}, bf16[128,32,128]{2,1,0:T(8,128)(2,1)}, u32[]{:S(2)}) copy-start(bf16[128,32,128]{2,1,0:T(8,128)(2,1)} %param.9) | copy-start | bytes 3145732
  0.7 39.3 %copy-start.7 = (bf16[128,32,128]{2,1,0:T(8,128)(2,1)S(1)}, bf16[128,32,128]{2,1,0:T(8,128)(2,1)}, u32[]{:S(2)}) copy-start(bf16[128,32,128]{2,1,0:T(8,128)(2,1)} %param.6) | copy-start | bytes 3145732
  2.0 11.2 %copy-start.11 = (bf16[128,16,128]{2,0,1:T(8,128)(2,1)}, bf16[128,16,128]{2,0,1:T(8,128)(2,1)S(1)}, u32[]{:S(2)}) copy-start(bf16[128,16,128]{2,0,1:T(8,128)(2,1)S(1)} %copy.26) | copy-start | bytes 1572868
  2.0 17.2 %collective-permute-start.11 = (bf16[1,16,128,128]{3,2,1,0:T(8,128)(2,1)S(1)}, bf16[1,16,128,128]{3,2,1,0:T(8,128)(2,1)}, u32[]{:S(2)}, u32[]{:S(2)}) collective-permute-start(bf16[1,16,128,128]{3,2,1,0:T(8,128)(2,1)S(1)} %bitcast.42), channel_id=1, source_target_pairs={{0,8},{2,10},{4,12},{6,14},{8,16},{10,18},{12,20},{14,22},{16,24},... | collective-permute-start | bytes 1572872 | tf_op jit(solution)/shard_map/ppermute | solution.py:20
  9.7 20.9 %collective-permute-start = (bf16[1,16,128,128]{3,2,1,0:T(8,128)(2,1)}, bf16[1,16,128,128]{3,2,1,0:T(8,128)(2,1)}, u32[]{:S(2)}, u32[]{:S(2)}) collective-permute-start(bf16[1,16,128,128]{3,2,1,0:T(8,128)(2,1)} %bitcast.35.refs_0_), channel_id=1, source_target_pairs={{0,8},{2,10},{4,12},{6,14},{8,16},{10,18},{12,20},{14,22},{16,24},... | collective-permute-start | bytes 1572872 | tf_op jit(solution)/shard_map/ppermute | solution.py:20
  13.2 22.6 %collective-permute-start.16 = (bf16[1,16,128,128]{3,2,1,0:T(8,128)(2,1)S(1)}, bf16[1,16,128,128]{3,2,1,0:T(8,128)(2,1)S(1)}, u32[]{:S(2)}, u32[]{:S(2)}) collective-permute-start(bf16[1,16,128,128]{3,2,1,0:T(8,128)(2,1)S(1)} %bitcast.43), channel_id=1, source_target_pairs={{0,4},{2,6},{8,12},{10,14},{16,20},{18,22},{24,28},{26,30},{1,5},{... | collective-permute-start | bytes 1572872 | tf_op jit(solution)/shard_map/ppermute | solution.py:29
  16.6 26.1 %collective-permute-start.5 = (bf16[1,16,128,128]{3,2,1,0:T(8,128)(2,1)}, bf16[1,16,128,128]{3,2,1,0:T(8,128)(2,1)}, u32[]{:S(2)}, u32[]{:S(2)}) collective-permute-start(bf16[1,16,128,128]{3,2,1,0:T(8,128)(2,1)} %bitcast.35.refs_0_), channel_id=1, source_target_pairs={{0,4},{2,6},{8,12},{10,14},{16,20},{18,22},{24,28},{26,30},{1,5},{... | collective-permute-start | bytes 1572872 | tf_op jit(solution)/shard_map/ppermute | solution.py:29
  19.2 28.8 %collective-permute-start.17 = (bf16[1,16,128,128]{3,2,1,0:T(8,128)(2,1)}, bf16[1,16,128,128]{3,2,1,0:T(8,128)(2,1)}, u32[]{:S(2)}, u32[]{:S(2)}) collective-permute-start(bf16[1,16,128,128]{3,2,1,0:T(8,128)(2,1)} %collective-permute-done.11.refs_10_), channel_id=1, source_target_pairs={{4,0},{6,2},{12,8},{14,10},{20,16},{22,18},{28,24},{30,26},{5,1},{... | collective-permute-start | bytes 1572872 | tf_op jit(solution)/shard_map/ppermute | solution.py:29
  20.5 28.8 %collective-permute-start.13 = (bf16[1,16,128,128]{3,2,1,0:T(8,128)(2,1)}, bf16[1,16,128,128]{3,2,1,0:T(8,128)(2,1)}, u32[]{:S(2)}, u32[]{:S(2)}) collective-permute-start(bf16[1,16,128,128]{3,2,1,0:T(8,128)(2,1)} %collective-permute-done.11.refs_10_), channel_id=1, source_target_pairs={{0,8},{2,10},{4,12},{6,14},{8,16},{10,18},{12,20},{14,22},{16,24},... | collective-permute-start | bytes 1572872 | tf_op jit(solution)/shard_map/ppermute | solution.py:20
  30.6 21.3 %collective-permute-start.2 = (bf16[1,16,128,128]{3,2,1,0:T(8,128)(2,1)}, bf16[1,16,128,128]{3,2,1,0:T(8,128)(2,1)}, u32[]{:S(2)}, u32[]{:S(2)}) collective-permute-start(bf16[1,16,128,128]{3,2,1,0:T(8,128)(2,1)} %collective-permute-done.refs_1_), channel_id=1, source_target_pairs={{0,8},{2,10},{4,12},{6,14},{8,16},{10,18},{12,20},{14,22},{16,24},... | collective-permute-start | bytes 1572872 | tf_op jit(solution)/shard_map/ppermute | solution.py:20
  36.6 17.8 %collective-permute-start.6 = (bf16[1,16,128,128]{3,2,1,0:T(8,128)(2,1)}, bf16[1,16,128,128]{3,2,1,0:T(8,128)(2,1)}, u32[]{:S(2)}, u32[]{:S(2)}) collective-permute-start(bf16[1,16,128,128]{3,2,1,0:T(8,128)(2,1)} %collective-permute-done.refs_1_), channel_id=1, source_target_pairs={{4,0},{6,2},{12,8},{14,10},{20,16},{22,18},{28,24},{30,26},{5,1},{... | collective-permute-start | bytes 1572872 | tf_op jit(solution)/shard_map/ppermute | solution.py:29
  39.9 13.3 %copy-start.14 = (bf16[1,16,128,128]{3,2,1,0:T(8,128)(2,1)S(1)}, bf16[1,16,128,128]{3,2,1,0:T(8,128)(2,1)}, u32[]{:S(2)}) copy-start(bf16[1,16,128,128]{3,2,1,0:T(8,128)(2,1)} %copy-done.13) | copy-start | bytes 1572868
  41.3 13.0 %copy-start.12 = (bf16[128,16,128]{2,0,1:T(8,128)(2,1)S(1)}, bf16[128,16,128]{2,0,1:T(8,128)(2,1)}, u32[]{:S(2)}) copy-start(bf16[128,16,128]{2,0,1:T(8,128)(2,1)} %copy-done.11) | copy-start | bytes 1572868
  42.7 18.0 %collective-permute-start.19 = (bf16[1,16,128,128]{3,2,1,0:T(8,128)(2,1)}, bf16[1,16,128,128]{3,2,1,0:T(8,128)(2,1)S(1)}, u32[]{:S(2)}, u32[]{:S(2)}) collective-permute-start(bf16[1,16,128,128]{3,2,1,0:T(8,128)(2,1)} %collective-permute-done.11.refs_10_), channel_id=1, source_target_pairs={{0,4},{2,6},{8,12},{10,14},{16,20},{18,22},{24,28},{26,30},{1,5},{... | collective-permute-start | bytes 1572872 | tf_op jit(solution)/shard_map/ppermute | solution.py:29
  48.0 20.1 %collective-permute-start.8 = (bf16[1,16,128,128]{3,2,1,0:T(8,128)(2,1)}, bf16[1,16,128,128]{3,2,1,0:T(8,128)(2,1)S(1)}, u32[]{:S(2)}, u32[]{:S(2)}) collective-permute-start(bf16[1,16,128,128]{3,2,1,0:T(8,128)(2,1)} %collective-permute-done.refs_1_), channel_id=1, source_target_pairs={{0,4},{2,6},{8,12},{10,14},{16,20},{18,22},{24,28},{26,30},{1,5},{... | collective-permute-start | bytes 1572872 | tf_op jit(solution)/shard_map/ppermute | solution.py:29
  49.4 18.8 %collective-permute-start.20 = (bf16[1,16,128,128]{3,2,1,0:T(8,128)(2,1)}, bf16[1,16,128,128]{3,2,1,0:T(8,128)(2,1)S(1)}, u32[]{:S(2)}, u32[]{:S(2)}) collective-permute-start(bf16[1,16,128,128]{3,2,1,0:T(8,128)(2,1)} %collective-permute-done.13.refs_12_), channel_id=1, source_target_pairs={{4,0},{6,2},{12,8},{14,10},{20,16},{22,18},{28,24},{30,26},{5,1},{... | collective-permute-start | bytes 1572872 | tf_op jit(solution)/shard_map/ppermute | solution.py:29
  51.9 21.6 %collective-permute-start.9 = (bf16[1,16,128,128]{3,2,1,0:T(8,128)(2,1)}, bf16[1,16,128,128]{3,2,1,0:T(8,128)(2,1)S(1)}, u32[]{:S(2)}, u32[]{:S(2)}) collective-permute-start(bf16[1,16,128,128]{3,2,1,0:T(8,128)(2,1)} %collective-permute-done.2.refs_3_), channel_id=1, source_target_pairs={{4,0},{6,2},{12,8},{14,10},{20,16},{22,18},{28,24},{30,26},{5,1},{... | collective-permute-start | bytes 1572872 | tf_op jit(solution)/shard_map/ppermute | solution.py:29
  54.3 21.9 %copy-start.15 = (bf16[1,16,128,128]{3,2,1,0:T(8,128)(2,1)}, bf16[1,16,128,128]{3,2,1,0:T(8,128)(2,1)S(1)}, u32[]{:S(2)}) copy-start(bf16[1,16,128,128]{3,2,1,0:T(8,128)(2,1)S(1)} %broadcast_select_fusion.1.refs_14_) | copy-start | bytes 1572868
  54.4 20.6 %collective-permute-start.14 = (bf16[1,16,128,128]{3,2,1,0:T(8,128)(2,1)S(1)}, bf16[1,16,128,128]{3,2,1,0:T(8,128)(2,1)S(1)}, u32[]{:S(2)}, u32[]{:S(2)}) collective-permute-start(bf16[1,16,128,128]{3,2,1,0:T(8,128)(2,1)S(1)} %bitcast.45), channel_id=1, source_target_pairs={{0,2},{4,6},{8,10},{12,14},{16,18},{20,22},{24,26},{28,30},{1,3},{... | collective-permute-start | bytes 1572872 | tf_op jit(solution)/shard_map/ppermute | solution.py:29
  56.8 21.7 %copy-start.16 = (bf16[1,16,128,128]{3,2,1,0:T(8,128)(2,1)}, bf16[1,16,128,128]{3,2,1,0:T(8,128)(2,1)S(1)}, u32[]{:S(2)}) copy-start(bf16[1,16,128,128]{3,2,1,0:T(8,128)(2,1)S(1)} %broadcast_select_fusion.3.refs_5_) | copy-start | bytes 1572868
  60.7 15.5 %collective-permute-start.3 = (bf16[1,16,128,128]{3,2,1,0:T(8,128)(2,1)}, bf16[1,16,128,128]{3,2,1,0:T(8,128)(2,1)S(1)}, u32[]{:S(2)}, u32[]{:S(2)}) collective-permute-start(bf16[1,16,128,128]{3,2,1,0:T(8,128)(2,1)} %bitcast.35.refs_0_), channel_id=1, source_target_pairs={{0,2},{4,6},{8,10},{12,14},{16,18},{20,22},{24,26},{28,30},{1,3},{... | collective-permute-start | bytes 1572872 | tf_op jit(solution)/shard_map/ppermute | solution.py:29
  68.1 8.2 %collective-permute-start.12 = (bf16[1,16,128,128]{3,2,1,0:T(8,128)(2,1)}, bf16[1,16,128,128]{3,2,1,0:T(8,128)(2,1)S(1)}, u32[]{:S(2)}, u32[]{:S(2)}) collective-permute-start(bf16[1,16,128,128]{3,2,1,0:T(8,128)(2,1)} %collective-permute-done.11.refs_10_), channel_id=1, source_target_pairs={{0,2},{2,0},{4,6},{6,4},{8,10},{10,8},{12,14},{14,12},{16,18},{18,... | collective-permute-start | bytes 1572872 | tf_op jit(solution)/shard_map/ppermute | solution.py:24
  68.1 8.6 %collective-permute-start.15 = (bf16[1,16,128,128]{3,2,1,0:T(8,128)(2,1)}, bf16[1,16,128,128]{3,2,1,0:T(8,128)(2,1)S(1)}, u32[]{:S(2)}, u32[]{:S(2)}) collective-permute-start(bf16[1,16,128,128]{3,2,1,0:T(8,128)(2,1)} %collective-permute-done.13.refs_12_), channel_id=1, source_target_pairs={{2,0},{6,4},{10,8},{14,12},{18,16},{22,20},{26,24},{30,28},{3,1},{... | collective-permute-start | bytes 1572872 | tf_op jit(solution)/shard_map/ppermute | solution.py:29
  73.5 4.0 %collective-permute-start.4 = (bf16[1,16,128,128]{3,2,1,0:T(8,128)(2,1)}, bf16[1,16,128,128]{3,2,1,0:T(8,128)(2,1)S(1)}, u32[]{:S(2)}, u32[]{:S(2)}) collective-permute-start(bf16[1,16,128,128]{3,2,1,0:T(8,128)(2,1)} %collective-permute-done.2.refs_3_), channel_id=1, source_target_pairs={{2,0},{6,4},{10,8},{14,12},{18,16},{22,20},{26,24},{30,28},{3,1},{... | collective-permute-start | bytes 1572872 | tf_op jit(solution)/shard_map/ppermute | solution.py:29
  74.9 4.5 %copy-start.17 = (bf16[1,16,128,128]{3,2,1,0:T(8,128)(2,1)}, bf16[1,16,128,128]{3,2,1,0:T(8,128)(2,1)S(1)}, u32[]{:S(2)}) copy-start(bf16[1,16,128,128]{3,2,1,0:T(8,128)(2,1)S(1)} %broadcast_select_fusion.refs_16_) | copy-start | bytes 1572868
  74.9 6.9 %copy-start.18 = (bf16[1,16,128,128]{3,2,1,0:T(8,128)(2,1)}, bf16[1,16,128,128]{3,2,1,0:T(8,128)(2,1)S(1)}, u32[]{:S(2)}) copy-start(bf16[1,16,128,128]{3,2,1,0:T(8,128)(2,1)S(1)} %broadcast_select_fusion.2.refs_7_) | copy-start | bytes 1572868
  75.0 4.4 %collective-permute-start.1 = (bf16[1,16,128,128]{3,2,1,0:T(8,128)(2,1)}, bf16[1,16,128,128]{3,2,1,0:T(8,128)(2,1)S(1)}, u32[]{:S(2)}, u32[]{:S(2)}) collective-permute-start(bf16[1,16,128,128]{3,2,1,0:T(8,128)(2,1)} %collective-permute-done.refs_1_), channel_id=1, source_target_pairs={{0,2},{2,0},{4,6},{6,4},{8,10},{10,8},{12,14},{14,12},{16,18},{18,... | collective-permute-start | bytes 1572872 | tf_op jit(solution)/shard_map/ppermute | solution.py:24
  76.2 3.2 %collective-permute-start.18 = (bf16[1,16,128,128]{3,2,1,0:T(8,128)(2,1)S(1)}, bf16[1,16,128,128]{3,2,1,0:T(8,128)(2,1)S(1)}, u32[]{:S(2)}, u32[]{:S(2)}) collective-permute-start(bf16[1,16,128,128]{3,2,1,0:T(8,128)(2,1)S(1)} %broadcast_select_fusion.1.refs_14_), channel_id=1, source_target_pairs={{0,2},{2,0},{4,6},{6,4},{8,10},{10,8},{12,14},{14,12},{16,18},{18,... | collective-permute-start | bytes 1572872 | tf_op jit(solution)/shard_map/ppermute | solution.py:24
  76.3 5.6 %copy-start.22 = (bf16[1,16,128,128]{3,2,1,0:T(8,128)(2,1)}, bf16[1,16,128,128]{3,2,1,0:T(8,128)(2,1)S(1)}, u32[]{:S(2)}) copy-start(bf16[1,16,128,128]{3,2,1,0:T(8,128)(2,1)S(1)} %collective-permute-done.12.refs_11_) | copy-start | bytes 1572868
  76.3 3.3 %collective-permute-start.7 = (bf16[1,16,128,128]{3,2,1,0:T(8,128)(2,1)S(1)}, bf16[1,16,128,128]{3,2,1,0:T(8,128)(2,1)S(1)}, u32[]{:S(2)}, u32[]{:S(2)}) collective-permute-start(bf16[1,16,128,128]{3,2,1,0:T(8,128)(2,1)S(1)} %broadcast_select_fusion.3.refs_5_), channel_id=1, source_target_pairs={{0,2},{2,0},{4,6},{6,4},{8,10},{10,8},{12,14},{14,12},{16,18},{18,... | collective-permute-start | bytes 1572872 | tf_op jit(solution)/shard_map/ppermute | solution.py:24
  76.7 3.6 %collective-permute-start.21 = (bf16[1,16,128,128]{3,2,1,0:T(8,128)(2,1)S(1)}, bf16[1,16,128,128]{3,2,1,0:T(8,128)(2,1)S(1)}, u32[]{:S(2)}, u32[]{:S(2)}) collective-permute-start(bf16[1,16,128,128]{3,2,1,0:T(8,128)(2,1)S(1)} %broadcast_select_fusion.refs_16_), channel_id=1, source_target_pairs={{0,2},{2,0},{4,6},{6,4},{8,10},{10,8},{12,14},{14,12},{16,18},{18,... | collective-permute-start | bytes 1572872 | tf_op jit(solution)/shard_map/ppermute | solution.py:24
  77.5 3.5 %collective-permute-start.10 = (bf16[1,16,128,128]{3,2,1,0:T(8,128)(2,1)S(1)}, bf16[1,16,128,128]{3,2,1,0:T(8,128)(2,1)S(1)}, u32[]{:S(2)}, u32[]{:S(2)}) collective-permute-start(bf16[1,16,128,128]{3,2,1,0:T(8,128)(2,1)S(1)} %broadcast_select_fusion.2.refs_7_), channel_id=1, source_target_pairs={{0,2},{2,0},{4,6},{6,4},{8,10},{10,8},{12,14},{14,12},{16,18},{18,... | collective-permute-start | bytes 1572872 | tf_op jit(solution)/shard_map/ppermute | solution.py:24
  79.3 2.5 %copy-start.24 = (bf16[1,16,128,128]{3,2,1,0:T(8,128)(2,1)}, bf16[1,16,128,128]{3,2,1,0:T(8,128)(2,1)S(1)}, u32[]{:S(2)}) copy-start(bf16[1,16,128,128]{3,2,1,0:T(8,128)(2,1)S(1)} %collective-permute-done.1.refs_2_) | copy-start | bytes 1572868
  79.3 1.7 copy-start.25
  79.6 1.5 copy-start.26
  113.8 6.3 %copy-start.10 = (bf16[1,16,128,128]{3,2,1,0:T(8,128)(2,1)S(1)}, bf16[1,16,128,128]{3,2,1,0:T(8,128)(2,1)}, u32[]{:S(2)}) copy-start(bf16[1,16,128,128]{3,2,1,0:T(8,128)(2,1)} %get-tuple-element.38) | copy-start | bytes 1572868
  113.8 2.2 %collective-permute-start.26 = (bf16[1,16,128,128]{3,2,1,0:T(8,128)(2,1)}, bf16[1,16,128,128]{3,2,1,0:T(8,128)(2,1)S(1)}, u32[]{:S(2)}, u32[]{:S(2)}) collective-permute-start(bf16[1,16,128,128]{3,2,1,0:T(8,128)(2,1)} %get-tuple-element.30), channel_id=1, source_target_pairs={{0,2},{2,0},{4,6},{6,4},{8,10},{10,8},{12,14},{14,12},{16,18},{18,... | collective-permute-start | bytes 1572872 | tf_op jit(solution)/shard_map/ppermute | solution.py:24
  114.2 3.4 %collective-permute-start.23 = (bf16[1,16,128,128]{3,2,1,0:T(8,128)(2,1)}, bf16[1,16,128,128]{3,2,1,0:T(8,128)(2,1)S(1)}, u32[]{:S(2)}, u32[]{:S(2)}) collective-permute-start(bf16[1,16,128,128]{3,2,1,0:T(8,128)(2,1)} %get-tuple-element.26), channel_id=1, source_target_pairs={{0,2},{2,0},{4,6},{6,4},{8,10},{10,8},{12,14},{14,12},{16,18},{18,... | collective-permute-start | bytes 1572872 | tf_op jit(solution)/shard_map/ppermute | solution.py:24
  114.4 5.4 %copy-start.23 = (bf16[1,16,128,128]{3,2,1,0:T(8,128)(2,1)S(1)}, bf16[1,16,128,128]{3,2,1,0:T(8,128)(2,1)}, u32[]{:S(2)}) copy-start(bf16[1,16,128,128]{3,2,1,0:T(8,128)(2,1)} %get-tuple-element.35) | copy-start | bytes 1572868
  114.4 5.8 %collective-permute-start.22 = (bf16[1,16,128,128]{3,2,1,0:T(8,128)(2,1)}, bf16[1,16,128,128]{3,2,1,0:T(8,128)(2,1)S(1)}, u32[]{:S(2)}, u32[]{:S(2)}) collective-permute-start(bf16[1,16,128,128]{3,2,1,0:T(8,128)(2,1)} %get-tuple-element.24), channel_id=1, source_target_pairs={{0,2},{2,0},{4,6},{6,4},{8,10},{10,8},{12,14},{14,12},{16,18},{18,... | collective-permute-start | bytes 1572872 | tf_op jit(solution)/shard_map/ppermute | solution.py:24
  114.7 40.8 %collective-permute-start.25 = (bf16[1,16,128,128]{3,2,1,0:T(8,128)(2,1)}, bf16[1,16,128,128]{3,2,1,0:T(8,128)(2,1)}, u32[]{:S(2)}, u32[]{:S(2)}) collective-permute-start(bf16[1,16,128,128]{3,2,1,0:T(8,128)(2,1)} %get-tuple-element.28), channel_id=1, source_target_pairs={{0,2},{2,0},{4,6},{6,4},{8,10},{10,8},{12,14},{14,12},{16,18},{18,... | collective-permute-start | bytes 1572872 | tf_op jit(solution)/shard_map/ppermute | solution.py:24
  114.9 20.8 %collective-permute-start.30 = (bf16[1,16,128,128]{3,2,1,0:T(8,128)(2,1)}, bf16[1,16,128,128]{3,2,1,0:T(8,128)(2,1)S(1)}, u32[]{:S(2)}, u32[]{:S(2)}) collective-permute-start(bf16[1,16,128,128]{3,2,1,0:T(8,128)(2,1)} %get-tuple-element.33), channel_id=1, source_target_pairs={{0,2},{2,0},{4,6},{6,4},{8,10},{10,8},{12,14},{14,12},{16,18},{18,... | collective-permute-start | bytes 1572872 | tf_op jit(solution)/shard_map/ppermute | solution.py:24
  116.0 3.7 %collective-permute-start.34 = (bf16[1,16,128,128]{3,2,1,0:T(8,128)(2,1)}, bf16[1,16,128,128]{3,2,1,0:T(8,128)(2,1)S(1)}, u32[]{:S(2)}, u32[]{:S(2)}) collective-permute-start(bf16[1,16,128,128]{3,2,1,0:T(8,128)(2,1)} %get-tuple-element.39), channel_id=1, source_target_pairs={{0,2},{2,0},{4,6},{6,4},{8,10},{10,8},{12,14},{14,12},{16,18},{18,... | collective-permute-start | bytes 1572872 | tf_op jit(solution)/shard_map/ppermute | solution.py:24
  116.3 16.1 %copy-start.21 = (bf16[1,16,128,128]{3,2,1,0:T(8,128)(2,1)S(1)}, bf16[1,16,128,128]{3,2,1,0:T(8,128)(2,1)}, u32[]{:S(2)}) copy-start(bf16[1,16,128,128]{3,2,1,0:T(8,128)(2,1)} %get-tuple-element.31) | copy-start | bytes 1572868
  117.5 14.8 %collective-permute-start.27 = (bf16[1,16,128,128]{3,2,1,0:T(8,128)(2,1)S(1)}, bf16[1,16,128,128]{3,2,1,0:T(8,128)(2,1)S(1)}, u32[]{:S(2)}, u32[]{:S(2)}) collective-permute-start(bf16[1,16,128,128]{3,2,1,0:T(8,128)(2,1)S(1)} %add_convert_fusion.2), channel_id=1, source_target_pairs={{0,4},{2,6},{4,0},{6,2},{8,12},{10,14},{12,8},{14,10},{16,20},{18,... | collective-permute-start | bytes 1572872 | tf_op jit(solution)/shard_map/ppermute | solution.py:24
  119.6 15.1 %copy-start.9 = (bf16[1,16,128,128]{3,2,1,0:T(8,128)(2,1)S(1)}, bf16[1,16,128,128]{3,2,1,0:T(8,128)(2,1)}, u32[]{:S(2)}) copy-start(bf16[1,16,128,128]{3,2,1,0:T(8,128)(2,1)} %get-tuple-element.34) | copy-start | bytes 1572868
  119.7 13.7 %collective-permute-start.31 = (bf16[1,16,128,128]{3,2,1,0:T(8,128)(2,1)S(1)}, bf16[1,16,128,128]{3,2,1,0:T(8,128)(2,1)S(1)}, u32[]{:S(2)}, u32[]{:S(2)}) collective-permute-start(bf16[1,16,128,128]{3,2,1,0:T(8,128)(2,1)S(1)} %copy-done.23), channel_id=1, source_target_pairs={{0,2},{2,0},{4,6},{6,4},{8,10},{10,8},{12,14},{14,12},{16,18},{18,... | collective-permute-start | bytes 1572872 | tf_op jit(solution)/shard_map/ppermute | solution.py:24
  120.2 34.2 %copy-start.20 = (bf16[1,16,128,128]{3,2,1,0:T(8,128)(2,1)S(1)}, bf16[1,16,128,128]{3,2,1,0:T(8,128)(2,1)}, u32[]{:S(2)}) copy-start(bf16[1,16,128,128]{3,2,1,0:T(8,128)(2,1)} %get-tuple-element.40) | copy-start | bytes 1572868
  120.2 36.6 %collective-permute-start.24 = (bf16[1,16,128,128]{3,2,1,0:T(8,128)(2,1)}, bf16[1,16,128,128]{3,2,1,0:T(8,128)(2,1)S(1)}, u32[]{:S(2)}, u32[]{:S(2)}) collective-permute-start(bf16[1,16,128,128]{3,2,1,0:T(8,128)(2,1)} %add_convert_fusion.3), channel_id=1, source_target_pairs={{0,4},{2,6},{4,0},{6,2},{8,12},{10,14},{12,8},{14,10},{16,20},{18,... | collective-permute-start | bytes 1572872 | tf_op jit(solution)/shard_map/ppermute | solution.py:24
  132.4 21.7 %collective-permute-start.35 = (bf16[1,16,128,128]{3,2,1,0:T(8,128)(2,1)S(1)}, bf16[1,16,128,128]{3,2,1,0:T(8,128)(2,1)S(1)}, u32[]{:S(2)}, u32[]{:S(2)}) collective-permute-start(bf16[1,16,128,128]{3,2,1,0:T(8,128)(2,1)S(1)} %add_convert_fusion), channel_id=1, source_target_pairs={{0,4},{2,6},{4,0},{6,2},{8,12},{10,14},{12,8},{14,10},{16,20},{18,... | collective-permute-start | bytes 1572872 | tf_op jit(solution)/shard_map/ppermute | solution.py:24
  133.5 23.3 %collective-permute-start.28 = (bf16[1,16,128,128]{3,2,1,0:T(8,128)(2,1)}, bf16[1,16,128,128]{3,2,1,0:T(8,128)(2,1)}, u32[]{:S(2)}, u32[]{:S(2)}) collective-permute-start(bf16[1,16,128,128]{3,2,1,0:T(8,128)(2,1)} %fusion.6), channel_id=1, source_target_pairs={{8,0},{10,2},{12,4},{14,6},{16,8},{18,10},{20,12},{22,14},{24,16},... | collective-permute-start | bytes 1572872 | tf_op jit(solution)/shard_map/ppermute | solution.py:20
  135.7 25.3 %collective-permute-start.33 = (bf16[1,16,128,128]{3,2,1,0:T(8,128)(2,1)}, bf16[1,16,128,128]{3,2,1,0:T(8,128)(2,1)}, u32[]{:S(2)}, u32[]{:S(2)}) collective-permute-start(bf16[1,16,128,128]{3,2,1,0:T(8,128)(2,1)} %get-tuple-element.37), channel_id=1, source_target_pairs={{0,2},{2,0},{4,6},{6,4},{8,10},{10,8},{12,14},{14,12},{16,18},{18,... | collective-permute-start | bytes 1572872 | tf_op jit(solution)/shard_map/ppermute | solution.py:24
  154.1 13.4 %collective-permute-start.32 = (bf16[1,16,128,128]{3,2,1,0:T(8,128)(2,1)}, bf16[1,16,128,128]{3,2,1,0:T(8,128)(2,1)S(1)}, u32[]{:S(2)}, u32[]{:S(2)}) collective-permute-start(bf16[1,16,128,128]{3,2,1,0:T(8,128)(2,1)} %add_convert_fusion.1), channel_id=1, source_target_pairs={{0,4},{2,6},{4,0},{6,2},{8,12},{10,14},{12,8},{14,10},{16,20},{18,... | collective-permute-start | bytes 1572872 | tf_op jit(solution)/shard_map/ppermute | solution.py:24
  155.5 17.1 %collective-permute-start.36 = (bf16[1,16,128,128]{3,2,1,0:T(8,128)(2,1)}, bf16[1,16,128,128]{3,2,1,0:T(8,128)(2,1)}, u32[]{:S(2)}, u32[]{:S(2)}) collective-permute-start(bf16[1,16,128,128]{3,2,1,0:T(8,128)(2,1)} %fusion.16), channel_id=1, source_target_pairs={{8,0},{10,2},{12,4},{14,6},{16,8},{18,10},{20,12},{22,14},{24,16},... | collective-permute-start | bytes 1572872 | tf_op jit(solution)/shard_map/ppermute | solution.py:20
  156.8 15.8 %copy-start.19 = (bf16[1,16,128,128]{3,2,1,0:T(8,128)(2,1)S(1)}, bf16[1,16,128,128]{3,2,1,0:T(8,128)(2,1)}, u32[]{:S(2)}) copy-start(bf16[1,16,128,128]{3,2,1,0:T(8,128)(2,1)} %get-tuple-element.36) | copy-start | bytes 1572868
  156.8 18.2 %copy-start.2 = (bf16[1,16,128,128]{3,2,1,0:T(8,128)(2,1)}, bf16[1,16,128,128]{3,2,1,0:T(8,128)(2,1)S(1)}, u32[]{:S(2)}) copy-start(bf16[1,16,128,128]{3,2,1,0:T(8,128)(2,1)S(1)} %collective-permute-done.24) | copy-start | bytes 1572868
  159.6 16.7 %copy-start.1 = (f32[16,128,256]{2,1,0:T(8,128)S(1)}, f32[16,128,256]{2,1,0:T(8,128)}, u32[]{:S(2)}) copy-start(f32[16,128,256]{2,1,0:T(8,128)} %get-tuple-element.22) | copy-start | bytes 6291460
  159.6 24.2 %collective-permute-start.29 = (bf16[1,16,128,128]{3,2,1,0:T(8,128)(2,1)}, bf16[1,16,128,128]{3,2,1,0:T(8,128)(2,1)}, u32[]{:S(2)}, u32[]{:S(2)}) collective-permute-start(bf16[1,16,128,128]{3,2,1,0:T(8,128)(2,1)} %fusion.9), channel_id=1, source_target_pairs={{8,0},{10,2},{12,4},{14,6},{16,8},{18,10},{20,12},{22,14},{24,16},... | collective-permute-start | bytes 1572872 | tf_op jit(solution)/shard_map/ppermute | solution.py:20
  167.5 8.8 %copy-start.4 = (bf16[1,16,128,128]{3,2,1,0:T(8,128)(2,1)}, bf16[1,16,128,128]{3,2,1,0:T(8,128)(2,1)S(1)}, u32[]{:S(2)}) copy-start(bf16[1,16,128,128]{3,2,1,0:T(8,128)(2,1)S(1)} %collective-permute-done.32) | copy-start | bytes 1572868
  175.0 18.4 %collective-permute-start.37 = (bf16[1,16,128,128]{3,2,1,0:T(8,128)(2,1)}, bf16[1,16,128,128]{3,2,1,0:T(8,128)(2,1)}, u32[]{:S(2)}, u32[]{:S(2)}) collective-permute-start(bf16[1,16,128,128]{3,2,1,0:T(8,128)(2,1)} %fusion.19), channel_id=1, source_target_pairs={{8,0},{10,2},{12,4},{14,6},{16,8},{18,10},{20,12},{22,14},{24,16},... | collective-permute-start | bytes 1572872 | tf_op jit(solution)/shard_map/ppermute | solution.py:20
  176.8 6.9 %copy-start.3 = (bf16[1,16,128,128]{3,2,1,0:T(8,128)(2,1)S(1)}, bf16[1,16,128,128]{3,2,1,0:T(8,128)(2,1)}, u32[]{:S(2)}) copy-start(bf16[1,16,128,128]{3,2,1,0:T(8,128)(2,1)} %copy-done.2) | copy-start | bytes 1572868
  180.6 12.8 %copy-start.5 = (bf16[1,16,128,128]{3,2,1,0:T(8,128)(2,1)S(1)}, bf16[1,16,128,128]{3,2,1,0:T(8,128)(2,1)}, u32[]{:S(2)}) copy-start(bf16[1,16,128,128]{3,2,1,0:T(8,128)(2,1)} %copy-done.4) | copy-start | bytes 1572868
  180.6 12.8 %copy-start.8 = (bf16[1,16,128,128]{3,2,1,0:T(8,128)(2,1)S(1)}, bf16[1,16,128,128]{3,2,1,0:T(8,128)(2,1)}, u32[]{:S(2)}) copy-start(bf16[1,16,128,128]{3,2,1,0:T(8,128)(2,1)} %get-tuple-element.32) | copy-start | bytes 1572868
  (3 other events, 2.4 us)

commit v7 on v6

--- a/solution.py
+++ b/solution.py
@@ -130,14 +130,23 @@
     return [x0, x1, cx1, x2, cxo, y0, d0, y1, d1]
 
 
-def unroute(terms, n, half, core):
+def gather_y(terms, n):
     tx0, tx1, tcx1, tx2, tcxo, ty0, td0, ty1, td1 = terms
     f32 = jnp.float32
     bf16 = jnp.bfloat16
+    ys0 = (ty0.astype(f32) + swap(td0, n, 1).astype(f32)).astype(bf16)
+    ys1 = (ty1.astype(f32) + swap(td1, n, 1).astype(f32)).astype(bf16)
+    return ys0, ys1
+
+
+def unroute(terms, ys0, ys1, n, half, core):
+    tx0, tx1, tcx1, tx2, tcxo, ty0, td0, ty1, td1 = terms
+    f32 = jnp.float32
+    bf16 = jnp.bfloat16
+    yret0 = swap(ys0, n, 2).astype(f32)
+    yret1 = swap(ys1, n, 2).astype(f32)
+    ro = swap(tcxo, n, 1).astype(f32)
     r1 = swap(tcx1, n, 1).astype(f32)
-    ro = swap(tcxo, n, 1).astype(f32)
-    yret0 = swap((ty0.astype(f32) + swap(td0, n, 1).astype(f32)).astype(bf16), n, 2).astype(f32)
-    yret1 = swap((ty1.astype(f32) + swap(td1, n, 1).astype(f32)).astype(bf16), n, 2).astype(f32)
     zero = jnp.zeros_like(r1)
     lo = half == 0
     part2 = tx2.astype(f32) + jnp.where(core == 1, ro, zero) + jnp.where(lo, zero, yret1)
@@ -166,12 +175,26 @@
     kb = route(normed_key_rows.transpose(1, 0, 2)[None], n, half, core)
     vb = route(value_rows.transpose(1, 0, 2)[None], n, half, core)
 
-    acc, terms = attend_blocks(
-        [0, 1, 1, 2, 1, 1, 1, 1, 1],
-        [0, PLANE, 3 + 2 * core, 2 * PLANE, 7 - 6 * core, 2, 1 + 2 * core, 6, 5 + 2 * core],
-        idx, q4, do4, lse3, delta3, None, kb + vb)
-    grad_k = unroute(terms[:9], n, half, core)
-    grad_v = unroute(terms[9:], n, half, core)
+    late = [3, 4, 5, 6, 7, 8]
+    early = [0, 1, 2]
+    modes = [0, 1, 1, 2, 1, 1, 1, 1, 1]
+    dist = [0, PLANE, 3 + 2 * core, 2 * PLANE, 7 - 6 * core, 2, 1 + 2 * core, 6, 5 + 2 * core]
+    terms = [None] * 18
+    acc = None
+    ys = None
+    qb = q4
+    for sel in (late, early):
+        acc, out = attend_blocks(
+            [modes[j] for j in sel], [dist[j] for j in sel], idx, qb, do4, lse3, delta3, acc,
+            [kb[j] for j in sel] + [vb[j] for j in sel])
+        for m, j in enumerate(sel):
+            terms[j] = out[m]
+            terms[9 + j] = out[len(sel) + m]
+        if ys is None:
+            ys = gather_y(terms[:9], n) + gather_y(terms[9:], n)
+            ys, qb = lax.optimization_barrier((ys, q4))
+    grad_k = unroute(terms[:9], ys[0], ys[1], n, half, core)
+    grad_v = unroute(terms[9:], ys[2], ys[3], n, half, core)
 
     dq = (acc * SCALE).astype(jnp.bfloat16).reshape(heads_kv, width, groups, tok)
     grad_query = dq.transpose(3, 0, 2, 1).reshape(tok, heads_q, width)

time: 197 us -> 188 us (0.954)
  waiting for transfers between devices: 74.3 us -> 52.6 us
  starting transfers between devices: 53.5 us -> 60.2 us
  Pallas kernels: 31.9 us -> 36 us
  other arithmetic: 20.1 us -> 22.5 us
    ppermute x18, waiting for transfers between devices: 38 us -> 21.4 us  [swap(): return lax.ppermute(x, 'seq', [(i, i ^ bit) for i in range(n)])]
    ppermute x12, starting transfers between devices: 22.5 us -> 28.8 us  [one_way(): return lax.ppermute(x, 'seq', pairs)]
    pallas_call x1 -> x2, Pallas kernels: 31.9 us -> 36 us  [attend_blocks(): pl.pallas_call(functools.partial(_blocks_kernel, tuple(modes), acc is not...]
    ppermute x12, waiting for transfers between devices: 14.8 us -> 12 us  [one_way(): return lax.ppermute(x, 'seq', pairs)]
    ppermute x8, waiting for transfers between devices: 21.6 us -> 19.2 us  [shift(): return lax.ppermute(x, 'seq', pairs)]
    unnamed x62 -> x56, local copies, waits for them, and re-layouts: 7.26 us -> 6.47 us
  transfers between devices with their start and end apart: 38 -> 38, of which waited for: 18 -> 14; matrix products, arithmetic and copies ran while one was open for 15% -> 17% of each run, Pallas kernels for 0% -> 7%
where the time goes in v7:
time: 188 us; the launch traced here: 187 us
  starting transfers between devices  60.2 us (32%)
  waiting for transfers between devices  52.6 us (28%)
  Pallas kernels  36 us (19%)
  other arithmetic  22.5 us (12%)
  local copies, waits for them, and re-layouts  14.1 us (8%)
    pallas_call x2, Pallas kernels, attend_blocks(): pl.pallas_call(functools.partial(_blocks_kernel, tuple(modes), acc is not...  36 us
    ppermute x12, starting transfers between devices, one_way(): return lax.ppermute(x, 'seq', pairs)  28.8 us
    ppermute x8, starting transfers between devices, shift(): return lax.ppermute(x, 'seq', pairs)  23.6 us
    ppermute x18, waiting for transfers between devices, swap(): return lax.ppermute(x, 'seq', [(i, i ^ bit) for i in range(n)])  21.4 us
    ppermute x8, waiting for transfers between devices, shift(): return lax.ppermute(x, 'seq', pairs)  19.2 us
    ppermute x12, waiting for transfers between devices, one_way(): return lax.ppermute(x, 'seq', pairs)  12 us
    ppermute x18, starting transfers between devices, swap(): return lax.ppermute(x, 'seq', [(i, i ^ bit) for i in range(n)])  7.78 us
    unnamed x56, local copies, waits for them, and re-layouts  6.47 us
  transfers between devices with their start and end apart: 38, of which 14 were waited for; matrix products, arithmetic and copies ran while one was open for 17% of the time, Pallas kernels for 7%

profile of v7, /device:TPU:0, one launch (start us, length us, event | category | flops | bytes accessed | tf_op | source)
XLA Modules:
  0.0 186.6 jit_solution(13274875400342766569)
XLA Ops:
  0.7 1.3 copy.27
  2.0 5.7 %collective-permute-start = (bf16[1,16,128,128]{3,2,1,0:T(8,128)(2,1)S(1)}, bf16[1,16,128,128]{3,2,1,0:T(8,128)(2,1)}, u32[]{:S(2)}, u32[]{:S(2)}) collective-permute-start(bf16[1,16,128,128]{3,2,1,0:T(8,128)(2,1)S(1)} %bitcast.44), channel_id=1, source_target_pairs={{0,8},{2,10},{4,12},{6,14},{8,16},{10,18},{12,20},{14,22},{16,24},... | collective-permute-start | bytes 1572872 | tf_op jit(solution)/shard_map/ppermute | solution.py:20
  7.7 1.2 copy.26
  8.9 3.5 %collective-permute-start.10 = (bf16[1,16,128,128]{3,2,1,0:T(8,128)(2,1)S(1)}, bf16[1,16,128,128]{3,2,1,0:T(8,128)(2,1)}, u32[]{:S(2)}, u32[]{:S(2)}) collective-permute-start(bf16[1,16,128,128]{3,2,1,0:T(8,128)(2,1)S(1)} %bitcast.48), channel_id=1, source_target_pairs={{0,8},{2,10},{4,12},{6,14},{8,16},{10,18},{12,20},{14,22},{16,24},... | collective-permute-start | bytes 1572872 | tf_op jit(solution)/shard_map/ppermute | solution.py:20
  12.4 3.4 %collective-permute-start.4 = (bf16[1,16,128,128]{3,2,1,0:T(8,128)(2,1)S(1)}, bf16[1,16,128,128]{3,2,1,0:T(8,128)(2,1)S(1)}, u32[]{:S(2)}, u32[]{:S(2)}) collective-permute-start(bf16[1,16,128,128]{3,2,1,0:T(8,128)(2,1)S(1)} %bitcast.45), channel_id=1, source_target_pairs={{0,4},{2,6},{8,12},{10,14},{16,20},{18,22},{24,28},{26,30},{1,5},{... | collective-permute-start | bytes 1572872 | tf_op jit(solution)/shard_map/ppermute | solution.py:29
  15.9 3.4 %collective-permute-done.refs_2_ = bf16[1,16,128,128]{3,2,1,0:T(8,128)(2,1)} collective-permute-done((bf16[1,16,128,128]{3,2,1,0:T(8,128)(2,1)S(1)}, bf16[1,16,128,128]{3,2,1,0:T(8,128)(2,1)}, u32[]{:S(2)}, u32[]{:S(2)}) %collective-permute-start) | collective-permute-done | bytes 524320 | tf_op jit(solution)/shard_map/ppermute | solution.py:20
  19.2 5.3 %collective-permute-start.1 = (bf16[1,16,128,128]{3,2,1,0:T(8,128)(2,1)}, bf16[1,16,128,128]{3,2,1,0:T(8,128)(2,1)}, u32[]{:S(2)}, u32[]{:S(2)}) collective-permute-start(bf16[1,16,128,128]{3,2,1,0:T(8,128)(2,1)} %collective-permute-done.refs_2_), channel_id=1, source_target_pairs={{0,8},{2,10},{4,12},{6,14},{8,16},{10,18},{12,20},{14,22},{16,24},... | collective-permute-start | bytes 1572872 | tf_op jit(solution)/shard_map/ppermute | solution.py:20
  24.5 1.3 collective-permute-start.5
  25.8 6.2 %collective-permute-start.14 = (bf16[1,16,128,128]{3,2,1,0:T(8,128)(2,1)S(1)}, bf16[1,16,128,128]{3,2,1,0:T(8,128)(2,1)}, u32[]{:S(2)}, u32[]{:S(2)}) collective-permute-start(bf16[1,16,128,128]{3,2,1,0:T(8,128)(2,1)S(1)} %bitcast.49), channel_id=1, source_target_pairs={{0,4},{2,6},{8,12},{10,14},{16,20},{18,22},{24,28},{26,30},{1,5},{... | collective-permute-start | bytes 1572872 | tf_op jit(solution)/shard_map/ppermute | solution.py:29
  32.0 3.8 %collective-permute-start.11 = (bf16[1,16,128,128]{3,2,1,0:T(8,128)(2,1)}, bf16[1,16,128,128]{3,2,1,0:T(8,128)(2,1)}, u32[]{:S(2)}, u32[]{:S(2)}) collective-permute-start(bf16[1,16,128,128]{3,2,1,0:T(8,128)(2,1)} %collective-permute-done.10.refs_5_), channel_id=1, source_target_pairs={{0,8},{2,10},{4,12},{6,14},{8,16},{10,18},{12,20},{14,22},{16,24},... | collective-permute-start | bytes 1572872 | tf_op jit(solution)/shard_map/ppermute | solution.py:20
  35.8 0.8 copy-done.13
  36.6 1.3 collective-permute-start.15
  38.6 1.4 copy.16
  40.0 1.4 copy.17
  41.4 0.6 multiply_reduce_fusion
  42.0 0.7 copy.18
  42.7 5.3 %collective-permute-start.7 = (bf16[1,16,128,128]{3,2,1,0:T(8,128)(2,1)}, bf16[1,16,128,128]{3,2,1,0:T(8,128)(2,1)S(1)}, u32[]{:S(2)}, u32[]{:S(2)}) collective-permute-start(bf16[1,16,128,128]{3,2,1,0:T(8,128)(2,1)} %collective-permute-done.refs_2_), channel_id=1, source_target_pairs={{0,4},{2,6},{8,12},{10,14},{16,20},{18,22},{24,28},{26,30},{1,5},{... | collective-permute-start | bytes 1572872 | tf_op jit(solution)/shard_map/ppermute | solution.py:29
  48.1 1.3 collective-permute-start.8
  49.4 1.1 broadcast_select_fusion.3.refs_2_
  50.5 1.3 collective-permute-start.2
  51.9 3.5 %collective-permute-start.17 = (bf16[1,16,128,128]{3,2,1,0:T(8,128)(2,1)}, bf16[1,16,128,128]{3,2,1,0:T(8,128)(2,1)S(1)}, u32[]{:S(2)}, u32[]{:S(2)}) collective-permute-start(bf16[1,16,128,128]{3,2,1,0:T(8,128)(2,1)} %collective-permute-done.10.refs_5_), channel_id=1, source_target_pairs={{0,4},{2,6},{8,12},{10,14},{16,20},{18,22},{24,28},{26,30},{1,5},{... | collective-permute-start | bytes 1572872 | tf_op jit(solution)/shard_map/ppermute | solution.py:29
  55.5 1.3 collective-permute-start.18
  56.8 1.1 broadcast_select_fusion.1.refs_8_
  57.9 1.2 collective-permute-done.7
  59.1 1.3 collective-permute-start.12
  60.4 3.3 %collective-permute-done.8 = bf16[1,16,128,128]{3,2,1,0:T(8,128)(2,1)S(1)} collective-permute-done((bf16[1,16,128,128]{3,2,1,0:T(8,128)(2,1)}, bf16[1,16,128,128]{3,2,1,0:T(8,128)(2,1)S(1)}, u32[]{:S(2)}, u32[]{:S(2)}) %collective-permute-start.8) | collective-permute-done | bytes 524320 | tf_op jit(solution)/shard_map/ppermute | solution.py:29
  63.7 1.3 collective-permute-start.3
  65.1 3.1 %collective-permute-done.17 = bf16[1,16,128,128]{3,2,1,0:T(8,128)(2,1)S(1)} collective-permute-done((bf16[1,16,128,128]{3,2,1,0:T(8,128)(2,1)}, bf16[1,16,128,128]{3,2,1,0:T(8,128)(2,1)S(1)}, u32[]{:S(2)}, u32[]{:S(2)}) %collective-permute-start.17) | collective-permute-done | bytes 524320 | tf_op jit(solution)/shard_map/ppermute | solution.py:29
  68.2 4.3 %collective-permute-done.18 = bf16[1,16,128,128]{3,2,1,0:T(8,128)(2,1)S(1)} collective-permute-done((bf16[1,16,128,128]{3,2,1,0:T(8,128)(2,1)}, bf16[1,16,128,128]{3,2,1,0:T(8,128)(2,1)S(1)}, u32[]{:S(2)}, u32[]{:S(2)}) %collective-permute-start.18) | collective-permute-done | bytes 524320 | tf_op jit(solution)/shard_map/ppermute | solution.py:29
  72.5 1.3 collective-permute-start.13
  73.9 1.2 collective-permute-start.16
  75.6 0.8 broadcast_select_fusion.5.refs_1_
  76.5 0.9 broadcast_select_fusion.4.refs_7_
  77.8 0.7 collective-permute-done.19.refs_11_
  78.5 0.8 copy-done.25
  79.4 22.6 %shard_map.85 = (f32[16,128,256]{2,1,0:T(8,128)}, bf16[1,16,128,128]{3,2,1,0:T(8,128)(2,1)}, bf16[1,16,128,128]{3,2,1,0:T(8,128)(2,1)}, bf16[1,16,128,128]{3,2,1...) custom-call(s32[6]{0:T(128)} %stack.58.valid_ref, ...), custom_call_target="tpu_custom_call" | custom-call | flops 4026531840 | bytes 14680064 | tf_op jit(solution)/shard_map/pallas_call | solution.py:105
  103.1 1.0 collective-permute-done.20
  104.3 2.0 %add_convert_fusion.3 = bf16[1,16,128,128]{3,2,1,0:T(8,128)(2,1)} fusion(bf16[1,16,128,128]{3,2,1,0:T(8,128)(2,1)S(1)} %collective-permute-done.20, bf16[1,16,128,128]{3,2,1,0:T(8,128)(2,1)} %get-tuple-element.28), kind=kLoop, calls=%fused_computation.35 | loop fusion | flops 1048576 | bytes 1572864 | tf_op jit(solution)/shard_map/convert_element_type | solution.py:137
  106.7 1.2 add_convert_fusion.2
  107.9 1.0 add_convert_fusion.1
  108.9 1.0 add_convert_fusion
  110.0 2.0 %collective-permute-start.35 = (bf16[1,16,128,128]{3,2,1,0:T(8,128)(2,1)}, bf16[1,16,128,128]{3,2,1,0:T(8,128)(2,1)S(1)}, u32[]{:S(2)}, u32[]{:S(2)}) collective-permute-start(bf16[1,16,128,128]{3,2,1,0:T(8,128)(2,1)} %add_convert_fusion), channel_id=1, source_target_pairs={{0,4},{2,6},{4,0},{6,2},{8,12},{10,14},{12,8},{14,10},{16,20},{18,... | collective-permute-start | bytes 1572872 | tf_op jit(solution)/shard_map/ppermute | solution.py:24
  111.9 0.7 add_convert_fusion.4.valid_ref
  112.7 13.5 %shard_map.86 = (f32[16,128,256]{2,1,0:T(8,128)}, bf16[1,16,128,128]{3,2,1,0:T(8,128)(2,1)}, bf16[1,16,128,128]{3,2,1,0:T(8,128)(2,1)}, bf16[1,16,128,128]{3,2,1...) custom-call(s32[3]{0:T(128)} %add_convert_fusion.4.valid_ref, ...), custom_call_target="tpu_custom_call" | custom-call | flops 2013265920 | bytes 10485760 | tf_op jit(solution)/shard_map/pallas_call | solution.py:105
  126.5 2.1 %fusion.6 = bf16[1,16,128,128]{3,2,1,0:T(8,128)(2,1)} fusion(bf16[1,16,128,128]{3,2,1,0:T(8,128)(2,1)S(1)} %collective-permute-done.26, bf16[1,16,128,128]{3,2,1,0:T(8,128)(2,1)S(1)} %collective-permute-done.29, bf16[1,16,128,128]{3,2,1,0:T(8,128)(2,1)} %get-tuple-element.45, pred[]{:T(512)S(6)} %eq.26, pred[]{:T(512)S(6)} %eq.11), kind=kLoop, calls=%fused_computation.18 | loop fusion | flops 2097152 | bytes 2097154 | tf_op jit(solution)/shard_map/convert_element_type | solution.py:154
  128.6 1.3 collective-permute-start.30
  129.9 1.9 collective-permute-start.33
  131.7 4.1 %collective-permute-done.35 = bf16[1,16,128,128]{3,2,1,0:T(8,128)(2,1)S(1)} collective-permute-done((bf16[1,16,128,128]{3,2,1,0:T(8,128)(2,1)}, bf16[1,16,128,128]{3,2,1,0:T(8,128)(2,1)S(1)}, u32[]{:S(2)}, u32[]{:S(2)}) %collective-permute-start.35) | collective-permute-done | bytes 524320 | tf_op jit(solution)/shard_map/ppermute | solution.py:24
  135.8 1.1 fusion.16
  136.9 10.2 %collective-permute-done.27 = bf16[1,16,128,128]{3,2,1,0:T(8,128)(2,1)S(1)} collective-permute-done((bf16[1,16,128,128]{3,2,1,0:T(8,128)(2,1)}, bf16[1,16,128,128]{3,2,1,0:T(8,128)(2,1)S(1)}, u32[]{:S(2)}, u32[]{:S(2)}) %collective-permute-start.27) | collective-permute-done | bytes 524320 | tf_op jit(solution)/shard_map/ppermute | solution.py:24
  147.0 1.3 collective-permute-start.36
  148.4 2.6 %fusion.9 = bf16[1,16,128,128]{3,2,1,0:T(8,128)(2,1)} fusion(bf16[1,16,128,128]{3,2,1,0:T(8,128)(2,1)S(1)} %collective-permute-done.27, bf16[1,16,128,128]{3,2,1,0:T(8,128)(2,1)S(1)} %collective-permute-done.29, bf16[1,16,128,128]{3,2,1,0:T(8,128)(2,1)} %collective-permute-done.30, bf16[1,16,128,128]{3,2,1,0:T(8,128)(2,1)} %collective-permute-done.28, ...), kind=kLoop, calls=%fused_computation.21 | loop fusion | flops 2621440 | bytes 3145729 | tf_op jit(solution)/shard_map/convert_element_type | solution.py:156
  151.0 1.4 collective-permute-start.31
  152.4 5.1 %collective-permute-done.33 = bf16[1,16,128,128]{3,2,1,0:T(8,128)(2,1)S(1)} collective-permute-done((bf16[1,16,128,128]{3,2,1,0:T(8,128)(2,1)}, bf16[1,16,128,128]{3,2,1,0:T(8,128)(2,1)S(1)}, u32[]{:S(2)}, u32[]{:S(2)}) %collective-permute-start.33) | collective-permute-done | bytes 524320 | tf_op jit(solution)/shard_map/ppermute | solution.py:24
  157.5 6.6 %collective-permute-done.36 = bf16[1,16,128,128]{3,2,1,0:T(8,128)(2,1)} collective-permute-done((bf16[1,16,128,128]{3,2,1,0:T(8,128)(2,1)}, bf16[1,16,128,128]{3,2,1,0:T(8,128)(2,1)}, u32[]{:S(2)}, u32[]{:S(2)}) %collective-permute-start.36) | collective-permute-done | bytes 524320 | tf_op jit(solution)/shard_map/ppermute | solution.py:20
  164.1 2.4 %fusion.19 = bf16[1,16,128,128]{3,2,1,0:T(8,128)(2,1)} fusion(bf16[1,16,128,128]{3,2,1,0:T(8,128)(2,1)S(1)} %collective-permute-done.33, bf16[1,16,128,128]{3,2,1,0:T(8,128)(2,1)S(1)} %collective-permute-done.35, bf16[1,16,128,128]{3,2,1,0:T(8,128)(2,1)} %collective-permute-done.36, bf16[1,16,128,128]{3,2,1,0:T(8,128)(2,1)} %collective-permute-done.34, ...), kind=kLoop, calls=%fused_computation.31 | loop fusion | flops 2621440 | bytes 3145729 | tf_op jit(solution)/shard_map/convert_element_type | solution.py:156
  166.6 1.3 collective-permute-start.37
  168.4 3.8 %copy.21 = bf16[128,16,2,128]{3,2,1,0:T(2,128)(2,1)} copy(bf16[128,16,2,128]{0,2,3,1:T(2,128)(2,1)S(1)} %bitcast.37) | data formatting | bytes 2097152 | tf_op jit(solution)/shard_map/transpose | solution.py:200
  172.2 3.2 %collective-permute-done.31 = bf16[1,16,128,128]{3,2,1,0:T(8,128)(2,1)} collective-permute-done((bf16[1,16,128,128]{3,2,1,0:T(8,128)(2,1)}, bf16[1,16,128,128]{3,2,1,0:T(8,128)(2,1)}, u32[]{:S(2)}, u32[]{:S(2)}) %collective-permute-start.31) | collective-permute-done | bytes 524320 | tf_op jit(solution)/shard_map/ppermute | solution.py:20
  175.3 1.6 fusion.21
  176.9 1.1 copy.22
  178.0 6.0 %collective-permute-done.37 = bf16[1,16,128,128]{3,2,1,0:T(8,128)(2,1)} collective-permute-done((bf16[1,16,128,128]{3,2,1,0:T(8,128)(2,1)}, bf16[1,16,128,128]{3,2,1,0:T(8,128)(2,1)}, u32[]{:S(2)}, u32[]{:S(2)}) %collective-permute-start.37) | collective-permute-done | bytes 524320 | tf_op jit(solution)/shard_map/ppermute | solution.py:20
  184.1 1.4 fusion.20
  185.5 1.1 copy.23
  (96 shorter events, 4.7 us)
Async XLA Ops:
  0.6 38.0 %copy-start.6 = (bf16[128,32,128]{2,1,0:T(8,128)(2,1)S(1)}, bf16[128,32,128]{2,1,0:T(8,128)(2,1)}, u32[]{:S(2)}) copy-start(bf16[128,32,128]{2,1,0:T(8,128)(2,1)} %param.6) | copy-start | bytes 3145732
  0.6 39.3 %copy-start = (bf16[128,32,128]{2,1,0:T(8,128)(2,1)S(1)}, bf16[128,32,128]{2,1,0:T(8,128)(2,1)}, u32[]{:S(2)}) copy-start(bf16[128,32,128]{2,1,0:T(8,128)(2,1)} %param.10) | copy-start | bytes 3145732
  2.0 48.5 %copy-start.11 = (bf16[128,16,128]{2,0,1:T(8,128)(2,1)}, bf16[128,16,128]{2,0,1:T(8,128)(2,1)S(1)}, u32[]{:S(2)}) copy-start(bf16[128,16,128]{2,0,1:T(8,128)(2,1)S(1)} %copy.27) | copy-start | bytes 1572868
  2.0 17.2 %collective-permute-start = (bf16[1,16,128,128]{3,2,1,0:T(8,128)(2,1)S(1)}, bf16[1,16,128,128]{3,2,1,0:T(8,128)(2,1)}, u32[]{:S(2)}, u32[]{:S(2)}) collective-permute-start(bf16[1,16,128,128]{3,2,1,0:T(8,128)(2,1)S(1)} %bitcast.44), channel_id=1, source_target_pairs={{0,8},{2,10},{4,12},{6,14},{8,16},{10,18},{12,20},{14,22},{16,24},... | collective-permute-start | bytes 1572872 | tf_op jit(solution)/shard_map/ppermute | solution.py:20
  8.9 50.2 %copy-start.12 = (bf16[128,16,128]{2,0,1:T(8,128)(2,1)}, bf16[128,16,128]{2,0,1:T(8,128)(2,1)S(1)}, u32[]{:S(2)}) copy-start(bf16[128,16,128]{2,0,1:T(8,128)(2,1)S(1)} %copy.26) | copy-start | bytes 1572868
  8.9 23.0 %collective-permute-start.10 = (bf16[1,16,128,128]{3,2,1,0:T(8,128)(2,1)S(1)}, bf16[1,16,128,128]{3,2,1,0:T(8,128)(2,1)}, u32[]{:S(2)}, u32[]{:S(2)}) collective-permute-start(bf16[1,16,128,128]{3,2,1,0:T(8,128)(2,1)S(1)} %bitcast.48), channel_id=1, source_target_pairs={{0,8},{2,10},{4,12},{6,14},{8,16},{10,18},{12,20},{14,22},{16,24},... | collective-permute-start | bytes 1572872 | tf_op jit(solution)/shard_map/ppermute | solution.py:20
  12.4 23.3 %collective-permute-start.4 = (bf16[1,16,128,128]{3,2,1,0:T(8,128)(2,1)S(1)}, bf16[1,16,128,128]{3,2,1,0:T(8,128)(2,1)S(1)}, u32[]{:S(2)}, u32[]{:S(2)}) collective-permute-start(bf16[1,16,128,128]{3,2,1,0:T(8,128)(2,1)S(1)} %bitcast.45), channel_id=1, source_target_pairs={{0,4},{2,6},{8,12},{10,14},{16,20},{18,22},{24,28},{26,30},{1,5},{... | collective-permute-start | bytes 1572872 | tf_op jit(solution)/shard_map/ppermute | solution.py:29
  19.2 23.5 %collective-permute-start.1 = (bf16[1,16,128,128]{3,2,1,0:T(8,128)(2,1)}, bf16[1,16,128,128]{3,2,1,0:T(8,128)(2,1)}, u32[]{:S(2)}, u32[]{:S(2)}) collective-permute-start(bf16[1,16,128,128]{3,2,1,0:T(8,128)(2,1)} %collective-permute-done.refs_2_), channel_id=1, source_target_pairs={{0,8},{2,10},{4,12},{6,14},{8,16},{10,18},{12,20},{14,22},{16,24},... | collective-permute-start | bytes 1572872 | tf_op jit(solution)/shard_map/ppermute | solution.py:20
  24.5 23.6 %collective-permute-start.5 = (bf16[1,16,128,128]{3,2,1,0:T(8,128)(2,1)}, bf16[1,16,128,128]{3,2,1,0:T(8,128)(2,1)}, u32[]{:S(2)}, u32[]{:S(2)}) collective-permute-start(bf16[1,16,128,128]{3,2,1,0:T(8,128)(2,1)} %collective-permute-done.refs_2_), channel_id=1, source_target_pairs={{4,0},{6,2},{12,8},{14,10},{20,16},{22,18},{28,24},{30,26},{5,1},{... | collective-permute-start | bytes 1572872 | tf_op jit(solution)/shard_map/ppermute | solution.py:29
  25.8 24.7 %collective-permute-start.14 = (bf16[1,16,128,128]{3,2,1,0:T(8,128)(2,1)S(1)}, bf16[1,16,128,128]{3,2,1,0:T(8,128)(2,1)}, u32[]{:S(2)}, u32[]{:S(2)}) collective-permute-start(bf16[1,16,128,128]{3,2,1,0:T(8,128)(2,1)S(1)} %bitcast.49), channel_id=1, source_target_pairs={{0,4},{2,6},{8,12},{10,14},{16,20},{18,22},{24,28},{26,30},{1,5},{... | collective-permute-start | bytes 1572872 | tf_op jit(solution)/shard_map/ppermute | solution.py:29
  32.0 19.9 %collective-permute-start.11 = (bf16[1,16,128,128]{3,2,1,0:T(8,128)(2,1)}, bf16[1,16,128,128]{3,2,1,0:T(8,128)(2,1)}, u32[]{:S(2)}, u32[]{:S(2)}) collective-permute-start(bf16[1,16,128,128]{3,2,1,0:T(8,128)(2,1)} %collective-permute-done.10.refs_5_), channel_id=1, source_target_pairs={{0,8},{2,10},{4,12},{6,14},{8,16},{10,18},{12,20},{14,22},{16,24},... | collective-permute-start | bytes 1572872 | tf_op jit(solution)/shard_map/ppermute | solution.py:20
  35.8 0.8 copy-start.13
  36.6 18.9 %collective-permute-start.15 = (bf16[1,16,128,128]{3,2,1,0:T(8,128)(2,1)}, bf16[1,16,128,128]{3,2,1,0:T(8,128)(2,1)}, u32[]{:S(2)}, u32[]{:S(2)}) collective-permute-start(bf16[1,16,128,128]{3,2,1,0:T(8,128)(2,1)} %collective-permute-done.10.refs_5_), channel_id=1, source_target_pairs={{4,0},{6,2},{12,8},{14,10},{20,16},{22,18},{28,24},{30,26},{5,1},{... | collective-permute-start | bytes 1572872 | tf_op jit(solution)/shard_map/ppermute | solution.py:29
  38.6 2.8 %copy-start.7 = (bf16[128,32,128]{2,1,0:T(8,128)(2,1)S(1)}, bf16[128,32,128]{2,1,0:T(8,128)(2,1)}, u32[]{:S(2)}) copy-start(bf16[128,32,128]{2,1,0:T(8,128)(2,1)} %param.9) | copy-start | bytes 3145732
  40.0 9.4 %copy-start.14 = (bf16[1,16,128,128]{3,2,1,0:T(8,128)(2,1)S(1)}, bf16[1,16,128,128]{3,2,1,0:T(8,128)(2,1)}, u32[]{:S(2)}) copy-start(bf16[1,16,128,128]{3,2,1,0:T(8,128)(2,1)} %copy-done.13) | copy-start | bytes 1572868
  42.7 16.4 %collective-permute-start.7 = (bf16[1,16,128,128]{3,2,1,0:T(8,128)(2,1)}, bf16[1,16,128,128]{3,2,1,0:T(8,128)(2,1)S(1)}, u32[]{:S(2)}, u32[]{:S(2)}) collective-permute-start(bf16[1,16,128,128]{3,2,1,0:T(8,128)(2,1)} %collective-permute-done.refs_2_), channel_id=1, source_target_pairs={{0,4},{2,6},{8,12},{10,14},{16,20},{18,22},{24,28},{26,30},{1,5},{... | collective-permute-start | bytes 1572872 | tf_op jit(solution)/shard_map/ppermute | solution.py:29
  48.1 15.6 %collective-permute-start.8 = (bf16[1,16,128,128]{3,2,1,0:T(8,128)(2,1)}, bf16[1,16,128,128]{3,2,1,0:T(8,128)(2,1)S(1)}, u32[]{:S(2)}, u32[]{:S(2)}) collective-permute-start(bf16[1,16,128,128]{3,2,1,0:T(8,128)(2,1)} %collective-permute-done.1.refs_0_), channel_id=1, source_target_pairs={{4,0},{6,2},{12,8},{14,10},{20,16},{22,18},{28,24},{30,26},{5,1},{... | collective-permute-start | bytes 1572872 | tf_op jit(solution)/shard_map/ppermute | solution.py:29
  50.5 23.4 %copy-start.15 = (bf16[1,16,128,128]{3,2,1,0:T(8,128)(2,1)}, bf16[1,16,128,128]{3,2,1,0:T(8,128)(2,1)S(1)}, u32[]{:S(2)}) copy-start(bf16[1,16,128,128]{3,2,1,0:T(8,128)(2,1)S(1)} %broadcast_select_fusion.3.refs_2_) | copy-start | bytes 1572868
  50.5 23.3 %collective-permute-start.2 = (bf16[1,16,128,128]{3,2,1,0:T(8,128)(2,1)S(1)}, bf16[1,16,128,128]{3,2,1,0:T(8,128)(2,1)S(1)}, u32[]{:S(2)}, u32[]{:S(2)}) collective-permute-start(bf16[1,16,128,128]{3,2,1,0:T(8,128)(2,1)S(1)} %bitcast.46), channel_id=1, source_target_pairs={{0,2},{4,6},{8,10},{12,14},{16,18},{20,22},{24,26},{28,30},{1,3},{... | collective-permute-start | bytes 1572872 | tf_op jit(solution)/shard_map/ppermute | solution.py:29
  51.9 16.3 %collective-permute-start.17 = (bf16[1,16,128,128]{3,2,1,0:T(8,128)(2,1)}, bf16[1,16,128,128]{3,2,1,0:T(8,128)(2,1)S(1)}, u32[]{:S(2)}, u32[]{:S(2)}) collective-permute-start(bf16[1,16,128,128]{3,2,1,0:T(8,128)(2,1)} %collective-permute-done.10.refs_5_), channel_id=1, source_target_pairs={{0,4},{2,6},{8,12},{10,14},{16,20},{18,22},{24,28},{26,30},{1,5},{... | collective-permute-start | bytes 1572872 | tf_op jit(solution)/shard_map/ppermute | solution.py:29
  55.5 17.0 %collective-permute-start.18 = (bf16[1,16,128,128]{3,2,1,0:T(8,128)(2,1)}, bf16[1,16,128,128]{3,2,1,0:T(8,128)(2,1)S(1)}, u32[]{:S(2)}, u32[]{:S(2)}) collective-permute-start(bf16[1,16,128,128]{3,2,1,0:T(8,128)(2,1)} %collective-permute-done.11.refs_6_), channel_id=1, source_target_pairs={{4,0},{6,2},{12,8},{14,10},{20,16},{22,18},{28,24},{30,26},{5,1},{... | collective-permute-start | bytes 1572872 | tf_op jit(solution)/shard_map/ppermute | solution.py:29
  57.9 18.6 %copy-start.16 = (bf16[1,16,128,128]{3,2,1,0:T(8,128)(2,1)}, bf16[1,16,128,128]{3,2,1,0:T(8,128)(2,1)S(1)}, u32[]{:S(2)}) copy-start(bf16[1,16,128,128]{3,2,1,0:T(8,128)(2,1)S(1)} %broadcast_select_fusion.1.refs_8_) | copy-start | bytes 1572868
  59.1 16.0 %collective-permute-start.12 = (bf16[1,16,128,128]{3,2,1,0:T(8,128)(2,1)S(1)}, bf16[1,16,128,128]{3,2,1,0:T(8,128)(2,1)S(1)}, u32[]{:S(2)}, u32[]{:S(2)}) collective-permute-start(bf16[1,16,128,128]{3,2,1,0:T(8,128)(2,1)S(1)} %bitcast.50), channel_id=1, source_target_pairs={{0,2},{4,6},{8,10},{12,14},{16,18},{20,22},{24,26},{28,30},{1,3},{... | collective-permute-start | bytes 1572872 | tf_op jit(solution)/shard_map/ppermute | solution.py:29
  63.7 11.5 %collective-permute-start.3 = (bf16[1,16,128,128]{3,2,1,0:T(8,128)(2,1)}, bf16[1,16,128,128]{3,2,1,0:T(8,128)(2,1)S(1)}, u32[]{:S(2)}, u32[]{:S(2)}) collective-permute-start(bf16[1,16,128,128]{3,2,1,0:T(8,128)(2,1)} %collective-permute-done.1.refs_0_), channel_id=1, source_target_pairs={{2,0},{6,4},{10,8},{14,12},{18,16},{22,20},{26,24},{30,28},{3,1},{... | collective-permute-start | bytes 1572872 | tf_op jit(solution)/shard_map/ppermute | solution.py:29
  65.1 12.3 %copy-start.17 = (bf16[1,16,128,128]{3,2,1,0:T(8,128)(2,1)}, bf16[1,16,128,128]{3,2,1,0:T(8,128)(2,1)S(1)}, u32[]{:S(2)}) copy-start(bf16[1,16,128,128]{3,2,1,0:T(8,128)(2,1)S(1)} %broadcast_select_fusion.2.refs_4_) | copy-start | bytes 1572868
  68.2 9.2 %collective-permute-start.6 = (bf16[1,16,128,128]{3,2,1,0:T(8,128)(2,1)S(1)}, bf16[1,16,128,128]{3,2,1,0:T(8,128)(2,1)S(1)}, u32[]{:S(2)}, u32[]{:S(2)}) collective-permute-start(bf16[1,16,128,128]{3,2,1,0:T(8,128)(2,1)S(1)} %broadcast_select_fusion.3.refs_2_), channel_id=1, source_target_pairs={{0,2},{2,0},{4,6},{6,4},{8,10},{10,8},{12,14},{14,12},{16,18},{18,... | collective-permute-start | bytes 1572872 | tf_op jit(solution)/shard_map/ppermute | solution.py:24
  72.5 4.0 %collective-permute-start.13 = (bf16[1,16,128,128]{3,2,1,0:T(8,128)(2,1)}, bf16[1,16,128,128]{3,2,1,0:T(8,128)(2,1)S(1)}, u32[]{:S(2)}, u32[]{:S(2)}) collective-permute-start(bf16[1,16,128,128]{3,2,1,0:T(8,128)(2,1)} %collective-permute-done.11.refs_6_), channel_id=1, source_target_pairs={{2,0},{6,4},{10,8},{14,12},{18,16},{22,20},{26,24},{30,28},{3,1},{... | collective-permute-start | bytes 1572872 | tf_op jit(solution)/shard_map/ppermute | solution.py:29
  73.9 3.9 %copy-start.18 = (bf16[1,16,128,128]{3,2,1,0:T(8,128)(2,1)}, bf16[1,16,128,128]{3,2,1,0:T(8,128)(2,1)S(1)}, u32[]{:S(2)}) copy-start(bf16[1,16,128,128]{3,2,1,0:T(8,128)(2,1)S(1)} %broadcast_select_fusion.refs_10_) | copy-start | bytes 1572868
  73.9 3.5 %collective-permute-start.16 = (bf16[1,16,128,128]{3,2,1,0:T(8,128)(2,1)S(1)}, bf16[1,16,128,128]{3,2,1,0:T(8,128)(2,1)S(1)}, u32[]{:S(2)}, u32[]{:S(2)}) collective-permute-start(bf16[1,16,128,128]{3,2,1,0:T(8,128)(2,1)S(1)} %broadcast_select_fusion.1.refs_8_), channel_id=1, source_target_pairs={{0,2},{2,0},{4,6},{6,4},{8,10},{10,8},{12,14},{14,12},{16,18},{18,... | collective-permute-start | bytes 1572872 | tf_op jit(solution)/shard_map/ppermute | solution.py:24
  75.1 2.7 %collective-permute-start.9 = (bf16[1,16,128,128]{3,2,1,0:T(8,128)(2,1)S(1)}, bf16[1,16,128,128]{3,2,1,0:T(8,128)(2,1)S(1)}, u32[]{:S(2)}, u32[]{:S(2)}) collective-permute-start(bf16[1,16,128,128]{3,2,1,0:T(8,128)(2,1)S(1)} %broadcast_select_fusion.2.refs_4_), channel_id=1, source_target_pairs={{0,2},{2,0},{4,6},{6,4},{8,10},{10,8},{12,14},{14,12},{16,18},{18,... | collective-permute-start | bytes 1572872 | tf_op jit(solution)/shard_map/ppermute | solution.py:24
  75.2 3.3 %collective-permute-start.19 = (bf16[1,16,128,128]{3,2,1,0:T(8,128)(2,1)S(1)}, bf16[1,16,128,128]{3,2,1,0:T(8,128)(2,1)S(1)}, u32[]{:S(2)}, u32[]{:S(2)}) collective-permute-start(bf16[1,16,128,128]{3,2,1,0:T(8,128)(2,1)S(1)} %broadcast_select_fusion.refs_10_), channel_id=1, source_target_pairs={{0,2},{2,0},{4,6},{6,4},{8,10},{10,8},{12,14},{14,12},{16,18},{18,... | collective-permute-start | bytes 1572872 | tf_op jit(solution)/shard_map/ppermute | solution.py:24
  77.4 1.2 copy-start.22
  77.4 2.0 %copy-start.23 = (bf16[1,16,128,128]{3,2,1,0:T(8,128)(2,1)}, bf16[1,16,128,128]{3,2,1,0:T(8,128)(2,1)S(1)}, u32[]{:S(2)}) copy-start(bf16[1,16,128,128]{3,2,1,0:T(8,128)(2,1)S(1)} %collective-permute-done.16.refs_9_) | copy-start | bytes 1572868
  77.8 1.6 copy-start.24
  78.5 0.8 copy-start.25
  101.9 5.9 %copy-start.10 = (bf16[1,16,128,128]{3,2,1,0:T(8,128)(2,1)S(1)}, bf16[1,16,128,128]{3,2,1,0:T(8,128)(2,1)}, u32[]{:S(2)}) copy-start(bf16[1,16,128,128]{3,2,1,0:T(8,128)(2,1)} %get-tuple-element.32) | copy-start | bytes 1572868
  101.9 2.2 %collective-permute-start.20 = (bf16[1,16,128,128]{3,2,1,0:T(8,128)(2,1)}, bf16[1,16,128,128]{3,2,1,0:T(8,128)(2,1)S(1)}, u32[]{:S(2)}, u32[]{:S(2)}) collective-permute-start(bf16[1,16,128,128]{3,2,1,0:T(8,128)(2,1)} %get-tuple-element.29), channel_id=1, source_target_pairs={{0,2},{2,0},{4,6},{6,4},{8,10},{10,8},{12,14},{14,12},{16,18},{18,... | collective-permute-start | bytes 1572872 | tf_op jit(solution)/shard_map/ppermute | solution.py:24
  102.1 4.2 %collective-permute-start.21 = (bf16[1,16,128,128]{3,2,1,0:T(8,128)(2,1)}, bf16[1,16,128,128]{3,2,1,0:T(8,128)(2,1)S(1)}, u32[]{:S(2)}, u32[]{:S(2)}) collective-permute-start(bf16[1,16,128,128]{3,2,1,0:T(8,128)(2,1)} %get-tuple-element.31), channel_id=1, source_target_pairs={{0,2},{2,0},{4,6},{6,4},{8,10},{10,8},{12,14},{14,12},{16,18},{18,... | collective-permute-start | bytes 1572872 | tf_op jit(solution)/shard_map/ppermute | solution.py:24
  102.5 7.4 %collective-permute-start.24 = (bf16[1,16,128,128]{3,2,1,0:T(8,128)(2,1)}, bf16[1,16,128,128]{3,2,1,0:T(8,128)(2,1)S(1)}, u32[]{:S(2)}, u32[]{:S(2)}) collective-permute-start(bf16[1,16,128,128]{3,2,1,0:T(8,128)(2,1)} %collective-permute-done.refs_2_), channel_id=1, source_target_pairs={{0,2},{2,0},{4,6},{6,4},{8,10},{10,8},{12,14},{14,12},{16,18},{18,... | collective-permute-start | bytes 1572872 | tf_op jit(solution)/shard_map/ppermute | solution.py:24
  102.6 9.9 %collective-permute-start.25 = (bf16[1,16,128,128]{3,2,1,0:T(8,128)(2,1)}, bf16[1,16,128,128]{3,2,1,0:T(8,128)(2,1)}, u32[]{:S(2)}, u32[]{:S(2)}) collective-permute-start(bf16[1,16,128,128]{3,2,1,0:T(8,128)(2,1)} %collective-permute-done.10.refs_5_), channel_id=1, source_target_pairs={{0,2},{2,0},{4,6},{6,4},{8,10},{10,8},{12,14},{14,12},{16,18},{18,... | collective-permute-start | bytes 1572872 | tf_op jit(solution)/shard_map/ppermute | solution.py:24
  103.0 4.8 %collective-permute-start.22 = (bf16[1,16,128,128]{3,2,1,0:T(8,128)(2,1)}, bf16[1,16,128,128]{3,2,1,0:T(8,128)(2,1)S(1)}, u32[]{:S(2)}, u32[]{:S(2)}) collective-permute-start(bf16[1,16,128,128]{3,2,1,0:T(8,128)(2,1)} %get-tuple-element.33), channel_id=1, source_target_pairs={{0,2},{2,0},{4,6},{6,4},{8,10},{10,8},{12,14},{14,12},{16,18},{18,... | collective-permute-start | bytes 1572872 | tf_op jit(solution)/shard_map/ppermute | solution.py:24
  104.1 4.7 %collective-permute-start.23 = (bf16[1,16,128,128]{3,2,1,0:T(8,128)(2,1)}, bf16[1,16,128,128]{3,2,1,0:T(8,128)(2,1)S(1)}, u32[]{:S(2)}, u32[]{:S(2)}) collective-permute-start(bf16[1,16,128,128]{3,2,1,0:T(8,128)(2,1)} %get-tuple-element.35), channel_id=1, source_target_pairs={{0,2},{2,0},{4,6},{6,4},{8,10},{10,8},{12,14},{14,12},{16,18},{18,... | collective-permute-start | bytes 1572872 | tf_op jit(solution)/shard_map/ppermute | solution.py:24
  104.3 4.6 %copy-start.9 = (bf16[1,16,128,128]{3,2,1,0:T(8,128)(2,1)S(1)}, bf16[1,16,128,128]{3,2,1,0:T(8,128)(2,1)}, u32[]{:S(2)}) copy-start(bf16[1,16,128,128]{3,2,1,0:T(8,128)(2,1)} %get-tuple-element.34) | copy-start | bytes 1572868
  106.3 19.9 %collective-permute-start.26 = (bf16[1,16,128,128]{3,2,1,0:T(8,128)(2,1)}, bf16[1,16,128,128]{3,2,1,0:T(8,128)(2,1)S(1)}, u32[]{:S(2)}, u32[]{:S(2)}) collective-permute-start(bf16[1,16,128,128]{3,2,1,0:T(8,128)(2,1)} %get-tuple-element.40), channel_id=1, source_target_pairs={{0,2},{2,0},{4,6},{6,4},{8,10},{10,8},{12,14},{14,12},{16,18},{18,... | collective-permute-start | bytes 1572872 | tf_op jit(solution)/shard_map/ppermute | solution.py:24
  109.8 16.6 %collective-permute-start.29 = (bf16[1,16,128,128]{3,2,1,0:T(8,128)(2,1)S(1)}, bf16[1,16,128,128]{3,2,1,0:T(8,128)(2,1)S(1)}, u32[]{:S(2)}, u32[]{:S(2)}) collective-permute-start(bf16[1,16,128,128]{3,2,1,0:T(8,128)(2,1)S(1)} %add_convert_fusion.2), channel_id=1, source_target_pairs={{0,4},{2,6},{4,0},{6,2},{8,12},{10,14},{12,8},{14,10},{16,20},{18,... | collective-permute-start | bytes 1572872 | tf_op jit(solution)/shard_map/ppermute | solution.py:24
  109.8 20.0 %collective-permute-start.32 = (bf16[1,16,128,128]{3,2,1,0:T(8,128)(2,1)}, bf16[1,16,128,128]{3,2,1,0:T(8,128)(2,1)S(1)}, u32[]{:S(2)}, u32[]{:S(2)}) collective-permute-start(bf16[1,16,128,128]{3,2,1,0:T(8,128)(2,1)} %get-tuple-element.47), channel_id=1, source_target_pairs={{0,2},{2,0},{4,6},{6,4},{8,10},{10,8},{12,14},{14,12},{16,18},{18,... | collective-permute-start | bytes 1572872 | tf_op jit(solution)/shard_map/ppermute | solution.py:24
  110.0 2.6 %copy-start.21 = (bf16[1,16,128,128]{3,2,1,0:T(8,128)(2,1)}, bf16[1,16,128,128]{3,2,1,0:T(8,128)(2,1)S(1)}, u32[]{:S(2)}) copy-start(bf16[1,16,128,128]{3,2,1,0:T(8,128)(2,1)S(1)} %collective-permute-done.24.refs_3_) | copy-start | bytes 1572868
  110.0 25.9 %collective-permute-start.35 = (bf16[1,16,128,128]{3,2,1,0:T(8,128)(2,1)}, bf16[1,16,128,128]{3,2,1,0:T(8,128)(2,1)S(1)}, u32[]{:S(2)}, u32[]{:S(2)}) collective-permute-start(bf16[1,16,128,128]{3,2,1,0:T(8,128)(2,1)} %add_convert_fusion), channel_id=1, source_target_pairs={{0,4},{2,6},{4,0},{6,2},{8,12},{10,14},{12,8},{14,10},{16,20},{18,... | collective-permute-start | bytes 1572872 | tf_op jit(solution)/shard_map/ppermute | solution.py:24
  112.6 34.5 %collective-permute-start.27 = (bf16[1,16,128,128]{3,2,1,0:T(8,128)(2,1)}, bf16[1,16,128,128]{3,2,1,0:T(8,128)(2,1)S(1)}, u32[]{:S(2)}, u32[]{:S(2)}) collective-permute-start(bf16[1,16,128,128]{3,2,1,0:T(8,128)(2,1)} %add_convert_fusion.3), channel_id=1, source_target_pairs={{0,4},{2,6},{4,0},{6,2},{8,12},{10,14},{12,8},{14,10},{16,20},{18,... | collective-permute-start | bytes 1572872 | tf_op jit(solution)/shard_map/ppermute | solution.py:24
  126.2 9.7 %copy-start.19 = (bf16[1,16,128,128]{3,2,1,0:T(8,128)(2,1)S(1)}, bf16[1,16,128,128]{3,2,1,0:T(8,128)(2,1)}, u32[]{:S(2)}) copy-start(bf16[1,16,128,128]{3,2,1,0:T(8,128)(2,1)} %get-tuple-element.52) | copy-start | bytes 1572868
  126.2 22.2 %collective-permute-start.28 = (bf16[1,16,128,128]{3,2,1,0:T(8,128)(2,1)}, bf16[1,16,128,128]{3,2,1,0:T(8,128)(2,1)}, u32[]{:S(2)}, u32[]{:S(2)}) collective-permute-start(bf16[1,16,128,128]{3,2,1,0:T(8,128)(2,1)} %get-tuple-element.43), channel_id=1, source_target_pairs={{0,2},{2,0},{4,6},{6,4},{8,10},{10,8},{12,14},{14,12},{16,18},{18,... | collective-permute-start | bytes 1572872 | tf_op jit(solution)/shard_map/ppermute | solution.py:24
  128.6 19.8 %collective-permute-start.30 = (bf16[1,16,128,128]{3,2,1,0:T(8,128)(2,1)}, bf16[1,16,128,128]{3,2,1,0:T(8,128)(2,1)}, u32[]{:S(2)}, u32[]{:S(2)}) collective-permute-start(bf16[1,16,128,128]{3,2,1,0:T(8,128)(2,1)} %fusion.6), channel_id=1, source_target_pairs={{8,0},{10,2},{12,4},{14,6},{16,8},{18,10},{20,12},{22,14},{24,16},... | collective-permute-start | bytes 1572872 | tf_op jit(solution)/shard_map/ppermute | solution.py:20
  129.9 27.6 %collective-permute-start.33 = (bf16[1,16,128,128]{3,2,1,0:T(8,128)(2,1)}, bf16[1,16,128,128]{3,2,1,0:T(8,128)(2,1)S(1)}, u32[]{:S(2)}, u32[]{:S(2)}) collective-permute-start(bf16[1,16,128,128]{3,2,1,0:T(8,128)(2,1)} %add_convert_fusion.1), channel_id=1, source_target_pairs={{0,4},{2,6},{4,0},{6,2},{8,12},{10,14},{12,8},{14,10},{16,20},{18,... | collective-permute-start | bytes 1572872 | tf_op jit(solution)/shard_map/ppermute | solution.py:24
  135.8 21.7 %collective-permute-start.34 = (bf16[1,16,128,128]{3,2,1,0:T(8,128)(2,1)}, bf16[1,16,128,128]{3,2,1,0:T(8,128)(2,1)}, u32[]{:S(2)}, u32[]{:S(2)}) collective-permute-start(bf16[1,16,128,128]{3,2,1,0:T(8,128)(2,1)} %get-tuple-element.50), channel_id=1, source_target_pairs={{0,2},{2,0},{4,6},{6,4},{8,10},{10,8},{12,14},{14,12},{16,18},{18,... | collective-permute-start | bytes 1572872 | tf_op jit(solution)/shard_map/ppermute | solution.py:24
  147.0 19.5 %copy-start.2 = (bf16[1,16,128,128]{3,2,1,0:T(8,128)(2,1)}, bf16[1,16,128,128]{3,2,1,0:T(8,128)(2,1)S(1)}, u32[]{:S(2)}) copy-start(bf16[1,16,128,128]{3,2,1,0:T(8,128)(2,1)S(1)} %collective-permute-done.27) | copy-start | bytes 1572868
  147.0 17.1 %collective-permute-start.36 = (bf16[1,16,128,128]{3,2,1,0:T(8,128)(2,1)}, bf16[1,16,128,128]{3,2,1,0:T(8,128)(2,1)}, u32[]{:S(2)}, u32[]{:S(2)}) collective-permute-start(bf16[1,16,128,128]{3,2,1,0:T(8,128)(2,1)} %fusion.16), channel_id=1, source_target_pairs={{8,0},{10,2},{12,4},{14,6},{16,8},{18,10},{20,12},{22,14},{24,16},... | collective-permute-start | bytes 1572872 | tf_op jit(solution)/shard_map/ppermute | solution.py:20
  148.3 15.8 %copy-start.20 = (bf16[1,16,128,128]{3,2,1,0:T(8,128)(2,1)S(1)}, bf16[1,16,128,128]{3,2,1,0:T(8,128)(2,1)}, u32[]{:S(2)}) copy-start(bf16[1,16,128,128]{3,2,1,0:T(8,128)(2,1)} %get-tuple-element.49) | copy-start | bytes 1572868
  151.0 16.8 %copy-start.1 = (f32[16,128,256]{2,1,0:T(8,128)S(1)}, f32[16,128,256]{2,1,0:T(8,128)}, u32[]{:S(2)}) copy-start(f32[16,128,256]{2,1,0:T(8,128)} %get-tuple-element.38) | copy-start | bytes 6291460
  151.0 24.3 %collective-permute-start.31 = (bf16[1,16,128,128]{3,2,1,0:T(8,128)(2,1)}, bf16[1,16,128,128]{3,2,1,0:T(8,128)(2,1)}, u32[]{:S(2)}, u32[]{:S(2)}) collective-permute-start(bf16[1,16,128,128]{3,2,1,0:T(8,128)(2,1)} %fusion.9), channel_id=1, source_target_pairs={{8,0},{10,2},{12,4},{14,6},{16,8},{18,10},{20,12},{22,14},{24,16},... | collective-permute-start | bytes 1572872 | tf_op jit(solution)/shard_map/ppermute | solution.py:20
  157.5 10.4 %copy-start.4 = (bf16[1,16,128,128]{3,2,1,0:T(8,128)(2,1)}, bf16[1,16,128,128]{3,2,1,0:T(8,128)(2,1)S(1)}, u32[]{:S(2)}) copy-start(bf16[1,16,128,128]{3,2,1,0:T(8,128)(2,1)S(1)} %collective-permute-done.33) | copy-start | bytes 1572868
  166.6 17.5 %collective-permute-start.37 = (bf16[1,16,128,128]{3,2,1,0:T(8,128)(2,1)}, bf16[1,16,128,128]{3,2,1,0:T(8,128)(2,1)}, u32[]{:S(2)}, u32[]{:S(2)}) collective-permute-start(bf16[1,16,128,128]{3,2,1,0:T(8,128)(2,1)} %fusion.19), channel_id=1, source_target_pairs={{8,0},{10,2},{12,4},{14,6},{16,8},{18,10},{20,12},{22,14},{24,16},... | collective-permute-start | bytes 1572872 | tf_op jit(solution)/shard_map/ppermute | solution.py:20
  168.4 6.9 %copy-start.3 = (bf16[1,16,128,128]{3,2,1,0:T(8,128)(2,1)S(1)}, bf16[1,16,128,128]{3,2,1,0:T(8,128)(2,1)}, u32[]{:S(2)}) copy-start(bf16[1,16,128,128]{3,2,1,0:T(8,128)(2,1)} %copy-done.2) | copy-start | bytes 1572868
  172.2 11.9 %copy-start.5 = (bf16[1,16,128,128]{3,2,1,0:T(8,128)(2,1)S(1)}, bf16[1,16,128,128]{3,2,1,0:T(8,128)(2,1)}, u32[]{:S(2)}) copy-start(bf16[1,16,128,128]{3,2,1,0:T(8,128)(2,1)} %copy-done.4) | copy-start | bytes 1572868
  172.2 11.9 %copy-start.8 = (bf16[1,16,128,128]{3,2,1,0:T(8,128)(2,1)S(1)}, bf16[1,16,128,128]{3,2,1,0:T(8,128)(2,1)}, u32[]{:S(2)}) copy-start(bf16[1,16,128,128]{3,2,1,0:T(8,128)(2,1)} %get-tuple-element.46) | copy-start | bytes 1572868

commit v8 on v7

--- a/solution.py
+++ b/solution.py
@@ -123,11 +123,9 @@
     yc = one_way(x1, n, 2, 0)
     yd = one_way(x2, n, 2, 2)
     y0 = jnp.where(half == 1, ya, yb)
-    d0 = swap(y0, n, 1)
     cxo = jnp.where(core == 1, ca, cb)
     y1 = jnp.where(half == 1, yc, yd)
-    d1 = swap(y1, n, 1)
-    return [x0, x1, cx1, x2, cxo, y0, d0, y1, d1]
+    return [x0, x1, cx1, x2, cxo, y0, None, y1, None]
 
 
 def gather_y(terms, n):
@@ -175,24 +173,25 @@
     kb = route(normed_key_rows.transpose(1, 0, 2)[None], n, half, core)
     vb = route(value_rows.transpose(1, 0, 2)[None], n, half, core)
 
-    late = [3, 4, 5, 6, 7, 8]
-    early = [0, 1, 2]
     modes = [0, 1, 1, 2, 1, 1, 1, 1, 1]
     dist = [0, PLANE, 3 + 2 * core, 2 * PLANE, 7 - 6 * core, 2, 1 + 2 * core, 6, 5 + 2 * core]
     terms = [None] * 18
-    acc = None
-    ys = None
-    qb = q4
-    for sel in (late, early):
+
+    def run(sel, acc, q):
         acc, out = attend_blocks(
-            [modes[j] for j in sel], [dist[j] for j in sel], idx, qb, do4, lse3, delta3, acc,
+            [modes[j] for j in sel], [dist[j] for j in sel], idx, q, do4, lse3, delta3, acc,
             [kb[j] for j in sel] + [vb[j] for j in sel])
         for m, j in enumerate(sel):
             terms[j] = out[m]
             terms[9 + j] = out[len(sel) + m]
-        if ys is None:
-            ys = gather_y(terms[:9], n) + gather_y(terms[9:], n)
-            ys, qb = lax.optimization_barrier((ys, q4))
+        return acc
+
+    acc = run([0, 1, 2], None, q4)
+    (kb[5], vb[5]), acc = lax.optimization_barrier(((kb[5], vb[5]), acc))
+    kb[6], vb[6] = swap(kb[5], n, 1), swap(vb[5], n, 1)
+    kb[8], vb[8] = swap(kb[7], n, 1), swap(vb[7], n, 1)
+    acc = run([3, 4, 5, 6, 7, 8], acc, q4)
+    ys = gather_y(terms[:9], n) + gather_y(terms[9:], n)
     grad_k = unroute(terms[:9], ys[0], ys[1], n, half, core)
     grad_v = unroute(terms[9:], ys[2], ys[3], n, half, core)
 

time: 188 us -> 209 us (1.11)
  waiting for transfers between devices: 52.6 us -> 78.8 us
  starting transfers between devices: 60.2 us -> 57.1 us
  other arithmetic: 22.5 us -> 19.6 us
    ppermute x18, waiting for transfers between devices: 21.4 us -> 38.1 us  [swap(): return lax.ppermute(x, 'seq', [(i, i ^ bit) for i in range(n)])]
    ppermute x8, waiting for transfers between devices: 19.2 us -> 27.2 us  [shift(): return lax.ppermute(x, 'seq', pairs)]
    ppermute x18, starting transfers between devices: 7.78 us -> 5.37 us  [swap(): return lax.ppermute(x, 'seq', [(i, i ^ bit) for i in range(n)])]
  transfers between devices with their start and end apart: 38 -> 38, of which waited for: 14 -> 16; matrix products, arithmetic and copies ran while one was open for 17% -> 14% of each run, Pallas kernels for 7% -> 6%
where the time goes in v8:
time: 209 us; the launch traced here: 208 us
  waiting for transfers between devices  78.8 us (38%)
  starting transfers between devices  57.1 us (27%)
  Pallas kernels  36 us (17%)
  other arithmetic  19.6 us (9%)
  local copies, waits for them, and re-layouts  14.9 us (7%)
    ppermute x18, waiting for transfers between devices, swap(): return lax.ppermute(x, 'seq', [(i, i ^ bit) for i in range(n)])  38.1 us
    pallas_call x2, Pallas kernels, attend_blocks(): pl.pallas_call(functools.partial(_blocks_kernel, tuple(modes), acc is not...  36 us
    ppermute x12, starting transfers between devices, one_way(): return lax.ppermute(x, 'seq', pairs)  29.2 us
    ppermute x8, waiting for transfers between devices, shift(): return lax.ppermute(x, 'seq', pairs)  27.2 us
    ppermute x8, starting transfers between devices, shift(): return lax.ppermute(x, 'seq', pairs)  22.5 us
    ppermute x12, waiting for transfers between devices, one_way(): return lax.ppermute(x, 'seq', pairs)  13.5 us
    unnamed x56, local copies, waits for them, and re-layouts  7.27 us
    ppermute x18, starting transfers between devices, swap(): return lax.ppermute(x, 'seq', [(i, i ^ bit) for i in range(n)])  5.37 us
  transfers between devices with their start and end apart: 38, of which 16 were waited for; matrix products, arithmetic and copies ran while one was open for 14% of the time, Pallas kernels for 6%

profile of v8, /device:TPU:0, one launch (start us, length us, event | category | flops | bytes accessed | tf_op | source)
XLA Modules:
  0.0 207.6 jit_solution(978808532617411971)
XLA Ops:
  0.7 2.1 %copy.26 = bf16[128,16,128]{2,0,1:T(8,128)(2,1)} copy(bf16[128,16,128]{2,1,0:T(8,128)(2,1)} %param.8) | data formatting | bytes 1048576 | tf_op args[2]
  2.8 5.7 %collective-permute-start.4 = (bf16[1,16,128,128]{3,2,1,0:T(8,128)(2,1)}, bf16[1,16,128,128]{3,2,1,0:T(8,128)(2,1)}, u32[]{:S(2)}, u32[]{:S(2)}) collective-permute-start(bf16[1,16,128,128]{3,2,1,0:T(8,128)(2,1)} %bitcast.34.refs_3_), channel_id=1, source_target_pairs={{0,8},{2,10},{4,12},{6,14},{8,16},{10,18},{12,20},{14,22},{16,24},... | collective-permute-start | bytes 1572872 | tf_op jit(solution)/shard_map/ppermute | solution.py:20
  8.5 1.2 copy.27
  9.7 0.8 copy-done.11
  10.5 3.5 %collective-permute-start.1 = (bf16[1,16,128,128]{3,2,1,0:T(8,128)(2,1)S(1)}, bf16[1,16,128,128]{3,2,1,0:T(8,128)(2,1)}, u32[]{:S(2)}, u32[]{:S(2)}) collective-permute-start(bf16[1,16,128,128]{3,2,1,0:T(8,128)(2,1)S(1)} %bitcast.44), channel_id=1, source_target_pairs={{0,8},{2,10},{4,12},{6,14},{8,16},{10,18},{12,20},{14,22},{16,24},... | collective-permute-start | bytes 1572872 | tf_op jit(solution)/shard_map/ppermute | solution.py:20
  14.0 4.2 %collective-permute-start.3 = (bf16[1,16,128,128]{3,2,1,0:T(8,128)(2,1)}, bf16[1,16,128,128]{3,2,1,0:T(8,128)(2,1)}, u32[]{:S(2)}, u32[]{:S(2)}) collective-permute-start(bf16[1,16,128,128]{3,2,1,0:T(8,128)(2,1)} %bitcast.34.refs_3_), channel_id=1, source_target_pairs={{0,4},{2,6},{8,12},{10,14},{16,20},{18,22},{24,28},{26,30},{1,5},{... | collective-permute-start | bytes 1572872 | tf_op jit(solution)/shard_map/ppermute | solution.py:29
  18.2 2.1 %collective-permute-done.4.refs_4_ = bf16[1,16,128,128]{3,2,1,0:T(8,128)(2,1)} collective-permute-done((bf16[1,16,128,128]{3,2,1,0:T(8,128)(2,1)}, bf16[1,16,128,128]{3,2,1,0:T(8,128)(2,1)}, u32[]{:S(2)}, u32[]{:S(2)}) %collective-permute-start.4) | collective-permute-done | bytes 524320 | tf_op jit(solution)/shard_map/ppermute | solution.py:20
  20.3 10.0 %collective-permute-done.1.refs_1_ = bf16[1,16,128,128]{3,2,1,0:T(8,128)(2,1)} collective-permute-done((bf16[1,16,128,128]{3,2,1,0:T(8,128)(2,1)S(1)}, bf16[1,16,128,128]{3,2,1,0:T(8,128)(2,1)}, u32[]{:S(2)}, u32[]{:S(2)}) %collective-permute-start.1) | collective-permute-done | bytes 524320 | tf_op jit(solution)/shard_map/ppermute | solution.py:20
  30.3 5.3 %collective-permute-start.15 = (bf16[1,16,128,128]{3,2,1,0:T(8,128)(2,1)}, bf16[1,16,128,128]{3,2,1,0:T(8,128)(2,1)}, u32[]{:S(2)}, u32[]{:S(2)}) collective-permute-start(bf16[1,16,128,128]{3,2,1,0:T(8,128)(2,1)} %collective-permute-done.4.refs_4_), channel_id=1, source_target_pairs={{0,8},{2,10},{4,12},{6,14},{8,16},{10,18},{12,20},{14,22},{16,24},... | collective-permute-start | bytes 1572872 | tf_op jit(solution)/shard_map/ppermute | solution.py:20
  35.6 1.3 collective-permute-start.5
  37.1 0.5 stack.53.valid_ref
  37.6 0.6 multiply_reduce_fusion
  38.2 0.7 copy.18
  38.9 1.4 copy.16
  40.3 1.4 copy.17
  41.7 5.3 %collective-permute-start = (bf16[1,16,128,128]{3,2,1,0:T(8,128)(2,1)S(1)}, bf16[1,16,128,128]{3,2,1,0:T(8,128)(2,1)S(1)}, u32[]{:S(2)}, u32[]{:S(2)}) collective-permute-start(bf16[1,16,128,128]{3,2,1,0:T(8,128)(2,1)S(1)} %bitcast.46), channel_id=1, source_target_pairs={{0,4},{2,6},{8,12},{10,14},{16,20},{18,22},{24,28},{26,30},{1,5},{... | collective-permute-start | bytes 1572872 | tf_op jit(solution)/shard_map/ppermute | solution.py:29
  47.0 2.7 %collective-permute-start.8 = (bf16[1,16,128,128]{3,2,1,0:T(8,128)(2,1)}, bf16[1,16,128,128]{3,2,1,0:T(8,128)(2,1)S(1)}, u32[]{:S(2)}, u32[]{:S(2)}) collective-permute-start(bf16[1,16,128,128]{3,2,1,0:T(8,128)(2,1)} %collective-permute-done.1.refs_1_), channel_id=1, source_target_pairs={{0,8},{2,10},{4,12},{6,14},{8,16},{10,18},{12,20},{14,22},{16,24},... | collective-permute-start | bytes 1572872 | tf_op jit(solution)/shard_map/ppermute | solution.py:20
  49.8 1.3 collective-permute-start.2
  51.1 0.6 add_convert_fusion.4.valid_ref
  51.7 13.4 %shard_map.85 = (f32[16,128,256]{2,1,0:T(8,128)}, bf16[1,16,128,128]{3,2,1,0:T(8,128)(2,1)}, bf16[1,16,128,128]{3,2,1,0:T(8,128)(2,1)}, bf16[1,16,128,128]{3,2,1...) custom-call(s32[3]{0:T(128)} %add_convert_fusion.4.valid_ref, ...), custom_call_target="tpu_custom_call" | custom-call | flops 2013265920 | bytes 8388608 | tf_op jit(solution)/shard_map/pallas_call | solution.py:105
  65.1 4.7 %collective-permute-start.19 = (bf16[1,16,128,128]{3,2,1,0:T(8,128)(2,1)}, bf16[1,16,128,128]{3,2,1,0:T(8,128)(2,1)S(1)}, u32[]{:S(2)}, u32[]{:S(2)}) collective-permute-start(bf16[1,16,128,128]{3,2,1,0:T(8,128)(2,1)} %collective-permute-done.4.refs_4_), channel_id=1, source_target_pairs={{0,4},{2,6},{8,12},{10,14},{16,20},{18,22},{24,28},{26,30},{1,5},{... | collective-permute-start | bytes 1572872 | tf_op jit(solution)/shard_map/ppermute | solution.py:29
  69.8 1.3 collective-permute-start.20
  71.1 1.1 broadcast_select_fusion.4.refs_9_
  72.3 1.3 collective-permute-start.16
  73.6 4.6 %collective-permute-start.12 = (bf16[1,16,128,128]{3,2,1,0:T(8,128)(2,1)}, bf16[1,16,128,128]{3,2,1,0:T(8,128)(2,1)S(1)}, u32[]{:S(2)}, u32[]{:S(2)}) collective-permute-start(bf16[1,16,128,128]{3,2,1,0:T(8,128)(2,1)} %collective-permute-done.1.refs_1_), channel_id=1, source_target_pairs={{0,4},{2,6},{8,12},{10,14},{16,20},{18,22},{24,28},{26,30},{1,5},{... | collective-permute-start | bytes 1572872 | tf_op jit(solution)/shard_map/ppermute | solution.py:29
  78.3 1.3 collective-permute-start.13
  79.6 2.9 %collective-permute-done.19 = bf16[1,16,128,128]{3,2,1,0:T(8,128)(2,1)S(1)} collective-permute-done((bf16[1,16,128,128]{3,2,1,0:T(8,128)(2,1)}, bf16[1,16,128,128]{3,2,1,0:T(8,128)(2,1)S(1)}, u32[]{:S(2)}, u32[]{:S(2)}) %collective-permute-start.19) | collective-permute-done | bytes 524320 | tf_op jit(solution)/shard_map/ppermute | solution.py:29
  82.5 1.3 collective-permute-start.9
  83.8 3.0 %collective-permute-done.20 = bf16[1,16,128,128]{3,2,1,0:T(8,128)(2,1)S(1)} collective-permute-done((bf16[1,16,128,128]{3,2,1,0:T(8,128)(2,1)}, bf16[1,16,128,128]{3,2,1,0:T(8,128)(2,1)S(1)}, u32[]{:S(2)}, u32[]{:S(2)}) %collective-permute-start.20) | collective-permute-done | bytes 524320 | tf_op jit(solution)/shard_map/ppermute | solution.py:29
  86.8 1.3 collective-permute-start.17
  88.2 3.6 %collective-permute-done.12 = bf16[1,16,128,128]{3,2,1,0:T(8,128)(2,1)S(1)} collective-permute-done((bf16[1,16,128,128]{3,2,1,0:T(8,128)(2,1)}, bf16[1,16,128,128]{3,2,1,0:T(8,128)(2,1)S(1)}, u32[]{:S(2)}, u32[]{:S(2)}) %collective-permute-start.12) | collective-permute-done | bytes 524320 | tf_op jit(solution)/shard_map/ppermute | solution.py:29
  91.8 4.0 %collective-permute-done.13 = bf16[1,16,128,128]{3,2,1,0:T(8,128)(2,1)S(1)} collective-permute-done((bf16[1,16,128,128]{3,2,1,0:T(8,128)(2,1)S(1)}, bf16[1,16,128,128]{3,2,1,0:T(8,128)(2,1)S(1)}, u32[]{:S(2)}, u32[]{:S(2)}) %collective-permute-start.13) | collective-permute-done | bytes 524320 | tf_op jit(solution)/shard_map/ppermute | solution.py:29
  95.8 1.3 collective-permute-start.10
  97.2 1.2 collective-permute-start.18
  98.5 0.4 collective-permute-start.14
  99.0 0.9 broadcast_select_fusion.refs_8_
  99.9 0.9 broadcast_select_fusion.1.refs_2_
  100.7 1.2 collective-permute-done.21.refs_12_
  101.9 0.8 copy-done.25
  102.7 22.6 %shard_map.86 = (f32[16,128,256]{2,1,0:T(8,128)}, bf16[1,16,128,128]{3,2,1,0:T(8,128)(2,1)}, bf16[1,16,128,128]{3,2,1,0:T(8,128)(2,1)}, bf16[1,16,128,128]{3,2,1...) custom-call(s32[6]{0:T(128)} %stack.53.valid_ref, ...), custom_call_target="tpu_custom_call" | custom-call | flops 4026531840 | bytes 16777216 | tf_op jit(solution)/shard_map/pallas_call | solution.py:105
  126.6 0.9 collective-permute-done.26
  127.7 1.2 add_convert_fusion.2
  129.0 2.0 add_convert_fusion.3
  131.6 1.8 collective-permute-start.24
  133.4 10.4 %collective-permute-done.27 = bf16[1,16,128,128]{3,2,1,0:T(8,128)(2,1)S(1)} collective-permute-done((bf16[1,16,128,128]{3,2,1,0:T(8,128)(2,1)S(1)}, bf16[1,16,128,128]{3,2,1,0:T(8,128)(2,1)S(1)}, u32[]{:S(2)}, u32[]{:S(2)}) %collective-permute-start.27) | collective-permute-done | bytes 524320 | tf_op jit(solution)/shard_map/ppermute | solution.py:24
  143.8 1.1 fusion.6
  144.8 1.3 collective-permute-start.28
  146.1 0.9 add_convert_fusion.1
  147.1 18.6 %collective-permute-done.35 = bf16[1,16,128,128]{3,2,1,0:T(8,128)(2,1)S(1)} collective-permute-done((bf16[1,16,128,128]{3,2,1,0:T(8,128)(2,1)S(1)}, bf16[1,16,128,128]{3,2,1,0:T(8,128)(2,1)S(1)}, u32[]{:S(2)}, u32[]{:S(2)}) %collective-permute-start.35) | collective-permute-done | bytes 524320 | tf_op jit(solution)/shard_map/ppermute | solution.py:24
  165.9 1.1 fusion.16
  167.0 1.3 collective-permute-start.36
  168.3 2.8 %fusion.9 = bf16[1,16,128,128]{3,2,1,0:T(8,128)(2,1)} fusion(bf16[1,16,128,128]{3,2,1,0:T(8,128)(2,1)S(1)} %collective-permute-done.24, bf16[1,16,128,128]{3,2,1,0:T(8,128)(2,1)S(1)} %collective-permute-done.27, bf16[1,16,128,128]{3,2,1,0:T(8,128)(2,1)} %collective-permute-done.28, bf16[1,16,128,128]{3,2,1,0:T(8,128)(2,1)} %collective-permute-done.25, ...), kind=kLoop, calls=%fused_computation.21 | loop fusion | flops 2621440 | bytes 3145729 | tf_op jit(solution)/shard_map/convert_element_type | solution.py:154
  171.1 1.4 collective-permute-start.29
  172.6 6.7 %collective-permute-done.32 = bf16[1,16,128,128]{3,2,1,0:T(8,128)(2,1)S(1)} collective-permute-done((bf16[1,16,128,128]{3,2,1,0:T(8,128)(2,1)}, bf16[1,16,128,128]{3,2,1,0:T(8,128)(2,1)S(1)}, u32[]{:S(2)}, u32[]{:S(2)}) %collective-permute-start.32) | collective-permute-done | bytes 524320 | tf_op jit(solution)/shard_map/ppermute | solution.py:24
  179.2 4.8 %collective-permute-done.36 = bf16[1,16,128,128]{3,2,1,0:T(8,128)(2,1)} collective-permute-done((bf16[1,16,128,128]{3,2,1,0:T(8,128)(2,1)}, bf16[1,16,128,128]{3,2,1,0:T(8,128)(2,1)}, u32[]{:S(2)}, u32[]{:S(2)}) %collective-permute-start.36) | collective-permute-done | bytes 524320 | tf_op jit(solution)/shard_map/ppermute | solution.py:20
  184.1 2.4 %fusion.19 = bf16[1,16,128,128]{3,2,1,0:T(8,128)(2,1)} fusion(bf16[1,16,128,128]{3,2,1,0:T(8,128)(2,1)S(1)} %collective-permute-done.32, bf16[1,16,128,128]{3,2,1,0:T(8,128)(2,1)S(1)} %collective-permute-done.35, bf16[1,16,128,128]{3,2,1,0:T(8,128)(2,1)} %collective-permute-done.36, bf16[1,16,128,128]{3,2,1,0:T(8,128)(2,1)} %collective-permute-done.33, ...), kind=kLoop, calls=%fused_computation.31 | loop fusion | flops 2621440 | bytes 3145729 | tf_op jit(solution)/shard_map/convert_element_type | solution.py:154
  186.5 1.3 collective-permute-start.37
  188.3 3.8 %copy.21 = bf16[128,16,2,128]{3,2,1,0:T(2,128)(2,1)} copy(bf16[128,16,2,128]{0,2,3,1:T(2,128)(2,1)S(1)} %bitcast.37) | data formatting | bytes 2097152 | tf_op jit(solution)/shard_map/transpose | solution.py:199
  192.1 3.2 %collective-permute-done.29 = bf16[1,16,128,128]{3,2,1,0:T(8,128)(2,1)} collective-permute-done((bf16[1,16,128,128]{3,2,1,0:T(8,128)(2,1)}, bf16[1,16,128,128]{3,2,1,0:T(8,128)(2,1)}, u32[]{:S(2)}, u32[]{:S(2)}) %collective-permute-start.29) | collective-permute-done | bytes 524320 | tf_op jit(solution)/shard_map/ppermute | solution.py:20
  195.3 1.6 fusion.21
  196.8 1.1 copy.22
  198.0 7.1 %collective-permute-done.37 = bf16[1,16,128,128]{3,2,1,0:T(8,128)(2,1)} collective-permute-done((bf16[1,16,128,128]{3,2,1,0:T(8,128)(2,1)}, bf16[1,16,128,128]{3,2,1,0:T(8,128)(2,1)}, u32[]{:S(2)}, u32[]{:S(2)}) %collective-permute-start.37) | collective-permute-done | bytes 524320 | tf_op jit(solution)/shard_map/ppermute | solution.py:20
  205.1 1.4 fusion.20
  206.5 1.1 copy.23
  (96 shorter events, 3.4 us)
Async XLA Ops:
  0.6 37.0 %copy-start = (bf16[128,32,128]{2,1,0:T(8,128)(2,1)S(1)}, bf16[128,32,128]{2,1,0:T(8,128)(2,1)}, u32[]{:S(2)}) copy-start(bf16[128,32,128]{2,1,0:T(8,128)(2,1)} %param.10) | copy-start | bytes 3145732
  0.6 36.9 %copy-start.6 = (bf16[128,32,128]{2,1,0:T(8,128)(2,1)S(1)}, bf16[128,32,128]{2,1,0:T(8,128)(2,1)}, u32[]{:S(2)}) copy-start(bf16[128,32,128]{2,1,0:T(8,128)(2,1)} %param.9) | copy-start | bytes 3145732
  0.7 38.2 %copy-start.7 = (bf16[128,32,128]{2,1,0:T(8,128)(2,1)S(1)}, bf16[128,32,128]{2,1,0:T(8,128)(2,1)}, u32[]{:S(2)}) copy-start(bf16[128,32,128]{2,1,0:T(8,128)(2,1)} %param.6) | copy-start | bytes 3145732
  2.8 17.6 %collective-permute-start.4 = (bf16[1,16,128,128]{3,2,1,0:T(8,128)(2,1)}, bf16[1,16,128,128]{3,2,1,0:T(8,128)(2,1)}, u32[]{:S(2)}, u32[]{:S(2)}) collective-permute-start(bf16[1,16,128,128]{3,2,1,0:T(8,128)(2,1)} %bitcast.34.refs_3_), channel_id=1, source_target_pairs={{0,8},{2,10},{4,12},{6,14},{8,16},{10,18},{12,20},{14,22},{16,24},... | collective-permute-start | bytes 1572872 | tf_op jit(solution)/shard_map/ppermute | solution.py:20
  9.7 0.8 copy-start.11
  10.5 19.8 %collective-permute-start.1 = (bf16[1,16,128,128]{3,2,1,0:T(8,128)(2,1)S(1)}, bf16[1,16,128,128]{3,2,1,0:T(8,128)(2,1)}, u32[]{:S(2)}, u32[]{:S(2)}) collective-permute-start(bf16[1,16,128,128]{3,2,1,0:T(8,128)(2,1)S(1)} %bitcast.44), channel_id=1, source_target_pairs={{0,8},{2,10},{4,12},{6,14},{8,16},{10,18},{12,20},{14,22},{16,24},... | collective-permute-start | bytes 1572872 | tf_op jit(solution)/shard_map/ppermute | solution.py:20
  14.0 27.7 %collective-permute-start.3 = (bf16[1,16,128,128]{3,2,1,0:T(8,128)(2,1)}, bf16[1,16,128,128]{3,2,1,0:T(8,128)(2,1)}, u32[]{:S(2)}, u32[]{:S(2)}) collective-permute-start(bf16[1,16,128,128]{3,2,1,0:T(8,128)(2,1)} %bitcast.34.refs_3_), channel_id=1, source_target_pairs={{0,4},{2,6},{8,12},{10,14},{16,20},{18,22},{24,28},{26,30},{1,5},{... | collective-permute-start | bytes 1572872 | tf_op jit(solution)/shard_map/ppermute | solution.py:29
  20.3 26.7 %collective-permute-start.7 = (bf16[1,16,128,128]{3,2,1,0:T(8,128)(2,1)}, bf16[1,16,128,128]{3,2,1,0:T(8,128)(2,1)}, u32[]{:S(2)}, u32[]{:S(2)}) collective-permute-start(bf16[1,16,128,128]{3,2,1,0:T(8,128)(2,1)} %collective-permute-done.4.refs_4_), channel_id=1, source_target_pairs={{0,2},{2,0},{4,6},{6,4},{8,10},{10,8},{12,14},{14,12},{16,18},{18,... | collective-permute-start | bytes 1572872 | tf_op jit(solution)/shard_map/ppermute | solution.py:24
  30.3 19.5 %collective-permute-start.6 = (bf16[1,16,128,128]{3,2,1,0:T(8,128)(2,1)}, bf16[1,16,128,128]{3,2,1,0:T(8,128)(2,1)}, u32[]{:S(2)}, u32[]{:S(2)}) collective-permute-start(bf16[1,16,128,128]{3,2,1,0:T(8,128)(2,1)} %collective-permute-done.1.refs_1_), channel_id=1, source_target_pairs={{0,2},{2,0},{4,6},{6,4},{8,10},{10,8},{12,14},{14,12},{16,18},{18,... | collective-permute-start | bytes 1572872 | tf_op jit(solution)/shard_map/ppermute | solution.py:24
  30.3 34.8 %collective-permute-start.15 = (bf16[1,16,128,128]{3,2,1,0:T(8,128)(2,1)}, bf16[1,16,128,128]{3,2,1,0:T(8,128)(2,1)}, u32[]{:S(2)}, u32[]{:S(2)}) collective-permute-start(bf16[1,16,128,128]{3,2,1,0:T(8,128)(2,1)} %collective-permute-done.4.refs_4_), channel_id=1, source_target_pairs={{0,8},{2,10},{4,12},{6,14},{8,16},{10,18},{12,20},{14,22},{16,24},... | collective-permute-start | bytes 1572872 | tf_op jit(solution)/shard_map/ppermute | solution.py:20
  35.6 34.2 %collective-permute-start.5 = (bf16[1,16,128,128]{3,2,1,0:T(8,128)(2,1)}, bf16[1,16,128,128]{3,2,1,0:T(8,128)(2,1)}, u32[]{:S(2)}, u32[]{:S(2)}) collective-permute-start(bf16[1,16,128,128]{3,2,1,0:T(8,128)(2,1)} %collective-permute-done.4.refs_4_), channel_id=1, source_target_pairs={{4,0},{6,2},{12,8},{14,10},{20,16},{22,18},{28,24},{30,26},{5,1},{... | collective-permute-start | bytes 1572872 | tf_op jit(solution)/shard_map/ppermute | solution.py:29
  38.9 2.8 %copy-start.12 = (bf16[128,16,128]{2,0,1:T(8,128)(2,1)S(1)}, bf16[128,16,128]{2,0,1:T(8,128)(2,1)}, u32[]{:S(2)}) copy-start(bf16[128,16,128]{2,0,1:T(8,128)(2,1)} %copy-done.11) | copy-start | bytes 1572868
  41.7 30.6 %collective-permute-start = (bf16[1,16,128,128]{3,2,1,0:T(8,128)(2,1)S(1)}, bf16[1,16,128,128]{3,2,1,0:T(8,128)(2,1)S(1)}, u32[]{:S(2)}, u32[]{:S(2)}) collective-permute-start(bf16[1,16,128,128]{3,2,1,0:T(8,128)(2,1)S(1)} %bitcast.46), channel_id=1, source_target_pairs={{0,4},{2,6},{8,12},{10,14},{16,20},{18,22},{24,28},{26,30},{1,5},{... | collective-permute-start | bytes 1572872 | tf_op jit(solution)/shard_map/ppermute | solution.py:29
  47.0 26.6 %collective-permute-start.8 = (bf16[1,16,128,128]{3,2,1,0:T(8,128)(2,1)}, bf16[1,16,128,128]{3,2,1,0:T(8,128)(2,1)S(1)}, u32[]{:S(2)}, u32[]{:S(2)}) collective-permute-start(bf16[1,16,128,128]{3,2,1,0:T(8,128)(2,1)} %collective-permute-done.1.refs_1_), channel_id=1, source_target_pairs={{0,8},{2,10},{4,12},{6,14},{8,16},{10,18},{12,20},{14,22},{16,24},... | collective-permute-start | bytes 1572872 | tf_op jit(solution)/shard_map/ppermute | solution.py:20
  49.8 28.5 %collective-permute-start.2 = (bf16[1,16,128,128]{3,2,1,0:T(8,128)(2,1)}, bf16[1,16,128,128]{3,2,1,0:T(8,128)(2,1)S(1)}, u32[]{:S(2)}, u32[]{:S(2)}) collective-permute-start(bf16[1,16,128,128]{3,2,1,0:T(8,128)(2,1)} %collective-permute-done.1.refs_1_), channel_id=1, source_target_pairs={{4,0},{6,2},{12,8},{14,10},{20,16},{22,18},{28,24},{30,26},{5,1},{... | collective-permute-start | bytes 1572872 | tf_op jit(solution)/shard_map/ppermute | solution.py:29
  65.1 17.4 %copy-start.13 = (bf16[128,16,128]{2,0,1:T(8,128)(2,1)S(1)}, bf16[128,16,128]{2,0,1:T(8,128)(2,1)}, u32[]{:S(2)}) copy-start(bf16[128,16,128]{2,0,1:T(8,128)(2,1)} %copy-done.11) | copy-start | bytes 1572868
  65.1 17.4 %collective-permute-start.19 = (bf16[1,16,128,128]{3,2,1,0:T(8,128)(2,1)}, bf16[1,16,128,128]{3,2,1,0:T(8,128)(2,1)S(1)}, u32[]{:S(2)}, u32[]{:S(2)}) collective-permute-start(bf16[1,16,128,128]{3,2,1,0:T(8,128)(2,1)} %collective-permute-done.4.refs_4_), channel_id=1, source_target_pairs={{0,4},{2,6},{8,12},{10,14},{16,20},{18,22},{24,28},{26,30},{1,5},{... | collective-permute-start | bytes 1572872 | tf_op jit(solution)/shard_map/ppermute | solution.py:29
  69.8 17.0 %collective-permute-start.20 = (bf16[1,16,128,128]{3,2,1,0:T(8,128)(2,1)}, bf16[1,16,128,128]{3,2,1,0:T(8,128)(2,1)S(1)}, u32[]{:S(2)}, u32[]{:S(2)}) collective-permute-start(bf16[1,16,128,128]{3,2,1,0:T(8,128)(2,1)} %collective-permute-done.15.refs_7_), channel_id=1, source_target_pairs={{4,0},{6,2},{12,8},{14,10},{20,16},{22,18},{28,24},{30,26},{5,1},{... | collective-permute-start | bytes 1572872 | tf_op jit(solution)/shard_map/ppermute | solution.py:29
  72.3 25.0 %copy-start.14 = (bf16[1,16,128,128]{3,2,1,0:T(8,128)(2,1)}, bf16[1,16,128,128]{3,2,1,0:T(8,128)(2,1)S(1)}, u32[]{:S(2)}) copy-start(bf16[1,16,128,128]{3,2,1,0:T(8,128)(2,1)S(1)} %broadcast_select_fusion.4.refs_9_) | copy-start | bytes 1572868
  72.3 24.9 %collective-permute-start.16 = (bf16[1,16,128,128]{3,2,1,0:T(8,128)(2,1)}, bf16[1,16,128,128]{3,2,1,0:T(8,128)(2,1)S(1)}, u32[]{:S(2)}, u32[]{:S(2)}) collective-permute-start(bf16[1,16,128,128]{3,2,1,0:T(8,128)(2,1)} %bitcast.34.refs_3_), channel_id=1, source_target_pairs={{0,2},{4,6},{8,10},{12,14},{16,18},{20,22},{24,26},{28,30},{1,3},{... | collective-permute-start | bytes 1572872 | tf_op jit(solution)/shard_map/ppermute | solution.py:29
  73.6 23.6 %copy-start.21 = (bf16[1,16,128,128]{3,2,1,0:T(8,128)(2,1)}, bf16[1,16,128,128]{3,2,1,0:T(8,128)(2,1)S(1)}, u32[]{:S(2)}) copy-start(bf16[1,16,128,128]{3,2,1,0:T(8,128)(2,1)S(1)} %collective-permute-done.8.refs_1_) | copy-start | bytes 1572868
  73.6 18.2 %collective-permute-start.12 = (bf16[1,16,128,128]{3,2,1,0:T(8,128)(2,1)}, bf16[1,16,128,128]{3,2,1,0:T(8,128)(2,1)S(1)}, u32[]{:S(2)}, u32[]{:S(2)}) collective-permute-start(bf16[1,16,128,128]{3,2,1,0:T(8,128)(2,1)} %collective-permute-done.1.refs_1_), channel_id=1, source_target_pairs={{0,4},{2,6},{8,12},{10,14},{16,20},{18,22},{24,28},{26,30},{1,5},{... | collective-permute-start | bytes 1572872 | tf_op jit(solution)/shard_map/ppermute | solution.py:29
  78.3 17.6 %collective-permute-start.13 = (bf16[1,16,128,128]{3,2,1,0:T(8,128)(2,1)S(1)}, bf16[1,16,128,128]{3,2,1,0:T(8,128)(2,1)S(1)}, u32[]{:S(2)}, u32[]{:S(2)}) collective-permute-start(bf16[1,16,128,128]{3,2,1,0:T(8,128)(2,1)S(1)} %collective-permute-done.8.refs_1_), channel_id=1, source_target_pairs={{4,0},{6,2},{12,8},{14,10},{20,16},{22,18},{28,24},{30,26},{5,1},{... | collective-permute-start | bytes 1572872 | tf_op jit(solution)/shard_map/ppermute | solution.py:29
  79.6 20.2 %copy-start.15 = (bf16[1,16,128,128]{3,2,1,0:T(8,128)(2,1)}, bf16[1,16,128,128]{3,2,1,0:T(8,128)(2,1)S(1)}, u32[]{:S(2)}) copy-start(bf16[1,16,128,128]{3,2,1,0:T(8,128)(2,1)S(1)} %broadcast_select_fusion.5.refs_3_) | copy-start | bytes 1572868
  82.5 16.0 %collective-permute-start.9 = (bf16[1,16,128,128]{3,2,1,0:T(8,128)(2,1)S(1)}, bf16[1,16,128,128]{3,2,1,0:T(8,128)(2,1)S(1)}, u32[]{:S(2)}, u32[]{:S(2)}) collective-permute-start(bf16[1,16,128,128]{3,2,1,0:T(8,128)(2,1)S(1)} %bitcast.47), channel_id=1, source_target_pairs={{0,2},{4,6},{8,10},{12,14},{16,18},{20,22},{24,26},{28,30},{1,3},{... | collective-permute-start | bytes 1572872 | tf_op jit(solution)/shard_map/ppermute | solution.py:29
  86.8 11.7 %collective-permute-start.17 = (bf16[1,16,128,128]{3,2,1,0:T(8,128)(2,1)}, bf16[1,16,128,128]{3,2,1,0:T(8,128)(2,1)S(1)}, u32[]{:S(2)}, u32[]{:S(2)}) collective-permute-start(bf16[1,16,128,128]{3,2,1,0:T(8,128)(2,1)} %collective-permute-done.15.refs_7_), channel_id=1, source_target_pairs={{2,0},{6,4},{10,8},{14,12},{18,16},{22,20},{26,24},{30,28},{3,1},{... | collective-permute-start | bytes 1572872 | tf_op jit(solution)/shard_map/ppermute | solution.py:29
  88.2 12.5 %copy-start.16 = (bf16[1,16,128,128]{3,2,1,0:T(8,128)(2,1)}, bf16[1,16,128,128]{3,2,1,0:T(8,128)(2,1)S(1)}, u32[]{:S(2)}) copy-start(bf16[1,16,128,128]{3,2,1,0:T(8,128)(2,1)S(1)} %broadcast_select_fusion.2.refs_11_) | copy-start | bytes 1572868
  91.8 8.9 %collective-permute-start.11 = (bf16[1,16,128,128]{3,2,1,0:T(8,128)(2,1)S(1)}, bf16[1,16,128,128]{3,2,1,0:T(8,128)(2,1)S(1)}, u32[]{:S(2)}, u32[]{:S(2)}) collective-permute-start(bf16[1,16,128,128]{3,2,1,0:T(8,128)(2,1)S(1)} %broadcast_select_fusion.5.refs_3_), channel_id=1, source_target_pairs={{0,2},{2,0},{4,6},{6,4},{8,10},{10,8},{12,14},{14,12},{16,18},{18,... | collective-permute-start | bytes 1572872 | tf_op jit(solution)/shard_map/ppermute | solution.py:24
  95.8 4.0 %collective-permute-start.10 = (bf16[1,16,128,128]{3,2,1,0:T(8,128)(2,1)S(1)}, bf16[1,16,128,128]{3,2,1,0:T(8,128)(2,1)S(1)}, u32[]{:S(2)}, u32[]{:S(2)}) collective-permute-start(bf16[1,16,128,128]{3,2,1,0:T(8,128)(2,1)S(1)} %collective-permute-done.8.refs_1_), channel_id=1, source_target_pairs={{2,0},{6,4},{10,8},{14,12},{18,16},{22,20},{26,24},{30,28},{3,1},{... | collective-permute-start | bytes 1572872 | tf_op jit(solution)/shard_map/ppermute | solution.py:29
  97.2 5.5 %copy-start.17 = (bf16[1,16,128,128]{3,2,1,0:T(8,128)(2,1)}, bf16[1,16,128,128]{3,2,1,0:T(8,128)(2,1)S(1)}, u32[]{:S(2)}) copy-start(bf16[1,16,128,128]{3,2,1,0:T(8,128)(2,1)S(1)} %broadcast_select_fusion.3.refs_5_) | copy-start | bytes 1572868
  97.2 3.5 %collective-permute-start.18 = (bf16[1,16,128,128]{3,2,1,0:T(8,128)(2,1)S(1)}, bf16[1,16,128,128]{3,2,1,0:T(8,128)(2,1)S(1)}, u32[]{:S(2)}, u32[]{:S(2)}) collective-permute-start(bf16[1,16,128,128]{3,2,1,0:T(8,128)(2,1)S(1)} %broadcast_select_fusion.4.refs_9_), channel_id=1, source_target_pairs={{0,2},{2,0},{4,6},{6,4},{8,10},{10,8},{12,14},{14,12},{16,18},{18,... | collective-permute-start | bytes 1572872 | tf_op jit(solution)/shard_map/ppermute | solution.py:24
  98.5 3.4 %collective-permute-start.21 = (bf16[1,16,128,128]{3,2,1,0:T(8,128)(2,1)S(1)}, bf16[1,16,128,128]{3,2,1,0:T(8,128)(2,1)S(1)}, u32[]{:S(2)}, u32[]{:S(2)}) collective-permute-start(bf16[1,16,128,128]{3,2,1,0:T(8,128)(2,1)S(1)} %broadcast_select_fusion.2.refs_11_), channel_id=1, source_target_pairs={{0,2},{2,0},{4,6},{6,4},{8,10},{10,8},{12,14},{14,12},{16,18},{18,... | collective-permute-start | bytes 1572872 | tf_op jit(solution)/shard_map/ppermute | solution.py:24
  98.5 4.2 %collective-permute-start.14 = (bf16[1,16,128,128]{3,2,1,0:T(8,128)(2,1)S(1)}, bf16[1,16,128,128]{3,2,1,0:T(8,128)(2,1)}, u32[]{:S(2)}, u32[]{:S(2)}) collective-permute-start(bf16[1,16,128,128]{3,2,1,0:T(8,128)(2,1)S(1)} %broadcast_select_fusion.3.refs_5_), channel_id=1, source_target_pairs={{0,2},{2,0},{4,6},{6,4},{8,10},{10,8},{12,14},{14,12},{16,18},{18,... | collective-permute-start | bytes 1572872 | tf_op jit(solution)/shard_map/ppermute | solution.py:24
  100.7 2.0 copy-start.23
  100.7 1.2 copy-start.24
  101.9 0.8 copy-start.25
  125.3 6.1 %copy-start.10 = (bf16[1,16,128,128]{3,2,1,0:T(8,128)(2,1)S(1)}, bf16[1,16,128,128]{3,2,1,0:T(8,128)(2,1)}, u32[]{:S(2)}) copy-start(bf16[1,16,128,128]{3,2,1,0:T(8,128)(2,1)} %get-tuple-element.46) | copy-start | bytes 1572868
  125.3 2.2 %collective-permute-start.26 = (bf16[1,16,128,128]{3,2,1,0:T(8,128)(2,1)}, bf16[1,16,128,128]{3,2,1,0:T(8,128)(2,1)S(1)}, u32[]{:S(2)}, u32[]{:S(2)}) collective-permute-start(bf16[1,16,128,128]{3,2,1,0:T(8,128)(2,1)} %get-tuple-element.38), channel_id=1, source_target_pairs={{0,2},{2,0},{4,6},{6,4},{8,10},{10,8},{12,14},{14,12},{16,18},{18,... | collective-permute-start | bytes 1572872 | tf_op jit(solution)/shard_map/ppermute | solution.py:24
  125.5 3.5 %collective-permute-start.23 = (bf16[1,16,128,128]{3,2,1,0:T(8,128)(2,1)}, bf16[1,16,128,128]{3,2,1,0:T(8,128)(2,1)S(1)}, u32[]{:S(2)}, u32[]{:S(2)}) collective-permute-start(bf16[1,16,128,128]{3,2,1,0:T(8,128)(2,1)} %get-tuple-element.34), channel_id=1, source_target_pairs={{0,2},{2,0},{4,6},{6,4},{8,10},{10,8},{12,14},{14,12},{16,18},{18,... | collective-permute-start | bytes 1572872 | tf_op jit(solution)/shard_map/ppermute | solution.py:24
  125.9 5.4 %copy-start.22 = (bf16[1,16,128,128]{3,2,1,0:T(8,128)(2,1)S(1)}, bf16[1,16,128,128]{3,2,1,0:T(8,128)(2,1)}, u32[]{:S(2)}) copy-start(bf16[1,16,128,128]{3,2,1,0:T(8,128)(2,1)} %get-tuple-element.43) | copy-start | bytes 1572868
  125.9 41.1 %collective-permute-start.25 = (bf16[1,16,128,128]{3,2,1,0:T(8,128)(2,1)}, bf16[1,16,128,128]{3,2,1,0:T(8,128)(2,1)}, u32[]{:S(2)}, u32[]{:S(2)}) collective-permute-start(bf16[1,16,128,128]{3,2,1,0:T(8,128)(2,1)} %get-tuple-element.36), channel_id=1, source_target_pairs={{0,2},{2,0},{4,6},{6,4},{8,10},{10,8},{12,14},{14,12},{16,18},{18,... | collective-permute-start | bytes 1572872 | tf_op jit(solution)/shard_map/ppermute | solution.py:24
  126.1 5.5 %collective-permute-start.22 = (bf16[1,16,128,128]{3,2,1,0:T(8,128)(2,1)}, bf16[1,16,128,128]{3,2,1,0:T(8,128)(2,1)S(1)}, u32[]{:S(2)}, u32[]{:S(2)}) collective-permute-start(bf16[1,16,128,128]{3,2,1,0:T(8,128)(2,1)} %get-tuple-element.32), channel_id=1, source_target_pairs={{0,2},{2,0},{4,6},{6,4},{8,10},{10,8},{12,14},{14,12},{16,18},{18,... | collective-permute-start | bytes 1572872 | tf_op jit(solution)/shard_map/ppermute | solution.py:24
  126.4 20.7 %collective-permute-start.30 = (bf16[1,16,128,128]{3,2,1,0:T(8,128)(2,1)}, bf16[1,16,128,128]{3,2,1,0:T(8,128)(2,1)S(1)}, u32[]{:S(2)}, u32[]{:S(2)}) collective-permute-start(bf16[1,16,128,128]{3,2,1,0:T(8,128)(2,1)} %get-tuple-element.41), channel_id=1, source_target_pairs={{0,2},{2,0},{4,6},{6,4},{8,10},{10,8},{12,14},{14,12},{16,18},{18,... | collective-permute-start | bytes 1572872 | tf_op jit(solution)/shard_map/ppermute | solution.py:24
  127.5 3.7 %collective-permute-start.34 = (bf16[1,16,128,128]{3,2,1,0:T(8,128)(2,1)}, bf16[1,16,128,128]{3,2,1,0:T(8,128)(2,1)S(1)}, u32[]{:S(2)}, u32[]{:S(2)}) collective-permute-start(bf16[1,16,128,128]{3,2,1,0:T(8,128)(2,1)} %get-tuple-element.47), channel_id=1, source_target_pairs={{0,2},{2,0},{4,6},{6,4},{8,10},{10,8},{12,14},{14,12},{16,18},{18,... | collective-permute-start | bytes 1572872 | tf_op jit(solution)/shard_map/ppermute | solution.py:24
  127.7 16.1 %copy-start.20 = (bf16[1,16,128,128]{3,2,1,0:T(8,128)(2,1)S(1)}, bf16[1,16,128,128]{3,2,1,0:T(8,128)(2,1)}, u32[]{:S(2)}) copy-start(bf16[1,16,128,128]{3,2,1,0:T(8,128)(2,1)} %get-tuple-element.39) | copy-start | bytes 1572868
  129.0 14.7 %collective-permute-start.27 = (bf16[1,16,128,128]{3,2,1,0:T(8,128)(2,1)S(1)}, bf16[1,16,128,128]{3,2,1,0:T(8,128)(2,1)S(1)}, u32[]{:S(2)}, u32[]{:S(2)}) collective-permute-start(bf16[1,16,128,128]{3,2,1,0:T(8,128)(2,1)S(1)} %add_convert_fusion.2), channel_id=1, source_target_pairs={{0,4},{2,6},{4,0},{6,2},{8,12},{10,14},{12,8},{14,10},{16,20},{18,... | collective-permute-start | bytes 1572872 | tf_op jit(solution)/shard_map/ppermute | solution.py:24
  131.0 15.1 %copy-start.9 = (bf16[1,16,128,128]{3,2,1,0:T(8,128)(2,1)S(1)}, bf16[1,16,128,128]{3,2,1,0:T(8,128)(2,1)}, u32[]{:S(2)}) copy-start(bf16[1,16,128,128]{3,2,1,0:T(8,128)(2,1)} %get-tuple-element.42) | copy-start | bytes 1572868
  131.3 13.6 %collective-permute-start.31 = (bf16[1,16,128,128]{3,2,1,0:T(8,128)(2,1)S(1)}, bf16[1,16,128,128]{3,2,1,0:T(8,128)(2,1)S(1)}, u32[]{:S(2)}, u32[]{:S(2)}) collective-permute-start(bf16[1,16,128,128]{3,2,1,0:T(8,128)(2,1)S(1)} %copy-done.22), channel_id=1, source_target_pairs={{0,2},{2,0},{4,6},{6,4},{8,10},{10,8},{12,14},{14,12},{16,18},{18,... | collective-permute-start | bytes 1572872 | tf_op jit(solution)/shard_map/ppermute | solution.py:24
  131.6 34.4 %copy-start.19 = (bf16[1,16,128,128]{3,2,1,0:T(8,128)(2,1)S(1)}, bf16[1,16,128,128]{3,2,1,0:T(8,128)(2,1)}, u32[]{:S(2)}) copy-start(bf16[1,16,128,128]{3,2,1,0:T(8,128)(2,1)} %get-tuple-element.48) | copy-start | bytes 1572868
  131.6 36.7 %collective-permute-start.24 = (bf16[1,16,128,128]{3,2,1,0:T(8,128)(2,1)}, bf16[1,16,128,128]{3,2,1,0:T(8,128)(2,1)S(1)}, u32[]{:S(2)}, u32[]{:S(2)}) collective-permute-start(bf16[1,16,128,128]{3,2,1,0:T(8,128)(2,1)} %add_convert_fusion.3), channel_id=1, source_target_pairs={{0,4},{2,6},{4,0},{6,2},{8,12},{10,14},{12,8},{14,10},{16,20},{18,... | collective-permute-start | bytes 1572872 | tf_op jit(solution)/shard_map/ppermute | solution.py:24
  143.8 21.9 %collective-permute-start.35 = (bf16[1,16,128,128]{3,2,1,0:T(8,128)(2,1)S(1)}, bf16[1,16,128,128]{3,2,1,0:T(8,128)(2,1)S(1)}, u32[]{:S(2)}, u32[]{:S(2)}) collective-permute-start(bf16[1,16,128,128]{3,2,1,0:T(8,128)(2,1)S(1)} %add_convert_fusion), channel_id=1, source_target_pairs={{0,4},{2,6},{4,0},{6,2},{8,12},{10,14},{12,8},{14,10},{16,20},{18,... | collective-permute-start | bytes 1572872 | tf_op jit(solution)/shard_map/ppermute | solution.py:24
  144.8 23.5 %collective-permute-start.28 = (bf16[1,16,128,128]{3,2,1,0:T(8,128)(2,1)}, bf16[1,16,128,128]{3,2,1,0:T(8,128)(2,1)}, u32[]{:S(2)}, u32[]{:S(2)}) collective-permute-start(bf16[1,16,128,128]{3,2,1,0:T(8,128)(2,1)} %fusion.6), channel_id=1, source_target_pairs={{8,0},{10,2},{12,4},{14,6},{16,8},{18,10},{20,12},{22,14},{24,16},... | collective-permute-start | bytes 1572872 | tf_op jit(solution)/shard_map/ppermute | solution.py:20
  147.1 25.5 %collective-permute-start.33 = (bf16[1,16,128,128]{3,2,1,0:T(8,128)(2,1)}, bf16[1,16,128,128]{3,2,1,0:T(8,128)(2,1)}, u32[]{:S(2)}, u32[]{:S(2)}) collective-permute-start(bf16[1,16,128,128]{3,2,1,0:T(8,128)(2,1)} %get-tuple-element.45), channel_id=1, source_target_pairs={{0,2},{2,0},{4,6},{6,4},{8,10},{10,8},{12,14},{14,12},{16,18},{18,... | collective-permute-start | bytes 1572872 | tf_op jit(solution)/shard_map/ppermute | solution.py:24
  165.6 13.6 %collective-permute-start.32 = (bf16[1,16,128,128]{3,2,1,0:T(8,128)(2,1)}, bf16[1,16,128,128]{3,2,1,0:T(8,128)(2,1)S(1)}, u32[]{:S(2)}, u32[]{:S(2)}) collective-permute-start(bf16[1,16,128,128]{3,2,1,0:T(8,128)(2,1)} %add_convert_fusion.1), channel_id=1, source_target_pairs={{0,4},{2,6},{4,0},{6,2},{8,12},{10,14},{12,8},{14,10},{16,20},{18,... | collective-permute-start | bytes 1572872 | tf_op jit(solution)/shard_map/ppermute | solution.py:24
  167.0 17.0 %collective-permute-start.36 = (bf16[1,16,128,128]{3,2,1,0:T(8,128)(2,1)}, bf16[1,16,128,128]{3,2,1,0:T(8,128)(2,1)}, u32[]{:S(2)}, u32[]{:S(2)}) collective-permute-start(bf16[1,16,128,128]{3,2,1,0:T(8,128)(2,1)} %fusion.16), channel_id=1, source_target_pairs={{8,0},{10,2},{12,4},{14,6},{16,8},{18,10},{20,12},{22,14},{24,16},... | collective-permute-start | bytes 1572872 | tf_op jit(solution)/shard_map/ppermute | solution.py:20
  168.3 15.8 %copy-start.18 = (bf16[1,16,128,128]{3,2,1,0:T(8,128)(2,1)S(1)}, bf16[1,16,128,128]{3,2,1,0:T(8,128)(2,1)}, u32[]{:S(2)}) copy-start(bf16[1,16,128,128]{3,2,1,0:T(8,128)(2,1)} %get-tuple-element.44) | copy-start | bytes 1572868
  168.3 18.1 %copy-start.2 = (bf16[1,16,128,128]{3,2,1,0:T(8,128)(2,1)}, bf16[1,16,128,128]{3,2,1,0:T(8,128)(2,1)S(1)}, u32[]{:S(2)}) copy-start(bf16[1,16,128,128]{3,2,1,0:T(8,128)(2,1)S(1)} %collective-permute-done.24) | copy-start | bytes 1572868
  171.1 16.6 %copy-start.1 = (f32[16,128,256]{2,1,0:T(8,128)S(1)}, f32[16,128,256]{2,1,0:T(8,128)}, u32[]{:S(2)}) copy-start(f32[16,128,256]{2,1,0:T(8,128)} %get-tuple-element.30) | copy-start | bytes 6291460
  171.1 24.2 %collective-permute-start.29 = (bf16[1,16,128,128]{3,2,1,0:T(8,128)(2,1)}, bf16[1,16,128,128]{3,2,1,0:T(8,128)(2,1)}, u32[]{:S(2)}, u32[]{:S(2)}) collective-permute-start(bf16[1,16,128,128]{3,2,1,0:T(8,128)(2,1)} %fusion.9), channel_id=1, source_target_pairs={{8,0},{10,2},{12,4},{14,6},{16,8},{18,10},{20,12},{22,14},{24,16},... | collective-permute-start | bytes 1572872 | tf_op jit(solution)/shard_map/ppermute | solution.py:20
  179.2 8.5 %copy-start.4 = (bf16[1,16,128,128]{3,2,1,0:T(8,128)(2,1)}, bf16[1,16,128,128]{3,2,1,0:T(8,128)(2,1)S(1)}, u32[]{:S(2)}) copy-start(bf16[1,16,128,128]{3,2,1,0:T(8,128)(2,1)S(1)} %collective-permute-done.32) | copy-start | bytes 1572868
  186.5 18.6 %collective-permute-start.37 = (bf16[1,16,128,128]{3,2,1,0:T(8,128)(2,1)}, bf16[1,16,128,128]{3,2,1,0:T(8,128)(2,1)}, u32[]{:S(2)}, u32[]{:S(2)}) collective-permute-start(bf16[1,16,128,128]{3,2,1,0:T(8,128)(2,1)} %fusion.19), channel_id=1, source_target_pairs={{8,0},{10,2},{12,4},{14,6},{16,8},{18,10},{20,12},{22,14},{24,16},... | collective-permute-start | bytes 1572872 | tf_op jit(solution)/shard_map/ppermute | solution.py:20
  188.3 7.0 %copy-start.3 = (bf16[1,16,128,128]{3,2,1,0:T(8,128)(2,1)S(1)}, bf16[1,16,128,128]{3,2,1,0:T(8,128)(2,1)}, u32[]{:S(2)}) copy-start(bf16[1,16,128,128]{3,2,1,0:T(8,128)(2,1)} %copy-done.2) | copy-start | bytes 1572868
  192.1 13.0 %copy-start.5 = (bf16[1,16,128,128]{3,2,1,0:T(8,128)(2,1)S(1)}, bf16[1,16,128,128]{3,2,1,0:T(8,128)(2,1)}, u32[]{:S(2)}) copy-start(bf16[1,16,128,128]{3,2,1,0:T(8,128)(2,1)} %copy-done.4) | copy-start | bytes 1572868
  192.1 13.0 %copy-start.8 = (bf16[1,16,128,128]{3,2,1,0:T(8,128)(2,1)S(1)}, bf16[1,16,128,128]{3,2,1,0:T(8,128)(2,1)}, u32[]{:S(2)}) copy-start(bf16[1,16,128,128]{3,2,1,0:T(8,128)(2,1)} %get-tuple-element.40) | copy-start | bytes 1572868

commit v9 on v7

--- a/solution.py
+++ b/solution.py
@@ -78,29 +78,33 @@
         dq_ref[g] = dq
 
 
-def attend_blocks(modes, dist, idx, q4, do4, lse3, delta3, acc, kvs):
+def attend_blocks(modes, dist, idx, q4, do4, lse3, delta3, acc, kvs, heads=None):
     nh, grp, tok, width = q4.shape
     gb = HEADS_PER_STEP
+    h0, h1 = (0, nh) if heads is None else heads
+    o = h0 // gb
     nb = len(modes)
     valid = jnp.stack([(idx >= d).astype(jnp.int32) for d in dist])
-    hspec = pl.BlockSpec((gb, grp, tok, width), lambda i, v: (i, 0, 0, 0))
+    nsel = h1 - h0
+    hspec = pl.BlockSpec((gb, grp, tok, width), lambda i, v: (i + o, 0, 0, 0))
     tspec = pl.BlockSpec((gb, width, grp * tok), lambda i, v: (i, 0, 0))
-    rspec = pl.BlockSpec((gb, 1, grp * tok), lambda i, v: (i, 0, 0))
-    kvspec = pl.BlockSpec((1, gb, tok, width), lambda i, v: (0, i, 0, 0))
+    rspec = pl.BlockSpec((gb, 1, grp * tok), lambda i, v: (i + o, 0, 0))
+    kvspec = pl.BlockSpec((1, gb, tok, width), lambda i, v: (0, i + o, 0, 0))
+    outspec = pl.BlockSpec((1, gb, tok, width), lambda i, v: (0, i, 0, 0))
     accs = [] if acc is None else [acc]
-    out_shape = [jax.ShapeDtypeStruct((nh, width, grp * tok), jnp.float32)]
-    out_shape += [jax.ShapeDtypeStruct(kv.shape, jnp.bfloat16) for kv in kvs]
+    out_shape = [jax.ShapeDtypeStruct((nsel, width, grp * tok), jnp.float32)]
+    out_shape += [jax.ShapeDtypeStruct((1, nsel) + kv.shape[2:], jnp.bfloat16) for kv in kvs]
     grid_spec = pltpu.PrefetchScalarGridSpec(
         num_scalar_prefetch=1,
-        grid=(nh // gb,),
+        grid=(nsel // gb,),
         in_specs=[hspec, hspec, rspec, rspec] + [tspec] * len(accs) + [kvspec] * (2 * nb),
-        out_specs=[tspec] + [kvspec] * (2 * nb),
-    )
-    scores = nh * grp * tok * tok * nb
+        out_specs=[tspec] + [outspec] * (2 * nb),
+    )
+    scores = nsel * grp * tok * tok * nb
     cost = pl.CostEstimate(
         flops=10 * scores * width,
         transcendentals=scores,
-        bytes_accessed=(2 + 2 * len(accs)) * q4.size * 2 + 2 * sum(kv.size for kv in kvs) * 2,
+        bytes_accessed=((2 + 2 * len(accs)) * q4.size * 2 + 2 * sum(kv.size for kv in kvs) * 2) * nsel // nh,
     )
     outs = pl.pallas_call(
         functools.partial(_blocks_kernel, tuple(modes), acc is not None),
@@ -179,22 +183,36 @@
     early = [0, 1, 2]
     modes = [0, 1, 1, 2, 1, 1, 1, 1, 1]
     dist = [0, PLANE, 3 + 2 * core, 2 * PLANE, 7 - 6 * core, 2, 1 + 2 * core, 6, 5 + 2 * core]
-    terms = [None] * 18
-    acc = None
-    ys = None
+    spans = ((0, heads_kv // 2), (heads_kv // 2, heads_kv))
     qb = q4
-    for sel in (late, early):
+    accs = []
+    halves = []
+    for span in spans:
         acc, out = attend_blocks(
-            [modes[j] for j in sel], [dist[j] for j in sel], idx, qb, do4, lse3, delta3, acc,
-            [kb[j] for j in sel] + [vb[j] for j in sel])
-        for m, j in enumerate(sel):
-            terms[j] = out[m]
-            terms[9 + j] = out[len(sel) + m]
-        if ys is None:
-            ys = gather_y(terms[:9], n) + gather_y(terms[9:], n)
-            ys, qb = lax.optimization_barrier((ys, q4))
-    grad_k = unroute(terms[:9], ys[0], ys[1], n, half, core)
-    grad_v = unroute(terms[9:], ys[2], ys[3], n, half, core)
+            [modes[j] for j in late], [dist[j] for j in late], idx, qb, do4, lse3, delta3, None,
+            [kb[j] for j in late] + [vb[j] for j in late], heads=span)
+        accs.append(acc)
+        tk = [None] * 9
+        tv = [None] * 9
+        for m, j in enumerate(late):
+            tk[j] = out[m]
+            tv[j] = out[len(late) + m]
+        ys = gather_y(tk, n) + gather_y(tv, n)
+        ys, qb = lax.optimization_barrier((ys, q4))
+        halves.append((tk, tv, ys))
+    acc, out = attend_blocks(
+        [modes[j] for j in early], [dist[j] for j in early], idx, qb, do4, lse3, delta3,
+        jnp.concatenate(accs, axis=0), [kb[j] for j in early] + [vb[j] for j in early])
+    gk = []
+    gv = []
+    for (h0, h1), (tk, tv, ys) in zip(spans, halves):
+        for m, j in enumerate(early):
+            tk[j] = out[m][:, h0:h1]
+            tv[j] = out[len(early) + m][:, h0:h1]
+        gk.append(unroute(tk, ys[0], ys[1], n, half, core))
+        gv.append(unroute(tv, ys[2], ys[3], n, half, core))
+    grad_k = jnp.concatenate(gk, axis=1)
+    grad_v = jnp.concatenate(gv, axis=1)
 
     dq = (acc * SCALE).astype(jnp.bfloat16).reshape(heads_kv, width, groups, tok)
     grad_query = dq.transpose(3, 0, 2, 1).reshape(tok, heads_q, width)

time: 188 us -> 207 us (1.10)
  starting transfers between devices: 60.2 us -> 71.4 us
  other arithmetic: 22.5 us -> 25.8 us
  local copies, waits for them, and re-layouts: 14.1 us -> 17.4 us
  Pallas kernels: 36 us -> 38.7 us
    ppermute x8 -> x12, waiting for transfers between devices: 19.2 us -> 29 us  [shift(): return lax.ppermute(x, 'seq', pairs)]
    ppermute x18 -> x30, waiting for transfers between devices: 21.4 us -> 11.9 us  [swap(): return lax.ppermute(x, 'seq', [(i, i ^ bit) for i in range(n)])]
    ppermute x18 -> x30, starting transfers between devices: 7.78 us -> 14.6 us  [swap(): return lax.ppermute(x, 'seq', [(i, i ^ bit) for i in range(n)])]
    ppermute x8 -> x12, starting transfers between devices: 23.6 us -> 27.9 us  [shift(): return lax.ppermute(x, 'seq', pairs)]
    concatenate x0 -> x1, other arithmetic: none -> 2.87 us  [per_device(): jnp.concatenate(accs, axis=0)]
    convert_element_type x2, other arithmetic: 5.07 us -> 2.28 us  [unroute(): part0 = part0 + shift(part1.astype(bf16), n, -PLANE).astype(f32)]
    pallas_call x2 -> x3, Pallas kernels: 36 us -> 38.7 us  [attend_blocks(): pl.pallas_call(functools.partial(_blocks_kernel, tuple(modes), acc is not...]
    convert_element_type x2 -> x4, other arithmetic: 3 us -> 4.99 us  [gather_y(): ys0 = (ty0.astype(f32) + swap(td0, n, 1).astype(f32)).astype(bf16)]
  transfers between devices with their start and end apart: 38 -> 54, of which waited for: 14 -> 18; matrix products, arithmetic and copies ran while one was open for 17% -> 18% of each run, Pallas kernels for 7% -> 7%
where the time goes in v9:
time: 207 us; the launch traced here: 206 us
  starting transfers between devices  71.4 us (34%)
  waiting for transfers between devices  51.3 us (25%)
  Pallas kernels  38.7 us (19%)
  other arithmetic  25.8 us (12%)
  local copies, waits for them, and re-layouts  17.4 us (8%)
    pallas_call x3, Pallas kernels, attend_blocks(): pl.pallas_call(functools.partial(_blocks_kernel, tuple(modes), acc is not...  38.7 us
    ppermute x12, waiting for transfers between devices, shift(): return lax.ppermute(x, 'seq', pairs)  29 us
    ppermute x12, starting transfers between devices, one_way(): return lax.ppermute(x, 'seq', pairs)  29 us
    ppermute x12, starting transfers between devices, shift(): return lax.ppermute(x, 'seq', pairs)  27.9 us
    ppermute x30, starting transfers between devices, swap(): return lax.ppermute(x, 'seq', [(i, i ^ bit) for i in range(n)])  14.6 us
    ppermute x30, waiting for transfers between devices, swap(): return lax.ppermute(x, 'seq', [(i, i ^ bit) for i in range(n)])  11.9 us
    ppermute x12, waiting for transfers between devices, one_way(): return lax.ppermute(x, 'seq', pairs)  10.5 us
    unnamed x98, local copies, waits for them, and re-layouts  8.13 us
  transfers between devices with their start and end apart: 54, of which 18 were waited for; matrix products, arithmetic and copies ran while one was open for 18% of the time, Pallas kernels for 7%

profile of v9, /device:TPU:0, one launch (start us, length us, event | category | flops | bytes accessed | tf_op | source)
XLA Modules:
  0.0 206.1 jit_solution(5244213910341837750)
XLA Ops:
  0.7 2.1 %copy.27 = bf16[128,16,128]{2,0,1:T(8,128)(2,1)} copy(bf16[128,16,128]{2,1,0:T(8,128)(2,1)} %param.7) | data formatting | bytes 1048576 | tf_op args[1]
  2.8 5.7 %collective-permute-start = (bf16[1,16,128,128]{3,2,1,0:T(8,128)(2,1)}, bf16[1,16,128,128]{3,2,1,0:T(8,128)(2,1)}, u32[]{:S(2)}, u32[]{:S(2)}) collective-permute-start(bf16[1,16,128,128]{3,2,1,0:T(8,128)(2,1)} %bitcast.35.refs_1_), channel_id=1, source_target_pairs={{0,8},{2,10},{4,12},{6,14},{8,16},{10,18},{12,20},{14,22},{16,24},... | collective-permute-start | bytes 1572872 | tf_op jit(solution)/shard_map/ppermute | solution.py:20
  8.5 2.0 copy.26
  10.5 3.5 %collective-permute-start.10 = (bf16[1,16,128,128]{3,2,1,0:T(8,128)(2,1)}, bf16[1,16,128,128]{3,2,1,0:T(8,128)(2,1)}, u32[]{:S(2)}, u32[]{:S(2)}) collective-permute-start(bf16[1,16,128,128]{3,2,1,0:T(8,128)(2,1)} %bitcast.34.refs_4_), channel_id=1, source_target_pairs={{0,8},{2,10},{4,12},{6,14},{8,16},{10,18},{12,20},{14,22},{16,24},... | collective-permute-start | bytes 1572872 | tf_op jit(solution)/shard_map/ppermute | solution.py:20
  14.0 4.2 %collective-permute-start.4 = (bf16[1,16,128,128]{3,2,1,0:T(8,128)(2,1)}, bf16[1,16,128,128]{3,2,1,0:T(8,128)(2,1)}, u32[]{:S(2)}, u32[]{:S(2)}) collective-permute-start(bf16[1,16,128,128]{3,2,1,0:T(8,128)(2,1)} %bitcast.35.refs_1_), channel_id=1, source_target_pairs={{0,4},{2,6},{8,12},{10,14},{16,20},{18,22},{24,28},{26,30},{1,5},{... | collective-permute-start | bytes 1572872 | tf_op jit(solution)/shard_map/ppermute | solution.py:29
  18.2 2.1 %collective-permute-done.refs_2_ = bf16[1,16,128,128]{3,2,1,0:T(8,128)(2,1)} collective-permute-done((bf16[1,16,128,128]{3,2,1,0:T(8,128)(2,1)}, bf16[1,16,128,128]{3,2,1,0:T(8,128)(2,1)}, u32[]{:S(2)}, u32[]{:S(2)}) %collective-permute-start) | collective-permute-done | bytes 524320 | tf_op jit(solution)/shard_map/ppermute | solution.py:20
  20.3 4.4 %collective-permute-start.1 = (bf16[1,16,128,128]{3,2,1,0:T(8,128)(2,1)}, bf16[1,16,128,128]{3,2,1,0:T(8,128)(2,1)S(1)}, u32[]{:S(2)}, u32[]{:S(2)}) collective-permute-start(bf16[1,16,128,128]{3,2,1,0:T(8,128)(2,1)} %collective-permute-done.refs_2_), channel_id=1, source_target_pairs={{0,8},{2,10},{4,12},{6,14},{8,16},{10,18},{12,20},{14,22},{16,24},... | collective-permute-start | bytes 1572872 | tf_op jit(solution)/shard_map/ppermute | solution.py:20
  24.7 1.3 collective-permute-start.5
  26.0 6.2 %collective-permute-start.14 = (bf16[1,16,128,128]{3,2,1,0:T(8,128)(2,1)}, bf16[1,16,128,128]{3,2,1,0:T(8,128)(2,1)}, u32[]{:S(2)}, u32[]{:S(2)}) collective-permute-start(bf16[1,16,128,128]{3,2,1,0:T(8,128)(2,1)} %bitcast.34.refs_4_), channel_id=1, source_target_pairs={{0,4},{2,6},{8,12},{10,14},{16,20},{18,22},{24,28},{26,30},{1,5},{... | collective-permute-start | bytes 1572872 | tf_op jit(solution)/shard_map/ppermute | solution.py:29
  32.2 3.8 %collective-permute-start.11 = (bf16[1,16,128,128]{3,2,1,0:T(8,128)(2,1)}, bf16[1,16,128,128]{3,2,1,0:T(8,128)(2,1)S(1)}, u32[]{:S(2)}, u32[]{:S(2)}) collective-permute-start(bf16[1,16,128,128]{3,2,1,0:T(8,128)(2,1)} %collective-permute-done.10.refs_5_), channel_id=1, source_target_pairs={{0,8},{2,10},{4,12},{6,14},{8,16},{10,18},{12,20},{14,22},{16,24},... | collective-permute-start | bytes 1572872 | tf_op jit(solution)/shard_map/ppermute | solution.py:20
  36.0 1.3 collective-permute-start.15
  38.0 1.4 copy.16
  39.3 1.4 copy.17
  42.8 4.6 %collective-permute-start.7 = (bf16[1,16,128,128]{3,2,1,0:T(8,128)(2,1)}, bf16[1,16,128,128]{3,2,1,0:T(8,128)(2,1)S(1)}, u32[]{:S(2)}, u32[]{:S(2)}) collective-permute-start(bf16[1,16,128,128]{3,2,1,0:T(8,128)(2,1)} %collective-permute-done.refs_2_), channel_id=1, source_target_pairs={{0,4},{2,6},{8,12},{10,14},{16,20},{18,22},{24,28},{26,30},{1,5},{... | collective-permute-start | bytes 1572872 | tf_op jit(solution)/shard_map/ppermute | solution.py:29
  47.4 1.3 collective-permute-start.8
  48.7 1.1 broadcast_select_fusion.3.refs_2_
  49.8 1.3 collective-permute-start.2
  51.2 1.7 collective-permute-done.11.refs_6_
  52.9 3.4 %collective-permute-start.17 = (bf16[1,16,128,128]{3,2,1,0:T(8,128)(2,1)}, bf16[1,16,128,128]{3,2,1,0:T(8,128)(2,1)S(1)}, u32[]{:S(2)}, u32[]{:S(2)}) collective-permute-start(bf16[1,16,128,128]{3,2,1,0:T(8,128)(2,1)} %collective-permute-done.10.refs_5_), channel_id=1, source_target_pairs={{0,4},{2,6},{8,12},{10,14},{16,20},{18,22},{24,28},{26,30},{1,5},{... | collective-permute-start | bytes 1572872 | tf_op jit(solution)/shard_map/ppermute | solution.py:29
  56.3 1.3 collective-permute-start.18
  57.6 1.1 broadcast_select_fusion.1.refs_8_
  58.8 1.3 collective-permute-start.12
  60.1 1.7 collective-permute-done.8
  61.8 1.3 collective-permute-start.3
  63.2 4.3 %collective-permute-done.17 = bf16[1,16,128,128]{3,2,1,0:T(8,128)(2,1)S(1)} collective-permute-done((bf16[1,16,128,128]{3,2,1,0:T(8,128)(2,1)}, bf16[1,16,128,128]{3,2,1,0:T(8,128)(2,1)S(1)}, u32[]{:S(2)}, u32[]{:S(2)}) %collective-permute-start.17) | collective-permute-done | bytes 524320 | tf_op jit(solution)/shard_map/ppermute | solution.py:29
  67.5 4.4 %collective-permute-done.18 = bf16[1,16,128,128]{3,2,1,0:T(8,128)(2,1)S(1)} collective-permute-done((bf16[1,16,128,128]{3,2,1,0:T(8,128)(2,1)S(1)}, bf16[1,16,128,128]{3,2,1,0:T(8,128)(2,1)S(1)}, u32[]{:S(2)}, u32[]{:S(2)}) %collective-permute-start.18) | collective-permute-done | bytes 524320 | tf_op jit(solution)/shard_map/ppermute | solution.py:29
  71.9 1.5 collective-permute-start.13
  73.5 1.2 collective-permute-start.16
  76.1 0.9 broadcast_select_fusion.4.refs_7_
  78.8 12.5 %shard_map.85 = (f32[8,128,256]{2,1,0:T(8,128)}, bf16[1,8,128,128]{3,2,1,0:T(8,128)(2,1)}, bf16[1,8,128,128]{3,2,1,0:T(8,128)(2,1)}, bf16[1,8,128,128]{3,2,1,0:T...) custom-call(s32[6]{0:T(128)} %stack.65.valid_ref, ...), custom_call_target="tpu_custom_call" | custom-call | flops 2013265920 | bytes 7340032 | tf_op jit(solution)/shard_map/pallas_call | solution.py:109
  93.1 1.7 add_convert_fusion.7
  94.8 1.0 add_convert_fusion.6
  95.9 1.7 add_convert_fusion.5
  98.4 12.7 %shard_map.86 = (f32[8,128,256]{2,1,0:T(8,128)}, bf16[1,8,128,128]{3,2,1,0:T(8,128)(2,1)}, bf16[1,8,128,128]{3,2,1,0:T(8,128)(2,1)}, bf16[1,8,128,128]{3,2,1,0:T...) custom-call(s32[6]{0:T(128)} %stack.65.valid_ref, ...), custom_call_target="tpu_custom_call" | custom-call | flops 2013265920 | bytes 7340032 | tf_op jit(solution)/shard_map/pallas_call | solution.py:109
  113.1 2.9 %pad_maximum_fusion.refs_0_ = f32[16,128,256]{2,1,0:T(8,128)} fusion(f32[8,128,256]{2,1,0:T(8,128)} %get-tuple-element.65, f32[8,128,256]{2,1,0:T(8,128)S(1)} %copy-done.13), kind=kLoop, calls=%fused_computation | loop fusion | flops 524288 | bytes 4194304 | tf_op jit(solution)/shard_map/concatenate | solution.py:205
  119.9 2.0 collective-permute-start.33
  123.6 13.5 %shard_map.87 = (f32[16,128,256]{2,1,0:T(8,128)}, bf16[1,16,128,128]{3,2,1,0:T(8,128)(2,1)}, bf16[1,16,128,128]{3,2,1,0:T(8,128)(2,1)}, bf16[1,16,128,128]{3,2,1...) custom-call(s32[3]{0:T(128)} %add_convert_fusion.8.valid_ref, ...), custom_call_target="tpu_custom_call" | custom-call | flops 2013265920 | bytes 10485760 | tf_op jit(solution)/shard_map/pallas_call | solution.py:109
  137.1 2.0 multiply_convert_fusion
  139.3 1.3 collective-permute-start.43
  143.4 1.2 collective-permute-start.51
  144.6 0.9 fusion.41
  145.5 8.5 %collective-permute-done.39 = bf16[1,8,128,128]{3,2,1,0:T(8,128)(2,1)S(1)} collective-permute-done((bf16[1,8,128,128]{3,2,1,0:T(8,128)(2,1)S(1)}, bf16[1,8,128,128]{3,2,1,0:T(8,128)(2,1)S(1)}, u32[]{:S(2)}, u32[]{:S(2)}) %collective-permute-start.39) | collective-permute-done | bytes 262176 | tf_op jit(solution)/shard_map/ppermute | solution.py:24
  154.1 1.3 collective-permute-start.34
  156.2 1.3 collective-permute-start.37
  157.7 1.5 collective-permute-done.51
  159.2 1.3 collective-permute-start.40
  161.7 3.8 %copy.21 = bf16[128,16,2,128]{3,2,1,0:T(2,128)(2,1)} copy(bf16[128,16,2,128]{0,2,3,1:T(2,128)(2,1)S(1)} %bitcast.43) | data formatting | bytes 2097152 | tf_op jit(solution)/shard_map/transpose | solution.py:218
  165.7 1.4 collective-permute-start.46
  167.2 1.3 collective-permute-start.49
  169.4 1.3 collective-permute-start.52
  170.7 1.9 fusion.9
  172.5 5.2 %collective-permute-done.46 = bf16[1,8,128,128]{3,2,1,0:T(8,128)(2,1)S(1)} collective-permute-done((bf16[1,8,128,128]{3,2,1,0:T(8,128)(2,1)}, bf16[1,8,128,128]{3,2,1,0:T(8,128)(2,1)S(1)}, u32[]{:S(2)}, u32[]{:S(2)}) %collective-permute-start.46) | collective-permute-done | bytes 262176 | tf_op jit(solution)/shard_map/ppermute | solution.py:20
  177.8 1.3 collective-permute-start.35
  179.1 1.3 collective-permute-start.41
  180.4 3.0 %collective-permute-done.52 = bf16[1,8,128,128]{3,2,1,0:T(8,128)(2,1)S(1)} collective-permute-done((bf16[1,8,128,128]{3,2,1,0:T(8,128)(2,1)S(1)}, bf16[1,8,128,128]{3,2,1,0:T(8,128)(2,1)S(1)}, u32[]{:S(2)}, u32[]{:S(2)}) %collective-permute-start.52) | collective-permute-done | bytes 262176 | tf_op jit(solution)/shard_map/ppermute | solution.py:20
  183.8 1.3 collective-permute-start.47
  185.1 1.3 collective-permute-start.53
  186.4 2.6 %collective-permute-done.35 = bf16[1,8,128,128]{3,2,1,0:T(8,128)(2,1)S(1)} collective-permute-done((bf16[1,8,128,128]{3,2,1,0:T(8,128)(2,1)S(1)}, bf16[1,8,128,128]{3,2,1,0:T(8,128)(2,1)S(1)}, u32[]{:S(2)}, u32[]{:S(2)}) %collective-permute-start.35) | collective-permute-done | bytes 262176 | tf_op jit(solution)/shard_map/ppermute | solution.py:20
  189.0 5.6 %collective-permute-done.41 = bf16[1,8,128,128]{3,2,1,0:T(8,128)(2,1)S(1)} collective-permute-done((bf16[1,8,128,128]{3,2,1,0:T(8,128)(2,1)S(1)}, bf16[1,8,128,128]{3,2,1,0:T(8,128)(2,1)S(1)}, u32[]{:S(2)}, u32[]{:S(2)}) %collective-permute-start.41) | collective-permute-done | bytes 262176 | tf_op jit(solution)/shard_map/ppermute | solution.py:20
  194.6 1.4 fusion.3
  196.0 1.1 copy.22
  197.2 3.1 %collective-permute-done.47 = bf16[1,8,128,128]{3,2,1,0:T(8,128)(2,1)S(1)} collective-permute-done((bf16[1,8,128,128]{3,2,1,0:T(8,128)(2,1)S(1)}, bf16[1,8,128,128]{3,2,1,0:T(8,128)(2,1)S(1)}, u32[]{:S(2)}, u32[]{:S(2)}) %collective-permute-start.47) | collective-permute-done | bytes 262176 | tf_op jit(solution)/shard_map/ppermute | solution.py:20
  200.2 4.3 %collective-permute-done.53 = bf16[1,8,128,128]{3,2,1,0:T(8,128)(2,1)S(1)} collective-permute-done((bf16[1,8,128,128]{3,2,1,0:T(8,128)(2,1)S(1)}, bf16[1,8,128,128]{3,2,1,0:T(8,128)(2,1)S(1)}, u32[]{:S(2)}, u32[]{:S(2)}) %collective-permute-start.53) | collective-permute-done | bytes 262176 | tf_op jit(solution)/shard_map/ppermute | solution.py:20
  205.0 1.1 copy.23
  (182 shorter events, 23.1 us)
Async XLA Ops:
  0.6 37.3 %copy-start.11 = (bf16[128,32,128]{2,1,0:T(8,128)(2,1)S(1)}, bf16[128,32,128]{2,1,0:T(8,128)(2,1)}, u32[]{:S(2)}) copy-start(bf16[128,32,128]{2,1,0:T(8,128)(2,1)} %param.6) | copy-start | bytes 3145732
  0.6 38.7 %copy-start.4 = (bf16[128,32,128]{2,1,0:T(8,128)(2,1)S(1)}, bf16[128,32,128]{2,1,0:T(8,128)(2,1)}, u32[]{:S(2)}) copy-start(bf16[128,32,128]{2,1,0:T(8,128)(2,1)} %param.10) | copy-start | bytes 3145732
  2.8 17.6 %collective-permute-start = (bf16[1,16,128,128]{3,2,1,0:T(8,128)(2,1)}, bf16[1,16,128,128]{3,2,1,0:T(8,128)(2,1)}, u32[]{:S(2)}, u32[]{:S(2)}) collective-permute-start(bf16[1,16,128,128]{3,2,1,0:T(8,128)(2,1)} %bitcast.35.refs_1_), channel_id=1, source_target_pairs={{0,8},{2,10},{4,12},{6,14},{8,16},{10,18},{12,20},{14,22},{16,24},... | collective-permute-start | bytes 1572872 | tf_op jit(solution)/shard_map/ppermute | solution.py:20
  10.5 21.7 %collective-permute-start.10 = (bf16[1,16,128,128]{3,2,1,0:T(8,128)(2,1)}, bf16[1,16,128,128]{3,2,1,0:T(8,128)(2,1)}, u32[]{:S(2)}, u32[]{:S(2)}) collective-permute-start(bf16[1,16,128,128]{3,2,1,0:T(8,128)(2,1)} %bitcast.34.refs_4_), channel_id=1, source_target_pairs={{0,8},{2,10},{4,12},{6,14},{8,16},{10,18},{12,20},{14,22},{16,24},... | collective-permute-start | bytes 1572872 | tf_op jit(solution)/shard_map/ppermute | solution.py:20
  14.0 22.0 %collective-permute-start.4 = (bf16[1,16,128,128]{3,2,1,0:T(8,128)(2,1)}, bf16[1,16,128,128]{3,2,1,0:T(8,128)(2,1)}, u32[]{:S(2)}, u32[]{:S(2)}) collective-permute-start(bf16[1,16,128,128]{3,2,1,0:T(8,128)(2,1)} %bitcast.35.refs_1_), channel_id=1, source_target_pairs={{0,4},{2,6},{8,12},{10,14},{16,20},{18,22},{24,28},{26,30},{1,5},{... | collective-permute-start | bytes 1572872 | tf_op jit(solution)/shard_map/ppermute | solution.py:29
  20.3 22.5 %collective-permute-start.1 = (bf16[1,16,128,128]{3,2,1,0:T(8,128)(2,1)}, bf16[1,16,128,128]{3,2,1,0:T(8,128)(2,1)S(1)}, u32[]{:S(2)}, u32[]{:S(2)}) collective-permute-start(bf16[1,16,128,128]{3,2,1,0:T(8,128)(2,1)} %collective-permute-done.refs_2_), channel_id=1, source_target_pairs={{0,8},{2,10},{4,12},{6,14},{8,16},{10,18},{12,20},{14,22},{16,24},... | collective-permute-start | bytes 1572872 | tf_op jit(solution)/shard_map/ppermute | solution.py:20
  24.7 22.6 %collective-permute-start.5 = (bf16[1,16,128,128]{3,2,1,0:T(8,128)(2,1)}, bf16[1,16,128,128]{3,2,1,0:T(8,128)(2,1)}, u32[]{:S(2)}, u32[]{:S(2)}) collective-permute-start(bf16[1,16,128,128]{3,2,1,0:T(8,128)(2,1)} %collective-permute-done.refs_2_), channel_id=1, source_target_pairs={{4,0},{6,2},{12,8},{14,10},{20,16},{22,18},{28,24},{30,26},{5,1},{... | collective-permute-start | bytes 1572872 | tf_op jit(solution)/shard_map/ppermute | solution.py:29
  26.0 23.8 %collective-permute-start.14 = (bf16[1,16,128,128]{3,2,1,0:T(8,128)(2,1)}, bf16[1,16,128,128]{3,2,1,0:T(8,128)(2,1)}, u32[]{:S(2)}, u32[]{:S(2)}) collective-permute-start(bf16[1,16,128,128]{3,2,1,0:T(8,128)(2,1)} %bitcast.34.refs_4_), channel_id=1, source_target_pairs={{0,4},{2,6},{8,12},{10,14},{16,20},{18,22},{24,28},{26,30},{1,5},{... | collective-permute-start | bytes 1572872 | tf_op jit(solution)/shard_map/ppermute | solution.py:29
  32.2 20.7 %collective-permute-start.11 = (bf16[1,16,128,128]{3,2,1,0:T(8,128)(2,1)}, bf16[1,16,128,128]{3,2,1,0:T(8,128)(2,1)S(1)}, u32[]{:S(2)}, u32[]{:S(2)}) collective-permute-start(bf16[1,16,128,128]{3,2,1,0:T(8,128)(2,1)} %collective-permute-done.10.refs_5_), channel_id=1, source_target_pairs={{0,8},{2,10},{4,12},{6,14},{8,16},{10,18},{12,20},{14,22},{16,24},... | collective-permute-start | bytes 1572872 | tf_op jit(solution)/shard_map/ppermute | solution.py:20
  36.0 20.4 %collective-permute-start.15 = (bf16[1,16,128,128]{3,2,1,0:T(8,128)(2,1)}, bf16[1,16,128,128]{3,2,1,0:T(8,128)(2,1)}, u32[]{:S(2)}, u32[]{:S(2)}) collective-permute-start(bf16[1,16,128,128]{3,2,1,0:T(8,128)(2,1)} %collective-permute-done.10.refs_5_), channel_id=1, source_target_pairs={{4,0},{6,2},{12,8},{14,10},{20,16},{22,18},{28,24},{30,26},{5,1},{... | collective-permute-start | bytes 1572872 | tf_op jit(solution)/shard_map/ppermute | solution.py:29
  42.8 20.4 %copy-start.5 = (bf16[1,16,128,128]{3,2,1,0:T(8,128)(2,1)}, bf16[1,16,128,128]{3,2,1,0:T(8,128)(2,1)S(1)}, u32[]{:S(2)}) copy-start(bf16[1,16,128,128]{3,2,1,0:T(8,128)(2,1)S(1)} %collective-permute-done.1.refs_0_) | copy-start | bytes 1572868
  42.8 16.0 %collective-permute-start.7 = (bf16[1,16,128,128]{3,2,1,0:T(8,128)(2,1)}, bf16[1,16,128,128]{3,2,1,0:T(8,128)(2,1)S(1)}, u32[]{:S(2)}, u32[]{:S(2)}) collective-permute-start(bf16[1,16,128,128]{3,2,1,0:T(8,128)(2,1)} %collective-permute-done.refs_2_), channel_id=1, source_target_pairs={{0,4},{2,6},{8,12},{10,14},{16,20},{18,22},{24,28},{26,30},{1,5},{... | collective-permute-start | bytes 1572872 | tf_op jit(solution)/shard_map/ppermute | solution.py:29
  47.4 14.4 %collective-permute-start.8 = (bf16[1,16,128,128]{3,2,1,0:T(8,128)(2,1)S(1)}, bf16[1,16,128,128]{3,2,1,0:T(8,128)(2,1)S(1)}, u32[]{:S(2)}, u32[]{:S(2)}) collective-permute-start(bf16[1,16,128,128]{3,2,1,0:T(8,128)(2,1)S(1)} %collective-permute-done.1.refs_0_), channel_id=1, source_target_pairs={{4,0},{6,2},{12,8},{14,10},{20,16},{22,18},{28,24},{30,26},{5,1},{... | collective-permute-start | bytes 1572872 | tf_op jit(solution)/shard_map/ppermute | solution.py:29
  49.8 23.7 %copy-start = (bf16[1,16,128,128]{3,2,1,0:T(8,128)(2,1)}, bf16[1,16,128,128]{3,2,1,0:T(8,128)(2,1)S(1)}, u32[]{:S(2)}) copy-start(bf16[1,16,128,128]{3,2,1,0:T(8,128)(2,1)S(1)} %broadcast_select_fusion.3.refs_2_) | copy-start | bytes 1572868
  49.8 23.7 %collective-permute-start.2 = (bf16[1,16,128,128]{3,2,1,0:T(8,128)(2,1)}, bf16[1,16,128,128]{3,2,1,0:T(8,128)(2,1)S(1)}, u32[]{:S(2)}, u32[]{:S(2)}) collective-permute-start(bf16[1,16,128,128]{3,2,1,0:T(8,128)(2,1)} %bitcast.35.refs_1_), channel_id=1, source_target_pairs={{0,2},{4,6},{8,10},{12,14},{16,18},{20,22},{24,26},{28,30},{1,3},{... | collective-permute-start | bytes 1572872 | tf_op jit(solution)/shard_map/ppermute | solution.py:29
  52.9 20.6 %copy-start.6 = (bf16[1,16,128,128]{3,2,1,0:T(8,128)(2,1)}, bf16[1,16,128,128]{3,2,1,0:T(8,128)(2,1)S(1)}, u32[]{:S(2)}) copy-start(bf16[1,16,128,128]{3,2,1,0:T(8,128)(2,1)S(1)} %collective-permute-done.11.refs_6_) | copy-start | bytes 1572868
  52.9 14.6 %collective-permute-start.17 = (bf16[1,16,128,128]{3,2,1,0:T(8,128)(2,1)}, bf16[1,16,128,128]{3,2,1,0:T(8,128)(2,1)S(1)}, u32[]{:S(2)}, u32[]{:S(2)}) collective-permute-start(bf16[1,16,128,128]{3,2,1,0:T(8,128)(2,1)} %collective-permute-done.10.refs_5_), channel_id=1, source_target_pairs={{0,4},{2,6},{8,12},{10,14},{16,20},{18,22},{24,28},{26,30},{1,5},{... | collective-permute-start | bytes 1572872 | tf_op jit(solution)/shard_map/ppermute | solution.py:29
  56.3 15.6 %collective-permute-start.18 = (bf16[1,16,128,128]{3,2,1,0:T(8,128)(2,1)S(1)}, bf16[1,16,128,128]{3,2,1,0:T(8,128)(2,1)S(1)}, u32[]{:S(2)}, u32[]{:S(2)}) collective-permute-start(bf16[1,16,128,128]{3,2,1,0:T(8,128)(2,1)S(1)} %collective-permute-done.11.refs_6_), channel_id=1, source_target_pairs={{4,0},{6,2},{12,8},{14,10},{20,16},{22,18},{28,24},{30,26},{5,1},{... | collective-permute-start | bytes 1572872 | tf_op jit(solution)/shard_map/ppermute | solution.py:29
  58.8 15.9 %collective-permute-start.12 = (bf16[1,16,128,128]{3,2,1,0:T(8,128)(2,1)}, bf16[1,16,128,128]{3,2,1,0:T(8,128)(2,1)S(1)}, u32[]{:S(2)}, u32[]{:S(2)}) collective-permute-start(bf16[1,16,128,128]{3,2,1,0:T(8,128)(2,1)} %bitcast.34.refs_4_), channel_id=1, source_target_pairs={{0,2},{4,6},{8,10},{12,14},{16,18},{20,22},{24,26},{28,30},{1,3},{... | collective-permute-start | bytes 1572872 | tf_op jit(solution)/shard_map/ppermute | solution.py:29
  61.8 13.0 %collective-permute-start.3 = (bf16[1,16,128,128]{3,2,1,0:T(8,128)(2,1)S(1)}, bf16[1,16,128,128]{3,2,1,0:T(8,128)(2,1)S(1)}, u32[]{:S(2)}, u32[]{:S(2)}) collective-permute-start(bf16[1,16,128,128]{3,2,1,0:T(8,128)(2,1)S(1)} %collective-permute-done.1.refs_0_), channel_id=1, source_target_pairs={{2,0},{6,4},{10,8},{14,12},{18,16},{22,20},{26,24},{30,28},{3,1},{... | collective-permute-start | bytes 1572872 | tf_op jit(solution)/shard_map/ppermute | solution.py:29
  67.5 9.5 %collective-permute-start.6 = (bf16[1,16,128,128]{3,2,1,0:T(8,128)(2,1)S(1)}, bf16[1,16,128,128]{3,2,1,0:T(8,128)(2,1)S(1)}, u32[]{:S(2)}, u32[]{:S(2)}) collective-permute-start(bf16[1,16,128,128]{3,2,1,0:T(8,128)(2,1)S(1)} %broadcast_select_fusion.3.refs_2_), channel_id=1, source_target_pairs={{0,2},{2,0},{4,6},{6,4},{8,10},{10,8},{12,14},{14,12},{16,18},{18,... | collective-permute-start | bytes 1572872 | tf_op jit(solution)/shard_map/ppermute | solution.py:24
  71.9 4.2 %collective-permute-start.13 = (bf16[1,16,128,128]{3,2,1,0:T(8,128)(2,1)S(1)}, bf16[1,16,128,128]{3,2,1,0:T(8,128)(2,1)S(1)}, u32[]{:S(2)}, u32[]{:S(2)}) collective-permute-start(bf16[1,16,128,128]{3,2,1,0:T(8,128)(2,1)S(1)} %collective-permute-done.11.refs_6_), channel_id=1, source_target_pairs={{2,0},{6,4},{10,8},{14,12},{18,16},{22,20},{26,24},{30,28},{3,1},{... | collective-permute-start | bytes 1572872 | tf_op jit(solution)/shard_map/ppermute | solution.py:29
  73.5 3.5 %collective-permute-start.16 = (bf16[1,16,128,128]{3,2,1,0:T(8,128)(2,1)S(1)}, bf16[1,16,128,128]{3,2,1,0:T(8,128)(2,1)S(1)}, u32[]{:S(2)}, u32[]{:S(2)}) collective-permute-start(bf16[1,16,128,128]{3,2,1,0:T(8,128)(2,1)S(1)} %broadcast_select_fusion.1.refs_8_), channel_id=1, source_target_pairs={{0,2},{2,0},{4,6},{6,4},{8,10},{10,8},{12,14},{14,12},{16,18},{18,... | collective-permute-start | bytes 1572872 | tf_op jit(solution)/shard_map/ppermute | solution.py:24
  74.7 2.5 %collective-permute-start.9 = (bf16[1,16,128,128]{3,2,1,0:T(8,128)(2,1)S(1)}, bf16[1,16,128,128]{3,2,1,0:T(8,128)(2,1)S(1)}, u32[]{:S(2)}, u32[]{:S(2)}) collective-permute-start(bf16[1,16,128,128]{3,2,1,0:T(8,128)(2,1)S(1)} %broadcast_select_fusion.2.refs_4_), channel_id=1, source_target_pairs={{0,2},{2,0},{4,6},{6,4},{8,10},{10,8},{12,14},{14,12},{16,18},{18,... | collective-permute-start | bytes 1572872 | tf_op jit(solution)/shard_map/ppermute | solution.py:24
  74.8 3.2 %collective-permute-start.19 = (bf16[1,16,128,128]{3,2,1,0:T(8,128)(2,1)S(1)}, bf16[1,16,128,128]{3,2,1,0:T(8,128)(2,1)S(1)}, u32[]{:S(2)}, u32[]{:S(2)}) collective-permute-start(bf16[1,16,128,128]{3,2,1,0:T(8,128)(2,1)S(1)} %broadcast_select_fusion.refs_10_), channel_id=1, source_target_pairs={{0,2},{2,0},{4,6},{6,4},{8,10},{10,8},{12,14},{14,12},{16,18},{18,... | collective-permute-start | bytes 1572872 | tf_op jit(solution)/shard_map/ppermute | solution.py:24
  91.3 1.8 collective-permute-start.20
  91.6 3.2 %collective-permute-start.21 = (bf16[1,8,128,128]{3,2,1,0:T(8,128)(2,1)}, bf16[1,8,128,128]{3,2,1,0:T(8,128)(2,1)S(1)}, u32[]{:S(2)}, u32[]{:S(2)}) collective-permute-start(bf16[1,8,128,128]{3,2,1,0:T(8,128)(2,1)} %get-tuple-element.49), channel_id=1, source_target_pairs={{0,2},{2,0},{4,6},{6,4},{8,10},{10,8},{12,14},{14,12},{16,18},{18,... | collective-permute-start | bytes 786440 | tf_op jit(solution)/shard_map/ppermute | solution.py:24
  91.9 4.0 %collective-permute-start.22 = (bf16[1,8,128,128]{3,2,1,0:T(8,128)(2,1)}, bf16[1,8,128,128]{3,2,1,0:T(8,128)(2,1)S(1)}, u32[]{:S(2)}, u32[]{:S(2)}) collective-permute-start(bf16[1,8,128,128]{3,2,1,0:T(8,128)(2,1)} %get-tuple-element.51), channel_id=1, source_target_pairs={{0,2},{2,0},{4,6},{6,4},{8,10},{10,8},{12,14},{14,12},{16,18},{18,... | collective-permute-start | bytes 786440 | tf_op jit(solution)/shard_map/ppermute | solution.py:24
  92.1 5.5 %collective-permute-start.23 = (bf16[1,8,128,128]{3,2,1,0:T(8,128)(2,1)}, bf16[1,8,128,128]{3,2,1,0:T(8,128)(2,1)S(1)}, u32[]{:S(2)}, u32[]{:S(2)}) collective-permute-start(bf16[1,8,128,128]{3,2,1,0:T(8,128)(2,1)} %get-tuple-element.53), channel_id=1, source_target_pairs={{0,2},{2,0},{4,6},{6,4},{8,10},{10,8},{12,14},{14,12},{16,18},{18,... | collective-permute-start | bytes 786440 | tf_op jit(solution)/shard_map/ppermute | solution.py:24
  111.1 4.8 %collective-permute-start.24 = (bf16[1,8,128,128]{3,2,1,0:T(8,128)(2,1)}, bf16[1,8,128,128]{3,2,1,0:T(8,128)(2,1)S(1)}, u32[]{:S(2)}, u32[]{:S(2)}) collective-permute-start(bf16[1,8,128,128]{3,2,1,0:T(8,128)(2,1)} %get-tuple-element.56), channel_id=1, source_target_pairs={{0,2},{2,0},{4,6},{6,4},{8,10},{10,8},{12,14},{14,12},{16,18},{18,... | collective-permute-start | bytes 786440 | tf_op jit(solution)/shard_map/ppermute | solution.py:24
  112.0 7.9 %collective-permute-start.28 = (bf16[1,16,128,128]{3,2,1,0:T(8,128)(2,1)}, bf16[1,16,128,128]{3,2,1,0:T(8,128)(2,1)S(1)}, u32[]{:S(2)}, u32[]{:S(2)}) collective-permute-start(bf16[1,16,128,128]{3,2,1,0:T(8,128)(2,1)} %collective-permute-done.refs_2_), channel_id=1, source_target_pairs={{0,2},{2,0},{4,6},{6,4},{8,10},{10,8},{12,14},{14,12},{16,18},{18,... | collective-permute-start | bytes 1572872 | tf_op jit(solution)/shard_map/ppermute | solution.py:24
  112.3 9.7 %collective-permute-start.29 = (bf16[1,16,128,128]{3,2,1,0:T(8,128)(2,1)}, bf16[1,16,128,128]{3,2,1,0:T(8,128)(2,1)S(1)}, u32[]{:S(2)}, u32[]{:S(2)}) collective-permute-start(bf16[1,16,128,128]{3,2,1,0:T(8,128)(2,1)} %collective-permute-done.10.refs_5_), channel_id=1, source_target_pairs={{0,2},{2,0},{4,6},{6,4},{8,10},{10,8},{12,14},{14,12},{16,18},{18,... | collective-permute-start | bytes 1572872 | tf_op jit(solution)/shard_map/ppermute | solution.py:24
  112.5 26.6 %collective-permute-start.30 = (bf16[1,8,128,128]{3,2,1,0:T(8,128)(2,1)}, bf16[1,8,128,128]{3,2,1,0:T(8,128)(2,1)S(1)}, u32[]{:S(2)}, u32[]{:S(2)}) collective-permute-start(bf16[1,8,128,128]{3,2,1,0:T(8,128)(2,1)} %get-tuple-element.68), channel_id=1, source_target_pairs={{0,2},{2,0},{4,6},{6,4},{8,10},{10,8},{12,14},{14,12},{16,18},{18,... | collective-permute-start | bytes 786440 | tf_op jit(solution)/shard_map/ppermute | solution.py:24
  112.8 4.3 %collective-permute-start.25 = (bf16[1,8,128,128]{3,2,1,0:T(8,128)(2,1)}, bf16[1,8,128,128]{3,2,1,0:T(8,128)(2,1)S(1)}, u32[]{:S(2)}, u32[]{:S(2)}) collective-permute-start(bf16[1,8,128,128]{3,2,1,0:T(8,128)(2,1)} %get-tuple-element.58), channel_id=1, source_target_pairs={{0,2},{2,0},{4,6},{6,4},{8,10},{10,8},{12,14},{14,12},{16,18},{18,... | collective-permute-start | bytes 786440 | tf_op jit(solution)/shard_map/ppermute | solution.py:24
  115.9 2.2 %collective-permute-start.26 = (bf16[1,8,128,128]{3,2,1,0:T(8,128)(2,1)S(1)}, bf16[1,8,128,128]{3,2,1,0:T(8,128)(2,1)S(1)}, u32[]{:S(2)}, u32[]{:S(2)}) collective-permute-start(bf16[1,8,128,128]{3,2,1,0:T(8,128)(2,1)S(1)} %copy-done.46), channel_id=1, source_target_pairs={{0,2},{2,0},{4,6},{6,4},{8,10},{10,8},{12,14},{14,12},{16,18},{18,... | collective-permute-start | bytes 786440 | tf_op jit(solution)/shard_map/ppermute | solution.py:24
  117.1 2.1 %collective-permute-start.27 = (bf16[1,8,128,128]{3,2,1,0:T(8,128)(2,1)S(1)}, bf16[1,8,128,128]{3,2,1,0:T(8,128)(2,1)S(1)}, u32[]{:S(2)}, u32[]{:S(2)}) collective-permute-start(bf16[1,8,128,128]{3,2,1,0:T(8,128)(2,1)S(1)} %copy-done.45), channel_id=1, source_target_pairs={{0,2},{2,0},{4,6},{6,4},{8,10},{10,8},{12,14},{14,12},{16,18},{18,... | collective-permute-start | bytes 786440 | tf_op jit(solution)/shard_map/ppermute | solution.py:24
  118.1 23.3 %collective-permute-start.42 = (bf16[1,8,128,128]{3,2,1,0:T(8,128)(2,1)}, bf16[1,8,128,128]{3,2,1,0:T(8,128)(2,1)S(1)}, u32[]{:S(2)}, u32[]{:S(2)}) collective-permute-start(bf16[1,8,128,128]{3,2,1,0:T(8,128)(2,1)} %get-tuple-element.79), channel_id=1, source_target_pairs={{0,2},{2,0},{4,6},{6,4},{8,10},{10,8},{12,14},{14,12},{16,18},{18,... | collective-permute-start | bytes 786440 | tf_op jit(solution)/shard_map/ppermute | solution.py:24
  119.2 37.0 %collective-permute-start.31 = (bf16[1,8,128,128]{3,2,1,0:T(8,128)(2,1)}, bf16[1,8,128,128]{3,2,1,0:T(8,128)(2,1)S(1)}, u32[]{:S(2)}, u32[]{:S(2)}) collective-permute-start(bf16[1,8,128,128]{3,2,1,0:T(8,128)(2,1)} %add_convert_fusion.7), channel_id=1, source_target_pairs={{0,4},{2,6},{4,0},{6,2},{8,12},{10,14},{12,8},{14,10},{16,20},{18,... | collective-permute-start | bytes 786440 | tf_op jit(solution)/shard_map/ppermute | solution.py:24
  119.9 19.3 %collective-permute-start.33 = (bf16[1,8,128,128]{3,2,1,0:T(8,128)(2,1)S(1)}, bf16[1,8,128,128]{3,2,1,0:T(8,128)(2,1)S(1)}, u32[]{:S(2)}, u32[]{:S(2)}) collective-permute-start(bf16[1,8,128,128]{3,2,1,0:T(8,128)(2,1)S(1)} %add_convert_fusion.6), channel_id=1, source_target_pairs={{0,4},{2,6},{4,0},{6,2},{8,12},{10,14},{12,8},{14,10},{16,20},{18,... | collective-permute-start | bytes 786440 | tf_op jit(solution)/shard_map/ppermute | solution.py:24
  122.8 18.9 %collective-permute-start.45 = (bf16[1,8,128,128]{3,2,1,0:T(8,128)(2,1)}, bf16[1,8,128,128]{3,2,1,0:T(8,128)(2,1)S(1)}, u32[]{:S(2)}, u32[]{:S(2)}) collective-permute-start(bf16[1,8,128,128]{3,2,1,0:T(8,128)(2,1)} %add_convert_fusion.4), channel_id=1, source_target_pairs={{0,4},{2,6},{4,0},{6,2},{8,12},{10,14},{12,8},{14,10},{16,20},{18,... | collective-permute-start | bytes 786440 | tf_op jit(solution)/shard_map/ppermute | solution.py:24
  139.2 4.2 %collective-permute-start.36 = (bf16[1,8,128,128]{3,2,1,0:T(8,128)(2,1)S(1)}, bf16[1,8,128,128]{3,2,1,0:T(8,128)(2,1)S(1)}, u32[]{:S(2)}, u32[]{:S(2)}) collective-permute-start(bf16[1,8,128,128]{3,2,1,0:T(8,128)(2,1)S(1)} %copy-done.44), channel_id=1, source_target_pairs={{0,2},{2,0},{4,6},{6,4},{8,10},{10,8},{12,14},{14,12},{16,18},{18,... | collective-permute-start | bytes 786440 | tf_op jit(solution)/shard_map/ppermute | solution.py:24
  139.3 16.9 %collective-permute-start.43 = (bf16[1,8,128,128]{3,2,1,0:T(8,128)(2,1)S(1)}, bf16[1,8,128,128]{3,2,1,0:T(8,128)(2,1)S(1)}, u32[]{:S(2)}, u32[]{:S(2)}) collective-permute-start(bf16[1,8,128,128]{3,2,1,0:T(8,128)(2,1)S(1)} %copy-done.32), channel_id=1, source_target_pairs={{0,4},{2,6},{4,0},{6,2},{8,12},{10,14},{12,8},{14,10},{16,20},{18,... | collective-permute-start | bytes 786440 | tf_op jit(solution)/shard_map/ppermute | solution.py:24
  140.6 20.0 %copy-start.26 = (bf16[1,16,128,128]{3,2,1,0:T(8,128)(2,1)S(1)}, bf16[1,16,128,128]{3,2,1,0:T(8,128)(2,1)}, u32[]{:S(2)}) copy-start(bf16[1,16,128,128]{3,2,1,0:T(8,128)(2,1)} %get-tuple-element.82) | copy-start | bytes 1572868
  141.4 16.1 %collective-permute-start.48 = (bf16[1,8,128,128]{3,2,1,0:T(8,128)(2,1)S(1)}, bf16[1,8,128,128]{3,2,1,0:T(8,128)(2,1)S(1)}, u32[]{:S(2)}, u32[]{:S(2)}) collective-permute-start(bf16[1,8,128,128]{3,2,1,0:T(8,128)(2,1)S(1)} %copy-done.43), channel_id=1, source_target_pairs={{0,2},{2,0},{4,6},{6,4},{8,10},{10,8},{12,14},{14,12},{16,18},{18,... | collective-permute-start | bytes 786440 | tf_op jit(solution)/shard_map/ppermute | solution.py:24
  141.7 18.8 %copy-start.16 = (bf16[1,8,128,128]{3,2,1,0:T(8,128)(2,1)}, bf16[1,8,128,128]{3,2,1,0:T(8,128)(2,1)S(1)}, u32[]{:S(2)}) copy-start(bf16[1,8,128,128]{3,2,1,0:T(8,128)(2,1)S(1)} %collective-permute-done.45) | copy-start | bytes 786436
  141.7 12.4 %collective-permute-start.39 = (bf16[1,8,128,128]{3,2,1,0:T(8,128)(2,1)S(1)}, bf16[1,8,128,128]{3,2,1,0:T(8,128)(2,1)S(1)}, u32[]{:S(2)}, u32[]{:S(2)}) collective-permute-start(bf16[1,8,128,128]{3,2,1,0:T(8,128)(2,1)S(1)} %copy-done.35), channel_id=1, source_target_pairs={{0,4},{2,6},{4,0},{6,2},{8,12},{10,14},{12,8},{14,10},{16,20},{18,... | collective-permute-start | bytes 786440 | tf_op jit(solution)/shard_map/ppermute | solution.py:24
  143.4 15.9 %collective-permute-start.51 = (bf16[1,8,128,128]{3,2,1,0:T(8,128)(2,1)S(1)}, bf16[1,8,128,128]{3,2,1,0:T(8,128)(2,1)S(1)}, u32[]{:S(2)}, u32[]{:S(2)}) collective-permute-start(bf16[1,8,128,128]{3,2,1,0:T(8,128)(2,1)S(1)} %copy-done.34), channel_id=1, source_target_pairs={{0,4},{2,6},{4,0},{6,2},{8,12},{10,14},{12,8},{14,10},{16,20},{18,... | collective-permute-start | bytes 786440 | tf_op jit(solution)/shard_map/ppermute | solution.py:24
  154.1 11.6 %collective-permute-start.34 = (bf16[1,8,128,128]{3,2,1,0:T(8,128)(2,1)}, bf16[1,8,128,128]{3,2,1,0:T(8,128)(2,1)}, u32[]{:S(2)}, u32[]{:S(2)}) collective-permute-start(bf16[1,8,128,128]{3,2,1,0:T(8,128)(2,1)} %fusion.6), channel_id=1, source_target_pairs={{8,0},{10,2},{12,4},{14,6},{16,8},{18,10},{20,12},{22,14},{24,16},... | collective-permute-start | bytes 786440 | tf_op jit(solution)/shard_map/ppermute | solution.py:20
  156.2 10.9 %collective-permute-start.32 = (bf16[1,8,128,128]{3,2,1,0:T(8,128)(2,1)}, bf16[1,8,128,128]{3,2,1,0:T(8,128)(2,1)}, u32[]{:S(2)}, u32[]{:S(2)}) collective-permute-start(bf16[1,8,128,128]{3,2,1,0:T(8,128)(2,1)} %get-tuple-element.105), channel_id=1, source_target_pairs={{0,2},{2,0},{4,6},{6,4},{8,10},{10,8},{12,14},{14,12},{16,18},{18,... | collective-permute-start | bytes 786440 | tf_op jit(solution)/shard_map/ppermute | solution.py:24
  156.2 11.0 %collective-permute-start.37 = (bf16[1,8,128,128]{3,2,1,0:T(8,128)(2,1)}, bf16[1,8,128,128]{3,2,1,0:T(8,128)(2,1)}, u32[]{:S(2)}, u32[]{:S(2)}) collective-permute-start(bf16[1,8,128,128]{3,2,1,0:T(8,128)(2,1)} %add_convert_fusion.3), channel_id=1, source_target_pairs={{0,4},{2,6},{4,0},{6,2},{8,12},{10,14},{12,8},{14,10},{16,20},{18,... | collective-permute-start | bytes 786440 | tf_op jit(solution)/shard_map/ppermute | solution.py:24
  157.5 11.0 %collective-permute-start.38 = (bf16[1,8,128,128]{3,2,1,0:T(8,128)(2,1)}, bf16[1,8,128,128]{3,2,1,0:T(8,128)(2,1)}, u32[]{:S(2)}, u32[]{:S(2)}) collective-permute-start(bf16[1,8,128,128]{3,2,1,0:T(8,128)(2,1)} %get-tuple-element.106), channel_id=1, source_target_pairs={{0,2},{2,0},{4,6},{6,4},{8,10},{10,8},{12,14},{14,12},{16,18},{18,... | collective-permute-start | bytes 786440 | tf_op jit(solution)/shard_map/ppermute | solution.py:24
  159.2 10.1 %collective-permute-start.40 = (bf16[1,8,128,128]{3,2,1,0:T(8,128)(2,1)}, bf16[1,8,128,128]{3,2,1,0:T(8,128)(2,1)}, u32[]{:S(2)}, u32[]{:S(2)}) collective-permute-start(bf16[1,8,128,128]{3,2,1,0:T(8,128)(2,1)} %fusion.16), channel_id=1, source_target_pairs={{8,0},{10,2},{12,4},{14,6},{16,8},{18,10},{20,12},{22,14},{24,16},... | collective-permute-start | bytes 786440 | tf_op jit(solution)/shard_map/ppermute | solution.py:20
  165.5 17.9 %copy-start.15 = (bf16[1,8,128,128]{3,2,1,0:T(8,128)(2,1)S(1)}, bf16[1,8,128,128]{3,2,1,0:T(8,128)(2,1)}, u32[]{:S(2)}) copy-start(bf16[1,8,128,128]{3,2,1,0:T(8,128)(2,1)} %copy-done.14) | copy-start | bytes 786436
  165.5 17.9 %copy-start.17 = (bf16[1,8,128,128]{3,2,1,0:T(8,128)(2,1)S(1)}, bf16[1,8,128,128]{3,2,1,0:T(8,128)(2,1)}, u32[]{:S(2)}) copy-start(bf16[1,8,128,128]{3,2,1,0:T(8,128)(2,1)} %copy-done.16) | copy-start | bytes 786436
  165.7 12.1 %collective-permute-start.46 = (bf16[1,8,128,128]{3,2,1,0:T(8,128)(2,1)}, bf16[1,8,128,128]{3,2,1,0:T(8,128)(2,1)S(1)}, u32[]{:S(2)}, u32[]{:S(2)}) collective-permute-start(bf16[1,8,128,128]{3,2,1,0:T(8,128)(2,1)} %fusion.26), channel_id=1, source_target_pairs={{8,0},{10,2},{12,4},{14,6},{16,8},{18,10},{20,12},{22,14},{24,16},... | collective-permute-start | bytes 786440 | tf_op jit(solution)/shard_map/ppermute | solution.py:20
  167.1 11.9 %collective-permute-start.44 = (bf16[1,8,128,128]{3,2,1,0:T(8,128)(2,1)}, bf16[1,8,128,128]{3,2,1,0:T(8,128)(2,1)S(1)}, u32[]{:S(2)}, u32[]{:S(2)}) collective-permute-start(bf16[1,8,128,128]{3,2,1,0:T(8,128)(2,1)} %get-tuple-element.99), channel_id=1, source_target_pairs={{0,2},{2,0},{4,6},{6,4},{8,10},{10,8},{12,14},{14,12},{16,18},{18,... | collective-permute-start | bytes 786440 | tf_op jit(solution)/shard_map/ppermute | solution.py:24
  167.2 13.1 %collective-permute-start.49 = (bf16[1,8,128,128]{3,2,1,0:T(8,128)(2,1)}, bf16[1,8,128,128]{3,2,1,0:T(8,128)(2,1)S(1)}, u32[]{:S(2)}, u32[]{:S(2)}) collective-permute-start(bf16[1,8,128,128]{3,2,1,0:T(8,128)(2,1)} %add_convert_fusion.1), channel_id=1, source_target_pairs={{0,4},{2,6},{4,0},{6,2},{8,12},{10,14},{12,8},{14,10},{16,20},{18,... | collective-permute-start | bytes 786440 | tf_op jit(solution)/shard_map/ppermute | solution.py:24
  168.5 11.8 %collective-permute-start.50 = (bf16[1,8,128,128]{3,2,1,0:T(8,128)(2,1)}, bf16[1,8,128,128]{3,2,1,0:T(8,128)(2,1)S(1)}, u32[]{:S(2)}, u32[]{:S(2)}) collective-permute-start(bf16[1,8,128,128]{3,2,1,0:T(8,128)(2,1)} %get-tuple-element.100), channel_id=1, source_target_pairs={{0,2},{2,0},{4,6},{6,4},{8,10},{10,8},{12,14},{14,12},{16,18},{18,... | collective-permute-start | bytes 786440 | tf_op jit(solution)/shard_map/ppermute | solution.py:24
  169.4 14.0 %collective-permute-start.52 = (bf16[1,8,128,128]{3,2,1,0:T(8,128)(2,1)S(1)}, bf16[1,8,128,128]{3,2,1,0:T(8,128)(2,1)S(1)}, u32[]{:S(2)}, u32[]{:S(2)}) collective-permute-start(bf16[1,8,128,128]{3,2,1,0:T(8,128)(2,1)S(1)} %fusion.36), channel_id=1, source_target_pairs={{8,0},{10,2},{12,4},{14,6},{16,8},{18,10},{20,12},{22,14},{24,16},... | collective-permute-start | bytes 786440 | tf_op jit(solution)/shard_map/ppermute | solution.py:20
  172.5 22.1 %copy-start.25 = (bf16[1,16,128,128]{3,2,1,0:T(8,128)(2,1)S(1)}, bf16[1,16,128,128]{3,2,1,0:T(8,128)(2,1)}, u32[]{:S(2)}) copy-start(bf16[1,16,128,128]{3,2,1,0:T(8,128)(2,1)} %get-tuple-element.67) | copy-start | bytes 1572868
  177.8 11.2 %collective-permute-start.35 = (bf16[1,8,128,128]{3,2,1,0:T(8,128)(2,1)S(1)}, bf16[1,8,128,128]{3,2,1,0:T(8,128)(2,1)S(1)}, u32[]{:S(2)}, u32[]{:S(2)}) collective-permute-start(bf16[1,8,128,128]{3,2,1,0:T(8,128)(2,1)S(1)} %get-tuple-element.103), channel_id=1, source_target_pairs={{8,0},{10,2},{12,4},{14,6},{16,8},{18,10},{20,12},{22,14},{24,16},... | collective-permute-start | bytes 786440 | tf_op jit(solution)/shard_map/ppermute | solution.py:20
  179.1 15.6 %collective-permute-start.41 = (bf16[1,8,128,128]{3,2,1,0:T(8,128)(2,1)S(1)}, bf16[1,8,128,128]{3,2,1,0:T(8,128)(2,1)S(1)}, u32[]{:S(2)}, u32[]{:S(2)}) collective-permute-start(bf16[1,8,128,128]{3,2,1,0:T(8,128)(2,1)S(1)} %get-tuple-element.104), channel_id=1, source_target_pairs={{8,0},{10,2},{12,4},{14,6},{16,8},{18,10},{20,12},{22,14},{24,16},... | collective-permute-start | bytes 786440 | tf_op jit(solution)/shard_map/ppermute | solution.py:20
  183.8 16.4 %collective-permute-start.47 = (bf16[1,8,128,128]{3,2,1,0:T(8,128)(2,1)S(1)}, bf16[1,8,128,128]{3,2,1,0:T(8,128)(2,1)S(1)}, u32[]{:S(2)}, u32[]{:S(2)}) collective-permute-start(bf16[1,8,128,128]{3,2,1,0:T(8,128)(2,1)S(1)} %get-tuple-element.97), channel_id=1, source_target_pairs={{8,0},{10,2},{12,4},{14,6},{16,8},{18,10},{20,12},{22,14},{24,16},... | collective-permute-start | bytes 786440 | tf_op jit(solution)/shard_map/ppermute | solution.py:20
  185.1 19.4 %collective-permute-start.53 = (bf16[1,8,128,128]{3,2,1,0:T(8,128)(2,1)S(1)}, bf16[1,8,128,128]{3,2,1,0:T(8,128)(2,1)S(1)}, u32[]{:S(2)}, u32[]{:S(2)}) collective-permute-start(bf16[1,8,128,128]{3,2,1,0:T(8,128)(2,1)S(1)} %get-tuple-element.98), channel_id=1, source_target_pairs={{8,0},{10,2},{12,4},{14,6},{16,8},{18,10},{20,12},{22,14},{24,16},... | collective-permute-start | bytes 786440 | tf_op jit(solution)/shard_map/ppermute | solution.py:20
  (37 other events, 209.1 us)

commit v10 on v7

--- a/solution.py
+++ b/solution.py
@@ -10,7 +10,7 @@
 WINDOW = 1024
 HOPS = 8
 PLANE = 4
-HEADS_PER_STEP = 2
+HEADS_PER_STEP = 4
 
 SCALE = 168.0 ** (-0.5)
 

time: 188 us -> 187 us (level)
  no operation moved by 1% of the time
where the time goes in v10:
time: 187 us; the launch traced here: 186 us
  starting transfers between devices  60.4 us (32%)
  waiting for transfers between devices  53 us (28%)
  Pallas kernels  35 us (19%)
  other arithmetic  22.5 us (12%)
  local copies, waits for them, and re-layouts  14.1 us (8%)
    pallas_call x2, Pallas kernels, attend_blocks(): pl.pallas_call(functools.partial(_blocks_kernel, tuple(modes), acc is not...  35 us
    ppermute x12, starting transfers between devices, one_way(): return lax.ppermute(x, 'seq', pairs)  29 us
    ppermute x8, starting transfers between devices, shift(): return lax.ppermute(x, 'seq', pairs)  23.6 us
    ppermute x18, waiting for transfers between devices, swap(): return lax.ppermute(x, 'seq', [(i, i ^ bit) for i in range(n)])  21.9 us
    ppermute x8, waiting for transfers between devices, shift(): return lax.ppermute(x, 'seq', pairs)  19.2 us
    ppermute x12, waiting for transfers between devices, one_way(): return lax.ppermute(x, 'seq', pairs)  11.9 us
    ppermute x18, starting transfers between devices, swap(): return lax.ppermute(x, 'seq', [(i, i ^ bit) for i in range(n)])  7.83 us
    unnamed x56, local copies, waits for them, and re-layouts  6.47 us
  transfers between devices with their start and end apart: 38, of which 14 were waited for; matrix products, arithmetic and copies ran while one was open for 17% of the time, Pallas kernels for 7%

profile of v10, /device:TPU:0, one launch (start us, length us, event | category | flops | bytes accessed | tf_op | source)
XLA Modules:
  0.0 186.2 jit_solution(1742897885943468875)
XLA Ops:
  0.7 1.3 copy.27
  2.0 5.7 %collective-permute-start = (bf16[1,16,128,128]{3,2,1,0:T(8,128)(2,1)S(1)}, bf16[1,16,128,128]{3,2,1,0:T(8,128)(2,1)}, u32[]{:S(2)}, u32[]{:S(2)}) collective-permute-start(bf16[1,16,128,128]{3,2,1,0:T(8,128)(2,1)S(1)} %bitcast.44), channel_id=1, source_target_pairs={{0,8},{2,10},{4,12},{6,14},{8,16},{10,18},{12,20},{14,22},{16,24},... | collective-permute-start | bytes 1572872 | tf_op jit(solution)/shard_map/ppermute | solution.py:20
  7.7 1.2 copy.26
  8.9 3.5 %collective-permute-start.10 = (bf16[1,16,128,128]{3,2,1,0:T(8,128)(2,1)S(1)}, bf16[1,16,128,128]{3,2,1,0:T(8,128)(2,1)}, u32[]{:S(2)}, u32[]{:S(2)}) collective-permute-start(bf16[1,16,128,128]{3,2,1,0:T(8,128)(2,1)S(1)} %bitcast.48), channel_id=1, source_target_pairs={{0,8},{2,10},{4,12},{6,14},{8,16},{10,18},{12,20},{14,22},{16,24},... | collective-permute-start | bytes 1572872 | tf_op jit(solution)/shard_map/ppermute | solution.py:20
  12.4 3.4 %collective-permute-start.4 = (bf16[1,16,128,128]{3,2,1,0:T(8,128)(2,1)S(1)}, bf16[1,16,128,128]{3,2,1,0:T(8,128)(2,1)S(1)}, u32[]{:S(2)}, u32[]{:S(2)}) collective-permute-start(bf16[1,16,128,128]{3,2,1,0:T(8,128)(2,1)S(1)} %bitcast.45), channel_id=1, source_target_pairs={{0,4},{2,6},{8,12},{10,14},{16,20},{18,22},{24,28},{26,30},{1,5},{... | collective-permute-start | bytes 1572872 | tf_op jit(solution)/shard_map/ppermute | solution.py:29
  15.9 3.4 %collective-permute-done.refs_2_ = bf16[1,16,128,128]{3,2,1,0:T(8,128)(2,1)} collective-permute-done((bf16[1,16,128,128]{3,2,1,0:T(8,128)(2,1)S(1)}, bf16[1,16,128,128]{3,2,1,0:T(8,128)(2,1)}, u32[]{:S(2)}, u32[]{:S(2)}) %collective-permute-start) | collective-permute-done | bytes 524320 | tf_op jit(solution)/shard_map/ppermute | solution.py:20
  19.2 5.3 %collective-permute-start.1 = (bf16[1,16,128,128]{3,2,1,0:T(8,128)(2,1)}, bf16[1,16,128,128]{3,2,1,0:T(8,128)(2,1)}, u32[]{:S(2)}, u32[]{:S(2)}) collective-permute-start(bf16[1,16,128,128]{3,2,1,0:T(8,128)(2,1)} %collective-permute-done.refs_2_), channel_id=1, source_target_pairs={{0,8},{2,10},{4,12},{6,14},{8,16},{10,18},{12,20},{14,22},{16,24},... | collective-permute-start | bytes 1572872 | tf_op jit(solution)/shard_map/ppermute | solution.py:20
  24.5 1.3 collective-permute-start.5
  25.8 6.2 %collective-permute-start.14 = (bf16[1,16,128,128]{3,2,1,0:T(8,128)(2,1)S(1)}, bf16[1,16,128,128]{3,2,1,0:T(8,128)(2,1)}, u32[]{:S(2)}, u32[]{:S(2)}) collective-permute-start(bf16[1,16,128,128]{3,2,1,0:T(8,128)(2,1)S(1)} %bitcast.49), channel_id=1, source_target_pairs={{0,4},{2,6},{8,12},{10,14},{16,20},{18,22},{24,28},{26,30},{1,5},{... | collective-permute-start | bytes 1572872 | tf_op jit(solution)/shard_map/ppermute | solution.py:29
  32.0 3.8 %collective-permute-start.11 = (bf16[1,16,128,128]{3,2,1,0:T(8,128)(2,1)}, bf16[1,16,128,128]{3,2,1,0:T(8,128)(2,1)}, u32[]{:S(2)}, u32[]{:S(2)}) collective-permute-start(bf16[1,16,128,128]{3,2,1,0:T(8,128)(2,1)} %collective-permute-done.10.refs_5_), channel_id=1, source_target_pairs={{0,8},{2,10},{4,12},{6,14},{8,16},{10,18},{12,20},{14,22},{16,24},... | collective-permute-start | bytes 1572872 | tf_op jit(solution)/shard_map/ppermute | solution.py:20
  35.8 0.8 copy-done.13
  36.6 1.3 collective-permute-start.15
  38.6 1.4 copy.16
  40.0 1.4 copy.17
  41.4 0.6 multiply_reduce_fusion
  42.0 0.7 copy.18
  42.7 5.3 %collective-permute-start.7 = (bf16[1,16,128,128]{3,2,1,0:T(8,128)(2,1)}, bf16[1,16,128,128]{3,2,1,0:T(8,128)(2,1)S(1)}, u32[]{:S(2)}, u32[]{:S(2)}) collective-permute-start(bf16[1,16,128,128]{3,2,1,0:T(8,128)(2,1)} %collective-permute-done.refs_2_), channel_id=1, source_target_pairs={{0,4},{2,6},{8,12},{10,14},{16,20},{18,22},{24,28},{26,30},{1,5},{... | collective-permute-start | bytes 1572872 | tf_op jit(solution)/shard_map/ppermute | solution.py:29
  48.1 1.3 collective-permute-start.8
  49.4 1.1 broadcast_select_fusion.3.refs_2_
  50.5 1.3 collective-permute-start.2
  51.9 3.5 %collective-permute-start.17 = (bf16[1,16,128,128]{3,2,1,0:T(8,128)(2,1)}, bf16[1,16,128,128]{3,2,1,0:T(8,128)(2,1)S(1)}, u32[]{:S(2)}, u32[]{:S(2)}) collective-permute-start(bf16[1,16,128,128]{3,2,1,0:T(8,128)(2,1)} %collective-permute-done.10.refs_5_), channel_id=1, source_target_pairs={{0,4},{2,6},{8,12},{10,14},{16,20},{18,22},{24,28},{26,30},{1,5},{... | collective-permute-start | bytes 1572872 | tf_op jit(solution)/shard_map/ppermute | solution.py:29
  55.5 1.3 collective-permute-start.18
  56.8 1.1 broadcast_select_fusion.1.refs_8_
  57.9 1.2 collective-permute-done.7
  59.1 1.3 collective-permute-start.12
  60.4 3.3 %collective-permute-done.8 = bf16[1,16,128,128]{3,2,1,0:T(8,128)(2,1)S(1)} collective-permute-done((bf16[1,16,128,128]{3,2,1,0:T(8,128)(2,1)}, bf16[1,16,128,128]{3,2,1,0:T(8,128)(2,1)S(1)}, u32[]{:S(2)}, u32[]{:S(2)}) %collective-permute-start.8) | collective-permute-done | bytes 524320 | tf_op jit(solution)/shard_map/ppermute | solution.py:29
  63.7 1.3 collective-permute-start.3
  65.1 3.1 %collective-permute-done.17 = bf16[1,16,128,128]{3,2,1,0:T(8,128)(2,1)S(1)} collective-permute-done((bf16[1,16,128,128]{3,2,1,0:T(8,128)(2,1)}, bf16[1,16,128,128]{3,2,1,0:T(8,128)(2,1)S(1)}, u32[]{:S(2)}, u32[]{:S(2)}) %collective-permute-start.17) | collective-permute-done | bytes 524320 | tf_op jit(solution)/shard_map/ppermute | solution.py:29
  68.2 4.3 %collective-permute-done.18 = bf16[1,16,128,128]{3,2,1,0:T(8,128)(2,1)S(1)} collective-permute-done((bf16[1,16,128,128]{3,2,1,0:T(8,128)(2,1)}, bf16[1,16,128,128]{3,2,1,0:T(8,128)(2,1)S(1)}, u32[]{:S(2)}, u32[]{:S(2)}) %collective-permute-start.18) | collective-permute-done | bytes 524320 | tf_op jit(solution)/shard_map/ppermute | solution.py:29
  72.5 1.5 collective-permute-start.13
  74.1 1.2 collective-permute-start.16
  75.8 0.8 broadcast_select_fusion.5.refs_1_
  76.7 0.9 broadcast_select_fusion.4.refs_7_
  77.8 0.7 collective-permute-done.19.refs_11_
  78.5 0.8 copy-done.25
  79.4 22.1 %shard_map.85 = (f32[16,128,256]{2,1,0:T(8,128)}, bf16[1,16,128,128]{3,2,1,0:T(8,128)(2,1)}, bf16[1,16,128,128]{3,2,1,0:T(8,128)(2,1)}, bf16[1,16,128,128]{3,2,1...) custom-call(s32[6]{0:T(128)} %stack.58.valid_ref, ...), custom_call_target="tpu_custom_call" | custom-call | flops 4026531840 | bytes 14680064 | tf_op jit(solution)/shard_map/pallas_call | solution.py:105
  102.7 0.9 collective-permute-done.20
  103.8 2.0 %add_convert_fusion.3 = bf16[1,16,128,128]{3,2,1,0:T(8,128)(2,1)} fusion(bf16[1,16,128,128]{3,2,1,0:T(8,128)(2,1)S(1)} %collective-permute-done.20, bf16[1,16,128,128]{3,2,1,0:T(8,128)(2,1)} %get-tuple-element.28), kind=kLoop, calls=%fused_computation.35 | loop fusion | flops 1048576 | bytes 1572864 | tf_op jit(solution)/shard_map/convert_element_type | solution.py:137
  106.2 1.2 add_convert_fusion.2
  107.4 1.0 add_convert_fusion.1
  108.4 1.0 add_convert_fusion
  109.5 1.9 %collective-permute-start.35 = (bf16[1,16,128,128]{3,2,1,0:T(8,128)(2,1)}, bf16[1,16,128,128]{3,2,1,0:T(8,128)(2,1)S(1)}, u32[]{:S(2)}, u32[]{:S(2)}) collective-permute-start(bf16[1,16,128,128]{3,2,1,0:T(8,128)(2,1)} %add_convert_fusion), channel_id=1, source_target_pairs={{0,4},{2,6},{4,0},{6,2},{8,12},{10,14},{12,8},{14,10},{16,20},{18,... | collective-permute-start | bytes 1572872 | tf_op jit(solution)/shard_map/ppermute | solution.py:24
  111.4 0.7 add_convert_fusion.4.valid_ref
  112.2 12.9 %shard_map.86 = (f32[16,128,256]{2,1,0:T(8,128)}, bf16[1,16,128,128]{3,2,1,0:T(8,128)(2,1)}, bf16[1,16,128,128]{3,2,1,0:T(8,128)(2,1)}, bf16[1,16,128,128]{3,2,1...) custom-call(s32[3]{0:T(128)} %add_convert_fusion.4.valid_ref, ...), custom_call_target="tpu_custom_call" | custom-call | flops 2013265920 | bytes 10485760 | tf_op jit(solution)/shard_map/pallas_call | solution.py:105
  125.4 2.1 %fusion.6 = bf16[1,16,128,128]{3,2,1,0:T(8,128)(2,1)} fusion(bf16[1,16,128,128]{3,2,1,0:T(8,128)(2,1)S(1)} %collective-permute-done.26, bf16[1,16,128,128]{3,2,1,0:T(8,128)(2,1)S(1)} %collective-permute-done.29, bf16[1,16,128,128]{3,2,1,0:T(8,128)(2,1)} %get-tuple-element.45, pred[]{:T(512)S(6)} %eq.26, pred[]{:T(512)S(6)} %eq.11), kind=kLoop, calls=%fused_computation.18 | loop fusion | flops 2097152 | bytes 2097154 | tf_op jit(solution)/shard_map/convert_element_type | solution.py:154
  127.5 1.3 collective-permute-start.30
  128.8 1.9 collective-permute-start.33
  130.7 4.7 %collective-permute-done.35 = bf16[1,16,128,128]{3,2,1,0:T(8,128)(2,1)S(1)} collective-permute-done((bf16[1,16,128,128]{3,2,1,0:T(8,128)(2,1)}, bf16[1,16,128,128]{3,2,1,0:T(8,128)(2,1)S(1)}, u32[]{:S(2)}, u32[]{:S(2)}) %collective-permute-start.35) | collective-permute-done | bytes 524320 | tf_op jit(solution)/shard_map/ppermute | solution.py:24
  135.3 1.1 fusion.16
  136.4 10.2 %collective-permute-done.27 = bf16[1,16,128,128]{3,2,1,0:T(8,128)(2,1)S(1)} collective-permute-done((bf16[1,16,128,128]{3,2,1,0:T(8,128)(2,1)}, bf16[1,16,128,128]{3,2,1,0:T(8,128)(2,1)S(1)}, u32[]{:S(2)}, u32[]{:S(2)}) %collective-permute-start.27) | collective-permute-done | bytes 524320 | tf_op jit(solution)/shard_map/ppermute | solution.py:24
  146.6 1.3 collective-permute-start.36
  147.9 2.6 %fusion.9 = bf16[1,16,128,128]{3,2,1,0:T(8,128)(2,1)} fusion(bf16[1,16,128,128]{3,2,1,0:T(8,128)(2,1)S(1)} %collective-permute-done.27, bf16[1,16,128,128]{3,2,1,0:T(8,128)(2,1)S(1)} %collective-permute-done.29, bf16[1,16,128,128]{3,2,1,0:T(8,128)(2,1)} %collective-permute-done.30, bf16[1,16,128,128]{3,2,1,0:T(8,128)(2,1)} %collective-permute-done.28, ...), kind=kLoop, calls=%fused_computation.21 | loop fusion | flops 2621440 | bytes 3145729 | tf_op jit(solution)/shard_map/convert_element_type | solution.py:156
  150.5 1.4 collective-permute-start.31
  151.9 5.1 %collective-permute-done.33 = bf16[1,16,128,128]{3,2,1,0:T(8,128)(2,1)S(1)} collective-permute-done((bf16[1,16,128,128]{3,2,1,0:T(8,128)(2,1)}, bf16[1,16,128,128]{3,2,1,0:T(8,128)(2,1)S(1)}, u32[]{:S(2)}, u32[]{:S(2)}) %collective-permute-start.33) | collective-permute-done | bytes 524320 | tf_op jit(solution)/shard_map/ppermute | solution.py:24
  157.0 6.6 %collective-permute-done.36 = bf16[1,16,128,128]{3,2,1,0:T(8,128)(2,1)} collective-permute-done((bf16[1,16,128,128]{3,2,1,0:T(8,128)(2,1)}, bf16[1,16,128,128]{3,2,1,0:T(8,128)(2,1)}, u32[]{:S(2)}, u32[]{:S(2)}) %collective-permute-start.36) | collective-permute-done | bytes 524320 | tf_op jit(solution)/shard_map/ppermute | solution.py:20
  163.6 2.4 %fusion.19 = bf16[1,16,128,128]{3,2,1,0:T(8,128)(2,1)} fusion(bf16[1,16,128,128]{3,2,1,0:T(8,128)(2,1)S(1)} %collective-permute-done.33, bf16[1,16,128,128]{3,2,1,0:T(8,128)(2,1)S(1)} %collective-permute-done.35, bf16[1,16,128,128]{3,2,1,0:T(8,128)(2,1)} %collective-permute-done.36, bf16[1,16,128,128]{3,2,1,0:T(8,128)(2,1)} %collective-permute-done.34, ...), kind=kLoop, calls=%fused_computation.31 | loop fusion | flops 2621440 | bytes 3145729 | tf_op jit(solution)/shard_map/convert_element_type | solution.py:156
  166.1 1.3 collective-permute-start.37
  167.9 3.8 %copy.21 = bf16[128,16,2,128]{3,2,1,0:T(2,128)(2,1)} copy(bf16[128,16,2,128]{0,2,3,1:T(2,128)(2,1)S(1)} %bitcast.37) | data formatting | bytes 2097152 | tf_op jit(solution)/shard_map/transpose | solution.py:200
  171.7 3.2 %collective-permute-done.31 = bf16[1,16,128,128]{3,2,1,0:T(8,128)(2,1)} collective-permute-done((bf16[1,16,128,128]{3,2,1,0:T(8,128)(2,1)}, bf16[1,16,128,128]{3,2,1,0:T(8,128)(2,1)}, u32[]{:S(2)}, u32[]{:S(2)}) %collective-permute-start.31) | collective-permute-done | bytes 524320 | tf_op jit(solution)/shard_map/ppermute | solution.py:20
  174.9 1.6 fusion.21
  176.4 1.1 copy.22
  177.6 6.1 %collective-permute-done.37 = bf16[1,16,128,128]{3,2,1,0:T(8,128)(2,1)} collective-permute-done((bf16[1,16,128,128]{3,2,1,0:T(8,128)(2,1)}, bf16[1,16,128,128]{3,2,1,0:T(8,128)(2,1)}, u32[]{:S(2)}, u32[]{:S(2)}) %collective-permute-start.37) | collective-permute-done | bytes 524320 | tf_op jit(solution)/shard_map/ppermute | solution.py:20
  183.6 1.4 fusion.20
  185.0 1.1 copy.23
  (96 shorter events, 4.6 us)
Async XLA Ops:
  0.6 38.0 %copy-start.6 = (bf16[128,32,128]{2,1,0:T(8,128)(2,1)S(1)}, bf16[128,32,128]{2,1,0:T(8,128)(2,1)}, u32[]{:S(2)}) copy-start(bf16[128,32,128]{2,1,0:T(8,128)(2,1)} %param.6) | copy-start | bytes 3145732
  0.6 39.3 %copy-start = (bf16[128,32,128]{2,1,0:T(8,128)(2,1)S(1)}, bf16[128,32,128]{2,1,0:T(8,128)(2,1)}, u32[]{:S(2)}) copy-start(bf16[128,32,128]{2,1,0:T(8,128)(2,1)} %param.10) | copy-start | bytes 3145732
  2.0 48.5 %copy-start.11 = (bf16[128,16,128]{2,0,1:T(8,128)(2,1)}, bf16[128,16,128]{2,0,1:T(8,128)(2,1)S(1)}, u32[]{:S(2)}) copy-start(bf16[128,16,128]{2,0,1:T(8,128)(2,1)S(1)} %copy.27) | copy-start | bytes 1572868
  2.0 17.2 %collective-permute-start = (bf16[1,16,128,128]{3,2,1,0:T(8,128)(2,1)S(1)}, bf16[1,16,128,128]{3,2,1,0:T(8,128)(2,1)}, u32[]{:S(2)}, u32[]{:S(2)}) collective-permute-start(bf16[1,16,128,128]{3,2,1,0:T(8,128)(2,1)S(1)} %bitcast.44), channel_id=1, source_target_pairs={{0,8},{2,10},{4,12},{6,14},{8,16},{10,18},{12,20},{14,22},{16,24},... | collective-permute-start | bytes 1572872 | tf_op jit(solution)/shard_map/ppermute | solution.py:20
  8.9 50.2 %copy-start.12 = (bf16[128,16,128]{2,0,1:T(8,128)(2,1)}, bf16[128,16,128]{2,0,1:T(8,128)(2,1)S(1)}, u32[]{:S(2)}) copy-start(bf16[128,16,128]{2,0,1:T(8,128)(2,1)S(1)} %copy.26) | copy-start | bytes 1572868
  8.9 23.0 %collective-permute-start.10 = (bf16[1,16,128,128]{3,2,1,0:T(8,128)(2,1)S(1)}, bf16[1,16,128,128]{3,2,1,0:T(8,128)(2,1)}, u32[]{:S(2)}, u32[]{:S(2)}) collective-permute-start(bf16[1,16,128,128]{3,2,1,0:T(8,128)(2,1)S(1)} %bitcast.48), channel_id=1, source_target_pairs={{0,8},{2,10},{4,12},{6,14},{8,16},{10,18},{12,20},{14,22},{16,24},... | collective-permute-start | bytes 1572872 | tf_op jit(solution)/shard_map/ppermute | solution.py:20
  12.4 23.3 %collective-permute-start.4 = (bf16[1,16,128,128]{3,2,1,0:T(8,128)(2,1)S(1)}, bf16[1,16,128,128]{3,2,1,0:T(8,128)(2,1)S(1)}, u32[]{:S(2)}, u32[]{:S(2)}) collective-permute-start(bf16[1,16,128,128]{3,2,1,0:T(8,128)(2,1)S(1)} %bitcast.45), channel_id=1, source_target_pairs={{0,4},{2,6},{8,12},{10,14},{16,20},{18,22},{24,28},{26,30},{1,5},{... | collective-permute-start | bytes 1572872 | tf_op jit(solution)/shard_map/ppermute | solution.py:29
  19.2 23.5 %collective-permute-start.1 = (bf16[1,16,128,128]{3,2,1,0:T(8,128)(2,1)}, bf16[1,16,128,128]{3,2,1,0:T(8,128)(2,1)}, u32[]{:S(2)}, u32[]{:S(2)}) collective-permute-start(bf16[1,16,128,128]{3,2,1,0:T(8,128)(2,1)} %collective-permute-done.refs_2_), channel_id=1, source_target_pairs={{0,8},{2,10},{4,12},{6,14},{8,16},{10,18},{12,20},{14,22},{16,24},... | collective-permute-start | bytes 1572872 | tf_op jit(solution)/shard_map/ppermute | solution.py:20
  24.5 23.6 %collective-permute-start.5 = (bf16[1,16,128,128]{3,2,1,0:T(8,128)(2,1)}, bf16[1,16,128,128]{3,2,1,0:T(8,128)(2,1)}, u32[]{:S(2)}, u32[]{:S(2)}) collective-permute-start(bf16[1,16,128,128]{3,2,1,0:T(8,128)(2,1)} %collective-permute-done.refs_2_), channel_id=1, source_target_pairs={{4,0},{6,2},{12,8},{14,10},{20,16},{22,18},{28,24},{30,26},{5,1},{... | collective-permute-start | bytes 1572872 | tf_op jit(solution)/shard_map/ppermute | solution.py:29
  25.8 24.7 %collective-permute-start.14 = (bf16[1,16,128,128]{3,2,1,0:T(8,128)(2,1)S(1)}, bf16[1,16,128,128]{3,2,1,0:T(8,128)(2,1)}, u32[]{:S(2)}, u32[]{:S(2)}) collective-permute-start(bf16[1,16,128,128]{3,2,1,0:T(8,128)(2,1)S(1)} %bitcast.49), channel_id=1, source_target_pairs={{0,4},{2,6},{8,12},{10,14},{16,20},{18,22},{24,28},{26,30},{1,5},{... | collective-permute-start | bytes 1572872 | tf_op jit(solution)/shard_map/ppermute | solution.py:29
  32.0 19.9 %collective-permute-start.11 = (bf16[1,16,128,128]{3,2,1,0:T(8,128)(2,1)}, bf16[1,16,128,128]{3,2,1,0:T(8,128)(2,1)}, u32[]{:S(2)}, u32[]{:S(2)}) collective-permute-start(bf16[1,16,128,128]{3,2,1,0:T(8,128)(2,1)} %collective-permute-done.10.refs_5_), channel_id=1, source_target_pairs={{0,8},{2,10},{4,12},{6,14},{8,16},{10,18},{12,20},{14,22},{16,24},... | collective-permute-start | bytes 1572872 | tf_op jit(solution)/shard_map/ppermute | solution.py:20
  35.8 0.8 copy-start.13
  36.6 18.9 %collective-permute-start.15 = (bf16[1,16,128,128]{3,2,1,0:T(8,128)(2,1)}, bf16[1,16,128,128]{3,2,1,0:T(8,128)(2,1)}, u32[]{:S(2)}, u32[]{:S(2)}) collective-permute-start(bf16[1,16,128,128]{3,2,1,0:T(8,128)(2,1)} %collective-permute-done.10.refs_5_), channel_id=1, source_target_pairs={{4,0},{6,2},{12,8},{14,10},{20,16},{22,18},{28,24},{30,26},{5,1},{... | collective-permute-start | bytes 1572872 | tf_op jit(solution)/shard_map/ppermute | solution.py:29
  38.6 2.8 %copy-start.7 = (bf16[128,32,128]{2,1,0:T(8,128)(2,1)S(1)}, bf16[128,32,128]{2,1,0:T(8,128)(2,1)}, u32[]{:S(2)}) copy-start(bf16[128,32,128]{2,1,0:T(8,128)(2,1)} %param.9) | copy-start | bytes 3145732
  40.0 9.4 %copy-start.14 = (bf16[1,16,128,128]{3,2,1,0:T(8,128)(2,1)S(1)}, bf16[1,16,128,128]{3,2,1,0:T(8,128)(2,1)}, u32[]{:S(2)}) copy-start(bf16[1,16,128,128]{3,2,1,0:T(8,128)(2,1)} %copy-done.13) | copy-start | bytes 1572868
  42.7 16.4 %collective-permute-start.7 = (bf16[1,16,128,128]{3,2,1,0:T(8,128)(2,1)}, bf16[1,16,128,128]{3,2,1,0:T(8,128)(2,1)S(1)}, u32[]{:S(2)}, u32[]{:S(2)}) collective-permute-start(bf16[1,16,128,128]{3,2,1,0:T(8,128)(2,1)} %collective-permute-done.refs_2_), channel_id=1, source_target_pairs={{0,4},{2,6},{8,12},{10,14},{16,20},{18,22},{24,28},{26,30},{1,5},{... | collective-permute-start | bytes 1572872 | tf_op jit(solution)/shard_map/ppermute | solution.py:29
  48.1 15.6 %collective-permute-start.8 = (bf16[1,16,128,128]{3,2,1,0:T(8,128)(2,1)}, bf16[1,16,128,128]{3,2,1,0:T(8,128)(2,1)S(1)}, u32[]{:S(2)}, u32[]{:S(2)}) collective-permute-start(bf16[1,16,128,128]{3,2,1,0:T(8,128)(2,1)} %collective-permute-done.1.refs_0_), channel_id=1, source_target_pairs={{4,0},{6,2},{12,8},{14,10},{20,16},{22,18},{28,24},{30,26},{5,1},{... | collective-permute-start | bytes 1572872 | tf_op jit(solution)/shard_map/ppermute | solution.py:29
  50.5 23.5 %copy-start.15 = (bf16[1,16,128,128]{3,2,1,0:T(8,128)(2,1)}, bf16[1,16,128,128]{3,2,1,0:T(8,128)(2,1)S(1)}, u32[]{:S(2)}) copy-start(bf16[1,16,128,128]{3,2,1,0:T(8,128)(2,1)S(1)} %broadcast_select_fusion.3.refs_2_) | copy-start | bytes 1572868
  50.5 23.5 %collective-permute-start.2 = (bf16[1,16,128,128]{3,2,1,0:T(8,128)(2,1)S(1)}, bf16[1,16,128,128]{3,2,1,0:T(8,128)(2,1)S(1)}, u32[]{:S(2)}, u32[]{:S(2)}) collective-permute-start(bf16[1,16,128,128]{3,2,1,0:T(8,128)(2,1)S(1)} %bitcast.46), channel_id=1, source_target_pairs={{0,2},{4,6},{8,10},{12,14},{16,18},{20,22},{24,26},{28,30},{1,3},{... | collective-permute-start | bytes 1572872 | tf_op jit(solution)/shard_map/ppermute | solution.py:29
  51.9 16.3 %collective-permute-start.17 = (bf16[1,16,128,128]{3,2,1,0:T(8,128)(2,1)}, bf16[1,16,128,128]{3,2,1,0:T(8,128)(2,1)S(1)}, u32[]{:S(2)}, u32[]{:S(2)}) collective-permute-start(bf16[1,16,128,128]{3,2,1,0:T(8,128)(2,1)} %collective-permute-done.10.refs_5_), channel_id=1, source_target_pairs={{0,4},{2,6},{8,12},{10,14},{16,20},{18,22},{24,28},{26,30},{1,5},{... | collective-permute-start | bytes 1572872 | tf_op jit(solution)/shard_map/ppermute | solution.py:29
  55.5 17.0 %collective-permute-start.18 = (bf16[1,16,128,128]{3,2,1,0:T(8,128)(2,1)}, bf16[1,16,128,128]{3,2,1,0:T(8,128)(2,1)S(1)}, u32[]{:S(2)}, u32[]{:S(2)}) collective-permute-start(bf16[1,16,128,128]{3,2,1,0:T(8,128)(2,1)} %collective-permute-done.11.refs_6_), channel_id=1, source_target_pairs={{4,0},{6,2},{12,8},{14,10},{20,16},{22,18},{28,24},{30,26},{5,1},{... | collective-permute-start | bytes 1572872 | tf_op jit(solution)/shard_map/ppermute | solution.py:29
  57.9 18.8 %copy-start.16 = (bf16[1,16,128,128]{3,2,1,0:T(8,128)(2,1)}, bf16[1,16,128,128]{3,2,1,0:T(8,128)(2,1)S(1)}, u32[]{:S(2)}) copy-start(bf16[1,16,128,128]{3,2,1,0:T(8,128)(2,1)S(1)} %broadcast_select_fusion.1.refs_8_) | copy-start | bytes 1572868
  59.1 16.2 %collective-permute-start.12 = (bf16[1,16,128,128]{3,2,1,0:T(8,128)(2,1)S(1)}, bf16[1,16,128,128]{3,2,1,0:T(8,128)(2,1)S(1)}, u32[]{:S(2)}, u32[]{:S(2)}) collective-permute-start(bf16[1,16,128,128]{3,2,1,0:T(8,128)(2,1)S(1)} %bitcast.50), channel_id=1, source_target_pairs={{0,2},{4,6},{8,10},{12,14},{16,18},{20,22},{24,26},{28,30},{1,3},{... | collective-permute-start | bytes 1572872 | tf_op jit(solution)/shard_map/ppermute | solution.py:29
  63.7 11.7 %collective-permute-start.3 = (bf16[1,16,128,128]{3,2,1,0:T(8,128)(2,1)}, bf16[1,16,128,128]{3,2,1,0:T(8,128)(2,1)S(1)}, u32[]{:S(2)}, u32[]{:S(2)}) collective-permute-start(bf16[1,16,128,128]{3,2,1,0:T(8,128)(2,1)} %collective-permute-done.1.refs_0_), channel_id=1, source_target_pairs={{2,0},{6,4},{10,8},{14,12},{18,16},{22,20},{26,24},{30,28},{3,1},{... | collective-permute-start | bytes 1572872 | tf_op jit(solution)/shard_map/ppermute | solution.py:29
  65.1 12.5 %copy-start.17 = (bf16[1,16,128,128]{3,2,1,0:T(8,128)(2,1)}, bf16[1,16,128,128]{3,2,1,0:T(8,128)(2,1)S(1)}, u32[]{:S(2)}) copy-start(bf16[1,16,128,128]{3,2,1,0:T(8,128)(2,1)S(1)} %broadcast_select_fusion.2.refs_4_) | copy-start | bytes 1572868
  68.2 9.4 %collective-permute-start.6 = (bf16[1,16,128,128]{3,2,1,0:T(8,128)(2,1)S(1)}, bf16[1,16,128,128]{3,2,1,0:T(8,128)(2,1)S(1)}, u32[]{:S(2)}, u32[]{:S(2)}) collective-permute-start(bf16[1,16,128,128]{3,2,1,0:T(8,128)(2,1)S(1)} %broadcast_select_fusion.3.refs_2_), channel_id=1, source_target_pairs={{0,2},{2,0},{4,6},{6,4},{8,10},{10,8},{12,14},{14,12},{16,18},{18,... | collective-permute-start | bytes 1572872 | tf_op jit(solution)/shard_map/ppermute | solution.py:24
  72.5 4.2 %collective-permute-start.13 = (bf16[1,16,128,128]{3,2,1,0:T(8,128)(2,1)}, bf16[1,16,128,128]{3,2,1,0:T(8,128)(2,1)S(1)}, u32[]{:S(2)}, u32[]{:S(2)}) collective-permute-start(bf16[1,16,128,128]{3,2,1,0:T(8,128)(2,1)} %collective-permute-done.11.refs_6_), channel_id=1, source_target_pairs={{2,0},{6,4},{10,8},{14,12},{18,16},{22,20},{26,24},{30,28},{3,1},{... | collective-permute-start | bytes 1572872 | tf_op jit(solution)/shard_map/ppermute | solution.py:29
  74.0 3.8 %copy-start.18 = (bf16[1,16,128,128]{3,2,1,0:T(8,128)(2,1)}, bf16[1,16,128,128]{3,2,1,0:T(8,128)(2,1)S(1)}, u32[]{:S(2)}) copy-start(bf16[1,16,128,128]{3,2,1,0:T(8,128)(2,1)S(1)} %broadcast_select_fusion.refs_10_) | copy-start | bytes 1572868
  74.1 3.5 %collective-permute-start.16 = (bf16[1,16,128,128]{3,2,1,0:T(8,128)(2,1)S(1)}, bf16[1,16,128,128]{3,2,1,0:T(8,128)(2,1)S(1)}, u32[]{:S(2)}, u32[]{:S(2)}) collective-permute-start(bf16[1,16,128,128]{3,2,1,0:T(8,128)(2,1)S(1)} %broadcast_select_fusion.1.refs_8_), channel_id=1, source_target_pairs={{0,2},{2,0},{4,6},{6,4},{8,10},{10,8},{12,14},{14,12},{16,18},{18,... | collective-permute-start | bytes 1572872 | tf_op jit(solution)/shard_map/ppermute | solution.py:24
  75.3 2.5 %collective-permute-start.9 = (bf16[1,16,128,128]{3,2,1,0:T(8,128)(2,1)S(1)}, bf16[1,16,128,128]{3,2,1,0:T(8,128)(2,1)S(1)}, u32[]{:S(2)}, u32[]{:S(2)}) collective-permute-start(bf16[1,16,128,128]{3,2,1,0:T(8,128)(2,1)S(1)} %broadcast_select_fusion.2.refs_4_), channel_id=1, source_target_pairs={{0,2},{2,0},{4,6},{6,4},{8,10},{10,8},{12,14},{14,12},{16,18},{18,... | collective-permute-start | bytes 1572872 | tf_op jit(solution)/shard_map/ppermute | solution.py:24
  75.4 3.2 %collective-permute-start.19 = (bf16[1,16,128,128]{3,2,1,0:T(8,128)(2,1)S(1)}, bf16[1,16,128,128]{3,2,1,0:T(8,128)(2,1)S(1)}, u32[]{:S(2)}, u32[]{:S(2)}) collective-permute-start(bf16[1,16,128,128]{3,2,1,0:T(8,128)(2,1)S(1)} %broadcast_select_fusion.refs_10_), channel_id=1, source_target_pairs={{0,2},{2,0},{4,6},{6,4},{8,10},{10,8},{12,14},{14,12},{16,18},{18,... | collective-permute-start | bytes 1572872 | tf_op jit(solution)/shard_map/ppermute | solution.py:24
  77.5 1.0 copy-start.22
  77.5 1.8 copy-start.23
  77.8 1.6 copy-start.24
  78.5 0.8 copy-start.25
  101.4 5.9 %copy-start.10 = (bf16[1,16,128,128]{3,2,1,0:T(8,128)(2,1)S(1)}, bf16[1,16,128,128]{3,2,1,0:T(8,128)(2,1)}, u32[]{:S(2)}) copy-start(bf16[1,16,128,128]{3,2,1,0:T(8,128)(2,1)} %get-tuple-element.32) | copy-start | bytes 1572868
  101.4 2.2 %collective-permute-start.20 = (bf16[1,16,128,128]{3,2,1,0:T(8,128)(2,1)}, bf16[1,16,128,128]{3,2,1,0:T(8,128)(2,1)S(1)}, u32[]{:S(2)}, u32[]{:S(2)}) collective-permute-start(bf16[1,16,128,128]{3,2,1,0:T(8,128)(2,1)} %get-tuple-element.29), channel_id=1, source_target_pairs={{0,2},{2,0},{4,6},{6,4},{8,10},{10,8},{12,14},{14,12},{16,18},{18,... | collective-permute-start | bytes 1572872 | tf_op jit(solution)/shard_map/ppermute | solution.py:24
  101.7 4.2 %collective-permute-start.21 = (bf16[1,16,128,128]{3,2,1,0:T(8,128)(2,1)}, bf16[1,16,128,128]{3,2,1,0:T(8,128)(2,1)S(1)}, u32[]{:S(2)}, u32[]{:S(2)}) collective-permute-start(bf16[1,16,128,128]{3,2,1,0:T(8,128)(2,1)} %get-tuple-element.31), channel_id=1, source_target_pairs={{0,2},{2,0},{4,6},{6,4},{8,10},{10,8},{12,14},{14,12},{16,18},{18,... | collective-permute-start | bytes 1572872 | tf_op jit(solution)/shard_map/ppermute | solution.py:24
  102.0 7.5 %collective-permute-start.24 = (bf16[1,16,128,128]{3,2,1,0:T(8,128)(2,1)}, bf16[1,16,128,128]{3,2,1,0:T(8,128)(2,1)S(1)}, u32[]{:S(2)}, u32[]{:S(2)}) collective-permute-start(bf16[1,16,128,128]{3,2,1,0:T(8,128)(2,1)} %collective-permute-done.refs_2_), channel_id=1, source_target_pairs={{0,2},{2,0},{4,6},{6,4},{8,10},{10,8},{12,14},{14,12},{16,18},{18,... | collective-permute-start | bytes 1572872 | tf_op jit(solution)/shard_map/ppermute | solution.py:24
  102.2 9.9 %collective-permute-start.25 = (bf16[1,16,128,128]{3,2,1,0:T(8,128)(2,1)}, bf16[1,16,128,128]{3,2,1,0:T(8,128)(2,1)}, u32[]{:S(2)}, u32[]{:S(2)}) collective-permute-start(bf16[1,16,128,128]{3,2,1,0:T(8,128)(2,1)} %collective-permute-done.10.refs_5_), channel_id=1, source_target_pairs={{0,2},{2,0},{4,6},{6,4},{8,10},{10,8},{12,14},{14,12},{16,18},{18,... | collective-permute-start | bytes 1572872 | tf_op jit(solution)/shard_map/ppermute | solution.py:24
  102.5 4.8 %collective-permute-start.22 = (bf16[1,16,128,128]{3,2,1,0:T(8,128)(2,1)}, bf16[1,16,128,128]{3,2,1,0:T(8,128)(2,1)S(1)}, u32[]{:S(2)}, u32[]{:S(2)}) collective-permute-start(bf16[1,16,128,128]{3,2,1,0:T(8,128)(2,1)} %get-tuple-element.33), channel_id=1, source_target_pairs={{0,2},{2,0},{4,6},{6,4},{8,10},{10,8},{12,14},{14,12},{16,18},{18,... | collective-permute-start | bytes 1572872 | tf_op jit(solution)/shard_map/ppermute | solution.py:24
  103.6 4.7 %collective-permute-start.23 = (bf16[1,16,128,128]{3,2,1,0:T(8,128)(2,1)}, bf16[1,16,128,128]{3,2,1,0:T(8,128)(2,1)S(1)}, u32[]{:S(2)}, u32[]{:S(2)}) collective-permute-start(bf16[1,16,128,128]{3,2,1,0:T(8,128)(2,1)} %get-tuple-element.35), channel_id=1, source_target_pairs={{0,2},{2,0},{4,6},{6,4},{8,10},{10,8},{12,14},{14,12},{16,18},{18,... | collective-permute-start | bytes 1572872 | tf_op jit(solution)/shard_map/ppermute | solution.py:24
  103.8 4.6 %copy-start.9 = (bf16[1,16,128,128]{3,2,1,0:T(8,128)(2,1)S(1)}, bf16[1,16,128,128]{3,2,1,0:T(8,128)(2,1)}, u32[]{:S(2)}) copy-start(bf16[1,16,128,128]{3,2,1,0:T(8,128)(2,1)} %get-tuple-element.34) | copy-start | bytes 1572868
  105.8 19.3 %collective-permute-start.26 = (bf16[1,16,128,128]{3,2,1,0:T(8,128)(2,1)}, bf16[1,16,128,128]{3,2,1,0:T(8,128)(2,1)S(1)}, u32[]{:S(2)}, u32[]{:S(2)}) collective-permute-start(bf16[1,16,128,128]{3,2,1,0:T(8,128)(2,1)} %get-tuple-element.40), channel_id=1, source_target_pairs={{0,2},{2,0},{4,6},{6,4},{8,10},{10,8},{12,14},{14,12},{16,18},{18,... | collective-permute-start | bytes 1572872 | tf_op jit(solution)/shard_map/ppermute | solution.py:24
  109.3 16.1 %collective-permute-start.29 = (bf16[1,16,128,128]{3,2,1,0:T(8,128)(2,1)S(1)}, bf16[1,16,128,128]{3,2,1,0:T(8,128)(2,1)S(1)}, u32[]{:S(2)}, u32[]{:S(2)}) collective-permute-start(bf16[1,16,128,128]{3,2,1,0:T(8,128)(2,1)S(1)} %add_convert_fusion.2), channel_id=1, source_target_pairs={{0,4},{2,6},{4,0},{6,2},{8,12},{10,14},{12,8},{14,10},{16,20},{18,... | collective-permute-start | bytes 1572872 | tf_op jit(solution)/shard_map/ppermute | solution.py:24
  109.3 19.5 %collective-permute-start.32 = (bf16[1,16,128,128]{3,2,1,0:T(8,128)(2,1)}, bf16[1,16,128,128]{3,2,1,0:T(8,128)(2,1)S(1)}, u32[]{:S(2)}, u32[]{:S(2)}) collective-permute-start(bf16[1,16,128,128]{3,2,1,0:T(8,128)(2,1)} %get-tuple-element.47), channel_id=1, source_target_pairs={{0,2},{2,0},{4,6},{6,4},{8,10},{10,8},{12,14},{14,12},{16,18},{18,... | collective-permute-start | bytes 1572872 | tf_op jit(solution)/shard_map/ppermute | solution.py:24
  109.5 2.6 %copy-start.21 = (bf16[1,16,128,128]{3,2,1,0:T(8,128)(2,1)}, bf16[1,16,128,128]{3,2,1,0:T(8,128)(2,1)S(1)}, u32[]{:S(2)}) copy-start(bf16[1,16,128,128]{3,2,1,0:T(8,128)(2,1)S(1)} %collective-permute-done.24.refs_3_) | copy-start | bytes 1572868
  109.5 25.8 %collective-permute-start.35 = (bf16[1,16,128,128]{3,2,1,0:T(8,128)(2,1)}, bf16[1,16,128,128]{3,2,1,0:T(8,128)(2,1)S(1)}, u32[]{:S(2)}, u32[]{:S(2)}) collective-permute-start(bf16[1,16,128,128]{3,2,1,0:T(8,128)(2,1)} %add_convert_fusion), channel_id=1, source_target_pairs={{0,4},{2,6},{4,0},{6,2},{8,12},{10,14},{12,8},{14,10},{16,20},{18,... | collective-permute-start | bytes 1572872 | tf_op jit(solution)/shard_map/ppermute | solution.py:24
  112.1 34.5 %collective-permute-start.27 = (bf16[1,16,128,128]{3,2,1,0:T(8,128)(2,1)}, bf16[1,16,128,128]{3,2,1,0:T(8,128)(2,1)S(1)}, u32[]{:S(2)}, u32[]{:S(2)}) collective-permute-start(bf16[1,16,128,128]{3,2,1,0:T(8,128)(2,1)} %add_convert_fusion.3), channel_id=1, source_target_pairs={{0,4},{2,6},{4,0},{6,2},{8,12},{10,14},{12,8},{14,10},{16,20},{18,... | collective-permute-start | bytes 1572872 | tf_op jit(solution)/shard_map/ppermute | solution.py:24
  125.1 10.2 %copy-start.19 = (bf16[1,16,128,128]{3,2,1,0:T(8,128)(2,1)S(1)}, bf16[1,16,128,128]{3,2,1,0:T(8,128)(2,1)}, u32[]{:S(2)}) copy-start(bf16[1,16,128,128]{3,2,1,0:T(8,128)(2,1)} %get-tuple-element.52) | copy-start | bytes 1572868
  125.1 22.7 %collective-permute-start.28 = (bf16[1,16,128,128]{3,2,1,0:T(8,128)(2,1)}, bf16[1,16,128,128]{3,2,1,0:T(8,128)(2,1)}, u32[]{:S(2)}, u32[]{:S(2)}) collective-permute-start(bf16[1,16,128,128]{3,2,1,0:T(8,128)(2,1)} %get-tuple-element.43), channel_id=1, source_target_pairs={{0,2},{2,0},{4,6},{6,4},{8,10},{10,8},{12,14},{14,12},{16,18},{18,... | collective-permute-start | bytes 1572872 | tf_op jit(solution)/shard_map/ppermute | solution.py:24
  127.5 20.4 %collective-permute-start.30 = (bf16[1,16,128,128]{3,2,1,0:T(8,128)(2,1)}, bf16[1,16,128,128]{3,2,1,0:T(8,128)(2,1)}, u32[]{:S(2)}, u32[]{:S(2)}) collective-permute-start(bf16[1,16,128,128]{3,2,1,0:T(8,128)(2,1)} %fusion.6), channel_id=1, source_target_pairs={{8,0},{10,2},{12,4},{14,6},{16,8},{18,10},{20,12},{22,14},{24,16},... | collective-permute-start | bytes 1572872 | tf_op jit(solution)/shard_map/ppermute | solution.py:20
  128.8 28.2 %collective-permute-start.33 = (bf16[1,16,128,128]{3,2,1,0:T(8,128)(2,1)}, bf16[1,16,128,128]{3,2,1,0:T(8,128)(2,1)S(1)}, u32[]{:S(2)}, u32[]{:S(2)}) collective-permute-start(bf16[1,16,128,128]{3,2,1,0:T(8,128)(2,1)} %add_convert_fusion.1), channel_id=1, source_target_pairs={{0,4},{2,6},{4,0},{6,2},{8,12},{10,14},{12,8},{14,10},{16,20},{18,... | collective-permute-start | bytes 1572872 | tf_op jit(solution)/shard_map/ppermute | solution.py:24
  135.3 21.7 %collective-permute-start.34 = (bf16[1,16,128,128]{3,2,1,0:T(8,128)(2,1)}, bf16[1,16,128,128]{3,2,1,0:T(8,128)(2,1)}, u32[]{:S(2)}, u32[]{:S(2)}) collective-permute-start(bf16[1,16,128,128]{3,2,1,0:T(8,128)(2,1)} %get-tuple-element.50), channel_id=1, source_target_pairs={{0,2},{2,0},{4,6},{6,4},{8,10},{10,8},{12,14},{14,12},{16,18},{18,... | collective-permute-start | bytes 1572872 | tf_op jit(solution)/shard_map/ppermute | solution.py:24
  146.6 19.5 %copy-start.2 = (bf16[1,16,128,128]{3,2,1,0:T(8,128)(2,1)}, bf16[1,16,128,128]{3,2,1,0:T(8,128)(2,1)S(1)}, u32[]{:S(2)}) copy-start(bf16[1,16,128,128]{3,2,1,0:T(8,128)(2,1)S(1)} %collective-permute-done.27) | copy-start | bytes 1572868
  146.6 17.1 %collective-permute-start.36 = (bf16[1,16,128,128]{3,2,1,0:T(8,128)(2,1)}, bf16[1,16,128,128]{3,2,1,0:T(8,128)(2,1)}, u32[]{:S(2)}, u32[]{:S(2)}) collective-permute-start(bf16[1,16,128,128]{3,2,1,0:T(8,128)(2,1)} %fusion.16), channel_id=1, source_target_pairs={{8,0},{10,2},{12,4},{14,6},{16,8},{18,10},{20,12},{22,14},{24,16},... | collective-permute-start | bytes 1572872 | tf_op jit(solution)/shard_map/ppermute | solution.py:20
  147.9 15.8 %copy-start.20 = (bf16[1,16,128,128]{3,2,1,0:T(8,128)(2,1)S(1)}, bf16[1,16,128,128]{3,2,1,0:T(8,128)(2,1)}, u32[]{:S(2)}) copy-start(bf16[1,16,128,128]{3,2,1,0:T(8,128)(2,1)} %get-tuple-element.49) | copy-start | bytes 1572868
  150.5 16.8 %copy-start.1 = (f32[16,128,256]{2,1,0:T(8,128)S(1)}, f32[16,128,256]{2,1,0:T(8,128)}, u32[]{:S(2)}) copy-start(f32[16,128,256]{2,1,0:T(8,128)} %get-tuple-element.38) | copy-start | bytes 6291460
  150.5 24.3 %collective-permute-start.31 = (bf16[1,16,128,128]{3,2,1,0:T(8,128)(2,1)}, bf16[1,16,128,128]{3,2,1,0:T(8,128)(2,1)}, u32[]{:S(2)}, u32[]{:S(2)}) collective-permute-start(bf16[1,16,128,128]{3,2,1,0:T(8,128)(2,1)} %fusion.9), channel_id=1, source_target_pairs={{8,0},{10,2},{12,4},{14,6},{16,8},{18,10},{20,12},{22,14},{24,16},... | collective-permute-start | bytes 1572872 | tf_op jit(solution)/shard_map/ppermute | solution.py:20
  157.0 10.3 %copy-start.4 = (bf16[1,16,128,128]{3,2,1,0:T(8,128)(2,1)}, bf16[1,16,128,128]{3,2,1,0:T(8,128)(2,1)S(1)}, u32[]{:S(2)}) copy-start(bf16[1,16,128,128]{3,2,1,0:T(8,128)(2,1)S(1)} %collective-permute-done.33) | copy-start | bytes 1572868
  166.1 17.6 %collective-permute-start.37 = (bf16[1,16,128,128]{3,2,1,0:T(8,128)(2,1)}, bf16[1,16,128,128]{3,2,1,0:T(8,128)(2,1)}, u32[]{:S(2)}, u32[]{:S(2)}) collective-permute-start(bf16[1,16,128,128]{3,2,1,0:T(8,128)(2,1)} %fusion.19), channel_id=1, source_target_pairs={{8,0},{10,2},{12,4},{14,6},{16,8},{18,10},{20,12},{22,14},{24,16},... | collective-permute-start | bytes 1572872 | tf_op jit(solution)/shard_map/ppermute | solution.py:20
  167.9 6.9 %copy-start.3 = (bf16[1,16,128,128]{3,2,1,0:T(8,128)(2,1)S(1)}, bf16[1,16,128,128]{3,2,1,0:T(8,128)(2,1)}, u32[]{:S(2)}) copy-start(bf16[1,16,128,128]{3,2,1,0:T(8,128)(2,1)} %copy-done.2) | copy-start | bytes 1572868
  171.7 11.9 %copy-start.5 = (bf16[1,16,128,128]{3,2,1,0:T(8,128)(2,1)S(1)}, bf16[1,16,128,128]{3,2,1,0:T(8,128)(2,1)}, u32[]{:S(2)}) copy-start(bf16[1,16,128,128]{3,2,1,0:T(8,128)(2,1)} %copy-done.4) | copy-start | bytes 1572868
  171.7 11.9 %copy-start.8 = (bf16[1,16,128,128]{3,2,1,0:T(8,128)(2,1)S(1)}, bf16[1,16,128,128]{3,2,1,0:T(8,128)(2,1)}, u32[]{:S(2)}) copy-start(bf16[1,16,128,128]{3,2,1,0:T(8,128)(2,1)} %get-tuple-element.46) | copy-start | bytes 1572868

commit v11 on v10

--- a/solution.py
+++ b/solution.py
@@ -175,8 +175,8 @@
     kb = route(normed_key_rows.transpose(1, 0, 2)[None], n, half, core)
     vb = route(value_rows.transpose(1, 0, 2)[None], n, half, core)
 
-    late = [3, 4, 5, 6, 7, 8]
-    early = [0, 1, 2]
+    late = [5, 6, 7, 8]
+    early = [0, 1, 2, 3, 4]
     modes = [0, 1, 1, 2, 1, 1, 1, 1, 1]
     dist = [0, PLANE, 3 + 2 * core, 2 * PLANE, 7 - 6 * core, 2, 1 + 2 * core, 6, 5 + 2 * core]
     terms = [None] * 18

time: 187 us -> 203 us (1.086)
  waiting for transfers between devices: 53 us -> 66.5 us
    ppermute x18, waiting for transfers between devices: 21.9 us -> 35.1 us  [swap(): return lax.ppermute(x, 'seq', [(i, i ^ bit) for i in range(n)])]
    ppermute x12, waiting for transfers between devices: 11.9 us -> 16.4 us  [one_way(): return lax.ppermute(x, 'seq', pairs)]
    ppermute x8, waiting for transfers between devices: 19.2 us -> 15 us  [shift(): return lax.ppermute(x, 'seq', pairs)]
    ppermute x18, starting transfers between devices: 7.83 us -> 5.49 us  [swap(): return lax.ppermute(x, 'seq', [(i, i ^ bit) for i in range(n)])]
    unnamed x56 -> x42, local copies, waits for them, and re-layouts: 6.47 us -> 7.21 us
  transfers between devices with their start and end apart: 38 -> 38, of which waited for: 14 -> 12; matrix products, arithmetic and copies ran while one was open for 17% -> 16% of each run, Pallas kernels for 7% -> 8%
where the time goes in v11:
time: 203 us; the launch traced here: 202 us
  waiting for transfers between devices  66.5 us (33%)
  starting transfers between devices  61.5 us (30%)
  Pallas kernels  34.9 us (17%)
  other arithmetic  22.9 us (11%)
  local copies, waits for them, and re-layouts  14.8 us (7%)
    ppermute x18, waiting for transfers between devices, swap(): return lax.ppermute(x, 'seq', [(i, i ^ bit) for i in range(n)])  35.1 us
    pallas_call x2, Pallas kernels, attend_blocks(): pl.pallas_call(functools.partial(_blocks_kernel, tuple(modes), acc is not...  34.9 us
    ppermute x12, starting transfers between devices, one_way(): return lax.ppermute(x, 'seq', pairs)  31 us
    ppermute x8, starting transfers between devices, shift(): return lax.ppermute(x, 'seq', pairs)  25.1 us
    ppermute x12, waiting for transfers between devices, one_way(): return lax.ppermute(x, 'seq', pairs)  16.4 us
    ppermute x8, waiting for transfers between devices, shift(): return lax.ppermute(x, 'seq', pairs)  15 us
    unnamed x42, local copies, waits for them, and re-layouts  7.21 us
    ppermute x18, starting transfers between devices, swap(): return lax.ppermute(x, 'seq', [(i, i ^ bit) for i in range(n)])  5.49 us
  transfers between devices with their start and end apart: 38, of which 12 were waited for; matrix products, arithmetic and copies ran while one was open for 16% of the time, Pallas kernels for 8%

profile of v11, /device:TPU:0, one launch (start us, length us, event | category | flops | bytes accessed | tf_op | source)
XLA Modules:
  0.0 201.8 jit_solution(18404701473907783141)
XLA Ops:
  0.6 2.0 copy.26
  2.6 5.7 %collective-permute-start.9 = (bf16[1,16,128,128]{3,2,1,0:T(8,128)(2,1)}, bf16[1,16,128,128]{3,2,1,0:T(8,128)(2,1)}, u32[]{:S(2)}, u32[]{:S(2)}) collective-permute-start(bf16[1,16,128,128]{3,2,1,0:T(8,128)(2,1)} %bitcast.34.refs_6_), channel_id=1, source_target_pairs={{0,8},{2,10},{4,12},{6,14},{8,16},{10,18},{12,20},{14,22},{16,24},... | collective-permute-start | bytes 1572872 | tf_op jit(solution)/shard_map/ppermute | solution.py:20
  8.3 2.0 copy.27
  10.3 3.5 %collective-permute-start.1 = (bf16[1,16,128,128]{3,2,1,0:T(8,128)(2,1)}, bf16[1,16,128,128]{3,2,1,0:T(8,128)(2,1)}, u32[]{:S(2)}, u32[]{:S(2)}) collective-permute-start(bf16[1,16,128,128]{3,2,1,0:T(8,128)(2,1)} %bitcast.35.refs_1_), channel_id=1, source_target_pairs={{0,8},{2,10},{4,12},{6,14},{8,16},{10,18},{12,20},{14,22},{16,24},... | collective-permute-start | bytes 1572872 | tf_op jit(solution)/shard_map/ppermute | solution.py:20
  13.8 3.4 %collective-permute-start.8 = (bf16[1,16,128,128]{3,2,1,0:T(8,128)(2,1)}, bf16[1,16,128,128]{3,2,1,0:T(8,128)(2,1)S(1)}, u32[]{:S(2)}, u32[]{:S(2)}) collective-permute-start(bf16[1,16,128,128]{3,2,1,0:T(8,128)(2,1)} %bitcast.34.refs_6_), channel_id=1, source_target_pairs={{0,4},{2,6},{8,12},{10,14},{16,20},{18,22},{24,28},{26,30},{1,5},{... | collective-permute-start | bytes 1572872 | tf_op jit(solution)/shard_map/ppermute | solution.py:29
  17.2 2.9 %collective-permute-done.9.refs_7_ = bf16[1,16,128,128]{3,2,1,0:T(8,128)(2,1)} collective-permute-done((bf16[1,16,128,128]{3,2,1,0:T(8,128)(2,1)}, bf16[1,16,128,128]{3,2,1,0:T(8,128)(2,1)}, u32[]{:S(2)}, u32[]{:S(2)}) %collective-permute-start.9) | collective-permute-done | bytes 524320 | tf_op jit(solution)/shard_map/ppermute | solution.py:20
  20.1 5.2 %collective-permute-start.13 = (bf16[1,16,128,128]{3,2,1,0:T(8,128)(2,1)}, bf16[1,16,128,128]{3,2,1,0:T(8,128)(2,1)}, u32[]{:S(2)}, u32[]{:S(2)}) collective-permute-start(bf16[1,16,128,128]{3,2,1,0:T(8,128)(2,1)} %collective-permute-done.9.refs_7_), channel_id=1, source_target_pairs={{0,8},{2,10},{4,12},{6,14},{8,16},{10,18},{12,20},{14,22},{16,24},... | collective-permute-start | bytes 1572872 | tf_op jit(solution)/shard_map/ppermute | solution.py:20
  25.4 1.3 collective-permute-start.10
  26.7 4.6 %collective-permute-start = (bf16[1,16,128,128]{3,2,1,0:T(8,128)(2,1)}, bf16[1,16,128,128]{3,2,1,0:T(8,128)(2,1)S(1)}, u32[]{:S(2)}, u32[]{:S(2)}) collective-permute-start(bf16[1,16,128,128]{3,2,1,0:T(8,128)(2,1)} %bitcast.35.refs_1_), channel_id=1, source_target_pairs={{0,4},{2,6},{8,12},{10,14},{16,20},{18,22},{24,28},{26,30},{1,5},{... | collective-permute-start | bytes 1572872 | tf_op jit(solution)/shard_map/ppermute | solution.py:29
  31.4 5.2 %collective-permute-start.5 = (bf16[1,16,128,128]{3,2,1,0:T(8,128)(2,1)}, bf16[1,16,128,128]{3,2,1,0:T(8,128)(2,1)}, u32[]{:S(2)}, u32[]{:S(2)}) collective-permute-start(bf16[1,16,128,128]{3,2,1,0:T(8,128)(2,1)} %collective-permute-done.1.refs_2_), channel_id=1, source_target_pairs={{0,8},{2,10},{4,12},{6,14},{8,16},{10,18},{12,20},{14,22},{16,24},... | collective-permute-start | bytes 1572872 | tf_op jit(solution)/shard_map/ppermute | solution.py:20
  36.6 1.3 collective-permute-start.2
  37.9 4.7 %collective-permute-done.13.refs_9_ = bf16[1,16,128,128]{3,2,1,0:T(8,128)(2,1)} collective-permute-done((bf16[1,16,128,128]{3,2,1,0:T(8,128)(2,1)}, bf16[1,16,128,128]{3,2,1,0:T(8,128)(2,1)}, u32[]{:S(2)}, u32[]{:S(2)}) %collective-permute-start.13) | collective-permute-done | bytes 524320 | tf_op jit(solution)/shard_map/ppermute | solution.py:20
  42.6 3.4 %collective-permute-start.12 = (bf16[1,16,128,128]{3,2,1,0:T(8,128)(2,1)}, bf16[1,16,128,128]{3,2,1,0:T(8,128)(2,1)S(1)}, u32[]{:S(2)}, u32[]{:S(2)}) collective-permute-start(bf16[1,16,128,128]{3,2,1,0:T(8,128)(2,1)} %collective-permute-done.9.refs_7_), channel_id=1, source_target_pairs={{0,4},{2,6},{8,12},{10,14},{16,20},{18,22},{24,28},{26,30},{1,5},{... | collective-permute-start | bytes 1572872 | tf_op jit(solution)/shard_map/ppermute | solution.py:29
  46.1 1.3 collective-permute-start.14
  47.4 0.9 broadcast_select_fusion.3.refs_4_
  48.3 4.7 %collective-permute-start.4 = (bf16[1,16,128,128]{3,2,1,0:T(8,128)(2,1)}, bf16[1,16,128,128]{3,2,1,0:T(8,128)(2,1)S(1)}, u32[]{:S(2)}, u32[]{:S(2)}) collective-permute-start(bf16[1,16,128,128]{3,2,1,0:T(8,128)(2,1)} %collective-permute-done.1.refs_2_), channel_id=1, source_target_pairs={{0,4},{2,6},{8,12},{10,14},{16,20},{18,22},{24,28},{26,30},{1,5},{... | collective-permute-start | bytes 1572872 | tf_op jit(solution)/shard_map/ppermute | solution.py:29
  53.1 1.3 collective-permute-start.6
  54.4 0.9 broadcast_select_fusion.5.refs_0_
  55.3 3.4 %collective-permute-done.12 = bf16[1,16,128,128]{3,2,1,0:T(8,128)(2,1)S(1)} collective-permute-done((bf16[1,16,128,128]{3,2,1,0:T(8,128)(2,1)}, bf16[1,16,128,128]{3,2,1,0:T(8,128)(2,1)S(1)}, u32[]{:S(2)}, u32[]{:S(2)}) %collective-permute-start.12) | collective-permute-done | bytes 524320 | tf_op jit(solution)/shard_map/ppermute | solution.py:29
  58.7 4.3 %collective-permute-done.14 = bf16[1,16,128,128]{3,2,1,0:T(8,128)(2,1)S(1)} collective-permute-done((bf16[1,16,128,128]{3,2,1,0:T(8,128)(2,1)}, bf16[1,16,128,128]{3,2,1,0:T(8,128)(2,1)S(1)}, u32[]{:S(2)}, u32[]{:S(2)}) %collective-permute-start.14) | collective-permute-done | bytes 524320 | tf_op jit(solution)/shard_map/ppermute | solution.py:29
  63.0 0.9 broadcast_select_fusion.2.refs_6_
  63.9 2.8 %collective-permute-done.4 = bf16[1,16,128,128]{3,2,1,0:T(8,128)(2,1)S(1)} collective-permute-done((bf16[1,16,128,128]{3,2,1,0:T(8,128)(2,1)}, bf16[1,16,128,128]{3,2,1,0:T(8,128)(2,1)S(1)}, u32[]{:S(2)}, u32[]{:S(2)}) %collective-permute-start.4) | collective-permute-done | bytes 524320 | tf_op jit(solution)/shard_map/ppermute | solution.py:29
  66.7 5.8 %collective-permute-done.6 = bf16[1,16,128,128]{3,2,1,0:T(8,128)(2,1)S(1)} collective-permute-done((bf16[1,16,128,128]{3,2,1,0:T(8,128)(2,1)}, bf16[1,16,128,128]{3,2,1,0:T(8,128)(2,1)S(1)}, u32[]{:S(2)}, u32[]{:S(2)}) %collective-permute-start.6) | collective-permute-done | bytes 524320 | tf_op jit(solution)/shard_map/ppermute | solution.py:29
  72.5 0.8 broadcast_select_fusion.4.refs_2_
  73.4 3.2 %collective-permute-start.24 = (bf16[1,16,128,128]{3,2,1,0:T(8,128)(2,1)}, bf16[1,16,128,128]{3,2,1,0:T(8,128)(2,1)}, u32[]{:S(2)}, u32[]{:S(2)}) collective-permute-start(bf16[1,16,128,128]{3,2,1,0:T(8,128)(2,1)} %bitcast.34.refs_6_), channel_id=1, source_target_pairs={{0,2},{4,6},{8,10},{12,14},{16,18},{20,22},{24,26},{28,30},{1,3},{... | collective-permute-start | bytes 1572872 | tf_op jit(solution)/shard_map/ppermute | solution.py:29
  76.6 1.3 collective-permute-start.25
  77.9 0.6 multiply_reduce_fusion
  78.5 3.8 %collective-permute-start.21 = (bf16[1,16,128,128]{3,2,1,0:T(8,128)(2,1)}, bf16[1,16,128,128]{3,2,1,0:T(8,128)(2,1)S(1)}, u32[]{:S(2)}, u32[]{:S(2)}) collective-permute-start(bf16[1,16,128,128]{3,2,1,0:T(8,128)(2,1)} %bitcast.35.refs_1_), channel_id=1, source_target_pairs={{0,2},{4,6},{8,10},{12,14},{16,18},{20,22},{24,26},{28,30},{1,3},{... | collective-permute-start | bytes 1572872 | tf_op jit(solution)/shard_map/ppermute | solution.py:29
  82.4 1.3 collective-permute-start.22
  83.7 0.6 add_convert_fusion.4.valid_ref
  84.4 0.5 stack.52.valid_ref
  84.9 0.7 copy.18
  85.6 1.4 copy.16
  87.0 1.4 copy.17
  88.4 1.2 collective-permute-start.23
  89.6 15.8 %shard_map.85 = (f32[16,128,256]{2,1,0:T(8,128)}, bf16[1,16,128,128]{3,2,1,0:T(8,128)(2,1)}, bf16[1,16,128,128]{3,2,1,0:T(8,128)(2,1)}, bf16[1,16,128,128]{3,2,1...) custom-call(s32[4]{0:T(128)} %add_convert_fusion.4.valid_ref, ...), custom_call_target="tpu_custom_call" | custom-call | flops 2684354560 | bytes 10485760 | tf_op jit(solution)/shard_map/pallas_call | solution.py:105
  105.5 0.5 collective-permute-start.16
  106.0 1.9 broadcast_select_fusion.refs_10_
  108.0 0.8 broadcast_select_fusion.1.refs_5_
  109.4 0.9 add_convert_fusion.3
  110.3 1.0 add_convert_fusion.2
  111.3 1.0 add_convert_fusion.1
  112.5 0.8 copy-done.15
  113.5 19.1 %shard_map.86 = (f32[16,128,256]{2,1,0:T(8,128)}, bf16[1,16,128,128]{3,2,1,0:T(8,128)(2,1)}, bf16[1,16,128,128]{3,2,1,0:T(8,128)(2,1)}, bf16[1,16,128,128]{3,2,1...) custom-call(s32[5]{0:T(128)} %stack.52.valid_ref, ...), custom_call_target="tpu_custom_call" | custom-call | flops 3355443200 | bytes 14680064 | tf_op jit(solution)/shard_map/pallas_call | solution.py:105
  132.6 0.5 collective-permute-start.26
  133.2 1.9 collective-permute-start.35
  135.6 12.4 %collective-permute-done.29 = bf16[1,16,128,128]{3,2,1,0:T(8,128)(2,1)S(1)} collective-permute-done((bf16[1,16,128,128]{3,2,1,0:T(8,128)(2,1)}, bf16[1,16,128,128]{3,2,1,0:T(8,128)(2,1)S(1)}, u32[]{:S(2)}, u32[]{:S(2)}) %collective-permute-start.29) | collective-permute-done | bytes 524320 | tf_op jit(solution)/shard_map/ppermute | solution.py:24
  148.0 2.1 %fusion.6 = bf16[1,16,128,128]{3,2,1,0:T(8,128)(2,1)} fusion(bf16[1,16,128,128]{3,2,1,0:T(8,128)(2,1)S(1)} %collective-permute-done.26, bf16[1,16,128,128]{3,2,1,0:T(8,128)(2,1)S(1)} %collective-permute-done.29, bf16[1,16,128,128]{3,2,1,0:T(8,128)(2,1)} %get-tuple-element.45, pred[]{:T(512)S(6)} %eq.26, pred[]{:T(512)S(6)} %eq.12), kind=kLoop, calls=%fused_computation.18 | loop fusion | flops 2097152 | bytes 2097154 | tf_op jit(solution)/shard_map/convert_element_type | solution.py:154
  150.1 1.5 collective-permute-start.30
  151.7 7.6 %collective-permute-done.35 = bf16[1,16,128,128]{3,2,1,0:T(8,128)(2,1)S(1)} collective-permute-done((bf16[1,16,128,128]{3,2,1,0:T(8,128)(2,1)S(1)}, bf16[1,16,128,128]{3,2,1,0:T(8,128)(2,1)S(1)}, u32[]{:S(2)}, u32[]{:S(2)}) %collective-permute-start.35) | collective-permute-done | bytes 524320 | tf_op jit(solution)/shard_map/ppermute | solution.py:24
  159.3 1.1 fusion.16
  160.3 1.3 collective-permute-start.36
  161.6 8.9 %collective-permute-done.27 = bf16[1,16,128,128]{3,2,1,0:T(8,128)(2,1)S(1)} collective-permute-done((bf16[1,16,128,128]{3,2,1,0:T(8,128)(2,1)}, bf16[1,16,128,128]{3,2,1,0:T(8,128)(2,1)S(1)}, u32[]{:S(2)}, u32[]{:S(2)}) %collective-permute-start.27) | collective-permute-done | bytes 524320 | tf_op jit(solution)/shard_map/ppermute | solution.py:24
  170.5 2.8 %fusion.9 = bf16[1,16,128,128]{3,2,1,0:T(8,128)(2,1)} fusion(bf16[1,16,128,128]{3,2,1,0:T(8,128)(2,1)S(1)} %collective-permute-done.27, bf16[1,16,128,128]{3,2,1,0:T(8,128)(2,1)S(1)} %collective-permute-done.29, bf16[1,16,128,128]{3,2,1,0:T(8,128)(2,1)} %collective-permute-done.30, bf16[1,16,128,128]{3,2,1,0:T(8,128)(2,1)} %collective-permute-done.28, ...), kind=kLoop, calls=%fused_computation.21 | loop fusion | flops 2621440 | bytes 3145729 | tf_op jit(solution)/shard_map/convert_element_type | solution.py:156
  173.3 1.4 collective-permute-start.31
  174.7 6.2 %collective-permute-done.33 = bf16[1,16,128,128]{3,2,1,0:T(8,128)(2,1)S(1)} collective-permute-done((bf16[1,16,128,128]{3,2,1,0:T(8,128)(2,1)}, bf16[1,16,128,128]{3,2,1,0:T(8,128)(2,1)S(1)}, u32[]{:S(2)}, u32[]{:S(2)}) %collective-permute-start.33) | collective-permute-done | bytes 524320 | tf_op jit(solution)/shard_map/ppermute | solution.py:24
  180.9 2.6 %fusion.19 = bf16[1,16,128,128]{3,2,1,0:T(8,128)(2,1)} fusion(bf16[1,16,128,128]{3,2,1,0:T(8,128)(2,1)S(1)} %collective-permute-done.33, bf16[1,16,128,128]{3,2,1,0:T(8,128)(2,1)S(1)} %collective-permute-done.35, bf16[1,16,128,128]{3,2,1,0:T(8,128)(2,1)} %collective-permute-done.36, bf16[1,16,128,128]{3,2,1,0:T(8,128)(2,1)} %collective-permute-done.34, ...), kind=kLoop, calls=%fused_computation.31 | loop fusion | flops 2621440 | bytes 3145729 | tf_op jit(solution)/shard_map/convert_element_type | solution.py:156
  183.5 1.3 collective-permute-start.37
  185.4 3.8 %copy.21 = bf16[128,16,2,128]{3,2,1,0:T(2,128)(2,1)} copy(bf16[128,16,2,128]{0,2,3,1:T(2,128)(2,1)S(1)} %bitcast.37) | data formatting | bytes 2097152 | tf_op jit(solution)/shard_map/transpose | solution.py:200
  189.2 1.6 fusion.21
  190.8 1.1 copy.22
  192.0 7.3 %collective-permute-done.37 = bf16[1,16,128,128]{3,2,1,0:T(8,128)(2,1)} collective-permute-done((bf16[1,16,128,128]{3,2,1,0:T(8,128)(2,1)}, bf16[1,16,128,128]{3,2,1,0:T(8,128)(2,1)}, u32[]{:S(2)}, u32[]{:S(2)}) %collective-permute-start.37) | collective-permute-done | bytes 524320 | tf_op jit(solution)/shard_map/ppermute | solution.py:20
  199.2 1.4 fusion.20
  200.6 1.1 copy.23
  (82 shorter events, 2.7 us)
Async XLA Ops:
  2.6 17.6 %collective-permute-start.9 = (bf16[1,16,128,128]{3,2,1,0:T(8,128)(2,1)}, bf16[1,16,128,128]{3,2,1,0:T(8,128)(2,1)}, u32[]{:S(2)}, u32[]{:S(2)}) collective-permute-start(bf16[1,16,128,128]{3,2,1,0:T(8,128)(2,1)} %bitcast.34.refs_6_), channel_id=1, source_target_pairs={{0,8},{2,10},{4,12},{6,14},{8,16},{10,18},{12,20},{14,22},{16,24},... | collective-permute-start | bytes 1572872 | tf_op jit(solution)/shard_map/ppermute | solution.py:20
  10.3 21.1 %collective-permute-start.1 = (bf16[1,16,128,128]{3,2,1,0:T(8,128)(2,1)}, bf16[1,16,128,128]{3,2,1,0:T(8,128)(2,1)}, u32[]{:S(2)}, u32[]{:S(2)}) collective-permute-start(bf16[1,16,128,128]{3,2,1,0:T(8,128)(2,1)} %bitcast.35.refs_1_), channel_id=1, source_target_pairs={{0,8},{2,10},{4,12},{6,14},{8,16},{10,18},{12,20},{14,22},{16,24},... | collective-permute-start | bytes 1572872 | tf_op jit(solution)/shard_map/ppermute | solution.py:20
  13.8 22.8 %collective-permute-start.8 = (bf16[1,16,128,128]{3,2,1,0:T(8,128)(2,1)}, bf16[1,16,128,128]{3,2,1,0:T(8,128)(2,1)S(1)}, u32[]{:S(2)}, u32[]{:S(2)}) collective-permute-start(bf16[1,16,128,128]{3,2,1,0:T(8,128)(2,1)} %bitcast.34.refs_6_), channel_id=1, source_target_pairs={{0,4},{2,6},{8,12},{10,14},{16,20},{18,22},{24,28},{26,30},{1,5},{... | collective-permute-start | bytes 1572872 | tf_op jit(solution)/shard_map/ppermute | solution.py:29
  20.1 22.5 %collective-permute-start.13 = (bf16[1,16,128,128]{3,2,1,0:T(8,128)(2,1)}, bf16[1,16,128,128]{3,2,1,0:T(8,128)(2,1)}, u32[]{:S(2)}, u32[]{:S(2)}) collective-permute-start(bf16[1,16,128,128]{3,2,1,0:T(8,128)(2,1)} %collective-permute-done.9.refs_7_), channel_id=1, source_target_pairs={{0,8},{2,10},{4,12},{6,14},{8,16},{10,18},{12,20},{14,22},{16,24},... | collective-permute-start | bytes 1572872 | tf_op jit(solution)/shard_map/ppermute | solution.py:20
  25.4 20.7 %collective-permute-start.10 = (bf16[1,16,128,128]{3,2,1,0:T(8,128)(2,1)}, bf16[1,16,128,128]{3,2,1,0:T(8,128)(2,1)S(1)}, u32[]{:S(2)}, u32[]{:S(2)}) collective-permute-start(bf16[1,16,128,128]{3,2,1,0:T(8,128)(2,1)} %collective-permute-done.9.refs_7_), channel_id=1, source_target_pairs={{4,0},{6,2},{12,8},{14,10},{20,16},{22,18},{28,24},{30,26},{5,1},{... | collective-permute-start | bytes 1572872 | tf_op jit(solution)/shard_map/ppermute | solution.py:29
  26.7 21.7 %collective-permute-start = (bf16[1,16,128,128]{3,2,1,0:T(8,128)(2,1)}, bf16[1,16,128,128]{3,2,1,0:T(8,128)(2,1)S(1)}, u32[]{:S(2)}, u32[]{:S(2)}) collective-permute-start(bf16[1,16,128,128]{3,2,1,0:T(8,128)(2,1)} %bitcast.35.refs_1_), channel_id=1, source_target_pairs={{0,4},{2,6},{8,12},{10,14},{16,20},{18,22},{24,28},{26,30},{1,5},{... | collective-permute-start | bytes 1572872 | tf_op jit(solution)/shard_map/ppermute | solution.py:29
  31.4 21.7 %collective-permute-start.5 = (bf16[1,16,128,128]{3,2,1,0:T(8,128)(2,1)}, bf16[1,16,128,128]{3,2,1,0:T(8,128)(2,1)}, u32[]{:S(2)}, u32[]{:S(2)}) collective-permute-start(bf16[1,16,128,128]{3,2,1,0:T(8,128)(2,1)} %collective-permute-done.1.refs_2_), channel_id=1, source_target_pairs={{0,8},{2,10},{4,12},{6,14},{8,16},{10,18},{12,20},{14,22},{16,24},... | collective-permute-start | bytes 1572872 | tf_op jit(solution)/shard_map/ppermute | solution.py:20
  36.6 16.6 %collective-permute-start.2 = (bf16[1,16,128,128]{3,2,1,0:T(8,128)(2,1)}, bf16[1,16,128,128]{3,2,1,0:T(8,128)(2,1)S(1)}, u32[]{:S(2)}, u32[]{:S(2)}) collective-permute-start(bf16[1,16,128,128]{3,2,1,0:T(8,128)(2,1)} %collective-permute-done.1.refs_2_), channel_id=1, source_target_pairs={{4,0},{6,2},{12,8},{14,10},{20,16},{22,18},{28,24},{30,26},{5,1},{... | collective-permute-start | bytes 1572872 | tf_op jit(solution)/shard_map/ppermute | solution.py:29
  42.6 16.1 %collective-permute-start.12 = (bf16[1,16,128,128]{3,2,1,0:T(8,128)(2,1)}, bf16[1,16,128,128]{3,2,1,0:T(8,128)(2,1)S(1)}, u32[]{:S(2)}, u32[]{:S(2)}) collective-permute-start(bf16[1,16,128,128]{3,2,1,0:T(8,128)(2,1)} %collective-permute-done.9.refs_7_), channel_id=1, source_target_pairs={{0,4},{2,6},{8,12},{10,14},{16,20},{18,22},{24,28},{26,30},{1,5},{... | collective-permute-start | bytes 1572872 | tf_op jit(solution)/shard_map/ppermute | solution.py:29
  46.1 17.0 %collective-permute-start.14 = (bf16[1,16,128,128]{3,2,1,0:T(8,128)(2,1)}, bf16[1,16,128,128]{3,2,1,0:T(8,128)(2,1)S(1)}, u32[]{:S(2)}, u32[]{:S(2)}) collective-permute-start(bf16[1,16,128,128]{3,2,1,0:T(8,128)(2,1)} %collective-permute-done.13.refs_9_), channel_id=1, source_target_pairs={{4,0},{6,2},{12,8},{14,10},{20,16},{22,18},{28,24},{30,26},{5,1},{... | collective-permute-start | bytes 1572872 | tf_op jit(solution)/shard_map/ppermute | solution.py:29
  48.3 29.6 %copy-start = (bf16[128,32,128]{2,1,0:T(8,128)(2,1)S(1)}, bf16[128,32,128]{2,1,0:T(8,128)(2,1)}, u32[]{:S(2)}) copy-start(bf16[128,32,128]{2,1,0:T(8,128)(2,1)} %param.10) | copy-start | bytes 3145732
  48.3 29.6 %copy-start.6 = (bf16[128,32,128]{2,1,0:T(8,128)(2,1)S(1)}, bf16[128,32,128]{2,1,0:T(8,128)(2,1)}, u32[]{:S(2)}) copy-start(bf16[128,32,128]{2,1,0:T(8,128)(2,1)} %param.9) | copy-start | bytes 3145732
  48.3 18.4 %collective-permute-start.4 = (bf16[1,16,128,128]{3,2,1,0:T(8,128)(2,1)}, bf16[1,16,128,128]{3,2,1,0:T(8,128)(2,1)S(1)}, u32[]{:S(2)}, u32[]{:S(2)}) collective-permute-start(bf16[1,16,128,128]{3,2,1,0:T(8,128)(2,1)} %collective-permute-done.1.refs_2_), channel_id=1, source_target_pairs={{0,4},{2,6},{8,12},{10,14},{16,20},{18,22},{24,28},{26,30},{1,5},{... | collective-permute-start | bytes 1572872 | tf_op jit(solution)/shard_map/ppermute | solution.py:29
  53.1 23.5 %collective-permute-start.11 = (bf16[1,16,128,128]{3,2,1,0:T(8,128)(2,1)}, bf16[1,16,128,128]{3,2,1,0:T(8,128)(2,1)}, u32[]{:S(2)}, u32[]{:S(2)}) collective-permute-start(bf16[1,16,128,128]{3,2,1,0:T(8,128)(2,1)} %broadcast_select_fusion.3.refs_4_), channel_id=1, source_target_pairs={{0,2},{2,0},{4,6},{6,4},{8,10},{10,8},{12,14},{14,12},{16,18},{18,... | collective-permute-start | bytes 1572872 | tf_op jit(solution)/shard_map/ppermute | solution.py:24
  53.1 19.4 %collective-permute-start.6 = (bf16[1,16,128,128]{3,2,1,0:T(8,128)(2,1)}, bf16[1,16,128,128]{3,2,1,0:T(8,128)(2,1)S(1)}, u32[]{:S(2)}, u32[]{:S(2)}) collective-permute-start(bf16[1,16,128,128]{3,2,1,0:T(8,128)(2,1)} %collective-permute-done.5.refs_4_), channel_id=1, source_target_pairs={{4,0},{6,2},{12,8},{14,10},{20,16},{22,18},{28,24},{30,26},{5,1},{... | collective-permute-start | bytes 1572872 | tf_op jit(solution)/shard_map/ppermute | solution.py:29
  58.7 19.8 %collective-permute-start.3 = (bf16[1,16,128,128]{3,2,1,0:T(8,128)(2,1)}, bf16[1,16,128,128]{3,2,1,0:T(8,128)(2,1)}, u32[]{:S(2)}, u32[]{:S(2)}) collective-permute-start(bf16[1,16,128,128]{3,2,1,0:T(8,128)(2,1)} %broadcast_select_fusion.5.refs_0_), channel_id=1, source_target_pairs={{0,2},{2,0},{4,6},{6,4},{8,10},{10,8},{12,14},{14,12},{16,18},{18,... | collective-permute-start | bytes 1572872 | tf_op jit(solution)/shard_map/ppermute | solution.py:24
  63.9 21.7 %copy-start.7 = (bf16[128,32,128]{2,1,0:T(8,128)(2,1)S(1)}, bf16[128,32,128]{2,1,0:T(8,128)(2,1)}, u32[]{:S(2)}) copy-start(bf16[128,32,128]{2,1,0:T(8,128)(2,1)} %param.6) | copy-start | bytes 3145732
  63.9 18.5 %collective-permute-start.15 = (bf16[1,16,128,128]{3,2,1,0:T(8,128)(2,1)}, bf16[1,16,128,128]{3,2,1,0:T(8,128)(2,1)}, u32[]{:S(2)}, u32[]{:S(2)}) collective-permute-start(bf16[1,16,128,128]{3,2,1,0:T(8,128)(2,1)} %broadcast_select_fusion.2.refs_6_), channel_id=1, source_target_pairs={{0,2},{2,0},{4,6},{6,4},{8,10},{10,8},{12,14},{14,12},{16,18},{18,... | collective-permute-start | bytes 1572872 | tf_op jit(solution)/shard_map/ppermute | solution.py:24
  73.4 15.0 %collective-permute-start.7 = (bf16[1,16,128,128]{3,2,1,0:T(8,128)(2,1)}, bf16[1,16,128,128]{3,2,1,0:T(8,128)(2,1)}, u32[]{:S(2)}, u32[]{:S(2)}) collective-permute-start(bf16[1,16,128,128]{3,2,1,0:T(8,128)(2,1)} %broadcast_select_fusion.4.refs_2_), channel_id=1, source_target_pairs={{0,2},{2,0},{4,6},{6,4},{8,10},{10,8},{12,14},{14,12},{16,18},{18,... | collective-permute-start | bytes 1572872 | tf_op jit(solution)/shard_map/ppermute | solution.py:24
  73.4 32.0 %collective-permute-start.24 = (bf16[1,16,128,128]{3,2,1,0:T(8,128)(2,1)}, bf16[1,16,128,128]{3,2,1,0:T(8,128)(2,1)}, u32[]{:S(2)}, u32[]{:S(2)}) collective-permute-start(bf16[1,16,128,128]{3,2,1,0:T(8,128)(2,1)} %bitcast.34.refs_6_), channel_id=1, source_target_pairs={{0,2},{4,6},{8,10},{12,14},{16,18},{20,22},{24,26},{28,30},{1,3},{... | collective-permute-start | bytes 1572872 | tf_op jit(solution)/shard_map/ppermute | solution.py:29
  76.6 28.9 %collective-permute-start.25 = (bf16[1,16,128,128]{3,2,1,0:T(8,128)(2,1)}, bf16[1,16,128,128]{3,2,1,0:T(8,128)(2,1)}, u32[]{:S(2)}, u32[]{:S(2)}) collective-permute-start(bf16[1,16,128,128]{3,2,1,0:T(8,128)(2,1)} %collective-permute-done.13.refs_9_), channel_id=1, source_target_pairs={{2,0},{6,4},{10,8},{14,12},{18,16},{22,20},{26,24},{30,28},{3,1},{... | collective-permute-start | bytes 1572872 | tf_op jit(solution)/shard_map/ppermute | solution.py:29
  78.5 29.4 %collective-permute-start.21 = (bf16[1,16,128,128]{3,2,1,0:T(8,128)(2,1)}, bf16[1,16,128,128]{3,2,1,0:T(8,128)(2,1)S(1)}, u32[]{:S(2)}, u32[]{:S(2)}) collective-permute-start(bf16[1,16,128,128]{3,2,1,0:T(8,128)(2,1)} %bitcast.35.refs_1_), channel_id=1, source_target_pairs={{0,2},{4,6},{8,10},{12,14},{16,18},{20,22},{24,26},{28,30},{1,3},{... | collective-permute-start | bytes 1572872 | tf_op jit(solution)/shard_map/ppermute | solution.py:29
  82.4 25.6 %collective-permute-start.22 = (bf16[1,16,128,128]{3,2,1,0:T(8,128)(2,1)}, bf16[1,16,128,128]{3,2,1,0:T(8,128)(2,1)S(1)}, u32[]{:S(2)}, u32[]{:S(2)}) collective-permute-start(bf16[1,16,128,128]{3,2,1,0:T(8,128)(2,1)} %collective-permute-done.5.refs_4_), channel_id=1, source_target_pairs={{2,0},{6,4},{10,8},{14,12},{18,16},{22,20},{26,24},{30,28},{3,1},{... | collective-permute-start | bytes 1572872 | tf_op jit(solution)/shard_map/ppermute | solution.py:29
  88.4 24.1 %collective-permute-start.23 = (bf16[1,16,128,128]{3,2,1,0:T(8,128)(2,1)}, bf16[1,16,128,128]{3,2,1,0:T(8,128)(2,1)S(1)}, u32[]{:S(2)}, u32[]{:S(2)}) collective-permute-start(bf16[1,16,128,128]{3,2,1,0:T(8,128)(2,1)} %collective-permute-done.9.refs_7_), channel_id=1, source_target_pairs={{0,2},{2,0},{4,6},{6,4},{8,10},{10,8},{12,14},{14,12},{16,18},{18,... | collective-permute-start | bytes 1572872 | tf_op jit(solution)/shard_map/ppermute | solution.py:24
  105.3 3.5 %copy-start.18 = (bf16[1,16,128,128]{3,2,1,0:T(8,128)(2,1)S(1)}, bf16[1,16,128,128]{3,2,1,0:T(8,128)(2,1)}, u32[]{:S(2)}) copy-start(bf16[1,16,128,128]{3,2,1,0:T(8,128)(2,1)} %get-tuple-element.33) | copy-start | bytes 1572868
  105.3 3.9 %copy-start.17 = (bf16[1,16,128,128]{3,2,1,0:T(8,128)(2,1)S(1)}, bf16[1,16,128,128]{3,2,1,0:T(8,128)(2,1)}, u32[]{:S(2)}) copy-start(bf16[1,16,128,128]{3,2,1,0:T(8,128)(2,1)} %get-tuple-element.35) | copy-start | bytes 1572868
  105.4 4.0 %copy-start.12 = (bf16[1,16,128,128]{3,2,1,0:T(8,128)(2,1)S(1)}, bf16[1,16,128,128]{3,2,1,0:T(8,128)(2,1)}, u32[]{:S(2)}) copy-start(bf16[1,16,128,128]{3,2,1,0:T(8,128)(2,1)} %get-tuple-element.28) | copy-start | bytes 1572868
  105.4 7.1 %collective-permute-start.20 = (bf16[1,16,128,128]{3,2,1,0:T(8,128)(2,1)}, bf16[1,16,128,128]{3,2,1,0:T(8,128)(2,1)S(1)}, u32[]{:S(2)}, u32[]{:S(2)}) collective-permute-start(bf16[1,16,128,128]{3,2,1,0:T(8,128)(2,1)} %collective-permute-done.1.refs_2_), channel_id=1, source_target_pairs={{0,2},{2,0},{4,6},{6,4},{8,10},{10,8},{12,14},{14,12},{16,18},{18,... | collective-permute-start | bytes 1572872 | tf_op jit(solution)/shard_map/ppermute | solution.py:24
  105.5 4.9 %copy-start.11 = (bf16[1,16,128,128]{3,2,1,0:T(8,128)(2,1)S(1)}, bf16[1,16,128,128]{3,2,1,0:T(8,128)(2,1)}, u32[]{:S(2)}) copy-start(bf16[1,16,128,128]{3,2,1,0:T(8,128)(2,1)} %get-tuple-element.30) | copy-start | bytes 1572868
  105.5 3.8 %collective-permute-start.16 = (bf16[1,16,128,128]{3,2,1,0:T(8,128)(2,1)}, bf16[1,16,128,128]{3,2,1,0:T(8,128)(2,1)S(1)}, u32[]{:S(2)}, u32[]{:S(2)}) collective-permute-start(bf16[1,16,128,128]{3,2,1,0:T(8,128)(2,1)} %get-tuple-element.29), channel_id=1, source_target_pairs={{0,2},{2,0},{4,6},{6,4},{8,10},{10,8},{12,14},{14,12},{16,18},{18,... | collective-permute-start | bytes 1572872 | tf_op jit(solution)/shard_map/ppermute | solution.py:24
  107.9 3.4 %copy-start.10 = (bf16[1,16,128,128]{3,2,1,0:T(8,128)(2,1)S(1)}, bf16[1,16,128,128]{3,2,1,0:T(8,128)(2,1)}, u32[]{:S(2)}) copy-start(bf16[1,16,128,128]{3,2,1,0:T(8,128)(2,1)} %get-tuple-element.32) | copy-start | bytes 1572868
  107.9 2.4 %collective-permute-start.17 = (bf16[1,16,128,128]{3,2,1,0:T(8,128)(2,1)}, bf16[1,16,128,128]{3,2,1,0:T(8,128)(2,1)S(1)}, u32[]{:S(2)}, u32[]{:S(2)}) collective-permute-start(bf16[1,16,128,128]{3,2,1,0:T(8,128)(2,1)} %get-tuple-element.31), channel_id=1, source_target_pairs={{0,2},{2,0},{4,6},{6,4},{8,10},{10,8},{12,14},{14,12},{16,18},{18,... | collective-permute-start | bytes 1572872 | tf_op jit(solution)/shard_map/ppermute | solution.py:24
  108.9 2.5 %collective-permute-start.18 = (bf16[1,16,128,128]{3,2,1,0:T(8,128)(2,1)S(1)}, bf16[1,16,128,128]{3,2,1,0:T(8,128)(2,1)S(1)}, u32[]{:S(2)}, u32[]{:S(2)}) collective-permute-start(bf16[1,16,128,128]{3,2,1,0:T(8,128)(2,1)S(1)} %copy-done.18), channel_id=1, source_target_pairs={{0,2},{2,0},{4,6},{6,4},{8,10},{10,8},{12,14},{14,12},{16,18},{18,... | collective-permute-start | bytes 1572872 | tf_op jit(solution)/shard_map/ppermute | solution.py:24
  109.3 3.1 %collective-permute-start.19 = (bf16[1,16,128,128]{3,2,1,0:T(8,128)(2,1)S(1)}, bf16[1,16,128,128]{3,2,1,0:T(8,128)(2,1)S(1)}, u32[]{:S(2)}, u32[]{:S(2)}) collective-permute-start(bf16[1,16,128,128]{3,2,1,0:T(8,128)(2,1)S(1)} %copy-done.17), channel_id=1, source_target_pairs={{0,2},{2,0},{4,6},{6,4},{8,10},{10,8},{12,14},{14,12},{16,18},{18,... | collective-permute-start | bytes 1572872 | tf_op jit(solution)/shard_map/ppermute | solution.py:24
  109.4 3.0 %copy-start.9 = (bf16[1,16,128,128]{3,2,1,0:T(8,128)(2,1)S(1)}, bf16[1,16,128,128]{3,2,1,0:T(8,128)(2,1)}, u32[]{:S(2)}) copy-start(bf16[1,16,128,128]{3,2,1,0:T(8,128)(2,1)} %get-tuple-element.34) | copy-start | bytes 1572868
  112.5 0.8 copy-start.15
  112.5 0.9 copy-start.16
  132.6 2.7 %collective-permute-start.26 = (bf16[1,16,128,128]{3,2,1,0:T(8,128)(2,1)}, bf16[1,16,128,128]{3,2,1,0:T(8,128)(2,1)S(1)}, u32[]{:S(2)}, u32[]{:S(2)}) collective-permute-start(bf16[1,16,128,128]{3,2,1,0:T(8,128)(2,1)} %get-tuple-element.40), channel_id=1, source_target_pairs={{0,2},{2,0},{4,6},{6,4},{8,10},{10,8},{12,14},{14,12},{16,18},{18,... | collective-permute-start | bytes 1572872 | tf_op jit(solution)/shard_map/ppermute | solution.py:24
  133.0 15.0 %collective-permute-start.29 = (bf16[1,16,128,128]{3,2,1,0:T(8,128)(2,1)}, bf16[1,16,128,128]{3,2,1,0:T(8,128)(2,1)S(1)}, u32[]{:S(2)}, u32[]{:S(2)}) collective-permute-start(bf16[1,16,128,128]{3,2,1,0:T(8,128)(2,1)} %add_convert_fusion.2), channel_id=1, source_target_pairs={{0,4},{2,6},{4,0},{6,2},{8,12},{10,14},{12,8},{14,10},{16,20},{18,... | collective-permute-start | bytes 1572872 | tf_op jit(solution)/shard_map/ppermute | solution.py:24
  133.0 18.6 %collective-permute-start.32 = (bf16[1,16,128,128]{3,2,1,0:T(8,128)(2,1)}, bf16[1,16,128,128]{3,2,1,0:T(8,128)(2,1)S(1)}, u32[]{:S(2)}, u32[]{:S(2)}) collective-permute-start(bf16[1,16,128,128]{3,2,1,0:T(8,128)(2,1)} %get-tuple-element.47), channel_id=1, source_target_pairs={{0,2},{2,0},{4,6},{6,4},{8,10},{10,8},{12,14},{14,12},{16,18},{18,... | collective-permute-start | bytes 1572872 | tf_op jit(solution)/shard_map/ppermute | solution.py:24
  133.2 26.1 %collective-permute-start.35 = (bf16[1,16,128,128]{3,2,1,0:T(8,128)(2,1)S(1)}, bf16[1,16,128,128]{3,2,1,0:T(8,128)(2,1)S(1)}, u32[]{:S(2)}, u32[]{:S(2)}) collective-permute-start(bf16[1,16,128,128]{3,2,1,0:T(8,128)(2,1)S(1)} %add_convert_fusion), channel_id=1, source_target_pairs={{0,4},{2,6},{4,0},{6,2},{8,12},{10,14},{12,8},{14,10},{16,20},{18,... | collective-permute-start | bytes 1572872 | tf_op jit(solution)/shard_map/ppermute | solution.py:24
  135.1 24.2 %copy-start.14 = (bf16[1,16,128,128]{3,2,1,0:T(8,128)(2,1)S(1)}, bf16[1,16,128,128]{3,2,1,0:T(8,128)(2,1)}, u32[]{:S(2)}) copy-start(bf16[1,16,128,128]{3,2,1,0:T(8,128)(2,1)} %get-tuple-element.52) | copy-start | bytes 1572868
  135.1 25.3 %collective-permute-start.28 = (bf16[1,16,128,128]{3,2,1,0:T(8,128)(2,1)}, bf16[1,16,128,128]{3,2,1,0:T(8,128)(2,1)}, u32[]{:S(2)}, u32[]{:S(2)}) collective-permute-start(bf16[1,16,128,128]{3,2,1,0:T(8,128)(2,1)} %get-tuple-element.43), channel_id=1, source_target_pairs={{0,2},{2,0},{4,6},{6,4},{8,10},{10,8},{12,14},{14,12},{16,18},{18,... | collective-permute-start | bytes 1572872 | tf_op jit(solution)/shard_map/ppermute | solution.py:24
  135.3 35.2 %collective-permute-start.27 = (bf16[1,16,128,128]{3,2,1,0:T(8,128)(2,1)}, bf16[1,16,128,128]{3,2,1,0:T(8,128)(2,1)S(1)}, u32[]{:S(2)}, u32[]{:S(2)}) collective-permute-start(bf16[1,16,128,128]{3,2,1,0:T(8,128)(2,1)} %add_convert_fusion.3), channel_id=1, source_target_pairs={{0,4},{2,6},{4,0},{6,2},{8,12},{10,14},{12,8},{14,10},{16,20},{18,... | collective-permute-start | bytes 1572872 | tf_op jit(solution)/shard_map/ppermute | solution.py:24
  150.1 20.4 %collective-permute-start.30 = (bf16[1,16,128,128]{3,2,1,0:T(8,128)(2,1)}, bf16[1,16,128,128]{3,2,1,0:T(8,128)(2,1)}, u32[]{:S(2)}, u32[]{:S(2)}) collective-permute-start(bf16[1,16,128,128]{3,2,1,0:T(8,128)(2,1)} %fusion.6), channel_id=1, source_target_pairs={{8,0},{10,2},{12,4},{14,6},{16,8},{18,10},{20,12},{22,14},{24,16},... | collective-permute-start | bytes 1572872 | tf_op jit(solution)/shard_map/ppermute | solution.py:20
  151.6 23.1 %collective-permute-start.34 = (bf16[1,16,128,128]{3,2,1,0:T(8,128)(2,1)}, bf16[1,16,128,128]{3,2,1,0:T(8,128)(2,1)}, u32[]{:S(2)}, u32[]{:S(2)}) collective-permute-start(bf16[1,16,128,128]{3,2,1,0:T(8,128)(2,1)} %get-tuple-element.50), channel_id=1, source_target_pairs={{0,2},{2,0},{4,6},{6,4},{8,10},{10,8},{12,14},{14,12},{16,18},{18,... | collective-permute-start | bytes 1572872 | tf_op jit(solution)/shard_map/ppermute | solution.py:24
  159.3 21.6 %collective-permute-start.33 = (bf16[1,16,128,128]{3,2,1,0:T(8,128)(2,1)}, bf16[1,16,128,128]{3,2,1,0:T(8,128)(2,1)S(1)}, u32[]{:S(2)}, u32[]{:S(2)}) collective-permute-start(bf16[1,16,128,128]{3,2,1,0:T(8,128)(2,1)} %add_convert_fusion.1), channel_id=1, source_target_pairs={{0,4},{2,6},{4,0},{6,2},{8,12},{10,14},{12,8},{14,10},{16,20},{18,... | collective-permute-start | bytes 1572872 | tf_op jit(solution)/shard_map/ppermute | solution.py:24
  160.3 20.6 %collective-permute-start.36 = (bf16[1,16,128,128]{3,2,1,0:T(8,128)(2,1)}, bf16[1,16,128,128]{3,2,1,0:T(8,128)(2,1)}, u32[]{:S(2)}, u32[]{:S(2)}) collective-permute-start(bf16[1,16,128,128]{3,2,1,0:T(8,128)(2,1)} %fusion.16), channel_id=1, source_target_pairs={{8,0},{10,2},{12,4},{14,6},{16,8},{18,10},{20,12},{22,14},{24,16},... | collective-permute-start | bytes 1572872 | tf_op jit(solution)/shard_map/ppermute | solution.py:20
  161.6 19.3 %copy-start.13 = (bf16[1,16,128,128]{3,2,1,0:T(8,128)(2,1)S(1)}, bf16[1,16,128,128]{3,2,1,0:T(8,128)(2,1)}, u32[]{:S(2)}) copy-start(bf16[1,16,128,128]{3,2,1,0:T(8,128)(2,1)} %get-tuple-element.49) | copy-start | bytes 1572868
  170.5 13.0 %copy-start.2 = (bf16[1,16,128,128]{3,2,1,0:T(8,128)(2,1)}, bf16[1,16,128,128]{3,2,1,0:T(8,128)(2,1)S(1)}, u32[]{:S(2)}) copy-start(bf16[1,16,128,128]{3,2,1,0:T(8,128)(2,1)S(1)} %collective-permute-done.27) | copy-start | bytes 1572868
  173.3 11.6 %copy-start.1 = (f32[16,128,256]{2,1,0:T(8,128)S(1)}, f32[16,128,256]{2,1,0:T(8,128)}, u32[]{:S(2)}) copy-start(f32[16,128,256]{2,1,0:T(8,128)} %get-tuple-element.38) | copy-start | bytes 6291460
  173.3 15.9 %collective-permute-start.31 = (bf16[1,16,128,128]{3,2,1,0:T(8,128)(2,1)}, bf16[1,16,128,128]{3,2,1,0:T(8,128)(2,1)}, u32[]{:S(2)}, u32[]{:S(2)}) collective-permute-start(bf16[1,16,128,128]{3,2,1,0:T(8,128)(2,1)} %fusion.9), channel_id=1, source_target_pairs={{8,0},{10,2},{12,4},{14,6},{16,8},{18,10},{20,12},{22,14},{24,16},... | collective-permute-start | bytes 1572872 | tf_op jit(solution)/shard_map/ppermute | solution.py:20
  180.9 3.9 %copy-start.4 = (bf16[1,16,128,128]{3,2,1,0:T(8,128)(2,1)}, bf16[1,16,128,128]{3,2,1,0:T(8,128)(2,1)S(1)}, u32[]{:S(2)}) copy-start(bf16[1,16,128,128]{3,2,1,0:T(8,128)(2,1)S(1)} %collective-permute-done.33) | copy-start | bytes 1572868
  183.5 15.7 %collective-permute-start.37 = (bf16[1,16,128,128]{3,2,1,0:T(8,128)(2,1)}, bf16[1,16,128,128]{3,2,1,0:T(8,128)(2,1)}, u32[]{:S(2)}, u32[]{:S(2)}) collective-permute-start(bf16[1,16,128,128]{3,2,1,0:T(8,128)(2,1)} %fusion.19), channel_id=1, source_target_pairs={{8,0},{10,2},{12,4},{14,6},{16,8},{18,10},{20,12},{22,14},{24,16},... | collective-permute-start | bytes 1572872 | tf_op jit(solution)/shard_map/ppermute | solution.py:20
  185.4 3.8 %copy-start.3 = (bf16[1,16,128,128]{3,2,1,0:T(8,128)(2,1)S(1)}, bf16[1,16,128,128]{3,2,1,0:T(8,128)(2,1)}, u32[]{:S(2)}) copy-start(bf16[1,16,128,128]{3,2,1,0:T(8,128)(2,1)} %copy-done.2) | copy-start | bytes 1572868
  189.2 10.1 %copy-start.5 = (bf16[1,16,128,128]{3,2,1,0:T(8,128)(2,1)S(1)}, bf16[1,16,128,128]{3,2,1,0:T(8,128)(2,1)}, u32[]{:S(2)}) copy-start(bf16[1,16,128,128]{3,2,1,0:T(8,128)(2,1)} %copy-done.4) | copy-start | bytes 1572868
  189.2 10.1 %copy-start.8 = (bf16[1,16,128,128]{3,2,1,0:T(8,128)(2,1)S(1)}, bf16[1,16,128,128]{3,2,1,0:T(8,128)(2,1)}, u32[]{:S(2)}) copy-start(bf16[1,16,128,128]{3,2,1,0:T(8,128)(2,1)} %get-tuple-element.46) | copy-start | bytes 1572868

commit v12 on v10

--- a/solution.py
+++ b/solution.py
@@ -87,20 +87,21 @@
     tspec = pl.BlockSpec((gb, width, grp * tok), lambda i, v: (i, 0, 0))
     rspec = pl.BlockSpec((gb, 1, grp * tok), lambda i, v: (i, 0, 0))
     kvspec = pl.BlockSpec((1, gb, tok, width), lambda i, v: (0, i, 0, 0))
+    kvspecs = [pl.BlockSpec((1, gb, tok, width), lambda i, v, s=s: (s, i, 0, 0)) for _, s in kvs]
     accs = [] if acc is None else [acc]
     out_shape = [jax.ShapeDtypeStruct((nh, width, grp * tok), jnp.float32)]
-    out_shape += [jax.ShapeDtypeStruct(kv.shape, jnp.bfloat16) for kv in kvs]
+    out_shape += [jax.ShapeDtypeStruct((1,) + kv.shape[1:], jnp.bfloat16) for kv, _ in kvs]
     grid_spec = pltpu.PrefetchScalarGridSpec(
         num_scalar_prefetch=1,
         grid=(nh // gb,),
-        in_specs=[hspec, hspec, rspec, rspec] + [tspec] * len(accs) + [kvspec] * (2 * nb),
+        in_specs=[hspec, hspec, rspec, rspec] + [tspec] * len(accs) + kvspecs,
         out_specs=[tspec] + [kvspec] * (2 * nb),
     )
     scores = nh * grp * tok * tok * nb
     cost = pl.CostEstimate(
         flops=10 * scores * width,
         transcendentals=scores,
-        bytes_accessed=(2 + 2 * len(accs)) * q4.size * 2 + 2 * sum(kv.size for kv in kvs) * 2,
+        bytes_accessed=(2 + 2 * len(accs)) * q4.size * 2 + 2 * sum(kv.size // kv.shape[0] for kv, _ in kvs) * 2,
     )
     outs = pl.pallas_call(
         functools.partial(_blocks_kernel, tuple(modes), acc is not None),
@@ -108,26 +109,32 @@
         out_shape=out_shape,
         cost_estimate=cost,
         compiler_params=pltpu.CompilerParams(dimension_semantics=("arbitrary",)),
-    )(valid, q4, do4, lse3, delta3, *accs, *kvs)
+    )(valid, q4, do4, lse3, delta3, *accs, *[kv for kv, _ in kvs])
     return outs[0], list(outs[1:])
 
 
-def route(x0, n, half, core):
-    x1 = shift(x0, n, PLANE)
-    ya = one_way(x0, n, 2, 0)
-    cx1 = swap(x1, n, 1)
-    yb = one_way(x1, n, 2, 2)
-    x2 = shift(x1, n, PLANE)
-    ca = one_way(x0, n, 1, 0)
-    cb = one_way(x2, n, 1, 1)
-    yc = one_way(x1, n, 2, 0)
-    yd = one_way(x2, n, 2, 2)
-    y0 = jnp.where(half == 1, ya, yb)
-    d0 = swap(y0, n, 1)
+def route(k0, v0, n, half, core):
+    def both(a, b):
+        return jnp.concatenate([a, b], axis=0)
+
+    x0 = (k0, v0)
+    x1 = tuple(shift(x, n, PLANE) for x in x0)
+    ya = tuple(one_way(x, n, 2, 0) for x in x0)
+    cx1 = swap(both(*x1), n, 1)
+    yb = tuple(one_way(x, n, 2, 2) for x in x1)
+    x2 = tuple(shift(x, n, PLANE) for x in x1)
+    ca = one_way(both(*x0), n, 1, 0)
+    cb = one_way(both(*x2), n, 1, 1)
+    yc = tuple(one_way(x, n, 2, 0) for x in x1)
+    yd = tuple(one_way(x, n, 2, 2) for x in x2)
+    y0 = tuple(jnp.where(half == 1, a, b) for a, b in zip(ya, yb))
+    d0 = swap(both(*y0), n, 1)
     cxo = jnp.where(core == 1, ca, cb)
-    y1 = jnp.where(half == 1, yc, yd)
-    d1 = swap(y1, n, 1)
-    return [x0, x1, cx1, x2, cxo, y0, d0, y1, d1]
+    y1 = tuple(jnp.where(half == 1, a, b) for a, b in zip(yc, yd))
+    d1 = swap(both(*y1), n, 1)
+    kb = [(x0[0], 0), (x1[0], 0), (cx1, 0), (x2[0], 0), (cxo, 0), (y0[0], 0), (d0, 0), (y1[0], 0), (d1, 0)]
+    vb = [(x0[1], 0), (x1[1], 0), (cx1, 1), (x2[1], 0), (cxo, 1), (y0[1], 0), (d0, 1), (y1[1], 0), (d1, 1)]
+    return kb, vb
 
 
 def gather_y(terms, n):
@@ -172,8 +179,8 @@
     delta = jnp.sum(grad_out.astype(jnp.float32) * out_in.astype(jnp.float32), axis=-1)
     delta3 = delta.T.reshape(heads_kv, 1, groups * tok)
     lse3 = lse.reshape(heads_kv, 1, groups * tok)
-    kb = route(normed_key_rows.transpose(1, 0, 2)[None], n, half, core)
-    vb = route(value_rows.transpose(1, 0, 2)[None], n, half, core)
+    kb, vb = route(normed_key_rows.transpose(1, 0, 2)[None], value_rows.transpose(1, 0, 2)[None],
+                   n, half, core)
 
     late = [3, 4, 5, 6, 7, 8]
     early = [0, 1, 2]

time: 187 us -> 196 us (1.048)
  starting transfers between devices: 60.4 us -> 51.3 us
  other arithmetic: 22.5 us -> 29.9 us
  waiting for transfers between devices: 53 us -> 60.4 us
  local copies, waits for them, and re-layouts: 14.1 us -> 16.8 us
    concatenate x0 -> x5, other arithmetic: none -> 6.8 us  [both(): return jnp.concatenate([a, b], axis=0)]
    ppermute x12 -> x10, starting transfers between devices: 29 us -> 22.6 us  [one_way(): return lax.ppermute(x, 'seq', pairs)]
    ppermute x8, waiting for transfers between devices: 19.2 us -> 24.4 us  [shift(): return lax.ppermute(x, 'seq', pairs)]
    ppermute x12 -> x10, waiting for transfers between devices: 11.9 us -> 15.7 us  [one_way(): return lax.ppermute(x, 'seq', pairs)]
    ppermute x18 -> x15, starting transfers between devices: 7.83 us -> 5.23 us  [swap(): return lax.ppermute(x, 'seq', [(i, i ^ bit) for i in range(n)])]
    ppermute x18 -> x15, waiting for transfers between devices: 21.9 us -> 20.2 us  [swap(): return lax.ppermute(x, 'seq', [(i, i ^ bit) for i in range(n)])]
    unnamed x56 -> x68, local copies, waits for them, and re-layouts: 6.47 us -> 7.88 us
  transfers between devices with their start and end apart: 38 -> 33, of which waited for: 14 -> 11; matrix products, arithmetic and copies ran while one was open for 17% -> 20% of each run, Pallas kernels for 7% -> 7%
where the time goes in v12:
time: 196 us; the launch traced here: 195 us
  waiting for transfers between devices  60.4 us (31%)
  starting transfers between devices  51.3 us (26%)
  Pallas kernels  35.1 us (18%)
  other arithmetic  29.9 us (15%)
  local copies, waits for them, and re-layouts  16.8 us (9%)
    pallas_call x2, Pallas kernels, attend_blocks(): pl.pallas_call(functools.partial(_blocks_kernel, tuple(modes), acc is not...  35.1 us
    ppermute x8, waiting for transfers between devices, shift(): return lax.ppermute(x, 'seq', pairs)  24.4 us
    ppermute x8, starting transfers between devices, shift(): return lax.ppermute(x, 'seq', pairs)  23.5 us
    ppermute x10, starting transfers between devices, one_way(): return lax.ppermute(x, 'seq', pairs)  22.6 us
    ppermute x15, waiting for transfers between devices, swap(): return lax.ppermute(x, 'seq', [(i, i ^ bit) for i in range(n)])  20.2 us
    ppermute x10, waiting for transfers between devices, one_way(): return lax.ppermute(x, 'seq', pairs)  15.7 us
    unnamed x68, local copies, waits for them, and re-layouts  7.88 us
    concatenate x5, other arithmetic, both(): return jnp.concatenate([a, b], axis=0)  6.8 us
  transfers between devices with their start and end apart: 33, of which 11 were waited for; matrix products, arithmetic and copies ran while one was open for 20% of the time, Pallas kernels for 7%

profile of v12, /device:TPU:0, one launch (start us, length us, event | category | flops | bytes accessed | tf_op | source)
XLA Modules:
  0.0 194.7 jit_solution(2314234763475391272)
XLA Ops:
  0.6 1.2 copy.27
  1.8 5.0 %collective-permute-start = (bf16[1,16,128,128]{3,2,1,0:T(8,128)(2,1)S(1)}, bf16[1,16,128,128]{3,2,1,0:T(8,128)(2,1)S(1)}, u32[]{:S(2)}, u32[]{:S(2)}) collective-permute-start(bf16[1,16,128,128]{3,2,1,0:T(8,128)(2,1)S(1)} %bitcast.36), channel_id=1, source_target_pairs={{0,8},{2,10},{4,12},{6,14},{8,16},{10,18},{12,20},{14,22},{16,24},... | collective-permute-start | bytes 1572872 | tf_op jit(solution)/shard_map/ppermute | solution.py:20
  6.8 1.2 copy.26
  8.0 3.5 %collective-permute-start.3 = (bf16[1,16,128,128]{3,2,1,0:T(8,128)(2,1)S(1)}, bf16[1,16,128,128]{3,2,1,0:T(8,128)(2,1)S(1)}, u32[]{:S(2)}, u32[]{:S(2)}) collective-permute-start(bf16[1,16,128,128]{3,2,1,0:T(8,128)(2,1)S(1)} %bitcast.40), channel_id=1, source_target_pairs={{0,8},{2,10},{4,12},{6,14},{8,16},{10,18},{12,20},{14,22},{16,24},... | collective-permute-start | bytes 1572872 | tf_op jit(solution)/shard_map/ppermute | solution.py:20
  11.5 3.5 %collective-permute-start.6 = (bf16[1,16,128,128]{3,2,1,0:T(8,128)(2,1)S(1)}, bf16[1,16,128,128]{3,2,1,0:T(8,128)(2,1)S(1)}, u32[]{:S(2)}, u32[]{:S(2)}) collective-permute-start(bf16[1,16,128,128]{3,2,1,0:T(8,128)(2,1)S(1)} %bitcast.37), channel_id=1, source_target_pairs={{0,4},{2,6},{8,12},{10,14},{16,20},{18,22},{24,28},{26,30},{1,5},{... | collective-permute-start | bytes 1572872 | tf_op jit(solution)/shard_map/ppermute | solution.py:29
  14.9 4.1 %collective-permute-done.refs_2_ = bf16[1,16,128,128]{3,2,1,0:T(8,128)(2,1)S(1)} collective-permute-done((bf16[1,16,128,128]{3,2,1,0:T(8,128)(2,1)S(1)}, bf16[1,16,128,128]{3,2,1,0:T(8,128)(2,1)S(1)}, u32[]{:S(2)}, u32[]{:S(2)}) %collective-permute-start) | collective-permute-done | bytes 524320 | tf_op jit(solution)/shard_map/ppermute | solution.py:20
  19.1 1.3 collective-permute-start.7
  20.4 5.4 %collective-permute-start.8 = (bf16[1,16,128,128]{3,2,1,0:T(8,128)(2,1)S(1)}, bf16[1,16,128,128]{3,2,1,0:T(8,128)(2,1)}, u32[]{:S(2)}, u32[]{:S(2)}) collective-permute-start(bf16[1,16,128,128]{3,2,1,0:T(8,128)(2,1)S(1)} %bitcast.41), channel_id=1, source_target_pairs={{0,4},{2,6},{8,12},{10,14},{16,20},{18,22},{24,28},{26,30},{1,5},{... | collective-permute-start | bytes 1572872 | tf_op jit(solution)/shard_map/ppermute | solution.py:29
  25.7 5.2 %collective-permute-start.1 = (bf16[1,16,128,128]{3,2,1,0:T(8,128)(2,1)S(1)}, bf16[1,16,128,128]{3,2,1,0:T(8,128)(2,1)}, u32[]{:S(2)}, u32[]{:S(2)}) collective-permute-start(bf16[1,16,128,128]{3,2,1,0:T(8,128)(2,1)S(1)} %collective-permute-done.refs_2_), channel_id=1, source_target_pairs={{0,8},{2,10},{4,12},{6,14},{8,16},{10,18},{12,20},{14,22},{16,24},... | collective-permute-start | bytes 1572872 | tf_op jit(solution)/shard_map/ppermute | solution.py:20
  30.9 4.6 %collective-permute-start.4 = (bf16[1,16,128,128]{3,2,1,0:T(8,128)(2,1)S(1)}, bf16[1,16,128,128]{3,2,1,0:T(8,128)(2,1)}, u32[]{:S(2)}, u32[]{:S(2)}) collective-permute-start(bf16[1,16,128,128]{3,2,1,0:T(8,128)(2,1)S(1)} %collective-permute-done.3.refs_5_), channel_id=1, source_target_pairs={{0,8},{2,10},{4,12},{6,14},{8,16},{10,18},{12,20},{14,22},{16,24},... | collective-permute-start | bytes 1572872 | tf_op jit(solution)/shard_map/ppermute | solution.py:20
  35.5 0.8 copy-done.25
  36.3 1.3 collective-permute-start.9
  37.7 1.1 pad_maximum_fusion
  38.8 0.8 copy-done.27
  39.5 2.3 %collective-permute-start.2 = (bf16[2,16,128,128]{3,2,1,0:T(8,128)(2,1)}, bf16[2,16,128,128]{3,2,1,0:T(8,128)(2,1)}, u32[]{:S(2)}, u32[]{:S(2)}) collective-permute-start(bf16[2,16,128,128]{3,2,1,0:T(8,128)(2,1)} %pad_maximum_fusion), channel_id=1, source_target_pairs={{0,2},{4,6},{8,10},{12,14},{16,18},{20,22},{24,26},{28,30},{1,3},{... | collective-permute-start | bytes 3145736 | tf_op jit(solution)/shard_map/ppermute | solution.py:29
  41.9 1.1 broadcast_select_fusion.4.refs_2_
  43.0 3.6 %collective-permute-start.11 = (bf16[1,16,128,128]{3,2,1,0:T(8,128)(2,1)S(1)}, bf16[1,16,128,128]{3,2,1,0:T(8,128)(2,1)S(1)}, u32[]{:S(2)}, u32[]{:S(2)}) collective-permute-start(bf16[1,16,128,128]{3,2,1,0:T(8,128)(2,1)S(1)} %collective-permute-done.refs_2_), channel_id=1, source_target_pairs={{0,4},{2,6},{8,12},{10,14},{16,20},{18,22},{24,28},{26,30},{1,5},{... | collective-permute-start | bytes 1572872 | tf_op jit(solution)/shard_map/ppermute | solution.py:29
  46.6 1.3 collective-permute-start.13
  47.9 3.7 %collective-permute-done.4.refs_6_ = bf16[1,16,128,128]{3,2,1,0:T(8,128)(2,1)} collective-permute-done((bf16[1,16,128,128]{3,2,1,0:T(8,128)(2,1)S(1)}, bf16[1,16,128,128]{3,2,1,0:T(8,128)(2,1)}, u32[]{:S(2)}, u32[]{:S(2)}) %collective-permute-start.4) | collective-permute-done | bytes 524320 | tf_op jit(solution)/shard_map/ppermute | solution.py:20
  51.6 1.3 collective-permute-start.12
  52.9 0.8 copy-done.24
  53.7 1.3 collective-permute-start.14
  55.0 1.1 broadcast_select_fusion.3.refs_8_
  56.1 1.2 pad_maximum_fusion.2
  57.4 2.3 %pad_maximum_fusion.1 = bf16[2,16,128,128]{3,2,1,0:T(8,128)(2,1)} fusion(bf16[1,16,128,128]{3,2,1,0:T(8,128)(2,1)} %collective-permute-done.4.refs_6_, bf16[1,16,128,128]{3,2,1,0:T(8,128)(2,1)} %collective-permute-done.1.refs_0_), kind=kLoop, calls=%fused_computation.33 | loop fusion | flops 524288 | bytes 2097152 | tf_op jit(solution)/shard_map/concatenate | solution.py:118
  59.6 1.5 collective-permute-start.5
  61.1 7.5 %collective-permute-done.12 = bf16[1,16,128,128]{3,2,1,0:T(8,128)(2,1)S(1)} collective-permute-done((bf16[1,16,128,128]{3,2,1,0:T(8,128)(2,1)}, bf16[1,16,128,128]{3,2,1,0:T(8,128)(2,1)S(1)}, u32[]{:S(2)}, u32[]{:S(2)}) %collective-permute-start.12) | collective-permute-done | bytes 524320 | tf_op jit(solution)/shard_map/ppermute | solution.py:29
  68.7 8.2 %collective-permute-done.14 = bf16[1,16,128,128]{3,2,1,0:T(8,128)(2,1)S(1)} collective-permute-done((bf16[1,16,128,128]{3,2,1,0:T(8,128)(2,1)}, bf16[1,16,128,128]{3,2,1,0:T(8,128)(2,1)S(1)}, u32[]{:S(2)}, u32[]{:S(2)}) %collective-permute-start.14) | collective-permute-done | bytes 524320 | tf_op jit(solution)/shard_map/ppermute | solution.py:29
  77.0 1.2 pad_maximum_fusion.3
  78.8 2.7 %copy.16 = bf16[32,128,128]{2,1,0:T(8,128)(2,1)} copy(bf16[32,128,128]{2,0,1:T(8,128)(2,1)} %bitcast.50) | data formatting | bytes 2097152 | tf_op jit(solution)/shard_map/transpose | solution.py:177
  81.5 1.4 copy.17
  83.0 0.6 multiply_reduce_fusion
  83.6 0.7 copy.18
  84.3 2.3 %broadcast_select_fusion.refs_1_.refs_7_ = bf16[2,16,128,128]{3,2,1,0:T(8,128)(2,1)} fusion(bf16[2,16,128,128]{3,2,1,0:T(8,128)(2,1)} %collective-permute-done.2, bf16[2,16,128,128]{3,2,1,0:T(8,128)(2,1)} %collective-permute-done.5, pred[]{:T(512)S(6)} %eq.11), kind=kLoop, calls=%fused_computation.41 | loop fusion | flops 524288 | bytes 3145729 | tf_op jit(solution)/shard_map/jit(_where)/select_n | solution.py:132
  86.6 22.2 %shard_map.85 = (f32[16,128,256]{2,1,0:T(8,128)}, bf16[1,16,128,128]{3,2,1,0:T(8,128)(2,1)}, bf16[1,16,128,128]{3,2,1,0:T(8,128)(2,1)}, bf16[1,16,128,128]{3,2,1...) custom-call(s32[6]{0:T(128)} %stack.58.valid_ref, ...), custom_call_target="tpu_custom_call" | custom-call | flops 4026531840 | bytes 14680064 | tf_op jit(solution)/shard_map/pallas_call | solution.py:106
  109.5 1.1 pad_maximum_fusion.4
  111.6 1.0 add_convert_fusion.3
  112.6 0.9 add_convert_fusion.2
  113.5 1.2 collective-permute-done.18
  114.8 0.9 add_convert_fusion.1
  115.7 1.0 add_convert_fusion
  116.9 1.8 collective-permute-start.30
  119.5 0.8 copy-done.2
  120.3 12.9 %shard_map.86 = (f32[16,128,256]{2,1,0:T(8,128)}, bf16[1,16,128,128]{3,2,1,0:T(8,128)(2,1)}, bf16[1,16,128,128]{3,2,1,0:T(8,128)(2,1)}, bf16[1,16,128,128]{3,2,1...) custom-call(s32[3]{0:T(128)} %add_convert_fusion.4.valid_ref, ...), custom_call_target="tpu_custom_call" | custom-call | flops 2013265920 | bytes 10485760 | tf_op jit(solution)/shard_map/pallas_call | solution.py:106
  133.5 2.3 %fusion.6 = bf16[1,16,128,128]{3,2,1,0:T(8,128)(2,1)} fusion(bf16[1,16,128,128]{3,2,1,0:T(8,128)(2,1)S(1)} %collective-permute-done.21, bf16[1,16,128,128]{3,2,1,0:T(8,128)(2,1)S(1)} %collective-permute-done.24, bf16[1,16,128,128]{3,2,1,0:T(8,128)(2,1)} %get-tuple-element.45, pred[]{:T(512)S(6)} %eq.11, pred[]{:T(512)S(6)} %eq.25), kind=kLoop, calls=%fused_computation.18 | loop fusion | flops 2097152 | bytes 2097154 | tf_op jit(solution)/shard_map/convert_element_type | solution.py:161
  135.8 1.3 collective-permute-start.25
  137.2 1.0 collective-permute-start.28
  138.1 4.8 %collective-permute-done.30 = bf16[1,16,128,128]{3,2,1,0:T(8,128)(2,1)} collective-permute-done((bf16[1,16,128,128]{3,2,1,0:T(8,128)(2,1)}, bf16[1,16,128,128]{3,2,1,0:T(8,128)(2,1)}, u32[]{:S(2)}, u32[]{:S(2)}) %collective-permute-start.30) | collective-permute-done | bytes 524320 | tf_op jit(solution)/shard_map/ppermute | solution.py:24
  143.0 2.1 %fusion.16 = bf16[1,16,128,128]{3,2,1,0:T(8,128)(2,1)} fusion(bf16[1,16,128,128]{3,2,1,0:T(8,128)(2,1)S(1)} %collective-permute-done.27, bf16[1,16,128,128]{3,2,1,0:T(8,128)(2,1)} %collective-permute-done.30, bf16[1,16,128,128]{3,2,1,0:T(8,128)(2,1)S(1)} %copy-done.28, pred[]{:T(512)S(6)} %eq.11, pred[]{:T(512)S(6)} %eq.25), kind=kLoop, calls=%fused_computation.28 | loop fusion | flops 2097152 | bytes 2097154 | tf_op jit(solution)/shard_map/convert_element_type | solution.py:161
  145.1 9.0 %collective-permute-done.22 = bf16[1,16,128,128]{3,2,1,0:T(8,128)(2,1)S(1)} collective-permute-done((bf16[1,16,128,128]{3,2,1,0:T(8,128)(2,1)}, bf16[1,16,128,128]{3,2,1,0:T(8,128)(2,1)S(1)}, u32[]{:S(2)}, u32[]{:S(2)}) %collective-permute-start.22) | collective-permute-done | bytes 524320 | tf_op jit(solution)/shard_map/ppermute | solution.py:24
  154.1 1.3 collective-permute-start.31
  155.4 2.6 %fusion.9 = bf16[1,16,128,128]{3,2,1,0:T(8,128)(2,1)} fusion(bf16[1,16,128,128]{3,2,1,0:T(8,128)(2,1)S(1)} %collective-permute-done.22, bf16[1,16,128,128]{3,2,1,0:T(8,128)(2,1)S(1)} %copy-done.16, bf16[1,16,128,128]{3,2,1,0:T(8,128)(2,1)} %collective-permute-done.25, bf16[1,16,128,128]{3,2,1,0:T(8,128)(2,1)} %collective-permute-done.23, ...), kind=kLoop, calls=%fused_computation.21 | loop fusion | flops 2621440 | bytes 3145729 | tf_op jit(solution)/shard_map/convert_element_type | solution.py:163
  158.1 1.4 collective-permute-start.26
  159.5 5.2 %collective-permute-done.28 = bf16[1,16,128,128]{3,2,1,0:T(8,128)(2,1)S(1)} collective-permute-done((bf16[1,16,128,128]{3,2,1,0:T(8,128)(2,1)S(1)}, bf16[1,16,128,128]{3,2,1,0:T(8,128)(2,1)S(1)}, u32[]{:S(2)}, u32[]{:S(2)}) %collective-permute-start.28) | collective-permute-done | bytes 524320 | tf_op jit(solution)/shard_map/ppermute | solution.py:24
  164.7 7.0 %collective-permute-done.31 = bf16[1,16,128,128]{3,2,1,0:T(8,128)(2,1)} collective-permute-done((bf16[1,16,128,128]{3,2,1,0:T(8,128)(2,1)}, bf16[1,16,128,128]{3,2,1,0:T(8,128)(2,1)}, u32[]{:S(2)}, u32[]{:S(2)}) %collective-permute-start.31) | collective-permute-done | bytes 524320 | tf_op jit(solution)/shard_map/ppermute | solution.py:20
  171.7 2.6 %fusion.19 = bf16[1,16,128,128]{3,2,1,0:T(8,128)(2,1)} fusion(bf16[1,16,128,128]{3,2,1,0:T(8,128)(2,1)S(1)} %collective-permute-done.28, bf16[1,16,128,128]{3,2,1,0:T(8,128)(2,1)} %collective-permute-done.30, bf16[1,16,128,128]{3,2,1,0:T(8,128)(2,1)} %collective-permute-done.31, bf16[1,16,128,128]{3,2,1,0:T(8,128)(2,1)} %collective-permute-done.29, ...), kind=kLoop, calls=%fused_computation.31 | loop fusion | flops 2621440 | bytes 3145729 | tf_op jit(solution)/shard_map/convert_element_type | solution.py:163
  174.3 1.3 collective-permute-start.32
  176.2 3.8 %copy.21 = bf16[128,16,2,128]{3,2,1,0:T(2,128)(2,1)} copy(bf16[128,16,2,128]{0,2,3,1:T(2,128)(2,1)S(1)} %bitcast.49) | data formatting | bytes 2097152 | tf_op jit(solution)/shard_map/transpose | solution.py:207
  179.9 3.0 %collective-permute-done.26 = bf16[1,16,128,128]{3,2,1,0:T(8,128)(2,1)} collective-permute-done((bf16[1,16,128,128]{3,2,1,0:T(8,128)(2,1)}, bf16[1,16,128,128]{3,2,1,0:T(8,128)(2,1)}, u32[]{:S(2)}, u32[]{:S(2)}) %collective-permute-start.26) | collective-permute-done | bytes 524320 | tf_op jit(solution)/shard_map/ppermute | solution.py:20
  182.9 1.6 fusion.21
  184.5 1.1 copy.22
  185.6 6.5 %collective-permute-done.32 = bf16[1,16,128,128]{3,2,1,0:T(8,128)(2,1)} collective-permute-done((bf16[1,16,128,128]{3,2,1,0:T(8,128)(2,1)}, bf16[1,16,128,128]{3,2,1,0:T(8,128)(2,1)}, u32[]{:S(2)}, u32[]{:S(2)}) %collective-permute-start.32) | collective-permute-done | bytes 524320 | tf_op jit(solution)/shard_map/ppermute | solution.py:20
  192.2 1.4 fusion.20
  193.6 1.1 copy.23
  (102 shorter events, 4.6 us)
Async XLA Ops:
  1.8 41.2 %copy-start = (bf16[128,16,128]{2,0,1:T(8,128)(2,1)}, bf16[128,16,128]{2,0,1:T(8,128)(2,1)S(1)}, u32[]{:S(2)}) copy-start(bf16[128,16,128]{2,0,1:T(8,128)(2,1)S(1)} %copy.27) | copy-start | bytes 1572868
  1.8 17.2 %collective-permute-start = (bf16[1,16,128,128]{3,2,1,0:T(8,128)(2,1)S(1)}, bf16[1,16,128,128]{3,2,1,0:T(8,128)(2,1)S(1)}, u32[]{:S(2)}, u32[]{:S(2)}) collective-permute-start(bf16[1,16,128,128]{3,2,1,0:T(8,128)(2,1)S(1)} %bitcast.36), channel_id=1, source_target_pairs={{0,8},{2,10},{4,12},{6,14},{8,16},{10,18},{12,20},{14,22},{16,24},... | collective-permute-start | bytes 1572872 | tf_op jit(solution)/shard_map/ppermute | solution.py:20
  8.0 48.2 %copy-start.1 = (bf16[128,16,128]{2,0,1:T(8,128)(2,1)}, bf16[128,16,128]{2,0,1:T(8,128)(2,1)S(1)}, u32[]{:S(2)}) copy-start(bf16[128,16,128]{2,0,1:T(8,128)(2,1)S(1)} %copy.26) | copy-start | bytes 1572868
  8.0 23.0 %collective-permute-start.3 = (bf16[1,16,128,128]{3,2,1,0:T(8,128)(2,1)S(1)}, bf16[1,16,128,128]{3,2,1,0:T(8,128)(2,1)S(1)}, u32[]{:S(2)}, u32[]{:S(2)}) collective-permute-start(bf16[1,16,128,128]{3,2,1,0:T(8,128)(2,1)S(1)} %bitcast.40), channel_id=1, source_target_pairs={{0,8},{2,10},{4,12},{6,14},{8,16},{10,18},{12,20},{14,22},{16,24},... | collective-permute-start | bytes 1572872 | tf_op jit(solution)/shard_map/ppermute | solution.py:20
  11.5 24.0 %collective-permute-start.6 = (bf16[1,16,128,128]{3,2,1,0:T(8,128)(2,1)S(1)}, bf16[1,16,128,128]{3,2,1,0:T(8,128)(2,1)S(1)}, u32[]{:S(2)}, u32[]{:S(2)}) collective-permute-start(bf16[1,16,128,128]{3,2,1,0:T(8,128)(2,1)S(1)} %bitcast.37), channel_id=1, source_target_pairs={{0,4},{2,6},{8,12},{10,14},{16,20},{18,22},{24,28},{26,30},{1,5},{... | collective-permute-start | bytes 1572872 | tf_op jit(solution)/shard_map/ppermute | solution.py:29
  19.1 90.4 %copy-start.5 = (bf16[1,16,128,128]{3,2,1,0:T(8,128)(2,1)}, bf16[1,16,128,128]{3,2,1,0:T(8,128)(2,1)S(1)}, u32[]{:S(2)}) copy-start(bf16[1,16,128,128]{3,2,1,0:T(8,128)(2,1)S(1)} %collective-permute-done.refs_2_) | copy-start | bytes 1572868
  19.1 19.7 %collective-permute-start.7 = (bf16[1,16,128,128]{3,2,1,0:T(8,128)(2,1)S(1)}, bf16[1,16,128,128]{3,2,1,0:T(8,128)(2,1)S(1)}, u32[]{:S(2)}, u32[]{:S(2)}) collective-permute-start(bf16[1,16,128,128]{3,2,1,0:T(8,128)(2,1)S(1)} %collective-permute-done.refs_2_), channel_id=1, source_target_pairs={{4,0},{6,2},{12,8},{14,10},{20,16},{22,18},{28,24},{30,26},{5,1},{... | collective-permute-start | bytes 1572872 | tf_op jit(solution)/shard_map/ppermute | solution.py:29
  20.4 22.6 %collective-permute-start.8 = (bf16[1,16,128,128]{3,2,1,0:T(8,128)(2,1)S(1)}, bf16[1,16,128,128]{3,2,1,0:T(8,128)(2,1)}, u32[]{:S(2)}, u32[]{:S(2)}) collective-permute-start(bf16[1,16,128,128]{3,2,1,0:T(8,128)(2,1)S(1)} %bitcast.41), channel_id=1, source_target_pairs={{0,4},{2,6},{8,12},{10,14},{16,20},{18,22},{24,28},{26,30},{1,5},{... | collective-permute-start | bytes 1572872 | tf_op jit(solution)/shard_map/ppermute | solution.py:29
  25.7 20.9 %collective-permute-start.1 = (bf16[1,16,128,128]{3,2,1,0:T(8,128)(2,1)S(1)}, bf16[1,16,128,128]{3,2,1,0:T(8,128)(2,1)}, u32[]{:S(2)}, u32[]{:S(2)}) collective-permute-start(bf16[1,16,128,128]{3,2,1,0:T(8,128)(2,1)S(1)} %collective-permute-done.refs_2_), channel_id=1, source_target_pairs={{0,8},{2,10},{4,12},{6,14},{8,16},{10,18},{12,20},{14,22},{16,24},... | collective-permute-start | bytes 1572872 | tf_op jit(solution)/shard_map/ppermute | solution.py:20
  30.9 78.6 %copy-start.6 = (bf16[1,16,128,128]{3,2,1,0:T(8,128)(2,1)}, bf16[1,16,128,128]{3,2,1,0:T(8,128)(2,1)S(1)}, u32[]{:S(2)}) copy-start(bf16[1,16,128,128]{3,2,1,0:T(8,128)(2,1)S(1)} %collective-permute-done.3.refs_5_) | copy-start | bytes 1572868
  30.9 20.7 %collective-permute-start.4 = (bf16[1,16,128,128]{3,2,1,0:T(8,128)(2,1)S(1)}, bf16[1,16,128,128]{3,2,1,0:T(8,128)(2,1)}, u32[]{:S(2)}, u32[]{:S(2)}) collective-permute-start(bf16[1,16,128,128]{3,2,1,0:T(8,128)(2,1)S(1)} %collective-permute-done.3.refs_5_), channel_id=1, source_target_pairs={{0,8},{2,10},{4,12},{6,14},{8,16},{10,18},{12,20},{14,22},{16,24},... | collective-permute-start | bytes 1572872 | tf_op jit(solution)/shard_map/ppermute | solution.py:20
  35.5 0.8 copy-start.25
  36.3 16.6 %collective-permute-start.9 = (bf16[1,16,128,128]{3,2,1,0:T(8,128)(2,1)S(1)}, bf16[1,16,128,128]{3,2,1,0:T(8,128)(2,1)S(1)}, u32[]{:S(2)}, u32[]{:S(2)}) collective-permute-start(bf16[1,16,128,128]{3,2,1,0:T(8,128)(2,1)S(1)} %collective-permute-done.3.refs_5_), channel_id=1, source_target_pairs={{4,0},{6,2},{12,8},{14,10},{20,16},{22,18},{28,24},{30,26},{5,1},{... | collective-permute-start | bytes 1572872 | tf_op jit(solution)/shard_map/ppermute | solution.py:29
  37.6 4.2 %copy-start.26 = (bf16[1,16,128,128]{3,2,1,0:T(8,128)(2,1)S(1)}, bf16[1,16,128,128]{3,2,1,0:T(8,128)(2,1)}, u32[]{:S(2)}) copy-start(bf16[1,16,128,128]{3,2,1,0:T(8,128)(2,1)} %copy-done.25) | copy-start | bytes 1572868
  39.5 44.7 %collective-permute-start.2 = (bf16[2,16,128,128]{3,2,1,0:T(8,128)(2,1)}, bf16[2,16,128,128]{3,2,1,0:T(8,128)(2,1)}, u32[]{:S(2)}, u32[]{:S(2)}) collective-permute-start(bf16[2,16,128,128]{3,2,1,0:T(8,128)(2,1)} %pad_maximum_fusion), channel_id=1, source_target_pairs={{0,2},{4,6},{8,10},{12,14},{16,18},{20,22},{24,26},{28,30},{1,3},{... | collective-permute-start | bytes 3145736 | tf_op jit(solution)/shard_map/ppermute | solution.py:29
  43.0 16.6 %copy-start.11 = (bf16[1,16,128,128]{3,2,1,0:T(8,128)(2,1)}, bf16[1,16,128,128]{3,2,1,0:T(8,128)(2,1)S(1)}, u32[]{:S(2)}) copy-start(bf16[1,16,128,128]{3,2,1,0:T(8,128)(2,1)S(1)} %broadcast_select_fusion.4.refs_2_) | copy-start | bytes 1572868
  43.0 16.6 %collective-permute-start.11 = (bf16[1,16,128,128]{3,2,1,0:T(8,128)(2,1)S(1)}, bf16[1,16,128,128]{3,2,1,0:T(8,128)(2,1)S(1)}, u32[]{:S(2)}, u32[]{:S(2)}) collective-permute-start(bf16[1,16,128,128]{3,2,1,0:T(8,128)(2,1)S(1)} %collective-permute-done.refs_2_), channel_id=1, source_target_pairs={{0,4},{2,6},{8,12},{10,14},{16,20},{18,22},{24,28},{26,30},{1,5},{... | collective-permute-start | bytes 1572872 | tf_op jit(solution)/shard_map/ppermute | solution.py:29
  46.6 22.1 %collective-permute-start.13 = (bf16[1,16,128,128]{3,2,1,0:T(8,128)(2,1)S(1)}, bf16[1,16,128,128]{3,2,1,0:T(8,128)(2,1)S(1)}, u32[]{:S(2)}, u32[]{:S(2)}) collective-permute-start(bf16[1,16,128,128]{3,2,1,0:T(8,128)(2,1)S(1)} %collective-permute-done.3.refs_5_), channel_id=1, source_target_pairs={{0,4},{2,6},{8,12},{10,14},{16,20},{18,22},{24,28},{26,30},{1,5},{... | collective-permute-start | bytes 1572872 | tf_op jit(solution)/shard_map/ppermute | solution.py:29
  51.6 17.0 %collective-permute-start.12 = (bf16[1,16,128,128]{3,2,1,0:T(8,128)(2,1)}, bf16[1,16,128,128]{3,2,1,0:T(8,128)(2,1)S(1)}, u32[]{:S(2)}, u32[]{:S(2)}) collective-permute-start(bf16[1,16,128,128]{3,2,1,0:T(8,128)(2,1)} %collective-permute-done.1.refs_0_), channel_id=1, source_target_pairs={{4,0},{6,2},{12,8},{14,10},{20,16},{22,18},{28,24},{30,26},{5,1},{... | collective-permute-start | bytes 1572872 | tf_op jit(solution)/shard_map/ppermute | solution.py:29
  52.9 0.8 copy-start.24
  53.7 23.2 %collective-permute-start.14 = (bf16[1,16,128,128]{3,2,1,0:T(8,128)(2,1)}, bf16[1,16,128,128]{3,2,1,0:T(8,128)(2,1)S(1)}, u32[]{:S(2)}, u32[]{:S(2)}) collective-permute-start(bf16[1,16,128,128]{3,2,1,0:T(8,128)(2,1)} %collective-permute-done.4.refs_6_), channel_id=1, source_target_pairs={{4,0},{6,2},{12,8},{14,10},{20,16},{22,18},{28,24},{30,26},{5,1},{... | collective-permute-start | bytes 1572872 | tf_op jit(solution)/shard_map/ppermute | solution.py:29
  56.1 12.5 %copy-start.12 = (bf16[1,16,128,128]{3,2,1,0:T(8,128)(2,1)}, bf16[1,16,128,128]{3,2,1,0:T(8,128)(2,1)S(1)}, u32[]{:S(2)}) copy-start(bf16[1,16,128,128]{3,2,1,0:T(8,128)(2,1)S(1)} %broadcast_select_fusion.3.refs_8_) | copy-start | bytes 1572868
  59.6 24.7 %collective-permute-start.5 = (bf16[2,16,128,128]{3,2,1,0:T(8,128)(2,1)}, bf16[2,16,128,128]{3,2,1,0:T(8,128)(2,1)}, u32[]{:S(2)}, u32[]{:S(2)}) collective-permute-start(bf16[2,16,128,128]{3,2,1,0:T(8,128)(2,1)} %pad_maximum_fusion.1), channel_id=1, source_target_pairs={{2,0},{6,4},{10,8},{14,12},{18,16},{22,20},{26,24},{30,28},{3,1},{... | collective-permute-start | bytes 3145736 | tf_op jit(solution)/shard_map/ppermute | solution.py:29
  68.6 18.0 %collective-permute-start.10 = (bf16[2,16,128,128]{3,2,1,0:T(8,128)(2,1)}, bf16[2,16,128,128]{3,2,1,0:T(8,128)(2,1)}, u32[]{:S(2)}, u32[]{:S(2)}) collective-permute-start(bf16[2,16,128,128]{3,2,1,0:T(8,128)(2,1)} %pad_maximum_fusion.2), channel_id=1, source_target_pairs={{0,2},{2,0},{4,6},{6,4},{8,10},{10,8},{12,14},{14,12},{16,18},{18,... | collective-permute-start | bytes 3145736 | tf_op jit(solution)/shard_map/ppermute | solution.py:24
  68.7 12.9 %copy-start.13 = (bf16[1,16,128,128]{3,2,1,0:T(8,128)(2,1)}, bf16[1,16,128,128]{3,2,1,0:T(8,128)(2,1)S(1)}, u32[]{:S(2)}) copy-start(bf16[1,16,128,128]{3,2,1,0:T(8,128)(2,1)S(1)} %broadcast_select_fusion.2.refs_4_) | copy-start | bytes 1572868
  77.0 4.6 %copy-start.14 = (bf16[1,16,128,128]{3,2,1,0:T(8,128)(2,1)}, bf16[1,16,128,128]{3,2,1,0:T(8,128)(2,1)S(1)}, u32[]{:S(2)}) copy-start(bf16[1,16,128,128]{3,2,1,0:T(8,128)(2,1)S(1)} %broadcast_select_fusion.1.refs_10_) | copy-start | bytes 1572868
  77.0 4.6 %copy-start.3 = (bf16[128,32,128]{2,1,0:T(8,128)(2,1)S(1)}, bf16[128,32,128]{2,1,0:T(8,128)(2,1)}, u32[]{:S(2)}) copy-start(bf16[128,32,128]{2,1,0:T(8,128)(2,1)} %param.10) | copy-start | bytes 3145732
  78.1 8.5 %collective-permute-start.15 = (bf16[2,16,128,128]{3,2,1,0:T(8,128)(2,1)}, bf16[2,16,128,128]{3,2,1,0:T(8,128)(2,1)}, u32[]{:S(2)}, u32[]{:S(2)}) collective-permute-start(bf16[2,16,128,128]{3,2,1,0:T(8,128)(2,1)} %pad_maximum_fusion.3), channel_id=1, source_target_pairs={{0,2},{2,0},{4,6},{6,4},{8,10},{10,8},{12,14},{14,12},{16,18},{18,... | collective-permute-start | bytes 3145736 | tf_op jit(solution)/shard_map/ppermute | solution.py:24
  78.8 4.1 %copy-start.17 = (bf16[128,32,128]{2,1,0:T(8,128)(2,1)S(1)}, bf16[128,32,128]{2,1,0:T(8,128)(2,1)}, u32[]{:S(2)}) copy-start(bf16[128,32,128]{2,1,0:T(8,128)(2,1)} %param.9) | copy-start | bytes 3145732
  108.8 2.2 %copy-start.31 = (bf16[1,16,128,128]{3,2,1,0:T(8,128)(2,1)S(1)}, bf16[1,16,128,128]{3,2,1,0:T(8,128)(2,1)}, u32[]{:S(2)}) copy-start(bf16[1,16,128,128]{3,2,1,0:T(8,128)(2,1)} %get-tuple-element.33) | copy-start | bytes 1572868
  108.8 2.3 %copy-start.30 = (bf16[1,16,128,128]{3,2,1,0:T(8,128)(2,1)S(1)}, bf16[1,16,128,128]{3,2,1,0:T(8,128)(2,1)}, u32[]{:S(2)}) copy-start(bf16[1,16,128,128]{3,2,1,0:T(8,128)(2,1)} %get-tuple-element.35) | copy-start | bytes 1572868
  108.8 2.8 %copy-start.23 = (bf16[1,16,128,128]{3,2,1,0:T(8,128)(2,1)S(1)}, bf16[1,16,128,128]{3,2,1,0:T(8,128)(2,1)}, u32[]{:S(2)}) copy-start(bf16[1,16,128,128]{3,2,1,0:T(8,128)(2,1)} %get-tuple-element.28) | copy-start | bytes 1572868
  108.8 3.8 %copy-start.22 = (bf16[1,16,128,128]{3,2,1,0:T(8,128)(2,1)S(1)}, bf16[1,16,128,128]{3,2,1,0:T(8,128)(2,1)}, u32[]{:S(2)}) copy-start(bf16[1,16,128,128]{3,2,1,0:T(8,128)(2,1)} %get-tuple-element.30) | copy-start | bytes 1572868
  108.8 2.7 %collective-permute-start.16 = (bf16[1,16,128,128]{3,2,1,0:T(8,128)(2,1)}, bf16[1,16,128,128]{3,2,1,0:T(8,128)(2,1)S(1)}, u32[]{:S(2)}, u32[]{:S(2)}) collective-permute-start(bf16[1,16,128,128]{3,2,1,0:T(8,128)(2,1)} %get-tuple-element.29), channel_id=1, source_target_pairs={{0,2},{2,0},{4,6},{6,4},{8,10},{10,8},{12,14},{14,12},{16,18},{18,... | collective-permute-start | bytes 1572872 | tf_op jit(solution)/shard_map/ppermute | solution.py:24
  109.4 3.2 %collective-permute-start.17 = (bf16[1,16,128,128]{3,2,1,0:T(8,128)(2,1)}, bf16[1,16,128,128]{3,2,1,0:T(8,128)(2,1)S(1)}, u32[]{:S(2)}, u32[]{:S(2)}) collective-permute-start(bf16[1,16,128,128]{3,2,1,0:T(8,128)(2,1)} %get-tuple-element.31), channel_id=1, source_target_pairs={{0,2},{2,0},{4,6},{6,4},{8,10},{10,8},{12,14},{14,12},{16,18},{18,... | collective-permute-start | bytes 1572872 | tf_op jit(solution)/shard_map/ppermute | solution.py:24
  110.6 4.2 %copy-start.21 = (bf16[1,16,128,128]{3,2,1,0:T(8,128)(2,1)S(1)}, bf16[1,16,128,128]{3,2,1,0:T(8,128)(2,1)}, u32[]{:S(2)}) copy-start(bf16[1,16,128,128]{3,2,1,0:T(8,128)(2,1)} %get-tuple-element.32) | copy-start | bytes 1572868
  110.6 8.7 %collective-permute-start.20 = (bf16[2,16,128,128]{3,2,1,0:T(8,128)(2,1)}, bf16[2,16,128,128]{3,2,1,0:T(8,128)(2,1)S(1)}, u32[]{:S(2)}, u32[]{:S(2)}) collective-permute-start(bf16[2,16,128,128]{3,2,1,0:T(8,128)(2,1)} %pad_maximum_fusion.4), channel_id=1, source_target_pairs={{0,2},{2,0},{4,6},{6,4},{8,10},{10,8},{12,14},{14,12},{16,18},{18,... | collective-permute-start | bytes 3145736 | tf_op jit(solution)/shard_map/ppermute | solution.py:24
  111.0 3.7 %collective-permute-start.18 = (bf16[1,16,128,128]{3,2,1,0:T(8,128)(2,1)S(1)}, bf16[1,16,128,128]{3,2,1,0:T(8,128)(2,1)S(1)}, u32[]{:S(2)}, u32[]{:S(2)}) collective-permute-start(bf16[1,16,128,128]{3,2,1,0:T(8,128)(2,1)S(1)} %copy-done.31), channel_id=1, source_target_pairs={{0,2},{2,0},{4,6},{6,4},{8,10},{10,8},{12,14},{14,12},{16,18},{18,... | collective-permute-start | bytes 1572872 | tf_op jit(solution)/shard_map/ppermute | solution.py:24
  111.1 4.6 %collective-permute-start.19 = (bf16[1,16,128,128]{3,2,1,0:T(8,128)(2,1)S(1)}, bf16[1,16,128,128]{3,2,1,0:T(8,128)(2,1)S(1)}, u32[]{:S(2)}, u32[]{:S(2)}) collective-permute-start(bf16[1,16,128,128]{3,2,1,0:T(8,128)(2,1)S(1)} %copy-done.30), channel_id=1, source_target_pairs={{0,2},{2,0},{4,6},{6,4},{8,10},{10,8},{12,14},{14,12},{16,18},{18,... | collective-permute-start | bytes 1572872 | tf_op jit(solution)/shard_map/ppermute | solution.py:24
  111.5 21.7 %collective-permute-start.21 = (bf16[1,16,128,128]{3,2,1,0:T(8,128)(2,1)}, bf16[1,16,128,128]{3,2,1,0:T(8,128)(2,1)S(1)}, u32[]{:S(2)}, u32[]{:S(2)}) collective-permute-start(bf16[1,16,128,128]{3,2,1,0:T(8,128)(2,1)} %get-tuple-element.40), channel_id=1, source_target_pairs={{0,2},{2,0},{4,6},{6,4},{8,10},{10,8},{12,14},{14,12},{16,18},{18,... | collective-permute-start | bytes 1572872 | tf_op jit(solution)/shard_map/ppermute | solution.py:24
  111.6 4.1 %copy-start.20 = (bf16[1,16,128,128]{3,2,1,0:T(8,128)(2,1)S(1)}, bf16[1,16,128,128]{3,2,1,0:T(8,128)(2,1)}, u32[]{:S(2)}) copy-start(bf16[1,16,128,128]{3,2,1,0:T(8,128)(2,1)} %get-tuple-element.34) | copy-start | bytes 1572868
  116.7 16.8 %collective-permute-start.24 = (bf16[1,16,128,128]{3,2,1,0:T(8,128)(2,1)}, bf16[1,16,128,128]{3,2,1,0:T(8,128)(2,1)S(1)}, u32[]{:S(2)}, u32[]{:S(2)}) collective-permute-start(bf16[1,16,128,128]{3,2,1,0:T(8,128)(2,1)} %add_convert_fusion.2), channel_id=1, source_target_pairs={{0,4},{2,6},{4,0},{6,2},{8,12},{10,14},{12,8},{14,10},{16,20},{18,... | collective-permute-start | bytes 1572872 | tf_op jit(solution)/shard_map/ppermute | solution.py:24
  116.7 20.5 %collective-permute-start.27 = (bf16[1,16,128,128]{3,2,1,0:T(8,128)(2,1)}, bf16[1,16,128,128]{3,2,1,0:T(8,128)(2,1)S(1)}, u32[]{:S(2)}, u32[]{:S(2)}) collective-permute-start(bf16[1,16,128,128]{3,2,1,0:T(8,128)(2,1)} %get-tuple-element.47), channel_id=1, source_target_pairs={{0,2},{2,0},{4,6},{6,4},{8,10},{10,8},{12,14},{14,12},{16,18},{18,... | collective-permute-start | bytes 1572872 | tf_op jit(solution)/shard_map/ppermute | solution.py:24
  116.9 26.1 %collective-permute-start.30 = (bf16[1,16,128,128]{3,2,1,0:T(8,128)(2,1)}, bf16[1,16,128,128]{3,2,1,0:T(8,128)(2,1)}, u32[]{:S(2)}, u32[]{:S(2)}) collective-permute-start(bf16[1,16,128,128]{3,2,1,0:T(8,128)(2,1)} %add_convert_fusion), channel_id=1, source_target_pairs={{0,4},{2,6},{4,0},{6,2},{8,12},{10,14},{12,8},{14,10},{16,20},{18,... | collective-permute-start | bytes 1572872 | tf_op jit(solution)/shard_map/ppermute | solution.py:24
  119.3 1.0 copy-start.2
  119.3 34.8 %collective-permute-start.22 = (bf16[1,16,128,128]{3,2,1,0:T(8,128)(2,1)}, bf16[1,16,128,128]{3,2,1,0:T(8,128)(2,1)S(1)}, u32[]{:S(2)}, u32[]{:S(2)}) collective-permute-start(bf16[1,16,128,128]{3,2,1,0:T(8,128)(2,1)} %add_convert_fusion.3), channel_id=1, source_target_pairs={{0,4},{2,6},{4,0},{6,2},{8,12},{10,14},{12,8},{14,10},{16,20},{18,... | collective-permute-start | bytes 1572872 | tf_op jit(solution)/shard_map/ppermute | solution.py:24
  133.2 4.0 %copy-start.18 = (bf16[1,16,128,128]{3,2,1,0:T(8,128)(2,1)S(1)}, bf16[1,16,128,128]{3,2,1,0:T(8,128)(2,1)}, u32[]{:S(2)}) copy-start(bf16[1,16,128,128]{3,2,1,0:T(8,128)(2,1)} %add_convert_fusion.1) | copy-start | bytes 1572868
  133.2 9.8 %copy-start.28 = (bf16[1,16,128,128]{3,2,1,0:T(8,128)(2,1)S(1)}, bf16[1,16,128,128]{3,2,1,0:T(8,128)(2,1)}, u32[]{:S(2)}) copy-start(bf16[1,16,128,128]{3,2,1,0:T(8,128)(2,1)} %get-tuple-element.52) | copy-start | bytes 1572868
  133.2 22.2 %collective-permute-start.23 = (bf16[1,16,128,128]{3,2,1,0:T(8,128)(2,1)}, bf16[1,16,128,128]{3,2,1,0:T(8,128)(2,1)}, u32[]{:S(2)}, u32[]{:S(2)}) collective-permute-start(bf16[1,16,128,128]{3,2,1,0:T(8,128)(2,1)} %get-tuple-element.43), channel_id=1, source_target_pairs={{0,2},{2,0},{4,6},{6,4},{8,10},{10,8},{12,14},{14,12},{16,18},{18,... | collective-permute-start | bytes 1572872 | tf_op jit(solution)/shard_map/ppermute | solution.py:24
  133.5 3.6 %copy-start.15 = (bf16[1,16,128,128]{3,2,1,0:T(8,128)(2,1)}, bf16[1,16,128,128]{3,2,1,0:T(8,128)(2,1)S(1)}, u32[]{:S(2)}) copy-start(bf16[1,16,128,128]{3,2,1,0:T(8,128)(2,1)S(1)} %collective-permute-done.24) | copy-start | bytes 1572868
  135.8 19.6 %collective-permute-start.25 = (bf16[1,16,128,128]{3,2,1,0:T(8,128)(2,1)}, bf16[1,16,128,128]{3,2,1,0:T(8,128)(2,1)}, u32[]{:S(2)}, u32[]{:S(2)}) collective-permute-start(bf16[1,16,128,128]{3,2,1,0:T(8,128)(2,1)} %fusion.6), channel_id=1, source_target_pairs={{8,0},{10,2},{12,4},{14,6},{16,8},{18,10},{20,12},{22,14},{24,16},... | collective-permute-start | bytes 1572872 | tf_op jit(solution)/shard_map/ppermute | solution.py:20
  137.2 18.3 %copy-start.16 = (bf16[1,16,128,128]{3,2,1,0:T(8,128)(2,1)S(1)}, bf16[1,16,128,128]{3,2,1,0:T(8,128)(2,1)}, u32[]{:S(2)}) copy-start(bf16[1,16,128,128]{3,2,1,0:T(8,128)(2,1)} %copy-done.15) | copy-start | bytes 1572868
  137.2 27.5 %collective-permute-start.28 = (bf16[1,16,128,128]{3,2,1,0:T(8,128)(2,1)S(1)}, bf16[1,16,128,128]{3,2,1,0:T(8,128)(2,1)S(1)}, u32[]{:S(2)}, u32[]{:S(2)}) collective-permute-start(bf16[1,16,128,128]{3,2,1,0:T(8,128)(2,1)S(1)} %copy-done.18), channel_id=1, source_target_pairs={{0,4},{2,6},{4,0},{6,2},{8,12},{10,14},{12,8},{14,10},{16,20},{18,... | collective-permute-start | bytes 1572872 | tf_op jit(solution)/shard_map/ppermute | solution.py:24
  143.0 21.7 %collective-permute-start.29 = (bf16[1,16,128,128]{3,2,1,0:T(8,128)(2,1)}, bf16[1,16,128,128]{3,2,1,0:T(8,128)(2,1)}, u32[]{:S(2)}, u32[]{:S(2)}) collective-permute-start(bf16[1,16,128,128]{3,2,1,0:T(8,128)(2,1)} %get-tuple-element.50), channel_id=1, source_target_pairs={{0,2},{2,0},{4,6},{6,4},{8,10},{10,8},{12,14},{14,12},{16,18},{18,... | collective-permute-start | bytes 1572872 | tf_op jit(solution)/shard_map/ppermute | solution.py:24
  154.1 20.2 %copy-start.7 = (bf16[1,16,128,128]{3,2,1,0:T(8,128)(2,1)}, bf16[1,16,128,128]{3,2,1,0:T(8,128)(2,1)S(1)}, u32[]{:S(2)}) copy-start(bf16[1,16,128,128]{3,2,1,0:T(8,128)(2,1)S(1)} %collective-permute-done.22) | copy-start | bytes 1572868
  154.1 17.6 %collective-permute-start.31 = (bf16[1,16,128,128]{3,2,1,0:T(8,128)(2,1)}, bf16[1,16,128,128]{3,2,1,0:T(8,128)(2,1)}, u32[]{:S(2)}, u32[]{:S(2)}) collective-permute-start(bf16[1,16,128,128]{3,2,1,0:T(8,128)(2,1)} %fusion.16), channel_id=1, source_target_pairs={{8,0},{10,2},{12,4},{14,6},{16,8},{18,10},{20,12},{22,14},{24,16},... | collective-permute-start | bytes 1572872 | tf_op jit(solution)/shard_map/ppermute | solution.py:20
  155.4 16.3 %copy-start.29 = (bf16[1,16,128,128]{3,2,1,0:T(8,128)(2,1)S(1)}, bf16[1,16,128,128]{3,2,1,0:T(8,128)(2,1)}, u32[]{:S(2)}) copy-start(bf16[1,16,128,128]{3,2,1,0:T(8,128)(2,1)} %get-tuple-element.49) | copy-start | bytes 1572868
  158.1 17.5 %copy-start.4 = (f32[16,128,256]{2,1,0:T(8,128)S(1)}, f32[16,128,256]{2,1,0:T(8,128)}, u32[]{:S(2)}) copy-start(f32[16,128,256]{2,1,0:T(8,128)} %get-tuple-element.38) | copy-start | bytes 6291460
  158.1 24.9 %collective-permute-start.26 = (bf16[1,16,128,128]{3,2,1,0:T(8,128)(2,1)}, bf16[1,16,128,128]{3,2,1,0:T(8,128)(2,1)}, u32[]{:S(2)}, u32[]{:S(2)}) collective-permute-start(bf16[1,16,128,128]{3,2,1,0:T(8,128)(2,1)} %fusion.9), channel_id=1, source_target_pairs={{8,0},{10,2},{12,4},{14,6},{16,8},{18,10},{20,12},{22,14},{24,16},... | collective-permute-start | bytes 1572872 | tf_op jit(solution)/shard_map/ppermute | solution.py:20
  164.7 10.9 %copy-start.9 = (bf16[1,16,128,128]{3,2,1,0:T(8,128)(2,1)}, bf16[1,16,128,128]{3,2,1,0:T(8,128)(2,1)S(1)}, u32[]{:S(2)}) copy-start(bf16[1,16,128,128]{3,2,1,0:T(8,128)(2,1)S(1)} %collective-permute-done.28) | copy-start | bytes 1572868
  174.3 17.9 %collective-permute-start.32 = (bf16[1,16,128,128]{3,2,1,0:T(8,128)(2,1)}, bf16[1,16,128,128]{3,2,1,0:T(8,128)(2,1)}, u32[]{:S(2)}, u32[]{:S(2)}) collective-permute-start(bf16[1,16,128,128]{3,2,1,0:T(8,128)(2,1)} %fusion.19), channel_id=1, source_target_pairs={{8,0},{10,2},{12,4},{14,6},{16,8},{18,10},{20,12},{22,14},{24,16},... | collective-permute-start | bytes 1572872 | tf_op jit(solution)/shard_map/ppermute | solution.py:20
  176.2 6.8 %copy-start.8 = (bf16[1,16,128,128]{3,2,1,0:T(8,128)(2,1)S(1)}, bf16[1,16,128,128]{3,2,1,0:T(8,128)(2,1)}, u32[]{:S(2)}) copy-start(bf16[1,16,128,128]{3,2,1,0:T(8,128)(2,1)} %copy-done.7) | copy-start | bytes 1572868
  179.9 12.2 %copy-start.10 = (bf16[1,16,128,128]{3,2,1,0:T(8,128)(2,1)S(1)}, bf16[1,16,128,128]{3,2,1,0:T(8,128)(2,1)}, u32[]{:S(2)}) copy-start(bf16[1,16,128,128]{3,2,1,0:T(8,128)(2,1)} %copy-done.9) | copy-start | bytes 1572868
  179.9 12.2 %copy-start.19 = (bf16[1,16,128,128]{3,2,1,0:T(8,128)(2,1)S(1)}, bf16[1,16,128,128]{3,2,1,0:T(8,128)(2,1)}, u32[]{:S(2)}) copy-start(bf16[1,16,128,128]{3,2,1,0:T(8,128)(2,1)} %get-tuple-element.46) | copy-start | bytes 1572868
  (1 other events, 0.8 us)

commit v13 on v10

--- a/solution.py
+++ b/solution.py
@@ -153,8 +153,8 @@
     part1 = tx1.astype(f32) + r1 + jnp.where(lo, yret1, yret0)
     part1 = part1 + shift(part2.astype(bf16), n, -PLANE).astype(f32)
     part0 = tx0.astype(f32) + jnp.where(core == 0, ro, zero) + jnp.where(lo, yret0, zero)
-    part0 = part0 + shift(part1.astype(bf16), n, -PLANE).astype(f32)
-    return part0.astype(bf16)
+    last = shift(part1.astype(bf16)[0].transpose(1, 0, 2), n, -PLANE)
+    return (part0[0].transpose(1, 0, 2) + last.astype(f32)).astype(bf16)
 
 
 def per_device(query, normed_key_rows, value_rows, out_in, grad_out, lse):
@@ -198,7 +198,7 @@
 
     dq = (acc * SCALE).astype(jnp.bfloat16).reshape(heads_kv, width, groups, tok)
     grad_query = dq.transpose(3, 0, 2, 1).reshape(tok, heads_q, width)
-    return (grad_query, grad_k[0].transpose(1, 0, 2), grad_v[0].transpose(1, 0, 2))
+    return (grad_query, grad_k, grad_v)
 
 
 def solution(mesh):

time: 187 us -> 187 us (level)
    convert_element_type x2, other arithmetic: 5.07 us -> 2.95 us  [unroute(): return (part0[0].transpose(1, 0, 2) + last.astype(f32)).astype(bf16)]
    transpose x2, other arithmetic: 2.95 us -> 5.05 us  [unroute(): last = shift(part1.astype(bf16)[0].transpose(1, 0, 2), n, -PLANE)]
where the time goes in v13:
time: 187 us; the launch traced here: 186 us
  starting transfers between devices  60.4 us (32%)
  waiting for transfers between devices  53 us (28%)
  Pallas kernels  35 us (19%)
  other arithmetic  22.5 us (12%)
  local copies, waits for them, and re-layouts  14.1 us (8%)
    pallas_call x2, Pallas kernels, attend_blocks(): pl.pallas_call(functools.partial(_blocks_kernel, tuple(modes), acc is not...  35 us
    ppermute x12, starting transfers between devices, one_way(): return lax.ppermute(x, 'seq', pairs)  29 us
    ppermute x8, starting transfers between devices, shift(): return lax.ppermute(x, 'seq', pairs)  23.6 us
    ppermute x18, waiting for transfers between devices, swap(): return lax.ppermute(x, 'seq', [(i, i ^ bit) for i in range(n)])  21.9 us
    ppermute x8, waiting for transfers between devices, shift(): return lax.ppermute(x, 'seq', pairs)  19.2 us
    ppermute x12, waiting for transfers between devices, one_way(): return lax.ppermute(x, 'seq', pairs)  11.9 us
    ppermute x18, starting transfers between devices, swap(): return lax.ppermute(x, 'seq', [(i, i ^ bit) for i in range(n)])  7.83 us
    unnamed x56, local copies, waits for them, and re-layouts  6.47 us
  transfers between devices with their start and end apart: 38, of which 14 were waited for; matrix products, arithmetic and copies ran while one was open for 17% of the time, Pallas kernels for 7%

profile of v13, /device:TPU:0, one launch (start us, length us, event | category | flops | bytes accessed | tf_op | source)
XLA Modules:
  0.0 186.2 jit_solution(16128887566623103101)
XLA Ops:
  0.7 1.3 copy.27
  2.0 5.7 %collective-permute-start = (bf16[1,16,128,128]{3,2,1,0:T(8,128)(2,1)S(1)}, bf16[1,16,128,128]{3,2,1,0:T(8,128)(2,1)}, u32[]{:S(2)}, u32[]{:S(2)}) collective-permute-start(bf16[1,16,128,128]{3,2,1,0:T(8,128)(2,1)S(1)} %bitcast.60), channel_id=1, source_target_pairs={{0,8},{2,10},{4,12},{6,14},{8,16},{10,18},{12,20},{14,22},{16,24},... | collective-permute-start | bytes 1572872 | tf_op jit(solution)/shard_map/ppermute | solution.py:20
  7.7 1.2 copy.26
  8.9 3.5 %collective-permute-start.10 = (bf16[1,16,128,128]{3,2,1,0:T(8,128)(2,1)S(1)}, bf16[1,16,128,128]{3,2,1,0:T(8,128)(2,1)}, u32[]{:S(2)}, u32[]{:S(2)}) collective-permute-start(bf16[1,16,128,128]{3,2,1,0:T(8,128)(2,1)S(1)} %bitcast.64), channel_id=1, source_target_pairs={{0,8},{2,10},{4,12},{6,14},{8,16},{10,18},{12,20},{14,22},{16,24},... | collective-permute-start | bytes 1572872 | tf_op jit(solution)/shard_map/ppermute | solution.py:20
  12.4 3.4 %collective-permute-start.4 = (bf16[1,16,128,128]{3,2,1,0:T(8,128)(2,1)S(1)}, bf16[1,16,128,128]{3,2,1,0:T(8,128)(2,1)S(1)}, u32[]{:S(2)}, u32[]{:S(2)}) collective-permute-start(bf16[1,16,128,128]{3,2,1,0:T(8,128)(2,1)S(1)} %bitcast.61), channel_id=1, source_target_pairs={{0,4},{2,6},{8,12},{10,14},{16,20},{18,22},{24,28},{26,30},{1,5},{... | collective-permute-start | bytes 1572872 | tf_op jit(solution)/shard_map/ppermute | solution.py:29
  15.9 3.4 %collective-permute-done.refs_2_ = bf16[1,16,128,128]{3,2,1,0:T(8,128)(2,1)} collective-permute-done((bf16[1,16,128,128]{3,2,1,0:T(8,128)(2,1)S(1)}, bf16[1,16,128,128]{3,2,1,0:T(8,128)(2,1)}, u32[]{:S(2)}, u32[]{:S(2)}) %collective-permute-start) | collective-permute-done | bytes 524320 | tf_op jit(solution)/shard_map/ppermute | solution.py:20
  19.2 5.3 %collective-permute-start.1 = (bf16[1,16,128,128]{3,2,1,0:T(8,128)(2,1)}, bf16[1,16,128,128]{3,2,1,0:T(8,128)(2,1)}, u32[]{:S(2)}, u32[]{:S(2)}) collective-permute-start(bf16[1,16,128,128]{3,2,1,0:T(8,128)(2,1)} %collective-permute-done.refs_2_), channel_id=1, source_target_pairs={{0,8},{2,10},{4,12},{6,14},{8,16},{10,18},{12,20},{14,22},{16,24},... | collective-permute-start | bytes 1572872 | tf_op jit(solution)/shard_map/ppermute | solution.py:20
  24.5 1.3 collective-permute-start.5
  25.8 6.2 %collective-permute-start.14 = (bf16[1,16,128,128]{3,2,1,0:T(8,128)(2,1)S(1)}, bf16[1,16,128,128]{3,2,1,0:T(8,128)(2,1)}, u32[]{:S(2)}, u32[]{:S(2)}) collective-permute-start(bf16[1,16,128,128]{3,2,1,0:T(8,128)(2,1)S(1)} %bitcast.65), channel_id=1, source_target_pairs={{0,4},{2,6},{8,12},{10,14},{16,20},{18,22},{24,28},{26,30},{1,5},{... | collective-permute-start | bytes 1572872 | tf_op jit(solution)/shard_map/ppermute | solution.py:29
  32.0 3.8 %collective-permute-start.11 = (bf16[1,16,128,128]{3,2,1,0:T(8,128)(2,1)}, bf16[1,16,128,128]{3,2,1,0:T(8,128)(2,1)}, u32[]{:S(2)}, u32[]{:S(2)}) collective-permute-start(bf16[1,16,128,128]{3,2,1,0:T(8,128)(2,1)} %collective-permute-done.10.refs_5_), channel_id=1, source_target_pairs={{0,8},{2,10},{4,12},{6,14},{8,16},{10,18},{12,20},{14,22},{16,24},... | collective-permute-start | bytes 1572872 | tf_op jit(solution)/shard_map/ppermute | solution.py:20
  35.8 0.8 copy-done.13
  36.6 1.3 collective-permute-start.15
  38.6 1.4 copy.16
  40.0 1.4 copy.17
  41.4 0.6 multiply_reduce_fusion
  42.0 0.7 copy.18
  42.7 5.3 %collective-permute-start.7 = (bf16[1,16,128,128]{3,2,1,0:T(8,128)(2,1)}, bf16[1,16,128,128]{3,2,1,0:T(8,128)(2,1)S(1)}, u32[]{:S(2)}, u32[]{:S(2)}) collective-permute-start(bf16[1,16,128,128]{3,2,1,0:T(8,128)(2,1)} %collective-permute-done.refs_2_), channel_id=1, source_target_pairs={{0,4},{2,6},{8,12},{10,14},{16,20},{18,22},{24,28},{26,30},{1,5},{... | collective-permute-start | bytes 1572872 | tf_op jit(solution)/shard_map/ppermute | solution.py:29
  48.1 1.3 collective-permute-start.8
  49.4 1.1 broadcast_select_fusion.3.refs_2_
  50.5 1.3 collective-permute-start.2
  51.9 3.5 %collective-permute-start.17 = (bf16[1,16,128,128]{3,2,1,0:T(8,128)(2,1)}, bf16[1,16,128,128]{3,2,1,0:T(8,128)(2,1)S(1)}, u32[]{:S(2)}, u32[]{:S(2)}) collective-permute-start(bf16[1,16,128,128]{3,2,1,0:T(8,128)(2,1)} %collective-permute-done.10.refs_5_), channel_id=1, source_target_pairs={{0,4},{2,6},{8,12},{10,14},{16,20},{18,22},{24,28},{26,30},{1,5},{... | collective-permute-start | bytes 1572872 | tf_op jit(solution)/shard_map/ppermute | solution.py:29
  55.5 1.3 collective-permute-start.18
  56.8 1.1 broadcast_select_fusion.1.refs_8_
  57.9 1.2 collective-permute-done.7
  59.1 1.3 collective-permute-start.12
  60.4 3.3 %collective-permute-done.8 = bf16[1,16,128,128]{3,2,1,0:T(8,128)(2,1)S(1)} collective-permute-done((bf16[1,16,128,128]{3,2,1,0:T(8,128)(2,1)}, bf16[1,16,128,128]{3,2,1,0:T(8,128)(2,1)S(1)}, u32[]{:S(2)}, u32[]{:S(2)}) %collective-permute-start.8) | collective-permute-done | bytes 524320 | tf_op jit(solution)/shard_map/ppermute | solution.py:29
  63.7 1.3 collective-permute-start.3
  65.1 3.1 %collective-permute-done.17 = bf16[1,16,128,128]{3,2,1,0:T(8,128)(2,1)S(1)} collective-permute-done((bf16[1,16,128,128]{3,2,1,0:T(8,128)(2,1)}, bf16[1,16,128,128]{3,2,1,0:T(8,128)(2,1)S(1)}, u32[]{:S(2)}, u32[]{:S(2)}) %collective-permute-start.17) | collective-permute-done | bytes 524320 | tf_op jit(solution)/shard_map/ppermute | solution.py:29
  68.2 4.3 %collective-permute-done.18 = bf16[1,16,128,128]{3,2,1,0:T(8,128)(2,1)S(1)} collective-permute-done((bf16[1,16,128,128]{3,2,1,0:T(8,128)(2,1)}, bf16[1,16,128,128]{3,2,1,0:T(8,128)(2,1)S(1)}, u32[]{:S(2)}, u32[]{:S(2)}) %collective-permute-start.18) | collective-permute-done | bytes 524320 | tf_op jit(solution)/shard_map/ppermute | solution.py:29
  72.5 1.5 collective-permute-start.13
  74.1 1.2 collective-permute-start.16
  75.8 0.8 broadcast_select_fusion.5.refs_1_
  76.7 0.9 broadcast_select_fusion.4.refs_7_
  77.8 0.7 collective-permute-done.19.refs_11_
  78.5 0.8 copy-done.25
  79.4 22.1 %shard_map.85 = (f32[16,128,256]{2,1,0:T(8,128)}, bf16[1,16,128,128]{3,2,1,0:T(8,128)(2,1)}, bf16[1,16,128,128]{3,2,1,0:T(8,128)(2,1)}, bf16[1,16,128,128]{3,2,1...) custom-call(s32[6]{0:T(128)} %stack.58.valid_ref, ...), custom_call_target="tpu_custom_call" | custom-call | flops 4026531840 | bytes 14680064 | tf_op jit(solution)/shard_map/pallas_call | solution.py:105
  102.7 0.9 collective-permute-done.20
  103.8 2.0 %add_convert_fusion.3 = bf16[1,16,128,128]{3,2,1,0:T(8,128)(2,1)} fusion(bf16[1,16,128,128]{3,2,1,0:T(8,128)(2,1)S(1)} %collective-permute-done.20, bf16[1,16,128,128]{3,2,1,0:T(8,128)(2,1)} %get-tuple-element.28), kind=kLoop, calls=%fused_computation.37 | loop fusion | flops 1048576 | bytes 1572864 | tf_op jit(solution)/shard_map/convert_element_type | solution.py:137
  106.2 1.2 add_convert_fusion.2
  107.4 1.0 add_convert_fusion.1
  108.3 1.0 add_convert_fusion
  109.5 1.9 %collective-permute-start.35 = (bf16[1,16,128,128]{3,2,1,0:T(8,128)(2,1)}, bf16[1,16,128,128]{3,2,1,0:T(8,128)(2,1)S(1)}, u32[]{:S(2)}, u32[]{:S(2)}) collective-permute-start(bf16[1,16,128,128]{3,2,1,0:T(8,128)(2,1)} %add_convert_fusion), channel_id=1, source_target_pairs={{0,4},{2,6},{4,0},{6,2},{8,12},{10,14},{12,8},{14,10},{16,20},{18,... | collective-permute-start | bytes 1572872 | tf_op jit(solution)/shard_map/ppermute | solution.py:24
  111.4 0.7 add_convert_fusion.4.valid_ref
  112.2 12.9 %shard_map.86 = (f32[16,128,256]{2,1,0:T(8,128)}, bf16[1,16,128,128]{3,2,1,0:T(8,128)(2,1)}, bf16[1,16,128,128]{3,2,1,0:T(8,128)(2,1)}, bf16[1,16,128,128]{3,2,1...) custom-call(s32[3]{0:T(128)} %add_convert_fusion.4.valid_ref, ...), custom_call_target="tpu_custom_call" | custom-call | flops 2013265920 | bytes 10485760 | tf_op jit(solution)/shard_map/pallas_call | solution.py:105
  125.4 2.1 %fusion.7 = bf16[1,16,128,128]{3,2,1,0:T(8,128)(2,1)} fusion(bf16[1,16,128,128]{3,2,1,0:T(8,128)(2,1)S(1)} %collective-permute-done.26, bf16[1,16,128,128]{3,2,1,0:T(8,128)(2,1)S(1)} %collective-permute-done.29, bf16[1,16,128,128]{3,2,1,0:T(8,128)(2,1)} %get-tuple-element.45, pred[]{:T(512)S(6)} %eq.26, pred[]{:T(512)S(6)} %eq.11), kind=kLoop, calls=%fused_computation.19 | loop fusion | flops 2097152 | bytes 2097154 | tf_op jit(solution)/shard_map/convert_element_type | solution.py:154
  127.5 1.3 collective-permute-start.30
  128.8 1.9 collective-permute-start.33
  130.6 4.7 %collective-permute-done.35 = bf16[1,16,128,128]{3,2,1,0:T(8,128)(2,1)S(1)} collective-permute-done((bf16[1,16,128,128]{3,2,1,0:T(8,128)(2,1)}, bf16[1,16,128,128]{3,2,1,0:T(8,128)(2,1)S(1)}, u32[]{:S(2)}, u32[]{:S(2)}) %collective-permute-start.35) | collective-permute-done | bytes 524320 | tf_op jit(solution)/shard_map/ppermute | solution.py:24
  135.3 1.1 fusion.18
  136.4 10.2 %collective-permute-done.27 = bf16[1,16,128,128]{3,2,1,0:T(8,128)(2,1)S(1)} collective-permute-done((bf16[1,16,128,128]{3,2,1,0:T(8,128)(2,1)}, bf16[1,16,128,128]{3,2,1,0:T(8,128)(2,1)S(1)}, u32[]{:S(2)}, u32[]{:S(2)}) %collective-permute-start.27) | collective-permute-done | bytes 524320 | tf_op jit(solution)/shard_map/ppermute | solution.py:24
  146.5 1.3 collective-permute-start.36
  147.9 2.6 %fusion.23 = bf16[128,16,128]{2,0,1:T(8,128)(2,1)} fusion(bf16[1,16,128,128]{3,2,1,0:T(8,128)(2,1)} %collective-permute-done.30, bf16[1,16,128,128]{3,2,1,0:T(8,128)(2,1)S(1)} %collective-permute-done.27, bf16[1,16,128,128]{3,2,1,0:T(8,128)(2,1)S(1)} %collective-permute-done.29, bf16[1,16,128,128]{3,2,1,0:T(8,128)(2,1)} %collective-permute-done.28, ...), kind=kLoop, calls=%fused_computation.39 | loop fusion | flops 2621440 | bytes 3145729 | tf_op jit(solution)/shard_map/transpose | solution.py:156
  150.5 1.4 collective-permute-start.31
  151.9 5.1 %collective-permute-done.33 = bf16[1,16,128,128]{3,2,1,0:T(8,128)(2,1)S(1)} collective-permute-done((bf16[1,16,128,128]{3,2,1,0:T(8,128)(2,1)}, bf16[1,16,128,128]{3,2,1,0:T(8,128)(2,1)S(1)}, u32[]{:S(2)}, u32[]{:S(2)}) %collective-permute-start.33) | collective-permute-done | bytes 524320 | tf_op jit(solution)/shard_map/ppermute | solution.py:24
  157.0 6.6 %collective-permute-done.36 = bf16[1,16,128,128]{3,2,1,0:T(8,128)(2,1)} collective-permute-done((bf16[1,16,128,128]{3,2,1,0:T(8,128)(2,1)}, bf16[1,16,128,128]{3,2,1,0:T(8,128)(2,1)}, u32[]{:S(2)}, u32[]{:S(2)}) %collective-permute-start.36) | collective-permute-done | bytes 524320 | tf_op jit(solution)/shard_map/ppermute | solution.py:20
  163.6 2.4 %fusion.22 = bf16[128,16,128]{2,0,1:T(8,128)(2,1)} fusion(bf16[1,16,128,128]{3,2,1,0:T(8,128)(2,1)} %collective-permute-done.36, bf16[1,16,128,128]{3,2,1,0:T(8,128)(2,1)S(1)} %collective-permute-done.33, bf16[1,16,128,128]{3,2,1,0:T(8,128)(2,1)S(1)} %collective-permute-done.35, bf16[1,16,128,128]{3,2,1,0:T(8,128)(2,1)} %collective-permute-done.34, ...), kind=kLoop, calls=%fused_computation.38 | loop fusion | flops 2621440 | bytes 3145729 | tf_op jit(solution)/shard_map/transpose | solution.py:156
  166.0 1.3 collective-permute-start.37
  167.9 3.8 %copy.21 = bf16[128,16,2,128]{3,2,1,0:T(2,128)(2,1)} copy(bf16[128,16,2,128]{0,2,3,1:T(2,128)(2,1)S(1)} %bitcast.53) | data formatting | bytes 2097152 | tf_op jit(solution)/shard_map/transpose | solution.py:200
  171.7 3.2 %collective-permute-done.31 = bf16[128,16,128]{2,0,1:T(8,128)(2,1)} collective-permute-done((bf16[128,16,128]{2,0,1:T(8,128)(2,1)}, bf16[128,16,128]{2,0,1:T(8,128)(2,1)}, u32[]{:S(2)}, u32[]{:S(2)}) %collective-permute-start.31) | collective-permute-done | bytes 524320 | tf_op jit(solution)/shard_map/ppermute | solution.py:20
  174.8 1.6 fusion.4
  176.4 1.1 copy.22
  177.5 6.1 %collective-permute-done.37 = bf16[128,16,128]{2,0,1:T(8,128)(2,1)} collective-permute-done((bf16[128,16,128]{2,0,1:T(8,128)(2,1)}, bf16[128,16,128]{2,0,1:T(8,128)(2,1)}, u32[]{:S(2)}, u32[]{:S(2)}) %collective-permute-start.37) | collective-permute-done | bytes 524320 | tf_op jit(solution)/shard_map/ppermute | solution.py:20
  183.6 1.4 fusion.15
  185.0 1.1 copy.23
  (96 shorter events, 4.6 us)
Async XLA Ops:
  0.6 38.0 %copy-start.6 = (bf16[128,32,128]{2,1,0:T(8,128)(2,1)S(1)}, bf16[128,32,128]{2,1,0:T(8,128)(2,1)}, u32[]{:S(2)}) copy-start(bf16[128,32,128]{2,1,0:T(8,128)(2,1)} %param.6) | copy-start | bytes 3145732
  0.6 39.3 %copy-start = (bf16[128,32,128]{2,1,0:T(8,128)(2,1)S(1)}, bf16[128,32,128]{2,1,0:T(8,128)(2,1)}, u32[]{:S(2)}) copy-start(bf16[128,32,128]{2,1,0:T(8,128)(2,1)} %param.10) | copy-start | bytes 3145732
  2.0 48.5 %copy-start.11 = (bf16[128,16,128]{2,0,1:T(8,128)(2,1)}, bf16[128,16,128]{2,0,1:T(8,128)(2,1)S(1)}, u32[]{:S(2)}) copy-start(bf16[128,16,128]{2,0,1:T(8,128)(2,1)S(1)} %copy.27) | copy-start | bytes 1572868
  2.0 17.2 %collective-permute-start = (bf16[1,16,128,128]{3,2,1,0:T(8,128)(2,1)S(1)}, bf16[1,16,128,128]{3,2,1,0:T(8,128)(2,1)}, u32[]{:S(2)}, u32[]{:S(2)}) collective-permute-start(bf16[1,16,128,128]{3,2,1,0:T(8,128)(2,1)S(1)} %bitcast.60), channel_id=1, source_target_pairs={{0,8},{2,10},{4,12},{6,14},{8,16},{10,18},{12,20},{14,22},{16,24},... | collective-permute-start | bytes 1572872 | tf_op jit(solution)/shard_map/ppermute | solution.py:20
  8.9 50.2 %copy-start.12 = (bf16[128,16,128]{2,0,1:T(8,128)(2,1)}, bf16[128,16,128]{2,0,1:T(8,128)(2,1)S(1)}, u32[]{:S(2)}) copy-start(bf16[128,16,128]{2,0,1:T(8,128)(2,1)S(1)} %copy.26) | copy-start | bytes 1572868
  8.9 23.0 %collective-permute-start.10 = (bf16[1,16,128,128]{3,2,1,0:T(8,128)(2,1)S(1)}, bf16[1,16,128,128]{3,2,1,0:T(8,128)(2,1)}, u32[]{:S(2)}, u32[]{:S(2)}) collective-permute-start(bf16[1,16,128,128]{3,2,1,0:T(8,128)(2,1)S(1)} %bitcast.64), channel_id=1, source_target_pairs={{0,8},{2,10},{4,12},{6,14},{8,16},{10,18},{12,20},{14,22},{16,24},... | collective-permute-start | bytes 1572872 | tf_op jit(solution)/shard_map/ppermute | solution.py:20
  12.4 23.3 %collective-permute-start.4 = (bf16[1,16,128,128]{3,2,1,0:T(8,128)(2,1)S(1)}, bf16[1,16,128,128]{3,2,1,0:T(8,128)(2,1)S(1)}, u32[]{:S(2)}, u32[]{:S(2)}) collective-permute-start(bf16[1,16,128,128]{3,2,1,0:T(8,128)(2,1)S(1)} %bitcast.61), channel_id=1, source_target_pairs={{0,4},{2,6},{8,12},{10,14},{16,20},{18,22},{24,28},{26,30},{1,5},{... | collective-permute-start | bytes 1572872 | tf_op jit(solution)/shard_map/ppermute | solution.py:29
  19.2 23.5 %collective-permute-start.1 = (bf16[1,16,128,128]{3,2,1,0:T(8,128)(2,1)}, bf16[1,16,128,128]{3,2,1,0:T(8,128)(2,1)}, u32[]{:S(2)}, u32[]{:S(2)}) collective-permute-start(bf16[1,16,128,128]{3,2,1,0:T(8,128)(2,1)} %collective-permute-done.refs_2_), channel_id=1, source_target_pairs={{0,8},{2,10},{4,12},{6,14},{8,16},{10,18},{12,20},{14,22},{16,24},... | collective-permute-start | bytes 1572872 | tf_op jit(solution)/shard_map/ppermute | solution.py:20
  24.5 23.6 %collective-permute-start.5 = (bf16[1,16,128,128]{3,2,1,0:T(8,128)(2,1)}, bf16[1,16,128,128]{3,2,1,0:T(8,128)(2,1)}, u32[]{:S(2)}, u32[]{:S(2)}) collective-permute-start(bf16[1,16,128,128]{3,2,1,0:T(8,128)(2,1)} %collective-permute-done.refs_2_), channel_id=1, source_target_pairs={{4,0},{6,2},{12,8},{14,10},{20,16},{22,18},{28,24},{30,26},{5,1},{... | collective-permute-start | bytes 1572872 | tf_op jit(solution)/shard_map/ppermute | solution.py:29
  25.8 24.7 %collective-permute-start.14 = (bf16[1,16,128,128]{3,2,1,0:T(8,128)(2,1)S(1)}, bf16[1,16,128,128]{3,2,1,0:T(8,128)(2,1)}, u32[]{:S(2)}, u32[]{:S(2)}) collective-permute-start(bf16[1,16,128,128]{3,2,1,0:T(8,128)(2,1)S(1)} %bitcast.65), channel_id=1, source_target_pairs={{0,4},{2,6},{8,12},{10,14},{16,20},{18,22},{24,28},{26,30},{1,5},{... | collective-permute-start | bytes 1572872 | tf_op jit(solution)/shard_map/ppermute | solution.py:29
  32.0 19.9 %collective-permute-start.11 = (bf16[1,16,128,128]{3,2,1,0:T(8,128)(2,1)}, bf16[1,16,128,128]{3,2,1,0:T(8,128)(2,1)}, u32[]{:S(2)}, u32[]{:S(2)}) collective-permute-start(bf16[1,16,128,128]{3,2,1,0:T(8,128)(2,1)} %collective-permute-done.10.refs_5_), channel_id=1, source_target_pairs={{0,8},{2,10},{4,12},{6,14},{8,16},{10,18},{12,20},{14,22},{16,24},... | collective-permute-start | bytes 1572872 | tf_op jit(solution)/shard_map/ppermute | solution.py:20
  35.8 0.8 copy-start.13
  36.6 18.9 %collective-permute-start.15 = (bf16[1,16,128,128]{3,2,1,0:T(8,128)(2,1)}, bf16[1,16,128,128]{3,2,1,0:T(8,128)(2,1)}, u32[]{:S(2)}, u32[]{:S(2)}) collective-permute-start(bf16[1,16,128,128]{3,2,1,0:T(8,128)(2,1)} %collective-permute-done.10.refs_5_), channel_id=1, source_target_pairs={{4,0},{6,2},{12,8},{14,10},{20,16},{22,18},{28,24},{30,26},{5,1},{... | collective-permute-start | bytes 1572872 | tf_op jit(solution)/shard_map/ppermute | solution.py:29
  38.6 2.8 %copy-start.7 = (bf16[128,32,128]{2,1,0:T(8,128)(2,1)S(1)}, bf16[128,32,128]{2,1,0:T(8,128)(2,1)}, u32[]{:S(2)}) copy-start(bf16[128,32,128]{2,1,0:T(8,128)(2,1)} %param.9) | copy-start | bytes 3145732
  40.0 9.4 %copy-start.14 = (bf16[1,16,128,128]{3,2,1,0:T(8,128)(2,1)S(1)}, bf16[1,16,128,128]{3,2,1,0:T(8,128)(2,1)}, u32[]{:S(2)}) copy-start(bf16[1,16,128,128]{3,2,1,0:T(8,128)(2,1)} %copy-done.13) | copy-start | bytes 1572868
  42.7 16.4 %collective-permute-start.7 = (bf16[1,16,128,128]{3,2,1,0:T(8,128)(2,1)}, bf16[1,16,128,128]{3,2,1,0:T(8,128)(2,1)S(1)}, u32[]{:S(2)}, u32[]{:S(2)}) collective-permute-start(bf16[1,16,128,128]{3,2,1,0:T(8,128)(2,1)} %collective-permute-done.refs_2_), channel_id=1, source_target_pairs={{0,4},{2,6},{8,12},{10,14},{16,20},{18,22},{24,28},{26,30},{1,5},{... | collective-permute-start | bytes 1572872 | tf_op jit(solution)/shard_map/ppermute | solution.py:29
  48.1 15.6 %collective-permute-start.8 = (bf16[1,16,128,128]{3,2,1,0:T(8,128)(2,1)}, bf16[1,16,128,128]{3,2,1,0:T(8,128)(2,1)S(1)}, u32[]{:S(2)}, u32[]{:S(2)}) collective-permute-start(bf16[1,16,128,128]{3,2,1,0:T(8,128)(2,1)} %collective-permute-done.1.refs_0_), channel_id=1, source_target_pairs={{4,0},{6,2},{12,8},{14,10},{20,16},{22,18},{28,24},{30,26},{5,1},{... | collective-permute-start | bytes 1572872 | tf_op jit(solution)/shard_map/ppermute | solution.py:29
  50.5 23.5 %copy-start.15 = (bf16[1,16,128,128]{3,2,1,0:T(8,128)(2,1)}, bf16[1,16,128,128]{3,2,1,0:T(8,128)(2,1)S(1)}, u32[]{:S(2)}) copy-start(bf16[1,16,128,128]{3,2,1,0:T(8,128)(2,1)S(1)} %broadcast_select_fusion.3.refs_2_) | copy-start | bytes 1572868
  50.5 23.5 %collective-permute-start.2 = (bf16[1,16,128,128]{3,2,1,0:T(8,128)(2,1)S(1)}, bf16[1,16,128,128]{3,2,1,0:T(8,128)(2,1)S(1)}, u32[]{:S(2)}, u32[]{:S(2)}) collective-permute-start(bf16[1,16,128,128]{3,2,1,0:T(8,128)(2,1)S(1)} %bitcast.62), channel_id=1, source_target_pairs={{0,2},{4,6},{8,10},{12,14},{16,18},{20,22},{24,26},{28,30},{1,3},{... | collective-permute-start | bytes 1572872 | tf_op jit(solution)/shard_map/ppermute | solution.py:29
  51.9 16.3 %collective-permute-start.17 = (bf16[1,16,128,128]{3,2,1,0:T(8,128)(2,1)}, bf16[1,16,128,128]{3,2,1,0:T(8,128)(2,1)S(1)}, u32[]{:S(2)}, u32[]{:S(2)}) collective-permute-start(bf16[1,16,128,128]{3,2,1,0:T(8,128)(2,1)} %collective-permute-done.10.refs_5_), channel_id=1, source_target_pairs={{0,4},{2,6},{8,12},{10,14},{16,20},{18,22},{24,28},{26,30},{1,5},{... | collective-permute-start | bytes 1572872 | tf_op jit(solution)/shard_map/ppermute | solution.py:29
  55.5 17.0 %collective-permute-start.18 = (bf16[1,16,128,128]{3,2,1,0:T(8,128)(2,1)}, bf16[1,16,128,128]{3,2,1,0:T(8,128)(2,1)S(1)}, u32[]{:S(2)}, u32[]{:S(2)}) collective-permute-start(bf16[1,16,128,128]{3,2,1,0:T(8,128)(2,1)} %collective-permute-done.11.refs_6_), channel_id=1, source_target_pairs={{4,0},{6,2},{12,8},{14,10},{20,16},{22,18},{28,24},{30,26},{5,1},{... | collective-permute-start | bytes 1572872 | tf_op jit(solution)/shard_map/ppermute | solution.py:29
  57.9 18.8 %copy-start.16 = (bf16[1,16,128,128]{3,2,1,0:T(8,128)(2,1)}, bf16[1,16,128,128]{3,2,1,0:T(8,128)(2,1)S(1)}, u32[]{:S(2)}) copy-start(bf16[1,16,128,128]{3,2,1,0:T(8,128)(2,1)S(1)} %broadcast_select_fusion.1.refs_8_) | copy-start | bytes 1572868
  59.1 16.2 %collective-permute-start.12 = (bf16[1,16,128,128]{3,2,1,0:T(8,128)(2,1)S(1)}, bf16[1,16,128,128]{3,2,1,0:T(8,128)(2,1)S(1)}, u32[]{:S(2)}, u32[]{:S(2)}) collective-permute-start(bf16[1,16,128,128]{3,2,1,0:T(8,128)(2,1)S(1)} %bitcast.66), channel_id=1, source_target_pairs={{0,2},{4,6},{8,10},{12,14},{16,18},{20,22},{24,26},{28,30},{1,3},{... | collective-permute-start | bytes 1572872 | tf_op jit(solution)/shard_map/ppermute | solution.py:29
  63.7 11.7 %collective-permute-start.3 = (bf16[1,16,128,128]{3,2,1,0:T(8,128)(2,1)}, bf16[1,16,128,128]{3,2,1,0:T(8,128)(2,1)S(1)}, u32[]{:S(2)}, u32[]{:S(2)}) collective-permute-start(bf16[1,16,128,128]{3,2,1,0:T(8,128)(2,1)} %collective-permute-done.1.refs_0_), channel_id=1, source_target_pairs={{2,0},{6,4},{10,8},{14,12},{18,16},{22,20},{26,24},{30,28},{3,1},{... | collective-permute-start | bytes 1572872 | tf_op jit(solution)/shard_map/ppermute | solution.py:29
  65.1 12.5 %copy-start.17 = (bf16[1,16,128,128]{3,2,1,0:T(8,128)(2,1)}, bf16[1,16,128,128]{3,2,1,0:T(8,128)(2,1)S(1)}, u32[]{:S(2)}) copy-start(bf16[1,16,128,128]{3,2,1,0:T(8,128)(2,1)S(1)} %broadcast_select_fusion.2.refs_4_) | copy-start | bytes 1572868
  68.2 9.4 %collective-permute-start.6 = (bf16[1,16,128,128]{3,2,1,0:T(8,128)(2,1)S(1)}, bf16[1,16,128,128]{3,2,1,0:T(8,128)(2,1)S(1)}, u32[]{:S(2)}, u32[]{:S(2)}) collective-permute-start(bf16[1,16,128,128]{3,2,1,0:T(8,128)(2,1)S(1)} %broadcast_select_fusion.3.refs_2_), channel_id=1, source_target_pairs={{0,2},{2,0},{4,6},{6,4},{8,10},{10,8},{12,14},{14,12},{16,18},{18,... | collective-permute-start | bytes 1572872 | tf_op jit(solution)/shard_map/ppermute | solution.py:24
  72.5 4.2 %collective-permute-start.13 = (bf16[1,16,128,128]{3,2,1,0:T(8,128)(2,1)}, bf16[1,16,128,128]{3,2,1,0:T(8,128)(2,1)S(1)}, u32[]{:S(2)}, u32[]{:S(2)}) collective-permute-start(bf16[1,16,128,128]{3,2,1,0:T(8,128)(2,1)} %collective-permute-done.11.refs_6_), channel_id=1, source_target_pairs={{2,0},{6,4},{10,8},{14,12},{18,16},{22,20},{26,24},{30,28},{3,1},{... | collective-permute-start | bytes 1572872 | tf_op jit(solution)/shard_map/ppermute | solution.py:29
  74.0 3.8 %copy-start.18 = (bf16[1,16,128,128]{3,2,1,0:T(8,128)(2,1)}, bf16[1,16,128,128]{3,2,1,0:T(8,128)(2,1)S(1)}, u32[]{:S(2)}) copy-start(bf16[1,16,128,128]{3,2,1,0:T(8,128)(2,1)S(1)} %broadcast_select_fusion.refs_10_) | copy-start | bytes 1572868
  74.1 3.5 %collective-permute-start.16 = (bf16[1,16,128,128]{3,2,1,0:T(8,128)(2,1)S(1)}, bf16[1,16,128,128]{3,2,1,0:T(8,128)(2,1)S(1)}, u32[]{:S(2)}, u32[]{:S(2)}) collective-permute-start(bf16[1,16,128,128]{3,2,1,0:T(8,128)(2,1)S(1)} %broadcast_select_fusion.1.refs_8_), channel_id=1, source_target_pairs={{0,2},{2,0},{4,6},{6,4},{8,10},{10,8},{12,14},{14,12},{16,18},{18,... | collective-permute-start | bytes 1572872 | tf_op jit(solution)/shard_map/ppermute | solution.py:24
  75.3 2.5 %collective-permute-start.9 = (bf16[1,16,128,128]{3,2,1,0:T(8,128)(2,1)S(1)}, bf16[1,16,128,128]{3,2,1,0:T(8,128)(2,1)S(1)}, u32[]{:S(2)}, u32[]{:S(2)}) collective-permute-start(bf16[1,16,128,128]{3,2,1,0:T(8,128)(2,1)S(1)} %broadcast_select_fusion.2.refs_4_), channel_id=1, source_target_pairs={{0,2},{2,0},{4,6},{6,4},{8,10},{10,8},{12,14},{14,12},{16,18},{18,... | collective-permute-start | bytes 1572872 | tf_op jit(solution)/shard_map/ppermute | solution.py:24
  75.4 3.2 %collective-permute-start.19 = (bf16[1,16,128,128]{3,2,1,0:T(8,128)(2,1)S(1)}, bf16[1,16,128,128]{3,2,1,0:T(8,128)(2,1)S(1)}, u32[]{:S(2)}, u32[]{:S(2)}) collective-permute-start(bf16[1,16,128,128]{3,2,1,0:T(8,128)(2,1)S(1)} %broadcast_select_fusion.refs_10_), channel_id=1, source_target_pairs={{0,2},{2,0},{4,6},{6,4},{8,10},{10,8},{12,14},{14,12},{16,18},{18,... | collective-permute-start | bytes 1572872 | tf_op jit(solution)/shard_map/ppermute | solution.py:24
  77.5 1.0 copy-start.22
  77.5 1.8 copy-start.23
  77.8 1.6 copy-start.24
  78.5 0.8 copy-start.25
  101.4 5.9 %copy-start.10 = (bf16[1,16,128,128]{3,2,1,0:T(8,128)(2,1)S(1)}, bf16[1,16,128,128]{3,2,1,0:T(8,128)(2,1)}, u32[]{:S(2)}) copy-start(bf16[1,16,128,128]{3,2,1,0:T(8,128)(2,1)} %get-tuple-element.32) | copy-start | bytes 1572868
  101.4 2.2 %collective-permute-start.20 = (bf16[1,16,128,128]{3,2,1,0:T(8,128)(2,1)}, bf16[1,16,128,128]{3,2,1,0:T(8,128)(2,1)S(1)}, u32[]{:S(2)}, u32[]{:S(2)}) collective-permute-start(bf16[1,16,128,128]{3,2,1,0:T(8,128)(2,1)} %get-tuple-element.29), channel_id=1, source_target_pairs={{0,2},{2,0},{4,6},{6,4},{8,10},{10,8},{12,14},{14,12},{16,18},{18,... | collective-permute-start | bytes 1572872 | tf_op jit(solution)/shard_map/ppermute | solution.py:24
  101.7 4.2 %collective-permute-start.21 = (bf16[1,16,128,128]{3,2,1,0:T(8,128)(2,1)}, bf16[1,16,128,128]{3,2,1,0:T(8,128)(2,1)S(1)}, u32[]{:S(2)}, u32[]{:S(2)}) collective-permute-start(bf16[1,16,128,128]{3,2,1,0:T(8,128)(2,1)} %get-tuple-element.31), channel_id=1, source_target_pairs={{0,2},{2,0},{4,6},{6,4},{8,10},{10,8},{12,14},{14,12},{16,18},{18,... | collective-permute-start | bytes 1572872 | tf_op jit(solution)/shard_map/ppermute | solution.py:24
  102.0 7.5 %collective-permute-start.24 = (bf16[1,16,128,128]{3,2,1,0:T(8,128)(2,1)}, bf16[1,16,128,128]{3,2,1,0:T(8,128)(2,1)S(1)}, u32[]{:S(2)}, u32[]{:S(2)}) collective-permute-start(bf16[1,16,128,128]{3,2,1,0:T(8,128)(2,1)} %collective-permute-done.refs_2_), channel_id=1, source_target_pairs={{0,2},{2,0},{4,6},{6,4},{8,10},{10,8},{12,14},{14,12},{16,18},{18,... | collective-permute-start | bytes 1572872 | tf_op jit(solution)/shard_map/ppermute | solution.py:24
  102.2 9.9 %collective-permute-start.25 = (bf16[1,16,128,128]{3,2,1,0:T(8,128)(2,1)}, bf16[1,16,128,128]{3,2,1,0:T(8,128)(2,1)}, u32[]{:S(2)}, u32[]{:S(2)}) collective-permute-start(bf16[1,16,128,128]{3,2,1,0:T(8,128)(2,1)} %collective-permute-done.10.refs_5_), channel_id=1, source_target_pairs={{0,2},{2,0},{4,6},{6,4},{8,10},{10,8},{12,14},{14,12},{16,18},{18,... | collective-permute-start | bytes 1572872 | tf_op jit(solution)/shard_map/ppermute | solution.py:24
  102.5 4.8 %collective-permute-start.22 = (bf16[1,16,128,128]{3,2,1,0:T(8,128)(2,1)}, bf16[1,16,128,128]{3,2,1,0:T(8,128)(2,1)S(1)}, u32[]{:S(2)}, u32[]{:S(2)}) collective-permute-start(bf16[1,16,128,128]{3,2,1,0:T(8,128)(2,1)} %get-tuple-element.33), channel_id=1, source_target_pairs={{0,2},{2,0},{4,6},{6,4},{8,10},{10,8},{12,14},{14,12},{16,18},{18,... | collective-permute-start | bytes 1572872 | tf_op jit(solution)/shard_map/ppermute | solution.py:24
  103.6 4.7 %collective-permute-start.23 = (bf16[1,16,128,128]{3,2,1,0:T(8,128)(2,1)}, bf16[1,16,128,128]{3,2,1,0:T(8,128)(2,1)S(1)}, u32[]{:S(2)}, u32[]{:S(2)}) collective-permute-start(bf16[1,16,128,128]{3,2,1,0:T(8,128)(2,1)} %get-tuple-element.35), channel_id=1, source_target_pairs={{0,2},{2,0},{4,6},{6,4},{8,10},{10,8},{12,14},{14,12},{16,18},{18,... | collective-permute-start | bytes 1572872 | tf_op jit(solution)/shard_map/ppermute | solution.py:24
  103.8 4.5 %copy-start.9 = (bf16[1,16,128,128]{3,2,1,0:T(8,128)(2,1)S(1)}, bf16[1,16,128,128]{3,2,1,0:T(8,128)(2,1)}, u32[]{:S(2)}) copy-start(bf16[1,16,128,128]{3,2,1,0:T(8,128)(2,1)} %get-tuple-element.34) | copy-start | bytes 1572868
  105.8 19.3 %collective-permute-start.26 = (bf16[1,16,128,128]{3,2,1,0:T(8,128)(2,1)}, bf16[1,16,128,128]{3,2,1,0:T(8,128)(2,1)S(1)}, u32[]{:S(2)}, u32[]{:S(2)}) collective-permute-start(bf16[1,16,128,128]{3,2,1,0:T(8,128)(2,1)} %get-tuple-element.40), channel_id=1, source_target_pairs={{0,2},{2,0},{4,6},{6,4},{8,10},{10,8},{12,14},{14,12},{16,18},{18,... | collective-permute-start | bytes 1572872 | tf_op jit(solution)/shard_map/ppermute | solution.py:24
  109.3 16.1 %collective-permute-start.29 = (bf16[1,16,128,128]{3,2,1,0:T(8,128)(2,1)S(1)}, bf16[1,16,128,128]{3,2,1,0:T(8,128)(2,1)S(1)}, u32[]{:S(2)}, u32[]{:S(2)}) collective-permute-start(bf16[1,16,128,128]{3,2,1,0:T(8,128)(2,1)S(1)} %add_convert_fusion.2), channel_id=1, source_target_pairs={{0,4},{2,6},{4,0},{6,2},{8,12},{10,14},{12,8},{14,10},{16,20},{18,... | collective-permute-start | bytes 1572872 | tf_op jit(solution)/shard_map/ppermute | solution.py:24
  109.3 19.5 %collective-permute-start.32 = (bf16[1,16,128,128]{3,2,1,0:T(8,128)(2,1)}, bf16[1,16,128,128]{3,2,1,0:T(8,128)(2,1)S(1)}, u32[]{:S(2)}, u32[]{:S(2)}) collective-permute-start(bf16[1,16,128,128]{3,2,1,0:T(8,128)(2,1)} %get-tuple-element.47), channel_id=1, source_target_pairs={{0,2},{2,0},{4,6},{6,4},{8,10},{10,8},{12,14},{14,12},{16,18},{18,... | collective-permute-start | bytes 1572872 | tf_op jit(solution)/shard_map/ppermute | solution.py:24
  109.5 2.6 %copy-start.21 = (bf16[1,16,128,128]{3,2,1,0:T(8,128)(2,1)}, bf16[1,16,128,128]{3,2,1,0:T(8,128)(2,1)S(1)}, u32[]{:S(2)}) copy-start(bf16[1,16,128,128]{3,2,1,0:T(8,128)(2,1)S(1)} %collective-permute-done.24.refs_3_) | copy-start | bytes 1572868
  109.5 25.8 %collective-permute-start.35 = (bf16[1,16,128,128]{3,2,1,0:T(8,128)(2,1)}, bf16[1,16,128,128]{3,2,1,0:T(8,128)(2,1)S(1)}, u32[]{:S(2)}, u32[]{:S(2)}) collective-permute-start(bf16[1,16,128,128]{3,2,1,0:T(8,128)(2,1)} %add_convert_fusion), channel_id=1, source_target_pairs={{0,4},{2,6},{4,0},{6,2},{8,12},{10,14},{12,8},{14,10},{16,20},{18,... | collective-permute-start | bytes 1572872 | tf_op jit(solution)/shard_map/ppermute | solution.py:24
  112.1 34.5 %collective-permute-start.27 = (bf16[1,16,128,128]{3,2,1,0:T(8,128)(2,1)}, bf16[1,16,128,128]{3,2,1,0:T(8,128)(2,1)S(1)}, u32[]{:S(2)}, u32[]{:S(2)}) collective-permute-start(bf16[1,16,128,128]{3,2,1,0:T(8,128)(2,1)} %add_convert_fusion.3), channel_id=1, source_target_pairs={{0,4},{2,6},{4,0},{6,2},{8,12},{10,14},{12,8},{14,10},{16,20},{18,... | collective-permute-start | bytes 1572872 | tf_op jit(solution)/shard_map/ppermute | solution.py:24
  125.1 10.2 %copy-start.19 = (bf16[1,16,128,128]{3,2,1,0:T(8,128)(2,1)S(1)}, bf16[1,16,128,128]{3,2,1,0:T(8,128)(2,1)}, u32[]{:S(2)}) copy-start(bf16[1,16,128,128]{3,2,1,0:T(8,128)(2,1)} %get-tuple-element.52) | copy-start | bytes 1572868
  125.1 22.7 %collective-permute-start.28 = (bf16[1,16,128,128]{3,2,1,0:T(8,128)(2,1)}, bf16[1,16,128,128]{3,2,1,0:T(8,128)(2,1)}, u32[]{:S(2)}, u32[]{:S(2)}) collective-permute-start(bf16[1,16,128,128]{3,2,1,0:T(8,128)(2,1)} %get-tuple-element.43), channel_id=1, source_target_pairs={{0,2},{2,0},{4,6},{6,4},{8,10},{10,8},{12,14},{14,12},{16,18},{18,... | collective-permute-start | bytes 1572872 | tf_op jit(solution)/shard_map/ppermute | solution.py:24
  127.5 20.4 %collective-permute-start.30 = (bf16[1,16,128,128]{3,2,1,0:T(8,128)(2,1)}, bf16[1,16,128,128]{3,2,1,0:T(8,128)(2,1)}, u32[]{:S(2)}, u32[]{:S(2)}) collective-permute-start(bf16[1,16,128,128]{3,2,1,0:T(8,128)(2,1)} %fusion.7), channel_id=1, source_target_pairs={{8,0},{10,2},{12,4},{14,6},{16,8},{18,10},{20,12},{22,14},{24,16},... | collective-permute-start | bytes 1572872 | tf_op jit(solution)/shard_map/ppermute | solution.py:20
  128.8 28.2 %collective-permute-start.33 = (bf16[1,16,128,128]{3,2,1,0:T(8,128)(2,1)}, bf16[1,16,128,128]{3,2,1,0:T(8,128)(2,1)S(1)}, u32[]{:S(2)}, u32[]{:S(2)}) collective-permute-start(bf16[1,16,128,128]{3,2,1,0:T(8,128)(2,1)} %add_convert_fusion.1), channel_id=1, source_target_pairs={{0,4},{2,6},{4,0},{6,2},{8,12},{10,14},{12,8},{14,10},{16,20},{18,... | collective-permute-start | bytes 1572872 | tf_op jit(solution)/shard_map/ppermute | solution.py:24
  135.3 21.7 %collective-permute-start.34 = (bf16[1,16,128,128]{3,2,1,0:T(8,128)(2,1)}, bf16[1,16,128,128]{3,2,1,0:T(8,128)(2,1)}, u32[]{:S(2)}, u32[]{:S(2)}) collective-permute-start(bf16[1,16,128,128]{3,2,1,0:T(8,128)(2,1)} %get-tuple-element.50), channel_id=1, source_target_pairs={{0,2},{2,0},{4,6},{6,4},{8,10},{10,8},{12,14},{14,12},{16,18},{18,... | collective-permute-start | bytes 1572872 | tf_op jit(solution)/shard_map/ppermute | solution.py:24
  146.5 19.5 %copy-start.2 = (bf16[1,16,128,128]{3,2,1,0:T(8,128)(2,1)}, bf16[1,16,128,128]{3,2,1,0:T(8,128)(2,1)S(1)}, u32[]{:S(2)}) copy-start(bf16[1,16,128,128]{3,2,1,0:T(8,128)(2,1)S(1)} %collective-permute-done.27) | copy-start | bytes 1572868
  146.5 17.1 %collective-permute-start.36 = (bf16[1,16,128,128]{3,2,1,0:T(8,128)(2,1)}, bf16[1,16,128,128]{3,2,1,0:T(8,128)(2,1)}, u32[]{:S(2)}, u32[]{:S(2)}) collective-permute-start(bf16[1,16,128,128]{3,2,1,0:T(8,128)(2,1)} %fusion.18), channel_id=1, source_target_pairs={{8,0},{10,2},{12,4},{14,6},{16,8},{18,10},{20,12},{22,14},{24,16},... | collective-permute-start | bytes 1572872 | tf_op jit(solution)/shard_map/ppermute | solution.py:20
  147.8 15.8 %copy-start.20 = (bf16[1,16,128,128]{3,2,1,0:T(8,128)(2,1)S(1)}, bf16[1,16,128,128]{3,2,1,0:T(8,128)(2,1)}, u32[]{:S(2)}) copy-start(bf16[1,16,128,128]{3,2,1,0:T(8,128)(2,1)} %get-tuple-element.49) | copy-start | bytes 1572868
  150.5 16.8 %copy-start.1 = (f32[16,128,256]{2,1,0:T(8,128)S(1)}, f32[16,128,256]{2,1,0:T(8,128)}, u32[]{:S(2)}) copy-start(f32[16,128,256]{2,1,0:T(8,128)} %get-tuple-element.38) | copy-start | bytes 6291460
  150.5 24.3 %collective-permute-start.31 = (bf16[128,16,128]{2,0,1:T(8,128)(2,1)}, bf16[128,16,128]{2,0,1:T(8,128)(2,1)}, u32[]{:S(2)}, u32[]{:S(2)}) collective-permute-start(bf16[128,16,128]{2,0,1:T(8,128)(2,1)} %fusion.23), channel_id=1, source_target_pairs={{8,0},{10,2},{12,4},{14,6},{16,8},{18,10},{20,12},{22,14},{24,16},... | collective-permute-start | bytes 1572872 | tf_op jit(solution)/shard_map/ppermute | solution.py:20
  157.0 10.3 %copy-start.4 = (bf16[1,16,128,128]{3,2,1,0:T(8,128)(2,1)}, bf16[1,16,128,128]{3,2,1,0:T(8,128)(2,1)S(1)}, u32[]{:S(2)}) copy-start(bf16[1,16,128,128]{3,2,1,0:T(8,128)(2,1)S(1)} %collective-permute-done.33) | copy-start | bytes 1572868
  166.0 17.6 %collective-permute-start.37 = (bf16[128,16,128]{2,0,1:T(8,128)(2,1)}, bf16[128,16,128]{2,0,1:T(8,128)(2,1)}, u32[]{:S(2)}, u32[]{:S(2)}) collective-permute-start(bf16[128,16,128]{2,0,1:T(8,128)(2,1)} %fusion.22), channel_id=1, source_target_pairs={{8,0},{10,2},{12,4},{14,6},{16,8},{18,10},{20,12},{22,14},{24,16},... | collective-permute-start | bytes 1572872 | tf_op jit(solution)/shard_map/ppermute | solution.py:20
  167.9 6.9 %copy-start.3 = (bf16[1,16,128,128]{3,2,1,0:T(8,128)(2,1)S(1)}, bf16[1,16,128,128]{3,2,1,0:T(8,128)(2,1)}, u32[]{:S(2)}) copy-start(bf16[1,16,128,128]{3,2,1,0:T(8,128)(2,1)} %copy-done.2) | copy-start | bytes 1572868
  171.7 12.0 %copy-start.5 = (bf16[1,16,128,128]{3,2,1,0:T(8,128)(2,1)S(1)}, bf16[1,16,128,128]{3,2,1,0:T(8,128)(2,1)}, u32[]{:S(2)}) copy-start(bf16[1,16,128,128]{3,2,1,0:T(8,128)(2,1)} %copy-done.4) | copy-start | bytes 1572868
  171.7 12.0 %copy-start.8 = (bf16[1,16,128,128]{3,2,1,0:T(8,128)(2,1)S(1)}, bf16[1,16,128,128]{3,2,1,0:T(8,128)(2,1)}, u32[]{:S(2)}) copy-start(bf16[1,16,128,128]{3,2,1,0:T(8,128)(2,1)} %get-tuple-element.46) | copy-start | bytes 1572868

commit v14 on v13

--- a/solution.py
+++ b/solution.py
@@ -59,7 +59,7 @@
             v = v_refs[b][0, g]
             off = jnp.where(valid_ref[b] > 0, 0.0, 1e30).astype(jnp.float32)
             s = lax.dot_general(k, q, (((1,), (1,)), ((), ())), preferred_element_type=jnp.float32)
-            e = jnp.exp(s * SCALE - lse - off)
+            e = jnp.exp(s * SCALE - (lse + off))
             if mode == 0:
                 p = jnp.where(causal, e, 0.0)
             elif mode == 2:

time: 187 us -> 187 us (level)
  no operation moved by 1% of the time
where the time goes in v14:
time: 187 us; the launch traced here: 186 us
  starting transfers between devices  60.4 us (32%)
  waiting for transfers between devices  53.1 us (28%)
  Pallas kernels  34.6 us (19%)
  other arithmetic  22.5 us (12%)
  local copies, waits for them, and re-layouts  14.1 us (8%)
    pallas_call x2, Pallas kernels, attend_blocks(): pl.pallas_call(functools.partial(_blocks_kernel, tuple(modes), acc is not...  34.6 us
    ppermute x12, starting transfers between devices, one_way(): return lax.ppermute(x, 'seq', pairs)  29 us
    ppermute x8, starting transfers between devices, shift(): return lax.ppermute(x, 'seq', pairs)  23.6 us
    ppermute x18, waiting for transfers between devices, swap(): return lax.ppermute(x, 'seq', [(i, i ^ bit) for i in range(n)])  21.9 us
    ppermute x8, waiting for transfers between devices, shift(): return lax.ppermute(x, 'seq', pairs)  19.2 us
    ppermute x12, waiting for transfers between devices, one_way(): return lax.ppermute(x, 'seq', pairs)  11.9 us
    ppermute x18, starting transfers between devices, swap(): return lax.ppermute(x, 'seq', [(i, i ^ bit) for i in range(n)])  7.79 us
    unnamed x56, local copies, waits for them, and re-layouts  6.47 us
  transfers between devices with their start and end apart: 38, of which 14 were waited for; matrix products, arithmetic and copies ran while one was open for 17% of the time, Pallas kernels for 7%

profile of v14, /device:TPU:0, one launch (start us, length us, event | category | flops | bytes accessed | tf_op | source)
XLA Modules:
  0.0 185.8 jit_solution(327425873193006759)
XLA Ops:
  0.7 1.3 copy.27
  2.0 5.7 %collective-permute-start = (bf16[1,16,128,128]{3,2,1,0:T(8,128)(2,1)S(1)}, bf16[1,16,128,128]{3,2,1,0:T(8,128)(2,1)}, u32[]{:S(2)}, u32[]{:S(2)}) collective-permute-start(bf16[1,16,128,128]{3,2,1,0:T(8,128)(2,1)S(1)} %bitcast.60), channel_id=1, source_target_pairs={{0,8},{2,10},{4,12},{6,14},{8,16},{10,18},{12,20},{14,22},{16,24},... | collective-permute-start | bytes 1572872 | tf_op jit(solution)/shard_map/ppermute | solution.py:20
  7.7 1.2 copy.26
  8.9 3.5 %collective-permute-start.10 = (bf16[1,16,128,128]{3,2,1,0:T(8,128)(2,1)S(1)}, bf16[1,16,128,128]{3,2,1,0:T(8,128)(2,1)}, u32[]{:S(2)}, u32[]{:S(2)}) collective-permute-start(bf16[1,16,128,128]{3,2,1,0:T(8,128)(2,1)S(1)} %bitcast.64), channel_id=1, source_target_pairs={{0,8},{2,10},{4,12},{6,14},{8,16},{10,18},{12,20},{14,22},{16,24},... | collective-permute-start | bytes 1572872 | tf_op jit(solution)/shard_map/ppermute | solution.py:20
  12.4 3.4 %collective-permute-start.4 = (bf16[1,16,128,128]{3,2,1,0:T(8,128)(2,1)S(1)}, bf16[1,16,128,128]{3,2,1,0:T(8,128)(2,1)S(1)}, u32[]{:S(2)}, u32[]{:S(2)}) collective-permute-start(bf16[1,16,128,128]{3,2,1,0:T(8,128)(2,1)S(1)} %bitcast.61), channel_id=1, source_target_pairs={{0,4},{2,6},{8,12},{10,14},{16,20},{18,22},{24,28},{26,30},{1,5},{... | collective-permute-start | bytes 1572872 | tf_op jit(solution)/shard_map/ppermute | solution.py:29
  15.9 3.4 %collective-permute-done.refs_2_ = bf16[1,16,128,128]{3,2,1,0:T(8,128)(2,1)} collective-permute-done((bf16[1,16,128,128]{3,2,1,0:T(8,128)(2,1)S(1)}, bf16[1,16,128,128]{3,2,1,0:T(8,128)(2,1)}, u32[]{:S(2)}, u32[]{:S(2)}) %collective-permute-start) | collective-permute-done | bytes 524320 | tf_op jit(solution)/shard_map/ppermute | solution.py:20
  19.2 5.3 %collective-permute-start.1 = (bf16[1,16,128,128]{3,2,1,0:T(8,128)(2,1)}, bf16[1,16,128,128]{3,2,1,0:T(8,128)(2,1)}, u32[]{:S(2)}, u32[]{:S(2)}) collective-permute-start(bf16[1,16,128,128]{3,2,1,0:T(8,128)(2,1)} %collective-permute-done.refs_2_), channel_id=1, source_target_pairs={{0,8},{2,10},{4,12},{6,14},{8,16},{10,18},{12,20},{14,22},{16,24},... | collective-permute-start | bytes 1572872 | tf_op jit(solution)/shard_map/ppermute | solution.py:20
  24.5 1.3 collective-permute-start.5
  25.8 6.2 %collective-permute-start.14 = (bf16[1,16,128,128]{3,2,1,0:T(8,128)(2,1)S(1)}, bf16[1,16,128,128]{3,2,1,0:T(8,128)(2,1)}, u32[]{:S(2)}, u32[]{:S(2)}) collective-permute-start(bf16[1,16,128,128]{3,2,1,0:T(8,128)(2,1)S(1)} %bitcast.65), channel_id=1, source_target_pairs={{0,4},{2,6},{8,12},{10,14},{16,20},{18,22},{24,28},{26,30},{1,5},{... | collective-permute-start | bytes 1572872 | tf_op jit(solution)/shard_map/ppermute | solution.py:29
  32.0 3.8 %collective-permute-start.11 = (bf16[1,16,128,128]{3,2,1,0:T(8,128)(2,1)}, bf16[1,16,128,128]{3,2,1,0:T(8,128)(2,1)}, u32[]{:S(2)}, u32[]{:S(2)}) collective-permute-start(bf16[1,16,128,128]{3,2,1,0:T(8,128)(2,1)} %collective-permute-done.10.refs_5_), channel_id=1, source_target_pairs={{0,8},{2,10},{4,12},{6,14},{8,16},{10,18},{12,20},{14,22},{16,24},... | collective-permute-start | bytes 1572872 | tf_op jit(solution)/shard_map/ppermute | solution.py:20
  35.8 0.8 copy-done.13
  36.6 1.3 collective-permute-start.15
  38.6 1.4 copy.16
  40.0 1.4 copy.17
  41.4 0.6 multiply_reduce_fusion
  42.0 0.7 copy.18
  42.7 5.3 %collective-permute-start.7 = (bf16[1,16,128,128]{3,2,1,0:T(8,128)(2,1)}, bf16[1,16,128,128]{3,2,1,0:T(8,128)(2,1)S(1)}, u32[]{:S(2)}, u32[]{:S(2)}) collective-permute-start(bf16[1,16,128,128]{3,2,1,0:T(8,128)(2,1)} %collective-permute-done.refs_2_), channel_id=1, source_target_pairs={{0,4},{2,6},{8,12},{10,14},{16,20},{18,22},{24,28},{26,30},{1,5},{... | collective-permute-start | bytes 1572872 | tf_op jit(solution)/shard_map/ppermute | solution.py:29
  48.1 1.3 collective-permute-start.8
  49.4 1.1 broadcast_select_fusion.3.refs_2_
  50.5 1.3 collective-permute-start.2
  51.9 3.5 %collective-permute-start.17 = (bf16[1,16,128,128]{3,2,1,0:T(8,128)(2,1)}, bf16[1,16,128,128]{3,2,1,0:T(8,128)(2,1)S(1)}, u32[]{:S(2)}, u32[]{:S(2)}) collective-permute-start(bf16[1,16,128,128]{3,2,1,0:T(8,128)(2,1)} %collective-permute-done.10.refs_5_), channel_id=1, source_target_pairs={{0,4},{2,6},{8,12},{10,14},{16,20},{18,22},{24,28},{26,30},{1,5},{... | collective-permute-start | bytes 1572872 | tf_op jit(solution)/shard_map/ppermute | solution.py:29
  55.5 1.3 collective-permute-start.18
  56.8 1.1 broadcast_select_fusion.1.refs_8_
  57.9 1.2 collective-permute-done.7
  59.1 1.3 collective-permute-start.12
  60.4 3.3 %collective-permute-done.8 = bf16[1,16,128,128]{3,2,1,0:T(8,128)(2,1)S(1)} collective-permute-done((bf16[1,16,128,128]{3,2,1,0:T(8,128)(2,1)}, bf16[1,16,128,128]{3,2,1,0:T(8,128)(2,1)S(1)}, u32[]{:S(2)}, u32[]{:S(2)}) %collective-permute-start.8) | collective-permute-done | bytes 524320 | tf_op jit(solution)/shard_map/ppermute | solution.py:29
  63.7 1.3 collective-permute-start.3
  65.1 3.1 %collective-permute-done.17 = bf16[1,16,128,128]{3,2,1,0:T(8,128)(2,1)S(1)} collective-permute-done((bf16[1,16,128,128]{3,2,1,0:T(8,128)(2,1)}, bf16[1,16,128,128]{3,2,1,0:T(8,128)(2,1)S(1)}, u32[]{:S(2)}, u32[]{:S(2)}) %collective-permute-start.17) | collective-permute-done | bytes 524320 | tf_op jit(solution)/shard_map/ppermute | solution.py:29
  68.2 4.3 %collective-permute-done.18 = bf16[1,16,128,128]{3,2,1,0:T(8,128)(2,1)S(1)} collective-permute-done((bf16[1,16,128,128]{3,2,1,0:T(8,128)(2,1)}, bf16[1,16,128,128]{3,2,1,0:T(8,128)(2,1)S(1)}, u32[]{:S(2)}, u32[]{:S(2)}) %collective-permute-start.18) | collective-permute-done | bytes 524320 | tf_op jit(solution)/shard_map/ppermute | solution.py:29
  72.5 1.5 collective-permute-start.13
  74.1 1.2 collective-permute-start.16
  75.8 0.8 broadcast_select_fusion.5.refs_1_
  76.7 0.9 broadcast_select_fusion.4.refs_7_
  77.8 0.7 collective-permute-done.19.refs_11_
  78.5 0.8 copy-done.25
  79.4 21.7 %shard_map.85 = (f32[16,128,256]{2,1,0:T(8,128)}, bf16[1,16,128,128]{3,2,1,0:T(8,128)(2,1)}, bf16[1,16,128,128]{3,2,1,0:T(8,128)(2,1)}, bf16[1,16,128,128]{3,2,1...) custom-call(s32[6]{0:T(128)} %stack.58.valid_ref, ...), custom_call_target="tpu_custom_call" | custom-call | flops 4026531840 | bytes 14680064 | tf_op jit(solution)/shard_map/pallas_call | solution.py:105
  102.3 1.0 collective-permute-done.20
  103.4 2.0 %add_convert_fusion.3 = bf16[1,16,128,128]{3,2,1,0:T(8,128)(2,1)} fusion(bf16[1,16,128,128]{3,2,1,0:T(8,128)(2,1)S(1)} %collective-permute-done.20, bf16[1,16,128,128]{3,2,1,0:T(8,128)(2,1)} %get-tuple-element.28), kind=kLoop, calls=%fused_computation.37 | loop fusion | flops 1048576 | bytes 1572864 | tf_op jit(solution)/shard_map/convert_element_type | solution.py:137
  105.9 1.2 add_convert_fusion.2
  107.1 1.0 add_convert_fusion.1
  108.0 1.0 add_convert_fusion
  109.1 2.0 %collective-permute-start.35 = (bf16[1,16,128,128]{3,2,1,0:T(8,128)(2,1)}, bf16[1,16,128,128]{3,2,1,0:T(8,128)(2,1)S(1)}, u32[]{:S(2)}, u32[]{:S(2)}) collective-permute-start(bf16[1,16,128,128]{3,2,1,0:T(8,128)(2,1)} %add_convert_fusion), channel_id=1, source_target_pairs={{0,4},{2,6},{4,0},{6,2},{8,12},{10,14},{12,8},{14,10},{16,20},{18,... | collective-permute-start | bytes 1572872 | tf_op jit(solution)/shard_map/ppermute | solution.py:24
  111.1 0.7 add_convert_fusion.4.valid_ref
  111.8 12.8 %shard_map.86 = (f32[16,128,256]{2,1,0:T(8,128)}, bf16[1,16,128,128]{3,2,1,0:T(8,128)(2,1)}, bf16[1,16,128,128]{3,2,1,0:T(8,128)(2,1)}, bf16[1,16,128,128]{3,2,1...) custom-call(s32[3]{0:T(128)} %add_convert_fusion.4.valid_ref, ...), custom_call_target="tpu_custom_call" | custom-call | flops 2013265920 | bytes 10485760 | tf_op jit(solution)/shard_map/pallas_call | solution.py:105
  124.9 2.1 %fusion.7 = bf16[1,16,128,128]{3,2,1,0:T(8,128)(2,1)} fusion(bf16[1,16,128,128]{3,2,1,0:T(8,128)(2,1)S(1)} %collective-permute-done.26, bf16[1,16,128,128]{3,2,1,0:T(8,128)(2,1)S(1)} %collective-permute-done.29, bf16[1,16,128,128]{3,2,1,0:T(8,128)(2,1)} %get-tuple-element.45, pred[]{:T(512)S(6)} %eq.26, pred[]{:T(512)S(6)} %eq.11), kind=kLoop, calls=%fused_computation.19 | loop fusion | flops 2097152 | bytes 2097154 | tf_op jit(solution)/shard_map/convert_element_type | solution.py:154
  127.1 1.3 collective-permute-start.30
  128.4 1.9 %collective-permute-start.33 = (bf16[1,16,128,128]{3,2,1,0:T(8,128)(2,1)}, bf16[1,16,128,128]{3,2,1,0:T(8,128)(2,1)S(1)}, u32[]{:S(2)}, u32[]{:S(2)}) collective-permute-start(bf16[1,16,128,128]{3,2,1,0:T(8,128)(2,1)} %add_convert_fusion.1), channel_id=1, source_target_pairs={{0,4},{2,6},{4,0},{6,2},{8,12},{10,14},{12,8},{14,10},{16,20},{18,... | collective-permute-start | bytes 1572872 | tf_op jit(solution)/shard_map/ppermute | solution.py:24
  130.2 4.7 %collective-permute-done.35 = bf16[1,16,128,128]{3,2,1,0:T(8,128)(2,1)S(1)} collective-permute-done((bf16[1,16,128,128]{3,2,1,0:T(8,128)(2,1)}, bf16[1,16,128,128]{3,2,1,0:T(8,128)(2,1)S(1)}, u32[]{:S(2)}, u32[]{:S(2)}) %collective-permute-start.35) | collective-permute-done | bytes 524320 | tf_op jit(solution)/shard_map/ppermute | solution.py:24
  135.0 1.1 fusion.18
  136.1 10.2 %collective-permute-done.27 = bf16[1,16,128,128]{3,2,1,0:T(8,128)(2,1)S(1)} collective-permute-done((bf16[1,16,128,128]{3,2,1,0:T(8,128)(2,1)}, bf16[1,16,128,128]{3,2,1,0:T(8,128)(2,1)S(1)}, u32[]{:S(2)}, u32[]{:S(2)}) %collective-permute-start.27) | collective-permute-done | bytes 524320 | tf_op jit(solution)/shard_map/ppermute | solution.py:24
  146.2 1.3 collective-permute-start.36
  147.5 2.6 %fusion.23 = bf16[128,16,128]{2,0,1:T(8,128)(2,1)} fusion(bf16[1,16,128,128]{3,2,1,0:T(8,128)(2,1)} %collective-permute-done.30, bf16[1,16,128,128]{3,2,1,0:T(8,128)(2,1)S(1)} %collective-permute-done.27, bf16[1,16,128,128]{3,2,1,0:T(8,128)(2,1)S(1)} %collective-permute-done.29, bf16[1,16,128,128]{3,2,1,0:T(8,128)(2,1)} %collective-permute-done.28, ...), kind=kLoop, calls=%fused_computation.39 | loop fusion | flops 2621440 | bytes 3145729 | tf_op jit(solution)/shard_map/transpose | solution.py:156
  150.2 1.4 collective-permute-start.31
  151.6 5.1 %collective-permute-done.33 = bf16[1,16,128,128]{3,2,1,0:T(8,128)(2,1)S(1)} collective-permute-done((bf16[1,16,128,128]{3,2,1,0:T(8,128)(2,1)}, bf16[1,16,128,128]{3,2,1,0:T(8,128)(2,1)S(1)}, u32[]{:S(2)}, u32[]{:S(2)}) %collective-permute-start.33) | collective-permute-done | bytes 524320 | tf_op jit(solution)/shard_map/ppermute | solution.py:24
  156.7 6.6 %collective-permute-done.36 = bf16[1,16,128,128]{3,2,1,0:T(8,128)(2,1)} collective-permute-done((bf16[1,16,128,128]{3,2,1,0:T(8,128)(2,1)}, bf16[1,16,128,128]{3,2,1,0:T(8,128)(2,1)}, u32[]{:S(2)}, u32[]{:S(2)}) %collective-permute-start.36) | collective-permute-done | bytes 524320 | tf_op jit(solution)/shard_map/ppermute | solution.py:20
  163.3 2.4 %fusion.22 = bf16[128,16,128]{2,0,1:T(8,128)(2,1)} fusion(bf16[1,16,128,128]{3,2,1,0:T(8,128)(2,1)} %collective-permute-done.36, bf16[1,16,128,128]{3,2,1,0:T(8,128)(2,1)S(1)} %collective-permute-done.33, bf16[1,16,128,128]{3,2,1,0:T(8,128)(2,1)S(1)} %collective-permute-done.35, bf16[1,16,128,128]{3,2,1,0:T(8,128)(2,1)} %collective-permute-done.34, ...), kind=kLoop, calls=%fused_computation.38 | loop fusion | flops 2621440 | bytes 3145729 | tf_op jit(solution)/shard_map/transpose | solution.py:156
  165.7 1.3 collective-permute-start.37
  167.6 3.8 %copy.21 = bf16[128,16,2,128]{3,2,1,0:T(2,128)(2,1)} copy(bf16[128,16,2,128]{0,2,3,1:T(2,128)(2,1)S(1)} %bitcast.53) | data formatting | bytes 2097152 | tf_op jit(solution)/shard_map/transpose | solution.py:200
  171.4 3.2 %collective-permute-done.31 = bf16[128,16,128]{2,0,1:T(8,128)(2,1)} collective-permute-done((bf16[128,16,128]{2,0,1:T(8,128)(2,1)}, bf16[128,16,128]{2,0,1:T(8,128)(2,1)}, u32[]{:S(2)}, u32[]{:S(2)}) %collective-permute-start.31) | collective-permute-done | bytes 524320 | tf_op jit(solution)/shard_map/ppermute | solution.py:20
  174.5 1.6 fusion.4
  176.1 1.1 copy.22
  177.2 6.0 %collective-permute-done.37 = bf16[128,16,128]{2,0,1:T(8,128)(2,1)} collective-permute-done((bf16[128,16,128]{2,0,1:T(8,128)(2,1)}, bf16[128,16,128]{2,0,1:T(8,128)(2,1)}, u32[]{:S(2)}, u32[]{:S(2)}) %collective-permute-start.37) | collective-permute-done | bytes 524320 | tf_op jit(solution)/shard_map/ppermute | solution.py:20
  183.2 1.4 fusion.15
  184.6 1.1 copy.23
  (96 shorter events, 4.5 us)
Async XLA Ops:
  0.6 38.0 %copy-start.6 = (bf16[128,32,128]{2,1,0:T(8,128)(2,1)S(1)}, bf16[128,32,128]{2,1,0:T(8,128)(2,1)}, u32[]{:S(2)}) copy-start(bf16[128,32,128]{2,1,0:T(8,128)(2,1)} %param.6) | copy-start | bytes 3145732
  0.6 39.3 %copy-start = (bf16[128,32,128]{2,1,0:T(8,128)(2,1)S(1)}, bf16[128,32,128]{2,1,0:T(8,128)(2,1)}, u32[]{:S(2)}) copy-start(bf16[128,32,128]{2,1,0:T(8,128)(2,1)} %param.10) | copy-start | bytes 3145732
  2.0 48.5 %copy-start.11 = (bf16[128,16,128]{2,0,1:T(8,128)(2,1)}, bf16[128,16,128]{2,0,1:T(8,128)(2,1)S(1)}, u32[]{:S(2)}) copy-start(bf16[128,16,128]{2,0,1:T(8,128)(2,1)S(1)} %copy.27) | copy-start | bytes 1572868
  2.0 17.2 %collective-permute-start = (bf16[1,16,128,128]{3,2,1,0:T(8,128)(2,1)S(1)}, bf16[1,16,128,128]{3,2,1,0:T(8,128)(2,1)}, u32[]{:S(2)}, u32[]{:S(2)}) collective-permute-start(bf16[1,16,128,128]{3,2,1,0:T(8,128)(2,1)S(1)} %bitcast.60), channel_id=1, source_target_pairs={{0,8},{2,10},{4,12},{6,14},{8,16},{10,18},{12,20},{14,22},{16,24},... | collective-permute-start | bytes 1572872 | tf_op jit(solution)/shard_map/ppermute | solution.py:20
  8.9 50.2 %copy-start.12 = (bf16[128,16,128]{2,0,1:T(8,128)(2,1)}, bf16[128,16,128]{2,0,1:T(8,128)(2,1)S(1)}, u32[]{:S(2)}) copy-start(bf16[128,16,128]{2,0,1:T(8,128)(2,1)S(1)} %copy.26) | copy-start | bytes 1572868
  8.9 23.0 %collective-permute-start.10 = (bf16[1,16,128,128]{3,2,1,0:T(8,128)(2,1)S(1)}, bf16[1,16,128,128]{3,2,1,0:T(8,128)(2,1)}, u32[]{:S(2)}, u32[]{:S(2)}) collective-permute-start(bf16[1,16,128,128]{3,2,1,0:T(8,128)(2,1)S(1)} %bitcast.64), channel_id=1, source_target_pairs={{0,8},{2,10},{4,12},{6,14},{8,16},{10,18},{12,20},{14,22},{16,24},... | collective-permute-start | bytes 1572872 | tf_op jit(solution)/shard_map/ppermute | solution.py:20
  12.4 23.3 %collective-permute-start.4 = (bf16[1,16,128,128]{3,2,1,0:T(8,128)(2,1)S(1)}, bf16[1,16,128,128]{3,2,1,0:T(8,128)(2,1)S(1)}, u32[]{:S(2)}, u32[]{:S(2)}) collective-permute-start(bf16[1,16,128,128]{3,2,1,0:T(8,128)(2,1)S(1)} %bitcast.61), channel_id=1, source_target_pairs={{0,4},{2,6},{8,12},{10,14},{16,20},{18,22},{24,28},{26,30},{1,5},{... | collective-permute-start | bytes 1572872 | tf_op jit(solution)/shard_map/ppermute | solution.py:29
  19.2 23.5 %collective-permute-start.1 = (bf16[1,16,128,128]{3,2,1,0:T(8,128)(2,1)}, bf16[1,16,128,128]{3,2,1,0:T(8,128)(2,1)}, u32[]{:S(2)}, u32[]{:S(2)}) collective-permute-start(bf16[1,16,128,128]{3,2,1,0:T(8,128)(2,1)} %collective-permute-done.refs_2_), channel_id=1, source_target_pairs={{0,8},{2,10},{4,12},{6,14},{8,16},{10,18},{12,20},{14,22},{16,24},... | collective-permute-start | bytes 1572872 | tf_op jit(solution)/shard_map/ppermute | solution.py:20
  24.5 23.6 %collective-permute-start.5 = (bf16[1,16,128,128]{3,2,1,0:T(8,128)(2,1)}, bf16[1,16,128,128]{3,2,1,0:T(8,128)(2,1)}, u32[]{:S(2)}, u32[]{:S(2)}) collective-permute-start(bf16[1,16,128,128]{3,2,1,0:T(8,128)(2,1)} %collective-permute-done.refs_2_), channel_id=1, source_target_pairs={{4,0},{6,2},{12,8},{14,10},{20,16},{22,18},{28,24},{30,26},{5,1},{... | collective-permute-start | bytes 1572872 | tf_op jit(solution)/shard_map/ppermute | solution.py:29
  25.8 24.7 %collective-permute-start.14 = (bf16[1,16,128,128]{3,2,1,0:T(8,128)(2,1)S(1)}, bf16[1,16,128,128]{3,2,1,0:T(8,128)(2,1)}, u32[]{:S(2)}, u32[]{:S(2)}) collective-permute-start(bf16[1,16,128,128]{3,2,1,0:T(8,128)(2,1)S(1)} %bitcast.65), channel_id=1, source_target_pairs={{0,4},{2,6},{8,12},{10,14},{16,20},{18,22},{24,28},{26,30},{1,5},{... | collective-permute-start | bytes 1572872 | tf_op jit(solution)/shard_map/ppermute | solution.py:29
  32.0 19.9 %collective-permute-start.11 = (bf16[1,16,128,128]{3,2,1,0:T(8,128)(2,1)}, bf16[1,16,128,128]{3,2,1,0:T(8,128)(2,1)}, u32[]{:S(2)}, u32[]{:S(2)}) collective-permute-start(bf16[1,16,128,128]{3,2,1,0:T(8,128)(2,1)} %collective-permute-done.10.refs_5_), channel_id=1, source_target_pairs={{0,8},{2,10},{4,12},{6,14},{8,16},{10,18},{12,20},{14,22},{16,24},... | collective-permute-start | bytes 1572872 | tf_op jit(solution)/shard_map/ppermute | solution.py:20
  35.8 0.8 copy-start.13
  36.6 18.9 %collective-permute-start.15 = (bf16[1,16,128,128]{3,2,1,0:T(8,128)(2,1)}, bf16[1,16,128,128]{3,2,1,0:T(8,128)(2,1)}, u32[]{:S(2)}, u32[]{:S(2)}) collective-permute-start(bf16[1,16,128,128]{3,2,1,0:T(8,128)(2,1)} %collective-permute-done.10.refs_5_), channel_id=1, source_target_pairs={{4,0},{6,2},{12,8},{14,10},{20,16},{22,18},{28,24},{30,26},{5,1},{... | collective-permute-start | bytes 1572872 | tf_op jit(solution)/shard_map/ppermute | solution.py:29
  38.6 2.8 %copy-start.7 = (bf16[128,32,128]{2,1,0:T(8,128)(2,1)S(1)}, bf16[128,32,128]{2,1,0:T(8,128)(2,1)}, u32[]{:S(2)}) copy-start(bf16[128,32,128]{2,1,0:T(8,128)(2,1)} %param.9) | copy-start | bytes 3145732
  40.0 9.4 %copy-start.14 = (bf16[1,16,128,128]{3,2,1,0:T(8,128)(2,1)S(1)}, bf16[1,16,128,128]{3,2,1,0:T(8,128)(2,1)}, u32[]{:S(2)}) copy-start(bf16[1,16,128,128]{3,2,1,0:T(8,128)(2,1)} %copy-done.13) | copy-start | bytes 1572868
  42.7 16.4 %collective-permute-start.7 = (bf16[1,16,128,128]{3,2,1,0:T(8,128)(2,1)}, bf16[1,16,128,128]{3,2,1,0:T(8,128)(2,1)S(1)}, u32[]{:S(2)}, u32[]{:S(2)}) collective-permute-start(bf16[1,16,128,128]{3,2,1,0:T(8,128)(2,1)} %collective-permute-done.refs_2_), channel_id=1, source_target_pairs={{0,4},{2,6},{8,12},{10,14},{16,20},{18,22},{24,28},{26,30},{1,5},{... | collective-permute-start | bytes 1572872 | tf_op jit(solution)/shard_map/ppermute | solution.py:29
  48.1 15.6 %collective-permute-start.8 = (bf16[1,16,128,128]{3,2,1,0:T(8,128)(2,1)}, bf16[1,16,128,128]{3,2,1,0:T(8,128)(2,1)S(1)}, u32[]{:S(2)}, u32[]{:S(2)}) collective-permute-start(bf16[1,16,128,128]{3,2,1,0:T(8,128)(2,1)} %collective-permute-done.1.refs_0_), channel_id=1, source_target_pairs={{4,0},{6,2},{12,8},{14,10},{20,16},{22,18},{28,24},{30,26},{5,1},{... | collective-permute-start | bytes 1572872 | tf_op jit(solution)/shard_map/ppermute | solution.py:29
  50.5 23.5 %copy-start.15 = (bf16[1,16,128,128]{3,2,1,0:T(8,128)(2,1)}, bf16[1,16,128,128]{3,2,1,0:T(8,128)(2,1)S(1)}, u32[]{:S(2)}) copy-start(bf16[1,16,128,128]{3,2,1,0:T(8,128)(2,1)S(1)} %broadcast_select_fusion.3.refs_2_) | copy-start | bytes 1572868
  50.5 23.5 %collective-permute-start.2 = (bf16[1,16,128,128]{3,2,1,0:T(8,128)(2,1)S(1)}, bf16[1,16,128,128]{3,2,1,0:T(8,128)(2,1)S(1)}, u32[]{:S(2)}, u32[]{:S(2)}) collective-permute-start(bf16[1,16,128,128]{3,2,1,0:T(8,128)(2,1)S(1)} %bitcast.62), channel_id=1, source_target_pairs={{0,2},{4,6},{8,10},{12,14},{16,18},{20,22},{24,26},{28,30},{1,3},{... | collective-permute-start | bytes 1572872 | tf_op jit(solution)/shard_map/ppermute | solution.py:29
  51.9 16.3 %collective-permute-start.17 = (bf16[1,16,128,128]{3,2,1,0:T(8,128)(2,1)}, bf16[1,16,128,128]{3,2,1,0:T(8,128)(2,1)S(1)}, u32[]{:S(2)}, u32[]{:S(2)}) collective-permute-start(bf16[1,16,128,128]{3,2,1,0:T(8,128)(2,1)} %collective-permute-done.10.refs_5_), channel_id=1, source_target_pairs={{0,4},{2,6},{8,12},{10,14},{16,20},{18,22},{24,28},{26,30},{1,5},{... | collective-permute-start | bytes 1572872 | tf_op jit(solution)/shard_map/ppermute | solution.py:29
  55.5 17.0 %collective-permute-start.18 = (bf16[1,16,128,128]{3,2,1,0:T(8,128)(2,1)}, bf16[1,16,128,128]{3,2,1,0:T(8,128)(2,1)S(1)}, u32[]{:S(2)}, u32[]{:S(2)}) collective-permute-start(bf16[1,16,128,128]{3,2,1,0:T(8,128)(2,1)} %collective-permute-done.11.refs_6_), channel_id=1, source_target_pairs={{4,0},{6,2},{12,8},{14,10},{20,16},{22,18},{28,24},{30,26},{5,1},{... | collective-permute-start | bytes 1572872 | tf_op jit(solution)/shard_map/ppermute | solution.py:29
  57.9 18.8 %copy-start.16 = (bf16[1,16,128,128]{3,2,1,0:T(8,128)(2,1)}, bf16[1,16,128,128]{3,2,1,0:T(8,128)(2,1)S(1)}, u32[]{:S(2)}) copy-start(bf16[1,16,128,128]{3,2,1,0:T(8,128)(2,1)S(1)} %broadcast_select_fusion.1.refs_8_) | copy-start | bytes 1572868
  59.1 16.2 %collective-permute-start.12 = (bf16[1,16,128,128]{3,2,1,0:T(8,128)(2,1)S(1)}, bf16[1,16,128,128]{3,2,1,0:T(8,128)(2,1)S(1)}, u32[]{:S(2)}, u32[]{:S(2)}) collective-permute-start(bf16[1,16,128,128]{3,2,1,0:T(8,128)(2,1)S(1)} %bitcast.66), channel_id=1, source_target_pairs={{0,2},{4,6},{8,10},{12,14},{16,18},{20,22},{24,26},{28,30},{1,3},{... | collective-permute-start | bytes 1572872 | tf_op jit(solution)/shard_map/ppermute | solution.py:29
  63.7 11.7 %collective-permute-start.3 = (bf16[1,16,128,128]{3,2,1,0:T(8,128)(2,1)}, bf16[1,16,128,128]{3,2,1,0:T(8,128)(2,1)S(1)}, u32[]{:S(2)}, u32[]{:S(2)}) collective-permute-start(bf16[1,16,128,128]{3,2,1,0:T(8,128)(2,1)} %collective-permute-done.1.refs_0_), channel_id=1, source_target_pairs={{2,0},{6,4},{10,8},{14,12},{18,16},{22,20},{26,24},{30,28},{3,1},{... | collective-permute-start | bytes 1572872 | tf_op jit(solution)/shard_map/ppermute | solution.py:29
  65.1 12.5 %copy-start.17 = (bf16[1,16,128,128]{3,2,1,0:T(8,128)(2,1)}, bf16[1,16,128,128]{3,2,1,0:T(8,128)(2,1)S(1)}, u32[]{:S(2)}) copy-start(bf16[1,16,128,128]{3,2,1,0:T(8,128)(2,1)S(1)} %broadcast_select_fusion.2.refs_4_) | copy-start | bytes 1572868
  68.2 9.4 %collective-permute-start.6 = (bf16[1,16,128,128]{3,2,1,0:T(8,128)(2,1)S(1)}, bf16[1,16,128,128]{3,2,1,0:T(8,128)(2,1)S(1)}, u32[]{:S(2)}, u32[]{:S(2)}) collective-permute-start(bf16[1,16,128,128]{3,2,1,0:T(8,128)(2,1)S(1)} %broadcast_select_fusion.3.refs_2_), channel_id=1, source_target_pairs={{0,2},{2,0},{4,6},{6,4},{8,10},{10,8},{12,14},{14,12},{16,18},{18,... | collective-permute-start | bytes 1572872 | tf_op jit(solution)/shard_map/ppermute | solution.py:24
  72.5 4.2 %collective-permute-start.13 = (bf16[1,16,128,128]{3,2,1,0:T(8,128)(2,1)}, bf16[1,16,128,128]{3,2,1,0:T(8,128)(2,1)S(1)}, u32[]{:S(2)}, u32[]{:S(2)}) collective-permute-start(bf16[1,16,128,128]{3,2,1,0:T(8,128)(2,1)} %collective-permute-done.11.refs_6_), channel_id=1, source_target_pairs={{2,0},{6,4},{10,8},{14,12},{18,16},{22,20},{26,24},{30,28},{3,1},{... | collective-permute-start | bytes 1572872 | tf_op jit(solution)/shard_map/ppermute | solution.py:29
  74.0 3.8 %copy-start.18 = (bf16[1,16,128,128]{3,2,1,0:T(8,128)(2,1)}, bf16[1,16,128,128]{3,2,1,0:T(8,128)(2,1)S(1)}, u32[]{:S(2)}) copy-start(bf16[1,16,128,128]{3,2,1,0:T(8,128)(2,1)S(1)} %broadcast_select_fusion.refs_10_) | copy-start | bytes 1572868
  74.1 3.5 %collective-permute-start.16 = (bf16[1,16,128,128]{3,2,1,0:T(8,128)(2,1)S(1)}, bf16[1,16,128,128]{3,2,1,0:T(8,128)(2,1)S(1)}, u32[]{:S(2)}, u32[]{:S(2)}) collective-permute-start(bf16[1,16,128,128]{3,2,1,0:T(8,128)(2,1)S(1)} %broadcast_select_fusion.1.refs_8_), channel_id=1, source_target_pairs={{0,2},{2,0},{4,6},{6,4},{8,10},{10,8},{12,14},{14,12},{16,18},{18,... | collective-permute-start | bytes 1572872 | tf_op jit(solution)/shard_map/ppermute | solution.py:24
  75.3 2.5 %collective-permute-start.9 = (bf16[1,16,128,128]{3,2,1,0:T(8,128)(2,1)S(1)}, bf16[1,16,128,128]{3,2,1,0:T(8,128)(2,1)S(1)}, u32[]{:S(2)}, u32[]{:S(2)}) collective-permute-start(bf16[1,16,128,128]{3,2,1,0:T(8,128)(2,1)S(1)} %broadcast_select_fusion.2.refs_4_), channel_id=1, source_target_pairs={{0,2},{2,0},{4,6},{6,4},{8,10},{10,8},{12,14},{14,12},{16,18},{18,... | collective-permute-start | bytes 1572872 | tf_op jit(solution)/shard_map/ppermute | solution.py:24
  75.4 3.2 %collective-permute-start.19 = (bf16[1,16,128,128]{3,2,1,0:T(8,128)(2,1)S(1)}, bf16[1,16,128,128]{3,2,1,0:T(8,128)(2,1)S(1)}, u32[]{:S(2)}, u32[]{:S(2)}) collective-permute-start(bf16[1,16,128,128]{3,2,1,0:T(8,128)(2,1)S(1)} %broadcast_select_fusion.refs_10_), channel_id=1, source_target_pairs={{0,2},{2,0},{4,6},{6,4},{8,10},{10,8},{12,14},{14,12},{16,18},{18,... | collective-permute-start | bytes 1572872 | tf_op jit(solution)/shard_map/ppermute | solution.py:24
  77.5 1.0 copy-start.22
  77.5 1.8 copy-start.23
  77.8 1.6 copy-start.24
  78.5 0.8 copy-start.25
  101.1 5.9 %copy-start.10 = (bf16[1,16,128,128]{3,2,1,0:T(8,128)(2,1)S(1)}, bf16[1,16,128,128]{3,2,1,0:T(8,128)(2,1)}, u32[]{:S(2)}) copy-start(bf16[1,16,128,128]{3,2,1,0:T(8,128)(2,1)} %get-tuple-element.32) | copy-start | bytes 1572868
  101.1 2.2 %collective-permute-start.20 = (bf16[1,16,128,128]{3,2,1,0:T(8,128)(2,1)}, bf16[1,16,128,128]{3,2,1,0:T(8,128)(2,1)S(1)}, u32[]{:S(2)}, u32[]{:S(2)}) collective-permute-start(bf16[1,16,128,128]{3,2,1,0:T(8,128)(2,1)} %get-tuple-element.29), channel_id=1, source_target_pairs={{0,2},{2,0},{4,6},{6,4},{8,10},{10,8},{12,14},{14,12},{16,18},{18,... | collective-permute-start | bytes 1572872 | tf_op jit(solution)/shard_map/ppermute | solution.py:24
  101.3 4.2 %collective-permute-start.21 = (bf16[1,16,128,128]{3,2,1,0:T(8,128)(2,1)}, bf16[1,16,128,128]{3,2,1,0:T(8,128)(2,1)S(1)}, u32[]{:S(2)}, u32[]{:S(2)}) collective-permute-start(bf16[1,16,128,128]{3,2,1,0:T(8,128)(2,1)} %get-tuple-element.31), channel_id=1, source_target_pairs={{0,2},{2,0},{4,6},{6,4},{8,10},{10,8},{12,14},{14,12},{16,18},{18,... | collective-permute-start | bytes 1572872 | tf_op jit(solution)/shard_map/ppermute | solution.py:24
  101.7 7.4 %collective-permute-start.24 = (bf16[1,16,128,128]{3,2,1,0:T(8,128)(2,1)}, bf16[1,16,128,128]{3,2,1,0:T(8,128)(2,1)S(1)}, u32[]{:S(2)}, u32[]{:S(2)}) collective-permute-start(bf16[1,16,128,128]{3,2,1,0:T(8,128)(2,1)} %collective-permute-done.refs_2_), channel_id=1, source_target_pairs={{0,2},{2,0},{4,6},{6,4},{8,10},{10,8},{12,14},{14,12},{16,18},{18,... | collective-permute-start | bytes 1572872 | tf_op jit(solution)/shard_map/ppermute | solution.py:24
  101.8 9.9 %collective-permute-start.25 = (bf16[1,16,128,128]{3,2,1,0:T(8,128)(2,1)}, bf16[1,16,128,128]{3,2,1,0:T(8,128)(2,1)}, u32[]{:S(2)}, u32[]{:S(2)}) collective-permute-start(bf16[1,16,128,128]{3,2,1,0:T(8,128)(2,1)} %collective-permute-done.10.refs_5_), channel_id=1, source_target_pairs={{0,2},{2,0},{4,6},{6,4},{8,10},{10,8},{12,14},{14,12},{16,18},{18,... | collective-permute-start | bytes 1572872 | tf_op jit(solution)/shard_map/ppermute | solution.py:24
  102.2 4.8 %collective-permute-start.22 = (bf16[1,16,128,128]{3,2,1,0:T(8,128)(2,1)}, bf16[1,16,128,128]{3,2,1,0:T(8,128)(2,1)S(1)}, u32[]{:S(2)}, u32[]{:S(2)}) collective-permute-start(bf16[1,16,128,128]{3,2,1,0:T(8,128)(2,1)} %get-tuple-element.33), channel_id=1, source_target_pairs={{0,2},{2,0},{4,6},{6,4},{8,10},{10,8},{12,14},{14,12},{16,18},{18,... | collective-permute-start | bytes 1572872 | tf_op jit(solution)/shard_map/ppermute | solution.py:24
  103.3 4.7 %collective-permute-start.23 = (bf16[1,16,128,128]{3,2,1,0:T(8,128)(2,1)}, bf16[1,16,128,128]{3,2,1,0:T(8,128)(2,1)S(1)}, u32[]{:S(2)}, u32[]{:S(2)}) collective-permute-start(bf16[1,16,128,128]{3,2,1,0:T(8,128)(2,1)} %get-tuple-element.35), channel_id=1, source_target_pairs={{0,2},{2,0},{4,6},{6,4},{8,10},{10,8},{12,14},{14,12},{16,18},{18,... | collective-permute-start | bytes 1572872 | tf_op jit(solution)/shard_map/ppermute | solution.py:24
  103.4 4.6 %copy-start.9 = (bf16[1,16,128,128]{3,2,1,0:T(8,128)(2,1)S(1)}, bf16[1,16,128,128]{3,2,1,0:T(8,128)(2,1)}, u32[]{:S(2)}) copy-start(bf16[1,16,128,128]{3,2,1,0:T(8,128)(2,1)} %get-tuple-element.34) | copy-start | bytes 1572868
  105.5 19.2 %collective-permute-start.26 = (bf16[1,16,128,128]{3,2,1,0:T(8,128)(2,1)}, bf16[1,16,128,128]{3,2,1,0:T(8,128)(2,1)S(1)}, u32[]{:S(2)}, u32[]{:S(2)}) collective-permute-start(bf16[1,16,128,128]{3,2,1,0:T(8,128)(2,1)} %get-tuple-element.40), channel_id=1, source_target_pairs={{0,2},{2,0},{4,6},{6,4},{8,10},{10,8},{12,14},{14,12},{16,18},{18,... | collective-permute-start | bytes 1572872 | tf_op jit(solution)/shard_map/ppermute | solution.py:24
  109.0 16.0 %collective-permute-start.29 = (bf16[1,16,128,128]{3,2,1,0:T(8,128)(2,1)S(1)}, bf16[1,16,128,128]{3,2,1,0:T(8,128)(2,1)S(1)}, u32[]{:S(2)}, u32[]{:S(2)}) collective-permute-start(bf16[1,16,128,128]{3,2,1,0:T(8,128)(2,1)S(1)} %add_convert_fusion.2), channel_id=1, source_target_pairs={{0,4},{2,6},{4,0},{6,2},{8,12},{10,14},{12,8},{14,10},{16,20},{18,... | collective-permute-start | bytes 1572872 | tf_op jit(solution)/shard_map/ppermute | solution.py:24
  109.0 19.4 %collective-permute-start.32 = (bf16[1,16,128,128]{3,2,1,0:T(8,128)(2,1)}, bf16[1,16,128,128]{3,2,1,0:T(8,128)(2,1)S(1)}, u32[]{:S(2)}, u32[]{:S(2)}) collective-permute-start(bf16[1,16,128,128]{3,2,1,0:T(8,128)(2,1)} %get-tuple-element.47), channel_id=1, source_target_pairs={{0,2},{2,0},{4,6},{6,4},{8,10},{10,8},{12,14},{14,12},{16,18},{18,... | collective-permute-start | bytes 1572872 | tf_op jit(solution)/shard_map/ppermute | solution.py:24
  109.1 2.6 %copy-start.21 = (bf16[1,16,128,128]{3,2,1,0:T(8,128)(2,1)}, bf16[1,16,128,128]{3,2,1,0:T(8,128)(2,1)S(1)}, u32[]{:S(2)}) copy-start(bf16[1,16,128,128]{3,2,1,0:T(8,128)(2,1)S(1)} %collective-permute-done.24.refs_3_) | copy-start | bytes 1572868
  109.1 25.9 %collective-permute-start.35 = (bf16[1,16,128,128]{3,2,1,0:T(8,128)(2,1)}, bf16[1,16,128,128]{3,2,1,0:T(8,128)(2,1)S(1)}, u32[]{:S(2)}, u32[]{:S(2)}) collective-permute-start(bf16[1,16,128,128]{3,2,1,0:T(8,128)(2,1)} %add_convert_fusion), channel_id=1, source_target_pairs={{0,4},{2,6},{4,0},{6,2},{8,12},{10,14},{12,8},{14,10},{16,20},{18,... | collective-permute-start | bytes 1572872 | tf_op jit(solution)/shard_map/ppermute | solution.py:24
  111.7 34.5 %collective-permute-start.27 = (bf16[1,16,128,128]{3,2,1,0:T(8,128)(2,1)}, bf16[1,16,128,128]{3,2,1,0:T(8,128)(2,1)S(1)}, u32[]{:S(2)}, u32[]{:S(2)}) collective-permute-start(bf16[1,16,128,128]{3,2,1,0:T(8,128)(2,1)} %add_convert_fusion.3), channel_id=1, source_target_pairs={{0,4},{2,6},{4,0},{6,2},{8,12},{10,14},{12,8},{14,10},{16,20},{18,... | collective-permute-start | bytes 1572872 | tf_op jit(solution)/shard_map/ppermute | solution.py:24
  124.7 10.3 %copy-start.19 = (bf16[1,16,128,128]{3,2,1,0:T(8,128)(2,1)S(1)}, bf16[1,16,128,128]{3,2,1,0:T(8,128)(2,1)}, u32[]{:S(2)}) copy-start(bf16[1,16,128,128]{3,2,1,0:T(8,128)(2,1)} %get-tuple-element.52) | copy-start | bytes 1572868
  124.7 22.8 %collective-permute-start.28 = (bf16[1,16,128,128]{3,2,1,0:T(8,128)(2,1)}, bf16[1,16,128,128]{3,2,1,0:T(8,128)(2,1)}, u32[]{:S(2)}, u32[]{:S(2)}) collective-permute-start(bf16[1,16,128,128]{3,2,1,0:T(8,128)(2,1)} %get-tuple-element.43), channel_id=1, source_target_pairs={{0,2},{2,0},{4,6},{6,4},{8,10},{10,8},{12,14},{14,12},{16,18},{18,... | collective-permute-start | bytes 1572872 | tf_op jit(solution)/shard_map/ppermute | solution.py:24
  127.1 20.5 %collective-permute-start.30 = (bf16[1,16,128,128]{3,2,1,0:T(8,128)(2,1)}, bf16[1,16,128,128]{3,2,1,0:T(8,128)(2,1)}, u32[]{:S(2)}, u32[]{:S(2)}) collective-permute-start(bf16[1,16,128,128]{3,2,1,0:T(8,128)(2,1)} %fusion.7), channel_id=1, source_target_pairs={{8,0},{10,2},{12,4},{14,6},{16,8},{18,10},{20,12},{22,14},{24,16},... | collective-permute-start | bytes 1572872 | tf_op jit(solution)/shard_map/ppermute | solution.py:20
  128.4 28.3 %collective-permute-start.33 = (bf16[1,16,128,128]{3,2,1,0:T(8,128)(2,1)}, bf16[1,16,128,128]{3,2,1,0:T(8,128)(2,1)S(1)}, u32[]{:S(2)}, u32[]{:S(2)}) collective-permute-start(bf16[1,16,128,128]{3,2,1,0:T(8,128)(2,1)} %add_convert_fusion.1), channel_id=1, source_target_pairs={{0,4},{2,6},{4,0},{6,2},{8,12},{10,14},{12,8},{14,10},{16,20},{18,... | collective-permute-start | bytes 1572872 | tf_op jit(solution)/shard_map/ppermute | solution.py:24
  135.0 21.7 %collective-permute-start.34 = (bf16[1,16,128,128]{3,2,1,0:T(8,128)(2,1)}, bf16[1,16,128,128]{3,2,1,0:T(8,128)(2,1)}, u32[]{:S(2)}, u32[]{:S(2)}) collective-permute-start(bf16[1,16,128,128]{3,2,1,0:T(8,128)(2,1)} %get-tuple-element.50), channel_id=1, source_target_pairs={{0,2},{2,0},{4,6},{6,4},{8,10},{10,8},{12,14},{14,12},{16,18},{18,... | collective-permute-start | bytes 1572872 | tf_op jit(solution)/shard_map/ppermute | solution.py:24
  146.2 19.5 %copy-start.2 = (bf16[1,16,128,128]{3,2,1,0:T(8,128)(2,1)}, bf16[1,16,128,128]{3,2,1,0:T(8,128)(2,1)S(1)}, u32[]{:S(2)}) copy-start(bf16[1,16,128,128]{3,2,1,0:T(8,128)(2,1)S(1)} %collective-permute-done.27) | copy-start | bytes 1572868
  146.2 17.1 %collective-permute-start.36 = (bf16[1,16,128,128]{3,2,1,0:T(8,128)(2,1)}, bf16[1,16,128,128]{3,2,1,0:T(8,128)(2,1)}, u32[]{:S(2)}, u32[]{:S(2)}) collective-permute-start(bf16[1,16,128,128]{3,2,1,0:T(8,128)(2,1)} %fusion.18), channel_id=1, source_target_pairs={{8,0},{10,2},{12,4},{14,6},{16,8},{18,10},{20,12},{22,14},{24,16},... | collective-permute-start | bytes 1572872 | tf_op jit(solution)/shard_map/ppermute | solution.py:20
  147.5 15.8 %copy-start.20 = (bf16[1,16,128,128]{3,2,1,0:T(8,128)(2,1)S(1)}, bf16[1,16,128,128]{3,2,1,0:T(8,128)(2,1)}, u32[]{:S(2)}) copy-start(bf16[1,16,128,128]{3,2,1,0:T(8,128)(2,1)} %get-tuple-element.49) | copy-start | bytes 1572868
  150.2 16.8 %copy-start.1 = (f32[16,128,256]{2,1,0:T(8,128)S(1)}, f32[16,128,256]{2,1,0:T(8,128)}, u32[]{:S(2)}) copy-start(f32[16,128,256]{2,1,0:T(8,128)} %get-tuple-element.38) | copy-start | bytes 6291460
  150.2 24.3 %collective-permute-start.31 = (bf16[128,16,128]{2,0,1:T(8,128)(2,1)}, bf16[128,16,128]{2,0,1:T(8,128)(2,1)}, u32[]{:S(2)}, u32[]{:S(2)}) collective-permute-start(bf16[128,16,128]{2,0,1:T(8,128)(2,1)} %fusion.23), channel_id=1, source_target_pairs={{8,0},{10,2},{12,4},{14,6},{16,8},{18,10},{20,12},{22,14},{24,16},... | collective-permute-start | bytes 1572872 | tf_op jit(solution)/shard_map/ppermute | solution.py:20
  156.7 10.3 %copy-start.4 = (bf16[1,16,128,128]{3,2,1,0:T(8,128)(2,1)}, bf16[1,16,128,128]{3,2,1,0:T(8,128)(2,1)S(1)}, u32[]{:S(2)}) copy-start(bf16[1,16,128,128]{3,2,1,0:T(8,128)(2,1)S(1)} %collective-permute-done.33) | copy-start | bytes 1572868
  165.7 17.5 %collective-permute-start.37 = (bf16[128,16,128]{2,0,1:T(8,128)(2,1)}, bf16[128,16,128]{2,0,1:T(8,128)(2,1)}, u32[]{:S(2)}, u32[]{:S(2)}) collective-permute-start(bf16[128,16,128]{2,0,1:T(8,128)(2,1)} %fusion.22), channel_id=1, source_target_pairs={{8,0},{10,2},{12,4},{14,6},{16,8},{18,10},{20,12},{22,14},{24,16},... | collective-permute-start | bytes 1572872 | tf_op jit(solution)/shard_map/ppermute | solution.py:20
  167.6 6.9 %copy-start.3 = (bf16[1,16,128,128]{3,2,1,0:T(8,128)(2,1)S(1)}, bf16[1,16,128,128]{3,2,1,0:T(8,128)(2,1)}, u32[]{:S(2)}) copy-start(bf16[1,16,128,128]{3,2,1,0:T(8,128)(2,1)} %copy-done.2) | copy-start | bytes 1572868
  171.3 11.9 %copy-start.5 = (bf16[1,16,128,128]{3,2,1,0:T(8,128)(2,1)S(1)}, bf16[1,16,128,128]{3,2,1,0:T(8,128)(2,1)}, u32[]{:S(2)}) copy-start(bf16[1,16,128,128]{3,2,1,0:T(8,128)(2,1)} %copy-done.4) | copy-start | bytes 1572868
  171.4 11.9 %copy-start.8 = (bf16[1,16,128,128]{3,2,1,0:T(8,128)(2,1)S(1)}, bf16[1,16,128,128]{3,2,1,0:T(8,128)(2,1)}, u32[]{:S(2)}) copy-start(bf16[1,16,128,128]{3,2,1,0:T(8,128)(2,1)} %get-tuple-element.46) | copy-start | bytes 1572868

commit v15 on v14

--- a/solution.py
+++ b/solution.py
@@ -10,7 +10,7 @@
 WINDOW = 1024
 HOPS = 8
 PLANE = 4
-HEADS_PER_STEP = 4
+HEADS_PER_STEP = 8
 
 SCALE = 168.0 ** (-0.5)
 

time: 187 us -> 187 us (level)
  no operation moved by 1% of the time
where the time goes in v15:
time: 187 us; the launch traced here: 186 us
  starting transfers between devices  60.4 us (32%)
  waiting for transfers between devices  52.4 us (28%)
  Pallas kernels  35.9 us (19%)
  other arithmetic  22.5 us (12%)
  local copies, waits for them, and re-layouts  14.1 us (8%)
    pallas_call x2, Pallas kernels, attend_blocks(): pl.pallas_call(functools.partial(_blocks_kernel, tuple(modes), acc is not...  35.9 us
    ppermute x12, starting transfers between devices, one_way(): return lax.ppermute(x, 'seq', pairs)  29 us
    ppermute x8, starting transfers between devices, shift(): return lax.ppermute(x, 'seq', pairs)  23.6 us
    ppermute x18, waiting for transfers between devices, swap(): return lax.ppermute(x, 'seq', [(i, i ^ bit) for i in range(n)])  21.3 us
    ppermute x8, waiting for transfers between devices, shift(): return lax.ppermute(x, 'seq', pairs)  19.2 us
    ppermute x12, waiting for transfers between devices, one_way(): return lax.ppermute(x, 'seq', pairs)  11.9 us
    ppermute x18, starting transfers between devices, swap(): return lax.ppermute(x, 'seq', [(i, i ^ bit) for i in range(n)])  7.81 us
    unnamed x56, local copies, waits for them, and re-layouts  6.47 us
  transfers between devices with their start and end apart: 38, of which 14 were waited for; matrix products, arithmetic and copies ran while one was open for 17% of the time, Pallas kernels for 7%

profile of v15, /device:TPU:0, one launch (start us, length us, event | category | flops | bytes accessed | tf_op | source)
XLA Modules:
  0.0 186.5 jit_solution(6116391091975843387)
XLA Ops:
  0.7 1.3 copy.27
  2.0 5.7 %collective-permute-start = (bf16[1,16,128,128]{3,2,1,0:T(8,128)(2,1)S(1)}, bf16[1,16,128,128]{3,2,1,0:T(8,128)(2,1)}, u32[]{:S(2)}, u32[]{:S(2)}) collective-permute-start(bf16[1,16,128,128]{3,2,1,0:T(8,128)(2,1)S(1)} %bitcast.60), channel_id=1, source_target_pairs={{0,8},{2,10},{4,12},{6,14},{8,16},{10,18},{12,20},{14,22},{16,24},... | collective-permute-start | bytes 1572872 | tf_op jit(solution)/shard_map/ppermute | solution.py:20
  7.7 1.2 copy.26
  8.9 3.5 %collective-permute-start.10 = (bf16[1,16,128,128]{3,2,1,0:T(8,128)(2,1)S(1)}, bf16[1,16,128,128]{3,2,1,0:T(8,128)(2,1)}, u32[]{:S(2)}, u32[]{:S(2)}) collective-permute-start(bf16[1,16,128,128]{3,2,1,0:T(8,128)(2,1)S(1)} %bitcast.64), channel_id=1, source_target_pairs={{0,8},{2,10},{4,12},{6,14},{8,16},{10,18},{12,20},{14,22},{16,24},... | collective-permute-start | bytes 1572872 | tf_op jit(solution)/shard_map/ppermute | solution.py:20
  12.4 3.4 %collective-permute-start.4 = (bf16[1,16,128,128]{3,2,1,0:T(8,128)(2,1)S(1)}, bf16[1,16,128,128]{3,2,1,0:T(8,128)(2,1)S(1)}, u32[]{:S(2)}, u32[]{:S(2)}) collective-permute-start(bf16[1,16,128,128]{3,2,1,0:T(8,128)(2,1)S(1)} %bitcast.61), channel_id=1, source_target_pairs={{0,4},{2,6},{8,12},{10,14},{16,20},{18,22},{24,28},{26,30},{1,5},{... | collective-permute-start | bytes 1572872 | tf_op jit(solution)/shard_map/ppermute | solution.py:29
  15.9 3.4 %collective-permute-done.refs_2_ = bf16[1,16,128,128]{3,2,1,0:T(8,128)(2,1)} collective-permute-done((bf16[1,16,128,128]{3,2,1,0:T(8,128)(2,1)S(1)}, bf16[1,16,128,128]{3,2,1,0:T(8,128)(2,1)}, u32[]{:S(2)}, u32[]{:S(2)}) %collective-permute-start) | collective-permute-done | bytes 524320 | tf_op jit(solution)/shard_map/ppermute | solution.py:20
  19.2 5.3 %collective-permute-start.1 = (bf16[1,16,128,128]{3,2,1,0:T(8,128)(2,1)}, bf16[1,16,128,128]{3,2,1,0:T(8,128)(2,1)}, u32[]{:S(2)}, u32[]{:S(2)}) collective-permute-start(bf16[1,16,128,128]{3,2,1,0:T(8,128)(2,1)} %collective-permute-done.refs_2_), channel_id=1, source_target_pairs={{0,8},{2,10},{4,12},{6,14},{8,16},{10,18},{12,20},{14,22},{16,24},... | collective-permute-start | bytes 1572872 | tf_op jit(solution)/shard_map/ppermute | solution.py:20
  24.5 1.3 collective-permute-start.5
  25.8 6.2 %collective-permute-start.14 = (bf16[1,16,128,128]{3,2,1,0:T(8,128)(2,1)S(1)}, bf16[1,16,128,128]{3,2,1,0:T(8,128)(2,1)}, u32[]{:S(2)}, u32[]{:S(2)}) collective-permute-start(bf16[1,16,128,128]{3,2,1,0:T(8,128)(2,1)S(1)} %bitcast.65), channel_id=1, source_target_pairs={{0,4},{2,6},{8,12},{10,14},{16,20},{18,22},{24,28},{26,30},{1,5},{... | collective-permute-start | bytes 1572872 | tf_op jit(solution)/shard_map/ppermute | solution.py:29
  32.0 3.8 %collective-permute-start.11 = (bf16[1,16,128,128]{3,2,1,0:T(8,128)(2,1)}, bf16[1,16,128,128]{3,2,1,0:T(8,128)(2,1)}, u32[]{:S(2)}, u32[]{:S(2)}) collective-permute-start(bf16[1,16,128,128]{3,2,1,0:T(8,128)(2,1)} %collective-permute-done.10.refs_5_), channel_id=1, source_target_pairs={{0,8},{2,10},{4,12},{6,14},{8,16},{10,18},{12,20},{14,22},{16,24},... | collective-permute-start | bytes 1572872 | tf_op jit(solution)/shard_map/ppermute | solution.py:20
  35.8 0.8 copy-done.13
  36.6 1.3 collective-permute-start.15
  38.6 1.4 copy.16
  40.0 1.4 copy.17
  41.4 0.6 multiply_reduce_fusion
  42.0 0.7 copy.18
  42.7 5.3 %collective-permute-start.7 = (bf16[1,16,128,128]{3,2,1,0:T(8,128)(2,1)}, bf16[1,16,128,128]{3,2,1,0:T(8,128)(2,1)S(1)}, u32[]{:S(2)}, u32[]{:S(2)}) collective-permute-start(bf16[1,16,128,128]{3,2,1,0:T(8,128)(2,1)} %collective-permute-done.refs_2_), channel_id=1, source_target_pairs={{0,4},{2,6},{8,12},{10,14},{16,20},{18,22},{24,28},{26,30},{1,5},{... | collective-permute-start | bytes 1572872 | tf_op jit(solution)/shard_map/ppermute | solution.py:29
  48.1 1.3 collective-permute-start.8
  49.4 1.1 broadcast_select_fusion.3.refs_2_
  50.5 1.3 collective-permute-start.2
  51.9 3.5 %collective-permute-start.17 = (bf16[1,16,128,128]{3,2,1,0:T(8,128)(2,1)}, bf16[1,16,128,128]{3,2,1,0:T(8,128)(2,1)S(1)}, u32[]{:S(2)}, u32[]{:S(2)}) collective-permute-start(bf16[1,16,128,128]{3,2,1,0:T(8,128)(2,1)} %collective-permute-done.10.refs_5_), channel_id=1, source_target_pairs={{0,4},{2,6},{8,12},{10,14},{16,20},{18,22},{24,28},{26,30},{1,5},{... | collective-permute-start | bytes 1572872 | tf_op jit(solution)/shard_map/ppermute | solution.py:29
  55.5 1.3 collective-permute-start.18
  56.8 1.1 broadcast_select_fusion.1.refs_8_
  57.9 1.2 collective-permute-done.7
  59.1 1.3 collective-permute-start.12
  60.4 3.3 %collective-permute-done.8 = bf16[1,16,128,128]{3,2,1,0:T(8,128)(2,1)S(1)} collective-permute-done((bf16[1,16,128,128]{3,2,1,0:T(8,128)(2,1)}, bf16[1,16,128,128]{3,2,1,0:T(8,128)(2,1)S(1)}, u32[]{:S(2)}, u32[]{:S(2)}) %collective-permute-start.8) | collective-permute-done | bytes 524320 | tf_op jit(solution)/shard_map/ppermute | solution.py:29
  63.7 1.3 collective-permute-start.3
  65.1 3.1 %collective-permute-done.17 = bf16[1,16,128,128]{3,2,1,0:T(8,128)(2,1)S(1)} collective-permute-done((bf16[1,16,128,128]{3,2,1,0:T(8,128)(2,1)}, bf16[1,16,128,128]{3,2,1,0:T(8,128)(2,1)S(1)}, u32[]{:S(2)}, u32[]{:S(2)}) %collective-permute-start.17) | collective-permute-done | bytes 524320 | tf_op jit(solution)/shard_map/ppermute | solution.py:29
  68.2 4.3 %collective-permute-done.18 = bf16[1,16,128,128]{3,2,1,0:T(8,128)(2,1)S(1)} collective-permute-done((bf16[1,16,128,128]{3,2,1,0:T(8,128)(2,1)}, bf16[1,16,128,128]{3,2,1,0:T(8,128)(2,1)S(1)}, u32[]{:S(2)}, u32[]{:S(2)}) %collective-permute-start.18) | collective-permute-done | bytes 524320 | tf_op jit(solution)/shard_map/ppermute | solution.py:29
  72.5 1.5 collective-permute-start.13
  74.1 1.2 collective-permute-start.16
  75.8 0.8 broadcast_select_fusion.5.refs_1_
  76.7 0.9 broadcast_select_fusion.4.refs_7_
  77.8 0.7 collective-permute-done.19.refs_11_
  78.5 0.8 copy-done.25
  79.4 22.4 %shard_map.85 = (f32[16,128,256]{2,1,0:T(8,128)}, bf16[1,16,128,128]{3,2,1,0:T(8,128)(2,1)}, bf16[1,16,128,128]{3,2,1,0:T(8,128)(2,1)}, bf16[1,16,128,128]{3,2,1...) custom-call(s32[6]{0:T(128)} %stack.58.valid_ref, ...), custom_call_target="tpu_custom_call" | custom-call | flops 4026531840 | bytes 14680064 | tf_op jit(solution)/shard_map/pallas_call | solution.py:105
  103.0 0.9 collective-permute-done.20
  104.1 2.0 %add_convert_fusion.3 = bf16[1,16,128,128]{3,2,1,0:T(8,128)(2,1)} fusion(bf16[1,16,128,128]{3,2,1,0:T(8,128)(2,1)S(1)} %collective-permute-done.20, bf16[1,16,128,128]{3,2,1,0:T(8,128)(2,1)} %get-tuple-element.28), kind=kLoop, calls=%fused_computation.37 | loop fusion | flops 1048576 | bytes 1572864 | tf_op jit(solution)/shard_map/convert_element_type | solution.py:137
  106.5 1.2 add_convert_fusion.2
  107.7 1.0 add_convert_fusion.1
  108.7 1.0 add_convert_fusion
  109.8 1.9 %collective-permute-start.35 = (bf16[1,16,128,128]{3,2,1,0:T(8,128)(2,1)}, bf16[1,16,128,128]{3,2,1,0:T(8,128)(2,1)S(1)}, u32[]{:S(2)}, u32[]{:S(2)}) collective-permute-start(bf16[1,16,128,128]{3,2,1,0:T(8,128)(2,1)} %add_convert_fusion), channel_id=1, source_target_pairs={{0,4},{2,6},{4,0},{6,2},{8,12},{10,14},{12,8},{14,10},{16,20},{18,... | collective-permute-start | bytes 1572872 | tf_op jit(solution)/shard_map/ppermute | solution.py:24
  111.7 0.7 add_convert_fusion.4.valid_ref
  112.5 13.5 %shard_map.86 = (f32[16,128,256]{2,1,0:T(8,128)}, bf16[1,16,128,128]{3,2,1,0:T(8,128)(2,1)}, bf16[1,16,128,128]{3,2,1,0:T(8,128)(2,1)}, bf16[1,16,128,128]{3,2,1...) custom-call(s32[3]{0:T(128)} %add_convert_fusion.4.valid_ref, ...), custom_call_target="tpu_custom_call" | custom-call | flops 2013265920 | bytes 10485760 | tf_op jit(solution)/shard_map/pallas_call | solution.py:105
  126.3 2.1 %fusion.7 = bf16[1,16,128,128]{3,2,1,0:T(8,128)(2,1)} fusion(bf16[1,16,128,128]{3,2,1,0:T(8,128)(2,1)S(1)} %collective-permute-done.26, bf16[1,16,128,128]{3,2,1,0:T(8,128)(2,1)S(1)} %collective-permute-done.29, bf16[1,16,128,128]{3,2,1,0:T(8,128)(2,1)} %get-tuple-element.45, pred[]{:T(512)S(6)} %eq.26, pred[]{:T(512)S(6)} %eq.11), kind=kLoop, calls=%fused_computation.19 | loop fusion | flops 2097152 | bytes 2097154 | tf_op jit(solution)/shard_map/convert_element_type | solution.py:154
  128.4 1.3 collective-permute-start.30
  129.7 1.9 collective-permute-start.33
  131.6 4.1 %collective-permute-done.35 = bf16[1,16,128,128]{3,2,1,0:T(8,128)(2,1)S(1)} collective-permute-done((bf16[1,16,128,128]{3,2,1,0:T(8,128)(2,1)}, bf16[1,16,128,128]{3,2,1,0:T(8,128)(2,1)S(1)}, u32[]{:S(2)}, u32[]{:S(2)}) %collective-permute-start.35) | collective-permute-done | bytes 524320 | tf_op jit(solution)/shard_map/ppermute | solution.py:24
  135.6 1.1 fusion.18
  136.7 10.2 %collective-permute-done.27 = bf16[1,16,128,128]{3,2,1,0:T(8,128)(2,1)S(1)} collective-permute-done((bf16[1,16,128,128]{3,2,1,0:T(8,128)(2,1)}, bf16[1,16,128,128]{3,2,1,0:T(8,128)(2,1)S(1)}, u32[]{:S(2)}, u32[]{:S(2)}) %collective-permute-start.27) | collective-permute-done | bytes 524320 | tf_op jit(solution)/shard_map/ppermute | solution.py:24
  146.9 1.3 collective-permute-start.36
  148.2 2.6 %fusion.23 = bf16[128,16,128]{2,0,1:T(8,128)(2,1)} fusion(bf16[1,16,128,128]{3,2,1,0:T(8,128)(2,1)} %collective-permute-done.30, bf16[1,16,128,128]{3,2,1,0:T(8,128)(2,1)S(1)} %collective-permute-done.27, bf16[1,16,128,128]{3,2,1,0:T(8,128)(2,1)S(1)} %collective-permute-done.29, bf16[1,16,128,128]{3,2,1,0:T(8,128)(2,1)} %collective-permute-done.28, ...), kind=kLoop, calls=%fused_computation.39 | loop fusion | flops 2621440 | bytes 3145729 | tf_op jit(solution)/shard_map/transpose | solution.py:156
  150.8 1.4 collective-permute-start.31
  152.2 5.1 %collective-permute-done.33 = bf16[1,16,128,128]{3,2,1,0:T(8,128)(2,1)S(1)} collective-permute-done((bf16[1,16,128,128]{3,2,1,0:T(8,128)(2,1)}, bf16[1,16,128,128]{3,2,1,0:T(8,128)(2,1)S(1)}, u32[]{:S(2)}, u32[]{:S(2)}) %collective-permute-start.33) | collective-permute-done | bytes 524320 | tf_op jit(solution)/shard_map/ppermute | solution.py:24
  157.3 6.6 %collective-permute-done.36 = bf16[1,16,128,128]{3,2,1,0:T(8,128)(2,1)} collective-permute-done((bf16[1,16,128,128]{3,2,1,0:T(8,128)(2,1)}, bf16[1,16,128,128]{3,2,1,0:T(8,128)(2,1)}, u32[]{:S(2)}, u32[]{:S(2)}) %collective-permute-start.36) | collective-permute-done | bytes 524320 | tf_op jit(solution)/shard_map/ppermute | solution.py:20
  163.9 2.4 %fusion.22 = bf16[128,16,128]{2,0,1:T(8,128)(2,1)} fusion(bf16[1,16,128,128]{3,2,1,0:T(8,128)(2,1)} %collective-permute-done.36, bf16[1,16,128,128]{3,2,1,0:T(8,128)(2,1)S(1)} %collective-permute-done.33, bf16[1,16,128,128]{3,2,1,0:T(8,128)(2,1)S(1)} %collective-permute-done.35, bf16[1,16,128,128]{3,2,1,0:T(8,128)(2,1)} %collective-permute-done.34, ...), kind=kLoop, calls=%fused_computation.38 | loop fusion | flops 2621440 | bytes 3145729 | tf_op jit(solution)/shard_map/transpose | solution.py:156
  166.4 1.3 collective-permute-start.37
  168.2 3.8 %copy.21 = bf16[128,16,2,128]{3,2,1,0:T(2,128)(2,1)} copy(bf16[128,16,2,128]{0,2,3,1:T(2,128)(2,1)S(1)} %bitcast.53) | data formatting | bytes 2097152 | tf_op jit(solution)/shard_map/transpose | solution.py:200
  172.0 3.2 %collective-permute-done.31 = bf16[128,16,128]{2,0,1:T(8,128)(2,1)} collective-permute-done((bf16[128,16,128]{2,0,1:T(8,128)(2,1)}, bf16[128,16,128]{2,0,1:T(8,128)(2,1)}, u32[]{:S(2)}, u32[]{:S(2)}) %collective-permute-start.31) | collective-permute-done | bytes 524320 | tf_op jit(solution)/shard_map/ppermute | solution.py:20
  175.2 1.6 fusion.4
  176.7 1.1 copy.22
  177.9 6.0 %collective-permute-done.37 = bf16[128,16,128]{2,0,1:T(8,128)(2,1)} collective-permute-done((bf16[128,16,128]{2,0,1:T(8,128)(2,1)}, bf16[128,16,128]{2,0,1:T(8,128)(2,1)}, u32[]{:S(2)}, u32[]{:S(2)}) %collective-permute-start.37) | collective-permute-done | bytes 524320 | tf_op jit(solution)/shard_map/ppermute | solution.py:20
  183.9 1.4 fusion.15
  185.3 1.1 copy.23
  (96 shorter events, 4.6 us)
Async XLA Ops:
  0.6 38.0 %copy-start.6 = (bf16[128,32,128]{2,1,0:T(8,128)(2,1)S(1)}, bf16[128,32,128]{2,1,0:T(8,128)(2,1)}, u32[]{:S(2)}) copy-start(bf16[128,32,128]{2,1,0:T(8,128)(2,1)} %param.6) | copy-start | bytes 3145732
  0.6 39.3 %copy-start = (bf16[128,32,128]{2,1,0:T(8,128)(2,1)S(1)}, bf16[128,32,128]{2,1,0:T(8,128)(2,1)}, u32[]{:S(2)}) copy-start(bf16[128,32,128]{2,1,0:T(8,128)(2,1)} %param.10) | copy-start | bytes 3145732
  2.0 48.5 %copy-start.11 = (bf16[128,16,128]{2,0,1:T(8,128)(2,1)}, bf16[128,16,128]{2,0,1:T(8,128)(2,1)S(1)}, u32[]{:S(2)}) copy-start(bf16[128,16,128]{2,0,1:T(8,128)(2,1)S(1)} %copy.27) | copy-start | bytes 1572868
  2.0 17.2 %collective-permute-start = (bf16[1,16,128,128]{3,2,1,0:T(8,128)(2,1)S(1)}, bf16[1,16,128,128]{3,2,1,0:T(8,128)(2,1)}, u32[]{:S(2)}, u32[]{:S(2)}) collective-permute-start(bf16[1,16,128,128]{3,2,1,0:T(8,128)(2,1)S(1)} %bitcast.60), channel_id=1, source_target_pairs={{0,8},{2,10},{4,12},{6,14},{8,16},{10,18},{12,20},{14,22},{16,24},... | collective-permute-start | bytes 1572872 | tf_op jit(solution)/shard_map/ppermute | solution.py:20
  8.9 50.2 %copy-start.12 = (bf16[128,16,128]{2,0,1:T(8,128)(2,1)}, bf16[128,16,128]{2,0,1:T(8,128)(2,1)S(1)}, u32[]{:S(2)}) copy-start(bf16[128,16,128]{2,0,1:T(8,128)(2,1)S(1)} %copy.26) | copy-start | bytes 1572868
  8.9 23.0 %collective-permute-start.10 = (bf16[1,16,128,128]{3,2,1,0:T(8,128)(2,1)S(1)}, bf16[1,16,128,128]{3,2,1,0:T(8,128)(2,1)}, u32[]{:S(2)}, u32[]{:S(2)}) collective-permute-start(bf16[1,16,128,128]{3,2,1,0:T(8,128)(2,1)S(1)} %bitcast.64), channel_id=1, source_target_pairs={{0,8},{2,10},{4,12},{6,14},{8,16},{10,18},{12,20},{14,22},{16,24},... | collective-permute-start | bytes 1572872 | tf_op jit(solution)/shard_map/ppermute | solution.py:20
  12.4 23.3 %collective-permute-start.4 = (bf16[1,16,128,128]{3,2,1,0:T(8,128)(2,1)S(1)}, bf16[1,16,128,128]{3,2,1,0:T(8,128)(2,1)S(1)}, u32[]{:S(2)}, u32[]{:S(2)}) collective-permute-start(bf16[1,16,128,128]{3,2,1,0:T(8,128)(2,1)S(1)} %bitcast.61), channel_id=1, source_target_pairs={{0,4},{2,6},{8,12},{10,14},{16,20},{18,22},{24,28},{26,30},{1,5},{... | collective-permute-start | bytes 1572872 | tf_op jit(solution)/shard_map/ppermute | solution.py:29
  19.2 23.5 %collective-permute-start.1 = (bf16[1,16,128,128]{3,2,1,0:T(8,128)(2,1)}, bf16[1,16,128,128]{3,2,1,0:T(8,128)(2,1)}, u32[]{:S(2)}, u32[]{:S(2)}) collective-permute-start(bf16[1,16,128,128]{3,2,1,0:T(8,128)(2,1)} %collective-permute-done.refs_2_), channel_id=1, source_target_pairs={{0,8},{2,10},{4,12},{6,14},{8,16},{10,18},{12,20},{14,22},{16,24},... | collective-permute-start | bytes 1572872 | tf_op jit(solution)/shard_map/ppermute | solution.py:20
  24.5 23.6 %collective-permute-start.5 = (bf16[1,16,128,128]{3,2,1,0:T(8,128)(2,1)}, bf16[1,16,128,128]{3,2,1,0:T(8,128)(2,1)}, u32[]{:S(2)}, u32[]{:S(2)}) collective-permute-start(bf16[1,16,128,128]{3,2,1,0:T(8,128)(2,1)} %collective-permute-done.refs_2_), channel_id=1, source_target_pairs={{4,0},{6,2},{12,8},{14,10},{20,16},{22,18},{28,24},{30,26},{5,1},{... | collective-permute-start | bytes 1572872 | tf_op jit(solution)/shard_map/ppermute | solution.py:29
  25.8 24.7 %collective-permute-start.14 = (bf16[1,16,128,128]{3,2,1,0:T(8,128)(2,1)S(1)}, bf16[1,16,128,128]{3,2,1,0:T(8,128)(2,1)}, u32[]{:S(2)}, u32[]{:S(2)}) collective-permute-start(bf16[1,16,128,128]{3,2,1,0:T(8,128)(2,1)S(1)} %bitcast.65), channel_id=1, source_target_pairs={{0,4},{2,6},{8,12},{10,14},{16,20},{18,22},{24,28},{26,30},{1,5},{... | collective-permute-start | bytes 1572872 | tf_op jit(solution)/shard_map/ppermute | solution.py:29
  32.0 19.9 %collective-permute-start.11 = (bf16[1,16,128,128]{3,2,1,0:T(8,128)(2,1)}, bf16[1,16,128,128]{3,2,1,0:T(8,128)(2,1)}, u32[]{:S(2)}, u32[]{:S(2)}) collective-permute-start(bf16[1,16,128,128]{3,2,1,0:T(8,128)(2,1)} %collective-permute-done.10.refs_5_), channel_id=1, source_target_pairs={{0,8},{2,10},{4,12},{6,14},{8,16},{10,18},{12,20},{14,22},{16,24},... | collective-permute-start | bytes 1572872 | tf_op jit(solution)/shard_map/ppermute | solution.py:20
  35.8 0.8 copy-start.13
  36.6 18.9 %collective-permute-start.15 = (bf16[1,16,128,128]{3,2,1,0:T(8,128)(2,1)}, bf16[1,16,128,128]{3,2,1,0:T(8,128)(2,1)}, u32[]{:S(2)}, u32[]{:S(2)}) collective-permute-start(bf16[1,16,128,128]{3,2,1,0:T(8,128)(2,1)} %collective-permute-done.10.refs_5_), channel_id=1, source_target_pairs={{4,0},{6,2},{12,8},{14,10},{20,16},{22,18},{28,24},{30,26},{5,1},{... | collective-permute-start | bytes 1572872 | tf_op jit(solution)/shard_map/ppermute | solution.py:29
  38.6 2.8 %copy-start.7 = (bf16[128,32,128]{2,1,0:T(8,128)(2,1)S(1)}, bf16[128,32,128]{2,1,0:T(8,128)(2,1)}, u32[]{:S(2)}) copy-start(bf16[128,32,128]{2,1,0:T(8,128)(2,1)} %param.9) | copy-start | bytes 3145732
  40.0 9.4 %copy-start.14 = (bf16[1,16,128,128]{3,2,1,0:T(8,128)(2,1)S(1)}, bf16[1,16,128,128]{3,2,1,0:T(8,128)(2,1)}, u32[]{:S(2)}) copy-start(bf16[1,16,128,128]{3,2,1,0:T(8,128)(2,1)} %copy-done.13) | copy-start | bytes 1572868
  42.7 16.4 %collective-permute-start.7 = (bf16[1,16,128,128]{3,2,1,0:T(8,128)(2,1)}, bf16[1,16,128,128]{3,2,1,0:T(8,128)(2,1)S(1)}, u32[]{:S(2)}, u32[]{:S(2)}) collective-permute-start(bf16[1,16,128,128]{3,2,1,0:T(8,128)(2,1)} %collective-permute-done.refs_2_), channel_id=1, source_target_pairs={{0,4},{2,6},{8,12},{10,14},{16,20},{18,22},{24,28},{26,30},{1,5},{... | collective-permute-start | bytes 1572872 | tf_op jit(solution)/shard_map/ppermute | solution.py:29
  48.1 15.6 %collective-permute-start.8 = (bf16[1,16,128,128]{3,2,1,0:T(8,128)(2,1)}, bf16[1,16,128,128]{3,2,1,0:T(8,128)(2,1)S(1)}, u32[]{:S(2)}, u32[]{:S(2)}) collective-permute-start(bf16[1,16,128,128]{3,2,1,0:T(8,128)(2,1)} %collective-permute-done.1.refs_0_), channel_id=1, source_target_pairs={{4,0},{6,2},{12,8},{14,10},{20,16},{22,18},{28,24},{30,26},{5,1},{... | collective-permute-start | bytes 1572872 | tf_op jit(solution)/shard_map/ppermute | solution.py:29
  50.5 23.5 %copy-start.15 = (bf16[1,16,128,128]{3,2,1,0:T(8,128)(2,1)}, bf16[1,16,128,128]{3,2,1,0:T(8,128)(2,1)S(1)}, u32[]{:S(2)}) copy-start(bf16[1,16,128,128]{3,2,1,0:T(8,128)(2,1)S(1)} %broadcast_select_fusion.3.refs_2_) | copy-start | bytes 1572868
  50.5 23.5 %collective-permute-start.2 = (bf16[1,16,128,128]{3,2,1,0:T(8,128)(2,1)S(1)}, bf16[1,16,128,128]{3,2,1,0:T(8,128)(2,1)S(1)}, u32[]{:S(2)}, u32[]{:S(2)}) collective-permute-start(bf16[1,16,128,128]{3,2,1,0:T(8,128)(2,1)S(1)} %bitcast.62), channel_id=1, source_target_pairs={{0,2},{4,6},{8,10},{12,14},{16,18},{20,22},{24,26},{28,30},{1,3},{... | collective-permute-start | bytes 1572872 | tf_op jit(solution)/shard_map/ppermute | solution.py:29
  51.9 16.3 %collective-permute-start.17 = (bf16[1,16,128,128]{3,2,1,0:T(8,128)(2,1)}, bf16[1,16,128,128]{3,2,1,0:T(8,128)(2,1)S(1)}, u32[]{:S(2)}, u32[]{:S(2)}) collective-permute-start(bf16[1,16,128,128]{3,2,1,0:T(8,128)(2,1)} %collective-permute-done.10.refs_5_), channel_id=1, source_target_pairs={{0,4},{2,6},{8,12},{10,14},{16,20},{18,22},{24,28},{26,30},{1,5},{... | collective-permute-start | bytes 1572872 | tf_op jit(solution)/shard_map/ppermute | solution.py:29
  55.5 17.0 %collective-permute-start.18 = (bf16[1,16,128,128]{3,2,1,0:T(8,128)(2,1)}, bf16[1,16,128,128]{3,2,1,0:T(8,128)(2,1)S(1)}, u32[]{:S(2)}, u32[]{:S(2)}) collective-permute-start(bf16[1,16,128,128]{3,2,1,0:T(8,128)(2,1)} %collective-permute-done.11.refs_6_), channel_id=1, source_target_pairs={{4,0},{6,2},{12,8},{14,10},{20,16},{22,18},{28,24},{30,26},{5,1},{... | collective-permute-start | bytes 1572872 | tf_op jit(solution)/shard_map/ppermute | solution.py:29
  57.9 18.8 %copy-start.16 = (bf16[1,16,128,128]{3,2,1,0:T(8,128)(2,1)}, bf16[1,16,128,128]{3,2,1,0:T(8,128)(2,1)S(1)}, u32[]{:S(2)}) copy-start(bf16[1,16,128,128]{3,2,1,0:T(8,128)(2,1)S(1)} %broadcast_select_fusion.1.refs_8_) | copy-start | bytes 1572868
  59.1 16.2 %collective-permute-start.12 = (bf16[1,16,128,128]{3,2,1,0:T(8,128)(2,1)S(1)}, bf16[1,16,128,128]{3,2,1,0:T(8,128)(2,1)S(1)}, u32[]{:S(2)}, u32[]{:S(2)}) collective-permute-start(bf16[1,16,128,128]{3,2,1,0:T(8,128)(2,1)S(1)} %bitcast.66), channel_id=1, source_target_pairs={{0,2},{4,6},{8,10},{12,14},{16,18},{20,22},{24,26},{28,30},{1,3},{... | collective-permute-start | bytes 1572872 | tf_op jit(solution)/shard_map/ppermute | solution.py:29
  63.7 11.7 %collective-permute-start.3 = (bf16[1,16,128,128]{3,2,1,0:T(8,128)(2,1)}, bf16[1,16,128,128]{3,2,1,0:T(8,128)(2,1)S(1)}, u32[]{:S(2)}, u32[]{:S(2)}) collective-permute-start(bf16[1,16,128,128]{3,2,1,0:T(8,128)(2,1)} %collective-permute-done.1.refs_0_), channel_id=1, source_target_pairs={{2,0},{6,4},{10,8},{14,12},{18,16},{22,20},{26,24},{30,28},{3,1},{... | collective-permute-start | bytes 1572872 | tf_op jit(solution)/shard_map/ppermute | solution.py:29
  65.1 12.5 %copy-start.17 = (bf16[1,16,128,128]{3,2,1,0:T(8,128)(2,1)}, bf16[1,16,128,128]{3,2,1,0:T(8,128)(2,1)S(1)}, u32[]{:S(2)}) copy-start(bf16[1,16,128,128]{3,2,1,0:T(8,128)(2,1)S(1)} %broadcast_select_fusion.2.refs_4_) | copy-start | bytes 1572868
  68.2 9.4 %collective-permute-start.6 = (bf16[1,16,128,128]{3,2,1,0:T(8,128)(2,1)S(1)}, bf16[1,16,128,128]{3,2,1,0:T(8,128)(2,1)S(1)}, u32[]{:S(2)}, u32[]{:S(2)}) collective-permute-start(bf16[1,16,128,128]{3,2,1,0:T(8,128)(2,1)S(1)} %broadcast_select_fusion.3.refs_2_), channel_id=1, source_target_pairs={{0,2},{2,0},{4,6},{6,4},{8,10},{10,8},{12,14},{14,12},{16,18},{18,... | collective-permute-start | bytes 1572872 | tf_op jit(solution)/shard_map/ppermute | solution.py:24
  72.5 4.2 %collective-permute-start.13 = (bf16[1,16,128,128]{3,2,1,0:T(8,128)(2,1)}, bf16[1,16,128,128]{3,2,1,0:T(8,128)(2,1)S(1)}, u32[]{:S(2)}, u32[]{:S(2)}) collective-permute-start(bf16[1,16,128,128]{3,2,1,0:T(8,128)(2,1)} %collective-permute-done.11.refs_6_), channel_id=1, source_target_pairs={{2,0},{6,4},{10,8},{14,12},{18,16},{22,20},{26,24},{30,28},{3,1},{... | collective-permute-start | bytes 1572872 | tf_op jit(solution)/shard_map/ppermute | solution.py:29
  74.0 3.8 %copy-start.18 = (bf16[1,16,128,128]{3,2,1,0:T(8,128)(2,1)}, bf16[1,16,128,128]{3,2,1,0:T(8,128)(2,1)S(1)}, u32[]{:S(2)}) copy-start(bf16[1,16,128,128]{3,2,1,0:T(8,128)(2,1)S(1)} %broadcast_select_fusion.refs_10_) | copy-start | bytes 1572868
  74.1 3.5 %collective-permute-start.16 = (bf16[1,16,128,128]{3,2,1,0:T(8,128)(2,1)S(1)}, bf16[1,16,128,128]{3,2,1,0:T(8,128)(2,1)S(1)}, u32[]{:S(2)}, u32[]{:S(2)}) collective-permute-start(bf16[1,16,128,128]{3,2,1,0:T(8,128)(2,1)S(1)} %broadcast_select_fusion.1.refs_8_), channel_id=1, source_target_pairs={{0,2},{2,0},{4,6},{6,4},{8,10},{10,8},{12,14},{14,12},{16,18},{18,... | collective-permute-start | bytes 1572872 | tf_op jit(solution)/shard_map/ppermute | solution.py:24
  75.3 2.5 %collective-permute-start.9 = (bf16[1,16,128,128]{3,2,1,0:T(8,128)(2,1)S(1)}, bf16[1,16,128,128]{3,2,1,0:T(8,128)(2,1)S(1)}, u32[]{:S(2)}, u32[]{:S(2)}) collective-permute-start(bf16[1,16,128,128]{3,2,1,0:T(8,128)(2,1)S(1)} %broadcast_select_fusion.2.refs_4_), channel_id=1, source_target_pairs={{0,2},{2,0},{4,6},{6,4},{8,10},{10,8},{12,14},{14,12},{16,18},{18,... | collective-permute-start | bytes 1572872 | tf_op jit(solution)/shard_map/ppermute | solution.py:24
  75.4 3.2 %collective-permute-start.19 = (bf16[1,16,128,128]{3,2,1,0:T(8,128)(2,1)S(1)}, bf16[1,16,128,128]{3,2,1,0:T(8,128)(2,1)S(1)}, u32[]{:S(2)}, u32[]{:S(2)}) collective-permute-start(bf16[1,16,128,128]{3,2,1,0:T(8,128)(2,1)S(1)} %broadcast_select_fusion.refs_10_), channel_id=1, source_target_pairs={{0,2},{2,0},{4,6},{6,4},{8,10},{10,8},{12,14},{14,12},{16,18},{18,... | collective-permute-start | bytes 1572872 | tf_op jit(solution)/shard_map/ppermute | solution.py:24
  77.5 1.0 copy-start.22
  77.5 1.8 copy-start.23
  77.8 1.6 copy-start.24
  78.5 0.8 copy-start.25
  101.8 5.9 %copy-start.10 = (bf16[1,16,128,128]{3,2,1,0:T(8,128)(2,1)S(1)}, bf16[1,16,128,128]{3,2,1,0:T(8,128)(2,1)}, u32[]{:S(2)}) copy-start(bf16[1,16,128,128]{3,2,1,0:T(8,128)(2,1)} %get-tuple-element.32) | copy-start | bytes 1572868
  101.8 2.2 %collective-permute-start.20 = (bf16[1,16,128,128]{3,2,1,0:T(8,128)(2,1)}, bf16[1,16,128,128]{3,2,1,0:T(8,128)(2,1)S(1)}, u32[]{:S(2)}, u32[]{:S(2)}) collective-permute-start(bf16[1,16,128,128]{3,2,1,0:T(8,128)(2,1)} %get-tuple-element.29), channel_id=1, source_target_pairs={{0,2},{2,0},{4,6},{6,4},{8,10},{10,8},{12,14},{14,12},{16,18},{18,... | collective-permute-start | bytes 1572872 | tf_op jit(solution)/shard_map/ppermute | solution.py:24
  102.0 4.2 %collective-permute-start.21 = (bf16[1,16,128,128]{3,2,1,0:T(8,128)(2,1)}, bf16[1,16,128,128]{3,2,1,0:T(8,128)(2,1)S(1)}, u32[]{:S(2)}, u32[]{:S(2)}) collective-permute-start(bf16[1,16,128,128]{3,2,1,0:T(8,128)(2,1)} %get-tuple-element.31), channel_id=1, source_target_pairs={{0,2},{2,0},{4,6},{6,4},{8,10},{10,8},{12,14},{14,12},{16,18},{18,... | collective-permute-start | bytes 1572872 | tf_op jit(solution)/shard_map/ppermute | solution.py:24
  102.3 7.4 %collective-permute-start.24 = (bf16[1,16,128,128]{3,2,1,0:T(8,128)(2,1)}, bf16[1,16,128,128]{3,2,1,0:T(8,128)(2,1)S(1)}, u32[]{:S(2)}, u32[]{:S(2)}) collective-permute-start(bf16[1,16,128,128]{3,2,1,0:T(8,128)(2,1)} %collective-permute-done.refs_2_), channel_id=1, source_target_pairs={{0,2},{2,0},{4,6},{6,4},{8,10},{10,8},{12,14},{14,12},{16,18},{18,... | collective-permute-start | bytes 1572872 | tf_op jit(solution)/shard_map/ppermute | solution.py:24
  102.5 9.9 %collective-permute-start.25 = (bf16[1,16,128,128]{3,2,1,0:T(8,128)(2,1)}, bf16[1,16,128,128]{3,2,1,0:T(8,128)(2,1)}, u32[]{:S(2)}, u32[]{:S(2)}) collective-permute-start(bf16[1,16,128,128]{3,2,1,0:T(8,128)(2,1)} %collective-permute-done.10.refs_5_), channel_id=1, source_target_pairs={{0,2},{2,0},{4,6},{6,4},{8,10},{10,8},{12,14},{14,12},{16,18},{18,... | collective-permute-start | bytes 1572872 | tf_op jit(solution)/shard_map/ppermute | solution.py:24
  102.9 4.8 %collective-permute-start.22 = (bf16[1,16,128,128]{3,2,1,0:T(8,128)(2,1)}, bf16[1,16,128,128]{3,2,1,0:T(8,128)(2,1)S(1)}, u32[]{:S(2)}, u32[]{:S(2)}) collective-permute-start(bf16[1,16,128,128]{3,2,1,0:T(8,128)(2,1)} %get-tuple-element.33), channel_id=1, source_target_pairs={{0,2},{2,0},{4,6},{6,4},{8,10},{10,8},{12,14},{14,12},{16,18},{18,... | collective-permute-start | bytes 1572872 | tf_op jit(solution)/shard_map/ppermute | solution.py:24
  104.0 4.7 %collective-permute-start.23 = (bf16[1,16,128,128]{3,2,1,0:T(8,128)(2,1)}, bf16[1,16,128,128]{3,2,1,0:T(8,128)(2,1)S(1)}, u32[]{:S(2)}, u32[]{:S(2)}) collective-permute-start(bf16[1,16,128,128]{3,2,1,0:T(8,128)(2,1)} %get-tuple-element.35), channel_id=1, source_target_pairs={{0,2},{2,0},{4,6},{6,4},{8,10},{10,8},{12,14},{14,12},{16,18},{18,... | collective-permute-start | bytes 1572872 | tf_op jit(solution)/shard_map/ppermute | solution.py:24
  104.1 4.6 %copy-start.9 = (bf16[1,16,128,128]{3,2,1,0:T(8,128)(2,1)S(1)}, bf16[1,16,128,128]{3,2,1,0:T(8,128)(2,1)}, u32[]{:S(2)}) copy-start(bf16[1,16,128,128]{3,2,1,0:T(8,128)(2,1)} %get-tuple-element.34) | copy-start | bytes 1572868
  106.2 19.8 %collective-permute-start.26 = (bf16[1,16,128,128]{3,2,1,0:T(8,128)(2,1)}, bf16[1,16,128,128]{3,2,1,0:T(8,128)(2,1)S(1)}, u32[]{:S(2)}, u32[]{:S(2)}) collective-permute-start(bf16[1,16,128,128]{3,2,1,0:T(8,128)(2,1)} %get-tuple-element.40), channel_id=1, source_target_pairs={{0,2},{2,0},{4,6},{6,4},{8,10},{10,8},{12,14},{14,12},{16,18},{18,... | collective-permute-start | bytes 1572872 | tf_op jit(solution)/shard_map/ppermute | solution.py:24
  109.6 16.7 %collective-permute-start.29 = (bf16[1,16,128,128]{3,2,1,0:T(8,128)(2,1)S(1)}, bf16[1,16,128,128]{3,2,1,0:T(8,128)(2,1)S(1)}, u32[]{:S(2)}, u32[]{:S(2)}) collective-permute-start(bf16[1,16,128,128]{3,2,1,0:T(8,128)(2,1)S(1)} %add_convert_fusion.2), channel_id=1, source_target_pairs={{0,4},{2,6},{4,0},{6,2},{8,12},{10,14},{12,8},{14,10},{16,20},{18,... | collective-permute-start | bytes 1572872 | tf_op jit(solution)/shard_map/ppermute | solution.py:24
  109.6 20.1 %collective-permute-start.32 = (bf16[1,16,128,128]{3,2,1,0:T(8,128)(2,1)}, bf16[1,16,128,128]{3,2,1,0:T(8,128)(2,1)S(1)}, u32[]{:S(2)}, u32[]{:S(2)}) collective-permute-start(bf16[1,16,128,128]{3,2,1,0:T(8,128)(2,1)} %get-tuple-element.47), channel_id=1, source_target_pairs={{0,2},{2,0},{4,6},{6,4},{8,10},{10,8},{12,14},{14,12},{16,18},{18,... | collective-permute-start | bytes 1572872 | tf_op jit(solution)/shard_map/ppermute | solution.py:24
  109.8 2.6 %copy-start.21 = (bf16[1,16,128,128]{3,2,1,0:T(8,128)(2,1)}, bf16[1,16,128,128]{3,2,1,0:T(8,128)(2,1)S(1)}, u32[]{:S(2)}) copy-start(bf16[1,16,128,128]{3,2,1,0:T(8,128)(2,1)S(1)} %collective-permute-done.24.refs_3_) | copy-start | bytes 1572868
  109.8 25.8 %collective-permute-start.35 = (bf16[1,16,128,128]{3,2,1,0:T(8,128)(2,1)}, bf16[1,16,128,128]{3,2,1,0:T(8,128)(2,1)S(1)}, u32[]{:S(2)}, u32[]{:S(2)}) collective-permute-start(bf16[1,16,128,128]{3,2,1,0:T(8,128)(2,1)} %add_convert_fusion), channel_id=1, source_target_pairs={{0,4},{2,6},{4,0},{6,2},{8,12},{10,14},{12,8},{14,10},{16,20},{18,... | collective-permute-start | bytes 1572872 | tf_op jit(solution)/shard_map/ppermute | solution.py:24
  112.4 34.5 %collective-permute-start.27 = (bf16[1,16,128,128]{3,2,1,0:T(8,128)(2,1)}, bf16[1,16,128,128]{3,2,1,0:T(8,128)(2,1)S(1)}, u32[]{:S(2)}, u32[]{:S(2)}) collective-permute-start(bf16[1,16,128,128]{3,2,1,0:T(8,128)(2,1)} %add_convert_fusion.3), channel_id=1, source_target_pairs={{0,4},{2,6},{4,0},{6,2},{8,12},{10,14},{12,8},{14,10},{16,20},{18,... | collective-permute-start | bytes 1572872 | tf_op jit(solution)/shard_map/ppermute | solution.py:24
  126.0 9.7 %copy-start.19 = (bf16[1,16,128,128]{3,2,1,0:T(8,128)(2,1)S(1)}, bf16[1,16,128,128]{3,2,1,0:T(8,128)(2,1)}, u32[]{:S(2)}) copy-start(bf16[1,16,128,128]{3,2,1,0:T(8,128)(2,1)} %get-tuple-element.52) | copy-start | bytes 1572868
  126.0 22.2 %collective-permute-start.28 = (bf16[1,16,128,128]{3,2,1,0:T(8,128)(2,1)}, bf16[1,16,128,128]{3,2,1,0:T(8,128)(2,1)}, u32[]{:S(2)}, u32[]{:S(2)}) collective-permute-start(bf16[1,16,128,128]{3,2,1,0:T(8,128)(2,1)} %get-tuple-element.43), channel_id=1, source_target_pairs={{0,2},{2,0},{4,6},{6,4},{8,10},{10,8},{12,14},{14,12},{16,18},{18,... | collective-permute-start | bytes 1572872 | tf_op jit(solution)/shard_map/ppermute | solution.py:24
  128.4 19.8 %collective-permute-start.30 = (bf16[1,16,128,128]{3,2,1,0:T(8,128)(2,1)}, bf16[1,16,128,128]{3,2,1,0:T(8,128)(2,1)}, u32[]{:S(2)}, u32[]{:S(2)}) collective-permute-start(bf16[1,16,128,128]{3,2,1,0:T(8,128)(2,1)} %fusion.7), channel_id=1, source_target_pairs={{8,0},{10,2},{12,4},{14,6},{16,8},{18,10},{20,12},{22,14},{24,16},... | collective-permute-start | bytes 1572872 | tf_op jit(solution)/shard_map/ppermute | solution.py:20
  129.7 27.6 %collective-permute-start.33 = (bf16[1,16,128,128]{3,2,1,0:T(8,128)(2,1)}, bf16[1,16,128,128]{3,2,1,0:T(8,128)(2,1)S(1)}, u32[]{:S(2)}, u32[]{:S(2)}) collective-permute-start(bf16[1,16,128,128]{3,2,1,0:T(8,128)(2,1)} %add_convert_fusion.1), channel_id=1, source_target_pairs={{0,4},{2,6},{4,0},{6,2},{8,12},{10,14},{12,8},{14,10},{16,20},{18,... | collective-permute-start | bytes 1572872 | tf_op jit(solution)/shard_map/ppermute | solution.py:24
  135.6 21.7 %collective-permute-start.34 = (bf16[1,16,128,128]{3,2,1,0:T(8,128)(2,1)}, bf16[1,16,128,128]{3,2,1,0:T(8,128)(2,1)}, u32[]{:S(2)}, u32[]{:S(2)}) collective-permute-start(bf16[1,16,128,128]{3,2,1,0:T(8,128)(2,1)} %get-tuple-element.50), channel_id=1, source_target_pairs={{0,2},{2,0},{4,6},{6,4},{8,10},{10,8},{12,14},{14,12},{16,18},{18,... | collective-permute-start | bytes 1572872 | tf_op jit(solution)/shard_map/ppermute | solution.py:24
  146.9 19.5 %copy-start.2 = (bf16[1,16,128,128]{3,2,1,0:T(8,128)(2,1)}, bf16[1,16,128,128]{3,2,1,0:T(8,128)(2,1)S(1)}, u32[]{:S(2)}) copy-start(bf16[1,16,128,128]{3,2,1,0:T(8,128)(2,1)S(1)} %collective-permute-done.27) | copy-start | bytes 1572868
  146.9 17.1 %collective-permute-start.36 = (bf16[1,16,128,128]{3,2,1,0:T(8,128)(2,1)}, bf16[1,16,128,128]{3,2,1,0:T(8,128)(2,1)}, u32[]{:S(2)}, u32[]{:S(2)}) collective-permute-start(bf16[1,16,128,128]{3,2,1,0:T(8,128)(2,1)} %fusion.18), channel_id=1, source_target_pairs={{8,0},{10,2},{12,4},{14,6},{16,8},{18,10},{20,12},{22,14},{24,16},... | collective-permute-start | bytes 1572872 | tf_op jit(solution)/shard_map/ppermute | solution.py:20
  148.2 15.8 %copy-start.20 = (bf16[1,16,128,128]{3,2,1,0:T(8,128)(2,1)S(1)}, bf16[1,16,128,128]{3,2,1,0:T(8,128)(2,1)}, u32[]{:S(2)}) copy-start(bf16[1,16,128,128]{3,2,1,0:T(8,128)(2,1)} %get-tuple-element.49) | copy-start | bytes 1572868
  150.8 16.8 %copy-start.1 = (f32[16,128,256]{2,1,0:T(8,128)S(1)}, f32[16,128,256]{2,1,0:T(8,128)}, u32[]{:S(2)}) copy-start(f32[16,128,256]{2,1,0:T(8,128)} %get-tuple-element.38) | copy-start | bytes 6291460
  150.8 24.3 %collective-permute-start.31 = (bf16[128,16,128]{2,0,1:T(8,128)(2,1)}, bf16[128,16,128]{2,0,1:T(8,128)(2,1)}, u32[]{:S(2)}, u32[]{:S(2)}) collective-permute-start(bf16[128,16,128]{2,0,1:T(8,128)(2,1)} %fusion.23), channel_id=1, source_target_pairs={{8,0},{10,2},{12,4},{14,6},{16,8},{18,10},{20,12},{22,14},{24,16},... | collective-permute-start | bytes 1572872 | tf_op jit(solution)/shard_map/ppermute | solution.py:20
  157.3 10.3 %copy-start.4 = (bf16[1,16,128,128]{3,2,1,0:T(8,128)(2,1)}, bf16[1,16,128,128]{3,2,1,0:T(8,128)(2,1)S(1)}, u32[]{:S(2)}) copy-start(bf16[1,16,128,128]{3,2,1,0:T(8,128)(2,1)S(1)} %collective-permute-done.33) | copy-start | bytes 1572868
  166.4 17.6 %collective-permute-start.37 = (bf16[128,16,128]{2,0,1:T(8,128)(2,1)}, bf16[128,16,128]{2,0,1:T(8,128)(2,1)}, u32[]{:S(2)}, u32[]{:S(2)}) collective-permute-start(bf16[128,16,128]{2,0,1:T(8,128)(2,1)} %fusion.22), channel_id=1, source_target_pairs={{8,0},{10,2},{12,4},{14,6},{16,8},{18,10},{20,12},{22,14},{24,16},... | collective-permute-start | bytes 1572872 | tf_op jit(solution)/shard_map/ppermute | solution.py:20
  168.2 6.9 %copy-start.3 = (bf16[1,16,128,128]{3,2,1,0:T(8,128)(2,1)S(1)}, bf16[1,16,128,128]{3,2,1,0:T(8,128)(2,1)}, u32[]{:S(2)}) copy-start(bf16[1,16,128,128]{3,2,1,0:T(8,128)(2,1)} %copy-done.2) | copy-start | bytes 1572868
  172.0 11.9 %copy-start.5 = (bf16[1,16,128,128]{3,2,1,0:T(8,128)(2,1)S(1)}, bf16[1,16,128,128]{3,2,1,0:T(8,128)(2,1)}, u32[]{:S(2)}) copy-start(bf16[1,16,128,128]{3,2,1,0:T(8,128)(2,1)} %copy-done.4) | copy-start | bytes 1572868
  172.0 11.9 %copy-start.8 = (bf16[1,16,128,128]{3,2,1,0:T(8,128)(2,1)S(1)}, bf16[1,16,128,128]{3,2,1,0:T(8,128)(2,1)}, u32[]{:S(2)}) copy-start(bf16[1,16,128,128]{3,2,1,0:T(8,128)(2,1)} %get-tuple-element.46) | copy-start | bytes 1572868

commit v16 on v14

--- a/solution.py
+++ b/solution.py
@@ -125,9 +125,7 @@
     y0 = jnp.where(half == 1, ya, yb)
     d0 = swap(y0, n, 1)
     cxo = jnp.where(core == 1, ca, cb)
-    y1 = jnp.where(half == 1, yc, yd)
-    d1 = swap(y1, n, 1)
-    return [x0, x1, cx1, x2, cxo, y0, d0, y1, d1]
+    return [x0, x1, cx1, x2, cxo, y0, d0, yc, yd]
 
 
 def gather_y(terms, n):
@@ -175,24 +173,28 @@
     kb = route(normed_key_rows.transpose(1, 0, 2)[None], n, half, core)
     vb = route(value_rows.transpose(1, 0, 2)[None], n, half, core)
 
-    late = [3, 4, 5, 6, 7, 8]
-    early = [0, 1, 2]
     modes = [0, 1, 1, 2, 1, 1, 1, 1, 1]
     dist = [0, PLANE, 3 + 2 * core, 2 * PLANE, 7 - 6 * core, 2, 1 + 2 * core, 6, 5 + 2 * core]
     terms = [None] * 18
-    acc = None
-    ys = None
-    qb = q4
-    for sel in (late, early):
+
+    def run(sel, acc, q):
         acc, out = attend_blocks(
-            [modes[j] for j in sel], [dist[j] for j in sel], idx, qb, do4, lse3, delta3, acc,
+            [modes[j] for j in sel], [dist[j] for j in sel], idx, q, do4, lse3, delta3, acc,
             [kb[j] for j in sel] + [vb[j] for j in sel])
         for m, j in enumerate(sel):
             terms[j] = out[m]
             terms[9 + j] = out[len(sel) + m]
-        if ys is None:
-            ys = gather_y(terms[:9], n) + gather_y(terms[9:], n)
-            ys, qb = lax.optimization_barrier((ys, q4))
+        return acc
+
+    acc = run([3, 4, 5, 6], None, q4)
+    (kb[7], kb[8], vb[7], vb[8]), acc = lax.optimization_barrier(((kb[7], kb[8], vb[7], vb[8]), acc))
+    for b in (kb, vb):
+        b[7] = jnp.where(half == 1, b[7], b[8])
+        b[8] = swap(b[7], n, 1)
+    acc = run([7, 8], acc, q4)
+    ys = gather_y(terms[:9], n) + gather_y(terms[9:], n)
+    ys, qb = lax.optimization_barrier((ys, q4))
+    acc = run([0, 1, 2], acc, qb)
     grad_k = unroute(terms[:9], ys[0], ys[1], n, half, core)
     grad_v = unroute(terms[9:], ys[2], ys[3], n, half, core)
 

time: 187 us -> 191 us (1.021)
  Pallas kernels: 34.6 us -> 38.2 us
  other arithmetic: 22.5 us -> 25 us
    ppermute x12, waiting for transfers between devices: 11.9 us -> 4.27 us  [one_way(): return lax.ppermute(x, 'seq', pairs)]
    ppermute x8, waiting for transfers between devices: 19.2 us -> 25.5 us  [shift(): return lax.ppermute(x, 'seq', pairs)]
    pallas_call x2 -> x3, Pallas kernels: 34.6 us -> 38.2 us  [attend_blocks(): pl.pallas_call(functools.partial(_blocks_kernel, tuple(modes), acc is not...]
    select_n x2, other arithmetic: 1.72 us -> 3.79 us  [route(): cxo = jnp.where(core == 1, ca, cb)]
    unnamed x56 -> x50, local copies, waits for them, and re-layouts: 6.47 us -> 6.44 us
  transfers between devices with their start and end apart: 38 -> 38, of which waited for: 14 -> 12; matrix products, arithmetic and copies ran while one was open for 17% -> 18% of each run, Pallas kernels for 7% -> 20%
where the time goes in v16:
time: 191 us; the launch traced here: 190 us
  starting transfers between devices  59.5 us (31%)
  waiting for transfers between devices  52.6 us (28%)
  Pallas kernels  38.2 us (20%)
  other arithmetic  25 us (13%)
  local copies, waits for them, and re-layouts  14 us (7%)
    pallas_call x3, Pallas kernels, attend_blocks(): pl.pallas_call(functools.partial(_blocks_kernel, tuple(modes), acc is not...  38.2 us
    ppermute x12, starting transfers between devices, one_way(): return lax.ppermute(x, 'seq', pairs)  27.2 us
    ppermute x8, waiting for transfers between devices, shift(): return lax.ppermute(x, 'seq', pairs)  25.5 us
    ppermute x8, starting transfers between devices, shift(): return lax.ppermute(x, 'seq', pairs)  23.3 us
    ppermute x18, waiting for transfers between devices, swap(): return lax.ppermute(x, 'seq', [(i, i ^ bit) for i in range(n)])  22.8 us
    ppermute x18, starting transfers between devices, swap(): return lax.ppermute(x, 'seq', [(i, i ^ bit) for i in range(n)])  9.05 us
    unnamed x50, local copies, waits for them, and re-layouts  6.44 us
    transpose x2, other arithmetic, unroute(): last = shift(part1.astype(bf16)[0].transpose(1, 0, 2), n, -PLANE)  5.06 us
  transfers between devices with their start and end apart: 38, of which 12 were waited for; matrix products, arithmetic and copies ran while one was open for 18% of the time, Pallas kernels for 20%

profile of v16, /device:TPU:0, one launch (start us, length us, event | category | flops | bytes accessed | tf_op | source)
XLA Modules:
  0.0 190.4 jit_solution(2286529478127694007)
XLA Ops:
  0.7 1.3 copy.27
  2.0 5.7 %collective-permute-start = (bf16[1,16,128,128]{3,2,1,0:T(8,128)(2,1)S(1)}, bf16[1,16,128,128]{3,2,1,0:T(8,128)(2,1)}, u32[]{:S(2)}, u32[]{:S(2)}) collective-permute-start(bf16[1,16,128,128]{3,2,1,0:T(8,128)(2,1)S(1)} %bitcast.62), channel_id=1, source_target_pairs={{0,8},{2,10},{4,12},{6,14},{8,16},{10,18},{12,20},{14,22},{16,24},... | collective-permute-start | bytes 1572872 | tf_op jit(solution)/shard_map/ppermute | solution.py:20
  7.7 1.2 copy.26
  8.9 3.5 %collective-permute-start.7 = (bf16[1,16,128,128]{3,2,1,0:T(8,128)(2,1)S(1)}, bf16[1,16,128,128]{3,2,1,0:T(8,128)(2,1)}, u32[]{:S(2)}, u32[]{:S(2)}) collective-permute-start(bf16[1,16,128,128]{3,2,1,0:T(8,128)(2,1)S(1)} %bitcast.66), channel_id=1, source_target_pairs={{0,8},{2,10},{4,12},{6,14},{8,16},{10,18},{12,20},{14,22},{16,24},... | collective-permute-start | bytes 1572872 | tf_op jit(solution)/shard_map/ppermute | solution.py:20
  12.4 4.2 %collective-permute-start.4 = (bf16[1,16,128,128]{3,2,1,0:T(8,128)(2,1)S(1)}, bf16[1,16,128,128]{3,2,1,0:T(8,128)(2,1)}, u32[]{:S(2)}, u32[]{:S(2)}) collective-permute-start(bf16[1,16,128,128]{3,2,1,0:T(8,128)(2,1)S(1)} %bitcast.63), channel_id=1, source_target_pairs={{0,4},{2,6},{8,12},{10,14},{16,20},{18,22},{24,28},{26,30},{1,5},{... | collective-permute-start | bytes 1572872 | tf_op jit(solution)/shard_map/ppermute | solution.py:29
  16.6 2.6 %collective-permute-done.refs_2_ = bf16[1,16,128,128]{3,2,1,0:T(8,128)(2,1)} collective-permute-done((bf16[1,16,128,128]{3,2,1,0:T(8,128)(2,1)S(1)}, bf16[1,16,128,128]{3,2,1,0:T(8,128)(2,1)}, u32[]{:S(2)}, u32[]{:S(2)}) %collective-permute-start) | collective-permute-done | bytes 524320 | tf_op jit(solution)/shard_map/ppermute | solution.py:20
  19.2 1.3 collective-permute-start.5
  20.5 6.1 %collective-permute-start.11 = (bf16[1,16,128,128]{3,2,1,0:T(8,128)(2,1)S(1)}, bf16[1,16,128,128]{3,2,1,0:T(8,128)(2,1)}, u32[]{:S(2)}, u32[]{:S(2)}) collective-permute-start(bf16[1,16,128,128]{3,2,1,0:T(8,128)(2,1)S(1)} %bitcast.67), channel_id=1, source_target_pairs={{0,4},{2,6},{8,12},{10,14},{16,20},{18,22},{24,28},{26,30},{1,5},{... | collective-permute-start | bytes 1572872 | tf_op jit(solution)/shard_map/ppermute | solution.py:29
  26.7 5.3 %collective-permute-start.1 = (bf16[1,16,128,128]{3,2,1,0:T(8,128)(2,1)}, bf16[1,16,128,128]{3,2,1,0:T(8,128)(2,1)}, u32[]{:S(2)}, u32[]{:S(2)}) collective-permute-start(bf16[1,16,128,128]{3,2,1,0:T(8,128)(2,1)} %collective-permute-done.refs_2_), channel_id=1, source_target_pairs={{0,8},{2,10},{4,12},{6,14},{8,16},{10,18},{12,20},{14,22},{16,24},... | collective-permute-start | bytes 1572872 | tf_op jit(solution)/shard_map/ppermute | solution.py:20
  32.0 3.5 %collective-permute-start.8 = (bf16[1,16,128,128]{3,2,1,0:T(8,128)(2,1)}, bf16[1,16,128,128]{3,2,1,0:T(8,128)(2,1)}, u32[]{:S(2)}, u32[]{:S(2)}) collective-permute-start(bf16[1,16,128,128]{3,2,1,0:T(8,128)(2,1)} %collective-permute-done.7.refs_5_), channel_id=1, source_target_pairs={{0,8},{2,10},{4,12},{6,14},{8,16},{10,18},{12,20},{14,22},{16,24},... | collective-permute-start | bytes 1572872 | tf_op jit(solution)/shard_map/ppermute | solution.py:20
  35.5 1.3 collective-permute-start.12
  36.8 1.4 copy.16
  38.2 1.4 copy.17
  39.6 2.1 %collective-permute-start.2 = (bf16[1,16,128,128]{3,2,1,0:T(8,128)(2,1)S(1)}, bf16[1,16,128,128]{3,2,1,0:T(8,128)(2,1)}, u32[]{:S(2)}, u32[]{:S(2)}) collective-permute-start(bf16[1,16,128,128]{3,2,1,0:T(8,128)(2,1)S(1)} %bitcast.64), channel_id=1, source_target_pairs={{0,2},{4,6},{8,10},{12,14},{16,18},{20,22},{24,26},{28,30},{1,3},{... | collective-permute-start | bytes 1572872 | tf_op jit(solution)/shard_map/ppermute | solution.py:29
  41.7 1.9 broadcast_select_fusion.3.refs_2_
  43.6 2.1 %collective-permute-start.9 = (bf16[1,16,128,128]{3,2,1,0:T(8,128)(2,1)S(1)}, bf16[1,16,128,128]{3,2,1,0:T(8,128)(2,1)}, u32[]{:S(2)}, u32[]{:S(2)}) collective-permute-start(bf16[1,16,128,128]{3,2,1,0:T(8,128)(2,1)S(1)} %bitcast.68), channel_id=1, source_target_pairs={{0,2},{4,6},{8,10},{12,14},{16,18},{20,22},{24,26},{28,30},{1,3},{... | collective-permute-start | bytes 1572872 | tf_op jit(solution)/shard_map/ppermute | solution.py:29
  45.7 6.2 %collective-permute-done.8.refs_4_ = bf16[1,16,128,128]{3,2,1,0:T(8,128)(2,1)} collective-permute-done((bf16[1,16,128,128]{3,2,1,0:T(8,128)(2,1)}, bf16[1,16,128,128]{3,2,1,0:T(8,128)(2,1)}, u32[]{:S(2)}, u32[]{:S(2)}) %collective-permute-start.8) | collective-permute-done | bytes 524320 | tf_op jit(solution)/shard_map/ppermute | solution.py:20
  51.9 1.3 collective-permute-start.3
  53.2 1.3 collective-permute-start.10
  54.5 0.6 multiply_reduce_fusion
  55.1 0.7 copy.18
  55.8 0.6 add_convert_fusion.5.valid_ref
  56.4 1.1 broadcast_select_fusion.2.refs_6_
  57.5 3.5 %collective-permute-start.15 = (bf16[1,16,128,128]{3,2,1,0:T(8,128)(2,1)}, bf16[1,16,128,128]{3,2,1,0:T(8,128)(2,1)S(1)}, u32[]{:S(2)}, u32[]{:S(2)}) collective-permute-start(bf16[1,16,128,128]{3,2,1,0:T(8,128)(2,1)} %collective-permute-done.refs_2_), channel_id=1, source_target_pairs={{0,4},{2,6},{8,12},{10,14},{16,20},{18,22},{24,28},{26,30},{1,5},{... | collective-permute-start | bytes 1572872 | tf_op jit(solution)/shard_map/ppermute | solution.py:29
  61.0 1.3 collective-permute-start.17
  62.4 2.5 %collective-permute-start.13 = (bf16[1,16,128,128]{3,2,1,0:T(8,128)(2,1)S(1)}, bf16[1,16,128,128]{3,2,1,0:T(8,128)(2,1)S(1)}, u32[]{:S(2)}, u32[]{:S(2)}) collective-permute-start(bf16[1,16,128,128]{3,2,1,0:T(8,128)(2,1)S(1)} %broadcast_select_fusion.2.refs_6_), channel_id=1, source_target_pairs={{0,2},{2,0},{4,6},{6,4},{8,10},{10,8},{12,14},{14,12},{16,18},{18,... | collective-permute-start | bytes 1572872 | tf_op jit(solution)/shard_map/ppermute | solution.py:24
  64.9 1.3 collective-permute-start.16
  66.2 1.5 collective-permute-start.18
  67.7 1.9 %broadcast_select_fusion.5.refs_1_ = bf16[1,16,128,128]{3,2,1,0:T(8,128)(2,1)} fusion(bf16[1,16,128,128]{3,2,1,0:T(8,128)(2,1)} %collective-permute-done.2, bf16[1,16,128,128]{3,2,1,0:T(8,128)(2,1)} %collective-permute-done.3, pred[]{:T(512)S(6)} %eq.11), kind=kLoop, calls=%fused_computation.47 | loop fusion | flops 262144 | bytes 1572865 | tf_op jit(solution)/shard_map/jit(_where)/select_n | solution.py:127
  69.6 1.9 broadcast_select_fusion.4.refs_5_
  71.5 0.8 copy-done.22
  72.3 15.5 %shard_map.85 = (f32[16,128,256]{2,1,0:T(8,128)}, bf16[1,16,128,128]{3,2,1,0:T(8,128)(2,1)}, bf16[1,16,128,128]{3,2,1,0:T(8,128)(2,1)}, bf16[1,16,128,128]{3,2,1...) custom-call(s32[4]{0:T(128)} %add_convert_fusion.5.valid_ref, ...), custom_call_target="tpu_custom_call" | custom-call | flops 2684354560 | bytes 10485760 | tf_op jit(solution)/shard_map/pallas_call | solution.py:105
  87.9 4.2 %collective-permute-done.18 = bf16[1,16,128,128]{3,2,1,0:T(8,128)(2,1)S(1)} collective-permute-done((bf16[1,16,128,128]{3,2,1,0:T(8,128)(2,1)}, bf16[1,16,128,128]{3,2,1,0:T(8,128)(2,1)S(1)}, u32[]{:S(2)}, u32[]{:S(2)}) %collective-permute-start.18) | collective-permute-done | bytes 524320 | tf_op jit(solution)/shard_map/ppermute | solution.py:29
  93.4 0.6 add_convert_fusion.6.valid_ref
  94.5 1.9 collective-permute-done.20.refs_4_
  96.4 0.8 copy-done.14
  97.3 9.8 %shard_map.86 = (f32[16,128,256]{2,1,0:T(8,128)}, bf16[1,16,128,128]{3,2,1,0:T(8,128)(2,1)}, bf16[1,16,128,128]{3,2,1,0:T(8,128)(2,1)}, bf16[1,16,128,128]{3,2,1,0:T(8,128)(2,1)}, bf16[1,16,128,128]{3,2,1,0:T(8,128)(2,1)}) custom-call(s32[2]{0:T(128)} %add_convert_fusion.6.valid_ref, bf16[16,2,128,128]{3,2,1,0:T(8,128)(2,1)} %bitcast.53, ...), custom_call_target="tpu_custom_call" | custom-call | flops 1342177280 | bytes 8388608 | tf_op jit(solution)/shard_map/pallas_call | solution.py:105
  107.5 2.1 %add_convert_fusion.3 = bf16[1,16,128,128]{3,2,1,0:T(8,128)(2,1)} fusion(bf16[1,16,128,128]{3,2,1,0:T(8,128)(2,1)} %collective-permute-done.14, bf16[1,16,128,128]{3,2,1,0:T(8,128)(2,1)S(1)} %copy-done.12), kind=kLoop, calls=%fused_computation.37 | loop fusion | flops 1048576 | bytes 1572864 | tf_op jit(solution)/shard_map/convert_element_type | solution.py:135
  109.8 1.0 add_convert_fusion.1
  110.9 0.7 collective-permute-done.23
  111.7 1.0 add_convert_fusion
  112.9 1.7 collective-permute-start.35
  114.7 0.7 add_convert_fusion.4.valid_ref
  115.6 12.8 %shard_map.87 = (f32[16,128,256]{2,1,0:T(8,128)}, bf16[1,16,128,128]{3,2,1,0:T(8,128)(2,1)}, bf16[1,16,128,128]{3,2,1,0:T(8,128)(2,1)}, bf16[1,16,128,128]{3,2,1...) custom-call(s32[3]{0:T(128)} %add_convert_fusion.4.valid_ref, ...), custom_call_target="tpu_custom_call" | custom-call | flops 2013265920 | bytes 10485760 | tf_op jit(solution)/shard_map/pallas_call | solution.py:105
  128.6 2.2 %fusion.7 = bf16[1,16,128,128]{3,2,1,0:T(8,128)(2,1)} fusion(bf16[1,16,128,128]{3,2,1,0:T(8,128)(2,1)S(1)} %collective-permute-done.26, bf16[1,16,128,128]{3,2,1,0:T(8,128)(2,1)S(1)} %collective-permute-done.29, bf16[1,16,128,128]{3,2,1,0:T(8,128)(2,1)} %get-tuple-element.57, pred[]{:T(512)S(6)} %eq.26, pred[]{:T(512)S(6)} %eq.11), kind=kLoop, calls=%fused_computation.19 | loop fusion | flops 2097152 | bytes 2097154 | tf_op jit(solution)/shard_map/convert_element_type | solution.py:152
  130.7 1.3 collective-permute-start.30
  132.0 1.8 collective-permute-start.33
  133.8 4.8 %collective-permute-done.35 = bf16[1,16,128,128]{3,2,1,0:T(8,128)(2,1)S(1)} collective-permute-done((bf16[1,16,128,128]{3,2,1,0:T(8,128)(2,1)}, bf16[1,16,128,128]{3,2,1,0:T(8,128)(2,1)S(1)}, u32[]{:S(2)}, u32[]{:S(2)}) %collective-permute-start.35) | collective-permute-done | bytes 524320 | tf_op jit(solution)/shard_map/ppermute | solution.py:24
  138.6 1.1 fusion.18
  139.7 10.1 %collective-permute-done.27 = bf16[1,16,128,128]{3,2,1,0:T(8,128)(2,1)S(1)} collective-permute-done((bf16[1,16,128,128]{3,2,1,0:T(8,128)(2,1)}, bf16[1,16,128,128]{3,2,1,0:T(8,128)(2,1)S(1)}, u32[]{:S(2)}, u32[]{:S(2)}) %collective-permute-start.27) | collective-permute-done | bytes 524320 | tf_op jit(solution)/shard_map/ppermute | solution.py:24
  149.8 1.3 collective-permute-start.36
  151.2 2.6 %fusion.23 = bf16[128,16,128]{2,0,1:T(8,128)(2,1)} fusion(bf16[1,16,128,128]{3,2,1,0:T(8,128)(2,1)} %collective-permute-done.30, bf16[1,16,128,128]{3,2,1,0:T(8,128)(2,1)S(1)} %collective-permute-done.27, bf16[1,16,128,128]{3,2,1,0:T(8,128)(2,1)S(1)} %collective-permute-done.29, bf16[1,16,128,128]{3,2,1,0:T(8,128)(2,1)} %collective-permute-done.28, ...), kind=kLoop, calls=%fused_computation.39 | loop fusion | flops 2621440 | bytes 3145729 | tf_op jit(solution)/shard_map/transpose | solution.py:154
  153.8 1.4 collective-permute-start.31
  155.2 5.2 %collective-permute-done.33 = bf16[1,16,128,128]{3,2,1,0:T(8,128)(2,1)S(1)} collective-permute-done((bf16[1,16,128,128]{3,2,1,0:T(8,128)(2,1)}, bf16[1,16,128,128]{3,2,1,0:T(8,128)(2,1)S(1)}, u32[]{:S(2)}, u32[]{:S(2)}) %collective-permute-start.33) | collective-permute-done | bytes 524320 | tf_op jit(solution)/shard_map/ppermute | solution.py:24
  160.4 6.9 %collective-permute-done.36 = bf16[1,16,128,128]{3,2,1,0:T(8,128)(2,1)} collective-permute-done((bf16[1,16,128,128]{3,2,1,0:T(8,128)(2,1)}, bf16[1,16,128,128]{3,2,1,0:T(8,128)(2,1)}, u32[]{:S(2)}, u32[]{:S(2)}) %collective-permute-start.36) | collective-permute-done | bytes 524320 | tf_op jit(solution)/shard_map/ppermute | solution.py:20
  167.4 2.4 %fusion.22 = bf16[128,16,128]{2,0,1:T(8,128)(2,1)} fusion(bf16[1,16,128,128]{3,2,1,0:T(8,128)(2,1)} %collective-permute-done.36, bf16[1,16,128,128]{3,2,1,0:T(8,128)(2,1)S(1)} %collective-permute-done.33, bf16[1,16,128,128]{3,2,1,0:T(8,128)(2,1)S(1)} %collective-permute-done.35, bf16[1,16,128,128]{3,2,1,0:T(8,128)(2,1)} %collective-permute-done.34, ...), kind=kLoop, calls=%fused_computation.38 | loop fusion | flops 2621440 | bytes 3145729 | tf_op jit(solution)/shard_map/transpose | solution.py:154
  169.8 1.3 collective-permute-start.37
  171.7 3.8 %copy.21 = bf16[128,16,2,128]{3,2,1,0:T(2,128)(2,1)} copy(bf16[128,16,2,128]{0,2,3,1:T(2,128)(2,1)S(1)} %bitcast.59) | data formatting | bytes 2097152 | tf_op jit(solution)/shard_map/transpose | solution.py:202
  175.4 3.2 %collective-permute-done.31 = bf16[128,16,128]{2,0,1:T(8,128)(2,1)} collective-permute-done((bf16[128,16,128]{2,0,1:T(8,128)(2,1)}, bf16[128,16,128]{2,0,1:T(8,128)(2,1)}, u32[]{:S(2)}, u32[]{:S(2)}) %collective-permute-start.31) | collective-permute-done | bytes 524320 | tf_op jit(solution)/shard_map/ppermute | solution.py:20
  178.6 1.6 fusion.4
  180.2 1.1 copy.22
  181.3 6.6 %collective-permute-done.37 = bf16[128,16,128]{2,0,1:T(8,128)(2,1)} collective-permute-done((bf16[128,16,128]{2,0,1:T(8,128)(2,1)}, bf16[128,16,128]{2,0,1:T(8,128)(2,1)}, u32[]{:S(2)}, u32[]{:S(2)}) %collective-permute-start.37) | collective-permute-done | bytes 524320 | tf_op jit(solution)/shard_map/ppermute | solution.py:20
  187.9 1.4 fusion.15
  189.3 1.1 copy.23
  (91 shorter events, 4.0 us)
Async XLA Ops:
  0.6 36.2 %copy-start.8 = (bf16[128,32,128]{2,1,0:T(8,128)(2,1)S(1)}, bf16[128,32,128]{2,1,0:T(8,128)(2,1)}, u32[]{:S(2)}) copy-start(bf16[128,32,128]{2,1,0:T(8,128)(2,1)} %param.6) | copy-start | bytes 3145732
  0.6 37.6 %copy-start = (bf16[128,32,128]{2,1,0:T(8,128)(2,1)S(1)}, bf16[128,32,128]{2,1,0:T(8,128)(2,1)}, u32[]{:S(2)}) copy-start(bf16[128,32,128]{2,1,0:T(8,128)(2,1)} %param.10) | copy-start | bytes 3145732
  2.0 37.6 %copy-start.17 = (bf16[128,16,128]{2,0,1:T(8,128)(2,1)}, bf16[128,16,128]{2,0,1:T(8,128)(2,1)S(1)}, u32[]{:S(2)}) copy-start(bf16[128,16,128]{2,0,1:T(8,128)(2,1)S(1)} %copy.27) | copy-start | bytes 1572868
  2.0 17.2 %collective-permute-start = (bf16[1,16,128,128]{3,2,1,0:T(8,128)(2,1)S(1)}, bf16[1,16,128,128]{3,2,1,0:T(8,128)(2,1)}, u32[]{:S(2)}, u32[]{:S(2)}) collective-permute-start(bf16[1,16,128,128]{3,2,1,0:T(8,128)(2,1)S(1)} %bitcast.62), channel_id=1, source_target_pairs={{0,8},{2,10},{4,12},{6,14},{8,16},{10,18},{12,20},{14,22},{16,24},... | collective-permute-start | bytes 1572872 | tf_op jit(solution)/shard_map/ppermute | solution.py:20
  8.9 34.7 %copy-start.18 = (bf16[128,16,128]{2,0,1:T(8,128)(2,1)}, bf16[128,16,128]{2,0,1:T(8,128)(2,1)S(1)}, u32[]{:S(2)}) copy-start(bf16[128,16,128]{2,0,1:T(8,128)(2,1)S(1)} %copy.26) | copy-start | bytes 1572868
  8.9 23.0 %collective-permute-start.7 = (bf16[1,16,128,128]{3,2,1,0:T(8,128)(2,1)S(1)}, bf16[1,16,128,128]{3,2,1,0:T(8,128)(2,1)}, u32[]{:S(2)}, u32[]{:S(2)}) collective-permute-start(bf16[1,16,128,128]{3,2,1,0:T(8,128)(2,1)S(1)} %bitcast.66), channel_id=1, source_target_pairs={{0,8},{2,10},{4,12},{6,14},{8,16},{10,18},{12,20},{14,22},{16,24},... | collective-permute-start | bytes 1572872 | tf_op jit(solution)/shard_map/ppermute | solution.py:20
  12.4 23.0 %collective-permute-start.4 = (bf16[1,16,128,128]{3,2,1,0:T(8,128)(2,1)S(1)}, bf16[1,16,128,128]{3,2,1,0:T(8,128)(2,1)}, u32[]{:S(2)}, u32[]{:S(2)}) collective-permute-start(bf16[1,16,128,128]{3,2,1,0:T(8,128)(2,1)S(1)} %bitcast.63), channel_id=1, source_target_pairs={{0,4},{2,6},{8,12},{10,14},{16,20},{18,22},{24,28},{26,30},{1,5},{... | collective-permute-start | bytes 1572872 | tf_op jit(solution)/shard_map/ppermute | solution.py:29
  19.2 20.4 %collective-permute-start.5 = (bf16[1,16,128,128]{3,2,1,0:T(8,128)(2,1)}, bf16[1,16,128,128]{3,2,1,0:T(8,128)(2,1)}, u32[]{:S(2)}, u32[]{:S(2)}) collective-permute-start(bf16[1,16,128,128]{3,2,1,0:T(8,128)(2,1)} %collective-permute-done.refs_2_), channel_id=1, source_target_pairs={{4,0},{6,2},{12,8},{14,10},{20,16},{22,18},{28,24},{30,26},{5,1},{... | collective-permute-start | bytes 1572872 | tf_op jit(solution)/shard_map/ppermute | solution.py:29
  20.5 23.1 %collective-permute-start.11 = (bf16[1,16,128,128]{3,2,1,0:T(8,128)(2,1)S(1)}, bf16[1,16,128,128]{3,2,1,0:T(8,128)(2,1)}, u32[]{:S(2)}, u32[]{:S(2)}) collective-permute-start(bf16[1,16,128,128]{3,2,1,0:T(8,128)(2,1)S(1)} %bitcast.67), channel_id=1, source_target_pairs={{0,4},{2,6},{8,12},{10,14},{16,20},{18,22},{24,28},{26,30},{1,5},{... | collective-permute-start | bytes 1572872 | tf_op jit(solution)/shard_map/ppermute | solution.py:29
  26.7 19.0 %collective-permute-start.1 = (bf16[1,16,128,128]{3,2,1,0:T(8,128)(2,1)}, bf16[1,16,128,128]{3,2,1,0:T(8,128)(2,1)}, u32[]{:S(2)}, u32[]{:S(2)}) collective-permute-start(bf16[1,16,128,128]{3,2,1,0:T(8,128)(2,1)} %collective-permute-done.refs_2_), channel_id=1, source_target_pairs={{0,8},{2,10},{4,12},{6,14},{8,16},{10,18},{12,20},{14,22},{16,24},... | collective-permute-start | bytes 1572872 | tf_op jit(solution)/shard_map/ppermute | solution.py:20
  32.0 19.9 %collective-permute-start.8 = (bf16[1,16,128,128]{3,2,1,0:T(8,128)(2,1)}, bf16[1,16,128,128]{3,2,1,0:T(8,128)(2,1)}, u32[]{:S(2)}, u32[]{:S(2)}) collective-permute-start(bf16[1,16,128,128]{3,2,1,0:T(8,128)(2,1)} %collective-permute-done.7.refs_5_), channel_id=1, source_target_pairs={{0,8},{2,10},{4,12},{6,14},{8,16},{10,18},{12,20},{14,22},{16,24},... | collective-permute-start | bytes 1572872 | tf_op jit(solution)/shard_map/ppermute | solution.py:20
  35.5 17.7 %collective-permute-start.12 = (bf16[1,16,128,128]{3,2,1,0:T(8,128)(2,1)}, bf16[1,16,128,128]{3,2,1,0:T(8,128)(2,1)}, u32[]{:S(2)}, u32[]{:S(2)}) collective-permute-start(bf16[1,16,128,128]{3,2,1,0:T(8,128)(2,1)} %collective-permute-done.7.refs_5_), channel_id=1, source_target_pairs={{4,0},{6,2},{12,8},{14,10},{20,16},{22,18},{28,24},{30,26},{5,1},{... | collective-permute-start | bytes 1572872 | tf_op jit(solution)/shard_map/ppermute | solution.py:29
  38.2 16.3 %copy-start.9 = (bf16[128,32,128]{2,1,0:T(8,128)(2,1)S(1)}, bf16[128,32,128]{2,1,0:T(8,128)(2,1)}, u32[]{:S(2)}) copy-start(bf16[128,32,128]{2,1,0:T(8,128)(2,1)} %param.9) | copy-start | bytes 3145732
  39.6 17.9 %collective-permute-start.2 = (bf16[1,16,128,128]{3,2,1,0:T(8,128)(2,1)S(1)}, bf16[1,16,128,128]{3,2,1,0:T(8,128)(2,1)}, u32[]{:S(2)}, u32[]{:S(2)}) collective-permute-start(bf16[1,16,128,128]{3,2,1,0:T(8,128)(2,1)S(1)} %bitcast.64), channel_id=1, source_target_pairs={{0,2},{4,6},{8,10},{12,14},{16,18},{20,22},{24,26},{28,30},{1,3},{... | collective-permute-start | bytes 1572872 | tf_op jit(solution)/shard_map/ppermute | solution.py:29
  43.6 17.4 %collective-permute-start.9 = (bf16[1,16,128,128]{3,2,1,0:T(8,128)(2,1)S(1)}, bf16[1,16,128,128]{3,2,1,0:T(8,128)(2,1)}, u32[]{:S(2)}, u32[]{:S(2)}) collective-permute-start(bf16[1,16,128,128]{3,2,1,0:T(8,128)(2,1)S(1)} %bitcast.68), channel_id=1, source_target_pairs={{0,2},{4,6},{8,10},{12,14},{16,18},{20,22},{24,26},{28,30},{1,3},{... | collective-permute-start | bytes 1572872 | tf_op jit(solution)/shard_map/ppermute | solution.py:29
  45.7 19.2 %collective-permute-start.6 = (bf16[1,16,128,128]{3,2,1,0:T(8,128)(2,1)}, bf16[1,16,128,128]{3,2,1,0:T(8,128)(2,1)}, u32[]{:S(2)}, u32[]{:S(2)}) collective-permute-start(bf16[1,16,128,128]{3,2,1,0:T(8,128)(2,1)} %broadcast_select_fusion.3.refs_2_), channel_id=1, source_target_pairs={{0,2},{2,0},{4,6},{6,4},{8,10},{10,8},{12,14},{14,12},{16,18},{18,... | collective-permute-start | bytes 1572872 | tf_op jit(solution)/shard_map/ppermute | solution.py:24
  51.9 10.4 %collective-permute-start.3 = (bf16[1,16,128,128]{3,2,1,0:T(8,128)(2,1)}, bf16[1,16,128,128]{3,2,1,0:T(8,128)(2,1)}, u32[]{:S(2)}, u32[]{:S(2)}) collective-permute-start(bf16[1,16,128,128]{3,2,1,0:T(8,128)(2,1)} %collective-permute-done.1.refs_0_), channel_id=1, source_target_pairs={{2,0},{6,4},{10,8},{14,12},{18,16},{22,20},{26,24},{30,28},{3,1},{... | collective-permute-start | bytes 1572872 | tf_op jit(solution)/shard_map/ppermute | solution.py:29
  53.2 13.0 %collective-permute-start.10 = (bf16[1,16,128,128]{3,2,1,0:T(8,128)(2,1)}, bf16[1,16,128,128]{3,2,1,0:T(8,128)(2,1)}, u32[]{:S(2)}, u32[]{:S(2)}) collective-permute-start(bf16[1,16,128,128]{3,2,1,0:T(8,128)(2,1)} %collective-permute-done.8.refs_4_), channel_id=1, source_target_pairs={{2,0},{6,4},{10,8},{14,12},{18,16},{22,20},{26,24},{30,28},{3,1},{... | collective-permute-start | bytes 1572872 | tf_op jit(solution)/shard_map/ppermute | solution.py:29
  57.5 14.0 %copy-start.19 = (bf16[1,16,128,128]{3,2,1,0:T(8,128)(2,1)}, bf16[1,16,128,128]{3,2,1,0:T(8,128)(2,1)S(1)}, u32[]{:S(2)}) copy-start(bf16[1,16,128,128]{3,2,1,0:T(8,128)(2,1)S(1)} %broadcast_select_fusion.2.refs_6_) | copy-start | bytes 1572868
  57.5 30.3 %collective-permute-start.15 = (bf16[1,16,128,128]{3,2,1,0:T(8,128)(2,1)}, bf16[1,16,128,128]{3,2,1,0:T(8,128)(2,1)S(1)}, u32[]{:S(2)}, u32[]{:S(2)}) collective-permute-start(bf16[1,16,128,128]{3,2,1,0:T(8,128)(2,1)} %collective-permute-done.refs_2_), channel_id=1, source_target_pairs={{0,4},{2,6},{8,12},{10,14},{16,20},{18,22},{24,28},{26,30},{1,5},{... | collective-permute-start | bytes 1572872 | tf_op jit(solution)/shard_map/ppermute | solution.py:29
  61.0 26.8 %collective-permute-start.17 = (bf16[1,16,128,128]{3,2,1,0:T(8,128)(2,1)}, bf16[1,16,128,128]{3,2,1,0:T(8,128)(2,1)S(1)}, u32[]{:S(2)}, u32[]{:S(2)}) collective-permute-start(bf16[1,16,128,128]{3,2,1,0:T(8,128)(2,1)} %collective-permute-done.7.refs_5_), channel_id=1, source_target_pairs={{0,4},{2,6},{8,12},{10,14},{16,20},{18,22},{24,28},{26,30},{1,5},{... | collective-permute-start | bytes 1572872 | tf_op jit(solution)/shard_map/ppermute | solution.py:29
  62.4 9.1 %collective-permute-start.13 = (bf16[1,16,128,128]{3,2,1,0:T(8,128)(2,1)S(1)}, bf16[1,16,128,128]{3,2,1,0:T(8,128)(2,1)S(1)}, u32[]{:S(2)}, u32[]{:S(2)}) collective-permute-start(bf16[1,16,128,128]{3,2,1,0:T(8,128)(2,1)S(1)} %broadcast_select_fusion.2.refs_6_), channel_id=1, source_target_pairs={{0,2},{2,0},{4,6},{6,4},{8,10},{10,8},{12,14},{14,12},{16,18},{18,... | collective-permute-start | bytes 1572872 | tf_op jit(solution)/shard_map/ppermute | solution.py:24
  64.9 22.9 %collective-permute-start.16 = (bf16[1,16,128,128]{3,2,1,0:T(8,128)(2,1)}, bf16[1,16,128,128]{3,2,1,0:T(8,128)(2,1)S(1)}, u32[]{:S(2)}, u32[]{:S(2)}) collective-permute-start(bf16[1,16,128,128]{3,2,1,0:T(8,128)(2,1)} %collective-permute-done.1.refs_0_), channel_id=1, source_target_pairs={{4,0},{6,2},{12,8},{14,10},{20,16},{22,18},{28,24},{30,26},{5,1},{... | collective-permute-start | bytes 1572872 | tf_op jit(solution)/shard_map/ppermute | solution.py:29
  66.2 25.9 %collective-permute-start.18 = (bf16[1,16,128,128]{3,2,1,0:T(8,128)(2,1)}, bf16[1,16,128,128]{3,2,1,0:T(8,128)(2,1)S(1)}, u32[]{:S(2)}, u32[]{:S(2)}) collective-permute-start(bf16[1,16,128,128]{3,2,1,0:T(8,128)(2,1)} %collective-permute-done.8.refs_4_), channel_id=1, source_target_pairs={{4,0},{6,2},{12,8},{14,10},{20,16},{22,18},{28,24},{30,26},{5,1},{... | collective-permute-start | bytes 1572872 | tf_op jit(solution)/shard_map/ppermute | solution.py:29
  71.5 0.8 copy-start.22
  92.2 5.2 %copy-start.1 = (bf16[1,16,128,128]{3,2,1,0:T(8,128)(2,1)}, bf16[1,16,128,128]{3,2,1,0:T(8,128)(2,1)S(1)}, u32[]{:S(2)}) copy-start(bf16[1,16,128,128]{3,2,1,0:T(8,128)(2,1)S(1)} %broadcast_select_fusion.1.refs_1_) | copy-start | bytes 1572868
  92.2 2.0 %collective-permute-start.19 = (bf16[1,16,128,128]{3,2,1,0:T(8,128)(2,1)S(1)}, bf16[1,16,128,128]{3,2,1,0:T(8,128)(2,1)S(1)}, u32[]{:S(2)}, u32[]{:S(2)}) collective-permute-start(bf16[1,16,128,128]{3,2,1,0:T(8,128)(2,1)S(1)} %broadcast_select_fusion.1.refs_1_), channel_id=1, source_target_pairs={{0,2},{2,0},{4,6},{6,4},{8,10},{10,8},{12,14},{14,12},{16,18},{18,... | collective-permute-start | bytes 1572872 | tf_op jit(solution)/shard_map/ppermute | solution.py:24
  92.3 5.0 %copy-start.2 = (bf16[1,16,128,128]{3,2,1,0:T(8,128)(2,1)}, bf16[1,16,128,128]{3,2,1,0:T(8,128)(2,1)S(1)}, u32[]{:S(2)}) copy-start(bf16[1,16,128,128]{3,2,1,0:T(8,128)(2,1)S(1)} %broadcast_select_fusion.refs_3_) | copy-start | bytes 1572868
  92.3 4.1 %collective-permute-start.20 = (bf16[1,16,128,128]{3,2,1,0:T(8,128)(2,1)S(1)}, bf16[1,16,128,128]{3,2,1,0:T(8,128)(2,1)S(1)}, u32[]{:S(2)}, u32[]{:S(2)}) collective-permute-start(bf16[1,16,128,128]{3,2,1,0:T(8,128)(2,1)S(1)} %broadcast_select_fusion.refs_3_), channel_id=1, source_target_pairs={{0,2},{2,0},{4,6},{6,4},{8,10},{10,8},{12,14},{14,12},{16,18},{18,... | collective-permute-start | bytes 1572872 | tf_op jit(solution)/shard_map/ppermute | solution.py:24
  92.9 14.3 %collective-permute-start.14 = (bf16[1,16,128,128]{3,2,1,0:T(8,128)(2,1)}, bf16[1,16,128,128]{3,2,1,0:T(8,128)(2,1)}, u32[]{:S(2)}, u32[]{:S(2)}) collective-permute-start(bf16[1,16,128,128]{3,2,1,0:T(8,128)(2,1)} %get-tuple-element.35), channel_id=1, source_target_pairs={{0,2},{2,0},{4,6},{6,4},{8,10},{10,8},{12,14},{14,12},{16,18},{18,... | collective-permute-start | bytes 1572872 | tf_op jit(solution)/shard_map/ppermute | solution.py:24
  93.0 16.6 %collective-permute-start.22 = (bf16[1,16,128,128]{3,2,1,0:T(8,128)(2,1)}, bf16[1,16,128,128]{3,2,1,0:T(8,128)(2,1)S(1)}, u32[]{:S(2)}, u32[]{:S(2)}) collective-permute-start(bf16[1,16,128,128]{3,2,1,0:T(8,128)(2,1)} %get-tuple-element.45), channel_id=1, source_target_pairs={{0,2},{2,0},{4,6},{6,4},{8,10},{10,8},{12,14},{14,12},{16,18},{18,... | collective-permute-start | bytes 1572872 | tf_op jit(solution)/shard_map/ppermute | solution.py:24
  94.0 18.9 %collective-permute-start.24 = (bf16[1,16,128,128]{3,2,1,0:T(8,128)(2,1)}, bf16[1,16,128,128]{3,2,1,0:T(8,128)(2,1)}, u32[]{:S(2)}, u32[]{:S(2)}) collective-permute-start(bf16[1,16,128,128]{3,2,1,0:T(8,128)(2,1)} %collective-permute-done.refs_2_), channel_id=1, source_target_pairs={{0,2},{2,0},{4,6},{6,4},{8,10},{10,8},{12,14},{14,12},{16,18},{18,... | collective-permute-start | bytes 1572872 | tf_op jit(solution)/shard_map/ppermute | solution.py:24
  94.1 2.3 %copy-start.13 = (bf16[1,16,128,128]{3,2,1,0:T(8,128)(2,1)}, bf16[1,16,128,128]{3,2,1,0:T(8,128)(2,1)S(1)}, u32[]{:S(2)}) copy-start(bf16[1,16,128,128]{3,2,1,0:T(8,128)(2,1)S(1)} %collective-permute-done.19.refs_2_) | copy-start | bytes 1572868
  94.1 21.2 %collective-permute-start.25 = (bf16[1,16,128,128]{3,2,1,0:T(8,128)(2,1)}, bf16[1,16,128,128]{3,2,1,0:T(8,128)(2,1)}, u32[]{:S(2)}, u32[]{:S(2)}) collective-permute-start(bf16[1,16,128,128]{3,2,1,0:T(8,128)(2,1)} %collective-permute-done.7.refs_5_), channel_id=1, source_target_pairs={{0,2},{2,0},{4,6},{6,4},{8,10},{10,8},{12,14},{14,12},{16,18},{18,... | collective-permute-start | bytes 1572872 | tf_op jit(solution)/shard_map/ppermute | solution.py:24
  96.4 0.8 copy-start.14
  97.2 10.3 %copy-start.12 = (bf16[1,16,128,128]{3,2,1,0:T(8,128)(2,1)S(1)}, bf16[1,16,128,128]{3,2,1,0:T(8,128)(2,1)}, u32[]{:S(2)}) copy-start(bf16[1,16,128,128]{3,2,1,0:T(8,128)(2,1)} %get-tuple-element.34) | copy-start | bytes 1572868
  97.2 12.7 %copy-start.11 = (bf16[1,16,128,128]{3,2,1,0:T(8,128)(2,1)S(1)}, bf16[1,16,128,128]{3,2,1,0:T(8,128)(2,1)}, u32[]{:S(2)}) copy-start(bf16[1,16,128,128]{3,2,1,0:T(8,128)(2,1)} %get-tuple-element.44) | copy-start | bytes 1572868
  97.2 31.3 %collective-permute-start.26 = (bf16[1,16,128,128]{3,2,1,0:T(8,128)(2,1)}, bf16[1,16,128,128]{3,2,1,0:T(8,128)(2,1)S(1)}, u32[]{:S(2)}, u32[]{:S(2)}) collective-permute-start(bf16[1,16,128,128]{3,2,1,0:T(8,128)(2,1)} %get-tuple-element.52), channel_id=1, source_target_pairs={{0,2},{2,0},{4,6},{6,4},{8,10},{10,8},{12,14},{14,12},{16,18},{18,... | collective-permute-start | bytes 1572872 | tf_op jit(solution)/shard_map/ppermute | solution.py:24
  107.2 3.6 %copy-start.16 = (bf16[1,16,128,128]{3,2,1,0:T(8,128)(2,1)S(1)}, bf16[1,16,128,128]{3,2,1,0:T(8,128)(2,1)}, u32[]{:S(2)}) copy-start(bf16[1,16,128,128]{3,2,1,0:T(8,128)(2,1)} %get-tuple-element.42) | copy-start | bytes 1572868
  107.2 3.6 %collective-permute-start.21 = (bf16[1,16,128,128]{3,2,1,0:T(8,128)(2,1)}, bf16[1,16,128,128]{3,2,1,0:T(8,128)(2,1)S(1)}, u32[]{:S(2)}, u32[]{:S(2)}) collective-permute-start(bf16[1,16,128,128]{3,2,1,0:T(8,128)(2,1)} %get-tuple-element.43), channel_id=1, source_target_pairs={{0,2},{2,0},{4,6},{6,4},{8,10},{10,8},{12,14},{14,12},{16,18},{18,... | collective-permute-start | bytes 1572872 | tf_op jit(solution)/shard_map/ppermute | solution.py:24
  107.5 4.2 %copy-start.15 = (bf16[1,16,128,128]{3,2,1,0:T(8,128)(2,1)S(1)}, bf16[1,16,128,128]{3,2,1,0:T(8,128)(2,1)}, u32[]{:S(2)}) copy-start(bf16[1,16,128,128]{3,2,1,0:T(8,128)(2,1)} %get-tuple-element.46) | copy-start | bytes 1572868
  109.5 2.1 %collective-permute-start.23 = (bf16[1,16,128,128]{3,2,1,0:T(8,128)(2,1)}, bf16[1,16,128,128]{3,2,1,0:T(8,128)(2,1)S(1)}, u32[]{:S(2)}, u32[]{:S(2)}) collective-permute-start(bf16[1,16,128,128]{3,2,1,0:T(8,128)(2,1)} %get-tuple-element.47), channel_id=1, source_target_pairs={{0,2},{2,0},{4,6},{6,4},{8,10},{10,8},{12,14},{14,12},{16,18},{18,... | collective-permute-start | bytes 1572872 | tf_op jit(solution)/shard_map/ppermute | solution.py:24
  112.6 15.9 %collective-permute-start.29 = (bf16[1,16,128,128]{3,2,1,0:T(8,128)(2,1)S(1)}, bf16[1,16,128,128]{3,2,1,0:T(8,128)(2,1)S(1)}, u32[]{:S(2)}, u32[]{:S(2)}) collective-permute-start(bf16[1,16,128,128]{3,2,1,0:T(8,128)(2,1)S(1)} %add_convert_fusion.2), channel_id=1, source_target_pairs={{0,4},{2,6},{4,0},{6,2},{8,12},{10,14},{12,8},{14,10},{16,20},{18,... | collective-permute-start | bytes 1572872 | tf_op jit(solution)/shard_map/ppermute | solution.py:24
  112.6 19.4 %collective-permute-start.32 = (bf16[1,16,128,128]{3,2,1,0:T(8,128)(2,1)}, bf16[1,16,128,128]{3,2,1,0:T(8,128)(2,1)S(1)}, u32[]{:S(2)}, u32[]{:S(2)}) collective-permute-start(bf16[1,16,128,128]{3,2,1,0:T(8,128)(2,1)} %get-tuple-element.59), channel_id=1, source_target_pairs={{0,2},{2,0},{4,6},{6,4},{8,10},{10,8},{12,14},{14,12},{16,18},{18,... | collective-permute-start | bytes 1572872 | tf_op jit(solution)/shard_map/ppermute | solution.py:24
  112.9 25.7 %collective-permute-start.35 = (bf16[1,16,128,128]{3,2,1,0:T(8,128)(2,1)}, bf16[1,16,128,128]{3,2,1,0:T(8,128)(2,1)S(1)}, u32[]{:S(2)}, u32[]{:S(2)}) collective-permute-start(bf16[1,16,128,128]{3,2,1,0:T(8,128)(2,1)} %add_convert_fusion), channel_id=1, source_target_pairs={{0,4},{2,6},{4,0},{6,2},{8,12},{10,14},{12,8},{14,10},{16,20},{18,... | collective-permute-start | bytes 1572872 | tf_op jit(solution)/shard_map/ppermute | solution.py:24
  115.3 34.5 %collective-permute-start.27 = (bf16[1,16,128,128]{3,2,1,0:T(8,128)(2,1)}, bf16[1,16,128,128]{3,2,1,0:T(8,128)(2,1)S(1)}, u32[]{:S(2)}, u32[]{:S(2)}) collective-permute-start(bf16[1,16,128,128]{3,2,1,0:T(8,128)(2,1)} %add_convert_fusion.3), channel_id=1, source_target_pairs={{0,4},{2,6},{4,0},{6,2},{8,12},{10,14},{12,8},{14,10},{16,20},{18,... | collective-permute-start | bytes 1572872 | tf_op jit(solution)/shard_map/ppermute | solution.py:24
  128.4 10.2 %copy-start.20 = (bf16[1,16,128,128]{3,2,1,0:T(8,128)(2,1)S(1)}, bf16[1,16,128,128]{3,2,1,0:T(8,128)(2,1)}, u32[]{:S(2)}) copy-start(bf16[1,16,128,128]{3,2,1,0:T(8,128)(2,1)} %get-tuple-element.64) | copy-start | bytes 1572868
  128.5 22.7 %collective-permute-start.28 = (bf16[1,16,128,128]{3,2,1,0:T(8,128)(2,1)}, bf16[1,16,128,128]{3,2,1,0:T(8,128)(2,1)}, u32[]{:S(2)}, u32[]{:S(2)}) collective-permute-start(bf16[1,16,128,128]{3,2,1,0:T(8,128)(2,1)} %get-tuple-element.55), channel_id=1, source_target_pairs={{0,2},{2,0},{4,6},{6,4},{8,10},{10,8},{12,14},{14,12},{16,18},{18,... | collective-permute-start | bytes 1572872 | tf_op jit(solution)/shard_map/ppermute | solution.py:24
  130.7 20.4 %collective-permute-start.30 = (bf16[1,16,128,128]{3,2,1,0:T(8,128)(2,1)}, bf16[1,16,128,128]{3,2,1,0:T(8,128)(2,1)}, u32[]{:S(2)}, u32[]{:S(2)}) collective-permute-start(bf16[1,16,128,128]{3,2,1,0:T(8,128)(2,1)} %fusion.7), channel_id=1, source_target_pairs={{8,0},{10,2},{12,4},{14,6},{16,8},{18,10},{20,12},{22,14},{24,16},... | collective-permute-start | bytes 1572872 | tf_op jit(solution)/shard_map/ppermute | solution.py:20
  132.0 28.4 %collective-permute-start.33 = (bf16[1,16,128,128]{3,2,1,0:T(8,128)(2,1)}, bf16[1,16,128,128]{3,2,1,0:T(8,128)(2,1)S(1)}, u32[]{:S(2)}, u32[]{:S(2)}) collective-permute-start(bf16[1,16,128,128]{3,2,1,0:T(8,128)(2,1)} %add_convert_fusion.1), channel_id=1, source_target_pairs={{0,4},{2,6},{4,0},{6,2},{8,12},{10,14},{12,8},{14,10},{16,20},{18,... | collective-permute-start | bytes 1572872 | tf_op jit(solution)/shard_map/ppermute | solution.py:24
  138.6 21.8 %collective-permute-start.34 = (bf16[1,16,128,128]{3,2,1,0:T(8,128)(2,1)}, bf16[1,16,128,128]{3,2,1,0:T(8,128)(2,1)}, u32[]{:S(2)}, u32[]{:S(2)}) collective-permute-start(bf16[1,16,128,128]{3,2,1,0:T(8,128)(2,1)} %get-tuple-element.62), channel_id=1, source_target_pairs={{0,2},{2,0},{4,6},{6,4},{8,10},{10,8},{12,14},{14,12},{16,18},{18,... | collective-permute-start | bytes 1572872 | tf_op jit(solution)/shard_map/ppermute | solution.py:24
  149.8 20.0 %copy-start.4 = (bf16[1,16,128,128]{3,2,1,0:T(8,128)(2,1)}, bf16[1,16,128,128]{3,2,1,0:T(8,128)(2,1)S(1)}, u32[]{:S(2)}) copy-start(bf16[1,16,128,128]{3,2,1,0:T(8,128)(2,1)S(1)} %collective-permute-done.27) | copy-start | bytes 1572868
  149.8 17.5 %collective-permute-start.36 = (bf16[1,16,128,128]{3,2,1,0:T(8,128)(2,1)}, bf16[1,16,128,128]{3,2,1,0:T(8,128)(2,1)}, u32[]{:S(2)}, u32[]{:S(2)}) collective-permute-start(bf16[1,16,128,128]{3,2,1,0:T(8,128)(2,1)} %fusion.18), channel_id=1, source_target_pairs={{8,0},{10,2},{12,4},{14,6},{16,8},{18,10},{20,12},{22,14},{24,16},... | collective-permute-start | bytes 1572872 | tf_op jit(solution)/shard_map/ppermute | solution.py:20
  151.1 16.2 %copy-start.21 = (bf16[1,16,128,128]{3,2,1,0:T(8,128)(2,1)S(1)}, bf16[1,16,128,128]{3,2,1,0:T(8,128)(2,1)}, u32[]{:S(2)}) copy-start(bf16[1,16,128,128]{3,2,1,0:T(8,128)(2,1)} %get-tuple-element.61) | copy-start | bytes 1572868
  153.8 17.3 %copy-start.3 = (f32[16,128,256]{2,1,0:T(8,128)S(1)}, f32[16,128,256]{2,1,0:T(8,128)}, u32[]{:S(2)}) copy-start(f32[16,128,256]{2,1,0:T(8,128)} %get-tuple-element.50) | copy-start | bytes 6291460
  153.8 24.8 %collective-permute-start.31 = (bf16[128,16,128]{2,0,1:T(8,128)(2,1)}, bf16[128,16,128]{2,0,1:T(8,128)(2,1)}, u32[]{:S(2)}, u32[]{:S(2)}) collective-permute-start(bf16[128,16,128]{2,0,1:T(8,128)(2,1)} %fusion.23), channel_id=1, source_target_pairs={{8,0},{10,2},{12,4},{14,6},{16,8},{18,10},{20,12},{22,14},{24,16},... | collective-permute-start | bytes 1572872 | tf_op jit(solution)/shard_map/ppermute | solution.py:20
  160.4 10.7 %copy-start.6 = (bf16[1,16,128,128]{3,2,1,0:T(8,128)(2,1)}, bf16[1,16,128,128]{3,2,1,0:T(8,128)(2,1)S(1)}, u32[]{:S(2)}) copy-start(bf16[1,16,128,128]{3,2,1,0:T(8,128)(2,1)S(1)} %collective-permute-done.33) | copy-start | bytes 1572868
  169.8 18.1 %collective-permute-start.37 = (bf16[128,16,128]{2,0,1:T(8,128)(2,1)}, bf16[128,16,128]{2,0,1:T(8,128)(2,1)}, u32[]{:S(2)}, u32[]{:S(2)}) collective-permute-start(bf16[128,16,128]{2,0,1:T(8,128)(2,1)} %fusion.22), channel_id=1, source_target_pairs={{8,0},{10,2},{12,4},{14,6},{16,8},{18,10},{20,12},{22,14},{24,16},... | collective-permute-start | bytes 1572872 | tf_op jit(solution)/shard_map/ppermute | solution.py:20
  171.7 6.9 %copy-start.5 = (bf16[1,16,128,128]{3,2,1,0:T(8,128)(2,1)S(1)}, bf16[1,16,128,128]{3,2,1,0:T(8,128)(2,1)}, u32[]{:S(2)}) copy-start(bf16[1,16,128,128]{3,2,1,0:T(8,128)(2,1)} %copy-done.4) | copy-start | bytes 1572868
  175.4 12.5 %copy-start.7 = (bf16[1,16,128,128]{3,2,1,0:T(8,128)(2,1)S(1)}, bf16[1,16,128,128]{3,2,1,0:T(8,128)(2,1)}, u32[]{:S(2)}) copy-start(bf16[1,16,128,128]{3,2,1,0:T(8,128)(2,1)} %copy-done.6) | copy-start | bytes 1572868
  175.4 12.5 %copy-start.10 = (bf16[1,16,128,128]{3,2,1,0:T(8,128)(2,1)S(1)}, bf16[1,16,128,128]{3,2,1,0:T(8,128)(2,1)}, u32[]{:S(2)}) copy-start(bf16[1,16,128,128]{3,2,1,0:T(8,128)(2,1)} %get-tuple-element.58) | copy-start | bytes 1572868

commit v17 on v14

--- a/solution.py
+++ b/solution.py
@@ -180,6 +180,7 @@
     modes = [0, 1, 1, 2, 1, 1, 1, 1, 1]
     dist = [0, PLANE, 3 + 2 * core, 2 * PLANE, 7 - 6 * core, 2, 1 + 2 * core, 6, 5 + 2 * core]
     terms = [None] * 18
+    spans = (slice(0, heads_kv // 2), slice(heads_kv // 2, heads_kv))
     acc = None
     ys = None
     qb = q4
@@ -191,10 +192,13 @@
             terms[j] = out[m]
             terms[9 + j] = out[len(sel) + m]
         if ys is None:
-            ys = gather_y(terms[:9], n) + gather_y(terms[9:], n)
+            ys = [gather_y([None if t is None else t[:, hs] for t in terms[base:base + 9]], n)
+                  for hs in spans for base in (0, 9)]
             ys, qb = lax.optimization_barrier((ys, q4))
-    grad_k = unroute(terms[:9], ys[0], ys[1], n, half, core)
-    grad_v = unroute(terms[9:], ys[2], ys[3], n, half, core)
+    grads = [unroute([t[:, hs] for t in terms[base:base + 9]], *ys[2 * i + s], n, half, core)
+             for i, hs in enumerate(spans) for s, base in enumerate((0, 9))]
+    grad_k = jnp.concatenate(grads[0::2], axis=1)
+    grad_v = jnp.concatenate(grads[1::2], axis=1)
 
     dq = (acc * SCALE).astype(jnp.bfloat16).reshape(heads_kv, width, groups, tok)
     grad_query = dq.transpose(3, 0, 2, 1).reshape(tok, heads_q, width)

time: 187 us -> 213 us (1.14)
  waiting for transfers between devices: 53.1 us -> 76.9 us
  other arithmetic: 22.5 us -> 12.8 us
  starting transfers between devices: 60.4 us -> 67.6 us
  local copies, waits for them, and re-layouts: 14.1 us -> 19.2 us
    ppermute x8 -> x12, waiting for transfers between devices: 19.2 us -> 32.9 us  [shift(): return lax.ppermute(x, 'seq', pairs)]
    ppermute x18 -> x30, waiting for transfers between devices: 21.9 us -> 31.4 us  [swap(): return lax.ppermute(x, 'seq', [(i, i ^ bit) for i in range(n)])]
    slice x0 -> x8, local copies, waits for them, and re-layouts: none -> 4.91 us  [per_device(): t[:, hs]]
    transpose x2, other arithmetic: 5.05 us -> 0.9 us  [unroute(): last = shift(part1.astype(bf16)[0].transpose(1, 0, 2), n, -PLANE)]
    ppermute x8 -> x12, starting transfers between devices: 23.6 us -> 27.7 us  [shift(): return lax.ppermute(x, 'seq', pairs)]
    ppermute x18 -> x30, starting transfers between devices: 7.79 us -> 11.4 us  [swap(): return lax.ppermute(x, 'seq', [(i, i ^ bit) for i in range(n)])]
    convert_element_type x2, other arithmetic: 3.19 us -> 0.56 us  [unroute(): part1 = part1 + shift(part2.astype(bf16), n, -PLANE).astype(f32)]
    convert_element_type x2, other arithmetic: 2.95 us -> 0.71 us  [unroute(): return (part0[0].transpose(1, 0, 2) + last.astype(f32)).astype(bf16)]
  transfers between devices with their start and end apart: 38 -> 54, of which waited for: 14 -> 21; matrix products, arithmetic and copies ran while one was open for 17% -> 12% of each run, Pallas kernels for 7% -> 6%
where the time goes in v17:
time: 213 us; the launch traced here: 212 us
  waiting for transfers between devices  76.9 us (36%)
  starting transfers between devices  67.6 us (32%)
  Pallas kernels  34.7 us (16%)
  local copies, waits for them, and re-layouts  19.2 us (9%)
  other arithmetic  12.8 us (6%)
    pallas_call x2, Pallas kernels, attend_blocks(): pl.pallas_call(functools.partial(_blocks_kernel, tuple(modes), acc is not...  34.7 us
    ppermute x12, waiting for transfers between devices, shift(): return lax.ppermute(x, 'seq', pairs)  32.9 us
    ppermute x30, waiting for transfers between devices, swap(): return lax.ppermute(x, 'seq', [(i, i ^ bit) for i in range(n)])  31.4 us
    ppermute x12, starting transfers between devices, one_way(): return lax.ppermute(x, 'seq', pairs)  28.5 us
    ppermute x12, starting transfers between devices, shift(): return lax.ppermute(x, 'seq', pairs)  27.7 us
    ppermute x12, waiting for transfers between devices, one_way(): return lax.ppermute(x, 'seq', pairs)  12.6 us
    ppermute x30, starting transfers between devices, swap(): return lax.ppermute(x, 'seq', [(i, i ^ bit) for i in range(n)])  11.4 us
    unnamed x76, local copies, waits for them, and re-layouts  6.65 us
  transfers between devices with their start and end apart: 54, of which 21 were waited for; matrix products, arithmetic and copies ran while one was open for 12% of the time, Pallas kernels for 6%

profile of v17, /device:TPU:0, one launch (start us, length us, event | category | flops | bytes accessed | tf_op | source)
XLA Modules:
  0.0 212.4 jit_solution(15691241950175924679)
XLA Ops:
  0.7 1.3 copy.27
  2.0 5.7 %collective-permute-start = (bf16[1,16,128,128]{3,2,1,0:T(8,128)(2,1)S(1)}, bf16[1,16,128,128]{3,2,1,0:T(8,128)(2,1)}, u32[]{:S(2)}, u32[]{:S(2)}) collective-permute-start(bf16[1,16,128,128]{3,2,1,0:T(8,128)(2,1)S(1)} %bitcast.84), channel_id=1, source_target_pairs={{0,8},{2,10},{4,12},{6,14},{8,16},{10,18},{12,20},{14,22},{16,24},... | collective-permute-start | bytes 1572872 | tf_op jit(solution)/shard_map/ppermute | solution.py:20
  7.7 1.2 copy.26
  8.9 3.5 %collective-permute-start.10 = (bf16[1,16,128,128]{3,2,1,0:T(8,128)(2,1)S(1)}, bf16[1,16,128,128]{3,2,1,0:T(8,128)(2,1)}, u32[]{:S(2)}, u32[]{:S(2)}) collective-permute-start(bf16[1,16,128,128]{3,2,1,0:T(8,128)(2,1)S(1)} %bitcast.88), channel_id=1, source_target_pairs={{0,8},{2,10},{4,12},{6,14},{8,16},{10,18},{12,20},{14,22},{16,24},... | collective-permute-start | bytes 1572872 | tf_op jit(solution)/shard_map/ppermute | solution.py:20
  12.4 4.2 %collective-permute-start.4 = (bf16[1,16,128,128]{3,2,1,0:T(8,128)(2,1)S(1)}, bf16[1,16,128,128]{3,2,1,0:T(8,128)(2,1)}, u32[]{:S(2)}, u32[]{:S(2)}) collective-permute-start(bf16[1,16,128,128]{3,2,1,0:T(8,128)(2,1)S(1)} %bitcast.85), channel_id=1, source_target_pairs={{0,4},{2,6},{8,12},{10,14},{16,20},{18,22},{24,28},{26,30},{1,5},{... | collective-permute-start | bytes 1572872 | tf_op jit(solution)/shard_map/ppermute | solution.py:29
  16.6 2.6 %collective-permute-done.refs_2_ = bf16[1,16,128,128]{3,2,1,0:T(8,128)(2,1)} collective-permute-done((bf16[1,16,128,128]{3,2,1,0:T(8,128)(2,1)S(1)}, bf16[1,16,128,128]{3,2,1,0:T(8,128)(2,1)}, u32[]{:S(2)}, u32[]{:S(2)}) %collective-permute-start) | collective-permute-done | bytes 524320 | tf_op jit(solution)/shard_map/ppermute | solution.py:20
  19.2 5.3 %collective-permute-start.1 = (bf16[1,16,128,128]{3,2,1,0:T(8,128)(2,1)}, bf16[1,16,128,128]{3,2,1,0:T(8,128)(2,1)}, u32[]{:S(2)}, u32[]{:S(2)}) collective-permute-start(bf16[1,16,128,128]{3,2,1,0:T(8,128)(2,1)} %collective-permute-done.refs_2_), channel_id=1, source_target_pairs={{0,8},{2,10},{4,12},{6,14},{8,16},{10,18},{12,20},{14,22},{16,24},... | collective-permute-start | bytes 1572872 | tf_op jit(solution)/shard_map/ppermute | solution.py:20
  24.5 1.3 collective-permute-start.5
  25.8 6.2 %collective-permute-start.14 = (bf16[1,16,128,128]{3,2,1,0:T(8,128)(2,1)S(1)}, bf16[1,16,128,128]{3,2,1,0:T(8,128)(2,1)}, u32[]{:S(2)}, u32[]{:S(2)}) collective-permute-start(bf16[1,16,128,128]{3,2,1,0:T(8,128)(2,1)S(1)} %bitcast.89), channel_id=1, source_target_pairs={{0,4},{2,6},{8,12},{10,14},{16,20},{18,22},{24,28},{26,30},{1,5},{... | collective-permute-start | bytes 1572872 | tf_op jit(solution)/shard_map/ppermute | solution.py:29
  32.6 1.4 copy.16
  34.0 1.4 copy.17
  35.4 2.7 %collective-permute-start.11 = (bf16[1,16,128,128]{3,2,1,0:T(8,128)(2,1)}, bf16[1,16,128,128]{3,2,1,0:T(8,128)(2,1)S(1)}, u32[]{:S(2)}, u32[]{:S(2)}) collective-permute-start(bf16[1,16,128,128]{3,2,1,0:T(8,128)(2,1)} %collective-permute-done.10.refs_5_), channel_id=1, source_target_pairs={{0,8},{2,10},{4,12},{6,14},{8,16},{10,18},{12,20},{14,22},{16,24},... | collective-permute-start | bytes 1572872 | tf_op jit(solution)/shard_map/ppermute | solution.py:20
  38.1 1.3 collective-permute-start.15
  41.8 4.1 %collective-permute-start.7 = (bf16[1,16,128,128]{3,2,1,0:T(8,128)(2,1)}, bf16[1,16,128,128]{3,2,1,0:T(8,128)(2,1)S(1)}, u32[]{:S(2)}, u32[]{:S(2)}) collective-permute-start(bf16[1,16,128,128]{3,2,1,0:T(8,128)(2,1)} %collective-permute-done.refs_2_), channel_id=1, source_target_pairs={{0,4},{2,6},{8,12},{10,14},{16,20},{18,22},{24,28},{26,30},{1,5},{... | collective-permute-start | bytes 1572872 | tf_op jit(solution)/shard_map/ppermute | solution.py:29
  46.0 1.3 collective-permute-start.8
  47.3 1.1 broadcast_select_fusion.3.refs_2_
  48.4 1.3 collective-permute-start.2
  49.7 2.2 %collective-permute-done.11.refs_6_ = bf16[1,16,128,128]{3,2,1,0:T(8,128)(2,1)S(1)} collective-permute-done((bf16[1,16,128,128]{3,2,1,0:T(8,128)(2,1)}, bf16[1,16,128,128]{3,2,1,0:T(8,128)(2,1)S(1)}, u32[]{:S(2)}, u32[]{:S(2)}) %collective-permute-start.11) | collective-permute-done | bytes 524320 | tf_op jit(solution)/shard_map/ppermute | solution.py:20
  51.9 3.4 %collective-permute-start.17 = (bf16[1,16,128,128]{3,2,1,0:T(8,128)(2,1)}, bf16[1,16,128,128]{3,2,1,0:T(8,128)(2,1)S(1)}, u32[]{:S(2)}, u32[]{:S(2)}) collective-permute-start(bf16[1,16,128,128]{3,2,1,0:T(8,128)(2,1)} %collective-permute-done.10.refs_5_), channel_id=1, source_target_pairs={{0,4},{2,6},{8,12},{10,14},{16,20},{18,22},{24,28},{26,30},{1,5},{... | collective-permute-start | bytes 1572872 | tf_op jit(solution)/shard_map/ppermute | solution.py:29
  55.4 1.3 collective-permute-start.18
  56.8 1.3 collective-permute-start.12
  58.1 7.1 %collective-permute-done.8 = bf16[1,16,128,128]{3,2,1,0:T(8,128)(2,1)S(1)} collective-permute-done((bf16[1,16,128,128]{3,2,1,0:T(8,128)(2,1)}, bf16[1,16,128,128]{3,2,1,0:T(8,128)(2,1)S(1)}, u32[]{:S(2)}, u32[]{:S(2)}) %collective-permute-start.8) | collective-permute-done | bytes 524320 | tf_op jit(solution)/shard_map/ppermute | solution.py:29
  65.2 1.3 collective-permute-start.3
  66.6 1.2 collective-permute-start.6
  67.8 5.5 %collective-permute-done.18 = bf16[1,16,128,128]{3,2,1,0:T(8,128)(2,1)S(1)} collective-permute-done((bf16[1,16,128,128]{3,2,1,0:T(8,128)(2,1)S(1)}, bf16[1,16,128,128]{3,2,1,0:T(8,128)(2,1)S(1)}, u32[]{:S(2)}, u32[]{:S(2)}) %collective-permute-start.18) | collective-permute-done | bytes 524320 | tf_op jit(solution)/shard_map/ppermute | solution.py:29
  73.2 1.5 collective-permute-start.13
  74.8 1.2 collective-permute-start.16
  76.5 0.8 broadcast_select_fusion.5.refs_1_
  77.4 0.9 broadcast_select_fusion.4.refs_7_
  80.1 21.8 %shard_map.85 = (f32[16,128,256]{2,1,0:T(8,128)}, bf16[1,16,128,128]{3,2,1,0:T(8,128)(2,1)}, bf16[1,16,128,128]{3,2,1,0:T(8,128)(2,1)}, bf16[1,16,128,128]{3,2,1...) custom-call(s32[6]{0:T(128)} %stack.58.valid_ref, ...), custom_call_target="tpu_custom_call" | custom-call | flops 4026531840 | bytes 14680064 | tf_op jit(solution)/shard_map/pallas_call | solution.py:105
  101.9 1.2 fusion.55
  103.7 1.1 fusion.54
  107.9 1.0 add_convert_fusion.3
  109.8 1.0 add_convert_fusion.2
  110.9 0.9 add_convert_fusion.1
  112.3 1.0 add_convert_fusion
  114.3 12.9 %shard_map.86 = (f32[16,128,256]{2,1,0:T(8,128)}, bf16[1,16,128,128]{3,2,1,0:T(8,128)(2,1)}, bf16[1,16,128,128]{3,2,1,0:T(8,128)(2,1)}, bf16[1,16,128,128]{3,2,1...) custom-call(s32[3]{0:T(128)} %add_convert_fusion.8.valid_ref, ...), custom_call_target="tpu_custom_call" | custom-call | flops 2013265920 | bytes 10485760 | tf_op jit(solution)/shard_map/pallas_call | solution.py:105
  127.1 1.9 multiply_convert_fusion
  129.1 2.0 collective-permute-start.39
  132.3 3.8 %copy.21 = bf16[128,16,2,128]{3,2,1,0:T(2,128)(2,1)} copy(bf16[128,16,2,128]{0,2,3,1:T(2,128)(2,1)S(1)} %bitcast.77) | data formatting | bytes 2097152 | tf_op jit(solution)/shard_map/transpose | solution.py:204
  136.8 1.7 collective-permute-done.33
  138.5 5.6 %collective-permute-done.39 = bf16[1,8,128,128]{3,2,1,0:T(8,128)(2,1)S(1)} collective-permute-done((bf16[1,8,128,128]{3,2,1,0:T(8,128)(2,1)}, bf16[1,8,128,128]{3,2,1,0:T(8,128)(2,1)S(1)}, u32[]{:S(2)}, u32[]{:S(2)}) %collective-permute-start.39) | collective-permute-done | bytes 262176 | tf_op jit(solution)/shard_map/ppermute | solution.py:24
  144.4 2.0 collective-permute-start.37
  146.5 3.2 %collective-permute-done.31 = bf16[1,8,128,128]{3,2,1,0:T(8,128)(2,1)S(1)} collective-permute-done((bf16[1,8,128,128]{3,2,1,0:T(8,128)(2,1)}, bf16[1,8,128,128]{3,2,1,0:T(8,128)(2,1)S(1)}, u32[]{:S(2)}, u32[]{:S(2)}) %collective-permute-start.31) | collective-permute-done | bytes 262176 | tf_op jit(solution)/shard_map/ppermute | solution.py:24
  149.8 5.5 %collective-permute-done.45 = bf16[1,8,128,128]{3,2,1,0:T(8,128)(2,1)S(1)} collective-permute-done((bf16[1,8,128,128]{3,2,1,0:T(8,128)(2,1)}, bf16[1,8,128,128]{3,2,1,0:T(8,128)(2,1)S(1)}, u32[]{:S(2)}, u32[]{:S(2)}) %collective-permute-start.45) | collective-permute-done | bytes 262176 | tf_op jit(solution)/shard_map/ppermute | solution.py:24
  155.3 1.3 collective-permute-start.34
  156.6 4.3 %collective-permute-done.51 = bf16[1,8,128,128]{3,2,1,0:T(8,128)(2,1)S(1)} collective-permute-done((bf16[1,8,128,128]{3,2,1,0:T(8,128)(2,1)}, bf16[1,8,128,128]{3,2,1,0:T(8,128)(2,1)S(1)}, u32[]{:S(2)}, u32[]{:S(2)}) %collective-permute-start.51) | collective-permute-done | bytes 262176 | tf_op jit(solution)/shard_map/ppermute | solution.py:24
  160.9 1.3 collective-permute-start.40
  162.5 4.0 %collective-permute-done.37 = bf16[1,8,128,128]{3,2,1,0:T(8,128)(2,1)S(1)} collective-permute-done((bf16[1,8,128,128]{3,2,1,0:T(8,128)(2,1)S(1)}, bf16[1,8,128,128]{3,2,1,0:T(8,128)(2,1)S(1)}, u32[]{:S(2)}, u32[]{:S(2)}) %collective-permute-start.37) | collective-permute-done | bytes 262176 | tf_op jit(solution)/shard_map/ppermute | solution.py:24
  166.7 5.5 %collective-permute-done.43 = bf16[1,8,128,128]{3,2,1,0:T(8,128)(2,1)S(1)} collective-permute-done((bf16[1,8,128,128]{3,2,1,0:T(8,128)(2,1)S(1)}, bf16[1,8,128,128]{3,2,1,0:T(8,128)(2,1)S(1)}, u32[]{:S(2)}, u32[]{:S(2)}) %collective-permute-start.43) | collective-permute-done | bytes 262176 | tf_op jit(solution)/shard_map/ppermute | solution.py:24
  172.2 1.3 collective-permute-start.46
  173.5 1.3 collective-permute-start.52
  175.2 1.4 collective-permute-start.35
  177.2 1.3 collective-permute-start.41
  178.5 4.6 %collective-permute-done.46 = bf16[1,8,128,128]{3,2,1,0:T(8,128)(2,1)S(1)} collective-permute-done((bf16[1,8,128,128]{3,2,1,0:T(8,128)(2,1)S(1)}, bf16[1,8,128,128]{3,2,1,0:T(8,128)(2,1)S(1)}, u32[]{:S(2)}, u32[]{:S(2)}) %collective-permute-start.46) | collective-permute-done | bytes 262176 | tf_op jit(solution)/shard_map/ppermute | solution.py:20
  183.2 5.6 %collective-permute-done.52 = bf16[1,8,128,128]{3,2,1,0:T(8,128)(2,1)S(1)} collective-permute-done((bf16[1,8,128,128]{3,2,1,0:T(8,128)(2,1)S(1)}, bf16[1,8,128,128]{3,2,1,0:T(8,128)(2,1)S(1)}, u32[]{:S(2)}, u32[]{:S(2)}) %collective-permute-start.52) | collective-permute-done | bytes 262176 | tf_op jit(solution)/shard_map/ppermute | solution.py:20
  189.3 1.3 collective-permute-start.47
  190.6 1.3 collective-permute-start.53
  191.9 2.5 %collective-permute-done.35 = bf16[128,8,128]{2,0,1:T(8,128)(2,1)S(1)} collective-permute-done((bf16[128,8,128]{2,0,1:T(8,128)(2,1)S(1)}, bf16[128,8,128]{2,0,1:T(8,128)(2,1)S(1)}, u32[]{:S(2)}, u32[]{:S(2)}) %collective-permute-start.35) | collective-permute-done | bytes 262176 | tf_op jit(solution)/shard_map/ppermute | solution.py:20
  194.4 5.6 %collective-permute-done.41 = bf16[128,8,128]{2,0,1:T(8,128)(2,1)S(1)} collective-permute-done((bf16[128,8,128]{2,0,1:T(8,128)(2,1)S(1)}, bf16[128,8,128]{2,0,1:T(8,128)(2,1)S(1)}, u32[]{:S(2)}, u32[]{:S(2)}) %collective-permute-start.41) | collective-permute-done | bytes 262176 | tf_op jit(solution)/shard_map/ppermute | solution.py:20
  200.4 1.1 copy.22
  201.6 4.1 %collective-permute-done.47 = bf16[128,8,128]{2,0,1:T(8,128)(2,1)S(1)} collective-permute-done((bf16[128,8,128]{2,0,1:T(8,128)(2,1)S(1)}, bf16[128,8,128]{2,0,1:T(8,128)(2,1)S(1)}, u32[]{:S(2)}, u32[]{:S(2)}) %collective-permute-start.47) | collective-permute-done | bytes 262176 | tf_op jit(solution)/shard_map/ppermute | solution.py:20
  205.6 5.2 %collective-permute-done.53 = bf16[128,8,128]{2,0,1:T(8,128)(2,1)S(1)} collective-permute-done((bf16[128,8,128]{2,0,1:T(8,128)(2,1)S(1)}, bf16[128,8,128]{2,0,1:T(8,128)(2,1)S(1)}, u32[]{:S(2)}, u32[]{:S(2)}) %collective-permute-start.53) | collective-permute-done | bytes 262176 | tf_op jit(solution)/shard_map/ppermute | solution.py:20
  211.3 1.1 copy.23
  (158 shorter events, 16.7 us)
Async XLA Ops:
  0.6 32.0 %copy-start.1 = (bf16[128,32,128]{2,1,0:T(8,128)(2,1)S(1)}, bf16[128,32,128]{2,1,0:T(8,128)(2,1)}, u32[]{:S(2)}) copy-start(bf16[128,32,128]{2,1,0:T(8,128)(2,1)} %param.6) | copy-start | bytes 3145732
  0.6 33.3 %copy-start = (bf16[128,32,128]{2,1,0:T(8,128)(2,1)S(1)}, bf16[128,32,128]{2,1,0:T(8,128)(2,1)}, u32[]{:S(2)}) copy-start(bf16[128,32,128]{2,1,0:T(8,128)(2,1)} %param.10) | copy-start | bytes 3145732
  2.0 46.4 %copy-start.9 = (bf16[128,16,128]{2,0,1:T(8,128)(2,1)}, bf16[128,16,128]{2,0,1:T(8,128)(2,1)S(1)}, u32[]{:S(2)}) copy-start(bf16[128,16,128]{2,0,1:T(8,128)(2,1)S(1)} %copy.27) | copy-start | bytes 1572868
  2.0 17.2 %collective-permute-start = (bf16[1,16,128,128]{3,2,1,0:T(8,128)(2,1)S(1)}, bf16[1,16,128,128]{3,2,1,0:T(8,128)(2,1)}, u32[]{:S(2)}, u32[]{:S(2)}) collective-permute-start(bf16[1,16,128,128]{3,2,1,0:T(8,128)(2,1)S(1)} %bitcast.84), channel_id=1, source_target_pairs={{0,8},{2,10},{4,12},{6,14},{8,16},{10,18},{12,20},{14,22},{16,24},... | collective-permute-start | bytes 1572872 | tf_op jit(solution)/shard_map/ppermute | solution.py:20
  8.9 47.9 %copy-start.10 = (bf16[128,16,128]{2,0,1:T(8,128)(2,1)}, bf16[128,16,128]{2,0,1:T(8,128)(2,1)S(1)}, u32[]{:S(2)}) copy-start(bf16[128,16,128]{2,0,1:T(8,128)(2,1)S(1)} %copy.26) | copy-start | bytes 1572868
  8.9 26.5 %collective-permute-start.10 = (bf16[1,16,128,128]{3,2,1,0:T(8,128)(2,1)S(1)}, bf16[1,16,128,128]{3,2,1,0:T(8,128)(2,1)}, u32[]{:S(2)}, u32[]{:S(2)}) collective-permute-start(bf16[1,16,128,128]{3,2,1,0:T(8,128)(2,1)S(1)} %bitcast.88), channel_id=1, source_target_pairs={{0,8},{2,10},{4,12},{6,14},{8,16},{10,18},{12,20},{14,22},{16,24},... | collective-permute-start | bytes 1572872 | tf_op jit(solution)/shard_map/ppermute | solution.py:20
  12.4 25.7 %collective-permute-start.4 = (bf16[1,16,128,128]{3,2,1,0:T(8,128)(2,1)S(1)}, bf16[1,16,128,128]{3,2,1,0:T(8,128)(2,1)}, u32[]{:S(2)}, u32[]{:S(2)}) collective-permute-start(bf16[1,16,128,128]{3,2,1,0:T(8,128)(2,1)S(1)} %bitcast.85), channel_id=1, source_target_pairs={{0,4},{2,6},{8,12},{10,14},{16,20},{18,22},{24,28},{26,30},{1,5},{... | collective-permute-start | bytes 1572872 | tf_op jit(solution)/shard_map/ppermute | solution.py:29
  19.2 22.6 %collective-permute-start.1 = (bf16[1,16,128,128]{3,2,1,0:T(8,128)(2,1)}, bf16[1,16,128,128]{3,2,1,0:T(8,128)(2,1)}, u32[]{:S(2)}, u32[]{:S(2)}) collective-permute-start(bf16[1,16,128,128]{3,2,1,0:T(8,128)(2,1)} %collective-permute-done.refs_2_), channel_id=1, source_target_pairs={{0,8},{2,10},{4,12},{6,14},{8,16},{10,18},{12,20},{14,22},{16,24},... | collective-permute-start | bytes 1572872 | tf_op jit(solution)/shard_map/ppermute | solution.py:20
  24.5 21.4 %collective-permute-start.5 = (bf16[1,16,128,128]{3,2,1,0:T(8,128)(2,1)}, bf16[1,16,128,128]{3,2,1,0:T(8,128)(2,1)}, u32[]{:S(2)}, u32[]{:S(2)}) collective-permute-start(bf16[1,16,128,128]{3,2,1,0:T(8,128)(2,1)} %collective-permute-done.refs_2_), channel_id=1, source_target_pairs={{4,0},{6,2},{12,8},{14,10},{20,16},{22,18},{28,24},{30,26},{5,1},{... | collective-permute-start | bytes 1572872 | tf_op jit(solution)/shard_map/ppermute | solution.py:29
  25.8 22.6 %collective-permute-start.14 = (bf16[1,16,128,128]{3,2,1,0:T(8,128)(2,1)S(1)}, bf16[1,16,128,128]{3,2,1,0:T(8,128)(2,1)}, u32[]{:S(2)}, u32[]{:S(2)}) collective-permute-start(bf16[1,16,128,128]{3,2,1,0:T(8,128)(2,1)S(1)} %bitcast.89), channel_id=1, source_target_pairs={{0,4},{2,6},{8,12},{10,14},{16,20},{18,22},{24,28},{26,30},{1,5},{... | collective-permute-start | bytes 1572872 | tf_op jit(solution)/shard_map/ppermute | solution.py:29
  35.4 16.5 %collective-permute-start.11 = (bf16[1,16,128,128]{3,2,1,0:T(8,128)(2,1)}, bf16[1,16,128,128]{3,2,1,0:T(8,128)(2,1)S(1)}, u32[]{:S(2)}, u32[]{:S(2)}) collective-permute-start(bf16[1,16,128,128]{3,2,1,0:T(8,128)(2,1)} %collective-permute-done.10.refs_5_), channel_id=1, source_target_pairs={{0,8},{2,10},{4,12},{6,14},{8,16},{10,18},{12,20},{14,22},{16,24},... | collective-permute-start | bytes 1572872 | tf_op jit(solution)/shard_map/ppermute | solution.py:20
  38.1 17.2 %collective-permute-start.15 = (bf16[1,16,128,128]{3,2,1,0:T(8,128)(2,1)}, bf16[1,16,128,128]{3,2,1,0:T(8,128)(2,1)S(1)}, u32[]{:S(2)}, u32[]{:S(2)}) collective-permute-start(bf16[1,16,128,128]{3,2,1,0:T(8,128)(2,1)} %collective-permute-done.10.refs_5_), channel_id=1, source_target_pairs={{4,0},{6,2},{12,8},{14,10},{20,16},{22,18},{28,24},{30,26},{5,1},{... | collective-permute-start | bytes 1572872 | tf_op jit(solution)/shard_map/ppermute | solution.py:29
  41.8 14.9 %collective-permute-start.7 = (bf16[1,16,128,128]{3,2,1,0:T(8,128)(2,1)}, bf16[1,16,128,128]{3,2,1,0:T(8,128)(2,1)S(1)}, u32[]{:S(2)}, u32[]{:S(2)}) collective-permute-start(bf16[1,16,128,128]{3,2,1,0:T(8,128)(2,1)} %collective-permute-done.refs_2_), channel_id=1, source_target_pairs={{0,4},{2,6},{8,12},{10,14},{16,20},{18,22},{24,28},{26,30},{1,5},{... | collective-permute-start | bytes 1572872 | tf_op jit(solution)/shard_map/ppermute | solution.py:29
  46.0 19.2 %collective-permute-start.8 = (bf16[1,16,128,128]{3,2,1,0:T(8,128)(2,1)}, bf16[1,16,128,128]{3,2,1,0:T(8,128)(2,1)S(1)}, u32[]{:S(2)}, u32[]{:S(2)}) collective-permute-start(bf16[1,16,128,128]{3,2,1,0:T(8,128)(2,1)} %collective-permute-done.1.refs_0_), channel_id=1, source_target_pairs={{4,0},{6,2},{12,8},{14,10},{20,16},{22,18},{28,24},{30,26},{5,1},{... | collective-permute-start | bytes 1572872 | tf_op jit(solution)/shard_map/ppermute | solution.py:29
  48.4 26.4 %copy-start.11 = (bf16[1,16,128,128]{3,2,1,0:T(8,128)(2,1)}, bf16[1,16,128,128]{3,2,1,0:T(8,128)(2,1)S(1)}, u32[]{:S(2)}) copy-start(bf16[1,16,128,128]{3,2,1,0:T(8,128)(2,1)S(1)} %broadcast_select_fusion.3.refs_2_) | copy-start | bytes 1572868
  48.4 26.4 %collective-permute-start.2 = (bf16[1,16,128,128]{3,2,1,0:T(8,128)(2,1)S(1)}, bf16[1,16,128,128]{3,2,1,0:T(8,128)(2,1)S(1)}, u32[]{:S(2)}, u32[]{:S(2)}) collective-permute-start(bf16[1,16,128,128]{3,2,1,0:T(8,128)(2,1)S(1)} %bitcast.86), channel_id=1, source_target_pairs={{0,2},{4,6},{8,10},{12,14},{16,18},{20,22},{24,26},{28,30},{1,3},{... | collective-permute-start | bytes 1572872 | tf_op jit(solution)/shard_map/ppermute | solution.py:29
  51.9 22.9 %copy-start.29 = (bf16[1,16,128,128]{3,2,1,0:T(8,128)(2,1)}, bf16[1,16,128,128]{3,2,1,0:T(8,128)(2,1)S(1)}, u32[]{:S(2)}) copy-start(bf16[1,16,128,128]{3,2,1,0:T(8,128)(2,1)S(1)} %collective-permute-done.11.refs_6_) | copy-start | bytes 1572868
  51.9 14.7 %collective-permute-start.17 = (bf16[1,16,128,128]{3,2,1,0:T(8,128)(2,1)}, bf16[1,16,128,128]{3,2,1,0:T(8,128)(2,1)S(1)}, u32[]{:S(2)}, u32[]{:S(2)}) collective-permute-start(bf16[1,16,128,128]{3,2,1,0:T(8,128)(2,1)} %collective-permute-done.10.refs_5_), channel_id=1, source_target_pairs={{0,4},{2,6},{8,12},{10,14},{16,20},{18,22},{24,28},{26,30},{1,5},{... | collective-permute-start | bytes 1572872 | tf_op jit(solution)/shard_map/ppermute | solution.py:29
  55.4 17.9 %collective-permute-start.18 = (bf16[1,16,128,128]{3,2,1,0:T(8,128)(2,1)S(1)}, bf16[1,16,128,128]{3,2,1,0:T(8,128)(2,1)S(1)}, u32[]{:S(2)}, u32[]{:S(2)}) collective-permute-start(bf16[1,16,128,128]{3,2,1,0:T(8,128)(2,1)S(1)} %collective-permute-done.11.refs_6_), channel_id=1, source_target_pairs={{4,0},{6,2},{12,8},{14,10},{20,16},{22,18},{28,24},{30,26},{5,1},{... | collective-permute-start | bytes 1572872 | tf_op jit(solution)/shard_map/ppermute | solution.py:29
  56.8 19.3 %collective-permute-start.12 = (bf16[1,16,128,128]{3,2,1,0:T(8,128)(2,1)S(1)}, bf16[1,16,128,128]{3,2,1,0:T(8,128)(2,1)S(1)}, u32[]{:S(2)}, u32[]{:S(2)}) collective-permute-start(bf16[1,16,128,128]{3,2,1,0:T(8,128)(2,1)S(1)} %bitcast.90), channel_id=1, source_target_pairs={{0,2},{4,6},{8,10},{12,14},{16,18},{20,22},{24,26},{28,30},{1,3},{... | collective-permute-start | bytes 1572872 | tf_op jit(solution)/shard_map/ppermute | solution.py:29
  65.2 10.9 %collective-permute-start.3 = (bf16[1,16,128,128]{3,2,1,0:T(8,128)(2,1)}, bf16[1,16,128,128]{3,2,1,0:T(8,128)(2,1)S(1)}, u32[]{:S(2)}, u32[]{:S(2)}) collective-permute-start(bf16[1,16,128,128]{3,2,1,0:T(8,128)(2,1)} %collective-permute-done.1.refs_0_), channel_id=1, source_target_pairs={{2,0},{6,4},{10,8},{14,12},{18,16},{22,20},{26,24},{30,28},{3,1},{... | collective-permute-start | bytes 1572872 | tf_op jit(solution)/shard_map/ppermute | solution.py:29
  66.6 11.7 %collective-permute-start.6 = (bf16[1,16,128,128]{3,2,1,0:T(8,128)(2,1)S(1)}, bf16[1,16,128,128]{3,2,1,0:T(8,128)(2,1)S(1)}, u32[]{:S(2)}, u32[]{:S(2)}) collective-permute-start(bf16[1,16,128,128]{3,2,1,0:T(8,128)(2,1)S(1)} %broadcast_select_fusion.3.refs_2_), channel_id=1, source_target_pairs={{0,2},{2,0},{4,6},{6,4},{8,10},{10,8},{12,14},{14,12},{16,18},{18,... | collective-permute-start | bytes 1572872 | tf_op jit(solution)/shard_map/ppermute | solution.py:24
  73.2 4.2 %collective-permute-start.13 = (bf16[1,16,128,128]{3,2,1,0:T(8,128)(2,1)S(1)}, bf16[1,16,128,128]{3,2,1,0:T(8,128)(2,1)S(1)}, u32[]{:S(2)}, u32[]{:S(2)}) collective-permute-start(bf16[1,16,128,128]{3,2,1,0:T(8,128)(2,1)S(1)} %collective-permute-done.11.refs_6_), channel_id=1, source_target_pairs={{2,0},{6,4},{10,8},{14,12},{18,16},{22,20},{26,24},{30,28},{3,1},{... | collective-permute-start | bytes 1572872 | tf_op jit(solution)/shard_map/ppermute | solution.py:29
  74.8 3.5 %collective-permute-start.16 = (bf16[1,16,128,128]{3,2,1,0:T(8,128)(2,1)S(1)}, bf16[1,16,128,128]{3,2,1,0:T(8,128)(2,1)S(1)}, u32[]{:S(2)}, u32[]{:S(2)}) collective-permute-start(bf16[1,16,128,128]{3,2,1,0:T(8,128)(2,1)S(1)} %broadcast_select_fusion.1.refs_8_), channel_id=1, source_target_pairs={{0,2},{2,0},{4,6},{6,4},{8,10},{10,8},{12,14},{14,12},{16,18},{18,... | collective-permute-start | bytes 1572872 | tf_op jit(solution)/shard_map/ppermute | solution.py:24
  76.0 2.5 %collective-permute-start.9 = (bf16[1,16,128,128]{3,2,1,0:T(8,128)(2,1)S(1)}, bf16[1,16,128,128]{3,2,1,0:T(8,128)(2,1)S(1)}, u32[]{:S(2)}, u32[]{:S(2)}) collective-permute-start(bf16[1,16,128,128]{3,2,1,0:T(8,128)(2,1)S(1)} %broadcast_select_fusion.2.refs_4_), channel_id=1, source_target_pairs={{0,2},{2,0},{4,6},{6,4},{8,10},{10,8},{12,14},{14,12},{16,18},{18,... | collective-permute-start | bytes 1572872 | tf_op jit(solution)/shard_map/ppermute | solution.py:24
  76.1 3.2 %collective-permute-start.19 = (bf16[1,16,128,128]{3,2,1,0:T(8,128)(2,1)S(1)}, bf16[1,16,128,128]{3,2,1,0:T(8,128)(2,1)S(1)}, u32[]{:S(2)}, u32[]{:S(2)}) collective-permute-start(bf16[1,16,128,128]{3,2,1,0:T(8,128)(2,1)S(1)} %broadcast_select_fusion.refs_10_), channel_id=1, source_target_pairs={{0,2},{2,0},{4,6},{6,4},{8,10},{10,8},{12,14},{14,12},{16,18},{18,... | collective-permute-start | bytes 1572872 | tf_op jit(solution)/shard_map/ppermute | solution.py:24
  103.1 4.3 %collective-permute-start.24 = (bf16[1,8,128,128]{3,2,1,0:T(8,128)(2,1)S(1)}, bf16[1,8,128,128]{3,2,1,0:T(8,128)(2,1)S(1)}, u32[]{:S(2)}, u32[]{:S(2)}) collective-permute-start(bf16[1,8,128,128]{3,2,1,0:T(8,128)(2,1)S(1)} %get-tuple-element.101), channel_id=1, source_target_pairs={{0,2},{2,0},{4,6},{6,4},{8,10},{10,8},{12,14},{14,12},{16,18},{18,... | collective-permute-start | bytes 786440 | tf_op jit(solution)/shard_map/ppermute | solution.py:24
  103.3 4.5 %collective-permute-start.20 = (bf16[1,8,128,128]{3,2,1,0:T(8,128)(2,1)S(1)}, bf16[1,8,128,128]{3,2,1,0:T(8,128)(2,1)S(1)}, u32[]{:S(2)}, u32[]{:S(2)}) collective-permute-start(bf16[1,8,128,128]{3,2,1,0:T(8,128)(2,1)S(1)} %get-tuple-element.102), channel_id=1, source_target_pairs={{0,2},{2,0},{4,6},{6,4},{8,10},{10,8},{12,14},{14,12},{16,18},{18,... | collective-permute-start | bytes 786440 | tf_op jit(solution)/shard_map/ppermute | solution.py:24
  104.8 4.0 %collective-permute-start.25 = (bf16[1,8,128,128]{3,2,1,0:T(8,128)(2,1)S(1)}, bf16[1,8,128,128]{3,2,1,0:T(8,128)(2,1)S(1)}, u32[]{:S(2)}, u32[]{:S(2)}) collective-permute-start(bf16[1,8,128,128]{3,2,1,0:T(8,128)(2,1)S(1)} %get-tuple-element.97), channel_id=1, source_target_pairs={{0,2},{2,0},{4,6},{6,4},{8,10},{10,8},{12,14},{14,12},{16,18},{18,... | collective-permute-start | bytes 786440 | tf_op jit(solution)/shard_map/ppermute | solution.py:24
  105.0 4.2 %collective-permute-start.21 = (bf16[1,8,128,128]{3,2,1,0:T(8,128)(2,1)S(1)}, bf16[1,8,128,128]{3,2,1,0:T(8,128)(2,1)S(1)}, u32[]{:S(2)}, u32[]{:S(2)}) collective-permute-start(bf16[1,8,128,128]{3,2,1,0:T(8,128)(2,1)S(1)} %get-tuple-element.98), channel_id=1, source_target_pairs={{0,2},{2,0},{4,6},{6,4},{8,10},{10,8},{12,14},{14,12},{16,18},{18,... | collective-permute-start | bytes 786440 | tf_op jit(solution)/shard_map/ppermute | solution.py:24
  105.4 3.9 %collective-permute-start.26 = (bf16[1,8,128,128]{3,2,1,0:T(8,128)(2,1)S(1)}, bf16[1,8,128,128]{3,2,1,0:T(8,128)(2,1)S(1)}, u32[]{:S(2)}, u32[]{:S(2)}) collective-permute-start(bf16[1,8,128,128]{3,2,1,0:T(8,128)(2,1)S(1)} %get-tuple-element.93), channel_id=1, source_target_pairs={{0,2},{2,0},{4,6},{6,4},{8,10},{10,8},{12,14},{14,12},{16,18},{18,... | collective-permute-start | bytes 786440 | tf_op jit(solution)/shard_map/ppermute | solution.py:24
  107.4 5.9 %collective-permute-start.28 = (bf16[1,16,128,128]{3,2,1,0:T(8,128)(2,1)}, bf16[1,16,128,128]{3,2,1,0:T(8,128)(2,1)S(1)}, u32[]{:S(2)}, u32[]{:S(2)}) collective-permute-start(bf16[1,16,128,128]{3,2,1,0:T(8,128)(2,1)} %collective-permute-done.refs_2_), channel_id=1, source_target_pairs={{0,2},{2,0},{4,6},{6,4},{8,10},{10,8},{12,14},{14,12},{16,18},{18,... | collective-permute-start | bytes 1572872 | tf_op jit(solution)/shard_map/ppermute | solution.py:24
  107.8 3.0 %collective-permute-start.22 = (bf16[1,8,128,128]{3,2,1,0:T(8,128)(2,1)S(1)}, bf16[1,8,128,128]{3,2,1,0:T(8,128)(2,1)S(1)}, u32[]{:S(2)}, u32[]{:S(2)}) collective-permute-start(bf16[1,8,128,128]{3,2,1,0:T(8,128)(2,1)S(1)} %get-tuple-element.94), channel_id=1, source_target_pairs={{0,2},{2,0},{4,6},{6,4},{8,10},{10,8},{12,14},{14,12},{16,18},{18,... | collective-permute-start | bytes 786440 | tf_op jit(solution)/shard_map/ppermute | solution.py:24
  108.8 4.5 %collective-permute-start.29 = (bf16[1,16,128,128]{3,2,1,0:T(8,128)(2,1)}, bf16[1,16,128,128]{3,2,1,0:T(8,128)(2,1)S(1)}, u32[]{:S(2)}, u32[]{:S(2)}) collective-permute-start(bf16[1,16,128,128]{3,2,1,0:T(8,128)(2,1)} %collective-permute-done.10.refs_5_), channel_id=1, source_target_pairs={{0,2},{2,0},{4,6},{6,4},{8,10},{10,8},{12,14},{14,12},{16,18},{18,... | collective-permute-start | bytes 1572872 | tf_op jit(solution)/shard_map/ppermute | solution.py:24
  109.2 2.6 %collective-permute-start.27 = (bf16[1,8,128,128]{3,2,1,0:T(8,128)(2,1)S(1)}, bf16[1,8,128,128]{3,2,1,0:T(8,128)(2,1)S(1)}, u32[]{:S(2)}, u32[]{:S(2)}) collective-permute-start(bf16[1,8,128,128]{3,2,1,0:T(8,128)(2,1)S(1)} %get-tuple-element.89), channel_id=1, source_target_pairs={{0,2},{2,0},{4,6},{6,4},{8,10},{10,8},{12,14},{14,12},{16,18},{18,... | collective-permute-start | bytes 786440 | tf_op jit(solution)/shard_map/ppermute | solution.py:24
  109.4 2.8 %collective-permute-start.23 = (bf16[1,8,128,128]{3,2,1,0:T(8,128)(2,1)S(1)}, bf16[1,8,128,128]{3,2,1,0:T(8,128)(2,1)S(1)}, u32[]{:S(2)}, u32[]{:S(2)}) collective-permute-start(bf16[1,8,128,128]{3,2,1,0:T(8,128)(2,1)S(1)} %get-tuple-element.90), channel_id=1, source_target_pairs={{0,2},{2,0},{4,6},{6,4},{8,10},{10,8},{12,14},{14,12},{16,18},{18,... | collective-permute-start | bytes 786440 | tf_op jit(solution)/shard_map/ppermute | solution.py:24
  110.7 25.4 %collective-permute-start.30 = (bf16[1,8,128,128]{3,2,1,0:T(8,128)(2,1)}, bf16[1,8,128,128]{3,2,1,0:T(8,128)(2,1)S(1)}, u32[]{:S(2)}, u32[]{:S(2)}) collective-permute-start(bf16[1,8,128,128]{3,2,1,0:T(8,128)(2,1)} %get-tuple-element.85), channel_id=1, source_target_pairs={{0,2},{2,0},{4,6},{6,4},{8,10},{10,8},{12,14},{14,12},{16,18},{18,... | collective-permute-start | bytes 786440 | tf_op jit(solution)/shard_map/ppermute | solution.py:24
  111.8 24.4 %collective-permute-start.36 = (bf16[1,8,128,128]{3,2,1,0:T(8,128)(2,1)}, bf16[1,8,128,128]{3,2,1,0:T(8,128)(2,1)S(1)}, u32[]{:S(2)}, u32[]{:S(2)}) collective-permute-start(bf16[1,8,128,128]{3,2,1,0:T(8,128)(2,1)} %get-tuple-element.86), channel_id=1, source_target_pairs={{0,2},{2,0},{4,6},{6,4},{8,10},{10,8},{12,14},{14,12},{16,18},{18,... | collective-permute-start | bytes 786440 | tf_op jit(solution)/shard_map/ppermute | solution.py:24
  112.2 24.1 %collective-permute-start.42 = (bf16[1,8,128,128]{3,2,1,0:T(8,128)(2,1)}, bf16[1,8,128,128]{3,2,1,0:T(8,128)(2,1)S(1)}, u32[]{:S(2)}, u32[]{:S(2)}) collective-permute-start(bf16[1,8,128,128]{3,2,1,0:T(8,128)(2,1)} %get-tuple-element.75), channel_id=1, source_target_pairs={{0,2},{2,0},{4,6},{6,4},{8,10},{10,8},{12,14},{14,12},{16,18},{18,... | collective-permute-start | bytes 786440 | tf_op jit(solution)/shard_map/ppermute | solution.py:24
  129.0 9.4 %collective-permute-start.33 = (bf16[1,8,128,128]{3,2,1,0:T(8,128)(2,1)}, bf16[1,8,128,128]{3,2,1,0:T(8,128)(2,1)S(1)}, u32[]{:S(2)}, u32[]{:S(2)}) collective-permute-start(bf16[1,8,128,128]{3,2,1,0:T(8,128)(2,1)} %get-tuple-element.48), channel_id=1, source_target_pairs={{0,4},{2,6},{4,0},{6,2},{8,12},{10,14},{12,8},{14,10},{16,20},{18,... | collective-permute-start | bytes 786440 | tf_op jit(solution)/shard_map/ppermute | solution.py:24
  129.1 15.0 %collective-permute-start.39 = (bf16[1,8,128,128]{3,2,1,0:T(8,128)(2,1)}, bf16[1,8,128,128]{3,2,1,0:T(8,128)(2,1)S(1)}, u32[]{:S(2)}, u32[]{:S(2)}) collective-permute-start(bf16[1,8,128,128]{3,2,1,0:T(8,128)(2,1)} %get-tuple-element.51), channel_id=1, source_target_pairs={{0,4},{2,6},{4,0},{6,2},{8,12},{10,14},{12,8},{14,10},{16,20},{18,... | collective-permute-start | bytes 786440 | tf_op jit(solution)/shard_map/ppermute | solution.py:24
  136.0 26.2 %copy-start.21 = (bf16[1,16,128,128]{3,2,1,0:T(8,128)(2,1)S(1)}, bf16[1,16,128,128]{3,2,1,0:T(8,128)(2,1)}, u32[]{:S(2)}) copy-start(bf16[1,16,128,128]{3,2,1,0:T(8,128)(2,1)} %get-tuple-element.58) | copy-start | bytes 1572868
  136.1 8.3 %collective-permute-start.48 = (bf16[1,8,128,128]{3,2,1,0:T(8,128)(2,1)}, bf16[1,8,128,128]{3,2,1,0:T(8,128)(2,1)S(1)}, u32[]{:S(2)}, u32[]{:S(2)}) collective-permute-start(bf16[1,8,128,128]{3,2,1,0:T(8,128)(2,1)} %get-tuple-element.76), channel_id=1, source_target_pairs={{0,2},{2,0},{4,6},{6,4},{8,10},{10,8},{12,14},{14,12},{16,18},{18,... | collective-permute-start | bytes 786440 | tf_op jit(solution)/shard_map/ppermute | solution.py:24
  136.2 13.5 %collective-permute-start.31 = (bf16[1,8,128,128]{3,2,1,0:T(8,128)(2,1)}, bf16[1,8,128,128]{3,2,1,0:T(8,128)(2,1)S(1)}, u32[]{:S(2)}, u32[]{:S(2)}) collective-permute-start(bf16[1,8,128,128]{3,2,1,0:T(8,128)(2,1)} %get-tuple-element.45), channel_id=1, source_target_pairs={{0,4},{2,6},{4,0},{6,2},{8,12},{10,14},{12,8},{14,10},{16,20},{18,... | collective-permute-start | bytes 786440 | tf_op jit(solution)/shard_map/ppermute | solution.py:24
  136.4 13.4 %collective-permute-start.32 = (bf16[1,8,128,128]{3,2,1,0:T(8,128)(2,1)}, bf16[1,8,128,128]{3,2,1,0:T(8,128)(2,1)S(1)}, u32[]{:S(2)}, u32[]{:S(2)}) collective-permute-start(bf16[1,8,128,128]{3,2,1,0:T(8,128)(2,1)} %get-tuple-element.81), channel_id=1, source_target_pairs={{0,2},{2,0},{4,6},{6,4},{8,10},{10,8},{12,14},{14,12},{16,18},{18,... | collective-permute-start | bytes 786440 | tf_op jit(solution)/shard_map/ppermute | solution.py:24
  138.5 16.9 %collective-permute-start.45 = (bf16[1,8,128,128]{3,2,1,0:T(8,128)(2,1)}, bf16[1,8,128,128]{3,2,1,0:T(8,128)(2,1)S(1)}, u32[]{:S(2)}, u32[]{:S(2)}) collective-permute-start(bf16[1,8,128,128]{3,2,1,0:T(8,128)(2,1)} %get-tuple-element.57), channel_id=1, source_target_pairs={{0,4},{2,6},{4,0},{6,2},{8,12},{10,14},{12,8},{14,10},{16,20},{18,... | collective-permute-start | bytes 786440 | tf_op jit(solution)/shard_map/ppermute | solution.py:24
  144.1 16.9 %collective-permute-start.51 = (bf16[1,8,128,128]{3,2,1,0:T(8,128)(2,1)}, bf16[1,8,128,128]{3,2,1,0:T(8,128)(2,1)S(1)}, u32[]{:S(2)}, u32[]{:S(2)}) collective-permute-start(bf16[1,8,128,128]{3,2,1,0:T(8,128)(2,1)} %get-tuple-element.60), channel_id=1, source_target_pairs={{0,4},{2,6},{4,0},{6,2},{8,12},{10,14},{12,8},{14,10},{16,20},{18,... | collective-permute-start | bytes 786440 | tf_op jit(solution)/shard_map/ppermute | solution.py:24
  144.1 30.6 %copy-start.24 = (bf16[1,16,128,128]{3,2,1,0:T(8,128)(2,1)S(1)}, bf16[1,16,128,128]{3,2,1,0:T(8,128)(2,1)}, u32[]{:S(2)}) copy-start(bf16[1,16,128,128]{3,2,1,0:T(8,128)(2,1)} %get-tuple-element.46) | copy-start | bytes 1572868
  144.4 22.1 %collective-permute-start.37 = (bf16[1,8,128,128]{3,2,1,0:T(8,128)(2,1)S(1)}, bf16[1,8,128,128]{3,2,1,0:T(8,128)(2,1)S(1)}, u32[]{:S(2)}, u32[]{:S(2)}) collective-permute-start(bf16[1,8,128,128]{3,2,1,0:T(8,128)(2,1)S(1)} %copy-done.26), channel_id=1, source_target_pairs={{0,4},{2,6},{4,0},{6,2},{8,12},{10,14},{12,8},{14,10},{16,20},{18,... | collective-permute-start | bytes 786440 | tf_op jit(solution)/shard_map/ppermute | solution.py:24
  149.7 16.9 %collective-permute-start.38 = (bf16[1,8,128,128]{3,2,1,0:T(8,128)(2,1)S(1)}, bf16[1,8,128,128]{3,2,1,0:T(8,128)(2,1)S(1)}, u32[]{:S(2)}, u32[]{:S(2)}) collective-permute-start(bf16[1,8,128,128]{3,2,1,0:T(8,128)(2,1)S(1)} %copy-done.28), channel_id=1, source_target_pairs={{0,2},{2,0},{4,6},{6,4},{8,10},{10,8},{12,14},{14,12},{16,18},{18,... | collective-permute-start | bytes 786440 | tf_op jit(solution)/shard_map/ppermute | solution.py:24
  149.7 22.4 %collective-permute-start.43 = (bf16[1,8,128,128]{3,2,1,0:T(8,128)(2,1)S(1)}, bf16[1,8,128,128]{3,2,1,0:T(8,128)(2,1)S(1)}, u32[]{:S(2)}, u32[]{:S(2)}) collective-permute-start(bf16[1,8,128,128]{3,2,1,0:T(8,128)(2,1)S(1)} %copy-done.27), channel_id=1, source_target_pairs={{0,4},{2,6},{4,0},{6,2},{8,12},{10,14},{12,8},{14,10},{16,20},{18,... | collective-permute-start | bytes 786440 | tf_op jit(solution)/shard_map/ppermute | solution.py:24
  155.3 16.9 %collective-permute-start.34 = (bf16[1,8,128,128]{3,2,1,0:T(8,128)(2,1)S(1)}, bf16[1,8,128,128]{3,2,1,0:T(8,128)(2,1)S(1)}, u32[]{:S(2)}, u32[]{:S(2)}) collective-permute-start(bf16[1,8,128,128]{3,2,1,0:T(8,128)(2,1)S(1)} %get-tuple-element.83), channel_id=1, source_target_pairs={{8,0},{10,2},{12,4},{14,6},{16,8},{18,10},{20,12},{22,14},{24,16},... | collective-permute-start | bytes 786440 | tf_op jit(solution)/shard_map/ppermute | solution.py:20
  160.9 12.5 %collective-permute-start.40 = (bf16[1,8,128,128]{3,2,1,0:T(8,128)(2,1)S(1)}, bf16[1,8,128,128]{3,2,1,0:T(8,128)(2,1)S(1)}, u32[]{:S(2)}, u32[]{:S(2)}) collective-permute-start(bf16[1,8,128,128]{3,2,1,0:T(8,128)(2,1)S(1)} %get-tuple-element.84), channel_id=1, source_target_pairs={{8,0},{10,2},{12,4},{14,6},{16,8},{18,10},{20,12},{22,14},{24,16},... | collective-permute-start | bytes 786440 | tf_op jit(solution)/shard_map/ppermute | solution.py:20
  162.5 26.3 %copy-start.23 = (bf16[1,16,128,128]{3,2,1,0:T(8,128)(2,1)S(1)}, bf16[1,16,128,128]{3,2,1,0:T(8,128)(2,1)}, u32[]{:S(2)}) copy-start(bf16[1,16,128,128]{3,2,1,0:T(8,128)(2,1)} %get-tuple-element.55) | copy-start | bytes 1572868
  166.5 8.7 %collective-permute-start.44 = (bf16[1,8,128,128]{3,2,1,0:T(8,128)(2,1)S(1)}, bf16[1,8,128,128]{3,2,1,0:T(8,128)(2,1)S(1)}, u32[]{:S(2)}, u32[]{:S(2)}) collective-permute-start(bf16[1,8,128,128]{3,2,1,0:T(8,128)(2,1)S(1)} %get-tuple-element.71), channel_id=1, source_target_pairs={{0,2},{2,0},{4,6},{6,4},{8,10},{10,8},{12,14},{14,12},{16,18},{18,... | collective-permute-start | bytes 786440 | tf_op jit(solution)/shard_map/ppermute | solution.py:24
  166.6 10.7 %collective-permute-start.49 = (bf16[1,8,128,128]{3,2,1,0:T(8,128)(2,1)S(1)}, bf16[1,8,128,128]{3,2,1,0:T(8,128)(2,1)S(1)}, u32[]{:S(2)}, u32[]{:S(2)}) collective-permute-start(bf16[1,8,128,128]{3,2,1,0:T(8,128)(2,1)S(1)} %copy-done.25), channel_id=1, source_target_pairs={{0,4},{2,6},{4,0},{6,2},{8,12},{10,14},{12,8},{14,10},{16,20},{18,... | collective-permute-start | bytes 786440 | tf_op jit(solution)/shard_map/ppermute | solution.py:24
  172.2 6.4 %collective-permute-start.50 = (bf16[1,8,128,128]{3,2,1,0:T(8,128)(2,1)S(1)}, bf16[1,8,128,128]{3,2,1,0:T(8,128)(2,1)S(1)}, u32[]{:S(2)}, u32[]{:S(2)}) collective-permute-start(bf16[1,8,128,128]{3,2,1,0:T(8,128)(2,1)S(1)} %get-tuple-element.72), channel_id=1, source_target_pairs={{0,2},{2,0},{4,6},{6,4},{8,10},{10,8},{12,14},{14,12},{16,18},{18,... | collective-permute-start | bytes 786440 | tf_op jit(solution)/shard_map/ppermute | solution.py:24
  172.2 11.0 %collective-permute-start.46 = (bf16[1,8,128,128]{3,2,1,0:T(8,128)(2,1)S(1)}, bf16[1,8,128,128]{3,2,1,0:T(8,128)(2,1)S(1)}, u32[]{:S(2)}, u32[]{:S(2)}) collective-permute-start(bf16[1,8,128,128]{3,2,1,0:T(8,128)(2,1)S(1)} %get-tuple-element.73), channel_id=1, source_target_pairs={{8,0},{10,2},{12,4},{14,6},{16,8},{18,10},{20,12},{22,14},{24,16},... | collective-permute-start | bytes 786440 | tf_op jit(solution)/shard_map/ppermute | solution.py:20
  173.5 15.3 %collective-permute-start.52 = (bf16[1,8,128,128]{3,2,1,0:T(8,128)(2,1)S(1)}, bf16[1,8,128,128]{3,2,1,0:T(8,128)(2,1)S(1)}, u32[]{:S(2)}, u32[]{:S(2)}) collective-permute-start(bf16[1,8,128,128]{3,2,1,0:T(8,128)(2,1)S(1)} %get-tuple-element.74), channel_id=1, source_target_pairs={{8,0},{10,2},{12,4},{14,6},{16,8},{18,10},{20,12},{22,14},{24,16},... | collective-permute-start | bytes 786440 | tf_op jit(solution)/shard_map/ppermute | solution.py:20
  175.2 24.8 %copy-start.4 = (bf16[1,16,128,128]{3,2,1,0:T(8,128)(2,1)S(1)}, bf16[1,16,128,128]{3,2,1,0:T(8,128)(2,1)}, u32[]{:S(2)}) copy-start(bf16[1,16,128,128]{3,2,1,0:T(8,128)(2,1)} %get-tuple-element.43) | copy-start | bytes 1572868
  175.2 19.2 %collective-permute-start.35 = (bf16[128,8,128]{2,0,1:T(8,128)(2,1)S(1)}, bf16[128,8,128]{2,0,1:T(8,128)(2,1)S(1)}, u32[]{:S(2)}, u32[]{:S(2)}) collective-permute-start(bf16[128,8,128]{2,0,1:T(8,128)(2,1)S(1)} %get-tuple-element.79), channel_id=1, source_target_pairs={{8,0},{10,2},{12,4},{14,6},{16,8},{18,10},{20,12},{22,14},{24,16},... | collective-permute-start | bytes 786440 | tf_op jit(solution)/shard_map/ppermute | solution.py:20
  177.2 22.8 %collective-permute-start.41 = (bf16[128,8,128]{2,0,1:T(8,128)(2,1)S(1)}, bf16[128,8,128]{2,0,1:T(8,128)(2,1)S(1)}, u32[]{:S(2)}, u32[]{:S(2)}) collective-permute-start(bf16[128,8,128]{2,0,1:T(8,128)(2,1)S(1)} %get-tuple-element.80), channel_id=1, source_target_pairs={{8,0},{10,2},{12,4},{14,6},{16,8},{18,10},{20,12},{22,14},{24,16},... | collective-permute-start | bytes 786440 | tf_op jit(solution)/shard_map/ppermute | solution.py:20
  189.3 16.4 %collective-permute-start.47 = (bf16[128,8,128]{2,0,1:T(8,128)(2,1)S(1)}, bf16[128,8,128]{2,0,1:T(8,128)(2,1)S(1)}, u32[]{:S(2)}, u32[]{:S(2)}) collective-permute-start(bf16[128,8,128]{2,0,1:T(8,128)(2,1)S(1)} %get-tuple-element.69), channel_id=1, source_target_pairs={{8,0},{10,2},{12,4},{14,6},{16,8},{18,10},{20,12},{22,14},{24,16},... | collective-permute-start | bytes 786440 | tf_op jit(solution)/shard_map/ppermute | solution.py:20
  190.6 20.3 %collective-permute-start.53 = (bf16[128,8,128]{2,0,1:T(8,128)(2,1)S(1)}, bf16[128,8,128]{2,0,1:T(8,128)(2,1)S(1)}, u32[]{:S(2)}, u32[]{:S(2)}) collective-permute-start(bf16[128,8,128]{2,0,1:T(8,128)(2,1)S(1)} %get-tuple-element.70), channel_id=1, source_target_pairs={{8,0},{10,2},{12,4},{14,6},{16,8},{18,10},{20,12},{22,14},{24,16},... | collective-permute-start | bytes 786440 | tf_op jit(solution)/shard_map/ppermute | solution.py:20
  (26 other events, 166.3 us)

commit v18 on v14

--- a/solution.py
+++ b/solution.py
@@ -191,8 +191,10 @@
             terms[j] = out[m]
             terms[9 + j] = out[len(sel) + m]
         if ys is None:
-            ys = gather_y(terms[:9], n) + gather_y(terms[9:], n)
-            ys, qb = lax.optimization_barrier((ys, q4))
+            ys = list(gather_y(terms[:9], n) + gather_y(terms[9:], n))
+            (ys[1], ys[3]), qb = lax.optimization_barrier(((ys[1], ys[3]), q4))
+    ys = list(ys)
+    (ys[0], ys[2]), acc = lax.optimization_barrier(((ys[0], ys[2]), acc))
     grad_k = unroute(terms[:9], ys[0], ys[1], n, half, core)
     grad_v = unroute(terms[9:], ys[2], ys[3], n, half, core)
 

time: 187 us -> 185 us (0.989)
  waiting for transfers between devices: 53.1 us -> 50.6 us
    ppermute x18, waiting for transfers between devices: 21.9 us -> 19.3 us  [swap(): return lax.ppermute(x, 'seq', [(i, i ^ bit) for i in range(n)])]
    unnamed x56 -> x58, local copies, waits for them, and re-layouts: 6.47 us -> 7.28 us
  transfers between devices with their start and end apart: 38 -> 38, of which waited for: 14 -> 15; matrix products, arithmetic and copies ran while one was open for 17% -> 17% of each run, Pallas kernels for 7% -> 7%
where the time goes in v18:
time: 185 us; the launch traced here: 184 us
  starting transfers between devices  60.4 us (33%)
  waiting for transfers between devices  50.6 us (27%)
  Pallas kernels  34.6 us (19%)
  other arithmetic  22.5 us (12%)
  local copies, waits for them, and re-layouts  14.9 us (8%)
    pallas_call x2, Pallas kernels, attend_blocks(): pl.pallas_call(functools.partial(_blocks_kernel, tuple(modes), acc is not...  34.6 us
    ppermute x12, starting transfers between devices, one_way(): return lax.ppermute(x, 'seq', pairs)  28.9 us
    ppermute x8, starting transfers between devices, shift(): return lax.ppermute(x, 'seq', pairs)  23.6 us
    ppermute x8, waiting for transfers between devices, shift(): return lax.ppermute(x, 'seq', pairs)  19.4 us
    ppermute x18, waiting for transfers between devices, swap(): return lax.ppermute(x, 'seq', [(i, i ^ bit) for i in range(n)])  19.3 us
    ppermute x12, waiting for transfers between devices, one_way(): return lax.ppermute(x, 'seq', pairs)  12 us
    ppermute x18, starting transfers between devices, swap(): return lax.ppermute(x, 'seq', [(i, i ^ bit) for i in range(n)])  7.85 us
    unnamed x58, local copies, waits for them, and re-layouts  7.28 us
  transfers between devices with their start and end apart: 38, of which 15 were waited for; matrix products, arithmetic and copies ran while one was open for 17% of the time, Pallas kernels for 7%

profile of v18, /device:TPU:0, one launch (start us, length us, event | category | flops | bytes accessed | tf_op | source)
XLA Modules:
  0.0 184.2 jit_solution(9572729277171966437)
XLA Ops:
  0.7 1.3 copy.26
  2.0 5.8 %collective-permute-start.10 = (bf16[1,16,128,128]{3,2,1,0:T(8,128)(2,1)S(1)}, bf16[1,16,128,128]{3,2,1,0:T(8,128)(2,1)}, u32[]{:S(2)}, u32[]{:S(2)}) collective-permute-start(bf16[1,16,128,128]{3,2,1,0:T(8,128)(2,1)S(1)} %bitcast.60), channel_id=1, source_target_pairs={{0,8},{2,10},{4,12},{6,14},{8,16},{10,18},{12,20},{14,22},{16,24},... | collective-permute-start | bytes 1572872 | tf_op jit(solution)/shard_map/ppermute | solution.py:20
  7.7 1.2 copy.27
  8.9 3.5 %collective-permute-start = (bf16[1,16,128,128]{3,2,1,0:T(8,128)(2,1)S(1)}, bf16[1,16,128,128]{3,2,1,0:T(8,128)(2,1)}, u32[]{:S(2)}, u32[]{:S(2)}) collective-permute-start(bf16[1,16,128,128]{3,2,1,0:T(8,128)(2,1)S(1)} %bitcast.64), channel_id=1, source_target_pairs={{0,8},{2,10},{4,12},{6,14},{8,16},{10,18},{12,20},{14,22},{16,24},... | collective-permute-start | bytes 1572872 | tf_op jit(solution)/shard_map/ppermute | solution.py:20
  12.4 3.4 %collective-permute-start.14 = (bf16[1,16,128,128]{3,2,1,0:T(8,128)(2,1)S(1)}, bf16[1,16,128,128]{3,2,1,0:T(8,128)(2,1)S(1)}, u32[]{:S(2)}, u32[]{:S(2)}) collective-permute-start(bf16[1,16,128,128]{3,2,1,0:T(8,128)(2,1)S(1)} %bitcast.61), channel_id=1, source_target_pairs={{0,4},{2,6},{8,12},{10,14},{16,20},{18,22},{24,28},{26,30},{1,5},{... | collective-permute-start | bytes 1572872 | tf_op jit(solution)/shard_map/ppermute | solution.py:29
  15.9 3.4 %collective-permute-done.10.refs_5_ = bf16[1,16,128,128]{3,2,1,0:T(8,128)(2,1)} collective-permute-done((bf16[1,16,128,128]{3,2,1,0:T(8,128)(2,1)S(1)}, bf16[1,16,128,128]{3,2,1,0:T(8,128)(2,1)}, u32[]{:S(2)}, u32[]{:S(2)}) %collective-permute-start.10) | collective-permute-done | bytes 524320 | tf_op jit(solution)/shard_map/ppermute | solution.py:20
  19.2 5.3 %collective-permute-start.11 = (bf16[1,16,128,128]{3,2,1,0:T(8,128)(2,1)}, bf16[1,16,128,128]{3,2,1,0:T(8,128)(2,1)}, u32[]{:S(2)}, u32[]{:S(2)}) collective-permute-start(bf16[1,16,128,128]{3,2,1,0:T(8,128)(2,1)} %collective-permute-done.10.refs_5_), channel_id=1, source_target_pairs={{0,8},{2,10},{4,12},{6,14},{8,16},{10,18},{12,20},{14,22},{16,24},... | collective-permute-start | bytes 1572872 | tf_op jit(solution)/shard_map/ppermute | solution.py:20
  24.5 1.3 collective-permute-start.15
  25.8 6.1 %collective-permute-start.4 = (bf16[1,16,128,128]{3,2,1,0:T(8,128)(2,1)S(1)}, bf16[1,16,128,128]{3,2,1,0:T(8,128)(2,1)}, u32[]{:S(2)}, u32[]{:S(2)}) collective-permute-start(bf16[1,16,128,128]{3,2,1,0:T(8,128)(2,1)S(1)} %bitcast.65), channel_id=1, source_target_pairs={{0,4},{2,6},{8,12},{10,14},{16,20},{18,22},{24,28},{26,30},{1,5},{... | collective-permute-start | bytes 1572872 | tf_op jit(solution)/shard_map/ppermute | solution.py:29
  32.0 3.8 %collective-permute-start.1 = (bf16[1,16,128,128]{3,2,1,0:T(8,128)(2,1)}, bf16[1,16,128,128]{3,2,1,0:T(8,128)(2,1)}, u32[]{:S(2)}, u32[]{:S(2)}) collective-permute-start(bf16[1,16,128,128]{3,2,1,0:T(8,128)(2,1)} %collective-permute-done.refs_2_), channel_id=1, source_target_pairs={{0,8},{2,10},{4,12},{6,14},{8,16},{10,18},{12,20},{14,22},{16,24},... | collective-permute-start | bytes 1572872 | tf_op jit(solution)/shard_map/ppermute | solution.py:20
  35.8 0.8 copy-done.13
  36.6 1.3 collective-permute-start.5
  38.6 1.4 copy.16
  40.0 1.4 copy.17
  41.4 0.6 multiply_reduce_fusion
  42.0 0.7 copy.18
  42.7 5.3 %collective-permute-start.17 = (bf16[1,16,128,128]{3,2,1,0:T(8,128)(2,1)}, bf16[1,16,128,128]{3,2,1,0:T(8,128)(2,1)S(1)}, u32[]{:S(2)}, u32[]{:S(2)}) collective-permute-start(bf16[1,16,128,128]{3,2,1,0:T(8,128)(2,1)} %collective-permute-done.10.refs_5_), channel_id=1, source_target_pairs={{0,4},{2,6},{8,12},{10,14},{16,20},{18,22},{24,28},{26,30},{1,5},{... | collective-permute-start | bytes 1572872 | tf_op jit(solution)/shard_map/ppermute | solution.py:29
  48.1 1.3 collective-permute-start.18
  49.4 1.1 broadcast_select_fusion.1.refs_8_
  50.5 1.3 collective-permute-start.12
  51.9 3.5 %collective-permute-start.7 = (bf16[1,16,128,128]{3,2,1,0:T(8,128)(2,1)}, bf16[1,16,128,128]{3,2,1,0:T(8,128)(2,1)S(1)}, u32[]{:S(2)}, u32[]{:S(2)}) collective-permute-start(bf16[1,16,128,128]{3,2,1,0:T(8,128)(2,1)} %collective-permute-done.refs_2_), channel_id=1, source_target_pairs={{0,4},{2,6},{8,12},{10,14},{16,20},{18,22},{24,28},{26,30},{1,5},{... | collective-permute-start | bytes 1572872 | tf_op jit(solution)/shard_map/ppermute | solution.py:29
  55.4 1.3 collective-permute-start.8
  56.7 1.1 broadcast_select_fusion.3.refs_2_
  57.9 1.2 collective-permute-done.17
  59.1 1.3 collective-permute-start.2
  60.4 3.3 %collective-permute-done.18 = bf16[1,16,128,128]{3,2,1,0:T(8,128)(2,1)S(1)} collective-permute-done((bf16[1,16,128,128]{3,2,1,0:T(8,128)(2,1)}, bf16[1,16,128,128]{3,2,1,0:T(8,128)(2,1)S(1)}, u32[]{:S(2)}, u32[]{:S(2)}) %collective-permute-start.18) | collective-permute-done | bytes 524320 | tf_op jit(solution)/shard_map/ppermute | solution.py:29
  63.7 1.3 collective-permute-start.13
  65.1 3.1 %collective-permute-done.7 = bf16[1,16,128,128]{3,2,1,0:T(8,128)(2,1)S(1)} collective-permute-done((bf16[1,16,128,128]{3,2,1,0:T(8,128)(2,1)}, bf16[1,16,128,128]{3,2,1,0:T(8,128)(2,1)S(1)}, u32[]{:S(2)}, u32[]{:S(2)}) %collective-permute-start.7) | collective-permute-done | bytes 524320 | tf_op jit(solution)/shard_map/ppermute | solution.py:29
  68.2 4.3 %collective-permute-done.8 = bf16[1,16,128,128]{3,2,1,0:T(8,128)(2,1)S(1)} collective-permute-done((bf16[1,16,128,128]{3,2,1,0:T(8,128)(2,1)}, bf16[1,16,128,128]{3,2,1,0:T(8,128)(2,1)S(1)}, u32[]{:S(2)}, u32[]{:S(2)}) %collective-permute-start.8) | collective-permute-done | bytes 524320 | tf_op jit(solution)/shard_map/ppermute | solution.py:29
  72.5 1.5 collective-permute-start.3
  74.1 1.2 collective-permute-start.6
  75.8 0.9 broadcast_select_fusion.4.refs_7_
  76.7 0.9 broadcast_select_fusion.5.refs_1_
  77.8 0.7 collective-permute-done.9.refs_5_
  78.5 0.8 copy-done.26
  79.4 21.7 %shard_map.85 = (f32[16,128,256]{2,1,0:T(8,128)}, bf16[1,16,128,128]{3,2,1,0:T(8,128)(2,1)}, bf16[1,16,128,128]{3,2,1,0:T(8,128)(2,1)}, bf16[1,16,128,128]{3,2,1...) custom-call(s32[6]{0:T(128)} %stack.53.valid_ref, ...), custom_call_target="tpu_custom_call" | custom-call | flops 4026531840 | bytes 14680064 | tf_op jit(solution)/shard_map/pallas_call | solution.py:105
  101.7 0.7 add_convert_fusion.4.valid_ref
  103.5 1.2 add_convert_fusion
  105.1 2.0 %add_convert_fusion.1 = bf16[1,16,128,128]{3,2,1,0:T(8,128)(2,1)} fusion(bf16[1,16,128,128]{3,2,1,0:T(8,128)(2,1)S(1)} %collective-permute-done.22, bf16[1,16,128,128]{3,2,1,0:T(8,128)(2,1)} %get-tuple-element.33), kind=kLoop, calls=%fused_computation.35 | loop fusion | flops 1048576 | bytes 1572864 | tf_op jit(solution)/shard_map/convert_element_type | solution.py:138
  107.2 0.9 add_convert_fusion.2
  108.3 1.9 %collective-permute-start.29 = (bf16[1,16,128,128]{3,2,1,0:T(8,128)(2,1)}, bf16[1,16,128,128]{3,2,1,0:T(8,128)(2,1)S(1)}, u32[]{:S(2)}, u32[]{:S(2)}) collective-permute-start(bf16[1,16,128,128]{3,2,1,0:T(8,128)(2,1)} %add_convert_fusion.1), channel_id=1, source_target_pairs={{0,4},{2,6},{4,0},{6,2},{8,12},{10,14},{12,8},{14,10},{16,20},{18,... | collective-permute-start | bytes 1572872 | tf_op jit(solution)/shard_map/ppermute | solution.py:24
  110.2 0.9 add_convert_fusion.3
  111.1 0.8 copy-done.22
  111.9 12.9 %shard_map.86 = (f32[16,128,256]{2,1,0:T(8,128)}, bf16[1,16,128,128]{3,2,1,0:T(8,128)(2,1)}, bf16[1,16,128,128]{3,2,1,0:T(8,128)(2,1)}, bf16[1,16,128,128]{3,2,1...) custom-call(s32[3]{0:T(128)} %add_convert_fusion.4.valid_ref, ...), custom_call_target="tpu_custom_call" | custom-call | flops 2013265920 | bytes 10485760 | tf_op jit(solution)/shard_map/pallas_call | solution.py:105
  125.2 2.1 %fusion.18 = bf16[1,16,128,128]{3,2,1,0:T(8,128)(2,1)} fusion(bf16[1,16,128,128]{3,2,1,0:T(8,128)(2,1)S(1)} %collective-permute-done.32, bf16[1,16,128,128]{3,2,1,0:T(8,128)(2,1)S(1)} %collective-permute-done.35, bf16[1,16,128,128]{3,2,1,0:T(8,128)(2,1)} %get-tuple-element.54, pred[]{:T(512)S(6)} %eq.26, pred[]{:T(512)S(6)} %eq.11), kind=kLoop, calls=%fused_computation.30 | loop fusion | flops 2097152 | bytes 2097154 | tf_op jit(solution)/shard_map/convert_element_type | solution.py:154
  127.3 1.3 collective-permute-start.36
  128.6 1.8 %collective-permute-start.27 = (bf16[1,16,128,128]{3,2,1,0:T(8,128)(2,1)}, bf16[1,16,128,128]{3,2,1,0:T(8,128)(2,1)S(1)}, u32[]{:S(2)}, u32[]{:S(2)}) collective-permute-start(bf16[1,16,128,128]{3,2,1,0:T(8,128)(2,1)} %add_convert_fusion.3), channel_id=1, source_target_pairs={{0,4},{2,6},{4,0},{6,2},{8,12},{10,14},{12,8},{14,10},{16,20},{18,... | collective-permute-start | bytes 1572872 | tf_op jit(solution)/shard_map/ppermute | solution.py:24
  130.4 2.7 %collective-permute-done.29 = bf16[1,16,128,128]{3,2,1,0:T(8,128)(2,1)S(1)} collective-permute-done((bf16[1,16,128,128]{3,2,1,0:T(8,128)(2,1)}, bf16[1,16,128,128]{3,2,1,0:T(8,128)(2,1)S(1)}, u32[]{:S(2)}, u32[]{:S(2)}) %collective-permute-start.29) | collective-permute-done | bytes 524320 | tf_op jit(solution)/shard_map/ppermute | solution.py:24
  133.2 1.1 fusion.7
  134.2 10.2 %collective-permute-done.33 = bf16[1,16,128,128]{3,2,1,0:T(8,128)(2,1)S(1)} collective-permute-done((bf16[1,16,128,128]{3,2,1,0:T(8,128)(2,1)}, bf16[1,16,128,128]{3,2,1,0:T(8,128)(2,1)S(1)}, u32[]{:S(2)}, u32[]{:S(2)}) %collective-permute-start.33) | collective-permute-done | bytes 524320 | tf_op jit(solution)/shard_map/ppermute | solution.py:24
  144.4 1.3 collective-permute-start.30
  145.7 2.6 %fusion.22 = bf16[128,16,128]{2,0,1:T(8,128)(2,1)} fusion(bf16[1,16,128,128]{3,2,1,0:T(8,128)(2,1)} %collective-permute-done.36, bf16[1,16,128,128]{3,2,1,0:T(8,128)(2,1)S(1)} %collective-permute-done.33, bf16[1,16,128,128]{3,2,1,0:T(8,128)(2,1)S(1)} %collective-permute-done.35, bf16[1,16,128,128]{3,2,1,0:T(8,128)(2,1)} %collective-permute-done.34, ...), kind=kLoop, calls=%fused_computation.38 | loop fusion | flops 2621440 | bytes 3145729 | tf_op jit(solution)/shard_map/transpose | solution.py:156
  148.4 1.4 collective-permute-start.37
  149.8 5.1 %collective-permute-done.27 = bf16[1,16,128,128]{3,2,1,0:T(8,128)(2,1)S(1)} collective-permute-done((bf16[1,16,128,128]{3,2,1,0:T(8,128)(2,1)}, bf16[1,16,128,128]{3,2,1,0:T(8,128)(2,1)S(1)}, u32[]{:S(2)}, u32[]{:S(2)}) %collective-permute-start.27) | collective-permute-done | bytes 524320 | tf_op jit(solution)/shard_map/ppermute | solution.py:24
  154.9 6.6 %collective-permute-done.30 = bf16[1,16,128,128]{3,2,1,0:T(8,128)(2,1)} collective-permute-done((bf16[1,16,128,128]{3,2,1,0:T(8,128)(2,1)}, bf16[1,16,128,128]{3,2,1,0:T(8,128)(2,1)}, u32[]{:S(2)}, u32[]{:S(2)}) %collective-permute-start.30) | collective-permute-done | bytes 524320 | tf_op jit(solution)/shard_map/ppermute | solution.py:20
  161.5 2.4 %fusion.23 = bf16[128,16,128]{2,0,1:T(8,128)(2,1)} fusion(bf16[1,16,128,128]{3,2,1,0:T(8,128)(2,1)} %collective-permute-done.30, bf16[1,16,128,128]{3,2,1,0:T(8,128)(2,1)S(1)} %collective-permute-done.27, bf16[1,16,128,128]{3,2,1,0:T(8,128)(2,1)S(1)} %collective-permute-done.29, bf16[1,16,128,128]{3,2,1,0:T(8,128)(2,1)} %collective-permute-done.28, ...), kind=kLoop, calls=%fused_computation.39 | loop fusion | flops 2621440 | bytes 3145729 | tf_op jit(solution)/shard_map/transpose | solution.py:156
  163.9 1.3 collective-permute-start.31
  165.7 3.8 %copy.21 = bf16[128,16,2,128]{3,2,1,0:T(2,128)(2,1)} copy(bf16[128,16,2,128]{0,2,3,1:T(2,128)(2,1)S(1)} %bitcast.53) | data formatting | bytes 2097152 | tf_op jit(solution)/shard_map/transpose | solution.py:202
  169.5 3.2 %collective-permute-done.37 = bf16[128,16,128]{2,0,1:T(8,128)(2,1)} collective-permute-done((bf16[128,16,128]{2,0,1:T(8,128)(2,1)}, bf16[128,16,128]{2,0,1:T(8,128)(2,1)}, u32[]{:S(2)}, u32[]{:S(2)}) %collective-permute-start.37) | collective-permute-done | bytes 524320 | tf_op jit(solution)/shard_map/ppermute | solution.py:20
  172.7 1.6 fusion.15
  174.2 1.1 copy.23
  175.4 6.2 %collective-permute-done.31 = bf16[128,16,128]{2,0,1:T(8,128)(2,1)} collective-permute-done((bf16[128,16,128]{2,0,1:T(8,128)(2,1)}, bf16[128,16,128]{2,0,1:T(8,128)(2,1)}, u32[]{:S(2)}, u32[]{:S(2)}) %collective-permute-start.31) | collective-permute-done | bytes 524320 | tf_op jit(solution)/shard_map/ppermute | solution.py:20
  181.6 1.4 fusion.4
  183.0 1.1 copy.22
  (98 shorter events, 4.9 us)
Async XLA Ops:
  0.6 38.0 %copy-start.6 = (bf16[128,32,128]{2,1,0:T(8,128)(2,1)S(1)}, bf16[128,32,128]{2,1,0:T(8,128)(2,1)}, u32[]{:S(2)}) copy-start(bf16[128,32,128]{2,1,0:T(8,128)(2,1)} %param.6) | copy-start | bytes 3145732
  0.6 39.3 %copy-start = (bf16[128,32,128]{2,1,0:T(8,128)(2,1)S(1)}, bf16[128,32,128]{2,1,0:T(8,128)(2,1)}, u32[]{:S(2)}) copy-start(bf16[128,32,128]{2,1,0:T(8,128)(2,1)} %param.10) | copy-start | bytes 3145732
  2.0 48.5 %copy-start.11 = (bf16[128,16,128]{2,0,1:T(8,128)(2,1)}, bf16[128,16,128]{2,0,1:T(8,128)(2,1)S(1)}, u32[]{:S(2)}) copy-start(bf16[128,16,128]{2,0,1:T(8,128)(2,1)S(1)} %copy.26) | copy-start | bytes 1572868
  2.0 17.2 %collective-permute-start.10 = (bf16[1,16,128,128]{3,2,1,0:T(8,128)(2,1)S(1)}, bf16[1,16,128,128]{3,2,1,0:T(8,128)(2,1)}, u32[]{:S(2)}, u32[]{:S(2)}) collective-permute-start(bf16[1,16,128,128]{3,2,1,0:T(8,128)(2,1)S(1)} %bitcast.60), channel_id=1, source_target_pairs={{0,8},{2,10},{4,12},{6,14},{8,16},{10,18},{12,20},{14,22},{16,24},... | collective-permute-start | bytes 1572872 | tf_op jit(solution)/shard_map/ppermute | solution.py:20
  8.9 50.2 %copy-start.12 = (bf16[128,16,128]{2,0,1:T(8,128)(2,1)}, bf16[128,16,128]{2,0,1:T(8,128)(2,1)S(1)}, u32[]{:S(2)}) copy-start(bf16[128,16,128]{2,0,1:T(8,128)(2,1)S(1)} %copy.27) | copy-start | bytes 1572868
  8.9 23.0 %collective-permute-start = (bf16[1,16,128,128]{3,2,1,0:T(8,128)(2,1)S(1)}, bf16[1,16,128,128]{3,2,1,0:T(8,128)(2,1)}, u32[]{:S(2)}, u32[]{:S(2)}) collective-permute-start(bf16[1,16,128,128]{3,2,1,0:T(8,128)(2,1)S(1)} %bitcast.64), channel_id=1, source_target_pairs={{0,8},{2,10},{4,12},{6,14},{8,16},{10,18},{12,20},{14,22},{16,24},... | collective-permute-start | bytes 1572872 | tf_op jit(solution)/shard_map/ppermute | solution.py:20
  12.4 23.4 %collective-permute-start.14 = (bf16[1,16,128,128]{3,2,1,0:T(8,128)(2,1)S(1)}, bf16[1,16,128,128]{3,2,1,0:T(8,128)(2,1)S(1)}, u32[]{:S(2)}, u32[]{:S(2)}) collective-permute-start(bf16[1,16,128,128]{3,2,1,0:T(8,128)(2,1)S(1)} %bitcast.61), channel_id=1, source_target_pairs={{0,4},{2,6},{8,12},{10,14},{16,20},{18,22},{24,28},{26,30},{1,5},{... | collective-permute-start | bytes 1572872 | tf_op jit(solution)/shard_map/ppermute | solution.py:29
  19.2 23.5 %collective-permute-start.11 = (bf16[1,16,128,128]{3,2,1,0:T(8,128)(2,1)}, bf16[1,16,128,128]{3,2,1,0:T(8,128)(2,1)}, u32[]{:S(2)}, u32[]{:S(2)}) collective-permute-start(bf16[1,16,128,128]{3,2,1,0:T(8,128)(2,1)} %collective-permute-done.10.refs_5_), channel_id=1, source_target_pairs={{0,8},{2,10},{4,12},{6,14},{8,16},{10,18},{12,20},{14,22},{16,24},... | collective-permute-start | bytes 1572872 | tf_op jit(solution)/shard_map/ppermute | solution.py:20
  24.5 23.5 %collective-permute-start.15 = (bf16[1,16,128,128]{3,2,1,0:T(8,128)(2,1)}, bf16[1,16,128,128]{3,2,1,0:T(8,128)(2,1)}, u32[]{:S(2)}, u32[]{:S(2)}) collective-permute-start(bf16[1,16,128,128]{3,2,1,0:T(8,128)(2,1)} %collective-permute-done.10.refs_5_), channel_id=1, source_target_pairs={{4,0},{6,2},{12,8},{14,10},{20,16},{22,18},{28,24},{30,26},{5,1},{... | collective-permute-start | bytes 1572872 | tf_op jit(solution)/shard_map/ppermute | solution.py:29
  25.8 24.7 %collective-permute-start.4 = (bf16[1,16,128,128]{3,2,1,0:T(8,128)(2,1)S(1)}, bf16[1,16,128,128]{3,2,1,0:T(8,128)(2,1)}, u32[]{:S(2)}, u32[]{:S(2)}) collective-permute-start(bf16[1,16,128,128]{3,2,1,0:T(8,128)(2,1)S(1)} %bitcast.65), channel_id=1, source_target_pairs={{0,4},{2,6},{8,12},{10,14},{16,20},{18,22},{24,28},{26,30},{1,5},{... | collective-permute-start | bytes 1572872 | tf_op jit(solution)/shard_map/ppermute | solution.py:29
  32.0 19.9 %collective-permute-start.1 = (bf16[1,16,128,128]{3,2,1,0:T(8,128)(2,1)}, bf16[1,16,128,128]{3,2,1,0:T(8,128)(2,1)}, u32[]{:S(2)}, u32[]{:S(2)}) collective-permute-start(bf16[1,16,128,128]{3,2,1,0:T(8,128)(2,1)} %collective-permute-done.refs_2_), channel_id=1, source_target_pairs={{0,8},{2,10},{4,12},{6,14},{8,16},{10,18},{12,20},{14,22},{16,24},... | collective-permute-start | bytes 1572872 | tf_op jit(solution)/shard_map/ppermute | solution.py:20
  36.6 18.9 %collective-permute-start.5 = (bf16[1,16,128,128]{3,2,1,0:T(8,128)(2,1)}, bf16[1,16,128,128]{3,2,1,0:T(8,128)(2,1)}, u32[]{:S(2)}, u32[]{:S(2)}) collective-permute-start(bf16[1,16,128,128]{3,2,1,0:T(8,128)(2,1)} %collective-permute-done.refs_2_), channel_id=1, source_target_pairs={{4,0},{6,2},{12,8},{14,10},{20,16},{22,18},{28,24},{30,26},{5,1},{... | collective-permute-start | bytes 1572872 | tf_op jit(solution)/shard_map/ppermute | solution.py:29
  38.6 2.8 %copy-start.7 = (bf16[128,32,128]{2,1,0:T(8,128)(2,1)S(1)}, bf16[128,32,128]{2,1,0:T(8,128)(2,1)}, u32[]{:S(2)}) copy-start(bf16[128,32,128]{2,1,0:T(8,128)(2,1)} %param.9) | copy-start | bytes 3145732
  40.0 9.4 %copy-start.14 = (bf16[1,16,128,128]{3,2,1,0:T(8,128)(2,1)S(1)}, bf16[1,16,128,128]{3,2,1,0:T(8,128)(2,1)}, u32[]{:S(2)}) copy-start(bf16[1,16,128,128]{3,2,1,0:T(8,128)(2,1)} %copy-done.13) | copy-start | bytes 1572868
  42.7 16.4 %collective-permute-start.17 = (bf16[1,16,128,128]{3,2,1,0:T(8,128)(2,1)}, bf16[1,16,128,128]{3,2,1,0:T(8,128)(2,1)S(1)}, u32[]{:S(2)}, u32[]{:S(2)}) collective-permute-start(bf16[1,16,128,128]{3,2,1,0:T(8,128)(2,1)} %collective-permute-done.10.refs_5_), channel_id=1, source_target_pairs={{0,4},{2,6},{8,12},{10,14},{16,20},{18,22},{24,28},{26,30},{1,5},{... | collective-permute-start | bytes 1572872 | tf_op jit(solution)/shard_map/ppermute | solution.py:29
  48.1 15.6 %collective-permute-start.18 = (bf16[1,16,128,128]{3,2,1,0:T(8,128)(2,1)}, bf16[1,16,128,128]{3,2,1,0:T(8,128)(2,1)S(1)}, u32[]{:S(2)}, u32[]{:S(2)}) collective-permute-start(bf16[1,16,128,128]{3,2,1,0:T(8,128)(2,1)} %collective-permute-done.11.refs_6_), channel_id=1, source_target_pairs={{4,0},{6,2},{12,8},{14,10},{20,16},{22,18},{28,24},{30,26},{5,1},{... | collective-permute-start | bytes 1572872 | tf_op jit(solution)/shard_map/ppermute | solution.py:29
  50.5 23.6 %copy-start.15 = (bf16[1,16,128,128]{3,2,1,0:T(8,128)(2,1)}, bf16[1,16,128,128]{3,2,1,0:T(8,128)(2,1)S(1)}, u32[]{:S(2)}) copy-start(bf16[1,16,128,128]{3,2,1,0:T(8,128)(2,1)S(1)} %broadcast_select_fusion.1.refs_8_) | copy-start | bytes 1572868
  50.5 23.5 %collective-permute-start.12 = (bf16[1,16,128,128]{3,2,1,0:T(8,128)(2,1)S(1)}, bf16[1,16,128,128]{3,2,1,0:T(8,128)(2,1)S(1)}, u32[]{:S(2)}, u32[]{:S(2)}) collective-permute-start(bf16[1,16,128,128]{3,2,1,0:T(8,128)(2,1)S(1)} %bitcast.62), channel_id=1, source_target_pairs={{0,2},{4,6},{8,10},{12,14},{16,18},{20,22},{24,26},{28,30},{1,3},{... | collective-permute-start | bytes 1572872 | tf_op jit(solution)/shard_map/ppermute | solution.py:29
  51.9 16.3 %collective-permute-start.7 = (bf16[1,16,128,128]{3,2,1,0:T(8,128)(2,1)}, bf16[1,16,128,128]{3,2,1,0:T(8,128)(2,1)S(1)}, u32[]{:S(2)}, u32[]{:S(2)}) collective-permute-start(bf16[1,16,128,128]{3,2,1,0:T(8,128)(2,1)} %collective-permute-done.refs_2_), channel_id=1, source_target_pairs={{0,4},{2,6},{8,12},{10,14},{16,20},{18,22},{24,28},{26,30},{1,5},{... | collective-permute-start | bytes 1572872 | tf_op jit(solution)/shard_map/ppermute | solution.py:29
  55.4 17.1 %collective-permute-start.8 = (bf16[1,16,128,128]{3,2,1,0:T(8,128)(2,1)}, bf16[1,16,128,128]{3,2,1,0:T(8,128)(2,1)S(1)}, u32[]{:S(2)}, u32[]{:S(2)}) collective-permute-start(bf16[1,16,128,128]{3,2,1,0:T(8,128)(2,1)} %collective-permute-done.1.refs_0_), channel_id=1, source_target_pairs={{4,0},{6,2},{12,8},{14,10},{20,16},{22,18},{28,24},{30,26},{5,1},{... | collective-permute-start | bytes 1572872 | tf_op jit(solution)/shard_map/ppermute | solution.py:29
  57.9 18.8 %copy-start.16 = (bf16[1,16,128,128]{3,2,1,0:T(8,128)(2,1)}, bf16[1,16,128,128]{3,2,1,0:T(8,128)(2,1)S(1)}, u32[]{:S(2)}) copy-start(bf16[1,16,128,128]{3,2,1,0:T(8,128)(2,1)S(1)} %broadcast_select_fusion.3.refs_2_) | copy-start | bytes 1572868
  59.1 16.2 %collective-permute-start.2 = (bf16[1,16,128,128]{3,2,1,0:T(8,128)(2,1)S(1)}, bf16[1,16,128,128]{3,2,1,0:T(8,128)(2,1)S(1)}, u32[]{:S(2)}, u32[]{:S(2)}) collective-permute-start(bf16[1,16,128,128]{3,2,1,0:T(8,128)(2,1)S(1)} %bitcast.66), channel_id=1, source_target_pairs={{0,2},{4,6},{8,10},{12,14},{16,18},{20,22},{24,26},{28,30},{1,3},{... | collective-permute-start | bytes 1572872 | tf_op jit(solution)/shard_map/ppermute | solution.py:29
  63.7 11.7 %collective-permute-start.13 = (bf16[1,16,128,128]{3,2,1,0:T(8,128)(2,1)}, bf16[1,16,128,128]{3,2,1,0:T(8,128)(2,1)S(1)}, u32[]{:S(2)}, u32[]{:S(2)}) collective-permute-start(bf16[1,16,128,128]{3,2,1,0:T(8,128)(2,1)} %collective-permute-done.11.refs_6_), channel_id=1, source_target_pairs={{2,0},{6,4},{10,8},{14,12},{18,16},{22,20},{26,24},{30,28},{3,1},{... | collective-permute-start | bytes 1572872 | tf_op jit(solution)/shard_map/ppermute | solution.py:29
  65.1 12.4 %copy-start.17 = (bf16[1,16,128,128]{3,2,1,0:T(8,128)(2,1)}, bf16[1,16,128,128]{3,2,1,0:T(8,128)(2,1)S(1)}, u32[]{:S(2)}) copy-start(bf16[1,16,128,128]{3,2,1,0:T(8,128)(2,1)S(1)} %broadcast_select_fusion.refs_10_) | copy-start | bytes 1572868
  68.2 9.4 %collective-permute-start.16 = (bf16[1,16,128,128]{3,2,1,0:T(8,128)(2,1)S(1)}, bf16[1,16,128,128]{3,2,1,0:T(8,128)(2,1)S(1)}, u32[]{:S(2)}, u32[]{:S(2)}) collective-permute-start(bf16[1,16,128,128]{3,2,1,0:T(8,128)(2,1)S(1)} %broadcast_select_fusion.1.refs_8_), channel_id=1, source_target_pairs={{0,2},{2,0},{4,6},{6,4},{8,10},{10,8},{12,14},{14,12},{16,18},{18,... | collective-permute-start | bytes 1572872 | tf_op jit(solution)/shard_map/ppermute | solution.py:24
  72.5 4.2 %collective-permute-start.3 = (bf16[1,16,128,128]{3,2,1,0:T(8,128)(2,1)}, bf16[1,16,128,128]{3,2,1,0:T(8,128)(2,1)S(1)}, u32[]{:S(2)}, u32[]{:S(2)}) collective-permute-start(bf16[1,16,128,128]{3,2,1,0:T(8,128)(2,1)} %collective-permute-done.1.refs_0_), channel_id=1, source_target_pairs={{2,0},{6,4},{10,8},{14,12},{18,16},{22,20},{26,24},{30,28},{3,1},{... | collective-permute-start | bytes 1572872 | tf_op jit(solution)/shard_map/ppermute | solution.py:29
  74.0 3.8 %copy-start.18 = (bf16[1,16,128,128]{3,2,1,0:T(8,128)(2,1)}, bf16[1,16,128,128]{3,2,1,0:T(8,128)(2,1)S(1)}, u32[]{:S(2)}) copy-start(bf16[1,16,128,128]{3,2,1,0:T(8,128)(2,1)S(1)} %broadcast_select_fusion.2.refs_4_) | copy-start | bytes 1572868
  74.1 3.5 %collective-permute-start.6 = (bf16[1,16,128,128]{3,2,1,0:T(8,128)(2,1)S(1)}, bf16[1,16,128,128]{3,2,1,0:T(8,128)(2,1)S(1)}, u32[]{:S(2)}, u32[]{:S(2)}) collective-permute-start(bf16[1,16,128,128]{3,2,1,0:T(8,128)(2,1)S(1)} %broadcast_select_fusion.3.refs_2_), channel_id=1, source_target_pairs={{0,2},{2,0},{4,6},{6,4},{8,10},{10,8},{12,14},{14,12},{16,18},{18,... | collective-permute-start | bytes 1572872 | tf_op jit(solution)/shard_map/ppermute | solution.py:24
  75.3 2.5 %collective-permute-start.19 = (bf16[1,16,128,128]{3,2,1,0:T(8,128)(2,1)S(1)}, bf16[1,16,128,128]{3,2,1,0:T(8,128)(2,1)S(1)}, u32[]{:S(2)}, u32[]{:S(2)}) collective-permute-start(bf16[1,16,128,128]{3,2,1,0:T(8,128)(2,1)S(1)} %broadcast_select_fusion.refs_10_), channel_id=1, source_target_pairs={{0,2},{2,0},{4,6},{6,4},{8,10},{10,8},{12,14},{14,12},{16,18},{18,... | collective-permute-start | bytes 1572872 | tf_op jit(solution)/shard_map/ppermute | solution.py:24
  75.4 3.2 %collective-permute-start.9 = (bf16[1,16,128,128]{3,2,1,0:T(8,128)(2,1)S(1)}, bf16[1,16,128,128]{3,2,1,0:T(8,128)(2,1)S(1)}, u32[]{:S(2)}, u32[]{:S(2)}) collective-permute-start(bf16[1,16,128,128]{3,2,1,0:T(8,128)(2,1)S(1)} %broadcast_select_fusion.2.refs_4_), channel_id=1, source_target_pairs={{0,2},{2,0},{4,6},{6,4},{8,10},{10,8},{12,14},{14,12},{16,18},{18,... | collective-permute-start | bytes 1572872 | tf_op jit(solution)/shard_map/ppermute | solution.py:24
  77.5 1.0 copy-start.23
  77.5 1.9 %copy-start.24 = (bf16[1,16,128,128]{3,2,1,0:T(8,128)(2,1)}, bf16[1,16,128,128]{3,2,1,0:T(8,128)(2,1)S(1)}, u32[]{:S(2)}) copy-start(bf16[1,16,128,128]{3,2,1,0:T(8,128)(2,1)S(1)} %collective-permute-done.6.refs_3_) | copy-start | bytes 1572868
  77.8 1.6 copy-start.25
  78.5 0.8 copy-start.26
  101.1 6.1 %copy-start.10 = (bf16[1,16,128,128]{3,2,1,0:T(8,128)(2,1)S(1)}, bf16[1,16,128,128]{3,2,1,0:T(8,128)(2,1)}, u32[]{:S(2)}) copy-start(bf16[1,16,128,128]{3,2,1,0:T(8,128)(2,1)} %get-tuple-element.31) | copy-start | bytes 1572868
  101.1 2.2 %collective-permute-start.23 = (bf16[1,16,128,128]{3,2,1,0:T(8,128)(2,1)}, bf16[1,16,128,128]{3,2,1,0:T(8,128)(2,1)S(1)}, u32[]{:S(2)}, u32[]{:S(2)}) collective-permute-start(bf16[1,16,128,128]{3,2,1,0:T(8,128)(2,1)} %get-tuple-element.36), channel_id=1, source_target_pairs={{0,2},{2,0},{4,6},{6,4},{8,10},{10,8},{12,14},{14,12},{16,18},{18,... | collective-permute-start | bytes 1572872 | tf_op jit(solution)/shard_map/ppermute | solution.py:24
  101.4 3.4 %collective-permute-start.22 = (bf16[1,16,128,128]{3,2,1,0:T(8,128)(2,1)}, bf16[1,16,128,128]{3,2,1,0:T(8,128)(2,1)S(1)}, u32[]{:S(2)}, u32[]{:S(2)}) collective-permute-start(bf16[1,16,128,128]{3,2,1,0:T(8,128)(2,1)} %get-tuple-element.34), channel_id=1, source_target_pairs={{0,2},{2,0},{4,6},{6,4},{8,10},{10,8},{12,14},{14,12},{16,18},{18,... | collective-permute-start | bytes 1572872 | tf_op jit(solution)/shard_map/ppermute | solution.py:24
  102.4 5.7 %collective-permute-start.24 = (bf16[1,16,128,128]{3,2,1,0:T(8,128)(2,1)}, bf16[1,16,128,128]{3,2,1,0:T(8,128)(2,1)S(1)}, u32[]{:S(2)}, u32[]{:S(2)}) collective-permute-start(bf16[1,16,128,128]{3,2,1,0:T(8,128)(2,1)} %collective-permute-done.refs_2_), channel_id=1, source_target_pairs={{0,2},{2,0},{4,6},{6,4},{8,10},{10,8},{12,14},{14,12},{16,18},{18,... | collective-permute-start | bytes 1572872 | tf_op jit(solution)/shard_map/ppermute | solution.py:24
  102.5 8.6 %collective-permute-start.25 = (bf16[1,16,128,128]{3,2,1,0:T(8,128)(2,1)}, bf16[1,16,128,128]{3,2,1,0:T(8,128)(2,1)S(1)}, u32[]{:S(2)}, u32[]{:S(2)}) collective-permute-start(bf16[1,16,128,128]{3,2,1,0:T(8,128)(2,1)} %collective-permute-done.10.refs_5_), channel_id=1, source_target_pairs={{0,2},{2,0},{4,6},{6,4},{8,10},{10,8},{12,14},{14,12},{16,18},{18,... | collective-permute-start | bytes 1572872 | tf_op jit(solution)/shard_map/ppermute | solution.py:24
  102.9 22.2 %collective-permute-start.32 = (bf16[1,16,128,128]{3,2,1,0:T(8,128)(2,1)}, bf16[1,16,128,128]{3,2,1,0:T(8,128)(2,1)S(1)}, u32[]{:S(2)}, u32[]{:S(2)}) collective-permute-start(bf16[1,16,128,128]{3,2,1,0:T(8,128)(2,1)} %get-tuple-element.49), channel_id=1, source_target_pairs={{0,2},{2,0},{4,6},{6,4},{8,10},{10,8},{12,14},{14,12},{16,18},{18,... | collective-permute-start | bytes 1572872 | tf_op jit(solution)/shard_map/ppermute | solution.py:24
  103.3 3.9 %collective-permute-start.21 = (bf16[1,16,128,128]{3,2,1,0:T(8,128)(2,1)}, bf16[1,16,128,128]{3,2,1,0:T(8,128)(2,1)S(1)}, u32[]{:S(2)}, u32[]{:S(2)}) collective-permute-start(bf16[1,16,128,128]{3,2,1,0:T(8,128)(2,1)} %get-tuple-element.32), channel_id=1, source_target_pairs={{0,2},{2,0},{4,6},{6,4},{8,10},{10,8},{12,14},{14,12},{16,18},{18,... | collective-permute-start | bytes 1572872 | tf_op jit(solution)/shard_map/ppermute | solution.py:24
  103.5 6.7 %copy-start.9 = (bf16[1,16,128,128]{3,2,1,0:T(8,128)(2,1)S(1)}, bf16[1,16,128,128]{3,2,1,0:T(8,128)(2,1)}, u32[]{:S(2)}) copy-start(bf16[1,16,128,128]{3,2,1,0:T(8,128)(2,1)} %get-tuple-element.29) | copy-start | bytes 1572868
  104.8 3.5 %collective-permute-start.20 = (bf16[1,16,128,128]{3,2,1,0:T(8,128)(2,1)}, bf16[1,16,128,128]{3,2,1,0:T(8,128)(2,1)S(1)}, u32[]{:S(2)}, u32[]{:S(2)}) collective-permute-start(bf16[1,16,128,128]{3,2,1,0:T(8,128)(2,1)} %get-tuple-element.30), channel_id=1, source_target_pairs={{0,2},{2,0},{4,6},{6,4},{8,10},{10,8},{12,14},{14,12},{16,18},{18,... | collective-permute-start | bytes 1572872 | tf_op jit(solution)/shard_map/ppermute | solution.py:24
  107.2 18.0 %collective-permute-start.35 = (bf16[1,16,128,128]{3,2,1,0:T(8,128)(2,1)S(1)}, bf16[1,16,128,128]{3,2,1,0:T(8,128)(2,1)S(1)}, u32[]{:S(2)}, u32[]{:S(2)}) collective-permute-start(bf16[1,16,128,128]{3,2,1,0:T(8,128)(2,1)S(1)} %add_convert_fusion), channel_id=1, source_target_pairs={{0,4},{2,6},{4,0},{6,2},{8,12},{10,14},{12,8},{14,10},{16,20},{18,... | collective-permute-start | bytes 1572872 | tf_op jit(solution)/shard_map/ppermute | solution.py:24
  108.1 3.0 %copy-start.21 = (bf16[1,16,128,128]{3,2,1,0:T(8,128)(2,1)}, bf16[1,16,128,128]{3,2,1,0:T(8,128)(2,1)S(1)}, u32[]{:S(2)}) copy-start(bf16[1,16,128,128]{3,2,1,0:T(8,128)(2,1)S(1)} %collective-permute-done.24.refs_3_) | copy-start | bytes 1572868
  108.1 20.5 %collective-permute-start.26 = (bf16[1,16,128,128]{3,2,1,0:T(8,128)(2,1)}, bf16[1,16,128,128]{3,2,1,0:T(8,128)(2,1)S(1)}, u32[]{:S(2)}, u32[]{:S(2)}) collective-permute-start(bf16[1,16,128,128]{3,2,1,0:T(8,128)(2,1)} %get-tuple-element.42), channel_id=1, source_target_pairs={{0,2},{2,0},{4,6},{6,4},{8,10},{10,8},{12,14},{14,12},{16,18},{18,... | collective-permute-start | bytes 1572872 | tf_op jit(solution)/shard_map/ppermute | solution.py:24
  108.3 24.9 %collective-permute-start.29 = (bf16[1,16,128,128]{3,2,1,0:T(8,128)(2,1)}, bf16[1,16,128,128]{3,2,1,0:T(8,128)(2,1)S(1)}, u32[]{:S(2)}, u32[]{:S(2)}) collective-permute-start(bf16[1,16,128,128]{3,2,1,0:T(8,128)(2,1)} %add_convert_fusion.1), channel_id=1, source_target_pairs={{0,4},{2,6},{4,0},{6,2},{8,12},{10,14},{12,8},{14,10},{16,20},{18,... | collective-permute-start | bytes 1572872 | tf_op jit(solution)/shard_map/ppermute | solution.py:24
  111.1 0.8 copy-start.22
  124.8 8.3 %copy-start.19 = (bf16[1,16,128,128]{3,2,1,0:T(8,128)(2,1)S(1)}, bf16[1,16,128,128]{3,2,1,0:T(8,128)(2,1)}, u32[]{:S(2)}) copy-start(bf16[1,16,128,128]{3,2,1,0:T(8,128)(2,1)} %get-tuple-element.47) | copy-start | bytes 1572868
  124.9 19.5 %collective-permute-start.33 = (bf16[1,16,128,128]{3,2,1,0:T(8,128)(2,1)}, bf16[1,16,128,128]{3,2,1,0:T(8,128)(2,1)S(1)}, u32[]{:S(2)}, u32[]{:S(2)}) collective-permute-start(bf16[1,16,128,128]{3,2,1,0:T(8,128)(2,1)} %add_convert_fusion.2), channel_id=1, source_target_pairs={{0,4},{2,6},{4,0},{6,2},{8,12},{10,14},{12,8},{14,10},{16,20},{18,... | collective-permute-start | bytes 1572872 | tf_op jit(solution)/shard_map/ppermute | solution.py:24
  125.0 20.6 %collective-permute-start.34 = (bf16[1,16,128,128]{3,2,1,0:T(8,128)(2,1)}, bf16[1,16,128,128]{3,2,1,0:T(8,128)(2,1)}, u32[]{:S(2)}, u32[]{:S(2)}) collective-permute-start(bf16[1,16,128,128]{3,2,1,0:T(8,128)(2,1)} %get-tuple-element.52), channel_id=1, source_target_pairs={{0,2},{2,0},{4,6},{6,4},{8,10},{10,8},{12,14},{14,12},{16,18},{18,... | collective-permute-start | bytes 1572872 | tf_op jit(solution)/shard_map/ppermute | solution.py:24
  127.3 18.4 %collective-permute-start.36 = (bf16[1,16,128,128]{3,2,1,0:T(8,128)(2,1)}, bf16[1,16,128,128]{3,2,1,0:T(8,128)(2,1)}, u32[]{:S(2)}, u32[]{:S(2)}) collective-permute-start(bf16[1,16,128,128]{3,2,1,0:T(8,128)(2,1)} %fusion.18), channel_id=1, source_target_pairs={{8,0},{10,2},{12,4},{14,6},{16,8},{18,10},{20,12},{22,14},{24,16},... | collective-permute-start | bytes 1572872 | tf_op jit(solution)/shard_map/ppermute | solution.py:20
  128.6 26.3 %collective-permute-start.27 = (bf16[1,16,128,128]{3,2,1,0:T(8,128)(2,1)}, bf16[1,16,128,128]{3,2,1,0:T(8,128)(2,1)S(1)}, u32[]{:S(2)}, u32[]{:S(2)}) collective-permute-start(bf16[1,16,128,128]{3,2,1,0:T(8,128)(2,1)} %add_convert_fusion.3), channel_id=1, source_target_pairs={{0,4},{2,6},{4,0},{6,2},{8,12},{10,14},{12,8},{14,10},{16,20},{18,... | collective-permute-start | bytes 1572872 | tf_op jit(solution)/shard_map/ppermute | solution.py:24
  133.2 21.7 %collective-permute-start.28 = (bf16[1,16,128,128]{3,2,1,0:T(8,128)(2,1)}, bf16[1,16,128,128]{3,2,1,0:T(8,128)(2,1)}, u32[]{:S(2)}, u32[]{:S(2)}) collective-permute-start(bf16[1,16,128,128]{3,2,1,0:T(8,128)(2,1)} %get-tuple-element.45), channel_id=1, source_target_pairs={{0,2},{2,0},{4,6},{6,4},{8,10},{10,8},{12,14},{14,12},{16,18},{18,... | collective-permute-start | bytes 1572872 | tf_op jit(solution)/shard_map/ppermute | solution.py:24
  144.4 19.5 %copy-start.2 = (bf16[1,16,128,128]{3,2,1,0:T(8,128)(2,1)}, bf16[1,16,128,128]{3,2,1,0:T(8,128)(2,1)S(1)}, u32[]{:S(2)}) copy-start(bf16[1,16,128,128]{3,2,1,0:T(8,128)(2,1)S(1)} %collective-permute-done.33) | copy-start | bytes 1572868
  144.4 17.1 %collective-permute-start.30 = (bf16[1,16,128,128]{3,2,1,0:T(8,128)(2,1)}, bf16[1,16,128,128]{3,2,1,0:T(8,128)(2,1)}, u32[]{:S(2)}, u32[]{:S(2)}) collective-permute-start(bf16[1,16,128,128]{3,2,1,0:T(8,128)(2,1)} %fusion.7), channel_id=1, source_target_pairs={{8,0},{10,2},{12,4},{14,6},{16,8},{18,10},{20,12},{22,14},{24,16},... | collective-permute-start | bytes 1572872 | tf_op jit(solution)/shard_map/ppermute | solution.py:20
  145.7 15.8 %copy-start.20 = (bf16[1,16,128,128]{3,2,1,0:T(8,128)(2,1)S(1)}, bf16[1,16,128,128]{3,2,1,0:T(8,128)(2,1)}, u32[]{:S(2)}) copy-start(bf16[1,16,128,128]{3,2,1,0:T(8,128)(2,1)} %get-tuple-element.44) | copy-start | bytes 1572868
  148.4 16.8 %copy-start.1 = (f32[16,128,256]{2,1,0:T(8,128)S(1)}, f32[16,128,256]{2,1,0:T(8,128)}, u32[]{:S(2)}) copy-start(f32[16,128,256]{2,1,0:T(8,128)} %get-tuple-element.40) | copy-start | bytes 6291460
  148.4 24.3 %collective-permute-start.37 = (bf16[128,16,128]{2,0,1:T(8,128)(2,1)}, bf16[128,16,128]{2,0,1:T(8,128)(2,1)}, u32[]{:S(2)}, u32[]{:S(2)}) collective-permute-start(bf16[128,16,128]{2,0,1:T(8,128)(2,1)} %fusion.22), channel_id=1, source_target_pairs={{8,0},{10,2},{12,4},{14,6},{16,8},{18,10},{20,12},{22,14},{24,16},... | collective-permute-start | bytes 1572872 | tf_op jit(solution)/shard_map/ppermute | solution.py:20
  154.9 9.0 %copy-start.4 = (bf16[1,16,128,128]{3,2,1,0:T(8,128)(2,1)}, bf16[1,16,128,128]{3,2,1,0:T(8,128)(2,1)S(1)}, u32[]{:S(2)}) copy-start(bf16[1,16,128,128]{3,2,1,0:T(8,128)(2,1)S(1)} %collective-permute-done.27) | copy-start | bytes 1572868
  163.9 17.8 %collective-permute-start.31 = (bf16[128,16,128]{2,0,1:T(8,128)(2,1)}, bf16[128,16,128]{2,0,1:T(8,128)(2,1)}, u32[]{:S(2)}, u32[]{:S(2)}) collective-permute-start(bf16[128,16,128]{2,0,1:T(8,128)(2,1)} %fusion.23), channel_id=1, source_target_pairs={{8,0},{10,2},{12,4},{14,6},{16,8},{18,10},{20,12},{22,14},{24,16},... | collective-permute-start | bytes 1572872 | tf_op jit(solution)/shard_map/ppermute | solution.py:20
  165.7 7.0 %copy-start.3 = (bf16[1,16,128,128]{3,2,1,0:T(8,128)(2,1)S(1)}, bf16[1,16,128,128]{3,2,1,0:T(8,128)(2,1)}, u32[]{:S(2)}) copy-start(bf16[1,16,128,128]{3,2,1,0:T(8,128)(2,1)} %copy-done.2) | copy-start | bytes 1572868
  169.5 12.1 %copy-start.5 = (bf16[1,16,128,128]{3,2,1,0:T(8,128)(2,1)S(1)}, bf16[1,16,128,128]{3,2,1,0:T(8,128)(2,1)}, u32[]{:S(2)}) copy-start(bf16[1,16,128,128]{3,2,1,0:T(8,128)(2,1)} %copy-done.4) | copy-start | bytes 1572868
  169.5 12.1 %copy-start.8 = (bf16[1,16,128,128]{3,2,1,0:T(8,128)(2,1)S(1)}, bf16[1,16,128,128]{3,2,1,0:T(8,128)(2,1)}, u32[]{:S(2)}) copy-start(bf16[1,16,128,128]{3,2,1,0:T(8,128)(2,1)} %get-tuple-element.41) | copy-start | bytes 1572868
  (1 other events, 0.8 us)
